TPU v7x, 32 devices: a whole 2x2x4 slice. The times are simulated.
32 devices in a mesh: grp: 2 (over y), seq: 16 (over z, x, core).
Axes of the slice: x: 2, y: 2, z: 4, core: 2. Of those that a mesh axis runs over, the one named last changes fastest.
Arguments:
- activations: bfloat16 [131072, 256], P(('grp', 'seq')), parts along dimension 0, may hold values from -6 to 6
- cotangent: bfloat16 [131072, 256], P(('grp', 'seq')), parts along dimension 0, may hold values from -6 to 6
- conv_weight: bfloat16 [768, 512], replicated, may hold values from -0.21875 to 0.21875
- out_weight: bfloat16 [256, 256], replicated, may hold values from -0.375 to 0.375
Outputs:
- grad_input: bfloat16 [131072, 256], P(('grp', 'seq')), parts along dimension 0
- grad_conv: float32 [1536, 512], P('grp'), parts along dimension 0
- grad_out: float32 [512, 256], P('grp'), parts along dimension 0
There are 2 independent parts, one for each index of `grp`. A program takes and returns all parts, laid end to end along the dimension named above; an argument that names none is the same for every part. Nothing has to cross between parts.
All inputs are finite; a program needn't handle non-finite values.
Results may differ from a plain program's by a relative error of at most 0.0032.
Values may be sent and summed in bfloat16 or wider, within the bound.
No kernel may reach another device: no remote copies, remote signals or barrier semaphores. Data moves between devices by JAX's collectives and lax.ppermute only.
A program may use at most 128 MiB of HBM per device.

v0:
```python
import math

import jax
import jax.numpy as jnp
from jax import lax
from jax.sharding import PartitionSpec as P

SPACING_DEVICES = 4


def from_behind(value, axis, steps):
    count = lax.axis_size(axis)
    pairs = [(source, (source + steps) % count) for source in range(count)]
    return lax.ppermute(value, axis, pairs)


def local_layer(left_tap_input, middle, right_tap_input, grad_in, conv_weight, out_weight):
    channels = middle.shape[1]
    w_low = conv_weight[:channels]
    w_mid = conv_weight[channels : 2 * channels]
    w_high = conv_weight[2 * channels :]
    preact = jnp.dot(left_tap_input, w_low, preferred_element_type=jnp.float32)
    preact = preact + jnp.dot(middle, w_mid, preferred_element_type=jnp.float32)
    preact = preact + jnp.dot(right_tap_input, w_high, preferred_element_type=jnp.float32)
    tanh_part = jnp.tanh(preact[:, :channels])
    sigm_part = jax.nn.sigmoid(preact[:, channels:])
    gated_out = (tanh_part * sigm_part).astype(jnp.bfloat16)
    first_dims = (((0,), (0,)), ((), ()))
    last_dims = (((1,), (1,)), ((), ()))
    grad_wout = lax.dot_general(gated_out, grad_in, first_dims, preferred_element_type=jnp.float32)
    grad_gated = lax.dot_general(grad_in, out_weight, last_dims, preferred_element_type=jnp.float32)
    grad_filt = grad_gated * sigm_part * (1.0 - tanh_part * tanh_part)
    grad_gate = grad_gated * tanh_part * sigm_part * (1.0 - sigm_part)
    grad_pre = jnp.concatenate([grad_filt, grad_gate], axis=1).astype(jnp.bfloat16)
    grad_wconv = jnp.concatenate(
        [
            lax.dot_general(
                left_tap_input, grad_pre, first_dims, preferred_element_type=jnp.float32
            ),
            lax.dot_general(middle, grad_pre, first_dims, preferred_element_type=jnp.float32),
            lax.dot_general(
                right_tap_input, grad_pre, first_dims, preferred_element_type=jnp.float32
            ),
        ],
        axis=0,
    )
    lower_term = lax.dot_general(
        grad_pre, w_low, last_dims, preferred_element_type=jnp.float32
    ).astype(jnp.bfloat16)
    term_mid = lax.dot_general(grad_pre, w_mid, last_dims, preferred_element_type=jnp.float32)
    upper_term = lax.dot_general(
        grad_pre, w_high, last_dims, preferred_element_type=jnp.float32
    ).astype(jnp.bfloat16)
    return (grad_wconv, grad_wout, lower_term, term_mid, upper_term)


def body(activations, cotangent, conv_weight, out_weight):
    positions, channels = activations.shape
    seq_size = lax.axis_size("seq")
    left_tap_input = from_behind(activations, "seq", SPACING_DEVICES)
    right_tap_input = from_behind(activations, "seq", -SPACING_DEVICES)
    grad_wconv, grad_wout, lower_term, term_mid, upper_term = local_layer(
        left_tap_input, activations, right_tap_input, cotangent, conv_weight, out_weight
    )
    sums = lax.psum((grad_wconv, grad_wout), "seq")
    base_part = cotangent.astype(jnp.float32) + term_mid
    received_ahead = from_behind(lower_term, "seq", -SPACING_DEVICES)
    received_behind = from_behind(upper_term, "seq", SPACING_DEVICES)
    total_sum = base_part + received_ahead.astype(jnp.float32) + received_behind.astype(jnp.float32)
    grad_input = total_sum.astype(jnp.bfloat16)
    norm_factor = 1.0 / math.sqrt(positions * seq_size)
    return (grad_input, sums[0] * norm_factor, sums[1] * norm_factor)


def solution(mesh):
    in_specs = (P(("grp", "seq"), None), P(("grp", "seq"), None), P(), P())
    out_specs = (P(("grp", "seq"), None), P("grp", None), P("grp", None))
    return jax.shard_map(body, mesh=mesh, in_specs=in_specs, out_specs=out_specs, check_vma=False)
```

profile of v0, /device:TPU:0, one launch (start us, length us, event | category | flops | bytes accessed | tf_op | source)
XLA Modules:
  0.0 295.5 jit_solution(2926784463371136727)
XLA Ops:
  7.2 0.0 copy-start
  7.2 0.0 copy-start.2
  7.2 0.0 all-reduce.3.cloned.1.call-start
  7.2 3.1 %collective-permute-start = (bf16[4096,256]{1,0:T(8,128)(2,1)}, bf16[4096,256]{1,0:T(8,128)(2,1)S(1)}, u32[]{:S(2)}, u32[]{:S(2)}) collective-permute-start(bf16[4096,256]{1,0:T(8,128)(2,1)} %param.4), channel_id=1, source_target_pairs={{0,4},{1,5},{2,6},{3,7},{4,8},{5,9},{6,10},{7,11},{8,12},{9,13},{1... | collective-permute-start | bytes 6291464 | tf_op jit(solution)/shard_map/ppermute | solution.py:14
  10.3 2.1 collective-permute-start.1
  12.4 2.9 fusion.10
  15.3 43.7 %collective-permute-done = bf16[4096,256]{1,0:T(8,128)(2,1)S(1)} collective-permute-done((bf16[4096,256]{1,0:T(8,128)(2,1)}, bf16[4096,256]{1,0:T(8,128)(2,1)S(1)}, u32[]{:S(2)}, u32[]{:S(2)}) %collective-permute-start) | collective-permute-done | bytes 2097184 | tf_op jit(solution)/shard_map/ppermute | solution.py:14
  59.1 0.0 copy-done.2
  59.1 1.3 fusion.13
  60.4 0.0 copy-start.3
  60.4 42.2 %collective-permute-done.1 = bf16[4096,256]{1,0:T(8,128)(2,1)S(1)} collective-permute-done((bf16[4096,256]{1,0:T(8,128)(2,1)}, bf16[4096,256]{1,0:T(8,128)(2,1)S(1)}, u32[]{:S(2)}, u32[]{:S(2)}) %collective-permute-start.1) | collective-permute-done | bytes 2097184 | tf_op jit(solution)/shard_map/ppermute | solution.py:14
  102.6 4.7 %add_add_fusion = f32[4096,512]{0,1:T(8,128)} fusion(f32[4096,512]{0,1:T(8,128)S(1)} %fusion.13, f32[4096,512]{0,1:T(8,128)S(1)} %fusion.10, bf16[4096,256]{1,0:T(8,128)(2,1)S(1)} %collective-permute-done.1, bf16[768,512]{1,0:T(8,128)(2,1)S(1)} %copy-done.2), kind=kOutput, calls=%fused_computation | convolution fusion | flops 1077936128 | bytes 27525120 | tf_op jit(solution)/shard_map/dot_general | solution.py:24
  107.3 0.0 copy-done
  107.3 5.0 %multiply_convert_fusion.2 = (bf16[4096,256]{0,1:T(8,128)(2,1)S(1)}, bf16[4096,256]{0,1:T(8,128)(2,1)S(1)}) fusion(f32[4096,512]{0,1:T(8,128)} %add_add_fusion, bf16[4096,256]{1,0:T(8,128)(2,1)S(1)} %copy-done.3, bf16[256,256]{1,0:T(8,128)(2,1)S(1)} %copy-done), kind=kOutput, calls=%fused_computation.13 | convolution fusion | flops 550502400 | bytes 14811136 | tf_op jit(solution)/shard_map/dot_general | solution.py:31
  112.3 1.3 convolution_bitcast_fusion.1
  113.6 2.7 convolution_convert_fusion.1
  116.3 2.6 convolution_convert_fusion
  118.9 1.2 collective-permute-start.3
  120.1 2.7 collective-permute-start.2
  122.7 1.3 convolution_bitcast_fusion.2
  124.0 0.0 slice-start.1
  124.1 1.3 convolution_bitcast_fusion
  125.4 1.3 pad_maximum_fusion.1
  126.6 0.0 slice-done
  126.6 2.5 fusion.3
  129.1 0.0 all-reduce.3.cloned.1.call-update
  129.1 148.6 %all-reduce.3.cloned.1.call-done = (f32[768,512]{1,0:T(8,128)}, f32[256,256]{1,0:T(8,128)}) async-done(((f32[768,512]{1,0:T(8,128)}, f32[256,256]{1,0:T(8,128)}), (f32[768,512]{1,0:T(8,128)}, f32[256,256]{1,0:T(8,128)})) %all-reduce.3.cloned.1.call-update) | async-done | bytes 1835024 | tf_op jit(solution)/shard_map/psum | solution.py:65
  277.8 1.7 broadcast_multiply_fusion.1
  279.4 2.7 broadcast_multiply_fusion
  282.2 0.0 collective-permute-done.3
  282.2 0.0 collective-permute-done.2
  282.2 6.5 %add_convert_fusion = bf16[4096,256]{1,0:T(8,128)(2,1)} fusion(bf16[4096,256]{1,0:T(8,128)(2,1)} %collective-permute-done.3, bf16[4096,256]{1,0:T(8,128)(2,1)} %collective-permute-done.2, bf16[4096,256]{1,0:T(8,128)(2,1)S(1)} %copy-done.3, bf16[768,512]{1,0:T(8,128)(2,1)S(1)} %copy-done.2, bf16[4096,256]{0,1:T(8,128)(2,1)} %copy-done.5, ...), kind=kOutput, calls=%fused_computation.11 | convolution fusion | flops 1089470464 | bytes 12845056 | tf_op jit(solution)/shard_map/dot_general | solution.py:50
  (10 shorter events, 0.0 us)
Async XLA Ops:
  7.2 100.1 %copy-start = (bf16[256,256]{1,0:T(8,128)(2,1)S(1)}, bf16[256,256]{1,0:T(8,128)(2,1)}, u32[]{:S(2)}) copy-start(bf16[256,256]{1,0:T(8,128)(2,1)} %param.7) | copy-start | bytes 393220
  7.2 51.9 %copy-start.2 = (bf16[768,512]{1,0:T(8,128)(2,1)S(1)}, bf16[768,512]{1,0:T(8,128)(2,1)}, u32[]{:S(2)}) copy-start(bf16[768,512]{1,0:T(8,128)(2,1)} %param.6) | copy-start | bytes 2359300
  7.2 270.6 %all-reduce.3.cloned.1.call-start = ((), (), s32[]{:S(2)}) async-start(), calls=%async_computation | async-start | bytes 3670016 | tf_op jit(solution)/shard_map/psum | solution.py:65
  7.2 51.8 %collective-permute-start = (bf16[4096,256]{1,0:T(8,128)(2,1)}, bf16[4096,256]{1,0:T(8,128)(2,1)S(1)}, u32[]{:S(2)}, u32[]{:S(2)}) collective-permute-start(bf16[4096,256]{1,0:T(8,128)(2,1)} %param.4), channel_id=1, source_target_pairs={{0,4},{1,5},{2,6},{3,7},{4,8},{5,9},{6,10},{7,11},{8,12},{9,13},{1... | collective-permute-start | bytes 6291464 | tf_op jit(solution)/shard_map/ppermute | solution.py:14
  10.3 92.2 %collective-permute-start.1 = (bf16[4096,256]{1,0:T(8,128)(2,1)}, bf16[4096,256]{1,0:T(8,128)(2,1)S(1)}, u32[]{:S(2)}, u32[]{:S(2)}) collective-permute-start(bf16[4096,256]{1,0:T(8,128)(2,1)} %param.4), channel_id=1, source_target_pairs={{0,12},{1,13},{2,14},{3,15},{4,0},{5,1},{6,2},{7,3},{8,4},{9,5},{1... | collective-permute-start | bytes 6291464 | tf_op jit(solution)/shard_map/ppermute | solution.py:14
  60.4 46.9 %copy-start.3 = (bf16[4096,256]{1,0:T(8,128)(2,1)S(1)}, bf16[4096,256]{1,0:T(8,128)(2,1)}, u32[]{:S(2)}) copy-start(bf16[4096,256]{1,0:T(8,128)(2,1)} %param.5) | copy-start | bytes 6291460
  107.3 5.0 %copy-start.1 = (bf16[4096,256]{1,0:T(8,128)(2,1)S(1)}, bf16[4096,256]{1,0:T(8,128)(2,1)}, u32[]{:S(2)}) copy-start(bf16[4096,256]{1,0:T(8,128)(2,1)} %param.4) | copy-start | bytes 6291460
  112.3 11.8 %copy-start.4 = (bf16[4096,256]{0,1:T(8,128)(2,1)}, bf16[4096,256]{0,1:T(8,128)(2,1)S(1)}, u32[]{:S(2)}) copy-start(bf16[4096,256]{0,1:T(8,128)(2,1)S(1)} %get-tuple-element.5) | copy-start | bytes 6291460
  112.3 11.8 %copy-start.5 = (bf16[4096,256]{0,1:T(8,128)(2,1)}, bf16[4096,256]{0,1:T(8,128)(2,1)S(1)}, u32[]{:S(2)}) copy-start(bf16[4096,256]{0,1:T(8,128)(2,1)S(1)} %get-tuple-element.6) | copy-start | bytes 6291460
  118.9 163.3 %collective-permute-start.3 = (bf16[4096,256]{1,0:T(8,128)(2,1)}, bf16[4096,256]{1,0:T(8,128)(2,1)}, u32[]{:S(2)}, u32[]{:S(2)}) collective-permute-start(bf16[4096,256]{1,0:T(8,128)(2,1)} %convolution_convert_fusion), channel_id=1, source_target_pairs={{0,4},{1,5},{2,6},{3,7},{4,8},{5,9},{6,10},{7,11},{8,12},{9,13},{1... | collective-permute-start | bytes 6291464 | tf_op jit(solution)/shard_map/ppermute | solution.py:14
  120.1 162.1 %collective-permute-start.2 = (bf16[4096,256]{1,0:T(8,128)(2,1)}, bf16[4096,256]{1,0:T(8,128)(2,1)}, u32[]{:S(2)}, u32[]{:S(2)}) collective-permute-start(bf16[4096,256]{1,0:T(8,128)(2,1)} %convolution_convert_fusion.1), channel_id=1, source_target_pairs={{0,12},{1,13},{2,14},{3,15},{4,0},{5,1},{6,2},{7,3},{8,4},{9,5},{1... | collective-permute-start | bytes 6291464 | tf_op jit(solution)/shard_map/ppermute | solution.py:14
  122.7 3.9 %slice-start = ((s8[8388608]{0:T(1024)(128)(4,1)}), s8[4194304]{0:T(1024)(128)(4,1)S(1)}, s32[]{:S(2)}) async-start(s8[8388608]{0:T(1024)(128)(4,1)} %bitcast.15), calls=%async_computation.1 | async-start | bytes 8388608
  124.0 2.6 slice-start.1
Sparse Core Ops, SparseCore 0:
  129.3 148.4 all-reduce.2
where the time goes:
time: 296 us
  waiting for transfers between devices  235 us (79%)
  matrix products  32.1 us (11%)
  between operations  14.2 us (5%)
  starting transfers between devices  9.03 us (3%)
  other arithmetic  5.65 us (2%)
    psum x1, waiting for transfers between devices, body(): sums = lax.psum((grad_wconv, grad_wout), 'seq')  149 us
    ppermute x4, waiting for transfers between devices, from_behind(): return lax.ppermute(value, axis, pairs)  85.9 us
    ppermute x4, starting transfers between devices, from_behind(): return lax.ppermute(value, axis, pairs)  8.99 us
    dot_general x1, matrix products, local_layer(): lax.dot_general(grad_pre, w_mid, last_dims, preferred_element_type=jnp.fl...  6.53 us
  transfers between devices with their start and end apart: 5, of which 3 were waited for; matrix products, arithmetic and copies ran while one was open for 5% of the time, Pallas kernels for 0%

commit v1 on v0

v1 whole, which is shorter than its diff:
```python
import math

import jax
import jax.numpy as jnp
from jax import lax
from jax.sharding import PartitionSpec as P

TAP_SPACING = 16384
CHUNKS = 4


def from_behind(value, axis, steps):
    count = lax.axis_size(axis)
    pairs = [(source, (source + steps) % count) for source in range(count)]
    return lax.ppermute(value, axis, pairs)


def exchange(value, axis, bit):
    count = lax.axis_size(axis)
    pairs = [(source, source ^ bit) for source in range(count)]
    return lax.ppermute(value, axis, pairs)


def all_reduce_sum(flat, axis, scale):
    count = lax.axis_size(axis)
    idx = lax.axis_index(axis)
    bits = []
    bit = 1
    while bit < count:
        bits.append(bit)
        bit *= 2
    buf = flat
    for bit in bits:
        half = buf.shape[0] // 2
        upper = (idx // bit) % 2
        mine = lax.dynamic_slice_in_dim(buf, upper * half, half)
        theirs = lax.dynamic_slice_in_dim(buf, (1 - upper) * half, half)
        buf = mine + exchange(theirs, axis, bit)
    buf = buf * scale
    for bit in reversed(bits):
        upper = (idx // bit) % 2
        other = exchange(buf, axis, bit)
        lo = jnp.where(upper == 1, other, buf)
        hi = jnp.where(upper == 1, buf, other)
        buf = jnp.concatenate([lo, hi])
    return buf


def chunk_layer(left_tap_input, middle, right_tap_input, grad_in, conv_weight, out_weight):
    channels = middle.shape[1]
    w_low = conv_weight[:channels]
    w_mid = conv_weight[channels : 2 * channels]
    w_high = conv_weight[2 * channels :]
    preact = jnp.dot(left_tap_input, w_low, preferred_element_type=jnp.float32)
    preact = preact + jnp.dot(middle, w_mid, preferred_element_type=jnp.float32)
    preact = preact + jnp.dot(right_tap_input, w_high, preferred_element_type=jnp.float32)
    tanh_part = jnp.tanh(preact[:, :channels])
    sigm_part = jax.nn.sigmoid(preact[:, channels:])
    gated_out = (tanh_part * sigm_part).astype(jnp.bfloat16)
    first_dims = (((0,), (0,)), ((), ()))
    last_dims = (((1,), (1,)), ((), ()))
    grad_wout = lax.dot_general(gated_out, grad_in, first_dims, preferred_element_type=jnp.float32)
    grad_gated = lax.dot_general(grad_in, out_weight, last_dims, preferred_element_type=jnp.float32)
    grad_filt = grad_gated * sigm_part * (1.0 - tanh_part * tanh_part)
    grad_gate = grad_gated * tanh_part * sigm_part * (1.0 - sigm_part)
    grad_pre = jnp.concatenate([grad_filt, grad_gate], axis=1).astype(jnp.bfloat16)
    grad_wconv = jnp.concatenate(
        [
            lax.dot_general(left_tap_input, grad_pre, first_dims, preferred_element_type=jnp.float32),
            lax.dot_general(middle, grad_pre, first_dims, preferred_element_type=jnp.float32),
            lax.dot_general(right_tap_input, grad_pre, first_dims, preferred_element_type=jnp.float32),
        ],
        axis=0,
    )
    lower_term = lax.dot_general(grad_pre, w_low, last_dims, preferred_element_type=jnp.float32).astype(jnp.bfloat16)
    term_mid = lax.dot_general(grad_pre, w_mid, last_dims, preferred_element_type=jnp.float32)
    upper_term = lax.dot_general(grad_pre, w_high, last_dims, preferred_element_type=jnp.float32).astype(jnp.bfloat16)
    return grad_wconv, grad_wout, lower_term, term_mid, upper_term


def body(activations, cotangent, conv_weight, out_weight):
    positions, channels = activations.shape
    seq_size = lax.axis_size("seq")
    spacing = TAP_SPACING // positions
    rows = positions // CHUNKS
    wconv_total = None
    wout_total = None
    outs = []
    for k in range(CHUNKS):
        middle = activations[k * rows : (k + 1) * rows]
        grad_in = cotangent[k * rows : (k + 1) * rows]
        left_tap_input = from_behind(middle, "seq", spacing)
        right_tap_input = from_behind(middle, "seq", -spacing)
        grad_wconv, grad_wout, lower_term, term_mid, upper_term = chunk_layer(
            left_tap_input, middle, right_tap_input, grad_in, conv_weight, out_weight
        )
        wconv_total = grad_wconv if wconv_total is None else wconv_total + grad_wconv
        wout_total = grad_wout if wout_total is None else wout_total + grad_wout
        received_ahead = from_behind(lower_term, "seq", -spacing)
        received_behind = from_behind(upper_term, "seq", spacing)
        total_sum = grad_in.astype(jnp.float32) + term_mid
        total_sum = total_sum + received_ahead.astype(jnp.float32) + received_behind.astype(jnp.float32)
        outs.append(total_sum.astype(jnp.bfloat16))
    grad_input = jnp.concatenate(outs, axis=0)
    norm_factor = 1.0 / math.sqrt(positions * seq_size)
    flat = jnp.concatenate([wconv_total.reshape(-1), wout_total.reshape(-1)])
    summed = all_reduce_sum(flat, "seq", jnp.float32(norm_factor))
    split = wconv_total.size
    grad_conv = summed[:split].reshape(wconv_total.shape)
    grad_out = summed[split:].reshape(wout_total.shape)
    return grad_input, grad_conv, grad_out


def solution(mesh):
    in_specs = (P(("grp", "seq"), None), P(("grp", "seq"), None), P(), P())
    out_specs = (P(("grp", "seq"), None), P("grp", None), P("grp", None))
    return jax.shard_map(body, mesh=mesh, in_specs=in_specs, out_specs=out_specs, check_vma=False)
```

time: 296 us -> 258 us (0.87)
  waiting for transfers between devices: 235 us -> 165 us
  starting transfers between devices: 9.03 us -> 40.6 us
  between operations: 14.2 us -> 1.49 us
  local copies, waits for them, and re-layouts: 0.04 us -> 6.91 us
  matrix products: 32.1 us -> 37.5 us
    psum x1 -> x0, waiting for transfers between devices: 149 us -> none  [body(): sums = lax.psum((grad_wconv, grad_wout), 'seq')]
    ppermute x0 -> x8, waiting for transfers between devices: none -> 68.1 us  [exchange(): return lax.ppermute(value, axis, pairs)]
    ppermute x4 -> x16, starting transfers between devices: 8.99 us -> 32.3 us  [from_behind(): return lax.ppermute(value, axis, pairs)]
    ppermute x4 -> x16, waiting for transfers between devices: 85.9 us -> 96.4 us  [from_behind(): return lax.ppermute(value, axis, pairs)]
    ppermute x0 -> x8, starting transfers between devices: none -> 8.37 us  [exchange(): return lax.ppermute(value, axis, pairs)]
    dot_general x11 -> x44, matrix products: 32.1 us -> 37.5 us  [the longest x4 6.51 us: chunk_layer(): preact = preact + jnp.dot(middle, w_mid, preferred_element_type=jnp.float32)]
    mul x2 -> x1, other arithmetic: 4.38 us -> 0.02 us  [all_reduce_sum(): buf = buf * scale]
    slice x0 -> x3, local copies, waits for them, and re-layouts: none -> 3.74 us  [the longest x1 2.95 us: body(): middle = activations[k * rows:(k + 1) * rows]]
  transfers between devices with their start and end apart: 5 -> 24, of which waited for: 3 -> 13; matrix products, arithmetic and copies ran while one was open for 5% -> 10% of each run, Pallas kernels for 0% -> 0%
where the time goes in v1:
time: 258 us; the launch traced here: 257 us
  waiting for transfers between devices  165 us (64%)
  starting transfers between devices  40.6 us (16%)
  matrix products  37.5 us (15%)
  local copies, waits for them, and re-layouts  6.91 us (3%)
  other arithmetic  6.41 us (2%)
    ppermute x16, waiting for transfers between devices, from_behind(): return lax.ppermute(value, axis, pairs)  96.4 us
    ppermute x8, waiting for transfers between devices, exchange(): return lax.ppermute(value, axis, pairs)  68.1 us
    ppermute x16, starting transfers between devices, from_behind(): return lax.ppermute(value, axis, pairs)  32.3 us
    ppermute x8, starting transfers between devices, exchange(): return lax.ppermute(value, axis, pairs)  8.37 us
    dot_general x4, matrix products, chunk_layer(): preact = preact + jnp.dot(middle, w_mid, preferred_element_type=jnp.float32)  6.51 us
  transfers between devices with their start and end apart: 24, of which 13 were waited for; matrix products, arithmetic and copies ran while one was open for 10% of the time, Pallas kernels for 0%

profile of v1, /device:TPU:0, one launch (start us, length us, event | category | flops | bytes accessed | tf_op | source)
XLA Modules:
  0.0 257.4 jit_solution(16046632304442979439)
XLA Ops:
  0.7 2.9 %fusion.85 = (bf16[1024,256]{1,0:T(8,128)(2,1)}, bf16[1024,256]{1,0:T(8,128)(2,1)}, bf16[1024,256]{1,0:T(8,128)(2,1)}, bf16[1024,256]{1,0:T(8,128)(2,1)}) fusion(bf16[4096,256]{1,0:T(8,128)(2,1)} %param.4), kind=kLoop, calls=%fused_computation.152 | loop fusion | bytes 4194304 | tf_op jit(solution)/shard_map/slice | solution.py:90
  3.6 5.0 %collective-permute-start.1 = (bf16[1024,256]{1,0:T(8,128)(2,1)}, bf16[1024,256]{1,0:T(8,128)(2,1)S(1)}, u32[]{:S(2)}, u32[]{:S(2)}) collective-permute-start(bf16[1024,256]{1,0:T(8,128)(2,1)} %get-tuple-element.11), channel_id=1, source_target_pairs={{0,12},{1,13},{2,14},{3,15},{4,0},{5,1},{6,2},{7,3},{8,4},{9,5},{1... | collective-permute-start | bytes 1572872 | tf_op jit(solution)/shard_map/ppermute | solution.py:15
  8.7 3.8 %collective-permute-start.9 = (bf16[1024,256]{1,0:T(8,128)(2,1)}, bf16[1024,256]{1,0:T(8,128)(2,1)}, u32[]{:S(2)}, u32[]{:S(2)}) collective-permute-start(bf16[1024,256]{1,0:T(8,128)(2,1)} %get-tuple-element.14), channel_id=1, source_target_pairs={{0,12},{1,13},{2,14},{3,15},{4,0},{5,1},{6,2},{7,3},{8,4},{9,5},{1... | collective-permute-start | bytes 1572872 | tf_op jit(solution)/shard_map/ppermute | solution.py:15
  12.5 3.8 %collective-permute-start.5 = (bf16[1024,256]{1,0:T(8,128)(2,1)}, bf16[1024,256]{1,0:T(8,128)(2,1)}, u32[]{:S(2)}, u32[]{:S(2)}) collective-permute-start(bf16[1024,256]{1,0:T(8,128)(2,1)} %get-tuple-element.12), channel_id=1, source_target_pairs={{0,12},{1,13},{2,14},{3,15},{4,0},{5,1},{6,2},{7,3},{8,4},{9,5},{1... | collective-permute-start | bytes 1572872 | tf_op jit(solution)/shard_map/ppermute | solution.py:15
  16.3 2.8 %fusion.53 = f32[1024,512]{0,1:T(8,128)} fusion(bf16[768,512]{1,0:T(8,128)(2,1)S(1)} %copy-done.2, bf16[4096,256]{1,0:T(8,128)(2,1)} %param.4), kind=kOutput, calls=%fused_computation.122 | convolution fusion | flops 268435456 | bytes 2883584 | tf_op jit(solution)/shard_map/dot_general | solution.py:55
  20.7 1.7 fusion.56
  23.0 33.0 %collective-permute-done.8 = bf16[1024,256]{1,0:T(8,128)(2,1)} collective-permute-done((bf16[1024,256]{1,0:T(8,128)(2,1)}, bf16[1024,256]{1,0:T(8,128)(2,1)}, u32[]{:S(2)}, u32[]{:S(2)}) %collective-permute-start.8) | collective-permute-done | bytes 524320 | tf_op jit(solution)/shard_map/ppermute | solution.py:15
  59.1 2.3 collective-permute-start.13
  61.4 1.5 add_add_fusion.1
  63.2 1.7 fusion.71
  67.5 32.3 %collective-permute-done.12 = bf16[1024,256]{1,0:T(8,128)(2,1)S(1)} collective-permute-done((bf16[1024,256]{1,0:T(8,128)(2,1)S(1)}, bf16[1024,256]{1,0:T(8,128)(2,1)S(1)}, u32[]{:S(2)}, u32[]{:S(2)}) %collective-permute-start.12) | collective-permute-done | bytes 524320 | tf_op jit(solution)/shard_map/ppermute | solution.py:15
  102.0 1.9 add_add_fusion.2
  119.2 1.6 convolution_convert_fusion.3
  123.3 1.6 collective-permute-start.17
  125.9 10.1 %collective-permute-done.17 = f32[114688]{0:T(1024)S(1)} collective-permute-done((f32[114688]{0:T(1024)S(1)}, f32[114688]{0:T(1024)S(1)}, u32[]{:S(2)}, u32[]{:S(2)}) %collective-permute-start.17) | collective-permute-done | bytes 458784 | tf_op jit(solution)/shard_map/ppermute | solution.py:21
  136.0 1.7 collective-permute-start.18
  138.3 4.7 %collective-permute-done.18 = f32[57344]{0:T(1024)S(1)} collective-permute-done((f32[57344]{0:T(1024)S(1)}, f32[57344]{0:T(1024)S(1)}, u32[]{:S(2)}, u32[]{:S(2)}) %collective-permute-start.18) | collective-permute-done | bytes 229408 | tf_op jit(solution)/shard_map/ppermute | solution.py:21
  143.0 2.3 collective-permute-start.19
  145.8 4.2 %collective-permute-done.19 = f32[28672]{0:T(1024)S(1)} collective-permute-done((f32[28672]{0:T(1024)S(1)}, f32[28672]{0:T(1024)S(1)}, u32[]{:S(2)}, u32[]{:S(2)}) %collective-permute-start.19) | collective-permute-done | bytes 114720 | tf_op jit(solution)/shard_map/ppermute | solution.py:21
  151.7 2.2 collective-permute-start.11
  153.9 1.7 collective-permute-start.10
  155.9 3.5 %collective-permute-start.14 = (bf16[1024,256]{1,0:T(8,128)(2,1)S(1)}, bf16[1024,256]{1,0:T(8,128)(2,1)S(1)}, u32[]{:S(2)}, u32[]{:S(2)}) collective-permute-start(bf16[1024,256]{1,0:T(8,128)(2,1)S(1)} %convolution_convert_fusion.1), channel_id=1, source_target_pairs={{0,12},{1,13},{2,14},{3,15},{4,0},{5,1},{6,2},{7,3},{8,4},{9,5},{1... | collective-permute-start | bytes 1572872 | tf_op jit(solution)/shard_map/ppermute | solution.py:15
  159.4 8.5 %collective-permute-done.20 = f32[28672]{0:T(1024)S(1)} collective-permute-done((f32[28672]{0:T(1024)S(1)}, f32[28672]{0:T(1024)S(1)}, u32[]{:S(2)}, u32[]{:S(2)}) %collective-permute-start.20) | collective-permute-done | bytes 114720 | tf_op jit(solution)/shard_map/ppermute | solution.py:21
  168.6 35.8 %collective-permute-done.21 = f32[57344]{0:T(1024)S(1)} collective-permute-done((f32[57344]{0:T(1024)S(1)}, f32[57344]{0:T(1024)S(1)}, u32[]{:S(2)}, u32[]{:S(2)}) %collective-permute-start.21) | collective-permute-done | bytes 229408 | tf_op jit(solution)/shard_map/ppermute | solution.py:21
  204.7 3.6 %collective-permute-start.6 = (bf16[1024,256]{1,0:T(8,128)(2,1)S(1)}, bf16[1024,256]{1,0:T(8,128)(2,1)S(1)}, u32[]{:S(2)}, u32[]{:S(2)}) collective-permute-start(bf16[1024,256]{1,0:T(8,128)(2,1)S(1)} %convolution_convert_fusion.5), channel_id=1, source_target_pairs={{0,12},{1,13},{2,14},{3,15},{4,0},{5,1},{6,2},{7,3},{8,4},{9,5},{1... | collective-permute-start | bytes 1572872 | tf_op jit(solution)/shard_map/ppermute | solution.py:15
  210.4 3.8 %collective-permute-start.2 = (bf16[1024,256]{1,0:T(8,128)(2,1)S(1)}, bf16[1024,256]{1,0:T(8,128)(2,1)S(1)}, u32[]{:S(2)}, u32[]{:S(2)}) collective-permute-start(bf16[1024,256]{1,0:T(8,128)(2,1)S(1)} %convolution_convert_fusion.7), channel_id=1, source_target_pairs={{0,12},{1,13},{2,14},{3,15},{4,0},{5,1},{6,2},{7,3},{8,4},{9,5},{1... | collective-permute-start | bytes 1572872 | tf_op jit(solution)/shard_map/ppermute | solution.py:15
  214.7 4.2 %collective-permute-done.22 = f32[114688]{0:T(1024)S(1)} collective-permute-done((f32[114688]{0:T(1024)S(1)}, f32[114688]{0:T(1024)S(1)}, u32[]{:S(2)}, u32[]{:S(2)}) %collective-permute-start.22) | collective-permute-done | bytes 458784 | tf_op jit(solution)/shard_map/ppermute | solution.py:21
  219.2 1.8 collective-permute-done.7
  221.0 18.3 %collective-permute-done.6 = bf16[1024,256]{1,0:T(8,128)(2,1)S(1)} collective-permute-done((bf16[1024,256]{1,0:T(8,128)(2,1)S(1)}, bf16[1024,256]{1,0:T(8,128)(2,1)S(1)}, u32[]{:S(2)}, u32[]{:S(2)}) %collective-permute-start.6) | collective-permute-done | bytes 524320 | tf_op jit(solution)/shard_map/ppermute | solution.py:15
  239.8 3.7 %collective-permute-done.3 = bf16[1024,256]{1,0:T(8,128)(2,1)S(1)} collective-permute-done((bf16[1024,256]{1,0:T(8,128)(2,1)S(1)}, bf16[1024,256]{1,0:T(8,128)(2,1)S(1)}, u32[]{:S(2)}, u32[]{:S(2)}) %collective-permute-start.3) | collective-permute-done | bytes 524320 | tf_op jit(solution)/shard_map/ppermute | solution.py:15
  243.5 7.3 %collective-permute-done.2 = bf16[1024,256]{1,0:T(8,128)(2,1)S(1)} collective-permute-done((bf16[1024,256]{1,0:T(8,128)(2,1)S(1)}, bf16[1024,256]{1,0:T(8,128)(2,1)S(1)}, u32[]{:S(2)}, u32[]{:S(2)}) %collective-permute-start.2) | collective-permute-done | bytes 524320 | tf_op jit(solution)/shard_map/ppermute | solution.py:15
  255.0 2.4 pad_maximum_fusion.1
  (135 shorter events, 40.2 us)
Async XLA Ops:
  0.6 64.3 %copy-start = (bf16[256,256]{1,0:T(8,128)(2,1)S(1)}, bf16[256,256]{1,0:T(8,128)(2,1)}, u32[]{:S(2)}) copy-start(bf16[256,256]{1,0:T(8,128)(2,1)} %param.7) | copy-start | bytes 393220
  3.6 62.1 %collective-permute-start.1 = (bf16[1024,256]{1,0:T(8,128)(2,1)}, bf16[1024,256]{1,0:T(8,128)(2,1)S(1)}, u32[]{:S(2)}, u32[]{:S(2)}) collective-permute-start(bf16[1024,256]{1,0:T(8,128)(2,1)} %get-tuple-element.11), channel_id=1, source_target_pairs={{0,12},{1,13},{2,14},{3,15},{4,0},{5,1},{6,2},{7,3},{8,4},{9,5},{1... | collective-permute-start | bytes 1572872 | tf_op jit(solution)/shard_map/ppermute | solution.py:15
  8.7 54.3 %collective-permute-start = (bf16[1024,256]{1,0:T(8,128)(2,1)}, bf16[1024,256]{1,0:T(8,128)(2,1)}, u32[]{:S(2)}, u32[]{:S(2)}) collective-permute-start(bf16[1024,256]{1,0:T(8,128)(2,1)} %get-tuple-element.11), channel_id=1, source_target_pairs={{0,4},{1,5},{2,6},{3,7},{4,8},{5,9},{6,10},{7,11},{8,12},{9,13},{1... | collective-permute-start | bytes 1572872 | tf_op jit(solution)/shard_map/ppermute | solution.py:15
  8.7 50.4 %collective-permute-start.9 = (bf16[1024,256]{1,0:T(8,128)(2,1)}, bf16[1024,256]{1,0:T(8,128)(2,1)}, u32[]{:S(2)}, u32[]{:S(2)}) collective-permute-start(bf16[1024,256]{1,0:T(8,128)(2,1)} %get-tuple-element.14), channel_id=1, source_target_pairs={{0,12},{1,13},{2,14},{3,15},{4,0},{5,1},{6,2},{7,3},{8,4},{9,5},{1... | collective-permute-start | bytes 1572872 | tf_op jit(solution)/shard_map/ppermute | solution.py:15
  12.5 43.5 %collective-permute-start.8 = (bf16[1024,256]{1,0:T(8,128)(2,1)}, bf16[1024,256]{1,0:T(8,128)(2,1)}, u32[]{:S(2)}, u32[]{:S(2)}) collective-permute-start(bf16[1024,256]{1,0:T(8,128)(2,1)} %get-tuple-element.14), channel_id=1, source_target_pairs={{0,4},{1,5},{2,6},{3,7},{4,8},{5,9},{6,10},{7,11},{8,12},{9,13},{1... | collective-permute-start | bytes 1572872 | tf_op jit(solution)/shard_map/ppermute | solution.py:15
  12.5 89.5 %collective-permute-start.5 = (bf16[1024,256]{1,0:T(8,128)(2,1)}, bf16[1024,256]{1,0:T(8,128)(2,1)}, u32[]{:S(2)}, u32[]{:S(2)}) collective-permute-start(bf16[1024,256]{1,0:T(8,128)(2,1)} %get-tuple-element.12), channel_id=1, source_target_pairs={{0,12},{1,13},{2,14},{3,15},{4,0},{5,1},{6,2},{7,3},{8,4},{9,5},{1... | collective-permute-start | bytes 1572872 | tf_op jit(solution)/shard_map/ppermute | solution.py:15
  22.9 36.1 %copy-start.5 = (bf16[1024,256]{1,0:T(8,128)(2,1)S(1)}, bf16[1024,256]{1,0:T(8,128)(2,1)}, u32[]{:S(2)}) copy-start(bf16[1024,256]{1,0:T(8,128)(2,1)} %get-tuple-element.13) | copy-start | bytes 1572868
  22.9 38.5 %copy-start.3 = (f32[1024,512]{0,1:T(8,128)S(1)}, f32[1024,512]{0,1:T(8,128)}, u32[]{:S(2)}) copy-start(f32[1024,512]{0,1:T(8,128)} %fusion.53) | copy-start | bytes 6291460
  56.0 44.8 %collective-permute-start.4 = (bf16[1024,256]{1,0:T(8,128)(2,1)}, bf16[1024,256]{1,0:T(8,128)(2,1)S(1)}, u32[]{:S(2)}, u32[]{:S(2)}) collective-permute-start(bf16[1024,256]{1,0:T(8,128)(2,1)} %get-tuple-element.12), channel_id=1, source_target_pairs={{0,4},{1,5},{2,6},{3,7},{4,8},{5,9},{6,10},{7,11},{8,12},{9,13},{1... | collective-permute-start | bytes 1572872 | tf_op jit(solution)/shard_map/ppermute | solution.py:15
  59.1 41.1 %collective-permute-start.13 = (bf16[1024,256]{1,0:T(8,128)(2,1)S(1)}, bf16[1024,256]{1,0:T(8,128)(2,1)S(1)}, u32[]{:S(2)}, u32[]{:S(2)}) collective-permute-start(bf16[1024,256]{1,0:T(8,128)(2,1)S(1)} %copy-done.5), channel_id=1, source_target_pairs={{0,12},{1,13},{2,14},{3,15},{4,0},{5,1},{6,2},{7,3},{8,4},{9,5},{1... | collective-permute-start | bytes 1572872 | tf_op jit(solution)/shard_map/ppermute | solution.py:15
  63.0 36.7 %collective-permute-start.12 = (bf16[1024,256]{1,0:T(8,128)(2,1)S(1)}, bf16[1024,256]{1,0:T(8,128)(2,1)S(1)}, u32[]{:S(2)}, u32[]{:S(2)}) collective-permute-start(bf16[1024,256]{1,0:T(8,128)(2,1)S(1)} %copy-done.5), channel_id=1, source_target_pairs={{0,4},{1,5},{2,6},{3,7},{4,8},{5,9},{6,10},{7,11},{8,12},{9,13},{1... | collective-permute-start | bytes 1572872 | tf_op jit(solution)/shard_map/ppermute | solution.py:15
  65.6 44.3 %copy-start.16 = (bf16[1024,256]{0,1:T(8,128)(2,1)}, bf16[1024,256]{0,1:T(8,128)(2,1)S(1)}, u32[]{:S(2)}) copy-start(bf16[1024,256]{0,1:T(8,128)(2,1)S(1)} %get-tuple-element.7) | copy-start | bytes 1572868
  65.7 44.3 %copy-start.18 = (bf16[1024,256]{0,1:T(8,128)(2,1)}, bf16[1024,256]{0,1:T(8,128)(2,1)S(1)}, u32[]{:S(2)}) copy-start(bf16[1024,256]{0,1:T(8,128)(2,1)S(1)} %get-tuple-element.8) | copy-start | bytes 1572868
  66.9 49.2 %copy-start.8 = (bf16[1024,256]{0,1:T(8,128)(2,1)}, bf16[1024,256]{0,1:T(8,128)(2,1)S(1)}, u32[]{:S(2)}) copy-start(bf16[1024,256]{0,1:T(8,128)(2,1)S(1)} %get-tuple-element.3) | copy-start | bytes 1572868
  66.9 49.2 %copy-start.10 = (bf16[1024,256]{0,1:T(8,128)(2,1)}, bf16[1024,256]{0,1:T(8,128)(2,1)S(1)}, u32[]{:S(2)}) copy-start(bf16[1024,256]{0,1:T(8,128)(2,1)S(1)} %get-tuple-element.4) | copy-start | bytes 1572868
  119.2 2.8 %collective-permute-start.16 = (f32[229376]{0:T(1024)}, f32[229376]{0:T(1024)}, u32[]{:S(2)}, u32[]{:S(2)}) collective-permute-start(f32[229376]{0:T(1024)} %dynamic_slice.25), channel_id=1, source_target_pairs={{0,1},{1,0},{2,3},{3,2},{4,5},{5,4},{6,7},{7,6},{8,9},{9,8},{10,11... | collective-permute-start | bytes 2752520 | tf_op jit(solution)/shard_map/ppermute | solution.py:21
  123.3 12.6 %collective-permute-start.17 = (f32[114688]{0:T(1024)S(1)}, f32[114688]{0:T(1024)S(1)}, u32[]{:S(2)}, u32[]{:S(2)}) collective-permute-start(f32[114688]{0:T(1024)S(1)} %dynamic_slice.27), channel_id=1, source_target_pairs={{0,2},{1,3},{2,0},{3,1},{4,6},{5,7},{6,4},{7,5},{8,10},{9,11},{10,... | collective-permute-start | bytes 1376264 | tf_op jit(solution)/shard_map/ppermute | solution.py:21
  136.0 6.9 %collective-permute-start.18 = (f32[57344]{0:T(1024)S(1)}, f32[57344]{0:T(1024)S(1)}, u32[]{:S(2)}, u32[]{:S(2)}) collective-permute-start(f32[57344]{0:T(1024)S(1)} %dynamic_slice.29), channel_id=1, source_target_pairs={{0,4},{1,5},{2,6},{3,7},{4,0},{5,1},{6,2},{7,3},{8,12},{9,13},{10,... | collective-permute-start | bytes 688136 | tf_op jit(solution)/shard_map/ppermute | solution.py:21
  143.0 7.0 %collective-permute-start.19 = (f32[28672]{0:T(1024)S(1)}, f32[28672]{0:T(1024)S(1)}, u32[]{:S(2)}, u32[]{:S(2)}) collective-permute-start(f32[28672]{0:T(1024)S(1)} %dynamic_slice.31), channel_id=1, source_target_pairs={{0,8},{1,9},{2,10},{3,11},{4,12},{5,13},{6,14},{7,15},{8,0},{9,1},... | collective-permute-start | bytes 344072 | tf_op jit(solution)/shard_map/ppermute | solution.py:21
  150.0 17.9 %collective-permute-start.20 = (f32[28672]{0:T(1024)S(1)}, f32[28672]{0:T(1024)S(1)}, u32[]{:S(2)}, u32[]{:S(2)}) collective-permute-start(f32[28672]{0:T(1024)S(1)} %add_multiply_fusion), channel_id=1, source_target_pairs={{0,8},{1,9},{2,10},{3,11},{4,12},{5,13},{6,14},{7,15},{8,0},{9,1},... | collective-permute-start | bytes 344072 | tf_op jit(solution)/shard_map/ppermute | solution.py:21
  151.7 53.0 %collective-permute-start.11 = (bf16[1024,256]{1,0:T(8,128)(2,1)S(1)}, bf16[1024,256]{1,0:T(8,128)(2,1)S(1)}, u32[]{:S(2)}, u32[]{:S(2)}) collective-permute-start(bf16[1024,256]{1,0:T(8,128)(2,1)S(1)} %convolution_convert_fusion.2), channel_id=1, source_target_pairs={{0,4},{1,5},{2,6},{3,7},{4,8},{5,9},{6,10},{7,11},{8,12},{9,13},{1... | collective-permute-start | bytes 1572872 | tf_op jit(solution)/shard_map/ppermute | solution.py:15
  153.9 54.4 %collective-permute-start.10 = (bf16[1024,256]{1,0:T(8,128)(2,1)S(1)}, bf16[1024,256]{1,0:T(8,128)(2,1)S(1)}, u32[]{:S(2)}, u32[]{:S(2)}) collective-permute-start(bf16[1024,256]{1,0:T(8,128)(2,1)S(1)} %convolution_convert_fusion.3), channel_id=1, source_target_pairs={{0,12},{1,13},{2,14},{3,15},{4,0},{5,1},{6,2},{7,3},{8,4},{9,5},{1... | collective-permute-start | bytes 1572872 | tf_op jit(solution)/shard_map/ppermute | solution.py:15
  155.6 54.8 %collective-permute-start.15 = (bf16[1024,256]{1,0:T(8,128)(2,1)S(1)}, bf16[1024,256]{1,0:T(8,128)(2,1)S(1)}, u32[]{:S(2)}, u32[]{:S(2)}) collective-permute-start(bf16[1024,256]{1,0:T(8,128)(2,1)S(1)} %convolution_convert_fusion), channel_id=1, source_target_pairs={{0,4},{1,5},{2,6},{3,7},{4,8},{5,9},{6,10},{7,11},{8,12},{9,13},{1... | collective-permute-start | bytes 1572872 | tf_op jit(solution)/shard_map/ppermute | solution.py:15
  155.9 54.5 %collective-permute-start.14 = (bf16[1024,256]{1,0:T(8,128)(2,1)S(1)}, bf16[1024,256]{1,0:T(8,128)(2,1)S(1)}, u32[]{:S(2)}, u32[]{:S(2)}) collective-permute-start(bf16[1024,256]{1,0:T(8,128)(2,1)S(1)} %convolution_convert_fusion.1), channel_id=1, source_target_pairs={{0,12},{1,13},{2,14},{3,15},{4,0},{5,1},{6,2},{7,3},{8,4},{9,5},{1... | collective-permute-start | bytes 1572872 | tf_op jit(solution)/shard_map/ppermute | solution.py:15
  168.0 41.8 %copy-start.7 = (bf16[4096,256]{1,0:T(8,128)(2,1)S(1)}, bf16[4096,256]{1,0:T(8,128)(2,1)}, u32[]{:S(2)}) copy-start(bf16[4096,256]{1,0:T(8,128)(2,1)} %param.5) | copy-start | bytes 6291460
  168.0 36.3 %collective-permute-start.21 = (f32[57344]{0:T(1024)S(1)}, f32[57344]{0:T(1024)S(1)}, u32[]{:S(2)}, u32[]{:S(2)}) collective-permute-start(f32[57344]{0:T(1024)S(1)} %pad_maximum_fusion.8), channel_id=1, source_target_pairs={{0,4},{1,5},{2,6},{3,7},{4,0},{5,1},{6,2},{7,3},{8,12},{9,13},{10,... | collective-permute-start | bytes 688136 | tf_op jit(solution)/shard_map/ppermute | solution.py:21
  204.3 16.7 %collective-permute-start.7 = (bf16[1024,256]{1,0:T(8,128)(2,1)S(1)}, bf16[1024,256]{1,0:T(8,128)(2,1)S(1)}, u32[]{:S(2)}, u32[]{:S(2)}) collective-permute-start(bf16[1024,256]{1,0:T(8,128)(2,1)S(1)} %convolution_convert_fusion.4), channel_id=1, source_target_pairs={{0,4},{1,5},{2,6},{3,7},{4,8},{5,9},{6,10},{7,11},{8,12},{9,13},{1... | collective-permute-start | bytes 1572872 | tf_op jit(solution)/shard_map/ppermute | solution.py:15
  204.7 34.6 %collective-permute-start.6 = (bf16[1024,256]{1,0:T(8,128)(2,1)S(1)}, bf16[1024,256]{1,0:T(8,128)(2,1)S(1)}, u32[]{:S(2)}, u32[]{:S(2)}) collective-permute-start(bf16[1024,256]{1,0:T(8,128)(2,1)S(1)} %convolution_convert_fusion.5), channel_id=1, source_target_pairs={{0,12},{1,13},{2,14},{3,15},{4,0},{5,1},{6,2},{7,3},{8,4},{9,5},{1... | collective-permute-start | bytes 1572872 | tf_op jit(solution)/shard_map/ppermute | solution.py:15
  208.3 10.6 %collective-permute-start.22 = (f32[114688]{0:T(1024)S(1)}, f32[114688]{0:T(1024)S(1)}, u32[]{:S(2)}, u32[]{:S(2)}) collective-permute-start(f32[114688]{0:T(1024)S(1)} %pad_maximum_fusion.7), channel_id=1, source_target_pairs={{0,2},{1,3},{2,0},{3,1},{4,6},{5,7},{6,4},{7,5},{8,10},{9,11},{10,... | collective-permute-start | bytes 1376264 | tf_op jit(solution)/shard_map/ppermute | solution.py:21
  210.3 33.2 %collective-permute-start.3 = (bf16[1024,256]{1,0:T(8,128)(2,1)S(1)}, bf16[1024,256]{1,0:T(8,128)(2,1)S(1)}, u32[]{:S(2)}, u32[]{:S(2)}) collective-permute-start(bf16[1024,256]{1,0:T(8,128)(2,1)S(1)} %convolution_convert_fusion.6), channel_id=1, source_target_pairs={{0,4},{1,5},{2,6},{3,7},{4,8},{5,9},{6,10},{7,11},{8,12},{9,13},{1... | collective-permute-start | bytes 1572872 | tf_op jit(solution)/shard_map/ppermute | solution.py:15
  210.4 40.4 %collective-permute-start.2 = (bf16[1024,256]{1,0:T(8,128)(2,1)S(1)}, bf16[1024,256]{1,0:T(8,128)(2,1)S(1)}, u32[]{:S(2)}, u32[]{:S(2)}) collective-permute-start(bf16[1024,256]{1,0:T(8,128)(2,1)S(1)} %convolution_convert_fusion.7), channel_id=1, source_target_pairs={{0,12},{1,13},{2,14},{3,15},{4,0},{5,1},{6,2},{7,3},{8,4},{9,5},{1... | collective-permute-start | bytes 1572872 | tf_op jit(solution)/shard_map/ppermute | solution.py:15
  219.1 33.7 %collective-permute-start.23 = (f32[229376]{0:T(1024)S(1)}, f32[229376]{0:T(1024)S(1)}, u32[]{:S(2)}, u32[]{:S(2)}) collective-permute-start(f32[229376]{0:T(1024)S(1)} %pad_maximum_fusion.6), channel_id=1, source_target_pairs={{0,1},{1,0},{2,3},{3,2},{4,5},{5,4},{6,7},{7,6},{8,9},{9,8},{10,11... | collective-permute-start | bytes 2752520 | tf_op jit(solution)/shard_map/ppermute | solution.py:21
  (16 other events, 121.1 us)

commit v2 on v1

--- a/solution.py
+++ b/solution.py
@@ -7,6 +7,7 @@
 
 TAP_SPACING = 16384
 CHUNKS = 4
+TERM_PIECES = 4
 
 
 def from_behind(value, axis, steps):
@@ -21,7 +22,7 @@
     return lax.ppermute(value, axis, pairs)
 
 
-def all_reduce_sum(flat, axis, scale):
+def all_reduce_sum(flat, axis, scale, riders):
     count = lax.axis_size(axis)
     idx = lax.axis_index(axis)
     bits = []
@@ -29,21 +30,29 @@
     while bit < count:
         bits.append(bit)
         bit *= 2
+    steps = [(bit, True) for bit in bits] + [(bit, False) for bit in reversed(bits)]
+    per_rider = -(-len(steps) // max(len(riders), 1))
+    results = []
     buf = flat
-    for bit in bits:
-        half = buf.shape[0] // 2
+    for number, (bit, down) in enumerate(steps):
+        if riders and number % per_rider == 0:
+            if results:
+                buf, results[-1] = lax.optimization_barrier((buf, results[-1]))
+            results.append(riders[len(results)]())
         upper = (idx // bit) % 2
-        mine = lax.dynamic_slice_in_dim(buf, upper * half, half)
-        theirs = lax.dynamic_slice_in_dim(buf, (1 - upper) * half, half)
-        buf = mine + exchange(theirs, axis, bit)
-    buf = buf * scale
-    for bit in reversed(bits):
-        upper = (idx // bit) % 2
-        other = exchange(buf, axis, bit)
-        lo = jnp.where(upper == 1, other, buf)
-        hi = jnp.where(upper == 1, buf, other)
-        buf = jnp.concatenate([lo, hi])
-    return buf
+        if down:
+            half = buf.shape[0] // 2
+            mine = lax.dynamic_slice_in_dim(buf, upper * half, half)
+            theirs = lax.dynamic_slice_in_dim(buf, (1 - upper) * half, half)
+            buf = mine + exchange(theirs, axis, bit)
+            if number == len(bits) - 1:
+                buf = buf * scale
+        else:
+            other = exchange(buf, axis, bit)
+            lo = jnp.where(upper == 1, other, buf)
+            hi = jnp.where(upper == 1, buf, other)
+            buf = jnp.concatenate([lo, hi])
+    return buf, results
 
 
 def chunk_layer(left_tap_input, middle, right_tap_input, grad_in, conv_weight, out_weight):
@@ -85,7 +94,7 @@
     rows = positions // CHUNKS
     wconv_total = None
     wout_total = None
-    outs = []
+    lows, mids, highs = [], [], []
     for k in range(CHUNKS):
         middle = activations[k * rows : (k + 1) * rows]
         grad_in = cotangent[k * rows : (k + 1) * rows]
@@ -96,15 +105,29 @@
         )
         wconv_total = grad_wconv if wconv_total is None else wconv_total + grad_wconv
         wout_total = grad_wout if wout_total is None else wout_total + grad_wout
-        received_ahead = from_behind(lower_term, "seq", -spacing)
-        received_behind = from_behind(upper_term, "seq", spacing)
-        total_sum = grad_in.astype(jnp.float32) + term_mid
-        total_sum = total_sum + received_ahead.astype(jnp.float32) + received_behind.astype(jnp.float32)
-        outs.append(total_sum.astype(jnp.bfloat16))
-    grad_input = jnp.concatenate(outs, axis=0)
+        lows.append(lower_term)
+        mids.append(term_mid)
+        highs.append(upper_term)
+    lower_all = jnp.concatenate(lows, axis=0)
+    upper_all = jnp.concatenate(highs, axis=0)
+    piece = positions // TERM_PIECES
+
+    def rider(p):
+        return lambda: (
+            from_behind(lower_all[p * piece : (p + 1) * piece], "seq", -spacing),
+            from_behind(upper_all[p * piece : (p + 1) * piece], "seq", spacing),
+        )
+
     norm_factor = 1.0 / math.sqrt(positions * seq_size)
     flat = jnp.concatenate([wconv_total.reshape(-1), wout_total.reshape(-1)])
-    summed = all_reduce_sum(flat, "seq", jnp.float32(norm_factor))
+    summed, received = all_reduce_sum(
+        flat, "seq", jnp.float32(norm_factor), [rider(p) for p in range(TERM_PIECES)]
+    )
+    received_ahead = jnp.concatenate([pair[0] for pair in received], axis=0)
+    received_behind = jnp.concatenate([pair[1] for pair in received], axis=0)
+    total_sum = cotangent.astype(jnp.float32) + jnp.concatenate(mids, axis=0)
+    total_sum = total_sum + received_ahead.astype(jnp.float32) + received_behind.astype(jnp.float32)
+    grad_input = total_sum.astype(jnp.bfloat16)
     split = wconv_total.size
     grad_conv = summed[:split].reshape(wconv_total.shape)
     grad_out = summed[split:].reshape(wout_total.shape)

time: 258 us -> 250 us (0.969)
  waiting for transfers between devices: 165 us -> 138 us
  starting transfers between devices: 40.6 us -> 64.8 us
  matrix products: 37.5 us -> 33.7 us
    ppermute x16, waiting for transfers between devices: 96.4 us -> 74.2 us  [from_behind(): return lax.ppermute(value, axis, pairs)]
    ppermute x16, starting transfers between devices: 32.3 us -> 45.8 us  [from_behind(): return lax.ppermute(value, axis, pairs)]
    ppermute x8, starting transfers between devices: 8.37 us -> 19 us  [exchange(): return lax.ppermute(value, axis, pairs)]
    ppermute x8, waiting for transfers between devices: 68.1 us -> 63.7 us  [exchange(): return lax.ppermute(value, axis, pairs)]
  transfers between devices with their start and end apart: 24 -> 24, of which waited for: 13 -> 16; matrix products, arithmetic and copies ran while one was open for 10% -> 9% of each run, Pallas kernels for 0% -> 0%
where the time goes in v2:
time: 250 us
  waiting for transfers between devices  138 us (55%)
  starting transfers between devices  64.8 us (26%)
  matrix products  33.7 us (13%)
  local copies, waits for them, and re-layouts  5.96 us (2%)
  other arithmetic  5.71 us (2%)
    ppermute x16, waiting for transfers between devices, from_behind(): return lax.ppermute(value, axis, pairs)  74.2 us
    ppermute x8, waiting for transfers between devices, exchange(): return lax.ppermute(value, axis, pairs)  63.7 us
    ppermute x16, starting transfers between devices, from_behind(): return lax.ppermute(value, axis, pairs)  45.8 us
    ppermute x8, starting transfers between devices, exchange(): return lax.ppermute(value, axis, pairs)  19 us
    dot_general x4, matrix products, chunk_layer(): lax.dot_general(left_tap_input, grad_pre, first_dims, preferred_element_t...  5.05 us
    dot_general x4, matrix products, chunk_layer(): preact = jnp.dot(left_tap_input, w_low, preferred_element_type=jnp.float32)  5.04 us
  transfers between devices with their start and end apart: 24, of which 16 were waited for; matrix products, arithmetic and copies ran while one was open for 9% of the time, Pallas kernels for 0%

profile of v2, /device:TPU:0, one launch (start us, length us, event | category | flops | bytes accessed | tf_op | source)
XLA Modules:
  0.0 249.6 jit_solution(9637726340872701510)
XLA Ops:
  0.7 3.0 %fusion.92 = (bf16[1024,256]{1,0:T(8,128)(2,1)}, bf16[1024,256]{1,0:T(8,128)(2,1)}, bf16[1024,256]{1,0:T(8,128)(2,1)}, bf16[1024,256]{1,0:T(8,128)(2,1)}) fusion(bf16[4096,256]{1,0:T(8,128)(2,1)} %param.4), kind=kLoop, calls=%fused_computation.151 | loop fusion | bytes 4194304 | tf_op jit(solution)/shard_map/slice | solution.py:99
  3.7 3.0 %collective-permute-start = (bf16[1024,256]{1,0:T(8,128)(2,1)}, bf16[1024,256]{1,0:T(8,128)(2,1)}, u32[]{:S(2)}, u32[]{:S(2)}) collective-permute-start(bf16[1024,256]{1,0:T(8,128)(2,1)} %get-tuple-element.29), channel_id=1, source_target_pairs={{0,4},{1,5},{2,6},{3,7},{4,8},{5,9},{6,10},{7,11},{8,12},{9,13},{1... | collective-permute-start | bytes 1572872 | tf_op jit(solution)/shard_map/ppermute | solution.py:16
  6.7 2.0 collective-permute-start.1
  8.8 3.8 %collective-permute-start.5 = (bf16[1024,256]{1,0:T(8,128)(2,1)}, bf16[1024,256]{1,0:T(8,128)(2,1)}, u32[]{:S(2)}, u32[]{:S(2)}) collective-permute-start(bf16[1024,256]{1,0:T(8,128)(2,1)} %get-tuple-element.32), channel_id=1, source_target_pairs={{0,12},{1,13},{2,14},{3,15},{4,0},{5,1},{6,2},{7,3},{8,4},{9,5},{1... | collective-permute-start | bytes 1572872 | tf_op jit(solution)/shard_map/ppermute | solution.py:16
  12.6 1.8 fusion.66
  15.0 1.7 fusion.62
  17.3 4.6 %collective-permute-done = bf16[1024,256]{1,0:T(8,128)(2,1)} collective-permute-done((bf16[1024,256]{1,0:T(8,128)(2,1)}, bf16[1024,256]{1,0:T(8,128)(2,1)}, u32[]{:S(2)}, u32[]{:S(2)}) %collective-permute-start) | collective-permute-done | bytes 524320 | tf_op jit(solution)/shard_map/ppermute | solution.py:16
  21.9 13.2 %collective-permute-start.3 = (bf16[1024,256]{1,0:T(8,128)(2,1)}, bf16[1024,256]{1,0:T(8,128)(2,1)S(1)}, u32[]{:S(2)}, u32[]{:S(2)}) collective-permute-start(bf16[1024,256]{1,0:T(8,128)(2,1)} %get-tuple-element.30), channel_id=1, source_target_pairs={{0,12},{1,13},{2,14},{3,15},{4,0},{5,1},{6,2},{7,3},{8,4},{9,5},{1... | collective-permute-start | bytes 1572872 | tf_op jit(solution)/shard_map/ppermute | solution.py:16
  37.3 7.1 %collective-permute-done.4 = bf16[1024,256]{1,0:T(8,128)(2,1)} collective-permute-done((bf16[1024,256]{1,0:T(8,128)(2,1)}, bf16[1024,256]{1,0:T(8,128)(2,1)}, u32[]{:S(2)}, u32[]{:S(2)}) %collective-permute-start.4) | collective-permute-done | bytes 524320 | tf_op jit(solution)/shard_map/ppermute | solution.py:16
  44.4 13.2 %collective-permute-start.7 = (bf16[1024,256]{1,0:T(8,128)(2,1)S(1)}, bf16[1024,256]{1,0:T(8,128)(2,1)S(1)}, u32[]{:S(2)}, u32[]{:S(2)}) collective-permute-start(bf16[1024,256]{1,0:T(8,128)(2,1)S(1)} %copy-done.7), channel_id=1, source_target_pairs={{0,12},{1,13},{2,14},{3,15},{4,0},{5,1},{6,2},{7,3},{8,4},{9,5},{1... | collective-permute-start | bytes 1572872 | tf_op jit(solution)/shard_map/ppermute | solution.py:16
  62.7 4.2 %collective-permute-done.2 = bf16[1024,256]{1,0:T(8,128)(2,1)} collective-permute-done((bf16[1024,256]{1,0:T(8,128)(2,1)}, bf16[1024,256]{1,0:T(8,128)(2,1)}, u32[]{:S(2)}, u32[]{:S(2)}) %collective-permute-start.2) | collective-permute-done | bytes 524320 | tf_op jit(solution)/shard_map/ppermute | solution.py:16
  68.4 9.6 %collective-permute-done.3 = bf16[1024,256]{1,0:T(8,128)(2,1)S(1)} collective-permute-done((bf16[1024,256]{1,0:T(8,128)(2,1)}, bf16[1024,256]{1,0:T(8,128)(2,1)S(1)}, u32[]{:S(2)}, u32[]{:S(2)}) %collective-permute-start.3) | collective-permute-done | bytes 524320 | tf_op jit(solution)/shard_map/ppermute | solution.py:16
  78.6 10.7 %collective-permute-done.6 = bf16[1024,256]{1,0:T(8,128)(2,1)S(1)} collective-permute-done((bf16[1024,256]{1,0:T(8,128)(2,1)S(1)}, bf16[1024,256]{1,0:T(8,128)(2,1)S(1)}, u32[]{:S(2)}, u32[]{:S(2)}) %collective-permute-start.6) | collective-permute-done | bytes 524320 | tf_op jit(solution)/shard_map/ppermute | solution.py:16
  90.5 8.5 %collective-permute-done.7 = bf16[1024,256]{1,0:T(8,128)(2,1)S(1)} collective-permute-done((bf16[1024,256]{1,0:T(8,128)(2,1)S(1)}, bf16[1024,256]{1,0:T(8,128)(2,1)S(1)}, u32[]{:S(2)}, u32[]{:S(2)}) %collective-permute-start.7) | collective-permute-done | bytes 524320 | tf_op jit(solution)/shard_map/ppermute | solution.py:16
  114.3 2.4 collective-permute-start.10
  120.9 10.1 %collective-permute-done.9 = f32[114688]{0:T(1024)S(1)} collective-permute-done((f32[114688]{0:T(1024)S(1)}, f32[114688]{0:T(1024)S(1)}, u32[]{:S(2)}, u32[]{:S(2)}) %collective-permute-start.9) | collective-permute-done | bytes 458784 | tf_op jit(solution)/shard_map/ppermute | solution.py:22
  131.1 9.5 %collective-permute-done.11 = bf16[1024,256]{1,0:T(8,128)(2,1)S(1)} collective-permute-done((bf16[1024,256]{1,0:T(8,128)(2,1)S(1)}, bf16[1024,256]{1,0:T(8,128)(2,1)S(1)}, u32[]{:S(2)}, u32[]{:S(2)}) %collective-permute-start.11) | collective-permute-done | bytes 524320 | tf_op jit(solution)/shard_map/ppermute | solution.py:16
  140.6 1.7 collective-permute-start.12
  142.8 5.1 %collective-permute-done.12 = f32[57344]{0:T(1024)S(1)} collective-permute-done((f32[57344]{0:T(1024)S(1)}, f32[57344]{0:T(1024)S(1)}, u32[]{:S(2)}, u32[]{:S(2)}) %collective-permute-start.12) | collective-permute-done | bytes 229408 | tf_op jit(solution)/shard_map/ppermute | solution.py:22
  148.0 2.2 collective-permute-start.13
  150.7 1.9 collective-permute-start.14
  152.8 3.8 %collective-permute-done.13 = f32[28672]{0:T(1024)S(1)} collective-permute-done((f32[28672]{0:T(1024)S(1)}, f32[28672]{0:T(1024)S(1)}, u32[]{:S(2)}, u32[]{:S(2)}) %collective-permute-start.13) | collective-permute-done | bytes 114720 | tf_op jit(solution)/shard_map/ppermute | solution.py:22
  156.5 9.2 %collective-permute-done.14 = bf16[1024,256]{1,0:T(8,128)(2,1)S(1)} collective-permute-done((bf16[1024,256]{1,0:T(8,128)(2,1)S(1)}, bf16[1024,256]{1,0:T(8,128)(2,1)S(1)}, u32[]{:S(2)}, u32[]{:S(2)}) %collective-permute-start.14) | collective-permute-done | bytes 524320 | tf_op jit(solution)/shard_map/ppermute | solution.py:16
  165.8 10.7 %collective-permute-done.15 = bf16[1024,256]{1,0:T(8,128)(2,1)S(1)} collective-permute-done((bf16[1024,256]{1,0:T(8,128)(2,1)S(1)}, bf16[1024,256]{1,0:T(8,128)(2,1)S(1)}, u32[]{:S(2)}, u32[]{:S(2)}) %collective-permute-start.15) | collective-permute-done | bytes 524320 | tf_op jit(solution)/shard_map/ppermute | solution.py:16
  176.5 2.1 collective-permute-start.16
  179.2 2.1 collective-permute-start.18
  181.2 3.8 %collective-permute-start.20 = (bf16[1024,256]{1,0:T(8,128)(2,1)S(1)}, bf16[1024,256]{1,0:T(8,128)(2,1)S(1)}, u32[]{:S(2)}, u32[]{:S(2)}) collective-permute-start(bf16[1024,256]{1,0:T(8,128)(2,1)S(1)} %convolution_convert_fusion.1), channel_id=1, source_target_pairs={{0,12},{1,13},{2,14},{3,15},{4,0},{5,1},{6,2},{7,3},{8,4},{9,5},{1... | collective-permute-start | bytes 1572872 | tf_op jit(solution)/shard_map/ppermute | solution.py:16
  185.2 9.8 %collective-permute-start.17 = (f32[57344]{0:T(1024)S(1)}, f32[57344]{0:T(1024)S(1)}, u32[]{:S(2)}, u32[]{:S(2)}) collective-permute-start(f32[57344]{0:T(1024)S(1)} %pad_maximum_fusion.7), channel_id=1, source_target_pairs={{0,4},{1,5},{2,6},{3,7},{4,0},{5,1},{6,2},{7,3},{8,12},{9,13},{10,... | collective-permute-start | bytes 688136 | tf_op jit(solution)/shard_map/ppermute | solution.py:22
  195.5 36.0 %collective-permute-done.17 = f32[57344]{0:T(1024)S(1)} collective-permute-done((f32[57344]{0:T(1024)S(1)}, f32[57344]{0:T(1024)S(1)}, u32[]{:S(2)}, u32[]{:S(2)}) %collective-permute-start.17) | collective-permute-done | bytes 229408 | tf_op jit(solution)/shard_map/ppermute | solution.py:22
  234.2 8.1 %collective-permute-done.22 = f32[114688]{0:T(1024)S(1)} collective-permute-done((f32[114688]{0:T(1024)S(1)}, f32[114688]{0:T(1024)S(1)}, u32[]{:S(2)}, u32[]{:S(2)}) %collective-permute-start.22) | collective-permute-done | bytes 458784 | tf_op jit(solution)/shard_map/ppermute | solution.py:22
  242.5 2.0 fusion.2
  247.1 2.4 pad_maximum_fusion
  (103 shorter events, 38.7 us)
Async XLA Ops:
  0.6 58.5 %copy-start = (bf16[256,256]{1,0:T(8,128)(2,1)S(1)}, bf16[256,256]{1,0:T(8,128)(2,1)}, u32[]{:S(2)}) copy-start(bf16[256,256]{1,0:T(8,128)(2,1)} %param.7) | copy-start | bytes 393220
  0.6 11.9 %copy-start.4 = (bf16[4096,256]{1,0:T(8,128)(2,1)S(1)}, bf16[4096,256]{1,0:T(8,128)(2,1)}, u32[]{:S(2)}) copy-start(bf16[4096,256]{1,0:T(8,128)(2,1)} %param.4) | copy-start | bytes 6291460
  0.7 11.9 %copy-start.2 = (bf16[768,512]{1,0:T(8,128)(2,1)S(1)}, bf16[768,512]{1,0:T(8,128)(2,1)}, u32[]{:S(2)}) copy-start(bf16[768,512]{1,0:T(8,128)(2,1)} %param.6) | copy-start | bytes 2359300
  3.7 18.2 %collective-permute-start = (bf16[1024,256]{1,0:T(8,128)(2,1)}, bf16[1024,256]{1,0:T(8,128)(2,1)}, u32[]{:S(2)}, u32[]{:S(2)}) collective-permute-start(bf16[1024,256]{1,0:T(8,128)(2,1)} %get-tuple-element.29), channel_id=1, source_target_pairs={{0,4},{1,5},{2,6},{3,7},{4,8},{5,9},{6,10},{7,11},{8,12},{9,13},{1... | collective-permute-start | bytes 1572872 | tf_op jit(solution)/shard_map/ppermute | solution.py:16
  6.7 29.9 %collective-permute-start.1 = (bf16[1024,256]{1,0:T(8,128)(2,1)}, bf16[1024,256]{1,0:T(8,128)(2,1)S(1)}, u32[]{:S(2)}, u32[]{:S(2)}) collective-permute-start(bf16[1024,256]{1,0:T(8,128)(2,1)} %get-tuple-element.29), channel_id=1, source_target_pairs={{0,12},{1,13},{2,14},{3,15},{4,0},{5,1},{6,2},{7,3},{8,4},{9,5},{1... | collective-permute-start | bytes 1572872 | tf_op jit(solution)/shard_map/ppermute | solution.py:16
  8.8 35.6 %collective-permute-start.4 = (bf16[1024,256]{1,0:T(8,128)(2,1)}, bf16[1024,256]{1,0:T(8,128)(2,1)}, u32[]{:S(2)}, u32[]{:S(2)}) collective-permute-start(bf16[1024,256]{1,0:T(8,128)(2,1)} %get-tuple-element.32), channel_id=1, source_target_pairs={{0,4},{1,5},{2,6},{3,7},{4,8},{5,9},{6,10},{7,11},{8,12},{9,13},{1... | collective-permute-start | bytes 1572872 | tf_op jit(solution)/shard_map/ppermute | solution.py:16
  8.8 51.1 %collective-permute-start.5 = (bf16[1024,256]{1,0:T(8,128)(2,1)}, bf16[1024,256]{1,0:T(8,128)(2,1)}, u32[]{:S(2)}, u32[]{:S(2)}) collective-permute-start(bf16[1024,256]{1,0:T(8,128)(2,1)} %get-tuple-element.32), channel_id=1, source_target_pairs={{0,12},{1,13},{2,14},{3,15},{4,0},{5,1},{6,2},{7,3},{8,4},{9,5},{1... | collective-permute-start | bytes 1572872 | tf_op jit(solution)/shard_map/ppermute | solution.py:16
  12.6 54.3 %collective-permute-start.2 = (bf16[1024,256]{1,0:T(8,128)(2,1)}, bf16[1024,256]{1,0:T(8,128)(2,1)}, u32[]{:S(2)}, u32[]{:S(2)}) collective-permute-start(bf16[1024,256]{1,0:T(8,128)(2,1)} %get-tuple-element.30), channel_id=1, source_target_pairs={{0,4},{1,5},{2,6},{3,7},{4,8},{5,9},{6,10},{7,11},{8,12},{9,13},{1... | collective-permute-start | bytes 1572872 | tf_op jit(solution)/shard_map/ppermute | solution.py:16
  15.0 1.8 copy-start.5
  17.3 19.4 %copy-start.7 = (bf16[1024,256]{1,0:T(8,128)(2,1)S(1)}, bf16[1024,256]{1,0:T(8,128)(2,1)}, u32[]{:S(2)}) copy-start(bf16[1024,256]{1,0:T(8,128)(2,1)} %get-tuple-element.31) | copy-start | bytes 1572868
  17.3 19.5 %copy-start.3 = (f32[1024,512]{0,1:T(8,128)S(1)}, f32[1024,512]{0,1:T(8,128)}, u32[]{:S(2)}) copy-start(f32[1024,512]{0,1:T(8,128)} %fusion.66) | copy-start | bytes 6291460
  21.9 56.2 %collective-permute-start.3 = (bf16[1024,256]{1,0:T(8,128)(2,1)}, bf16[1024,256]{1,0:T(8,128)(2,1)S(1)}, u32[]{:S(2)}, u32[]{:S(2)}) collective-permute-start(bf16[1024,256]{1,0:T(8,128)(2,1)} %get-tuple-element.30), channel_id=1, source_target_pairs={{0,12},{1,13},{2,14},{3,15},{4,0},{5,1},{6,2},{7,3},{8,4},{9,5},{1... | collective-permute-start | bytes 1572872 | tf_op jit(solution)/shard_map/ppermute | solution.py:16
  36.7 52.6 %collective-permute-start.6 = (bf16[1024,256]{1,0:T(8,128)(2,1)S(1)}, bf16[1024,256]{1,0:T(8,128)(2,1)S(1)}, u32[]{:S(2)}, u32[]{:S(2)}) collective-permute-start(bf16[1024,256]{1,0:T(8,128)(2,1)S(1)} %copy-done.7), channel_id=1, source_target_pairs={{0,4},{1,5},{2,6},{3,7},{4,8},{5,9},{6,10},{7,11},{8,12},{9,13},{1... | collective-permute-start | bytes 1572872 | tf_op jit(solution)/shard_map/ppermute | solution.py:16
  37.2 21.9 %copy-start.6 = (bf16[4096,256]{1,0:T(8,128)(2,1)S(1)}, bf16[4096,256]{1,0:T(8,128)(2,1)}, u32[]{:S(2)}) copy-start(bf16[4096,256]{1,0:T(8,128)(2,1)} %param.5) | copy-start | bytes 6291460
  44.4 54.6 %collective-permute-start.7 = (bf16[1024,256]{1,0:T(8,128)(2,1)S(1)}, bf16[1024,256]{1,0:T(8,128)(2,1)S(1)}, u32[]{:S(2)}, u32[]{:S(2)}) collective-permute-start(bf16[1024,256]{1,0:T(8,128)(2,1)S(1)} %copy-done.7), channel_id=1, source_target_pairs={{0,12},{1,13},{2,14},{3,15},{4,0},{5,1},{6,2},{7,3},{8,4},{9,5},{1... | collective-permute-start | bytes 1572872 | tf_op jit(solution)/shard_map/ppermute | solution.py:16
  113.7 4.5 %collective-permute-start.8 = (f32[229376]{0:T(1024)S(1)}, f32[229376]{0:T(1024)S(1)}, u32[]{:S(2)}, u32[]{:S(2)}) collective-permute-start(f32[229376]{0:T(1024)S(1)} %dynamic_slice.25), channel_id=1, source_target_pairs={{0,1},{1,0},{2,3},{3,2},{4,5},{5,4},{6,7},{7,6},{8,9},{9,8},{10,11... | collective-permute-start | bytes 2752520 | tf_op jit(solution)/shard_map/ppermute | solution.py:22
  114.3 16.9 %collective-permute-start.10 = (bf16[1024,256]{1,0:T(8,128)(2,1)S(1)}, bf16[1024,256]{1,0:T(8,128)(2,1)S(1)}, u32[]{:S(2)}, u32[]{:S(2)}) collective-permute-start(bf16[1024,256]{1,0:T(8,128)(2,1)S(1)} %convolution_convert_fusion.7), channel_id=1, source_target_pairs={{0,12},{1,13},{2,14},{3,15},{4,0},{5,1},{6,2},{7,3},{8,4},{9,5},{1... | collective-permute-start | bytes 1572872 | tf_op jit(solution)/shard_map/ppermute | solution.py:16
  117.1 23.5 %collective-permute-start.11 = (bf16[1024,256]{1,0:T(8,128)(2,1)S(1)}, bf16[1024,256]{1,0:T(8,128)(2,1)S(1)}, u32[]{:S(2)}, u32[]{:S(2)}) collective-permute-start(bf16[1024,256]{1,0:T(8,128)(2,1)S(1)} %convolution_convert_fusion.6), channel_id=1, source_target_pairs={{0,4},{1,5},{2,6},{3,7},{4,8},{5,9},{6,10},{7,11},{8,12},{9,13},{1... | collective-permute-start | bytes 1572872 | tf_op jit(solution)/shard_map/ppermute | solution.py:16
  118.4 12.7 %collective-permute-start.9 = (f32[114688]{0:T(1024)S(1)}, f32[114688]{0:T(1024)S(1)}, u32[]{:S(2)}, u32[]{:S(2)}) collective-permute-start(f32[114688]{0:T(1024)S(1)} %dynamic_slice.27), channel_id=1, source_target_pairs={{0,2},{1,3},{2,0},{3,1},{4,6},{5,7},{6,4},{7,5},{8,10},{9,11},{10,... | collective-permute-start | bytes 1376264 | tf_op jit(solution)/shard_map/ppermute | solution.py:22
  140.6 7.3 %collective-permute-start.12 = (f32[57344]{0:T(1024)S(1)}, f32[57344]{0:T(1024)S(1)}, u32[]{:S(2)}, u32[]{:S(2)}) collective-permute-start(f32[57344]{0:T(1024)S(1)} %dynamic_slice.29), channel_id=1, source_target_pairs={{0,4},{1,5},{2,6},{3,7},{4,0},{5,1},{6,2},{7,3},{8,12},{9,13},{10,... | collective-permute-start | bytes 688136 | tf_op jit(solution)/shard_map/ppermute | solution.py:22
  148.0 8.5 %collective-permute-start.13 = (f32[28672]{0:T(1024)S(1)}, f32[28672]{0:T(1024)S(1)}, u32[]{:S(2)}, u32[]{:S(2)}) collective-permute-start(f32[28672]{0:T(1024)S(1)} %dynamic_slice.31), channel_id=1, source_target_pairs={{0,8},{1,9},{2,10},{3,11},{4,12},{5,13},{6,14},{7,15},{8,0},{9,1},... | collective-permute-start | bytes 344072 | tf_op jit(solution)/shard_map/ppermute | solution.py:22
  150.7 15.1 %collective-permute-start.14 = (bf16[1024,256]{1,0:T(8,128)(2,1)S(1)}, bf16[1024,256]{1,0:T(8,128)(2,1)S(1)}, u32[]{:S(2)}, u32[]{:S(2)}) collective-permute-start(bf16[1024,256]{1,0:T(8,128)(2,1)S(1)} %convolution_convert_fusion.5), channel_id=1, source_target_pairs={{0,12},{1,13},{2,14},{3,15},{4,0},{5,1},{6,2},{7,3},{8,4},{9,5},{1... | collective-permute-start | bytes 1572872 | tf_op jit(solution)/shard_map/ppermute | solution.py:16
  152.6 23.9 %collective-permute-start.15 = (bf16[1024,256]{1,0:T(8,128)(2,1)S(1)}, bf16[1024,256]{1,0:T(8,128)(2,1)S(1)}, u32[]{:S(2)}, u32[]{:S(2)}) collective-permute-start(bf16[1024,256]{1,0:T(8,128)(2,1)S(1)} %convolution_convert_fusion.4), channel_id=1, source_target_pairs={{0,4},{1,5},{2,6},{3,7},{4,8},{5,9},{6,10},{7,11},{8,12},{9,13},{1... | collective-permute-start | bytes 1572872 | tf_op jit(solution)/shard_map/ppermute | solution.py:16
  176.5 8.7 %collective-permute-start.16 = (f32[28672]{0:T(1024)S(1)}, f32[28672]{0:T(1024)S(1)}, u32[]{:S(2)}, u32[]{:S(2)}) collective-permute-start(f32[28672]{0:T(1024)S(1)} %add_multiply_fusion), channel_id=1, source_target_pairs={{0,8},{1,9},{2,10},{3,11},{4,12},{5,13},{6,14},{7,15},{8,0},{9,1},... | collective-permute-start | bytes 344072 | tf_op jit(solution)/shard_map/ppermute | solution.py:22
  179.2 52.4 %collective-permute-start.18 = (bf16[1024,256]{1,0:T(8,128)(2,1)S(1)}, bf16[1024,256]{1,0:T(8,128)(2,1)S(1)}, u32[]{:S(2)}, u32[]{:S(2)}) collective-permute-start(bf16[1024,256]{1,0:T(8,128)(2,1)S(1)} %convolution_convert_fusion.3), channel_id=1, source_target_pairs={{0,12},{1,13},{2,14},{3,15},{4,0},{5,1},{6,2},{7,3},{8,4},{9,5},{1... | collective-permute-start | bytes 1572872 | tf_op jit(solution)/shard_map/ppermute | solution.py:16
  181.2 50.3 %collective-permute-start.19 = (bf16[1024,256]{1,0:T(8,128)(2,1)S(1)}, bf16[1024,256]{1,0:T(8,128)(2,1)S(1)}, u32[]{:S(2)}, u32[]{:S(2)}) collective-permute-start(bf16[1024,256]{1,0:T(8,128)(2,1)S(1)} %convolution_convert_fusion.2), channel_id=1, source_target_pairs={{0,4},{1,5},{2,6},{3,7},{4,8},{5,9},{6,10},{7,11},{8,12},{9,13},{1... | collective-permute-start | bytes 1572872 | tf_op jit(solution)/shard_map/ppermute | solution.py:16
  181.2 61.3 %collective-permute-start.20 = (bf16[1024,256]{1,0:T(8,128)(2,1)S(1)}, bf16[1024,256]{1,0:T(8,128)(2,1)S(1)}, u32[]{:S(2)}, u32[]{:S(2)}) collective-permute-start(bf16[1024,256]{1,0:T(8,128)(2,1)S(1)} %convolution_convert_fusion.1), channel_id=1, source_target_pairs={{0,12},{1,13},{2,14},{3,15},{4,0},{5,1},{6,2},{7,3},{8,4},{9,5},{1... | collective-permute-start | bytes 1572872 | tf_op jit(solution)/shard_map/ppermute | solution.py:16
  185.1 57.5 %collective-permute-start.21 = (bf16[1024,256]{1,0:T(8,128)(2,1)S(1)}, bf16[1024,256]{1,0:T(8,128)(2,1)S(1)}, u32[]{:S(2)}, u32[]{:S(2)}) collective-permute-start(bf16[1024,256]{1,0:T(8,128)(2,1)S(1)} %convolution_convert_fusion), channel_id=1, source_target_pairs={{0,4},{1,5},{2,6},{3,7},{4,8},{5,9},{6,10},{7,11},{8,12},{9,13},{1... | collective-permute-start | bytes 1572872 | tf_op jit(solution)/shard_map/ppermute | solution.py:16
  185.2 46.2 %collective-permute-start.17 = (f32[57344]{0:T(1024)S(1)}, f32[57344]{0:T(1024)S(1)}, u32[]{:S(2)}, u32[]{:S(2)}) collective-permute-start(f32[57344]{0:T(1024)S(1)} %pad_maximum_fusion.7), channel_id=1, source_target_pairs={{0,4},{1,5},{2,6},{3,7},{4,0},{5,1},{6,2},{7,3},{8,12},{9,13},{10,... | collective-permute-start | bytes 688136 | tf_op jit(solution)/shard_map/ppermute | solution.py:22
  231.6 10.7 %collective-permute-start.22 = (f32[114688]{0:T(1024)S(1)}, f32[114688]{0:T(1024)S(1)}, u32[]{:S(2)}, u32[]{:S(2)}) collective-permute-start(f32[114688]{0:T(1024)S(1)} %pad_maximum_fusion.6), channel_id=1, source_target_pairs={{0,2},{1,3},{2,0},{3,1},{4,6},{5,7},{6,4},{7,5},{8,10},{9,11},{10,... | collective-permute-start | bytes 1376264 | tf_op jit(solution)/shard_map/ppermute | solution.py:22
  242.4 2.5 %collective-permute-start.23 = (f32[229376]{0:T(1024)S(1)}, f32[229376]{0:T(1024)S(1)}, u32[]{:S(2)}, u32[]{:S(2)}) collective-permute-start(f32[229376]{0:T(1024)S(1)} %pad_maximum_fusion.5), channel_id=1, source_target_pairs={{0,1},{1,0},{2,3},{3,2},{4,5},{5,4},{6,7},{7,6},{8,9},{9,8},{10,11... | collective-permute-start | bytes 2752520 | tf_op jit(solution)/shard_map/ppermute | solution.py:22
  245.3 4.3 %copy-start.1 = (bf16[256,256]{1,0:T(8,128)(2,1)S(1)}, bf16[256,256]{1,0:T(8,128)(2,1)}, u32[]{:S(2)}) copy-start(bf16[256,256]{1,0:T(8,128)(2,1)} %param.7) | copy-start | bytes 393220

commit v3 on v1

--- a/solution.py
+++ b/solution.py
@@ -6,7 +6,8 @@
 from jax.sharding import PartitionSpec as P
 
 TAP_SPACING = 16384
-CHUNKS = 4
+CHUNK_EIGHTHS = (2, 2, 2, 1, 1)
+EARLY = 1
 
 
 def from_behind(value, axis, steps):
@@ -21,29 +22,27 @@
     return lax.ppermute(value, axis, pairs)
 
 
-def all_reduce_sum(flat, axis, scale):
-    count = lax.axis_size(axis)
-    idx = lax.axis_index(axis)
+def chain_steps(count):
     bits = []
     bit = 1
     while bit < count:
         bits.append(bit)
         bit *= 2
-    buf = flat
-    for bit in bits:
+    return [(bit, True) for bit in bits] + [(bit, False) for bit in reversed(bits)]
+
+
+def chain_step(buf, axis, bit, down):
+    idx = lax.axis_index(axis)
+    upper = (idx // bit) % 2
+    if down:
         half = buf.shape[0] // 2
-        upper = (idx // bit) % 2
         mine = lax.dynamic_slice_in_dim(buf, upper * half, half)
         theirs = lax.dynamic_slice_in_dim(buf, (1 - upper) * half, half)
-        buf = mine + exchange(theirs, axis, bit)
-    buf = buf * scale
-    for bit in reversed(bits):
-        upper = (idx // bit) % 2
-        other = exchange(buf, axis, bit)
-        lo = jnp.where(upper == 1, other, buf)
-        hi = jnp.where(upper == 1, buf, other)
-        buf = jnp.concatenate([lo, hi])
-    return buf
+        return mine + exchange(theirs, axis, bit)
+    other = exchange(buf, axis, bit)
+    lo = jnp.where(upper == 1, other, buf)
+    hi = jnp.where(upper == 1, buf, other)
+    return jnp.concatenate([lo, hi])
 
 
 def chunk_layer(left_tap_input, middle, right_tap_input, grad_in, conv_weight, out_weight):
@@ -82,32 +81,66 @@
     positions, channels = activations.shape
     seq_size = lax.axis_size("seq")
     spacing = TAP_SPACING // positions
-    rows = positions // CHUNKS
+    bounds = [0]
+    for eighths in CHUNK_EIGHTHS:
+        bounds.append(bounds[-1] + positions * eighths // 8)
+    chunks = len(CHUNK_EIGHTHS)
     wconv_total = None
     wout_total = None
-    outs = []
-    for k in range(CHUNKS):
-        middle = activations[k * rows : (k + 1) * rows]
-        grad_in = cotangent[k * rows : (k + 1) * rows]
+    lows, mids, highs = [], [], []
+    early = []
+    for k in range(chunks):
+        middle = activations[bounds[k] : bounds[k + 1]]
+        grad_in = cotangent[bounds[k] : bounds[k + 1]]
         left_tap_input = from_behind(middle, "seq", spacing)
         right_tap_input = from_behind(middle, "seq", -spacing)
+        if k == chunks - 1:
+            left_tap_input, right_tap_input, lows_early, highs_early = lax.optimization_barrier(
+                (left_tap_input, right_tap_input, lows[:EARLY], highs[:EARLY])
+            )
+            for low, high in zip(lows_early, highs_early):
+                early.append((from_behind(low, "seq", -spacing), from_behind(high, "seq", spacing)))
         grad_wconv, grad_wout, lower_term, term_mid, upper_term = chunk_layer(
             left_tap_input, middle, right_tap_input, grad_in, conv_weight, out_weight
         )
         wconv_total = grad_wconv if wconv_total is None else wconv_total + grad_wconv
         wout_total = grad_wout if wout_total is None else wout_total + grad_wout
-        received_ahead = from_behind(lower_term, "seq", -spacing)
-        received_behind = from_behind(upper_term, "seq", spacing)
-        total_sum = grad_in.astype(jnp.float32) + term_mid
-        total_sum = total_sum + received_ahead.astype(jnp.float32) + received_behind.astype(jnp.float32)
-        outs.append(total_sum.astype(jnp.bfloat16))
-    grad_input = jnp.concatenate(outs, axis=0)
+        lows.append(lower_term)
+        mids.append(term_mid)
+        highs.append(upper_term)
     norm_factor = 1.0 / math.sqrt(positions * seq_size)
-    flat = jnp.concatenate([wconv_total.reshape(-1), wout_total.reshape(-1)])
-    summed = all_reduce_sum(flat, "seq", jnp.float32(norm_factor))
+    buf = jnp.concatenate([wconv_total.reshape(-1), wout_total.reshape(-1)])
+    steps = chain_steps(seq_size)
+    late = []
+    sent_late = False
+    for number, (bit, down) in enumerate(steps):
+        if down and bit == 4:
+            buf, early = lax.optimization_barrier((buf, early))
+        if not down and bit == 2:
+            rest_low = jnp.concatenate(lows[EARLY:], axis=0)
+            rest_high = jnp.concatenate(highs[EARLY:], axis=0)
+            buf, rest_low, rest_high = lax.optimization_barrier((buf, rest_low, rest_high))
+            late.append((from_behind(rest_low, "seq", -spacing), from_behind(rest_high, "seq", spacing)))
+            sent_late = True
+        if not down and bit == 1 and late:
+            buf, late = lax.optimization_barrier((buf, late))
+        buf = chain_step(buf, "seq", bit, down)
+        if down and number == len(steps) // 2 - 1:
+            buf = buf * jnp.float32(norm_factor)
+    if not steps:
+        buf = buf * jnp.float32(norm_factor)
+    if not sent_late:
+        for low, high in zip(lows[EARLY:], highs[EARLY:]):
+            late.append((from_behind(low, "seq", -spacing), from_behind(high, "seq", spacing)))
+    received = early + late
+    received_ahead = jnp.concatenate([pair[0] for pair in received], axis=0)
+    received_behind = jnp.concatenate([pair[1] for pair in received], axis=0)
+    total_sum = cotangent.astype(jnp.float32) + jnp.concatenate(mids, axis=0)
+    total_sum = total_sum + received_ahead.astype(jnp.float32) + received_behind.astype(jnp.float32)
+    grad_input = total_sum.astype(jnp.bfloat16)
     split = wconv_total.size
-    grad_conv = summed[:split].reshape(wconv_total.shape)
-    grad_out = summed[split:].reshape(wout_total.shape)
+    grad_conv = buf[:split].reshape(wconv_total.shape)
+    grad_out = buf[split:].reshape(wout_total.shape)
     return grad_input, grad_conv, grad_out
 
 

time: 258 us -> 237 us (0.919)
  waiting for transfers between devices: 165 us -> 145 us
  starting transfers between devices: 40.6 us -> 36.3 us
  local copies, waits for them, and re-layouts: 6.91 us -> 9.52 us
    ppermute x8, waiting for transfers between devices: 68.1 us -> 30.2 us  [exchange(): return lax.ppermute(value, axis, pairs)]
    ppermute x16 -> x14, waiting for transfers between devices: 96.4 us -> 115 us  [from_behind(): return lax.ppermute(value, axis, pairs)]
    ppermute x16 -> x14, starting transfers between devices: 32.3 us -> 27.2 us  [from_behind(): return lax.ppermute(value, axis, pairs)]
    dot_general x4 -> x5, matrix products: 6.51 us -> 8.98 us  [chunk_layer(): preact = preact + jnp.dot(middle, w_mid, preferred_element_type=jnp.float32)]
    slice x3 -> x4, local copies, waits for them, and re-layouts: 3.74 us -> 5.26 us  [the longest x2 4.46 us: body(): middle = activations[bounds[k]:bounds[k + 1]]]
  transfers between devices with their start and end apart: 24 -> 22, of which waited for: 13 -> 14; matrix products, arithmetic and copies ran while one was open for 10% -> 18% of each run, Pallas kernels for 0% -> 0%
where the time goes in v3:
time: 237 us
  waiting for transfers between devices  145 us (61%)
  matrix products  37.5 us (16%)
  starting transfers between devices  36.3 us (15%)
  local copies, waits for them, and re-layouts  9.52 us (4%)
  other arithmetic  6.79 us (3%)
    ppermute x14, waiting for transfers between devices, from_behind(): return lax.ppermute(value, axis, pairs)  115 us
    ppermute x8, waiting for transfers between devices, exchange(): return lax.ppermute(value, axis, pairs)  30.2 us
    ppermute x14, starting transfers between devices, from_behind(): return lax.ppermute(value, axis, pairs)  27.2 us
    ppermute x8, starting transfers between devices, exchange(): return lax.ppermute(value, axis, pairs)  9.02 us
    dot_general x5, matrix products, chunk_layer(): preact = preact + jnp.dot(middle, w_mid, preferred_element_type=jnp.float32)  8.98 us
    dot_general x5, matrix products, chunk_layer(): jnp.dot(right_tap_input, w_high, preferred_element_type=jnp.float32)  5.13 us
    dot_general x5, matrix products, chunk_layer(): lax.dot_general(right_tap_input, grad_pre, first_dims, preferred_element_...  5.09 us
  transfers between devices with their start and end apart: 22, of which 14 were waited for; matrix products, arithmetic and copies ran while one was open for 18% of the time, Pallas kernels for 0%

profile of v3, /device:TPU:0, one launch (start us, length us, event | category | flops | bytes accessed | tf_op | source)
XLA Modules:
  0.0 236.6 jit_solution(17120211175905570896)
XLA Ops:
  0.7 1.9 fusion.104
  2.6 5.0 %collective-permute-start.9 = (bf16[512,256]{1,0:T(8,128)(2,1)}, bf16[512,256]{1,0:T(8,128)(2,1)}, u32[]{:S(2)}, u32[]{:S(2)}) collective-permute-start(bf16[512,256]{1,0:T(8,128)(2,1)} %get-tuple-element.35), channel_id=1, source_target_pairs={{0,12},{1,13},{2,14},{3,15},{4,0},{5,1},{6,2},{7,3},{8,4},{9,5},{1... | collective-permute-start | bytes 786440 | tf_op jit(solution)/shard_map/ppermute | solution.py:16
  7.6 3.8 %collective-permute-start.7 = (bf16[512,256]{1,0:T(8,128)(2,1)}, bf16[512,256]{1,0:T(8,128)(2,1)}, u32[]{:S(2)}, u32[]{:S(2)}) collective-permute-start(bf16[512,256]{1,0:T(8,128)(2,1)} %get-tuple-element.36), channel_id=1, source_target_pairs={{0,12},{1,13},{2,14},{3,15},{4,0},{5,1},{6,2},{7,3},{8,4},{9,5},{1... | collective-permute-start | bytes 786440 | tf_op jit(solution)/shard_map/ppermute | solution.py:16
  11.5 2.5 %fusion.105 = (bf16[1024,256]{1,0:T(8,128)(2,1)}, bf16[1024,256]{1,0:T(8,128)(2,1)}, bf16[1024,256]{1,0:T(8,128)(2,1)}) fusion(bf16[4096,256]{1,0:T(8,128)(2,1)} %param.4), kind=kLoop, calls=%fused_computation.183 | loop fusion | bytes 3145728 | tf_op jit(solution)/shard_map/slice | solution.py:93
  14.0 3.8 %collective-permute-start.1 = (bf16[1024,256]{1,0:T(8,128)(2,1)}, bf16[1024,256]{1,0:T(8,128)(2,1)}, u32[]{:S(2)}, u32[]{:S(2)}) collective-permute-start(bf16[1024,256]{1,0:T(8,128)(2,1)} %get-tuple-element.39), channel_id=1, source_target_pairs={{0,12},{1,13},{2,14},{3,15},{4,0},{5,1},{6,2},{7,3},{8,4},{9,5},{1... | collective-permute-start | bytes 1572872 | tf_op jit(solution)/shard_map/ppermute | solution.py:16
  17.8 2.4 %fusion.63 = f32[512,512]{0,1:T(8,128)} fusion(bf16[768,512]{1,0:T(8,128)(2,1)S(1)} %copy-done.2, bf16[4096,256]{1,0:T(8,128)(2,1)} %param.4), kind=kOutput, calls=%fused_computation.146 | convolution fusion | flops 134217728 | bytes 1572864 | tf_op jit(solution)/shard_map/dot_general | solution.py:54
  20.2 2.9 %fusion.66 = f32[1024,512]{0,1:T(8,128)} fusion(bf16[768,512]{1,0:T(8,128)(2,1)S(1)} %copy-done.2, bf16[4096,256]{1,0:T(8,128)(2,1)} %param.4), kind=kOutput, calls=%fused_computation.149 | convolution fusion | flops 268435456 | bytes 2883584 | tf_op jit(solution)/shard_map/dot_general | solution.py:54
  23.6 1.8 fusion.72
  28.8 3.6 %collective-permute-done.6 = bf16[512,256]{1,0:T(8,128)(2,1)S(1)} collective-permute-done((bf16[512,256]{1,0:T(8,128)(2,1)}, bf16[512,256]{1,0:T(8,128)(2,1)S(1)}, u32[]{:S(2)}, u32[]{:S(2)}) %collective-permute-start.6) | collective-permute-done | bytes 262176 | tf_op jit(solution)/shard_map/ppermute | solution.py:16
  32.4 2.8 %collective-permute-start.5 = (bf16[1024,256]{1,0:T(8,128)(2,1)S(1)}, bf16[1024,256]{1,0:T(8,128)(2,1)S(1)}, u32[]{:S(2)}, u32[]{:S(2)}) collective-permute-start(bf16[1024,256]{1,0:T(8,128)(2,1)S(1)} %copy-done.10), channel_id=1, source_target_pairs={{0,12},{1,13},{2,14},{3,15},{4,0},{5,1},{6,2},{7,3},{8,4},{9,5},{1... | collective-permute-start | bytes 1572872 | tf_op jit(solution)/shard_map/ppermute | solution.py:16
  39.9 15.0 %collective-permute-done = bf16[1024,256]{1,0:T(8,128)(2,1)S(1)} collective-permute-done((bf16[1024,256]{1,0:T(8,128)(2,1)}, bf16[1024,256]{1,0:T(8,128)(2,1)S(1)}, u32[]{:S(2)}, u32[]{:S(2)}) %collective-permute-start) | collective-permute-done | bytes 524320 | tf_op jit(solution)/shard_map/ppermute | solution.py:16
  54.9 1.5 collective-permute-start.4
  57.0 2.3 collective-permute-start.3
  59.3 1.5 add_add_fusion.2
  65.8 33.0 %collective-permute-done.2 = bf16[1024,256]{1,0:T(8,128)(2,1)S(1)} collective-permute-done((bf16[1024,256]{1,0:T(8,128)(2,1)S(1)}, bf16[1024,256]{1,0:T(8,128)(2,1)S(1)}, u32[]{:S(2)}, u32[]{:S(2)}) %collective-permute-start.2) | collective-permute-done | bytes 524320 | tf_op jit(solution)/shard_map/ppermute | solution.py:16
  106.9 2.6 %collective-permute-start.12 = (bf16[1024,256]{1,0:T(8,128)(2,1)S(1)}, bf16[1024,256]{1,0:T(8,128)(2,1)S(1)}, u32[]{:S(2)}, u32[]{:S(2)}) collective-permute-start(bf16[1024,256]{1,0:T(8,128)(2,1)S(1)} %convolution_convert_fusion.5), channel_id=1, source_target_pairs={{0,12},{1,13},{2,14},{3,15},{4,0},{5,1},{6,2},{7,3},{8,4},{9,5},{1... | collective-permute-start | bytes 1572872 | tf_op jit(solution)/shard_map/ppermute | solution.py:16
  113.4 1.5 convolution_bitcast_fusion.10
  119.3 1.6 collective-permute-start.11
  121.7 10.2 %collective-permute-done.11 = f32[114688]{0:T(1024)S(1)} collective-permute-done((f32[114688]{0:T(1024)S(1)}, f32[114688]{0:T(1024)S(1)}, u32[]{:S(2)}, u32[]{:S(2)}) %collective-permute-start.11) | collective-permute-done | bytes 458784 | tf_op jit(solution)/shard_map/ppermute | solution.py:22
  134.3 5.1 %collective-permute-done.14 = f32[57344]{0:T(1024)S(1)} collective-permute-done((f32[57344]{0:T(1024)S(1)}, f32[57344]{0:T(1024)S(1)}, u32[]{:S(2)}, u32[]{:S(2)}) %collective-permute-start.14) | collective-permute-done | bytes 229408 | tf_op jit(solution)/shard_map/ppermute | solution.py:22
  139.5 2.2 collective-permute-start.15
  142.2 4.3 %collective-permute-done.15 = f32[28672]{0:T(1024)S(1)} collective-permute-done((f32[28672]{0:T(1024)S(1)}, f32[28672]{0:T(1024)S(1)}, u32[]{:S(2)}, u32[]{:S(2)}) %collective-permute-start.15) | collective-permute-done | bytes 114720 | tf_op jit(solution)/shard_map/ppermute | solution.py:22
  148.1 4.3 %collective-permute-done.16 = f32[28672]{0:T(1024)S(1)} collective-permute-done((f32[28672]{0:T(1024)S(1)}, f32[28672]{0:T(1024)S(1)}, u32[]{:S(2)}, u32[]{:S(2)}) %collective-permute-start.16) | collective-permute-done | bytes 114720 | tf_op jit(solution)/shard_map/ppermute | solution.py:22
  152.4 2.0 collective-permute-start.17
  154.9 3.6 %collective-permute-done.17 = f32[57344]{0:T(1024)S(1)} collective-permute-done((f32[57344]{0:T(1024)S(1)}, f32[57344]{0:T(1024)S(1)}, u32[]{:S(2)}, u32[]{:S(2)}) %collective-permute-start.17) | collective-permute-done | bytes 229408 | tf_op jit(solution)/shard_map/ppermute | solution.py:22
  158.6 1.6 collective-permute-start.18
  160.9 4.4 %collective-permute-start.19 = (bf16[3072,256]{1,0:T(8,128)(2,1)S(1)}, bf16[3072,256]{1,0:T(8,128)(2,1)S(1)}, u32[]{:S(2)}, u32[]{:S(2)}) collective-permute-start(bf16[3072,256]{1,0:T(8,128)(2,1)S(1)} %get-tuple-element.23), channel_id=1, source_target_pairs={{0,12},{1,13},{2,14},{3,15},{4,0},{5,1},{6,2},{7,3},{8,4},{9,5},{1... | collective-permute-start | bytes 4718600 | tf_op jit(solution)/shard_map/ppermute | solution.py:16
  165.2 1.9 collective-permute-done.18
  167.3 32.8 %collective-permute-done.19 = bf16[3072,256]{1,0:T(8,128)(2,1)S(1)} collective-permute-done((bf16[3072,256]{1,0:T(8,128)(2,1)S(1)}, bf16[3072,256]{1,0:T(8,128)(2,1)S(1)}, u32[]{:S(2)}, u32[]{:S(2)}) %collective-permute-start.19) | collective-permute-done | bytes 1572896 | tf_op jit(solution)/shard_map/ppermute | solution.py:16
  200.1 29.4 %collective-permute-done.20 = bf16[3072,256]{1,0:T(8,128)(2,1)S(1)} collective-permute-done((bf16[3072,256]{1,0:T(8,128)(2,1)S(1)}, bf16[3072,256]{1,0:T(8,128)(2,1)S(1)}, u32[]{:S(2)}, u32[]{:S(2)}) %collective-permute-start.20) | collective-permute-done | bytes 1572896 | tf_op jit(solution)/shard_map/ppermute | solution.py:16
  229.5 2.2 add_convert_fusion
  234.2 2.4 %pad_maximum_fusion = f32[768,512]{1,0:T(8,128)} fusion(f32[448,512]{1,0:T(8,128)S(1)} %concatenate.90, f32[448,512]{1,0:T(8,128)} %concatenate.89), kind=kLoop, calls=%fused_computation.4 | loop fusion | flops 393216 | bytes 3407872 | tf_op jit(solution)/shard_map/concatenate | solution.py:45
  (118 shorter events, 39.1 us)
Async XLA Ops:
  0.6 34.9 %copy-start = (bf16[256,256]{1,0:T(8,128)(2,1)S(1)}, bf16[256,256]{1,0:T(8,128)(2,1)}, u32[]{:S(2)}) copy-start(bf16[256,256]{1,0:T(8,128)(2,1)} %param.7) | copy-start | bytes 393220
  0.6 17.2 %copy-start.2 = (bf16[768,512]{1,0:T(8,128)(2,1)S(1)}, bf16[768,512]{1,0:T(8,128)(2,1)}, u32[]{:S(2)}) copy-start(bf16[768,512]{1,0:T(8,128)(2,1)} %param.6) | copy-start | bytes 2359300
  2.6 60.0 %collective-permute-start.9 = (bf16[512,256]{1,0:T(8,128)(2,1)}, bf16[512,256]{1,0:T(8,128)(2,1)}, u32[]{:S(2)}, u32[]{:S(2)}) collective-permute-start(bf16[512,256]{1,0:T(8,128)(2,1)} %get-tuple-element.35), channel_id=1, source_target_pairs={{0,12},{1,13},{2,14},{3,15},{4,0},{5,1},{6,2},{7,3},{8,4},{9,5},{1... | collective-permute-start | bytes 786440 | tf_op jit(solution)/shard_map/ppermute | solution.py:16
  7.6 55.2 %collective-permute-start.8 = (bf16[512,256]{1,0:T(8,128)(2,1)}, bf16[512,256]{1,0:T(8,128)(2,1)S(1)}, u32[]{:S(2)}, u32[]{:S(2)}) collective-permute-start(bf16[512,256]{1,0:T(8,128)(2,1)} %get-tuple-element.35), channel_id=1, source_target_pairs={{0,4},{1,5},{2,6},{3,7},{4,8},{5,9},{6,10},{7,11},{8,12},{9,13},{1... | collective-permute-start | bytes 786440 | tf_op jit(solution)/shard_map/ppermute | solution.py:16
  7.6 19.2 %collective-permute-start.7 = (bf16[512,256]{1,0:T(8,128)(2,1)}, bf16[512,256]{1,0:T(8,128)(2,1)}, u32[]{:S(2)}, u32[]{:S(2)}) collective-permute-start(bf16[512,256]{1,0:T(8,128)(2,1)} %get-tuple-element.36), channel_id=1, source_target_pairs={{0,12},{1,13},{2,14},{3,15},{4,0},{5,1},{6,2},{7,3},{8,4},{9,5},{1... | collective-permute-start | bytes 786440 | tf_op jit(solution)/shard_map/ppermute | solution.py:16
  11.5 20.9 %collective-permute-start.6 = (bf16[512,256]{1,0:T(8,128)(2,1)}, bf16[512,256]{1,0:T(8,128)(2,1)S(1)}, u32[]{:S(2)}, u32[]{:S(2)}) collective-permute-start(bf16[512,256]{1,0:T(8,128)(2,1)} %get-tuple-element.36), channel_id=1, source_target_pairs={{0,4},{1,5},{2,6},{3,7},{4,8},{5,9},{6,10},{7,11},{8,12},{9,13},{1... | collective-permute-start | bytes 786440 | tf_op jit(solution)/shard_map/ppermute | solution.py:16
  14.0 42.9 %collective-permute-start.1 = (bf16[1024,256]{1,0:T(8,128)(2,1)}, bf16[1024,256]{1,0:T(8,128)(2,1)}, u32[]{:S(2)}, u32[]{:S(2)}) collective-permute-start(bf16[1024,256]{1,0:T(8,128)(2,1)} %get-tuple-element.39), channel_id=1, source_target_pairs={{0,12},{1,13},{2,14},{3,15},{4,0},{5,1},{6,2},{7,3},{8,4},{9,5},{1... | collective-permute-start | bytes 1572872 | tf_op jit(solution)/shard_map/ppermute | solution.py:16
  17.8 5.3 %copy-start.5 = (bf16[4096,256]{1,0:T(8,128)(2,1)S(1)}, bf16[4096,256]{1,0:T(8,128)(2,1)}, u32[]{:S(2)}) copy-start(bf16[4096,256]{1,0:T(8,128)(2,1)} %param.4) | copy-start | bytes 6291460
  25.4 7.0 %copy-start.10 = (bf16[1024,256]{1,0:T(8,128)(2,1)S(1)}, bf16[1024,256]{1,0:T(8,128)(2,1)}, u32[]{:S(2)}) copy-start(bf16[1024,256]{1,0:T(8,128)(2,1)} %get-tuple-element.37) | copy-start | bytes 1572868
  25.4 9.8 %copy-start.7 = (f32[512,512]{0,1:T(8,128)S(1)}, f32[512,512]{0,1:T(8,128)}, u32[]{:S(2)}) copy-start(f32[512,512]{0,1:T(8,128)} %fusion.63) | copy-start | bytes 3145732
  26.8 28.1 %collective-permute-start = (bf16[1024,256]{1,0:T(8,128)(2,1)}, bf16[1024,256]{1,0:T(8,128)(2,1)S(1)}, u32[]{:S(2)}, u32[]{:S(2)}) collective-permute-start(bf16[1024,256]{1,0:T(8,128)(2,1)} %get-tuple-element.39), channel_id=1, source_target_pairs={{0,4},{1,5},{2,6},{3,7},{4,8},{5,9},{6,10},{7,11},{8,12},{9,13},{1... | collective-permute-start | bytes 1572872 | tf_op jit(solution)/shard_map/ppermute | solution.py:16
  28.8 6.8 %copy-start.8 = (bf16[4096,256]{1,0:T(8,128)(2,1)S(1)}, bf16[4096,256]{1,0:T(8,128)(2,1)}, u32[]{:S(2)}) copy-start(bf16[4096,256]{1,0:T(8,128)(2,1)} %param.5) | copy-start | bytes 6291460
  32.4 69.2 %collective-permute-start.5 = (bf16[1024,256]{1,0:T(8,128)(2,1)S(1)}, bf16[1024,256]{1,0:T(8,128)(2,1)S(1)}, u32[]{:S(2)}, u32[]{:S(2)}) collective-permute-start(bf16[1024,256]{1,0:T(8,128)(2,1)S(1)} %copy-done.10), channel_id=1, source_target_pairs={{0,12},{1,13},{2,14},{3,15},{4,0},{5,1},{6,2},{7,3},{8,4},{9,5},{1... | collective-permute-start | bytes 1572872 | tf_op jit(solution)/shard_map/ppermute | solution.py:16
  35.6 1.6 copy-start.6
  39.6 17.4 %copy-start.9 = (bf16[1024,256]{1,0:T(8,128)(2,1)S(1)}, bf16[1024,256]{1,0:T(8,128)(2,1)}, u32[]{:S(2)}) copy-start(bf16[1024,256]{1,0:T(8,128)(2,1)} %get-tuple-element.38) | copy-start | bytes 1572868
  39.6 19.8 %copy-start.4 = (f32[1024,512]{0,1:T(8,128)S(1)}, f32[1024,512]{0,1:T(8,128)}, u32[]{:S(2)}) copy-start(f32[1024,512]{0,1:T(8,128)} %fusion.72) | copy-start | bytes 6291460
  54.9 44.3 %collective-permute-start.4 = (bf16[1024,256]{1,0:T(8,128)(2,1)S(1)}, bf16[1024,256]{1,0:T(8,128)(2,1)S(1)}, u32[]{:S(2)}, u32[]{:S(2)}) collective-permute-start(bf16[1024,256]{1,0:T(8,128)(2,1)S(1)} %copy-done.10), channel_id=1, source_target_pairs={{0,4},{1,5},{2,6},{3,7},{4,8},{5,9},{6,10},{7,11},{8,12},{9,13},{1... | collective-permute-start | bytes 1572872 | tf_op jit(solution)/shard_map/ppermute | solution.py:16
  57.0 47.3 %collective-permute-start.3 = (bf16[1024,256]{1,0:T(8,128)(2,1)S(1)}, bf16[1024,256]{1,0:T(8,128)(2,1)S(1)}, u32[]{:S(2)}, u32[]{:S(2)}) collective-permute-start(bf16[1024,256]{1,0:T(8,128)(2,1)S(1)} %copy-done.9), channel_id=1, source_target_pairs={{0,12},{1,13},{2,14},{3,15},{4,0},{5,1},{6,2},{7,3},{8,4},{9,5},{1... | collective-permute-start | bytes 1572872 | tf_op jit(solution)/shard_map/ppermute | solution.py:16
  62.6 36.2 %collective-permute-start.2 = (bf16[1024,256]{1,0:T(8,128)(2,1)S(1)}, bf16[1024,256]{1,0:T(8,128)(2,1)S(1)}, u32[]{:S(2)}, u32[]{:S(2)}) collective-permute-start(bf16[1024,256]{1,0:T(8,128)(2,1)S(1)} %copy-done.9), channel_id=1, source_target_pairs={{0,4},{1,5},{2,6},{3,7},{4,8},{5,9},{6,10},{7,11},{8,12},{9,13},{1... | collective-permute-start | bytes 1572872 | tf_op jit(solution)/shard_map/ppermute | solution.py:16
  106.9 25.1 %collective-permute-start.12 = (bf16[1024,256]{1,0:T(8,128)(2,1)S(1)}, bf16[1024,256]{1,0:T(8,128)(2,1)S(1)}, u32[]{:S(2)}, u32[]{:S(2)}) collective-permute-start(bf16[1024,256]{1,0:T(8,128)(2,1)S(1)} %convolution_convert_fusion.5), channel_id=1, source_target_pairs={{0,12},{1,13},{2,14},{3,15},{4,0},{5,1},{6,2},{7,3},{8,4},{9,5},{1... | collective-permute-start | bytes 1572872 | tf_op jit(solution)/shard_map/ppermute | solution.py:16
  109.5 23.7 %collective-permute-start.13 = (bf16[1024,256]{1,0:T(8,128)(2,1)S(1)}, bf16[1024,256]{1,0:T(8,128)(2,1)S(1)}, u32[]{:S(2)}, u32[]{:S(2)}) collective-permute-start(bf16[1024,256]{1,0:T(8,128)(2,1)S(1)} %convolution_convert_fusion.4), channel_id=1, source_target_pairs={{0,4},{1,5},{2,6},{3,7},{4,8},{5,9},{6,10},{7,11},{8,12},{9,13},{1... | collective-permute-start | bytes 1572872 | tf_op jit(solution)/shard_map/ppermute | solution.py:16
  116.6 2.5 %collective-permute-start.10 = (f32[229376]{0:T(1024)S(1)}, f32[229376]{0:T(1024)S(1)}, u32[]{:S(2)}, u32[]{:S(2)}) collective-permute-start(f32[229376]{0:T(1024)S(1)} %dynamic_slice.25), channel_id=1, source_target_pairs={{0,1},{1,0},{2,3},{3,2},{4,5},{5,4},{6,7},{7,6},{8,9},{9,8},{10,11... | collective-permute-start | bytes 2752520 | tf_op jit(solution)/shard_map/ppermute | solution.py:22
  119.3 12.6 %collective-permute-start.11 = (f32[114688]{0:T(1024)S(1)}, f32[114688]{0:T(1024)S(1)}, u32[]{:S(2)}, u32[]{:S(2)}) collective-permute-start(f32[114688]{0:T(1024)S(1)} %dynamic_slice.27), channel_id=1, source_target_pairs={{0,2},{1,3},{2,0},{3,1},{4,6},{5,7},{6,4},{7,5},{8,10},{9,11},{10,... | collective-permute-start | bytes 1376264 | tf_op jit(solution)/shard_map/ppermute | solution.py:22
  133.2 6.3 %collective-permute-start.14 = (f32[57344]{0:T(1024)S(1)}, f32[57344]{0:T(1024)S(1)}, u32[]{:S(2)}, u32[]{:S(2)}) collective-permute-start(f32[57344]{0:T(1024)S(1)} %dynamic_slice.29), channel_id=1, source_target_pairs={{0,4},{1,5},{2,6},{3,7},{4,0},{5,1},{6,2},{7,3},{8,12},{9,13},{10,... | collective-permute-start | bytes 688136 | tf_op jit(solution)/shard_map/ppermute | solution.py:22
  139.5 7.0 %collective-permute-start.15 = (f32[28672]{0:T(1024)S(1)}, f32[28672]{0:T(1024)S(1)}, u32[]{:S(2)}, u32[]{:S(2)}) collective-permute-start(f32[28672]{0:T(1024)S(1)} %dynamic_slice.31), channel_id=1, source_target_pairs={{0,8},{1,9},{2,10},{3,11},{4,12},{5,13},{6,14},{7,15},{8,0},{9,1},... | collective-permute-start | bytes 344072 | tf_op jit(solution)/shard_map/ppermute | solution.py:22
  146.5 5.8 %collective-permute-start.16 = (f32[28672]{0:T(1024)S(1)}, f32[28672]{0:T(1024)S(1)}, u32[]{:S(2)}, u32[]{:S(2)}) collective-permute-start(f32[28672]{0:T(1024)S(1)} %add_multiply_fusion), channel_id=1, source_target_pairs={{0,8},{1,9},{2,10},{3,11},{4,12},{5,13},{6,14},{7,15},{8,0},{9,1},... | collective-permute-start | bytes 344072 | tf_op jit(solution)/shard_map/ppermute | solution.py:22
  152.4 6.1 %collective-permute-start.17 = (f32[57344]{0:T(1024)S(1)}, f32[57344]{0:T(1024)S(1)}, u32[]{:S(2)}, u32[]{:S(2)}) collective-permute-start(f32[57344]{0:T(1024)S(1)} %pad_maximum_fusion.10), channel_id=1, source_target_pairs={{0,4},{1,5},{2,6},{3,7},{4,0},{5,1},{6,2},{7,3},{8,12},{9,13},{10,... | collective-permute-start | bytes 688136 | tf_op jit(solution)/shard_map/ppermute | solution.py:22
  158.6 8.6 %collective-permute-start.18 = (f32[114688]{0:T(1024)S(1)}, f32[114688]{0:T(1024)S(1)}, u32[]{:S(2)}, u32[]{:S(2)}) collective-permute-start(f32[114688]{0:T(1024)S(1)} %pad_maximum_fusion.9), channel_id=1, source_target_pairs={{0,2},{1,3},{2,0},{3,1},{4,6},{5,7},{6,4},{7,5},{8,10},{9,11},{10,... | collective-permute-start | bytes 1376264 | tf_op jit(solution)/shard_map/ppermute | solution.py:22
  160.9 39.2 %collective-permute-start.19 = (bf16[3072,256]{1,0:T(8,128)(2,1)S(1)}, bf16[3072,256]{1,0:T(8,128)(2,1)S(1)}, u32[]{:S(2)}, u32[]{:S(2)}) collective-permute-start(bf16[3072,256]{1,0:T(8,128)(2,1)S(1)} %get-tuple-element.23), channel_id=1, source_target_pairs={{0,12},{1,13},{2,14},{3,15},{4,0},{5,1},{6,2},{7,3},{8,4},{9,5},{1... | collective-permute-start | bytes 4718600 | tf_op jit(solution)/shard_map/ppermute | solution.py:16
  165.2 64.3 %collective-permute-start.20 = (bf16[3072,256]{1,0:T(8,128)(2,1)S(1)}, bf16[3072,256]{1,0:T(8,128)(2,1)S(1)}, u32[]{:S(2)}, u32[]{:S(2)}) collective-permute-start(bf16[3072,256]{1,0:T(8,128)(2,1)S(1)} %get-tuple-element.24), channel_id=1, source_target_pairs={{0,4},{1,5},{2,6},{3,7},{4,8},{5,9},{6,10},{7,11},{8,12},{9,13},{1... | collective-permute-start | bytes 4718600 | tf_op jit(solution)/shard_map/ppermute | solution.py:16
  229.5 2.5 %collective-permute-start.21 = (f32[229376]{0:T(1024)S(1)}, f32[229376]{0:T(1024)S(1)}, u32[]{:S(2)}, u32[]{:S(2)}) collective-permute-start(f32[229376]{0:T(1024)S(1)} %pad_maximum_fusion.6), channel_id=1, source_target_pairs={{0,1},{1,0},{2,3},{3,2},{4,5},{5,4},{6,7},{7,6},{8,9},{9,8},{10,11... | collective-permute-start | bytes 2752520 | tf_op jit(solution)/shard_map/ppermute | solution.py:22
  232.3 4.3 %copy-start.1 = (bf16[256,256]{1,0:T(8,128)(2,1)S(1)}, bf16[256,256]{1,0:T(8,128)(2,1)}, u32[]{:S(2)}) copy-start(bf16[256,256]{1,0:T(8,128)(2,1)} %param.7) | copy-start | bytes 393220
  (1 other events, 1.6 us)

commit v4 on v3

--- a/solution.py
+++ b/solution.py
@@ -8,6 +8,7 @@
 TAP_SPACING = 16384
 CHUNK_EIGHTHS = (2, 2, 2, 1, 1)
 EARLY = 1
+RIDER_ROWS = 256
 
 
 def from_behind(value, axis, steps):
@@ -110,18 +111,35 @@
         highs.append(upper_term)
     norm_factor = 1.0 / math.sqrt(positions * seq_size)
     buf = jnp.concatenate([wconv_total.reshape(-1), wout_total.reshape(-1)])
+    lower_all = jnp.concatenate(lows, axis=0)
+    upper_all = jnp.concatenate(highs, axis=0)
+
+    def send_rows(low_high, start, stop):
+        return (
+            from_behind(low_high[0][start:stop], "seq", -spacing),
+            from_behind(low_high[1][start:stop], "seq", spacing),
+        )
+
     steps = chain_steps(seq_size)
+    rider_steps = [(4, True), (8, True), (8, False), (4, False)]
+    sent_rows = bounds[EARLY]
+    pending = None
     late = []
-    sent_late = False
     for number, (bit, down) in enumerate(steps):
         if down and bit == 4:
             buf, early = lax.optimization_barrier((buf, early))
-        if not down and bit == 2:
-            rest_low = jnp.concatenate(lows[EARLY:], axis=0)
-            rest_high = jnp.concatenate(highs[EARLY:], axis=0)
-            buf, rest_low, rest_high = lax.optimization_barrier((buf, rest_low, rest_high))
-            late.append((from_behind(rest_low, "seq", -spacing), from_behind(rest_high, "seq", spacing)))
-            sent_late = True
+        if pending is not None:
+            buf, pending = lax.optimization_barrier((buf, pending))
+            early.append(pending)
+            pending = None
+        if (bit, down) in rider_steps and sent_rows + RIDER_ROWS <= positions:
+            buf, pieces = lax.optimization_barrier((buf, (lower_all, upper_all)))
+            pending = send_rows(pieces, sent_rows, sent_rows + RIDER_ROWS)
+            sent_rows += RIDER_ROWS
+        if not down and bit == 2 and not late:
+            buf, pieces = lax.optimization_barrier((buf, (lower_all, upper_all)))
+            late.append(send_rows(pieces, sent_rows, positions))
+            sent_rows = positions
         if not down and bit == 1 and late:
             buf, late = lax.optimization_barrier((buf, late))
         buf = chain_step(buf, "seq", bit, down)
@@ -129,9 +147,10 @@
             buf = buf * jnp.float32(norm_factor)
     if not steps:
         buf = buf * jnp.float32(norm_factor)
-    if not sent_late:
-        for low, high in zip(lows[EARLY:], highs[EARLY:]):
-            late.append((from_behind(low, "seq", -spacing), from_behind(high, "seq", spacing)))
+    if pending is not None:
+        early.append(pending)
+    if sent_rows < positions:
+        late.append(send_rows((lower_all, upper_all), sent_rows, positions))
     received = early + late
     received_ahead = jnp.concatenate([pair[0] for pair in received], axis=0)
     received_behind = jnp.concatenate([pair[1] for pair in received], axis=0)

time: 237 us -> 232 us (0.979)
  waiting for transfers between devices: 145 us -> 110 us
  starting transfers between devices: 36.3 us -> 68.1 us
    ppermute x14 -> x22, starting transfers between devices: 27.2 us -> 56.4 us  [from_behind(): return lax.ppermute(value, axis, pairs)]
    ppermute x14 -> x22, waiting for transfers between devices: 115 us -> 89 us  [from_behind(): return lax.ppermute(value, axis, pairs)]
    ppermute x8, waiting for transfers between devices: 30.2 us -> 21 us  [exchange(): return lax.ppermute(value, axis, pairs)]
    ppermute x8, starting transfers between devices: 9.02 us -> 11.7 us  [exchange(): return lax.ppermute(value, axis, pairs)]
  transfers between devices with their start and end apart: 22 -> 30, of which waited for: 14 -> 18; matrix products, arithmetic and copies ran while one was open for 18% -> 17% of each run, Pallas kernels for 0% -> 0%
where the time goes in v4:
time: 232 us; the launch traced here: 231 us
  waiting for transfers between devices  110 us (47%)
  starting transfers between devices  68.1 us (29%)
  matrix products  37.5 us (16%)
  local copies, waits for them, and re-layouts  9.11 us (4%)
  other arithmetic  5.03 us (2%)
    ppermute x22, waiting for transfers between devices, from_behind(): return lax.ppermute(value, axis, pairs)  89 us
    ppermute x22, starting transfers between devices, from_behind(): return lax.ppermute(value, axis, pairs)  56.4 us
    ppermute x8, waiting for transfers between devices, exchange(): return lax.ppermute(value, axis, pairs)  21 us
    ppermute x8, starting transfers between devices, exchange(): return lax.ppermute(value, axis, pairs)  11.7 us
    dot_general x5, matrix products, chunk_layer(): preact = preact + jnp.dot(middle, w_mid, preferred_element_type=jnp.float32)  8.97 us
    dot_general x5, matrix products, chunk_layer(): lax.dot_general(right_tap_input, grad_pre, first_dims, preferred_element_...  5.23 us
    dot_general x5, matrix products, chunk_layer(): jnp.dot(right_tap_input, w_high, preferred_element_type=jnp.float32)  5.13 us
  transfers between devices with their start and end apart: 30, of which 18 were waited for; matrix products, arithmetic and copies ran while one was open for 17% of the time, Pallas kernels for 0%

profile of v4, /device:TPU:0, one launch (start us, length us, event | category | flops | bytes accessed | tf_op | source)
XLA Modules:
  0.0 231.2 jit_solution(17010682732801315190)
XLA Ops:
  0.7 1.9 fusion.112
  2.6 5.0 %collective-permute-start.9 = (bf16[512,256]{1,0:T(8,128)(2,1)}, bf16[512,256]{1,0:T(8,128)(2,1)}, u32[]{:S(2)}, u32[]{:S(2)}) collective-permute-start(bf16[512,256]{1,0:T(8,128)(2,1)} %get-tuple-element.83), channel_id=1, source_target_pairs={{0,12},{1,13},{2,14},{3,15},{4,0},{5,1},{6,2},{7,3},{8,4},{9,5},{1... | collective-permute-start | bytes 786440 | tf_op jit(solution)/shard_map/ppermute | solution.py:17
  7.7 3.8 %collective-permute-start.7 = (bf16[512,256]{1,0:T(8,128)(2,1)}, bf16[512,256]{1,0:T(8,128)(2,1)}, u32[]{:S(2)}, u32[]{:S(2)}) collective-permute-start(bf16[512,256]{1,0:T(8,128)(2,1)} %get-tuple-element.84), channel_id=1, source_target_pairs={{0,12},{1,13},{2,14},{3,15},{4,0},{5,1},{6,2},{7,3},{8,4},{9,5},{1... | collective-permute-start | bytes 786440 | tf_op jit(solution)/shard_map/ppermute | solution.py:17
  11.5 2.6 %fusion.113 = (bf16[1024,256]{1,0:T(8,128)(2,1)}, bf16[1024,256]{1,0:T(8,128)(2,1)}, bf16[1024,256]{1,0:T(8,128)(2,1)}) fusion(bf16[4096,256]{1,0:T(8,128)(2,1)} %param.4), kind=kLoop, calls=%fused_computation.203 | loop fusion | bytes 3145728 | tf_op jit(solution)/shard_map/slice | solution.py:94
  14.0 3.8 %collective-permute-start.1 = (bf16[1024,256]{1,0:T(8,128)(2,1)}, bf16[1024,256]{1,0:T(8,128)(2,1)}, u32[]{:S(2)}, u32[]{:S(2)}) collective-permute-start(bf16[1024,256]{1,0:T(8,128)(2,1)} %get-tuple-element.87), channel_id=1, source_target_pairs={{0,12},{1,13},{2,14},{3,15},{4,0},{5,1},{6,2},{7,3},{8,4},{9,5},{1... | collective-permute-start | bytes 1572872 | tf_op jit(solution)/shard_map/ppermute | solution.py:17
  17.9 2.4 %fusion.71 = f32[512,512]{0,1:T(8,128)} fusion(bf16[768,512]{1,0:T(8,128)(2,1)S(1)} %copy-done.2, bf16[4096,256]{1,0:T(8,128)(2,1)} %param.4), kind=kOutput, calls=%fused_computation.166 | convolution fusion | flops 134217728 | bytes 1572864 | tf_op jit(solution)/shard_map/dot_general | solution.py:55
  20.3 2.9 %fusion.74 = f32[1024,512]{0,1:T(8,128)} fusion(bf16[768,512]{1,0:T(8,128)(2,1)S(1)} %copy-done.2, bf16[4096,256]{1,0:T(8,128)(2,1)} %param.4), kind=kOutput, calls=%fused_computation.169 | convolution fusion | flops 268435456 | bytes 2883584 | tf_op jit(solution)/shard_map/dot_general | solution.py:55
  28.8 3.6 %collective-permute-done.6 = bf16[512,256]{1,0:T(8,128)(2,1)S(1)} collective-permute-done((bf16[512,256]{1,0:T(8,128)(2,1)}, bf16[512,256]{1,0:T(8,128)(2,1)S(1)}, u32[]{:S(2)}, u32[]{:S(2)}) %collective-permute-start.6) | collective-permute-done | bytes 262176 | tf_op jit(solution)/shard_map/ppermute | solution.py:17
  32.4 2.8 %collective-permute-start.5 = (bf16[1024,256]{1,0:T(8,128)(2,1)S(1)}, bf16[1024,256]{1,0:T(8,128)(2,1)S(1)}, u32[]{:S(2)}, u32[]{:S(2)}) collective-permute-start(bf16[1024,256]{1,0:T(8,128)(2,1)S(1)} %copy-done.10), channel_id=1, source_target_pairs={{0,12},{1,13},{2,14},{3,15},{4,0},{5,1},{6,2},{7,3},{8,4},{9,5},{1... | collective-permute-start | bytes 1572872 | tf_op jit(solution)/shard_map/ppermute | solution.py:17
  39.4 15.6 %collective-permute-done = bf16[1024,256]{1,0:T(8,128)(2,1)S(1)} collective-permute-done((bf16[1024,256]{1,0:T(8,128)(2,1)}, bf16[1024,256]{1,0:T(8,128)(2,1)S(1)}, u32[]{:S(2)}, u32[]{:S(2)}) %collective-permute-start) | collective-permute-done | bytes 524320 | tf_op jit(solution)/shard_map/ppermute | solution.py:17
  57.0 2.3 %collective-permute-start.3 = (bf16[1024,256]{1,0:T(8,128)(2,1)S(1)}, bf16[1024,256]{1,0:T(8,128)(2,1)S(1)}, u32[]{:S(2)}, u32[]{:S(2)}) collective-permute-start(bf16[1024,256]{1,0:T(8,128)(2,1)S(1)} %copy-done.9), channel_id=1, source_target_pairs={{0,12},{1,13},{2,14},{3,15},{4,0},{5,1},{6,2},{7,3},{8,4},{9,5},{1... | collective-permute-start | bytes 1572872 | tf_op jit(solution)/shard_map/ppermute | solution.py:17
  65.8 33.0 %collective-permute-done.2 = bf16[1024,256]{1,0:T(8,128)(2,1)S(1)} collective-permute-done((bf16[1024,256]{1,0:T(8,128)(2,1)S(1)}, bf16[1024,256]{1,0:T(8,128)(2,1)S(1)}, u32[]{:S(2)}, u32[]{:S(2)}) %collective-permute-start.2) | collective-permute-done | bytes 524320 | tf_op jit(solution)/shard_map/ppermute | solution.py:17
  110.6 2.6 %collective-permute-start.12 = (bf16[1024,256]{1,0:T(8,128)(2,1)S(1)}, bf16[1024,256]{1,0:T(8,128)(2,1)S(1)}, u32[]{:S(2)}, u32[]{:S(2)}) collective-permute-start(bf16[1024,256]{1,0:T(8,128)(2,1)S(1)} %get-tuple-element.42), channel_id=1, source_target_pairs={{0,12},{1,13},{2,14},{3,15},{4,0},{5,1},{6,2},{7,3},{8,4},{9,5},{1... | collective-permute-start | bytes 1572872 | tf_op jit(solution)/shard_map/ppermute | solution.py:17
  124.3 10.4 %collective-permute-done.11 = f32[114688]{0:T(1024)S(1)} collective-permute-done((f32[114688]{0:T(1024)S(1)}, f32[114688]{0:T(1024)S(1)}, u32[]{:S(2)}, u32[]{:S(2)}) %collective-permute-start.11) | collective-permute-done | bytes 458784 | tf_op jit(solution)/shard_map/ppermute | solution.py:23
  134.7 2.1 collective-permute-done.13
  139.4 2.3 %collective-permute-start.15 = (bf16[256,256]{1,0:T(8,128)(2,1)S(1)}, bf16[256,256]{1,0:T(8,128)(2,1)S(1)}, u32[]{:S(2)}, u32[]{:S(2)}) collective-permute-start(bf16[256,256]{1,0:T(8,128)(2,1)S(1)} %slice.151), channel_id=1, source_target_pairs={{0,12},{1,13},{2,14},{3,15},{4,0},{5,1},{6,2},{7,3},{8,4},{9,5},{1... | collective-permute-start | bytes 393224 | tf_op jit(solution)/shard_map/ppermute | solution.py:17
  141.8 4.3 %collective-permute-done.14 = f32[57344]{0:T(1024)S(1)} collective-permute-done((f32[57344]{0:T(1024)S(1)}, f32[57344]{0:T(1024)S(1)}, u32[]{:S(2)}, u32[]{:S(2)}) %collective-permute-start.14) | collective-permute-done | bytes 229408 | tf_op jit(solution)/shard_map/ppermute | solution.py:23
  146.1 2.3 %collective-permute-done.16 = bf16[256,256]{1,0:T(8,128)(2,1)S(1)} collective-permute-done((bf16[256,256]{1,0:T(8,128)(2,1)S(1)}, bf16[256,256]{1,0:T(8,128)(2,1)S(1)}, u32[]{:S(2)}, u32[]{:S(2)}) %collective-permute-start.16) | collective-permute-done | bytes 131104 | tf_op jit(solution)/shard_map/ppermute | solution.py:17
  148.8 2.3 %collective-permute-start.17 = (f32[28672]{0:T(1024)S(1)}, f32[28672]{0:T(1024)S(1)}, u32[]{:S(2)}, u32[]{:S(2)}) collective-permute-start(f32[28672]{0:T(1024)S(1)} %dynamic_slice.31), channel_id=1, source_target_pairs={{0,8},{1,9},{2,10},{3,11},{4,12},{5,13},{6,14},{7,15},{8,0},{9,1},... | collective-permute-start | bytes 344072 | tf_op jit(solution)/shard_map/ppermute | solution.py:23
  152.0 3.0 %collective-permute-start.18 = (bf16[256,256]{1,0:T(8,128)(2,1)S(1)}, bf16[256,256]{1,0:T(8,128)(2,1)S(1)}, u32[]{:S(2)}, u32[]{:S(2)}) collective-permute-start(bf16[256,256]{1,0:T(8,128)(2,1)S(1)} %slice.153), channel_id=1, source_target_pairs={{0,12},{1,13},{2,14},{3,15},{4,0},{5,1},{6,2},{7,3},{8,4},{9,5},{1... | collective-permute-start | bytes 393224 | tf_op jit(solution)/shard_map/ppermute | solution.py:17
  155.0 3.5 %collective-permute-done.17 = f32[28672]{0:T(1024)S(1)} collective-permute-done((f32[28672]{0:T(1024)S(1)}, f32[28672]{0:T(1024)S(1)}, u32[]{:S(2)}, u32[]{:S(2)}) %collective-permute-start.17) | collective-permute-done | bytes 114720 | tf_op jit(solution)/shard_map/ppermute | solution.py:23
  160.1 2.8 %collective-permute-start.20 = (f32[28672]{0:T(1024)S(1)}, f32[28672]{0:T(1024)S(1)}, u32[]{:S(2)}, u32[]{:S(2)}) collective-permute-start(f32[28672]{0:T(1024)S(1)} %add_multiply_fusion), channel_id=1, source_target_pairs={{0,8},{1,9},{2,10},{3,11},{4,12},{5,13},{6,14},{7,15},{8,0},{9,1},... | collective-permute-start | bytes 344072 | tf_op jit(solution)/shard_map/ppermute | solution.py:23
  163.0 3.8 %collective-permute-start.21 = (bf16[256,256]{1,0:T(8,128)(2,1)S(1)}, bf16[256,256]{1,0:T(8,128)(2,1)S(1)}, u32[]{:S(2)}, u32[]{:S(2)}) collective-permute-start(bf16[256,256]{1,0:T(8,128)(2,1)S(1)} %slice.155), channel_id=1, source_target_pairs={{0,12},{1,13},{2,14},{3,15},{4,0},{5,1},{6,2},{7,3},{8,4},{9,5},{1... | collective-permute-start | bytes 393224 | tf_op jit(solution)/shard_map/ppermute | solution.py:17
  166.8 3.5 %collective-permute-done.22 = bf16[256,256]{1,0:T(8,128)(2,1)S(1)} collective-permute-done((bf16[256,256]{1,0:T(8,128)(2,1)S(1)}, bf16[256,256]{1,0:T(8,128)(2,1)S(1)}, u32[]{:S(2)}, u32[]{:S(2)}) %collective-permute-start.22) | collective-permute-done | bytes 131104 | tf_op jit(solution)/shard_map/ppermute | solution.py:17
  172.9 2.5 %collective-permute-start.24 = (bf16[256,256]{1,0:T(8,128)(2,1)S(1)}, bf16[256,256]{1,0:T(8,128)(2,1)S(1)}, u32[]{:S(2)}, u32[]{:S(2)}) collective-permute-start(bf16[256,256]{1,0:T(8,128)(2,1)S(1)} %slice.157), channel_id=1, source_target_pairs={{0,12},{1,13},{2,14},{3,15},{4,0},{5,1},{6,2},{7,3},{8,4},{9,5},{1... | collective-permute-start | bytes 393224 | tf_op jit(solution)/shard_map/ppermute | solution.py:17
  175.3 2.1 collective-permute-done.23
  177.5 3.2 %collective-permute-done.25 = bf16[256,256]{1,0:T(8,128)(2,1)S(1)} collective-permute-done((bf16[256,256]{1,0:T(8,128)(2,1)S(1)}, bf16[256,256]{1,0:T(8,128)(2,1)S(1)}, u32[]{:S(2)}, u32[]{:S(2)}) %collective-permute-start.25) | collective-permute-done | bytes 131104 | tf_op jit(solution)/shard_map/ppermute | solution.py:17
  180.7 3.8 %collective-permute-start.26 = (f32[114688]{0:T(1024)S(1)}, f32[114688]{0:T(1024)S(1)}, u32[]{:S(2)}, u32[]{:S(2)}) collective-permute-start(f32[114688]{0:T(1024)S(1)} %pad_maximum_fusion.7), channel_id=1, source_target_pairs={{0,2},{1,3},{2,0},{3,1},{4,6},{5,7},{6,4},{7,5},{8,10},{9,11},{10,... | collective-permute-start | bytes 1376264 | tf_op jit(solution)/shard_map/ppermute | solution.py:23
  184.7 18.0 %collective-permute-start.28 = (bf16[2048,256]{1,0:T(8,128)(2,1)S(1)}, bf16[2048,256]{1,0:T(8,128)(2,1)S(1)}, u32[]{:S(2)}, u32[]{:S(2)}) collective-permute-start(bf16[2048,256]{1,0:T(8,128)(2,1)S(1)} %slice.160), channel_id=1, source_target_pairs={{0,4},{1,5},{2,6},{3,7},{4,8},{5,9},{6,10},{7,11},{8,12},{9,13},{1... | collective-permute-start | bytes 3145736 | tf_op jit(solution)/shard_map/ppermute | solution.py:17
  202.9 12.1 %collective-permute-done.28 = bf16[2048,256]{1,0:T(8,128)(2,1)S(1)} collective-permute-done((bf16[2048,256]{1,0:T(8,128)(2,1)S(1)}, bf16[2048,256]{1,0:T(8,128)(2,1)S(1)}, u32[]{:S(2)}, u32[]{:S(2)}) %collective-permute-start.28) | collective-permute-done | bytes 1048608 | tf_op jit(solution)/shard_map/ppermute | solution.py:17
  215.0 11.2 %collective-permute-done.27 = bf16[2048,256]{1,0:T(8,128)(2,1)S(1)} collective-permute-done((bf16[2048,256]{1,0:T(8,128)(2,1)S(1)}, bf16[2048,256]{1,0:T(8,128)(2,1)S(1)}, u32[]{:S(2)}, u32[]{:S(2)}) %collective-permute-start.27) | collective-permute-done | bytes 1048608 | tf_op jit(solution)/shard_map/ppermute | solution.py:17
  226.4 2.2 add_convert_fusion
  (154 shorter events, 51.9 us)
Async XLA Ops:
  0.6 35.0 %copy-start = (bf16[256,256]{1,0:T(8,128)(2,1)S(1)}, bf16[256,256]{1,0:T(8,128)(2,1)}, u32[]{:S(2)}) copy-start(bf16[256,256]{1,0:T(8,128)(2,1)} %param.7) | copy-start | bytes 393220
  2.6 60.0 %collective-permute-start.9 = (bf16[512,256]{1,0:T(8,128)(2,1)}, bf16[512,256]{1,0:T(8,128)(2,1)}, u32[]{:S(2)}, u32[]{:S(2)}) collective-permute-start(bf16[512,256]{1,0:T(8,128)(2,1)} %get-tuple-element.83), channel_id=1, source_target_pairs={{0,12},{1,13},{2,14},{3,15},{4,0},{5,1},{6,2},{7,3},{8,4},{9,5},{1... | collective-permute-start | bytes 786440 | tf_op jit(solution)/shard_map/ppermute | solution.py:17
  7.6 55.2 %collective-permute-start.8 = (bf16[512,256]{1,0:T(8,128)(2,1)}, bf16[512,256]{1,0:T(8,128)(2,1)S(1)}, u32[]{:S(2)}, u32[]{:S(2)}) collective-permute-start(bf16[512,256]{1,0:T(8,128)(2,1)} %get-tuple-element.83), channel_id=1, source_target_pairs={{0,4},{1,5},{2,6},{3,7},{4,8},{5,9},{6,10},{7,11},{8,12},{9,13},{1... | collective-permute-start | bytes 786440 | tf_op jit(solution)/shard_map/ppermute | solution.py:17
  7.7 19.2 %collective-permute-start.7 = (bf16[512,256]{1,0:T(8,128)(2,1)}, bf16[512,256]{1,0:T(8,128)(2,1)}, u32[]{:S(2)}, u32[]{:S(2)}) collective-permute-start(bf16[512,256]{1,0:T(8,128)(2,1)} %get-tuple-element.84), channel_id=1, source_target_pairs={{0,12},{1,13},{2,14},{3,15},{4,0},{5,1},{6,2},{7,3},{8,4},{9,5},{1... | collective-permute-start | bytes 786440 | tf_op jit(solution)/shard_map/ppermute | solution.py:17
  11.5 20.9 %collective-permute-start.6 = (bf16[512,256]{1,0:T(8,128)(2,1)}, bf16[512,256]{1,0:T(8,128)(2,1)S(1)}, u32[]{:S(2)}, u32[]{:S(2)}) collective-permute-start(bf16[512,256]{1,0:T(8,128)(2,1)} %get-tuple-element.84), channel_id=1, source_target_pairs={{0,4},{1,5},{2,6},{3,7},{4,8},{5,9},{6,10},{7,11},{8,12},{9,13},{1... | collective-permute-start | bytes 786440 | tf_op jit(solution)/shard_map/ppermute | solution.py:17
  14.0 42.9 %collective-permute-start.1 = (bf16[1024,256]{1,0:T(8,128)(2,1)}, bf16[1024,256]{1,0:T(8,128)(2,1)}, u32[]{:S(2)}, u32[]{:S(2)}) collective-permute-start(bf16[1024,256]{1,0:T(8,128)(2,1)} %get-tuple-element.87), channel_id=1, source_target_pairs={{0,12},{1,13},{2,14},{3,15},{4,0},{5,1},{6,2},{7,3},{8,4},{9,5},{1... | collective-permute-start | bytes 1572872 | tf_op jit(solution)/shard_map/ppermute | solution.py:17
  26.9 28.1 %collective-permute-start = (bf16[1024,256]{1,0:T(8,128)(2,1)}, bf16[1024,256]{1,0:T(8,128)(2,1)S(1)}, u32[]{:S(2)}, u32[]{:S(2)}) collective-permute-start(bf16[1024,256]{1,0:T(8,128)(2,1)} %get-tuple-element.87), channel_id=1, source_target_pairs={{0,4},{1,5},{2,6},{3,7},{4,8},{5,9},{6,10},{7,11},{8,12},{9,13},{1... | collective-permute-start | bytes 1572872 | tf_op jit(solution)/shard_map/ppermute | solution.py:17
  32.4 69.2 %collective-permute-start.5 = (bf16[1024,256]{1,0:T(8,128)(2,1)S(1)}, bf16[1024,256]{1,0:T(8,128)(2,1)S(1)}, u32[]{:S(2)}, u32[]{:S(2)}) collective-permute-start(bf16[1024,256]{1,0:T(8,128)(2,1)S(1)} %copy-done.10), channel_id=1, source_target_pairs={{0,12},{1,13},{2,14},{3,15},{4,0},{5,1},{6,2},{7,3},{8,4},{9,5},{1... | collective-permute-start | bytes 1572872 | tf_op jit(solution)/shard_map/ppermute | solution.py:17
  37.9 21.4 %copy-start.4 = (f32[1024,512]{0,1:T(8,128)S(1)}, f32[1024,512]{0,1:T(8,128)}, u32[]{:S(2)}) copy-start(f32[1024,512]{0,1:T(8,128)} %fusion.80) | copy-start | bytes 6291460
  54.9 44.3 %collective-permute-start.4 = (bf16[1024,256]{1,0:T(8,128)(2,1)S(1)}, bf16[1024,256]{1,0:T(8,128)(2,1)S(1)}, u32[]{:S(2)}, u32[]{:S(2)}) collective-permute-start(bf16[1024,256]{1,0:T(8,128)(2,1)S(1)} %copy-done.10), channel_id=1, source_target_pairs={{0,4},{1,5},{2,6},{3,7},{4,8},{5,9},{6,10},{7,11},{8,12},{9,13},{1... | collective-permute-start | bytes 1572872 | tf_op jit(solution)/shard_map/ppermute | solution.py:17
  57.0 47.2 %collective-permute-start.3 = (bf16[1024,256]{1,0:T(8,128)(2,1)S(1)}, bf16[1024,256]{1,0:T(8,128)(2,1)S(1)}, u32[]{:S(2)}, u32[]{:S(2)}) collective-permute-start(bf16[1024,256]{1,0:T(8,128)(2,1)S(1)} %copy-done.9), channel_id=1, source_target_pairs={{0,12},{1,13},{2,14},{3,15},{4,0},{5,1},{6,2},{7,3},{8,4},{9,5},{1... | collective-permute-start | bytes 1572872 | tf_op jit(solution)/shard_map/ppermute | solution.py:17
  62.6 36.2 %collective-permute-start.2 = (bf16[1024,256]{1,0:T(8,128)(2,1)S(1)}, bf16[1024,256]{1,0:T(8,128)(2,1)S(1)}, u32[]{:S(2)}, u32[]{:S(2)}) collective-permute-start(bf16[1024,256]{1,0:T(8,128)(2,1)S(1)} %copy-done.9), channel_id=1, source_target_pairs={{0,4},{1,5},{2,6},{3,7},{4,8},{5,9},{6,10},{7,11},{8,12},{9,13},{1... | collective-permute-start | bytes 1572872 | tf_op jit(solution)/shard_map/ppermute | solution.py:17
  110.6 24.1 %collective-permute-start.12 = (bf16[1024,256]{1,0:T(8,128)(2,1)S(1)}, bf16[1024,256]{1,0:T(8,128)(2,1)S(1)}, u32[]{:S(2)}, u32[]{:S(2)}) collective-permute-start(bf16[1024,256]{1,0:T(8,128)(2,1)S(1)} %get-tuple-element.42), channel_id=1, source_target_pairs={{0,12},{1,13},{2,14},{3,15},{4,0},{5,1},{6,2},{7,3},{8,4},{9,5},{1... | collective-permute-start | bytes 1572872 | tf_op jit(solution)/shard_map/ppermute | solution.py:17
  113.2 23.7 %collective-permute-start.13 = (bf16[1024,256]{1,0:T(8,128)(2,1)S(1)}, bf16[1024,256]{1,0:T(8,128)(2,1)S(1)}, u32[]{:S(2)}, u32[]{:S(2)}) collective-permute-start(bf16[1024,256]{1,0:T(8,128)(2,1)S(1)} %get-tuple-element.43), channel_id=1, source_target_pairs={{0,4},{1,5},{2,6},{3,7},{4,8},{5,9},{6,10},{7,11},{8,12},{9,13},{1... | collective-permute-start | bytes 1572872 | tf_op jit(solution)/shard_map/ppermute | solution.py:17
  119.3 2.5 %collective-permute-start.10 = (f32[229376]{0:T(1024)S(1)}, f32[229376]{0:T(1024)S(1)}, u32[]{:S(2)}, u32[]{:S(2)}) collective-permute-start(f32[229376]{0:T(1024)S(1)} %dynamic_slice.25), channel_id=1, source_target_pairs={{0,1},{1,0},{2,3},{3,2},{4,5},{5,4},{6,7},{7,6},{8,9},{9,8},{10,11... | collective-permute-start | bytes 2752520 | tf_op jit(solution)/shard_map/ppermute | solution.py:23
  122.0 12.6 %collective-permute-start.11 = (f32[114688]{0:T(1024)S(1)}, f32[114688]{0:T(1024)S(1)}, u32[]{:S(2)}, u32[]{:S(2)}) collective-permute-start(f32[114688]{0:T(1024)S(1)} %dynamic_slice.27), channel_id=1, source_target_pairs={{0,2},{1,3},{2,0},{3,1},{4,6},{5,7},{6,4},{7,5},{8,10},{9,11},{10,... | collective-permute-start | bytes 1376264 | tf_op jit(solution)/shard_map/ppermute | solution.py:23
  136.9 9.3 %collective-permute-start.14 = (f32[57344]{0:T(1024)S(1)}, f32[57344]{0:T(1024)S(1)}, u32[]{:S(2)}, u32[]{:S(2)}) collective-permute-start(f32[57344]{0:T(1024)S(1)} %dynamic_slice.29), channel_id=1, source_target_pairs={{0,4},{1,5},{2,6},{3,7},{4,0},{5,1},{6,2},{7,3},{8,12},{9,13},{10,... | collective-permute-start | bytes 688136 | tf_op jit(solution)/shard_map/ppermute | solution.py:23
  137.9 10.6 %collective-permute-start.16 = (bf16[256,256]{1,0:T(8,128)(2,1)S(1)}, bf16[256,256]{1,0:T(8,128)(2,1)S(1)}, u32[]{:S(2)}, u32[]{:S(2)}) collective-permute-start(bf16[256,256]{1,0:T(8,128)(2,1)S(1)} %slice.152), channel_id=1, source_target_pairs={{0,4},{1,5},{2,6},{3,7},{4,8},{5,9},{6,10},{7,11},{8,12},{9,13},{1... | collective-permute-start | bytes 393224 | tf_op jit(solution)/shard_map/ppermute | solution.py:17
  139.4 9.3 %collective-permute-start.15 = (bf16[256,256]{1,0:T(8,128)(2,1)S(1)}, bf16[256,256]{1,0:T(8,128)(2,1)S(1)}, u32[]{:S(2)}, u32[]{:S(2)}) collective-permute-start(bf16[256,256]{1,0:T(8,128)(2,1)S(1)} %slice.151), channel_id=1, source_target_pairs={{0,12},{1,13},{2,14},{3,15},{4,0},{5,1},{6,2},{7,3},{8,4},{9,5},{1... | collective-permute-start | bytes 393224 | tf_op jit(solution)/shard_map/ppermute | solution.py:17
  148.8 9.7 %collective-permute-start.17 = (f32[28672]{0:T(1024)S(1)}, f32[28672]{0:T(1024)S(1)}, u32[]{:S(2)}, u32[]{:S(2)}) collective-permute-start(f32[28672]{0:T(1024)S(1)} %dynamic_slice.31), channel_id=1, source_target_pairs={{0,8},{1,9},{2,10},{3,11},{4,12},{5,13},{6,14},{7,15},{8,0},{9,1},... | collective-permute-start | bytes 344072 | tf_op jit(solution)/shard_map/ppermute | solution.py:23
  151.1 7.4 %collective-permute-start.19 = (bf16[256,256]{1,0:T(8,128)(2,1)S(1)}, bf16[256,256]{1,0:T(8,128)(2,1)S(1)}, u32[]{:S(2)}, u32[]{:S(2)}) collective-permute-start(bf16[256,256]{1,0:T(8,128)(2,1)S(1)} %slice.154), channel_id=1, source_target_pairs={{0,4},{1,5},{2,6},{3,7},{4,8},{5,9},{6,10},{7,11},{8,12},{9,13},{1... | collective-permute-start | bytes 393224 | tf_op jit(solution)/shard_map/ppermute | solution.py:17
  152.0 8.1 %collective-permute-start.18 = (bf16[256,256]{1,0:T(8,128)(2,1)S(1)}, bf16[256,256]{1,0:T(8,128)(2,1)S(1)}, u32[]{:S(2)}, u32[]{:S(2)}) collective-permute-start(bf16[256,256]{1,0:T(8,128)(2,1)S(1)} %slice.153), channel_id=1, source_target_pairs={{0,12},{1,13},{2,14},{3,15},{4,0},{5,1},{6,2},{7,3},{8,4},{9,5},{1... | collective-permute-start | bytes 393224 | tf_op jit(solution)/shard_map/ppermute | solution.py:17
  160.1 6.7 %collective-permute-start.20 = (f32[28672]{0:T(1024)S(1)}, f32[28672]{0:T(1024)S(1)}, u32[]{:S(2)}, u32[]{:S(2)}) collective-permute-start(f32[28672]{0:T(1024)S(1)} %add_multiply_fusion), channel_id=1, source_target_pairs={{0,8},{1,9},{2,10},{3,11},{4,12},{5,13},{6,14},{7,15},{8,0},{9,1},... | collective-permute-start | bytes 344072 | tf_op jit(solution)/shard_map/ppermute | solution.py:23
  162.9 7.4 %collective-permute-start.22 = (bf16[256,256]{1,0:T(8,128)(2,1)S(1)}, bf16[256,256]{1,0:T(8,128)(2,1)S(1)}, u32[]{:S(2)}, u32[]{:S(2)}) collective-permute-start(bf16[256,256]{1,0:T(8,128)(2,1)S(1)} %slice.156), channel_id=1, source_target_pairs={{0,4},{1,5},{2,6},{3,7},{4,8},{5,9},{6,10},{7,11},{8,12},{9,13},{1... | collective-permute-start | bytes 393224 | tf_op jit(solution)/shard_map/ppermute | solution.py:17
  163.0 7.8 %collective-permute-start.21 = (bf16[256,256]{1,0:T(8,128)(2,1)S(1)}, bf16[256,256]{1,0:T(8,128)(2,1)S(1)}, u32[]{:S(2)}, u32[]{:S(2)}) collective-permute-start(bf16[256,256]{1,0:T(8,128)(2,1)S(1)} %slice.155), channel_id=1, source_target_pairs={{0,12},{1,13},{2,14},{3,15},{4,0},{5,1},{6,2},{7,3},{8,4},{9,5},{1... | collective-permute-start | bytes 393224 | tf_op jit(solution)/shard_map/ppermute | solution.py:17
  170.7 6.7 %collective-permute-start.23 = (f32[57344]{0:T(1024)S(1)}, f32[57344]{0:T(1024)S(1)}, u32[]{:S(2)}, u32[]{:S(2)}) collective-permute-start(f32[57344]{0:T(1024)S(1)} %pad_maximum_fusion.8), channel_id=1, source_target_pairs={{0,4},{1,5},{2,6},{3,7},{4,0},{5,1},{6,2},{7,3},{8,12},{9,13},{10,... | collective-permute-start | bytes 688136 | tf_op jit(solution)/shard_map/ppermute | solution.py:23
  171.4 9.3 %collective-permute-start.25 = (bf16[256,256]{1,0:T(8,128)(2,1)S(1)}, bf16[256,256]{1,0:T(8,128)(2,1)S(1)}, u32[]{:S(2)}, u32[]{:S(2)}) collective-permute-start(bf16[256,256]{1,0:T(8,128)(2,1)S(1)} %slice.158), channel_id=1, source_target_pairs={{0,4},{1,5},{2,6},{3,7},{4,8},{5,9},{6,10},{7,11},{8,12},{9,13},{1... | collective-permute-start | bytes 393224 | tf_op jit(solution)/shard_map/ppermute | solution.py:17
  172.9 7.8 %collective-permute-start.24 = (bf16[256,256]{1,0:T(8,128)(2,1)S(1)}, bf16[256,256]{1,0:T(8,128)(2,1)S(1)}, u32[]{:S(2)}, u32[]{:S(2)}) collective-permute-start(bf16[256,256]{1,0:T(8,128)(2,1)S(1)} %slice.157), channel_id=1, source_target_pairs={{0,12},{1,13},{2,14},{3,15},{4,0},{5,1},{6,2},{7,3},{8,4},{9,5},{1... | collective-permute-start | bytes 393224 | tf_op jit(solution)/shard_map/ppermute | solution.py:17
  180.7 22.0 %collective-permute-start.26 = (f32[114688]{0:T(1024)S(1)}, f32[114688]{0:T(1024)S(1)}, u32[]{:S(2)}, u32[]{:S(2)}) collective-permute-start(f32[114688]{0:T(1024)S(1)} %pad_maximum_fusion.7), channel_id=1, source_target_pairs={{0,2},{1,3},{2,0},{3,1},{4,6},{5,7},{6,4},{7,5},{8,10},{9,11},{10,... | collective-permute-start | bytes 1376264 | tf_op jit(solution)/shard_map/ppermute | solution.py:23
  184.7 30.3 %collective-permute-start.28 = (bf16[2048,256]{1,0:T(8,128)(2,1)S(1)}, bf16[2048,256]{1,0:T(8,128)(2,1)S(1)}, u32[]{:S(2)}, u32[]{:S(2)}) collective-permute-start(bf16[2048,256]{1,0:T(8,128)(2,1)S(1)} %slice.160), channel_id=1, source_target_pairs={{0,4},{1,5},{2,6},{3,7},{4,8},{5,9},{6,10},{7,11},{8,12},{9,13},{1... | collective-permute-start | bytes 3145736 | tf_op jit(solution)/shard_map/ppermute | solution.py:17
  202.7 23.6 %collective-permute-start.27 = (bf16[2048,256]{1,0:T(8,128)(2,1)S(1)}, bf16[2048,256]{1,0:T(8,128)(2,1)S(1)}, u32[]{:S(2)}, u32[]{:S(2)}) collective-permute-start(bf16[2048,256]{1,0:T(8,128)(2,1)S(1)} %slice.159), channel_id=1, source_target_pairs={{0,12},{1,13},{2,14},{3,15},{4,0},{5,1},{6,2},{7,3},{8,4},{9,5},{1... | collective-permute-start | bytes 3145736 | tf_op jit(solution)/shard_map/ppermute | solution.py:17
  226.2 2.5 %collective-permute-start.29 = (f32[229376]{0:T(1024)S(1)}, f32[229376]{0:T(1024)S(1)}, u32[]{:S(2)}, u32[]{:S(2)}) collective-permute-start(f32[229376]{0:T(1024)S(1)} %pad_maximum_fusion.4), channel_id=1, source_target_pairs={{0,1},{1,0},{2,3},{3,2},{4,5},{5,4},{6,7},{7,6},{8,9},{9,8},{10,11... | collective-permute-start | bytes 2752520 | tf_op jit(solution)/shard_map/ppermute | solution.py:23
  (9 other events, 70.5 us)

commit v5 on v4

--- a/solution.py
+++ b/solution.py
@@ -8,7 +8,8 @@
 TAP_SPACING = 16384
 CHUNK_EIGHTHS = (2, 2, 2, 1, 1)
 EARLY = 1
-RIDER_ROWS = 256
+RIDER_ROWS = 512
+RIDER_SPAN = 2
 
 
 def from_behind(value, axis, steps):
@@ -123,18 +124,19 @@
     steps = chain_steps(seq_size)
     rider_steps = [(4, True), (8, True), (8, False), (4, False)]
     sent_rows = bounds[EARLY]
-    pending = None
+    pending = []
     late = []
     for number, (bit, down) in enumerate(steps):
         if down and bit == 4:
             buf, early = lax.optimization_barrier((buf, early))
-        if pending is not None:
-            buf, pending = lax.optimization_barrier((buf, pending))
-            early.append(pending)
-            pending = None
+        due = [item for item in pending if item[1] <= number]
+        if due:
+            buf, landed = lax.optimization_barrier((buf, [item[0] for item in due]))
+            early.extend(landed)
+            pending = [item for item in pending if item[1] > number]
         if (bit, down) in rider_steps and sent_rows + RIDER_ROWS <= positions:
             buf, pieces = lax.optimization_barrier((buf, (lower_all, upper_all)))
-            pending = send_rows(pieces, sent_rows, sent_rows + RIDER_ROWS)
+            pending.append((send_rows(pieces, sent_rows, sent_rows + RIDER_ROWS), number + RIDER_SPAN))
             sent_rows += RIDER_ROWS
         if not down and bit == 2 and not late:
             buf, pieces = lax.optimization_barrier((buf, (lower_all, upper_all)))
@@ -147,8 +149,7 @@
             buf = buf * jnp.float32(norm_factor)
     if not steps:
         buf = buf * jnp.float32(norm_factor)
-    if pending is not None:
-        early.append(pending)
+    early.extend(item[0] for item in pending)
     if sent_rows < positions:
         late.append(send_rows((lower_all, upper_all), sent_rows, positions))
     received = early + late

time: 232 us -> 232 us (level)
  waiting for transfers between devices: 110 us -> 125 us
  starting transfers between devices: 68.1 us -> 54.1 us
    ppermute x8, waiting for transfers between devices: 21 us -> 39.5 us  [exchange(): return lax.ppermute(value, axis, pairs)]
    ppermute x22, starting transfers between devices: 56.4 us -> 42.2 us  [from_behind(): return lax.ppermute(value, axis, pairs)]
    ppermute x22, waiting for transfers between devices: 89 us -> 85.3 us  [from_behind(): return lax.ppermute(value, axis, pairs)]
where the time goes in v5:
time: 232 us
  waiting for transfers between devices  125 us (54%)
  starting transfers between devices  54.1 us (23%)
  matrix products  37.4 us (16%)
  local copies, waits for them, and re-layouts  9.13 us (4%)
  other arithmetic  5.02 us (2%)
    ppermute x22, waiting for transfers between devices, from_behind(): return lax.ppermute(value, axis, pairs)  85.3 us
    ppermute x22, starting transfers between devices, from_behind(): return lax.ppermute(value, axis, pairs)  42.2 us
    ppermute x8, waiting for transfers between devices, exchange(): return lax.ppermute(value, axis, pairs)  39.5 us
    ppermute x8, starting transfers between devices, exchange(): return lax.ppermute(value, axis, pairs)  11.9 us
    dot_general x5, matrix products, chunk_layer(): preact = preact + jnp.dot(middle, w_mid, preferred_element_type=jnp.float32)  8.97 us
    dot_general x5, matrix products, chunk_layer(): lax.dot_general(right_tap_input, grad_pre, first_dims, preferred_element_...  5.23 us
    dot_general x5, matrix products, chunk_layer(): jnp.dot(right_tap_input, w_high, preferred_element_type=jnp.float32)  5.13 us
  transfers between devices with their start and end apart: 30, of which 18 were waited for; matrix products, arithmetic and copies ran while one was open for 17% of the time, Pallas kernels for 0%

profile of v5, /device:TPU:0, one launch (start us, length us, event | category | flops | bytes accessed | tf_op | source)
XLA Modules:
  0.0 232.0 jit_solution(1181373892425046612)
XLA Ops:
  2.6 5.0 %collective-permute-start.9 = (bf16[512,256]{1,0:T(8,128)(2,1)}, bf16[512,256]{1,0:T(8,128)(2,1)}, u32[]{:S(2)}, u32[]{:S(2)}) collective-permute-start(bf16[512,256]{1,0:T(8,128)(2,1)} %get-tuple-element.83), channel_id=1, source_target_pairs={{0,12},{1,13},{2,14},{3,15},{4,0},{5,1},{6,2},{7,3},{8,4},{9,5},{1... | collective-permute-start | bytes 786440 | tf_op jit(solution)/shard_map/ppermute | solution.py:18
  7.7 3.8 %collective-permute-start.7 = (bf16[512,256]{1,0:T(8,128)(2,1)}, bf16[512,256]{1,0:T(8,128)(2,1)}, u32[]{:S(2)}, u32[]{:S(2)}) collective-permute-start(bf16[512,256]{1,0:T(8,128)(2,1)} %get-tuple-element.84), channel_id=1, source_target_pairs={{0,12},{1,13},{2,14},{3,15},{4,0},{5,1},{6,2},{7,3},{8,4},{9,5},{1... | collective-permute-start | bytes 786440 | tf_op jit(solution)/shard_map/ppermute | solution.py:18
  11.5 2.6 %fusion.113 = (bf16[1024,256]{1,0:T(8,128)(2,1)}, bf16[1024,256]{1,0:T(8,128)(2,1)}, bf16[1024,256]{1,0:T(8,128)(2,1)}) fusion(bf16[4096,256]{1,0:T(8,128)(2,1)} %param.4), kind=kLoop, calls=%fused_computation.203 | loop fusion | bytes 3145728 | tf_op jit(solution)/shard_map/slice | solution.py:95
  14.0 3.8 %collective-permute-start.1 = (bf16[1024,256]{1,0:T(8,128)(2,1)}, bf16[1024,256]{1,0:T(8,128)(2,1)}, u32[]{:S(2)}, u32[]{:S(2)}) collective-permute-start(bf16[1024,256]{1,0:T(8,128)(2,1)} %get-tuple-element.87), channel_id=1, source_target_pairs={{0,12},{1,13},{2,14},{3,15},{4,0},{5,1},{6,2},{7,3},{8,4},{9,5},{1... | collective-permute-start | bytes 1572872 | tf_op jit(solution)/shard_map/ppermute | solution.py:18
  17.9 2.4 %fusion.71 = f32[512,512]{0,1:T(8,128)} fusion(bf16[768,512]{1,0:T(8,128)(2,1)S(1)} %copy-done.2, bf16[4096,256]{1,0:T(8,128)(2,1)} %param.4), kind=kOutput, calls=%fused_computation.166 | convolution fusion | flops 134217728 | bytes 1572864 | tf_op jit(solution)/shard_map/dot_general | solution.py:56
  20.3 2.9 %fusion.74 = f32[1024,512]{0,1:T(8,128)} fusion(bf16[768,512]{1,0:T(8,128)(2,1)S(1)} %copy-done.2, bf16[4096,256]{1,0:T(8,128)(2,1)} %param.4), kind=kOutput, calls=%fused_computation.169 | convolution fusion | flops 268435456 | bytes 2883584 | tf_op jit(solution)/shard_map/dot_general | solution.py:56
  28.8 3.6 %collective-permute-done.6 = bf16[512,256]{1,0:T(8,128)(2,1)S(1)} collective-permute-done((bf16[512,256]{1,0:T(8,128)(2,1)}, bf16[512,256]{1,0:T(8,128)(2,1)S(1)}, u32[]{:S(2)}, u32[]{:S(2)}) %collective-permute-start.6) | collective-permute-done | bytes 262176 | tf_op jit(solution)/shard_map/ppermute | solution.py:18
  32.4 2.8 %collective-permute-start.5 = (bf16[1024,256]{1,0:T(8,128)(2,1)S(1)}, bf16[1024,256]{1,0:T(8,128)(2,1)S(1)}, u32[]{:S(2)}, u32[]{:S(2)}) collective-permute-start(bf16[1024,256]{1,0:T(8,128)(2,1)S(1)} %copy-done.10), channel_id=1, source_target_pairs={{0,12},{1,13},{2,14},{3,15},{4,0},{5,1},{6,2},{7,3},{8,4},{9,5},{1... | collective-permute-start | bytes 1572872 | tf_op jit(solution)/shard_map/ppermute | solution.py:18
  39.4 15.6 %collective-permute-done = bf16[1024,256]{1,0:T(8,128)(2,1)S(1)} collective-permute-done((bf16[1024,256]{1,0:T(8,128)(2,1)}, bf16[1024,256]{1,0:T(8,128)(2,1)S(1)}, u32[]{:S(2)}, u32[]{:S(2)}) %collective-permute-start) | collective-permute-done | bytes 524320 | tf_op jit(solution)/shard_map/ppermute | solution.py:18
  57.0 2.3 %collective-permute-start.3 = (bf16[1024,256]{1,0:T(8,128)(2,1)S(1)}, bf16[1024,256]{1,0:T(8,128)(2,1)S(1)}, u32[]{:S(2)}, u32[]{:S(2)}) collective-permute-start(bf16[1024,256]{1,0:T(8,128)(2,1)S(1)} %copy-done.9), channel_id=1, source_target_pairs={{0,12},{1,13},{2,14},{3,15},{4,0},{5,1},{6,2},{7,3},{8,4},{9,5},{1... | collective-permute-start | bytes 1572872 | tf_op jit(solution)/shard_map/ppermute | solution.py:18
  65.7 33.0 %collective-permute-done.2 = bf16[1024,256]{1,0:T(8,128)(2,1)S(1)} collective-permute-done((bf16[1024,256]{1,0:T(8,128)(2,1)S(1)}, bf16[1024,256]{1,0:T(8,128)(2,1)S(1)}, u32[]{:S(2)}, u32[]{:S(2)}) %collective-permute-start.2) | collective-permute-done | bytes 524320 | tf_op jit(solution)/shard_map/ppermute | solution.py:18
  110.2 2.6 %collective-permute-start.12 = (bf16[1024,256]{1,0:T(8,128)(2,1)S(1)}, bf16[1024,256]{1,0:T(8,128)(2,1)S(1)}, u32[]{:S(2)}, u32[]{:S(2)}) collective-permute-start(bf16[1024,256]{1,0:T(8,128)(2,1)S(1)} %get-tuple-element.42), channel_id=1, source_target_pairs={{0,12},{1,13},{2,14},{3,15},{4,0},{5,1},{6,2},{7,3},{8,4},{9,5},{1... | collective-permute-start | bytes 1572872 | tf_op jit(solution)/shard_map/ppermute | solution.py:18
  124.0 10.2 %collective-permute-done.11 = f32[114688]{0:T(1024)S(1)} collective-permute-done((f32[114688]{0:T(1024)S(1)}, f32[114688]{0:T(1024)S(1)}, u32[]{:S(2)}, u32[]{:S(2)}) %collective-permute-start.11) | collective-permute-done | bytes 458784 | tf_op jit(solution)/shard_map/ppermute | solution.py:24
  134.3 2.1 collective-permute-done.13
  137.4 5.3 %collective-permute-done.14 = f32[57344]{0:T(1024)S(1)} collective-permute-done((f32[57344]{0:T(1024)S(1)}, f32[57344]{0:T(1024)S(1)}, u32[]{:S(2)}, u32[]{:S(2)}) %collective-permute-start.14) | collective-permute-done | bytes 229408 | tf_op jit(solution)/shard_map/ppermute | solution.py:24
  146.3 2.4 %collective-permute-start.16 = (bf16[512,256]{1,0:T(8,128)(2,1)S(1)}, bf16[512,256]{1,0:T(8,128)(2,1)S(1)}, u32[]{:S(2)}, u32[]{:S(2)}) collective-permute-start(bf16[512,256]{1,0:T(8,128)(2,1)S(1)} %slice.151), channel_id=1, source_target_pairs={{0,12},{1,13},{2,14},{3,15},{4,0},{5,1},{6,2},{7,3},{8,4},{9,5},{1... | collective-permute-start | bytes 786440 | tf_op jit(solution)/shard_map/ppermute | solution.py:18
  148.8 7.8 %collective-permute-done.15 = f32[28672]{0:T(1024)S(1)} collective-permute-done((f32[28672]{0:T(1024)S(1)}, f32[28672]{0:T(1024)S(1)}, u32[]{:S(2)}, u32[]{:S(2)}) %collective-permute-start.15) | collective-permute-done | bytes 114720 | tf_op jit(solution)/shard_map/ppermute | solution.py:24
  156.6 2.7 %collective-permute-done.16 = bf16[512,256]{1,0:T(8,128)(2,1)S(1)} collective-permute-done((bf16[512,256]{1,0:T(8,128)(2,1)S(1)}, bf16[512,256]{1,0:T(8,128)(2,1)S(1)}, u32[]{:S(2)}, u32[]{:S(2)}) %collective-permute-start.16) | collective-permute-done | bytes 262176 | tf_op jit(solution)/shard_map/ppermute | solution.py:18
  159.3 3.8 %collective-permute-start.18 = (f32[28672]{0:T(1024)S(1)}, f32[28672]{0:T(1024)S(1)}, u32[]{:S(2)}, u32[]{:S(2)}) collective-permute-start(f32[28672]{0:T(1024)S(1)} %add_multiply_fusion), channel_id=1, source_target_pairs={{0,8},{1,9},{2,10},{3,11},{4,12},{5,13},{6,14},{7,15},{8,0},{9,1},... | collective-permute-start | bytes 344072 | tf_op jit(solution)/shard_map/ppermute | solution.py:24
  163.3 3.8 %collective-permute-start.19 = (bf16[512,256]{1,0:T(8,128)(2,1)S(1)}, bf16[512,256]{1,0:T(8,128)(2,1)S(1)}, u32[]{:S(2)}, u32[]{:S(2)}) collective-permute-start(bf16[512,256]{1,0:T(8,128)(2,1)S(1)} %slice.153), channel_id=1, source_target_pairs={{0,12},{1,13},{2,14},{3,15},{4,0},{5,1},{6,2},{7,3},{8,4},{9,5},{1... | collective-permute-start | bytes 786440 | tf_op jit(solution)/shard_map/ppermute | solution.py:18
  167.2 3.8 %collective-permute-start.22 = (bf16[512,256]{1,0:T(8,128)(2,1)S(1)}, bf16[512,256]{1,0:T(8,128)(2,1)S(1)}, u32[]{:S(2)}, u32[]{:S(2)}) collective-permute-start(bf16[512,256]{1,0:T(8,128)(2,1)S(1)} %slice.155), channel_id=1, source_target_pairs={{0,12},{1,13},{2,14},{3,15},{4,0},{5,1},{6,2},{7,3},{8,4},{9,5},{1... | collective-permute-start | bytes 786440 | tf_op jit(solution)/shard_map/ppermute | solution.py:18
  171.0 2.7 %collective-permute-done.18 = f32[28672]{0:T(1024)S(1)} collective-permute-done((f32[28672]{0:T(1024)S(1)}, f32[28672]{0:T(1024)S(1)}, u32[]{:S(2)}, u32[]{:S(2)}) %collective-permute-start.18) | collective-permute-done | bytes 114720 | tf_op jit(solution)/shard_map/ppermute | solution.py:24
  174.3 8.5 %collective-permute-done.19 = bf16[512,256]{1,0:T(8,128)(2,1)S(1)} collective-permute-done((bf16[512,256]{1,0:T(8,128)(2,1)S(1)}, bf16[512,256]{1,0:T(8,128)(2,1)S(1)}, u32[]{:S(2)}, u32[]{:S(2)}) %collective-permute-start.19) | collective-permute-done | bytes 262176 | tf_op jit(solution)/shard_map/ppermute | solution.py:18
  182.8 2.6 %collective-permute-start.21 = (f32[57344]{0:T(1024)S(1)}, f32[57344]{0:T(1024)S(1)}, u32[]{:S(2)}, u32[]{:S(2)}) collective-permute-start(f32[57344]{0:T(1024)S(1)} %pad_maximum_fusion.8), channel_id=1, source_target_pairs={{0,4},{1,5},{2,6},{3,7},{4,0},{5,1},{6,2},{7,3},{8,12},{9,13},{10,... | collective-permute-start | bytes 688136 | tf_op jit(solution)/shard_map/ppermute | solution.py:24
  185.6 3.8 %collective-permute-start.25 = (bf16[512,256]{1,0:T(8,128)(2,1)S(1)}, bf16[512,256]{1,0:T(8,128)(2,1)S(1)}, u32[]{:S(2)}, u32[]{:S(2)}) collective-permute-start(bf16[512,256]{1,0:T(8,128)(2,1)S(1)} %slice.157), channel_id=1, source_target_pairs={{0,12},{1,13},{2,14},{3,15},{4,0},{5,1},{6,2},{7,3},{8,4},{9,5},{1... | collective-permute-start | bytes 786440 | tf_op jit(solution)/shard_map/ppermute | solution.py:18
  189.5 9.5 %collective-permute-done.21 = f32[57344]{0:T(1024)S(1)} collective-permute-done((f32[57344]{0:T(1024)S(1)}, f32[57344]{0:T(1024)S(1)}, u32[]{:S(2)}, u32[]{:S(2)}) %collective-permute-start.21) | collective-permute-done | bytes 229408 | tf_op jit(solution)/shard_map/ppermute | solution.py:24
  200.9 3.8 %collective-permute-start.27 = (bf16[1024,256]{1,0:T(8,128)(2,1)S(1)}, bf16[1024,256]{1,0:T(8,128)(2,1)S(1)}, u32[]{:S(2)}, u32[]{:S(2)}) collective-permute-start(bf16[1024,256]{1,0:T(8,128)(2,1)S(1)} %slice.159), channel_id=1, source_target_pairs={{0,12},{1,13},{2,14},{3,15},{4,0},{5,1},{6,2},{7,3},{8,4},{9,5},{1... | collective-permute-start | bytes 1572872 | tf_op jit(solution)/shard_map/ppermute | solution.py:18
  204.7 2.9 %collective-permute-done.24 = f32[114688]{0:T(1024)S(1)} collective-permute-done((f32[114688]{0:T(1024)S(1)}, f32[114688]{0:T(1024)S(1)}, u32[]{:S(2)}, u32[]{:S(2)}) %collective-permute-start.24) | collective-permute-done | bytes 458784 | tf_op jit(solution)/shard_map/ppermute | solution.py:24
  207.8 8.0 %collective-permute-done.25 = bf16[512,256]{1,0:T(8,128)(2,1)S(1)} collective-permute-done((bf16[512,256]{1,0:T(8,128)(2,1)S(1)}, bf16[512,256]{1,0:T(8,128)(2,1)S(1)}, u32[]{:S(2)}, u32[]{:S(2)}) %collective-permute-start.25) | collective-permute-done | bytes 262176 | tf_op jit(solution)/shard_map/ppermute | solution.py:18
  215.9 2.7 %collective-permute-done.28 = bf16[1024,256]{1,0:T(8,128)(2,1)S(1)} collective-permute-done((bf16[1024,256]{1,0:T(8,128)(2,1)S(1)}, bf16[1024,256]{1,0:T(8,128)(2,1)S(1)}, u32[]{:S(2)}, u32[]{:S(2)}) %collective-permute-start.28) | collective-permute-done | bytes 524320 | tf_op jit(solution)/shard_map/ppermute | solution.py:18
  218.6 8.4 %collective-permute-done.27 = bf16[1024,256]{1,0:T(8,128)(2,1)S(1)} collective-permute-done((bf16[1024,256]{1,0:T(8,128)(2,1)S(1)}, bf16[1024,256]{1,0:T(8,128)(2,1)S(1)}, u32[]{:S(2)}, u32[]{:S(2)}) %collective-permute-start.27) | collective-permute-done | bytes 524320 | tf_op jit(solution)/shard_map/ppermute | solution.py:18
  227.1 2.2 add_convert_fusion
  (154 shorter events, 52.7 us)
Async XLA Ops:
  0.6 35.0 %copy-start = (bf16[256,256]{1,0:T(8,128)(2,1)S(1)}, bf16[256,256]{1,0:T(8,128)(2,1)}, u32[]{:S(2)}) copy-start(bf16[256,256]{1,0:T(8,128)(2,1)} %param.7) | copy-start | bytes 393220
  2.6 60.0 %collective-permute-start.9 = (bf16[512,256]{1,0:T(8,128)(2,1)}, bf16[512,256]{1,0:T(8,128)(2,1)}, u32[]{:S(2)}, u32[]{:S(2)}) collective-permute-start(bf16[512,256]{1,0:T(8,128)(2,1)} %get-tuple-element.83), channel_id=1, source_target_pairs={{0,12},{1,13},{2,14},{3,15},{4,0},{5,1},{6,2},{7,3},{8,4},{9,5},{1... | collective-permute-start | bytes 786440 | tf_op jit(solution)/shard_map/ppermute | solution.py:18
  7.6 55.2 %collective-permute-start.8 = (bf16[512,256]{1,0:T(8,128)(2,1)}, bf16[512,256]{1,0:T(8,128)(2,1)S(1)}, u32[]{:S(2)}, u32[]{:S(2)}) collective-permute-start(bf16[512,256]{1,0:T(8,128)(2,1)} %get-tuple-element.83), channel_id=1, source_target_pairs={{0,4},{1,5},{2,6},{3,7},{4,8},{5,9},{6,10},{7,11},{8,12},{9,13},{1... | collective-permute-start | bytes 786440 | tf_op jit(solution)/shard_map/ppermute | solution.py:18
  7.7 19.2 %collective-permute-start.7 = (bf16[512,256]{1,0:T(8,128)(2,1)}, bf16[512,256]{1,0:T(8,128)(2,1)}, u32[]{:S(2)}, u32[]{:S(2)}) collective-permute-start(bf16[512,256]{1,0:T(8,128)(2,1)} %get-tuple-element.84), channel_id=1, source_target_pairs={{0,12},{1,13},{2,14},{3,15},{4,0},{5,1},{6,2},{7,3},{8,4},{9,5},{1... | collective-permute-start | bytes 786440 | tf_op jit(solution)/shard_map/ppermute | solution.py:18
  11.5 20.9 %collective-permute-start.6 = (bf16[512,256]{1,0:T(8,128)(2,1)}, bf16[512,256]{1,0:T(8,128)(2,1)S(1)}, u32[]{:S(2)}, u32[]{:S(2)}) collective-permute-start(bf16[512,256]{1,0:T(8,128)(2,1)} %get-tuple-element.84), channel_id=1, source_target_pairs={{0,4},{1,5},{2,6},{3,7},{4,8},{5,9},{6,10},{7,11},{8,12},{9,13},{1... | collective-permute-start | bytes 786440 | tf_op jit(solution)/shard_map/ppermute | solution.py:18
  14.0 42.9 %collective-permute-start.1 = (bf16[1024,256]{1,0:T(8,128)(2,1)}, bf16[1024,256]{1,0:T(8,128)(2,1)}, u32[]{:S(2)}, u32[]{:S(2)}) collective-permute-start(bf16[1024,256]{1,0:T(8,128)(2,1)} %get-tuple-element.87), channel_id=1, source_target_pairs={{0,12},{1,13},{2,14},{3,15},{4,0},{5,1},{6,2},{7,3},{8,4},{9,5},{1... | collective-permute-start | bytes 1572872 | tf_op jit(solution)/shard_map/ppermute | solution.py:18
  26.9 28.1 %collective-permute-start = (bf16[1024,256]{1,0:T(8,128)(2,1)}, bf16[1024,256]{1,0:T(8,128)(2,1)S(1)}, u32[]{:S(2)}, u32[]{:S(2)}) collective-permute-start(bf16[1024,256]{1,0:T(8,128)(2,1)} %get-tuple-element.87), channel_id=1, source_target_pairs={{0,4},{1,5},{2,6},{3,7},{4,8},{5,9},{6,10},{7,11},{8,12},{9,13},{1... | collective-permute-start | bytes 1572872 | tf_op jit(solution)/shard_map/ppermute | solution.py:18
  32.4 69.2 %collective-permute-start.5 = (bf16[1024,256]{1,0:T(8,128)(2,1)S(1)}, bf16[1024,256]{1,0:T(8,128)(2,1)S(1)}, u32[]{:S(2)}, u32[]{:S(2)}) collective-permute-start(bf16[1024,256]{1,0:T(8,128)(2,1)S(1)} %copy-done.10), channel_id=1, source_target_pairs={{0,12},{1,13},{2,14},{3,15},{4,0},{5,1},{6,2},{7,3},{8,4},{9,5},{1... | collective-permute-start | bytes 1572872 | tf_op jit(solution)/shard_map/ppermute | solution.py:18
  37.9 21.4 %copy-start.4 = (f32[1024,512]{0,1:T(8,128)S(1)}, f32[1024,512]{0,1:T(8,128)}, u32[]{:S(2)}) copy-start(f32[1024,512]{0,1:T(8,128)} %fusion.80) | copy-start | bytes 6291460
  54.9 44.3 %collective-permute-start.4 = (bf16[1024,256]{1,0:T(8,128)(2,1)S(1)}, bf16[1024,256]{1,0:T(8,128)(2,1)S(1)}, u32[]{:S(2)}, u32[]{:S(2)}) collective-permute-start(bf16[1024,256]{1,0:T(8,128)(2,1)S(1)} %copy-done.10), channel_id=1, source_target_pairs={{0,4},{1,5},{2,6},{3,7},{4,8},{5,9},{6,10},{7,11},{8,12},{9,13},{1... | collective-permute-start | bytes 1572872 | tf_op jit(solution)/shard_map/ppermute | solution.py:18
  57.0 47.3 %collective-permute-start.3 = (bf16[1024,256]{1,0:T(8,128)(2,1)S(1)}, bf16[1024,256]{1,0:T(8,128)(2,1)S(1)}, u32[]{:S(2)}, u32[]{:S(2)}) collective-permute-start(bf16[1024,256]{1,0:T(8,128)(2,1)S(1)} %copy-done.9), channel_id=1, source_target_pairs={{0,12},{1,13},{2,14},{3,15},{4,0},{5,1},{6,2},{7,3},{8,4},{9,5},{1... | collective-permute-start | bytes 1572872 | tf_op jit(solution)/shard_map/ppermute | solution.py:18
  62.6 36.2 %collective-permute-start.2 = (bf16[1024,256]{1,0:T(8,128)(2,1)S(1)}, bf16[1024,256]{1,0:T(8,128)(2,1)S(1)}, u32[]{:S(2)}, u32[]{:S(2)}) collective-permute-start(bf16[1024,256]{1,0:T(8,128)(2,1)S(1)} %copy-done.9), channel_id=1, source_target_pairs={{0,4},{1,5},{2,6},{3,7},{4,8},{5,9},{6,10},{7,11},{8,12},{9,13},{1... | collective-permute-start | bytes 1572872 | tf_op jit(solution)/shard_map/ppermute | solution.py:18
  110.2 24.1 %collective-permute-start.12 = (bf16[1024,256]{1,0:T(8,128)(2,1)S(1)}, bf16[1024,256]{1,0:T(8,128)(2,1)S(1)}, u32[]{:S(2)}, u32[]{:S(2)}) collective-permute-start(bf16[1024,256]{1,0:T(8,128)(2,1)S(1)} %get-tuple-element.42), channel_id=1, source_target_pairs={{0,12},{1,13},{2,14},{3,15},{4,0},{5,1},{6,2},{7,3},{8,4},{9,5},{1... | collective-permute-start | bytes 1572872 | tf_op jit(solution)/shard_map/ppermute | solution.py:18
  112.8 23.7 %collective-permute-start.13 = (bf16[1024,256]{1,0:T(8,128)(2,1)S(1)}, bf16[1024,256]{1,0:T(8,128)(2,1)S(1)}, u32[]{:S(2)}, u32[]{:S(2)}) collective-permute-start(bf16[1024,256]{1,0:T(8,128)(2,1)S(1)} %get-tuple-element.43), channel_id=1, source_target_pairs={{0,4},{1,5},{2,6},{3,7},{4,8},{5,9},{6,10},{7,11},{8,12},{9,13},{1... | collective-permute-start | bytes 1572872 | tf_op jit(solution)/shard_map/ppermute | solution.py:18
  119.0 2.5 %collective-permute-start.10 = (f32[229376]{0:T(1024)S(1)}, f32[229376]{0:T(1024)S(1)}, u32[]{:S(2)}, u32[]{:S(2)}) collective-permute-start(f32[229376]{0:T(1024)S(1)} %dynamic_slice.25), channel_id=1, source_target_pairs={{0,1},{1,0},{2,3},{3,2},{4,5},{5,4},{6,7},{7,6},{8,9},{9,8},{10,11... | collective-permute-start | bytes 2752520 | tf_op jit(solution)/shard_map/ppermute | solution.py:24
  121.7 12.6 %collective-permute-start.11 = (f32[114688]{0:T(1024)S(1)}, f32[114688]{0:T(1024)S(1)}, u32[]{:S(2)}, u32[]{:S(2)}) collective-permute-start(f32[114688]{0:T(1024)S(1)} %dynamic_slice.27), channel_id=1, source_target_pairs={{0,2},{1,3},{2,0},{3,1},{4,6},{5,7},{6,4},{7,5},{8,10},{9,11},{10,... | collective-permute-start | bytes 1376264 | tf_op jit(solution)/shard_map/ppermute | solution.py:24
  136.5 6.3 %collective-permute-start.14 = (f32[57344]{0:T(1024)S(1)}, f32[57344]{0:T(1024)S(1)}, u32[]{:S(2)}, u32[]{:S(2)}) collective-permute-start(f32[57344]{0:T(1024)S(1)} %dynamic_slice.29), channel_id=1, source_target_pairs={{0,4},{1,5},{2,6},{3,7},{4,0},{5,1},{6,2},{7,3},{8,12},{9,13},{10,... | collective-permute-start | bytes 688136 | tf_op jit(solution)/shard_map/ppermute | solution.py:24
  142.8 13.8 %collective-permute-start.15 = (f32[28672]{0:T(1024)S(1)}, f32[28672]{0:T(1024)S(1)}, u32[]{:S(2)}, u32[]{:S(2)}) collective-permute-start(f32[28672]{0:T(1024)S(1)} %dynamic_slice.31), channel_id=1, source_target_pairs={{0,8},{1,9},{2,10},{3,11},{4,12},{5,13},{6,14},{7,15},{8,0},{9,1},... | collective-permute-start | bytes 344072 | tf_op jit(solution)/shard_map/ppermute | solution.py:24
  144.9 11.7 %collective-permute-start.17 = (bf16[512,256]{1,0:T(8,128)(2,1)S(1)}, bf16[512,256]{1,0:T(8,128)(2,1)S(1)}, u32[]{:S(2)}, u32[]{:S(2)}) collective-permute-start(bf16[512,256]{1,0:T(8,128)(2,1)S(1)} %slice.152), channel_id=1, source_target_pairs={{0,4},{1,5},{2,6},{3,7},{4,8},{5,9},{6,10},{7,11},{8,12},{9,13},{1... | collective-permute-start | bytes 786440 | tf_op jit(solution)/shard_map/ppermute | solution.py:18
  146.3 12.9 %collective-permute-start.16 = (bf16[512,256]{1,0:T(8,128)(2,1)S(1)}, bf16[512,256]{1,0:T(8,128)(2,1)S(1)}, u32[]{:S(2)}, u32[]{:S(2)}) collective-permute-start(bf16[512,256]{1,0:T(8,128)(2,1)S(1)} %slice.151), channel_id=1, source_target_pairs={{0,12},{1,13},{2,14},{3,15},{4,0},{5,1},{6,2},{7,3},{8,4},{9,5},{1... | collective-permute-start | bytes 786440 | tf_op jit(solution)/shard_map/ppermute | solution.py:18
  159.3 14.4 %collective-permute-start.18 = (f32[28672]{0:T(1024)S(1)}, f32[28672]{0:T(1024)S(1)}, u32[]{:S(2)}, u32[]{:S(2)}) collective-permute-start(f32[28672]{0:T(1024)S(1)} %add_multiply_fusion), channel_id=1, source_target_pairs={{0,8},{1,9},{2,10},{3,11},{4,12},{5,13},{6,14},{7,15},{8,0},{9,1},... | collective-permute-start | bytes 344072 | tf_op jit(solution)/shard_map/ppermute | solution.py:24
  163.2 11.1 %collective-permute-start.20 = (bf16[512,256]{1,0:T(8,128)(2,1)S(1)}, bf16[512,256]{1,0:T(8,128)(2,1)S(1)}, u32[]{:S(2)}, u32[]{:S(2)}) collective-permute-start(bf16[512,256]{1,0:T(8,128)(2,1)S(1)} %slice.154), channel_id=1, source_target_pairs={{0,4},{1,5},{2,6},{3,7},{4,8},{5,9},{6,10},{7,11},{8,12},{9,13},{1... | collective-permute-start | bytes 786440 | tf_op jit(solution)/shard_map/ppermute | solution.py:18
  163.3 19.6 %collective-permute-start.19 = (bf16[512,256]{1,0:T(8,128)(2,1)S(1)}, bf16[512,256]{1,0:T(8,128)(2,1)S(1)}, u32[]{:S(2)}, u32[]{:S(2)}) collective-permute-start(bf16[512,256]{1,0:T(8,128)(2,1)S(1)} %slice.153), channel_id=1, source_target_pairs={{0,12},{1,13},{2,14},{3,15},{4,0},{5,1},{6,2},{7,3},{8,4},{9,5},{1... | collective-permute-start | bytes 786440 | tf_op jit(solution)/shard_map/ppermute | solution.py:18
  167.1 31.9 %collective-permute-start.23 = (bf16[512,256]{1,0:T(8,128)(2,1)S(1)}, bf16[512,256]{1,0:T(8,128)(2,1)S(1)}, u32[]{:S(2)}, u32[]{:S(2)}) collective-permute-start(bf16[512,256]{1,0:T(8,128)(2,1)S(1)} %slice.156), channel_id=1, source_target_pairs={{0,4},{1,5},{2,6},{3,7},{4,8},{5,9},{6,10},{7,11},{8,12},{9,13},{1... | collective-permute-start | bytes 786440 | tf_op jit(solution)/shard_map/ppermute | solution.py:18
  167.2 31.9 %collective-permute-start.22 = (bf16[512,256]{1,0:T(8,128)(2,1)S(1)}, bf16[512,256]{1,0:T(8,128)(2,1)S(1)}, u32[]{:S(2)}, u32[]{:S(2)}) collective-permute-start(bf16[512,256]{1,0:T(8,128)(2,1)S(1)} %slice.155), channel_id=1, source_target_pairs={{0,12},{1,13},{2,14},{3,15},{4,0},{5,1},{6,2},{7,3},{8,4},{9,5},{1... | collective-permute-start | bytes 786440 | tf_op jit(solution)/shard_map/ppermute | solution.py:18
  182.8 16.2 %collective-permute-start.21 = (f32[57344]{0:T(1024)S(1)}, f32[57344]{0:T(1024)S(1)}, u32[]{:S(2)}, u32[]{:S(2)}) collective-permute-start(f32[57344]{0:T(1024)S(1)} %pad_maximum_fusion.8), channel_id=1, source_target_pairs={{0,4},{1,5},{2,6},{3,7},{4,0},{5,1},{6,2},{7,3},{8,12},{9,13},{10,... | collective-permute-start | bytes 688136 | tf_op jit(solution)/shard_map/ppermute | solution.py:24
  185.6 22.2 %collective-permute-start.26 = (bf16[512,256]{1,0:T(8,128)(2,1)S(1)}, bf16[512,256]{1,0:T(8,128)(2,1)S(1)}, u32[]{:S(2)}, u32[]{:S(2)}) collective-permute-start(bf16[512,256]{1,0:T(8,128)(2,1)S(1)} %slice.158), channel_id=1, source_target_pairs={{0,4},{1,5},{2,6},{3,7},{4,8},{5,9},{6,10},{7,11},{8,12},{9,13},{1... | collective-permute-start | bytes 786440 | tf_op jit(solution)/shard_map/ppermute | solution.py:18
  185.6 30.2 %collective-permute-start.25 = (bf16[512,256]{1,0:T(8,128)(2,1)S(1)}, bf16[512,256]{1,0:T(8,128)(2,1)S(1)}, u32[]{:S(2)}, u32[]{:S(2)}) collective-permute-start(bf16[512,256]{1,0:T(8,128)(2,1)S(1)} %slice.157), channel_id=1, source_target_pairs={{0,12},{1,13},{2,14},{3,15},{4,0},{5,1},{6,2},{7,3},{8,4},{9,5},{1... | collective-permute-start | bytes 786440 | tf_op jit(solution)/shard_map/ppermute | solution.py:18
  199.1 8.5 %collective-permute-start.24 = (f32[114688]{0:T(1024)S(1)}, f32[114688]{0:T(1024)S(1)}, u32[]{:S(2)}, u32[]{:S(2)}) collective-permute-start(f32[114688]{0:T(1024)S(1)} %pad_maximum_fusion.7), channel_id=1, source_target_pairs={{0,2},{1,3},{2,0},{3,1},{4,6},{5,7},{6,4},{7,5},{8,10},{9,11},{10,... | collective-permute-start | bytes 1376264 | tf_op jit(solution)/shard_map/ppermute | solution.py:24
  200.8 17.8 %collective-permute-start.28 = (bf16[1024,256]{1,0:T(8,128)(2,1)S(1)}, bf16[1024,256]{1,0:T(8,128)(2,1)S(1)}, u32[]{:S(2)}, u32[]{:S(2)}) collective-permute-start(bf16[1024,256]{1,0:T(8,128)(2,1)S(1)} %slice.160), channel_id=1, source_target_pairs={{0,4},{1,5},{2,6},{3,7},{4,8},{5,9},{6,10},{7,11},{8,12},{9,13},{1... | collective-permute-start | bytes 1572872 | tf_op jit(solution)/shard_map/ppermute | solution.py:18
  200.9 26.1 %collective-permute-start.27 = (bf16[1024,256]{1,0:T(8,128)(2,1)S(1)}, bf16[1024,256]{1,0:T(8,128)(2,1)S(1)}, u32[]{:S(2)}, u32[]{:S(2)}) collective-permute-start(bf16[1024,256]{1,0:T(8,128)(2,1)S(1)} %slice.159), channel_id=1, source_target_pairs={{0,12},{1,13},{2,14},{3,15},{4,0},{5,1},{6,2},{7,3},{8,4},{9,5},{1... | collective-permute-start | bytes 1572872 | tf_op jit(solution)/shard_map/ppermute | solution.py:18
  227.0 2.5 %collective-permute-start.29 = (f32[229376]{0:T(1024)S(1)}, f32[229376]{0:T(1024)S(1)}, u32[]{:S(2)}, u32[]{:S(2)}) collective-permute-start(f32[229376]{0:T(1024)S(1)} %pad_maximum_fusion.4), channel_id=1, source_target_pairs={{0,1},{1,0},{2,3},{3,2},{4,5},{5,4},{6,7},{7,6},{8,9},{9,8},{10,11... | collective-permute-start | bytes 2752520 | tf_op jit(solution)/shard_map/ppermute | solution.py:24
  (9 other events, 70.5 us)

commit v6 on v5

--- a/solution.py
+++ b/solution.py
@@ -102,6 +102,10 @@
             )
             for low, high in zip(lows_early, highs_early):
                 early.append((from_behind(low, "seq", -spacing), from_behind(high, "seq", spacing)))
+        if wconv_total is not None:
+            left_tap_input, right_tap_input, wconv_total, wout_total = lax.optimization_barrier(
+                (left_tap_input, right_tap_input, wconv_total, wout_total)
+            )
         grad_wconv, grad_wout, lower_term, term_mid, upper_term = chunk_layer(
             left_tap_input, middle, right_tap_input, grad_in, conv_weight, out_weight
         )

time: 232 us -> 232 us (level)
  starting transfers between devices: 54.1 us -> 85.8 us
  waiting for transfers between devices: 125 us -> 95 us
  matrix products: 37.4 us -> 33.5 us
    ppermute x22, starting transfers between devices: 42.2 us -> 73.7 us  [from_behind(): return lax.ppermute(value, axis, pairs)]
    ppermute x22, waiting for transfers between devices: 85.3 us -> 68.6 us  [from_behind(): return lax.ppermute(value, axis, pairs)]
    ppermute x8, waiting for transfers between devices: 39.5 us -> 26.3 us  [exchange(): return lax.ppermute(value, axis, pairs)]
    dot_general x5, matrix products: 8.97 us -> 4.65 us  [chunk_layer(): preact = preact + jnp.dot(middle, w_mid, preferred_element_type=jnp.float32)]
  transfers between devices with their start and end apart: 30 -> 30, of which waited for: 18 -> 19; matrix products, arithmetic and copies ran while one was open for 17% -> 16% of each run, Pallas kernels for 0% -> 0%
where the time goes in v6:
time: 232 us
  waiting for transfers between devices  95 us (41%)
  starting transfers between devices  85.8 us (37%)
  matrix products  33.5 us (14%)
  local copies, waits for them, and re-layouts  8.93 us (4%)
  other arithmetic  6.85 us (3%)
    ppermute x22, starting transfers between devices, from_behind(): return lax.ppermute(value, axis, pairs)  73.7 us
    ppermute x22, waiting for transfers between devices, from_behind(): return lax.ppermute(value, axis, pairs)  68.6 us
    ppermute x8, waiting for transfers between devices, exchange(): return lax.ppermute(value, axis, pairs)  26.3 us
    ppermute x8, starting transfers between devices, exchange(): return lax.ppermute(value, axis, pairs)  12.1 us
    dot_general x5, matrix products, chunk_layer(): preact = preact + jnp.dot(middle, w_mid, preferred_element_type=jnp.float32)  4.65 us
  transfers between devices with their start and end apart: 30, of which 19 were waited for; matrix products, arithmetic and copies ran while one was open for 16% of the time, Pallas kernels for 0%

profile of v6, /device:TPU:0, one launch (start us, length us, event | category | flops | bytes accessed | tf_op | source)
XLA Modules:
  0.0 231.7 jit_solution(12661018437850755305)
XLA Ops:
  0.7 2.0 fusion.117
  2.7 3.0 %collective-permute-start.8 = (bf16[512,256]{1,0:T(8,128)(2,1)}, bf16[512,256]{1,0:T(8,128)(2,1)S(1)}, u32[]{:S(2)}, u32[]{:S(2)}) collective-permute-start(bf16[512,256]{1,0:T(8,128)(2,1)} %get-tuple-element.119), channel_id=1, source_target_pairs={{0,4},{1,5},{2,6},{3,7},{4,8},{5,9},{6,10},{7,11},{8,12},{9,13},{1... | collective-permute-start | bytes 786440 | tf_op jit(solution)/shard_map/ppermute | solution.py:18
  5.7 2.0 collective-permute-start.9
  7.7 2.6 %fusion.116 = (bf16[1024,256]{1,0:T(8,128)(2,1)}, bf16[1024,256]{1,0:T(8,128)(2,1)}, bf16[1024,256]{1,0:T(8,128)(2,1)}) fusion(bf16[4096,256]{1,0:T(8,128)(2,1)} %param.4), kind=kLoop, calls=%fused_computation.202 | loop fusion | bytes 3145728 | tf_op jit(solution)/shard_map/slice | solution.py:95
  10.3 3.8 %collective-permute-start.1 = (bf16[1024,256]{1,0:T(8,128)(2,1)}, bf16[1024,256]{1,0:T(8,128)(2,1)}, u32[]{:S(2)}, u32[]{:S(2)}) collective-permute-start(bf16[1024,256]{1,0:T(8,128)(2,1)} %get-tuple-element.117), channel_id=1, source_target_pairs={{0,12},{1,13},{2,14},{3,15},{4,0},{5,1},{6,2},{7,3},{8,4},{9,5},{1... | collective-permute-start | bytes 1572872 | tf_op jit(solution)/shard_map/ppermute | solution.py:18
  18.6 13.5 %collective-permute-done = bf16[1024,256]{1,0:T(8,128)(2,1)} collective-permute-done((bf16[1024,256]{1,0:T(8,128)(2,1)}, bf16[1024,256]{1,0:T(8,128)(2,1)}, u32[]{:S(2)}, u32[]{:S(2)}) %collective-permute-start) | collective-permute-done | bytes 524320 | tf_op jit(solution)/shard_map/ppermute | solution.py:18
  32.1 13.2 %collective-permute-start.3 = (bf16[1024,256]{1,0:T(8,128)(2,1)}, bf16[1024,256]{1,0:T(8,128)(2,1)S(1)}, u32[]{:S(2)}, u32[]{:S(2)}) collective-permute-start(bf16[1024,256]{1,0:T(8,128)(2,1)} %get-tuple-element.115), channel_id=1, source_target_pairs={{0,12},{1,13},{2,14},{3,15},{4,0},{5,1},{6,2},{7,3},{8,4},{9,5},{1... | collective-permute-start | bytes 1572872 | tf_op jit(solution)/shard_map/ppermute | solution.py:18
  54.6 13.2 %collective-permute-start.5 = (bf16[1024,256]{1,0:T(8,128)(2,1)S(1)}, bf16[1024,256]{1,0:T(8,128)(2,1)S(1)}, u32[]{:S(2)}, u32[]{:S(2)}) collective-permute-start(bf16[1024,256]{1,0:T(8,128)(2,1)S(1)} %copy-done.7), channel_id=1, source_target_pairs={{0,12},{1,13},{2,14},{3,15},{4,0},{5,1},{6,2},{7,3},{8,4},{9,5},{1... | collective-permute-start | bytes 1572872 | tf_op jit(solution)/shard_map/ppermute | solution.py:18
  67.8 8.3 %collective-permute-start.6 = (bf16[512,256]{1,0:T(8,128)(2,1)S(1)}, bf16[512,256]{1,0:T(8,128)(2,1)S(1)}, u32[]{:S(2)}, u32[]{:S(2)}) collective-permute-start(bf16[512,256]{1,0:T(8,128)(2,1)S(1)} %copy-done.8), channel_id=1, source_target_pairs={{0,4},{1,5},{2,6},{3,7},{4,8},{5,9},{6,10},{7,11},{8,12},{9,13},{1... | collective-permute-start | bytes 786440 | tf_op jit(solution)/shard_map/ppermute | solution.py:18
  82.3 7.8 %collective-permute-start.7 = (bf16[512,256]{1,0:T(8,128)(2,1)S(1)}, bf16[512,256]{1,0:T(8,128)(2,1)S(1)}, u32[]{:S(2)}, u32[]{:S(2)}) collective-permute-start(bf16[512,256]{1,0:T(8,128)(2,1)S(1)} %copy-done.8), channel_id=1, source_target_pairs={{0,12},{1,13},{2,14},{3,15},{4,0},{5,1},{6,2},{7,3},{8,4},{9,5},{1... | collective-permute-start | bytes 786440 | tf_op jit(solution)/shard_map/ppermute | solution.py:18
  94.8 3.1 %collective-permute-done.7 = bf16[512,256]{1,0:T(8,128)(2,1)S(1)} collective-permute-done((bf16[512,256]{1,0:T(8,128)(2,1)S(1)}, bf16[512,256]{1,0:T(8,128)(2,1)S(1)}, u32[]{:S(2)}, u32[]{:S(2)}) %collective-permute-start.7) | collective-permute-done | bytes 262176 | tf_op jit(solution)/shard_map/ppermute | solution.py:18
  105.4 2.4 %collective-permute-start.12 = (bf16[1024,256]{1,0:T(8,128)(2,1)S(1)}, bf16[1024,256]{1,0:T(8,128)(2,1)S(1)}, u32[]{:S(2)}, u32[]{:S(2)}) collective-permute-start(bf16[1024,256]{1,0:T(8,128)(2,1)S(1)} %get-tuple-element.74), channel_id=1, source_target_pairs={{0,12},{1,13},{2,14},{3,15},{4,0},{5,1},{6,2},{7,3},{8,4},{9,5},{1... | collective-permute-start | bytes 1572872 | tf_op jit(solution)/shard_map/ppermute | solution.py:18
  114.4 10.3 %collective-permute-done.11 = f32[114688]{0:T(1024)S(1)} collective-permute-done((f32[114688]{0:T(1024)S(1)}, f32[114688]{0:T(1024)S(1)}, u32[]{:S(2)}, u32[]{:S(2)}) %collective-permute-start.11) | collective-permute-done | bytes 458784 | tf_op jit(solution)/shard_map/ppermute | solution.py:24
  124.7 7.1 %collective-permute-done.13 = bf16[1024,256]{1,0:T(8,128)(2,1)S(1)} collective-permute-done((bf16[1024,256]{1,0:T(8,128)(2,1)S(1)}, bf16[1024,256]{1,0:T(8,128)(2,1)S(1)}, u32[]{:S(2)}, u32[]{:S(2)}) %collective-permute-start.13) | collective-permute-done | bytes 524320 | tf_op jit(solution)/shard_map/ppermute | solution.py:18
  133.8 5.2 %collective-permute-done.14 = f32[57344]{0:T(1024)S(1)} collective-permute-done((f32[57344]{0:T(1024)S(1)}, f32[57344]{0:T(1024)S(1)}, u32[]{:S(2)}, u32[]{:S(2)}) %collective-permute-start.14) | collective-permute-done | bytes 229408 | tf_op jit(solution)/shard_map/ppermute | solution.py:24
  140.8 2.8 %collective-permute-start.16 = (bf16[512,256]{1,0:T(8,128)(2,1)S(1)}, bf16[512,256]{1,0:T(8,128)(2,1)S(1)}, u32[]{:S(2)}, u32[]{:S(2)}) collective-permute-start(bf16[512,256]{1,0:T(8,128)(2,1)S(1)} %slice.151), channel_id=1, source_target_pairs={{0,12},{1,13},{2,14},{3,15},{4,0},{5,1},{6,2},{7,3},{8,4},{9,5},{1... | collective-permute-start | bytes 786440 | tf_op jit(solution)/shard_map/ppermute | solution.py:18
  143.6 3.9 %collective-permute-done.15 = f32[28672]{0:T(1024)S(1)} collective-permute-done((f32[28672]{0:T(1024)S(1)}, f32[28672]{0:T(1024)S(1)}, u32[]{:S(2)}, u32[]{:S(2)}) %collective-permute-start.15) | collective-permute-done | bytes 114720 | tf_op jit(solution)/shard_map/ppermute | solution.py:24
  147.5 3.1 %collective-permute-done.16 = bf16[512,256]{1,0:T(8,128)(2,1)S(1)} collective-permute-done((bf16[512,256]{1,0:T(8,128)(2,1)S(1)}, bf16[512,256]{1,0:T(8,128)(2,1)S(1)}, u32[]{:S(2)}, u32[]{:S(2)}) %collective-permute-start.16) | collective-permute-done | bytes 262176 | tf_op jit(solution)/shard_map/ppermute | solution.py:18
  150.7 5.6 %collective-permute-done.17 = bf16[512,256]{1,0:T(8,128)(2,1)S(1)} collective-permute-done((bf16[512,256]{1,0:T(8,128)(2,1)S(1)}, bf16[512,256]{1,0:T(8,128)(2,1)S(1)}, u32[]{:S(2)}, u32[]{:S(2)}) %collective-permute-start.17) | collective-permute-done | bytes 262176 | tf_op jit(solution)/shard_map/ppermute | solution.py:18
  158.1 2.6 %collective-permute-start.19 = (bf16[512,256]{1,0:T(8,128)(2,1)S(1)}, bf16[512,256]{1,0:T(8,128)(2,1)S(1)}, u32[]{:S(2)}, u32[]{:S(2)}) collective-permute-start(bf16[512,256]{1,0:T(8,128)(2,1)S(1)} %slice.153), channel_id=1, source_target_pairs={{0,12},{1,13},{2,14},{3,15},{4,0},{5,1},{6,2},{7,3},{8,4},{9,5},{1... | collective-permute-start | bytes 786440 | tf_op jit(solution)/shard_map/ppermute | solution.py:18
  160.8 3.9 %collective-permute-start.22 = (bf16[512,256]{1,0:T(8,128)(2,1)S(1)}, bf16[512,256]{1,0:T(8,128)(2,1)S(1)}, u32[]{:S(2)}, u32[]{:S(2)}) collective-permute-start(bf16[512,256]{1,0:T(8,128)(2,1)S(1)} %slice.155), channel_id=1, source_target_pairs={{0,12},{1,13},{2,14},{3,15},{4,0},{5,1},{6,2},{7,3},{8,4},{9,5},{1... | collective-permute-start | bytes 786440 | tf_op jit(solution)/shard_map/ppermute | solution.py:18
  165.1 7.2 %collective-permute-done.19 = bf16[512,256]{1,0:T(8,128)(2,1)S(1)} collective-permute-done((bf16[512,256]{1,0:T(8,128)(2,1)S(1)}, bf16[512,256]{1,0:T(8,128)(2,1)S(1)}, u32[]{:S(2)}, u32[]{:S(2)}) %collective-permute-start.19) | collective-permute-done | bytes 262176 | tf_op jit(solution)/shard_map/ppermute | solution.py:18
  172.3 3.5 %collective-permute-done.20 = bf16[512,256]{1,0:T(8,128)(2,1)S(1)} collective-permute-done((bf16[512,256]{1,0:T(8,128)(2,1)S(1)}, bf16[512,256]{1,0:T(8,128)(2,1)S(1)}, u32[]{:S(2)}, u32[]{:S(2)}) %collective-permute-start.20) | collective-permute-done | bytes 262176 | tf_op jit(solution)/shard_map/ppermute | solution.py:18
  175.9 4.4 %collective-permute-start.21 = (f32[57344]{0:T(1024)S(1)}, f32[57344]{0:T(1024)S(1)}, u32[]{:S(2)}, u32[]{:S(2)}) collective-permute-start(f32[57344]{0:T(1024)S(1)} %pad_maximum_fusion.9), channel_id=1, source_target_pairs={{0,4},{1,5},{2,6},{3,7},{4,0},{5,1},{6,2},{7,3},{8,12},{9,13},{10,... | collective-permute-start | bytes 688136 | tf_op jit(solution)/shard_map/ppermute | solution.py:24
  180.3 3.7 %collective-permute-start.25 = (bf16[512,256]{1,0:T(8,128)(2,1)S(1)}, bf16[512,256]{1,0:T(8,128)(2,1)S(1)}, u32[]{:S(2)}, u32[]{:S(2)}) collective-permute-start(bf16[512,256]{1,0:T(8,128)(2,1)S(1)} %slice.157), channel_id=1, source_target_pairs={{0,12},{1,13},{2,14},{3,15},{4,0},{5,1},{6,2},{7,3},{8,4},{9,5},{1... | collective-permute-start | bytes 786440 | tf_op jit(solution)/shard_map/ppermute | solution.py:18
  184.0 6.2 %collective-permute-done.21 = f32[57344]{0:T(1024)S(1)} collective-permute-done((f32[57344]{0:T(1024)S(1)}, f32[57344]{0:T(1024)S(1)}, u32[]{:S(2)}, u32[]{:S(2)}) %collective-permute-start.21) | collective-permute-done | bytes 229408 | tf_op jit(solution)/shard_map/ppermute | solution.py:24
  192.0 6.7 %collective-permute-start.27 = (bf16[1024,256]{1,0:T(8,128)(2,1)S(1)}, bf16[1024,256]{1,0:T(8,128)(2,1)S(1)}, u32[]{:S(2)}, u32[]{:S(2)}) collective-permute-start(bf16[1024,256]{1,0:T(8,128)(2,1)S(1)} %slice.159), channel_id=1, source_target_pairs={{0,12},{1,13},{2,14},{3,15},{4,0},{5,1},{6,2},{7,3},{8,4},{9,5},{1... | collective-permute-start | bytes 1572872 | tf_op jit(solution)/shard_map/ppermute | solution.py:18
  199.6 3.7 %collective-permute-done.26 = bf16[512,256]{1,0:T(8,128)(2,1)S(1)} collective-permute-done((bf16[512,256]{1,0:T(8,128)(2,1)S(1)}, bf16[512,256]{1,0:T(8,128)(2,1)S(1)}, u32[]{:S(2)}, u32[]{:S(2)}) %collective-permute-start.26) | collective-permute-done | bytes 262176 | tf_op jit(solution)/shard_map/ppermute | solution.py:18
  203.4 8.4 %collective-permute-done.27 = bf16[1024,256]{1,0:T(8,128)(2,1)S(1)} collective-permute-done((bf16[1024,256]{1,0:T(8,128)(2,1)S(1)}, bf16[1024,256]{1,0:T(8,128)(2,1)S(1)}, u32[]{:S(2)}, u32[]{:S(2)}) %collective-permute-start.27) | collective-permute-done | bytes 524320 | tf_op jit(solution)/shard_map/ppermute | solution.py:18
  211.8 11.9 %collective-permute-done.28 = bf16[1024,256]{1,0:T(8,128)(2,1)S(1)} collective-permute-done((bf16[1024,256]{1,0:T(8,128)(2,1)S(1)}, bf16[1024,256]{1,0:T(8,128)(2,1)S(1)}, u32[]{:S(2)}, u32[]{:S(2)}) %collective-permute-start.28) | collective-permute-done | bytes 524320 | tf_op jit(solution)/shard_map/ppermute | solution.py:18
  223.8 2.2 add_convert_fusion
  229.3 2.4 %pad_maximum_fusion = f32[768,512]{1,0:T(8,128)} fusion(f32[448,512]{1,0:T(8,128)S(1)} %copy-done.5, f32[448,512]{1,0:T(8,128)} %concatenate.89), kind=kLoop, calls=%fused_computation.4 | loop fusion | flops 393216 | bytes 3407872 | tf_op jit(solution)/shard_map/concatenate | solution.py:47
  (157 shorter events, 50.4 us)
Async XLA Ops:
  0.6 48.0 %copy-start = (bf16[256,256]{1,0:T(8,128)(2,1)S(1)}, bf16[256,256]{1,0:T(8,128)(2,1)}, u32[]{:S(2)}) copy-start(bf16[256,256]{1,0:T(8,128)(2,1)} %param.7) | copy-start | bytes 393220
  2.7 98.3 %collective-permute-start.8 = (bf16[512,256]{1,0:T(8,128)(2,1)}, bf16[512,256]{1,0:T(8,128)(2,1)S(1)}, u32[]{:S(2)}, u32[]{:S(2)}) collective-permute-start(bf16[512,256]{1,0:T(8,128)(2,1)} %get-tuple-element.119), channel_id=1, source_target_pairs={{0,4},{1,5},{2,6},{3,7},{4,8},{5,9},{6,10},{7,11},{8,12},{9,13},{1... | collective-permute-start | bytes 786440 | tf_op jit(solution)/shard_map/ppermute | solution.py:18
  5.7 95.3 %collective-permute-start.9 = (bf16[512,256]{1,0:T(8,128)(2,1)}, bf16[512,256]{1,0:T(8,128)(2,1)S(1)}, u32[]{:S(2)}, u32[]{:S(2)}) collective-permute-start(bf16[512,256]{1,0:T(8,128)(2,1)} %get-tuple-element.119), channel_id=1, source_target_pairs={{0,12},{1,13},{2,14},{3,15},{4,0},{5,1},{6,2},{7,3},{8,4},{9,5},{1... | collective-permute-start | bytes 786440 | tf_op jit(solution)/shard_map/ppermute | solution.py:18
  10.3 21.8 %collective-permute-start = (bf16[1024,256]{1,0:T(8,128)(2,1)}, bf16[1024,256]{1,0:T(8,128)(2,1)}, u32[]{:S(2)}, u32[]{:S(2)}) collective-permute-start(bf16[1024,256]{1,0:T(8,128)(2,1)} %get-tuple-element.117), channel_id=1, source_target_pairs={{0,4},{1,5},{2,6},{3,7},{4,8},{5,9},{6,10},{7,11},{8,12},{9,13},{1... | collective-permute-start | bytes 1572872 | tf_op jit(solution)/shard_map/ppermute | solution.py:18
  10.3 36.6 %collective-permute-start.1 = (bf16[1024,256]{1,0:T(8,128)(2,1)}, bf16[1024,256]{1,0:T(8,128)(2,1)}, u32[]{:S(2)}, u32[]{:S(2)}) collective-permute-start(bf16[1024,256]{1,0:T(8,128)(2,1)} %get-tuple-element.117), channel_id=1, source_target_pairs={{0,12},{1,13},{2,14},{3,15},{4,0},{5,1},{6,2},{7,3},{8,4},{9,5},{1... | collective-permute-start | bytes 1572872 | tf_op jit(solution)/shard_map/ppermute | solution.py:18
  14.1 40.5 %collective-permute-start.2 = (bf16[1024,256]{1,0:T(8,128)(2,1)}, bf16[1024,256]{1,0:T(8,128)(2,1)}, u32[]{:S(2)}, u32[]{:S(2)}) collective-permute-start(bf16[1024,256]{1,0:T(8,128)(2,1)} %get-tuple-element.115), channel_id=1, source_target_pairs={{0,4},{1,5},{2,6},{3,7},{4,8},{5,9},{6,10},{7,11},{8,12},{9,13},{1... | collective-permute-start | bytes 1572872 | tf_op jit(solution)/shard_map/ppermute | solution.py:18
  18.3 28.6 %copy-start.2 = (f32[1024,512]{0,1:T(8,128)S(1)}, f32[1024,512]{0,1:T(8,128)}, u32[]{:S(2)}) copy-start(f32[1024,512]{0,1:T(8,128)} %fusion.77) | copy-start | bytes 6291460
  32.1 35.7 %collective-permute-start.3 = (bf16[1024,256]{1,0:T(8,128)(2,1)}, bf16[1024,256]{1,0:T(8,128)(2,1)S(1)}, u32[]{:S(2)}, u32[]{:S(2)}) collective-permute-start(bf16[1024,256]{1,0:T(8,128)(2,1)} %get-tuple-element.115), channel_id=1, source_target_pairs={{0,12},{1,13},{2,14},{3,15},{4,0},{5,1},{6,2},{7,3},{8,4},{9,5},{1... | collective-permute-start | bytes 1572872 | tf_op jit(solution)/shard_map/ppermute | solution.py:18
  46.9 35.4 %collective-permute-start.4 = (bf16[1024,256]{1,0:T(8,128)(2,1)S(1)}, bf16[1024,256]{1,0:T(8,128)(2,1)S(1)}, u32[]{:S(2)}, u32[]{:S(2)}) collective-permute-start(bf16[1024,256]{1,0:T(8,128)(2,1)S(1)} %copy-done.7), channel_id=1, source_target_pairs={{0,4},{1,5},{2,6},{3,7},{4,8},{5,9},{6,10},{7,11},{8,12},{9,13},{1... | collective-permute-start | bytes 1572872 | tf_op jit(solution)/shard_map/ppermute | solution.py:18
  54.6 35.5 %collective-permute-start.5 = (bf16[1024,256]{1,0:T(8,128)(2,1)S(1)}, bf16[1024,256]{1,0:T(8,128)(2,1)S(1)}, u32[]{:S(2)}, u32[]{:S(2)}) collective-permute-start(bf16[1024,256]{1,0:T(8,128)(2,1)S(1)} %copy-done.7), channel_id=1, source_target_pairs={{0,12},{1,13},{2,14},{3,15},{4,0},{5,1},{6,2},{7,3},{8,4},{9,5},{1... | collective-permute-start | bytes 1572872 | tf_op jit(solution)/shard_map/ppermute | solution.py:18
  67.8 27.0 %collective-permute-start.6 = (bf16[512,256]{1,0:T(8,128)(2,1)S(1)}, bf16[512,256]{1,0:T(8,128)(2,1)S(1)}, u32[]{:S(2)}, u32[]{:S(2)}) collective-permute-start(bf16[512,256]{1,0:T(8,128)(2,1)S(1)} %copy-done.8), channel_id=1, source_target_pairs={{0,4},{1,5},{2,6},{3,7},{4,8},{5,9},{6,10},{7,11},{8,12},{9,13},{1... | collective-permute-start | bytes 786440 | tf_op jit(solution)/shard_map/ppermute | solution.py:18
  82.3 15.6 %collective-permute-start.7 = (bf16[512,256]{1,0:T(8,128)(2,1)S(1)}, bf16[512,256]{1,0:T(8,128)(2,1)S(1)}, u32[]{:S(2)}, u32[]{:S(2)}) collective-permute-start(bf16[512,256]{1,0:T(8,128)(2,1)S(1)} %copy-done.8), channel_id=1, source_target_pairs={{0,12},{1,13},{2,14},{3,15},{4,0},{5,1},{6,2},{7,3},{8,4},{9,5},{1... | collective-permute-start | bytes 786440 | tf_op jit(solution)/shard_map/ppermute | solution.py:18
  105.4 6.5 %collective-permute-start.10 = (f32[229376]{0:T(1024)S(1)}, f32[229376]{0:T(1024)S(1)}, u32[]{:S(2)}, u32[]{:S(2)}) collective-permute-start(f32[229376]{0:T(1024)S(1)} %dynamic_slice.25), channel_id=1, source_target_pairs={{0,1},{1,0},{2,3},{3,2},{4,5},{5,4},{6,7},{7,6},{8,9},{9,8},{10,11... | collective-permute-start | bytes 2752520 | tf_op jit(solution)/shard_map/ppermute | solution.py:24
  105.4 19.3 %collective-permute-start.12 = (bf16[1024,256]{1,0:T(8,128)(2,1)S(1)}, bf16[1024,256]{1,0:T(8,128)(2,1)S(1)}, u32[]{:S(2)}, u32[]{:S(2)}) collective-permute-start(bf16[1024,256]{1,0:T(8,128)(2,1)S(1)} %get-tuple-element.74), channel_id=1, source_target_pairs={{0,12},{1,13},{2,14},{3,15},{4,0},{5,1},{6,2},{7,3},{8,4},{9,5},{1... | collective-permute-start | bytes 1572872 | tf_op jit(solution)/shard_map/ppermute | solution.py:18
  107.8 24.0 %collective-permute-start.13 = (bf16[1024,256]{1,0:T(8,128)(2,1)S(1)}, bf16[1024,256]{1,0:T(8,128)(2,1)S(1)}, u32[]{:S(2)}, u32[]{:S(2)}) collective-permute-start(bf16[1024,256]{1,0:T(8,128)(2,1)S(1)} %get-tuple-element.75), channel_id=1, source_target_pairs={{0,4},{1,5},{2,6},{3,7},{4,8},{5,9},{6,10},{7,11},{8,12},{9,13},{1... | collective-permute-start | bytes 1572872 | tf_op jit(solution)/shard_map/ppermute | solution.py:18
  112.0 12.6 %collective-permute-start.11 = (f32[114688]{0:T(1024)S(1)}, f32[114688]{0:T(1024)S(1)}, u32[]{:S(2)}, u32[]{:S(2)}) collective-permute-start(f32[114688]{0:T(1024)S(1)} %dynamic_slice.27), channel_id=1, source_target_pairs={{0,2},{1,3},{2,0},{3,1},{4,6},{5,7},{6,4},{7,5},{8,10},{9,11},{10,... | collective-permute-start | bytes 1376264 | tf_op jit(solution)/shard_map/ppermute | solution.py:24
  131.8 7.2 %collective-permute-start.14 = (f32[57344]{0:T(1024)S(1)}, f32[57344]{0:T(1024)S(1)}, u32[]{:S(2)}, u32[]{:S(2)}) collective-permute-start(f32[57344]{0:T(1024)S(1)} %dynamic_slice.29), channel_id=1, source_target_pairs={{0,4},{1,5},{2,6},{3,7},{4,0},{5,1},{6,2},{7,3},{8,12},{9,13},{10,... | collective-permute-start | bytes 688136 | tf_op jit(solution)/shard_map/ppermute | solution.py:24
  139.1 8.4 %collective-permute-start.15 = (f32[28672]{0:T(1024)S(1)}, f32[28672]{0:T(1024)S(1)}, u32[]{:S(2)}, u32[]{:S(2)}) collective-permute-start(f32[28672]{0:T(1024)S(1)} %dynamic_slice.31), channel_id=1, source_target_pairs={{0,8},{1,9},{2,10},{3,11},{4,12},{5,13},{6,14},{7,15},{8,0},{9,1},... | collective-permute-start | bytes 344072 | tf_op jit(solution)/shard_map/ppermute | solution.py:24
  140.8 9.9 %collective-permute-start.16 = (bf16[512,256]{1,0:T(8,128)(2,1)S(1)}, bf16[512,256]{1,0:T(8,128)(2,1)S(1)}, u32[]{:S(2)}, u32[]{:S(2)}) collective-permute-start(bf16[512,256]{1,0:T(8,128)(2,1)S(1)} %slice.151), channel_id=1, source_target_pairs={{0,12},{1,13},{2,14},{3,15},{4,0},{5,1},{6,2},{7,3},{8,4},{9,5},{1... | collective-permute-start | bytes 786440 | tf_op jit(solution)/shard_map/ppermute | solution.py:18
  143.6 12.7 %collective-permute-start.17 = (bf16[512,256]{1,0:T(8,128)(2,1)S(1)}, bf16[512,256]{1,0:T(8,128)(2,1)S(1)}, u32[]{:S(2)}, u32[]{:S(2)}) collective-permute-start(bf16[512,256]{1,0:T(8,128)(2,1)S(1)} %slice.152), channel_id=1, source_target_pairs={{0,4},{1,5},{2,6},{3,7},{4,8},{5,9},{6,10},{7,11},{8,12},{9,13},{1... | collective-permute-start | bytes 786440 | tf_op jit(solution)/shard_map/ppermute | solution.py:18
  156.3 8.8 %collective-permute-start.18 = (f32[28672]{0:T(1024)S(1)}, f32[28672]{0:T(1024)S(1)}, u32[]{:S(2)}, u32[]{:S(2)}) collective-permute-start(f32[28672]{0:T(1024)S(1)} %add_multiply_fusion), channel_id=1, source_target_pairs={{0,8},{1,9},{2,10},{3,11},{4,12},{5,13},{6,14},{7,15},{8,0},{9,1},... | collective-permute-start | bytes 344072 | tf_op jit(solution)/shard_map/ppermute | solution.py:24
  158.1 14.2 %collective-permute-start.19 = (bf16[512,256]{1,0:T(8,128)(2,1)S(1)}, bf16[512,256]{1,0:T(8,128)(2,1)S(1)}, u32[]{:S(2)}, u32[]{:S(2)}) collective-permute-start(bf16[512,256]{1,0:T(8,128)(2,1)S(1)} %slice.153), channel_id=1, source_target_pairs={{0,12},{1,13},{2,14},{3,15},{4,0},{5,1},{6,2},{7,3},{8,4},{9,5},{1... | collective-permute-start | bytes 786440 | tf_op jit(solution)/shard_map/ppermute | solution.py:18
  160.7 15.2 %collective-permute-start.20 = (bf16[512,256]{1,0:T(8,128)(2,1)S(1)}, bf16[512,256]{1,0:T(8,128)(2,1)S(1)}, u32[]{:S(2)}, u32[]{:S(2)}) collective-permute-start(bf16[512,256]{1,0:T(8,128)(2,1)S(1)} %slice.154), channel_id=1, source_target_pairs={{0,4},{1,5},{2,6},{3,7},{4,8},{5,9},{6,10},{7,11},{8,12},{9,13},{1... | collective-permute-start | bytes 786440 | tf_op jit(solution)/shard_map/ppermute | solution.py:18
  160.8 29.5 %collective-permute-start.22 = (bf16[512,256]{1,0:T(8,128)(2,1)S(1)}, bf16[512,256]{1,0:T(8,128)(2,1)S(1)}, u32[]{:S(2)}, u32[]{:S(2)}) collective-permute-start(bf16[512,256]{1,0:T(8,128)(2,1)S(1)} %slice.155), channel_id=1, source_target_pairs={{0,12},{1,13},{2,14},{3,15},{4,0},{5,1},{6,2},{7,3},{8,4},{9,5},{1... | collective-permute-start | bytes 786440 | tf_op jit(solution)/shard_map/ppermute | solution.py:18
  164.7 25.7 %collective-permute-start.23 = (bf16[512,256]{1,0:T(8,128)(2,1)S(1)}, bf16[512,256]{1,0:T(8,128)(2,1)S(1)}, u32[]{:S(2)}, u32[]{:S(2)}) collective-permute-start(bf16[512,256]{1,0:T(8,128)(2,1)S(1)} %slice.156), channel_id=1, source_target_pairs={{0,4},{1,5},{2,6},{3,7},{4,8},{5,9},{6,10},{7,11},{8,12},{9,13},{1... | collective-permute-start | bytes 786440 | tf_op jit(solution)/shard_map/ppermute | solution.py:18
  175.9 14.4 %collective-permute-start.21 = (f32[57344]{0:T(1024)S(1)}, f32[57344]{0:T(1024)S(1)}, u32[]{:S(2)}, u32[]{:S(2)}) collective-permute-start(f32[57344]{0:T(1024)S(1)} %pad_maximum_fusion.9), channel_id=1, source_target_pairs={{0,4},{1,5},{2,6},{3,7},{4,0},{5,1},{6,2},{7,3},{8,12},{9,13},{10,... | collective-permute-start | bytes 688136 | tf_op jit(solution)/shard_map/ppermute | solution.py:24
  180.3 19.3 %collective-permute-start.25 = (bf16[512,256]{1,0:T(8,128)(2,1)S(1)}, bf16[512,256]{1,0:T(8,128)(2,1)S(1)}, u32[]{:S(2)}, u32[]{:S(2)}) collective-permute-start(bf16[512,256]{1,0:T(8,128)(2,1)S(1)} %slice.157), channel_id=1, source_target_pairs={{0,12},{1,13},{2,14},{3,15},{4,0},{5,1},{6,2},{7,3},{8,4},{9,5},{1... | collective-permute-start | bytes 786440 | tf_op jit(solution)/shard_map/ppermute | solution.py:18
  184.0 19.4 %collective-permute-start.26 = (bf16[512,256]{1,0:T(8,128)(2,1)S(1)}, bf16[512,256]{1,0:T(8,128)(2,1)S(1)}, u32[]{:S(2)}, u32[]{:S(2)}) collective-permute-start(bf16[512,256]{1,0:T(8,128)(2,1)S(1)} %slice.158), channel_id=1, source_target_pairs={{0,4},{1,5},{2,6},{3,7},{4,8},{5,9},{6,10},{7,11},{8,12},{9,13},{1... | collective-permute-start | bytes 786440 | tf_op jit(solution)/shard_map/ppermute | solution.py:18
  190.3 8.7 %collective-permute-start.24 = (f32[114688]{0:T(1024)S(1)}, f32[114688]{0:T(1024)S(1)}, u32[]{:S(2)}, u32[]{:S(2)}) collective-permute-start(f32[114688]{0:T(1024)S(1)} %pad_maximum_fusion.8), channel_id=1, source_target_pairs={{0,2},{1,3},{2,0},{3,1},{4,6},{5,7},{6,4},{7,5},{8,10},{9,11},{10,... | collective-permute-start | bytes 1376264 | tf_op jit(solution)/shard_map/ppermute | solution.py:24
  192.0 19.8 %collective-permute-start.27 = (bf16[1024,256]{1,0:T(8,128)(2,1)S(1)}, bf16[1024,256]{1,0:T(8,128)(2,1)S(1)}, u32[]{:S(2)}, u32[]{:S(2)}) collective-permute-start(bf16[1024,256]{1,0:T(8,128)(2,1)S(1)} %slice.159), channel_id=1, source_target_pairs={{0,12},{1,13},{2,14},{3,15},{4,0},{5,1},{6,2},{7,3},{8,4},{9,5},{1... | collective-permute-start | bytes 1572872 | tf_op jit(solution)/shard_map/ppermute | solution.py:18
  198.7 25.1 %collective-permute-start.28 = (bf16[1024,256]{1,0:T(8,128)(2,1)S(1)}, bf16[1024,256]{1,0:T(8,128)(2,1)S(1)}, u32[]{:S(2)}, u32[]{:S(2)}) collective-permute-start(bf16[1024,256]{1,0:T(8,128)(2,1)S(1)} %slice.160), channel_id=1, source_target_pairs={{0,4},{1,5},{2,6},{3,7},{4,8},{5,9},{6,10},{7,11},{8,12},{9,13},{1... | collective-permute-start | bytes 1572872 | tf_op jit(solution)/shard_map/ppermute | solution.py:18
  223.7 2.5 %collective-permute-start.29 = (f32[229376]{0:T(1024)S(1)}, f32[229376]{0:T(1024)S(1)}, u32[]{:S(2)}, u32[]{:S(2)}) collective-permute-start(f32[229376]{0:T(1024)S(1)} %pad_maximum_fusion.5), channel_id=1, source_target_pairs={{0,1},{1,0},{2,3},{3,2},{4,5},{5,4},{6,7},{7,6},{8,9},{9,8},{10,11... | collective-permute-start | bytes 2752520 | tf_op jit(solution)/shard_map/ppermute | solution.py:24
  (7 other events, 75.6 us)

commit v7 on v6

--- a/solution.py
+++ b/solution.py
@@ -101,7 +101,9 @@
                 (left_tap_input, right_tap_input, lows[:EARLY], highs[:EARLY])
             )
             for low, high in zip(lows_early, highs_early):
-                early.append((from_behind(low, "seq", -spacing), from_behind(high, "seq", spacing)))
+                half = low.shape[0] // 2
+                for part in (slice(0, half), slice(half, low.shape[0])):
+                    early.append((from_behind(low[part], "seq", -spacing), from_behind(high[part], "seq", spacing)))
         if wconv_total is not None:
             left_tap_input, right_tap_input, wconv_total, wout_total = lax.optimization_barrier(
                 (left_tap_input, right_tap_input, wconv_total, wout_total)
@@ -144,7 +146,9 @@
             sent_rows += RIDER_ROWS
         if not down and bit == 2 and not late:
             buf, pieces = lax.optimization_barrier((buf, (lower_all, upper_all)))
-            late.append(send_rows(pieces, sent_rows, positions))
+            middle_row = sent_rows + (positions - sent_rows) // 2
+            late.append(send_rows(pieces, sent_rows, middle_row))
+            late.append(send_rows(pieces, middle_row, positions))
             sent_rows = positions
         if not down and bit == 1 and late:
             buf, late = lax.optimization_barrier((buf, late))

time: 232 us -> 226 us (0.974)
  waiting for transfers between devices: 95 us -> 82 us
  starting transfers between devices: 85.8 us -> 92.7 us
    ppermute x22 -> x26, waiting for transfers between devices: 68.6 us -> 38.3 us  [from_behind(): return lax.ppermute(value, axis, pairs)]
    ppermute x8, waiting for transfers between devices: 26.3 us -> 43.7 us  [exchange(): return lax.ppermute(value, axis, pairs)]
    ppermute x22 -> x26, starting transfers between devices: 73.7 us -> 80.1 us  [from_behind(): return lax.ppermute(value, axis, pairs)]
  transfers between devices with their start and end apart: 30 -> 34, of which waited for: 19 -> 15; matrix products, arithmetic and copies ran while one was open for 16% -> 16% of each run, Pallas kernels for 0% -> 0%
where the time goes in v7:
time: 226 us
  starting transfers between devices  92.7 us (41%)
  waiting for transfers between devices  82 us (36%)
  matrix products  33.6 us (15%)
  local copies, waits for them, and re-layouts  8.99 us (4%)
  other arithmetic  6.85 us (3%)
    ppermute x26, starting transfers between devices, from_behind(): return lax.ppermute(value, axis, pairs)  80.1 us
    ppermute x8, waiting for transfers between devices, exchange(): return lax.ppermute(value, axis, pairs)  43.7 us
    ppermute x26, waiting for transfers between devices, from_behind(): return lax.ppermute(value, axis, pairs)  38.3 us
    ppermute x8, starting transfers between devices, exchange(): return lax.ppermute(value, axis, pairs)  12.6 us
    dot_general x5, matrix products, chunk_layer(): preact = preact + jnp.dot(middle, w_mid, preferred_element_type=jnp.float32)  4.65 us
    slice x2, local copies, waits for them, and re-layouts, body(): middle = activations[bounds[k]:bounds[k + 1]]  4.53 us
  transfers between devices with their start and end apart: 34, of which 15 were waited for; matrix products, arithmetic and copies ran while one was open for 16% of the time, Pallas kernels for 0%

profile of v7, /device:TPU:0, one launch (start us, length us, event | category | flops | bytes accessed | tf_op | source)
XLA Modules:
  0.0 225.9 jit_solution(18215440071301981273)
XLA Ops:
  0.7 2.0 fusion.119
  2.7 3.0 %collective-permute-start.8 = (bf16[512,256]{1,0:T(8,128)(2,1)}, bf16[512,256]{1,0:T(8,128)(2,1)S(1)}, u32[]{:S(2)}, u32[]{:S(2)}) collective-permute-start(bf16[512,256]{1,0:T(8,128)(2,1)} %get-tuple-element.131), channel_id=1, source_target_pairs={{0,4},{1,5},{2,6},{3,7},{4,8},{5,9},{6,10},{7,11},{8,12},{9,13},{1... | collective-permute-start | bytes 786440 | tf_op jit(solution)/shard_map/ppermute | solution.py:18
  5.7 2.0 collective-permute-start.9
  7.7 2.5 %fusion.118 = (bf16[1024,256]{1,0:T(8,128)(2,1)}, bf16[1024,256]{1,0:T(8,128)(2,1)}, bf16[1024,256]{1,0:T(8,128)(2,1)}) fusion(bf16[4096,256]{1,0:T(8,128)(2,1)} %param.4), kind=kLoop, calls=%fused_computation.208 | loop fusion | bytes 3145728 | tf_op jit(solution)/shard_map/slice | solution.py:95
  10.3 3.8 %collective-permute-start.1 = (bf16[1024,256]{1,0:T(8,128)(2,1)}, bf16[1024,256]{1,0:T(8,128)(2,1)}, u32[]{:S(2)}, u32[]{:S(2)}) collective-permute-start(bf16[1024,256]{1,0:T(8,128)(2,1)} %get-tuple-element.129), channel_id=1, source_target_pairs={{0,12},{1,13},{2,14},{3,15},{4,0},{5,1},{6,2},{7,3},{8,4},{9,5},{1... | collective-permute-start | bytes 1572872 | tf_op jit(solution)/shard_map/ppermute | solution.py:18
  14.1 1.8 fusion.77
  18.6 13.5 %collective-permute-done = bf16[1024,256]{1,0:T(8,128)(2,1)} collective-permute-done((bf16[1024,256]{1,0:T(8,128)(2,1)}, bf16[1024,256]{1,0:T(8,128)(2,1)}, u32[]{:S(2)}, u32[]{:S(2)}) %collective-permute-start) | collective-permute-done | bytes 524320 | tf_op jit(solution)/shard_map/ppermute | solution.py:18
  32.1 13.2 %collective-permute-start.3 = (bf16[1024,256]{1,0:T(8,128)(2,1)}, bf16[1024,256]{1,0:T(8,128)(2,1)S(1)}, u32[]{:S(2)}, u32[]{:S(2)}) collective-permute-start(bf16[1024,256]{1,0:T(8,128)(2,1)} %get-tuple-element.127), channel_id=1, source_target_pairs={{0,12},{1,13},{2,14},{3,15},{4,0},{5,1},{6,2},{7,3},{8,4},{9,5},{1... | collective-permute-start | bytes 1572872 | tf_op jit(solution)/shard_map/ppermute | solution.py:18
  54.6 13.2 %collective-permute-start.5 = (bf16[1024,256]{1,0:T(8,128)(2,1)S(1)}, bf16[1024,256]{1,0:T(8,128)(2,1)S(1)}, u32[]{:S(2)}, u32[]{:S(2)}) collective-permute-start(bf16[1024,256]{1,0:T(8,128)(2,1)S(1)} %copy-done.7), channel_id=1, source_target_pairs={{0,12},{1,13},{2,14},{3,15},{4,0},{5,1},{6,2},{7,3},{8,4},{9,5},{1... | collective-permute-start | bytes 1572872 | tf_op jit(solution)/shard_map/ppermute | solution.py:18
  67.8 8.3 %collective-permute-start.6 = (bf16[512,256]{1,0:T(8,128)(2,1)S(1)}, bf16[512,256]{1,0:T(8,128)(2,1)S(1)}, u32[]{:S(2)}, u32[]{:S(2)}) collective-permute-start(bf16[512,256]{1,0:T(8,128)(2,1)S(1)} %copy-done.8), channel_id=1, source_target_pairs={{0,4},{1,5},{2,6},{3,7},{4,8},{5,9},{6,10},{7,11},{8,12},{9,13},{1... | collective-permute-start | bytes 786440 | tf_op jit(solution)/shard_map/ppermute | solution.py:18
  82.3 7.8 %collective-permute-start.7 = (bf16[512,256]{1,0:T(8,128)(2,1)S(1)}, bf16[512,256]{1,0:T(8,128)(2,1)S(1)}, u32[]{:S(2)}, u32[]{:S(2)}) collective-permute-start(bf16[512,256]{1,0:T(8,128)(2,1)S(1)} %copy-done.8), channel_id=1, source_target_pairs={{0,12},{1,13},{2,14},{3,15},{4,0},{5,1},{6,2},{7,3},{8,4},{9,5},{1... | collective-permute-start | bytes 786440 | tf_op jit(solution)/shard_map/ppermute | solution.py:18
  94.8 3.1 %collective-permute-done.7 = bf16[512,256]{1,0:T(8,128)(2,1)S(1)} collective-permute-done((bf16[512,256]{1,0:T(8,128)(2,1)S(1)}, bf16[512,256]{1,0:T(8,128)(2,1)S(1)}, u32[]{:S(2)}, u32[]{:S(2)}) %collective-permute-start.7) | collective-permute-done | bytes 262176 | tf_op jit(solution)/shard_map/ppermute | solution.py:18
  106.0 2.3 %collective-permute-start.12 = (bf16[512,256]{1,0:T(8,128)(2,1)S(1)}, bf16[512,256]{1,0:T(8,128)(2,1)S(1)}, u32[]{:S(2)}, u32[]{:S(2)}) collective-permute-start(bf16[512,256]{1,0:T(8,128)(2,1)S(1)} %get-tuple-element.143), channel_id=1, source_target_pairs={{0,12},{1,13},{2,14},{3,15},{4,0},{5,1},{6,2},{7,3},{8,4},{9,5},{1... | collective-permute-start | bytes 786440 | tf_op jit(solution)/shard_map/ppermute | solution.py:18
  108.5 3.8 %collective-permute-start.14 = (bf16[512,256]{1,0:T(8,128)(2,1)S(1)}, bf16[512,256]{1,0:T(8,128)(2,1)S(1)}, u32[]{:S(2)}, u32[]{:S(2)}) collective-permute-start(bf16[512,256]{1,0:T(8,128)(2,1)S(1)} %get-tuple-element.142), channel_id=1, source_target_pairs={{0,12},{1,13},{2,14},{3,15},{4,0},{5,1},{6,2},{7,3},{8,4},{9,5},{1... | collective-permute-start | bytes 786440 | tf_op jit(solution)/shard_map/ppermute | solution.py:18
  119.1 9.9 %collective-permute-done.11 = f32[114688]{0:T(1024)S(1)} collective-permute-done((f32[114688]{0:T(1024)S(1)}, f32[114688]{0:T(1024)S(1)}, u32[]{:S(2)}, u32[]{:S(2)}) %collective-permute-start.11) | collective-permute-done | bytes 458784 | tf_op jit(solution)/shard_map/ppermute | solution.py:24
  129.1 3.4 %collective-permute-done.15 = bf16[512,256]{1,0:T(8,128)(2,1)S(1)} collective-permute-done((bf16[512,256]{1,0:T(8,128)(2,1)S(1)}, bf16[512,256]{1,0:T(8,128)(2,1)S(1)}, u32[]{:S(2)}, u32[]{:S(2)}) %collective-permute-start.15) | collective-permute-done | bytes 262176 | tf_op jit(solution)/shard_map/ppermute | solution.py:18
  136.3 4.7 %collective-permute-done.16 = f32[57344]{0:T(1024)S(1)} collective-permute-done((f32[57344]{0:T(1024)S(1)}, f32[57344]{0:T(1024)S(1)}, u32[]{:S(2)}, u32[]{:S(2)}) %collective-permute-start.16) | collective-permute-done | bytes 229408 | tf_op jit(solution)/shard_map/ppermute | solution.py:24
  142.8 2.4 %collective-permute-start.21 = (bf16[512,256]{1,0:T(8,128)(2,1)S(1)}, bf16[512,256]{1,0:T(8,128)(2,1)S(1)}, u32[]{:S(2)}, u32[]{:S(2)}) collective-permute-start(bf16[512,256]{1,0:T(8,128)(2,1)S(1)} %slice.175), channel_id=1, source_target_pairs={{0,12},{1,13},{2,14},{3,15},{4,0},{5,1},{6,2},{7,3},{8,4},{9,5},{1... | collective-permute-start | bytes 786440 | tf_op jit(solution)/shard_map/ppermute | solution.py:18
  145.3 10.1 %collective-permute-done.17 = f32[28672]{0:T(1024)S(1)} collective-permute-done((f32[28672]{0:T(1024)S(1)}, f32[28672]{0:T(1024)S(1)}, u32[]{:S(2)}, u32[]{:S(2)}) %collective-permute-start.17) | collective-permute-done | bytes 114720 | tf_op jit(solution)/shard_map/ppermute | solution.py:24
  155.4 2.1 collective-permute-start.20
  159.7 11.9 %collective-permute-done.20 = f32[28672]{0:T(1024)S(1)} collective-permute-done((f32[28672]{0:T(1024)S(1)}, f32[28672]{0:T(1024)S(1)}, u32[]{:S(2)}, u32[]{:S(2)}) %collective-permute-start.20) | collective-permute-done | bytes 114720 | tf_op jit(solution)/shard_map/ppermute | solution.py:24
  171.7 4.1 %collective-permute-start.23 = (f32[57344]{0:T(1024)S(1)}, f32[57344]{0:T(1024)S(1)}, u32[]{:S(2)}, u32[]{:S(2)}) collective-permute-start(f32[57344]{0:T(1024)S(1)} %pad_maximum_fusion.9), channel_id=1, source_target_pairs={{0,4},{1,5},{2,6},{3,7},{4,0},{5,1},{6,2},{7,3},{8,12},{9,13},{10,... | collective-permute-start | bytes 688136 | tf_op jit(solution)/shard_map/ppermute | solution.py:24
  175.8 2.9 %collective-permute-start.27 = (bf16[512,256]{1,0:T(8,128)(2,1)S(1)}, bf16[512,256]{1,0:T(8,128)(2,1)S(1)}, u32[]{:S(2)}, u32[]{:S(2)}) collective-permute-start(bf16[512,256]{1,0:T(8,128)(2,1)S(1)} %slice.179), channel_id=1, source_target_pairs={{0,12},{1,13},{2,14},{3,15},{4,0},{5,1},{6,2},{7,3},{8,4},{9,5},{1... | collective-permute-start | bytes 786440 | tf_op jit(solution)/shard_map/ppermute | solution.py:18
  178.8 5.8 %collective-permute-done.23 = f32[57344]{0:T(1024)S(1)} collective-permute-done((f32[57344]{0:T(1024)S(1)}, f32[57344]{0:T(1024)S(1)}, u32[]{:S(2)}, u32[]{:S(2)}) %collective-permute-start.23) | collective-permute-done | bytes 229408 | tf_op jit(solution)/shard_map/ppermute | solution.py:24
  186.3 7.1 %collective-permute-start.29 = (bf16[512,256]{1,0:T(8,128)(2,1)S(1)}, bf16[512,256]{1,0:T(8,128)(2,1)S(1)}, u32[]{:S(2)}, u32[]{:S(2)}) collective-permute-start(bf16[512,256]{1,0:T(8,128)(2,1)S(1)} %get-tuple-element.126), channel_id=1, source_target_pairs={{0,12},{1,13},{2,14},{3,15},{4,0},{5,1},{6,2},{7,3},{8,4},{9,5},{1... | collective-permute-start | bytes 786440 | tf_op jit(solution)/shard_map/ppermute | solution.py:18
  194.7 5.7 %collective-permute-start.31 = (bf16[512,256]{1,0:T(8,128)(2,1)S(1)}, bf16[512,256]{1,0:T(8,128)(2,1)S(1)}, u32[]{:S(2)}, u32[]{:S(2)}) collective-permute-start(bf16[512,256]{1,0:T(8,128)(2,1)S(1)} %get-tuple-element.125), channel_id=1, source_target_pairs={{0,12},{1,13},{2,14},{3,15},{4,0},{5,1},{6,2},{7,3},{8,4},{9,5},{1... | collective-permute-start | bytes 786440 | tf_op jit(solution)/shard_map/ppermute | solution.py:18
  200.6 5.2 %collective-permute-done.29 = bf16[512,256]{1,0:T(8,128)(2,1)S(1)} collective-permute-done((bf16[512,256]{1,0:T(8,128)(2,1)S(1)}, bf16[512,256]{1,0:T(8,128)(2,1)S(1)}, u32[]{:S(2)}, u32[]{:S(2)}) %collective-permute-start.29) | collective-permute-done | bytes 262176 | tf_op jit(solution)/shard_map/ppermute | solution.py:18
  205.8 2.5 %collective-permute-done.30 = bf16[512,256]{1,0:T(8,128)(2,1)S(1)} collective-permute-done((bf16[512,256]{1,0:T(8,128)(2,1)S(1)}, bf16[512,256]{1,0:T(8,128)(2,1)S(1)}, u32[]{:S(2)}, u32[]{:S(2)}) %collective-permute-start.30) | collective-permute-done | bytes 262176 | tf_op jit(solution)/shard_map/ppermute | solution.py:18
  208.3 3.8 %collective-permute-done.31 = bf16[512,256]{1,0:T(8,128)(2,1)S(1)} collective-permute-done((bf16[512,256]{1,0:T(8,128)(2,1)S(1)}, bf16[512,256]{1,0:T(8,128)(2,1)S(1)}, u32[]{:S(2)}, u32[]{:S(2)}) %collective-permute-start.31) | collective-permute-done | bytes 262176 | tf_op jit(solution)/shard_map/ppermute | solution.py:18
  212.1 5.8 %collective-permute-done.32 = bf16[512,256]{1,0:T(8,128)(2,1)S(1)} collective-permute-done((bf16[512,256]{1,0:T(8,128)(2,1)S(1)}, bf16[512,256]{1,0:T(8,128)(2,1)S(1)}, u32[]{:S(2)}, u32[]{:S(2)}) %collective-permute-start.32) | collective-permute-done | bytes 262176 | tf_op jit(solution)/shard_map/ppermute | solution.py:18
  218.1 2.2 add_convert_fusion
  223.5 2.4 %pad_maximum_fusion = f32[768,512]{1,0:T(8,128)} fusion(f32[448,512]{1,0:T(8,128)S(1)} %copy-done.5, f32[448,512]{1,0:T(8,128)} %concatenate.89), kind=kLoop, calls=%fused_computation.4 | loop fusion | flops 393216 | bytes 3407872 | tf_op jit(solution)/shard_map/concatenate | solution.py:47
  (171 shorter events, 51.8 us)
Async XLA Ops:
  2.7 98.3 %collective-permute-start.8 = (bf16[512,256]{1,0:T(8,128)(2,1)}, bf16[512,256]{1,0:T(8,128)(2,1)S(1)}, u32[]{:S(2)}, u32[]{:S(2)}) collective-permute-start(bf16[512,256]{1,0:T(8,128)(2,1)} %get-tuple-element.131), channel_id=1, source_target_pairs={{0,4},{1,5},{2,6},{3,7},{4,8},{5,9},{6,10},{7,11},{8,12},{9,13},{1... | collective-permute-start | bytes 786440 | tf_op jit(solution)/shard_map/ppermute | solution.py:18
  5.7 95.3 %collective-permute-start.9 = (bf16[512,256]{1,0:T(8,128)(2,1)}, bf16[512,256]{1,0:T(8,128)(2,1)S(1)}, u32[]{:S(2)}, u32[]{:S(2)}) collective-permute-start(bf16[512,256]{1,0:T(8,128)(2,1)} %get-tuple-element.131), channel_id=1, source_target_pairs={{0,12},{1,13},{2,14},{3,15},{4,0},{5,1},{6,2},{7,3},{8,4},{9,5},{1... | collective-permute-start | bytes 786440 | tf_op jit(solution)/shard_map/ppermute | solution.py:18
  10.3 21.9 %collective-permute-start = (bf16[1024,256]{1,0:T(8,128)(2,1)}, bf16[1024,256]{1,0:T(8,128)(2,1)}, u32[]{:S(2)}, u32[]{:S(2)}) collective-permute-start(bf16[1024,256]{1,0:T(8,128)(2,1)} %get-tuple-element.129), channel_id=1, source_target_pairs={{0,4},{1,5},{2,6},{3,7},{4,8},{5,9},{6,10},{7,11},{8,12},{9,13},{1... | collective-permute-start | bytes 1572872 | tf_op jit(solution)/shard_map/ppermute | solution.py:18
  10.3 36.6 %collective-permute-start.1 = (bf16[1024,256]{1,0:T(8,128)(2,1)}, bf16[1024,256]{1,0:T(8,128)(2,1)}, u32[]{:S(2)}, u32[]{:S(2)}) collective-permute-start(bf16[1024,256]{1,0:T(8,128)(2,1)} %get-tuple-element.129), channel_id=1, source_target_pairs={{0,12},{1,13},{2,14},{3,15},{4,0},{5,1},{6,2},{7,3},{8,4},{9,5},{1... | collective-permute-start | bytes 1572872 | tf_op jit(solution)/shard_map/ppermute | solution.py:18
  14.1 40.6 %collective-permute-start.2 = (bf16[1024,256]{1,0:T(8,128)(2,1)}, bf16[1024,256]{1,0:T(8,128)(2,1)}, u32[]{:S(2)}, u32[]{:S(2)}) collective-permute-start(bf16[1024,256]{1,0:T(8,128)(2,1)} %get-tuple-element.127), channel_id=1, source_target_pairs={{0,4},{1,5},{2,6},{3,7},{4,8},{5,9},{6,10},{7,11},{8,12},{9,13},{1... | collective-permute-start | bytes 1572872 | tf_op jit(solution)/shard_map/ppermute | solution.py:18
  32.1 35.7 %collective-permute-start.3 = (bf16[1024,256]{1,0:T(8,128)(2,1)}, bf16[1024,256]{1,0:T(8,128)(2,1)S(1)}, u32[]{:S(2)}, u32[]{:S(2)}) collective-permute-start(bf16[1024,256]{1,0:T(8,128)(2,1)} %get-tuple-element.127), channel_id=1, source_target_pairs={{0,12},{1,13},{2,14},{3,15},{4,0},{5,1},{6,2},{7,3},{8,4},{9,5},{1... | collective-permute-start | bytes 1572872 | tf_op jit(solution)/shard_map/ppermute | solution.py:18
  46.9 35.4 %collective-permute-start.4 = (bf16[1024,256]{1,0:T(8,128)(2,1)S(1)}, bf16[1024,256]{1,0:T(8,128)(2,1)S(1)}, u32[]{:S(2)}, u32[]{:S(2)}) collective-permute-start(bf16[1024,256]{1,0:T(8,128)(2,1)S(1)} %copy-done.7), channel_id=1, source_target_pairs={{0,4},{1,5},{2,6},{3,7},{4,8},{5,9},{6,10},{7,11},{8,12},{9,13},{1... | collective-permute-start | bytes 1572872 | tf_op jit(solution)/shard_map/ppermute | solution.py:18
  54.6 35.5 %collective-permute-start.5 = (bf16[1024,256]{1,0:T(8,128)(2,1)S(1)}, bf16[1024,256]{1,0:T(8,128)(2,1)S(1)}, u32[]{:S(2)}, u32[]{:S(2)}) collective-permute-start(bf16[1024,256]{1,0:T(8,128)(2,1)S(1)} %copy-done.7), channel_id=1, source_target_pairs={{0,12},{1,13},{2,14},{3,15},{4,0},{5,1},{6,2},{7,3},{8,4},{9,5},{1... | collective-permute-start | bytes 1572872 | tf_op jit(solution)/shard_map/ppermute | solution.py:18
  67.8 27.0 %collective-permute-start.6 = (bf16[512,256]{1,0:T(8,128)(2,1)S(1)}, bf16[512,256]{1,0:T(8,128)(2,1)S(1)}, u32[]{:S(2)}, u32[]{:S(2)}) collective-permute-start(bf16[512,256]{1,0:T(8,128)(2,1)S(1)} %copy-done.8), channel_id=1, source_target_pairs={{0,4},{1,5},{2,6},{3,7},{4,8},{5,9},{6,10},{7,11},{8,12},{9,13},{1... | collective-permute-start | bytes 786440 | tf_op jit(solution)/shard_map/ppermute | solution.py:18
  82.3 15.6 %collective-permute-start.7 = (bf16[512,256]{1,0:T(8,128)(2,1)S(1)}, bf16[512,256]{1,0:T(8,128)(2,1)S(1)}, u32[]{:S(2)}, u32[]{:S(2)}) collective-permute-start(bf16[512,256]{1,0:T(8,128)(2,1)S(1)} %copy-done.8), channel_id=1, source_target_pairs={{0,12},{1,13},{2,14},{3,15},{4,0},{5,1},{6,2},{7,3},{8,4},{9,5},{1... | collective-permute-start | bytes 786440 | tf_op jit(solution)/shard_map/ppermute | solution.py:18
  105.9 10.8 %collective-permute-start.10 = (f32[229376]{0:T(1024)S(1)}, f32[229376]{0:T(1024)S(1)}, u32[]{:S(2)}, u32[]{:S(2)}) collective-permute-start(f32[229376]{0:T(1024)S(1)} %dynamic_slice.25), channel_id=1, source_target_pairs={{0,1},{1,0},{2,3},{3,2},{4,5},{5,4},{6,7},{7,6},{8,9},{9,8},{10,11... | collective-permute-start | bytes 2752520 | tf_op jit(solution)/shard_map/ppermute | solution.py:24
  106.0 23.0 %collective-permute-start.12 = (bf16[512,256]{1,0:T(8,128)(2,1)S(1)}, bf16[512,256]{1,0:T(8,128)(2,1)S(1)}, u32[]{:S(2)}, u32[]{:S(2)}) collective-permute-start(bf16[512,256]{1,0:T(8,128)(2,1)S(1)} %get-tuple-element.143), channel_id=1, source_target_pairs={{0,12},{1,13},{2,14},{3,15},{4,0},{5,1},{6,2},{7,3},{8,4},{9,5},{1... | collective-permute-start | bytes 786440 | tf_op jit(solution)/shard_map/ppermute | solution.py:18
  108.4 20.6 %collective-permute-start.13 = (bf16[512,256]{1,0:T(8,128)(2,1)S(1)}, bf16[512,256]{1,0:T(8,128)(2,1)S(1)}, u32[]{:S(2)}, u32[]{:S(2)}) collective-permute-start(bf16[512,256]{1,0:T(8,128)(2,1)S(1)} %get-tuple-element.141), channel_id=1, source_target_pairs={{0,4},{1,5},{2,6},{3,7},{4,8},{5,9},{6,10},{7,11},{8,12},{9,13},{1... | collective-permute-start | bytes 786440 | tf_op jit(solution)/shard_map/ppermute | solution.py:18
  108.5 20.6 %collective-permute-start.14 = (bf16[512,256]{1,0:T(8,128)(2,1)S(1)}, bf16[512,256]{1,0:T(8,128)(2,1)S(1)}, u32[]{:S(2)}, u32[]{:S(2)}) collective-permute-start(bf16[512,256]{1,0:T(8,128)(2,1)S(1)} %get-tuple-element.142), channel_id=1, source_target_pairs={{0,12},{1,13},{2,14},{3,15},{4,0},{5,1},{6,2},{7,3},{8,4},{9,5},{1... | collective-permute-start | bytes 786440 | tf_op jit(solution)/shard_map/ppermute | solution.py:18
  112.3 20.2 %collective-permute-start.15 = (bf16[512,256]{1,0:T(8,128)(2,1)S(1)}, bf16[512,256]{1,0:T(8,128)(2,1)S(1)}, u32[]{:S(2)}, u32[]{:S(2)}) collective-permute-start(bf16[512,256]{1,0:T(8,128)(2,1)S(1)} %get-tuple-element.140), channel_id=1, source_target_pairs={{0,4},{1,5},{2,6},{3,7},{4,8},{5,9},{6,10},{7,11},{8,12},{9,13},{1... | collective-permute-start | bytes 786440 | tf_op jit(solution)/shard_map/ppermute | solution.py:18
  116.8 12.1 %collective-permute-start.11 = (f32[114688]{0:T(1024)S(1)}, f32[114688]{0:T(1024)S(1)}, u32[]{:S(2)}, u32[]{:S(2)}) collective-permute-start(f32[114688]{0:T(1024)S(1)} %dynamic_slice.27), channel_id=1, source_target_pairs={{0,2},{1,3},{2,0},{3,1},{4,6},{5,7},{6,4},{7,5},{8,10},{9,11},{10,... | collective-permute-start | bytes 1376264 | tf_op jit(solution)/shard_map/ppermute | solution.py:24
  134.1 21.2 %collective-permute-start.18 = (bf16[512,256]{1,0:T(8,128)(2,1)S(1)}, bf16[512,256]{1,0:T(8,128)(2,1)S(1)}, u32[]{:S(2)}, u32[]{:S(2)}) collective-permute-start(bf16[512,256]{1,0:T(8,128)(2,1)S(1)} %slice.173), channel_id=1, source_target_pairs={{0,12},{1,13},{2,14},{3,15},{4,0},{5,1},{6,2},{7,3},{8,4},{9,5},{1... | collective-permute-start | bytes 786440 | tf_op jit(solution)/shard_map/ppermute | solution.py:18
  135.7 19.7 %collective-permute-start.19 = (bf16[512,256]{1,0:T(8,128)(2,1)S(1)}, bf16[512,256]{1,0:T(8,128)(2,1)S(1)}, u32[]{:S(2)}, u32[]{:S(2)}) collective-permute-start(bf16[512,256]{1,0:T(8,128)(2,1)S(1)} %slice.174), channel_id=1, source_target_pairs={{0,4},{1,5},{2,6},{3,7},{4,8},{5,9},{6,10},{7,11},{8,12},{9,13},{1... | collective-permute-start | bytes 786440 | tf_op jit(solution)/shard_map/ppermute | solution.py:18
  141.1 14.2 %collective-permute-start.17 = (f32[28672]{0:T(1024)S(1)}, f32[28672]{0:T(1024)S(1)}, u32[]{:S(2)}, u32[]{:S(2)}) collective-permute-start(f32[28672]{0:T(1024)S(1)} %dynamic_slice.31), channel_id=1, source_target_pairs={{0,8},{1,9},{2,10},{3,11},{4,12},{5,13},{6,14},{7,15},{8,0},{9,1},... | collective-permute-start | bytes 344072 | tf_op jit(solution)/shard_map/ppermute | solution.py:24
  142.8 28.8 %collective-permute-start.21 = (bf16[512,256]{1,0:T(8,128)(2,1)S(1)}, bf16[512,256]{1,0:T(8,128)(2,1)S(1)}, u32[]{:S(2)}, u32[]{:S(2)}) collective-permute-start(bf16[512,256]{1,0:T(8,128)(2,1)S(1)} %slice.175), channel_id=1, source_target_pairs={{0,12},{1,13},{2,14},{3,15},{4,0},{5,1},{6,2},{7,3},{8,4},{9,5},{1... | collective-permute-start | bytes 786440 | tf_op jit(solution)/shard_map/ppermute | solution.py:18
  145.2 26.5 %collective-permute-start.22 = (bf16[512,256]{1,0:T(8,128)(2,1)S(1)}, bf16[512,256]{1,0:T(8,128)(2,1)S(1)}, u32[]{:S(2)}, u32[]{:S(2)}) collective-permute-start(bf16[512,256]{1,0:T(8,128)(2,1)S(1)} %slice.176), channel_id=1, source_target_pairs={{0,4},{1,5},{2,6},{3,7},{4,8},{5,9},{6,10},{7,11},{8,12},{9,13},{1... | collective-permute-start | bytes 786440 | tf_op jit(solution)/shard_map/ppermute | solution.py:18
  155.4 16.2 %collective-permute-start.20 = (f32[28672]{0:T(1024)S(1)}, f32[28672]{0:T(1024)S(1)}, u32[]{:S(2)}, u32[]{:S(2)}) collective-permute-start(f32[28672]{0:T(1024)S(1)} %add_multiply_fusion), channel_id=1, source_target_pairs={{0,8},{1,9},{2,10},{3,11},{4,12},{5,13},{6,14},{7,15},{8,0},{9,1},... | collective-permute-start | bytes 344072 | tf_op jit(solution)/shard_map/ppermute | solution.py:24
  157.5 27.2 %collective-permute-start.24 = (bf16[512,256]{1,0:T(8,128)(2,1)S(1)}, bf16[512,256]{1,0:T(8,128)(2,1)S(1)}, u32[]{:S(2)}, u32[]{:S(2)}) collective-permute-start(bf16[512,256]{1,0:T(8,128)(2,1)S(1)} %slice.177), channel_id=1, source_target_pairs={{0,12},{1,13},{2,14},{3,15},{4,0},{5,1},{6,2},{7,3},{8,4},{9,5},{1... | collective-permute-start | bytes 786440 | tf_op jit(solution)/shard_map/ppermute | solution.py:18
  158.9 25.7 %collective-permute-start.25 = (bf16[512,256]{1,0:T(8,128)(2,1)S(1)}, bf16[512,256]{1,0:T(8,128)(2,1)S(1)}, u32[]{:S(2)}, u32[]{:S(2)}) collective-permute-start(bf16[512,256]{1,0:T(8,128)(2,1)S(1)} %slice.178), channel_id=1, source_target_pairs={{0,4},{1,5},{2,6},{3,7},{4,8},{5,9},{6,10},{7,11},{8,12},{9,13},{1... | collective-permute-start | bytes 786440 | tf_op jit(solution)/shard_map/ppermute | solution.py:18
  171.7 12.9 %collective-permute-start.23 = (f32[57344]{0:T(1024)S(1)}, f32[57344]{0:T(1024)S(1)}, u32[]{:S(2)}, u32[]{:S(2)}) collective-permute-start(f32[57344]{0:T(1024)S(1)} %pad_maximum_fusion.9), channel_id=1, source_target_pairs={{0,4},{1,5},{2,6},{3,7},{4,0},{5,1},{6,2},{7,3},{8,12},{9,13},{10,... | collective-permute-start | bytes 688136 | tf_op jit(solution)/shard_map/ppermute | solution.py:24
  175.8 24.6 %collective-permute-start.27 = (bf16[512,256]{1,0:T(8,128)(2,1)S(1)}, bf16[512,256]{1,0:T(8,128)(2,1)S(1)}, u32[]{:S(2)}, u32[]{:S(2)}) collective-permute-start(bf16[512,256]{1,0:T(8,128)(2,1)S(1)} %slice.179), channel_id=1, source_target_pairs={{0,12},{1,13},{2,14},{3,15},{4,0},{5,1},{6,2},{7,3},{8,4},{9,5},{1... | collective-permute-start | bytes 786440 | tf_op jit(solution)/shard_map/ppermute | solution.py:18
  178.7 21.9 %collective-permute-start.28 = (bf16[512,256]{1,0:T(8,128)(2,1)S(1)}, bf16[512,256]{1,0:T(8,128)(2,1)S(1)}, u32[]{:S(2)}, u32[]{:S(2)}) collective-permute-start(bf16[512,256]{1,0:T(8,128)(2,1)S(1)} %slice.180), channel_id=1, source_target_pairs={{0,4},{1,5},{2,6},{3,7},{4,8},{5,9},{6,10},{7,11},{8,12},{9,13},{1... | collective-permute-start | bytes 786440 | tf_op jit(solution)/shard_map/ppermute | solution.py:18
  184.7 10.0 %collective-permute-start.26 = (f32[114688]{0:T(1024)S(1)}, f32[114688]{0:T(1024)S(1)}, u32[]{:S(2)}, u32[]{:S(2)}) collective-permute-start(f32[114688]{0:T(1024)S(1)} %pad_maximum_fusion.8), channel_id=1, source_target_pairs={{0,2},{1,3},{2,0},{3,1},{4,6},{5,7},{6,4},{7,5},{8,10},{9,11},{10,... | collective-permute-start | bytes 1376264 | tf_op jit(solution)/shard_map/ppermute | solution.py:24
  186.3 19.5 %collective-permute-start.29 = (bf16[512,256]{1,0:T(8,128)(2,1)S(1)}, bf16[512,256]{1,0:T(8,128)(2,1)S(1)}, u32[]{:S(2)}, u32[]{:S(2)}) collective-permute-start(bf16[512,256]{1,0:T(8,128)(2,1)S(1)} %get-tuple-element.126), channel_id=1, source_target_pairs={{0,12},{1,13},{2,14},{3,15},{4,0},{5,1},{6,2},{7,3},{8,4},{9,5},{1... | collective-permute-start | bytes 786440 | tf_op jit(solution)/shard_map/ppermute | solution.py:18
  193.4 14.9 %collective-permute-start.30 = (bf16[512,256]{1,0:T(8,128)(2,1)S(1)}, bf16[512,256]{1,0:T(8,128)(2,1)S(1)}, u32[]{:S(2)}, u32[]{:S(2)}) collective-permute-start(bf16[512,256]{1,0:T(8,128)(2,1)S(1)} %get-tuple-element.124), channel_id=1, source_target_pairs={{0,4},{1,5},{2,6},{3,7},{4,8},{5,9},{6,10},{7,11},{8,12},{9,13},{1... | collective-permute-start | bytes 786440 | tf_op jit(solution)/shard_map/ppermute | solution.py:18
  194.7 17.4 %collective-permute-start.31 = (bf16[512,256]{1,0:T(8,128)(2,1)S(1)}, bf16[512,256]{1,0:T(8,128)(2,1)S(1)}, u32[]{:S(2)}, u32[]{:S(2)}) collective-permute-start(bf16[512,256]{1,0:T(8,128)(2,1)S(1)} %get-tuple-element.125), channel_id=1, source_target_pairs={{0,12},{1,13},{2,14},{3,15},{4,0},{5,1},{6,2},{7,3},{8,4},{9,5},{1... | collective-permute-start | bytes 786440 | tf_op jit(solution)/shard_map/ppermute | solution.py:18
  200.4 17.5 %collective-permute-start.32 = (bf16[512,256]{1,0:T(8,128)(2,1)S(1)}, bf16[512,256]{1,0:T(8,128)(2,1)S(1)}, u32[]{:S(2)}, u32[]{:S(2)}) collective-permute-start(bf16[512,256]{1,0:T(8,128)(2,1)S(1)} %get-tuple-element.123), channel_id=1, source_target_pairs={{0,4},{1,5},{2,6},{3,7},{4,8},{5,9},{6,10},{7,11},{8,12},{9,13},{1... | collective-permute-start | bytes 786440 | tf_op jit(solution)/shard_map/ppermute | solution.py:18
  (11 other events, 163.4 us)

commit v8 on v7

--- a/solution.py
+++ b/solution.py
@@ -9,7 +9,8 @@
 CHUNK_EIGHTHS = (2, 2, 2, 1, 1)
 EARLY = 1
 RIDER_ROWS = 512
-RIDER_SPAN = 2
+RIDER_PARTS = 2
+RIDER_SPAN = 1
 
 
 def from_behind(value, axis, steps):
@@ -142,7 +143,10 @@
             pending = [item for item in pending if item[1] > number]
         if (bit, down) in rider_steps and sent_rows + RIDER_ROWS <= positions:
             buf, pieces = lax.optimization_barrier((buf, (lower_all, upper_all)))
-            pending.append((send_rows(pieces, sent_rows, sent_rows + RIDER_ROWS), number + RIDER_SPAN))
+            for part in range(RIDER_PARTS):
+                start = sent_rows + part * RIDER_ROWS // RIDER_PARTS
+                stop = sent_rows + (part + 1) * RIDER_ROWS // RIDER_PARTS
+                pending.append((send_rows(pieces, start, stop), number + RIDER_SPAN))
             sent_rows += RIDER_ROWS
         if not down and bit == 2 and not late:
             buf, pieces = lax.optimization_barrier((buf, (lower_all, upper_all)))

time: 226 us -> 236 us (1.044)
  waiting for transfers between devices: 82 us -> 89 us
  starting transfers between devices: 92.7 us -> 95.7 us
    ppermute x26 -> x34, waiting for transfers between devices: 38.3 us -> 70.8 us  [from_behind(): return lax.ppermute(value, axis, pairs)]
    ppermute x8, waiting for transfers between devices: 43.7 us -> 18.2 us  [exchange(): return lax.ppermute(value, axis, pairs)]
    ppermute x26 -> x34, starting transfers between devices: 80.1 us -> 86.9 us  [from_behind(): return lax.ppermute(value, axis, pairs)]
    ppermute x8, starting transfers between devices: 12.6 us -> 8.84 us  [exchange(): return lax.ppermute(value, axis, pairs)]
  transfers between devices with their start and end apart: 34 -> 42, of which waited for: 15 -> 26; matrix products, arithmetic and copies ran while one was open for 16% -> 16% of each run, Pallas kernels for 0% -> 0%
where the time goes in v8:
time: 236 us
  starting transfers between devices  95.7 us (41%)
  waiting for transfers between devices  89 us (38%)
  matrix products  33.6 us (14%)
  local copies, waits for them, and re-layouts  9.05 us (4%)
  other arithmetic  6.85 us (3%)
    ppermute x34, starting transfers between devices, from_behind(): return lax.ppermute(value, axis, pairs)  86.9 us
    ppermute x34, waiting for transfers between devices, from_behind(): return lax.ppermute(value, axis, pairs)  70.8 us
    ppermute x8, waiting for transfers between devices, exchange(): return lax.ppermute(value, axis, pairs)  18.2 us
    ppermute x8, starting transfers between devices, exchange(): return lax.ppermute(value, axis, pairs)  8.84 us
  transfers between devices with their start and end apart: 42, of which 26 were waited for; matrix products, arithmetic and copies ran while one was open for 16% of the time, Pallas kernels for 0%

profile of v8, /device:TPU:0, one launch (start us, length us, event | category | flops | bytes accessed | tf_op | source)
XLA Modules:
  0.0 236.0 jit_solution(5829747694740801367)
XLA Ops:
  2.7 3.0 %collective-permute-start.8 = (bf16[512,256]{1,0:T(8,128)(2,1)}, bf16[512,256]{1,0:T(8,128)(2,1)S(1)}, u32[]{:S(2)}, u32[]{:S(2)}) collective-permute-start(bf16[512,256]{1,0:T(8,128)(2,1)} %get-tuple-element.163), channel_id=1, source_target_pairs={{0,4},{1,5},{2,6},{3,7},{4,8},{5,9},{6,10},{7,11},{8,12},{9,13},{1... | collective-permute-start | bytes 786440 | tf_op jit(solution)/shard_map/ppermute | solution.py:19
  7.7 2.5 %fusion.126 = (bf16[1024,256]{1,0:T(8,128)(2,1)}, bf16[1024,256]{1,0:T(8,128)(2,1)}, bf16[1024,256]{1,0:T(8,128)(2,1)}) fusion(bf16[4096,256]{1,0:T(8,128)(2,1)} %param.4), kind=kLoop, calls=%fused_computation.224 | loop fusion | bytes 3145728 | tf_op jit(solution)/shard_map/slice | solution.py:96
  10.3 3.8 %collective-permute-start.1 = (bf16[1024,256]{1,0:T(8,128)(2,1)}, bf16[1024,256]{1,0:T(8,128)(2,1)}, u32[]{:S(2)}, u32[]{:S(2)}) collective-permute-start(bf16[1024,256]{1,0:T(8,128)(2,1)} %get-tuple-element.161), channel_id=1, source_target_pairs={{0,12},{1,13},{2,14},{3,15},{4,0},{5,1},{6,2},{7,3},{8,4},{9,5},{1... | collective-permute-start | bytes 1572872 | tf_op jit(solution)/shard_map/ppermute | solution.py:19
  18.7 13.5 %collective-permute-done = bf16[1024,256]{1,0:T(8,128)(2,1)} collective-permute-done((bf16[1024,256]{1,0:T(8,128)(2,1)}, bf16[1024,256]{1,0:T(8,128)(2,1)}, u32[]{:S(2)}, u32[]{:S(2)}) %collective-permute-start) | collective-permute-done | bytes 524320 | tf_op jit(solution)/shard_map/ppermute | solution.py:19
  32.1 13.2 %collective-permute-start.3 = (bf16[1024,256]{1,0:T(8,128)(2,1)}, bf16[1024,256]{1,0:T(8,128)(2,1)S(1)}, u32[]{:S(2)}, u32[]{:S(2)}) collective-permute-start(bf16[1024,256]{1,0:T(8,128)(2,1)} %get-tuple-element.159), channel_id=1, source_target_pairs={{0,12},{1,13},{2,14},{3,15},{4,0},{5,1},{6,2},{7,3},{8,4},{9,5},{1... | collective-permute-start | bytes 1572872 | tf_op jit(solution)/shard_map/ppermute | solution.py:19
  54.6 13.2 %collective-permute-start.5 = (bf16[1024,256]{1,0:T(8,128)(2,1)S(1)}, bf16[1024,256]{1,0:T(8,128)(2,1)S(1)}, u32[]{:S(2)}, u32[]{:S(2)}) collective-permute-start(bf16[1024,256]{1,0:T(8,128)(2,1)S(1)} %copy-done.7), channel_id=1, source_target_pairs={{0,12},{1,13},{2,14},{3,15},{4,0},{5,1},{6,2},{7,3},{8,4},{9,5},{1... | collective-permute-start | bytes 1572872 | tf_op jit(solution)/shard_map/ppermute | solution.py:19
  67.8 8.3 %collective-permute-start.6 = (bf16[512,256]{1,0:T(8,128)(2,1)S(1)}, bf16[512,256]{1,0:T(8,128)(2,1)S(1)}, u32[]{:S(2)}, u32[]{:S(2)}) collective-permute-start(bf16[512,256]{1,0:T(8,128)(2,1)S(1)} %copy-done.8), channel_id=1, source_target_pairs={{0,4},{1,5},{2,6},{3,7},{4,8},{5,9},{6,10},{7,11},{8,12},{9,13},{1... | collective-permute-start | bytes 786440 | tf_op jit(solution)/shard_map/ppermute | solution.py:19
  82.3 7.8 %collective-permute-start.7 = (bf16[512,256]{1,0:T(8,128)(2,1)S(1)}, bf16[512,256]{1,0:T(8,128)(2,1)S(1)}, u32[]{:S(2)}, u32[]{:S(2)}) collective-permute-start(bf16[512,256]{1,0:T(8,128)(2,1)S(1)} %copy-done.8), channel_id=1, source_target_pairs={{0,12},{1,13},{2,14},{3,15},{4,0},{5,1},{6,2},{7,3},{8,4},{9,5},{1... | collective-permute-start | bytes 786440 | tf_op jit(solution)/shard_map/ppermute | solution.py:19
  94.8 3.1 %collective-permute-done.7 = bf16[512,256]{1,0:T(8,128)(2,1)S(1)} collective-permute-done((bf16[512,256]{1,0:T(8,128)(2,1)S(1)}, bf16[512,256]{1,0:T(8,128)(2,1)S(1)}, u32[]{:S(2)}, u32[]{:S(2)}) %collective-permute-start.7) | collective-permute-done | bytes 262176 | tf_op jit(solution)/shard_map/ppermute | solution.py:19
  106.0 2.3 collective-permute-start.12
  108.5 3.8 %collective-permute-start.14 = (bf16[512,256]{1,0:T(8,128)(2,1)S(1)}, bf16[512,256]{1,0:T(8,128)(2,1)S(1)}, u32[]{:S(2)}, u32[]{:S(2)}) collective-permute-start(bf16[512,256]{1,0:T(8,128)(2,1)S(1)} %get-tuple-element.174), channel_id=1, source_target_pairs={{0,12},{1,13},{2,14},{3,15},{4,0},{5,1},{6,2},{7,3},{8,4},{9,5},{1... | collective-permute-start | bytes 786440 | tf_op jit(solution)/shard_map/ppermute | solution.py:19
  119.1 9.9 %collective-permute-done.11 = f32[114688]{0:T(1024)S(1)} collective-permute-done((f32[114688]{0:T(1024)S(1)}, f32[114688]{0:T(1024)S(1)}, u32[]{:S(2)}, u32[]{:S(2)}) %collective-permute-start.11) | collective-permute-done | bytes 458784 | tf_op jit(solution)/shard_map/ppermute | solution.py:25
  129.1 3.4 %collective-permute-done.15 = bf16[512,256]{1,0:T(8,128)(2,1)S(1)} collective-permute-done((bf16[512,256]{1,0:T(8,128)(2,1)S(1)}, bf16[512,256]{1,0:T(8,128)(2,1)S(1)}, u32[]{:S(2)}, u32[]{:S(2)}) %collective-permute-start.15) | collective-permute-done | bytes 262176 | tf_op jit(solution)/shard_map/ppermute | solution.py:19
  136.3 3.3 %collective-permute-start.19 = (bf16[256,256]{1,0:T(8,128)(2,1)S(1)}, bf16[256,256]{1,0:T(8,128)(2,1)S(1)}, u32[]{:S(2)}, u32[]{:S(2)}) collective-permute-start(bf16[256,256]{1,0:T(8,128)(2,1)S(1)} %get-tuple-element.157), channel_id=1, source_target_pairs={{0,12},{1,13},{2,14},{3,15},{4,0},{5,1},{6,2},{7,3},{8,4},{9,5},{1... | collective-permute-start | bytes 393224 | tf_op jit(solution)/shard_map/ppermute | solution.py:19
  141.1 4.6 %collective-permute-done.17 = bf16[256,256]{1,0:T(8,128)(2,1)S(1)} collective-permute-done((bf16[256,256]{1,0:T(8,128)(2,1)S(1)}, bf16[256,256]{1,0:T(8,128)(2,1)S(1)}, u32[]{:S(2)}, u32[]{:S(2)}) %collective-permute-start.17) | collective-permute-done | bytes 131104 | tf_op jit(solution)/shard_map/ppermute | solution.py:19
  149.2 2.5 %collective-permute-done.20 = bf16[256,256]{1,0:T(8,128)(2,1)S(1)} collective-permute-done((bf16[256,256]{1,0:T(8,128)(2,1)S(1)}, bf16[256,256]{1,0:T(8,128)(2,1)S(1)}, u32[]{:S(2)}, u32[]{:S(2)}) %collective-permute-start.20) | collective-permute-done | bytes 131104 | tf_op jit(solution)/shard_map/ppermute | solution.py:19
  151.8 3.3 %collective-permute-start.22 = (bf16[256,256]{1,0:T(8,128)(2,1)S(1)}, bf16[256,256]{1,0:T(8,128)(2,1)S(1)}, u32[]{:S(2)}, u32[]{:S(2)}) collective-permute-start(bf16[256,256]{1,0:T(8,128)(2,1)S(1)} %get-tuple-element.154), channel_id=1, source_target_pairs={{0,12},{1,13},{2,14},{3,15},{4,0},{5,1},{6,2},{7,3},{8,4},{9,5},{1... | collective-permute-start | bytes 393224 | tf_op jit(solution)/shard_map/ppermute | solution.py:19
  155.2 3.8 %collective-permute-start.24 = (bf16[256,256]{1,0:T(8,128)(2,1)S(1)}, bf16[256,256]{1,0:T(8,128)(2,1)S(1)}, u32[]{:S(2)}, u32[]{:S(2)}) collective-permute-start(bf16[256,256]{1,0:T(8,128)(2,1)S(1)} %get-tuple-element.153), channel_id=1, source_target_pairs={{0,12},{1,13},{2,14},{3,15},{4,0},{5,1},{6,2},{7,3},{8,4},{9,5},{1... | collective-permute-start | bytes 393224 | tf_op jit(solution)/shard_map/ppermute | solution.py:19
  161.5 3.1 %collective-permute-done.23 = bf16[256,256]{1,0:T(8,128)(2,1)S(1)} collective-permute-done((bf16[256,256]{1,0:T(8,128)(2,1)S(1)}, bf16[256,256]{1,0:T(8,128)(2,1)S(1)}, u32[]{:S(2)}, u32[]{:S(2)}) %collective-permute-start.23) | collective-permute-done | bytes 131104 | tf_op jit(solution)/shard_map/ppermute | solution.py:19
  164.6 3.8 %collective-permute-done.25 = bf16[256,256]{1,0:T(8,128)(2,1)S(1)} collective-permute-done((bf16[256,256]{1,0:T(8,128)(2,1)S(1)}, bf16[256,256]{1,0:T(8,128)(2,1)S(1)}, u32[]{:S(2)}, u32[]{:S(2)}) %collective-permute-start.25) | collective-permute-done | bytes 131104 | tf_op jit(solution)/shard_map/ppermute | solution.py:19
  169.9 2.7 %collective-permute-start.27 = (bf16[256,256]{1,0:T(8,128)(2,1)S(1)}, bf16[256,256]{1,0:T(8,128)(2,1)S(1)}, u32[]{:S(2)}, u32[]{:S(2)}) collective-permute-start(bf16[256,256]{1,0:T(8,128)(2,1)S(1)} %get-tuple-element.150), channel_id=1, source_target_pairs={{0,12},{1,13},{2,14},{3,15},{4,0},{5,1},{6,2},{7,3},{8,4},{9,5},{1... | collective-permute-start | bytes 393224 | tf_op jit(solution)/shard_map/ppermute | solution.py:19
  172.7 3.8 %collective-permute-start.29 = (bf16[256,256]{1,0:T(8,128)(2,1)S(1)}, bf16[256,256]{1,0:T(8,128)(2,1)S(1)}, u32[]{:S(2)}, u32[]{:S(2)}) collective-permute-start(bf16[256,256]{1,0:T(8,128)(2,1)S(1)} %get-tuple-element.149), channel_id=1, source_target_pairs={{0,12},{1,13},{2,14},{3,15},{4,0},{5,1},{6,2},{7,3},{8,4},{9,5},{1... | collective-permute-start | bytes 393224 | tf_op jit(solution)/shard_map/ppermute | solution.py:19
  178.4 3.7 %collective-permute-done.28 = bf16[256,256]{1,0:T(8,128)(2,1)S(1)} collective-permute-done((bf16[256,256]{1,0:T(8,128)(2,1)S(1)}, bf16[256,256]{1,0:T(8,128)(2,1)S(1)}, u32[]{:S(2)}, u32[]{:S(2)}) %collective-permute-start.28) | collective-permute-done | bytes 131104 | tf_op jit(solution)/shard_map/ppermute | solution.py:19
  188.6 3.8 %collective-permute-start.34 = (bf16[256,256]{1,0:T(8,128)(2,1)S(1)}, bf16[256,256]{1,0:T(8,128)(2,1)S(1)}, u32[]{:S(2)}, u32[]{:S(2)}) collective-permute-start(bf16[256,256]{1,0:T(8,128)(2,1)S(1)} %get-tuple-element.145), channel_id=1, source_target_pairs={{0,12},{1,13},{2,14},{3,15},{4,0},{5,1},{6,2},{7,3},{8,4},{9,5},{1... | collective-permute-start | bytes 393224 | tf_op jit(solution)/shard_map/ppermute | solution.py:19
  192.7 2.6 %collective-permute-done.32 = bf16[256,256]{1,0:T(8,128)(2,1)S(1)} collective-permute-done((bf16[256,256]{1,0:T(8,128)(2,1)S(1)}, bf16[256,256]{1,0:T(8,128)(2,1)S(1)}, u32[]{:S(2)}, u32[]{:S(2)}) %collective-permute-start.32) | collective-permute-done | bytes 131104 | tf_op jit(solution)/shard_map/ppermute | solution.py:19
  195.2 5.3 %collective-permute-done.33 = bf16[256,256]{1,0:T(8,128)(2,1)S(1)} collective-permute-done((bf16[256,256]{1,0:T(8,128)(2,1)S(1)}, bf16[256,256]{1,0:T(8,128)(2,1)S(1)}, u32[]{:S(2)}, u32[]{:S(2)}) %collective-permute-start.33) | collective-permute-done | bytes 131104 | tf_op jit(solution)/shard_map/ppermute | solution.py:19
  200.6 3.7 %collective-permute-done.35 = bf16[256,256]{1,0:T(8,128)(2,1)S(1)} collective-permute-done((bf16[256,256]{1,0:T(8,128)(2,1)S(1)}, bf16[256,256]{1,0:T(8,128)(2,1)S(1)}, u32[]{:S(2)}, u32[]{:S(2)}) %collective-permute-start.35) | collective-permute-done | bytes 131104 | tf_op jit(solution)/shard_map/ppermute | solution.py:19
  204.3 2.4 %collective-permute-start.36 = (f32[114688]{0:T(1024)S(1)}, f32[114688]{0:T(1024)S(1)}, u32[]{:S(2)}, u32[]{:S(2)}) collective-permute-start(f32[114688]{0:T(1024)S(1)} %pad_maximum_fusion.8), channel_id=1, source_target_pairs={{0,2},{1,3},{2,0},{3,1},{4,6},{5,7},{6,4},{7,5},{8,10},{9,11},{10,... | collective-permute-start | bytes 1376264 | tf_op jit(solution)/shard_map/ppermute | solution.py:25
  211.1 3.0 %collective-permute-done.36 = f32[114688]{0:T(1024)S(1)} collective-permute-done((f32[114688]{0:T(1024)S(1)}, f32[114688]{0:T(1024)S(1)}, u32[]{:S(2)}, u32[]{:S(2)}) %collective-permute-start.36) | collective-permute-done | bytes 458784 | tf_op jit(solution)/shard_map/ppermute | solution.py:25
  214.1 6.7 %collective-permute-done.37 = bf16[512,256]{1,0:T(8,128)(2,1)S(1)} collective-permute-done((bf16[512,256]{1,0:T(8,128)(2,1)S(1)}, bf16[512,256]{1,0:T(8,128)(2,1)S(1)}, u32[]{:S(2)}, u32[]{:S(2)}) %collective-permute-start.37) | collective-permute-done | bytes 262176 | tf_op jit(solution)/shard_map/ppermute | solution.py:19
  220.9 7.1 %collective-permute-done.39 = bf16[512,256]{1,0:T(8,128)(2,1)S(1)} collective-permute-done((bf16[512,256]{1,0:T(8,128)(2,1)S(1)}, bf16[512,256]{1,0:T(8,128)(2,1)S(1)}, u32[]{:S(2)}, u32[]{:S(2)}) %collective-permute-start.39) | collective-permute-done | bytes 262176 | tf_op jit(solution)/shard_map/ppermute | solution.py:19
  233.5 2.4 %pad_maximum_fusion = f32[768,512]{1,0:T(8,128)} fusion(f32[448,512]{1,0:T(8,128)S(1)} %copy-done.5, f32[448,512]{1,0:T(8,128)} %concatenate.89), kind=kLoop, calls=%fused_computation.4 | loop fusion | flops 393216 | bytes 3407872 | tf_op jit(solution)/shard_map/concatenate | solution.py:48
  (195 shorter events, 74.7 us)
Async XLA Ops:
  2.7 98.3 %collective-permute-start.8 = (bf16[512,256]{1,0:T(8,128)(2,1)}, bf16[512,256]{1,0:T(8,128)(2,1)S(1)}, u32[]{:S(2)}, u32[]{:S(2)}) collective-permute-start(bf16[512,256]{1,0:T(8,128)(2,1)} %get-tuple-element.163), channel_id=1, source_target_pairs={{0,4},{1,5},{2,6},{3,7},{4,8},{5,9},{6,10},{7,11},{8,12},{9,13},{1... | collective-permute-start | bytes 786440 | tf_op jit(solution)/shard_map/ppermute | solution.py:19
  5.7 95.3 %collective-permute-start.9 = (bf16[512,256]{1,0:T(8,128)(2,1)}, bf16[512,256]{1,0:T(8,128)(2,1)S(1)}, u32[]{:S(2)}, u32[]{:S(2)}) collective-permute-start(bf16[512,256]{1,0:T(8,128)(2,1)} %get-tuple-element.163), channel_id=1, source_target_pairs={{0,12},{1,13},{2,14},{3,15},{4,0},{5,1},{6,2},{7,3},{8,4},{9,5},{1... | collective-permute-start | bytes 786440 | tf_op jit(solution)/shard_map/ppermute | solution.py:19
  10.3 21.8 %collective-permute-start = (bf16[1024,256]{1,0:T(8,128)(2,1)}, bf16[1024,256]{1,0:T(8,128)(2,1)}, u32[]{:S(2)}, u32[]{:S(2)}) collective-permute-start(bf16[1024,256]{1,0:T(8,128)(2,1)} %get-tuple-element.161), channel_id=1, source_target_pairs={{0,4},{1,5},{2,6},{3,7},{4,8},{5,9},{6,10},{7,11},{8,12},{9,13},{1... | collective-permute-start | bytes 1572872 | tf_op jit(solution)/shard_map/ppermute | solution.py:19
  10.3 36.6 %collective-permute-start.1 = (bf16[1024,256]{1,0:T(8,128)(2,1)}, bf16[1024,256]{1,0:T(8,128)(2,1)}, u32[]{:S(2)}, u32[]{:S(2)}) collective-permute-start(bf16[1024,256]{1,0:T(8,128)(2,1)} %get-tuple-element.161), channel_id=1, source_target_pairs={{0,12},{1,13},{2,14},{3,15},{4,0},{5,1},{6,2},{7,3},{8,4},{9,5},{1... | collective-permute-start | bytes 1572872 | tf_op jit(solution)/shard_map/ppermute | solution.py:19
  14.1 40.5 %collective-permute-start.2 = (bf16[1024,256]{1,0:T(8,128)(2,1)}, bf16[1024,256]{1,0:T(8,128)(2,1)}, u32[]{:S(2)}, u32[]{:S(2)}) collective-permute-start(bf16[1024,256]{1,0:T(8,128)(2,1)} %get-tuple-element.159), channel_id=1, source_target_pairs={{0,4},{1,5},{2,6},{3,7},{4,8},{5,9},{6,10},{7,11},{8,12},{9,13},{1... | collective-permute-start | bytes 1572872 | tf_op jit(solution)/shard_map/ppermute | solution.py:19
  32.1 35.7 %collective-permute-start.3 = (bf16[1024,256]{1,0:T(8,128)(2,1)}, bf16[1024,256]{1,0:T(8,128)(2,1)S(1)}, u32[]{:S(2)}, u32[]{:S(2)}) collective-permute-start(bf16[1024,256]{1,0:T(8,128)(2,1)} %get-tuple-element.159), channel_id=1, source_target_pairs={{0,12},{1,13},{2,14},{3,15},{4,0},{5,1},{6,2},{7,3},{8,4},{9,5},{1... | collective-permute-start | bytes 1572872 | tf_op jit(solution)/shard_map/ppermute | solution.py:19
  46.9 35.4 %collective-permute-start.4 = (bf16[1024,256]{1,0:T(8,128)(2,1)S(1)}, bf16[1024,256]{1,0:T(8,128)(2,1)S(1)}, u32[]{:S(2)}, u32[]{:S(2)}) collective-permute-start(bf16[1024,256]{1,0:T(8,128)(2,1)S(1)} %copy-done.7), channel_id=1, source_target_pairs={{0,4},{1,5},{2,6},{3,7},{4,8},{5,9},{6,10},{7,11},{8,12},{9,13},{1... | collective-permute-start | bytes 1572872 | tf_op jit(solution)/shard_map/ppermute | solution.py:19
  54.6 35.5 %collective-permute-start.5 = (bf16[1024,256]{1,0:T(8,128)(2,1)S(1)}, bf16[1024,256]{1,0:T(8,128)(2,1)S(1)}, u32[]{:S(2)}, u32[]{:S(2)}) collective-permute-start(bf16[1024,256]{1,0:T(8,128)(2,1)S(1)} %copy-done.7), channel_id=1, source_target_pairs={{0,12},{1,13},{2,14},{3,15},{4,0},{5,1},{6,2},{7,3},{8,4},{9,5},{1... | collective-permute-start | bytes 1572872 | tf_op jit(solution)/shard_map/ppermute | solution.py:19
  67.8 27.0 %collective-permute-start.6 = (bf16[512,256]{1,0:T(8,128)(2,1)S(1)}, bf16[512,256]{1,0:T(8,128)(2,1)S(1)}, u32[]{:S(2)}, u32[]{:S(2)}) collective-permute-start(bf16[512,256]{1,0:T(8,128)(2,1)S(1)} %copy-done.8), channel_id=1, source_target_pairs={{0,4},{1,5},{2,6},{3,7},{4,8},{5,9},{6,10},{7,11},{8,12},{9,13},{1... | collective-permute-start | bytes 786440 | tf_op jit(solution)/shard_map/ppermute | solution.py:19
  82.3 15.6 %collective-permute-start.7 = (bf16[512,256]{1,0:T(8,128)(2,1)S(1)}, bf16[512,256]{1,0:T(8,128)(2,1)S(1)}, u32[]{:S(2)}, u32[]{:S(2)}) collective-permute-start(bf16[512,256]{1,0:T(8,128)(2,1)S(1)} %copy-done.8), channel_id=1, source_target_pairs={{0,12},{1,13},{2,14},{3,15},{4,0},{5,1},{6,2},{7,3},{8,4},{9,5},{1... | collective-permute-start | bytes 786440 | tf_op jit(solution)/shard_map/ppermute | solution.py:19
  105.9 10.8 %collective-permute-start.10 = (f32[229376]{0:T(1024)S(1)}, f32[229376]{0:T(1024)S(1)}, u32[]{:S(2)}, u32[]{:S(2)}) collective-permute-start(f32[229376]{0:T(1024)S(1)} %dynamic_slice.25), channel_id=1, source_target_pairs={{0,1},{1,0},{2,3},{3,2},{4,5},{5,4},{6,7},{7,6},{8,9},{9,8},{10,11... | collective-permute-start | bytes 2752520 | tf_op jit(solution)/shard_map/ppermute | solution.py:25
  106.0 23.0 %collective-permute-start.12 = (bf16[512,256]{1,0:T(8,128)(2,1)S(1)}, bf16[512,256]{1,0:T(8,128)(2,1)S(1)}, u32[]{:S(2)}, u32[]{:S(2)}) collective-permute-start(bf16[512,256]{1,0:T(8,128)(2,1)S(1)} %get-tuple-element.175), channel_id=1, source_target_pairs={{0,12},{1,13},{2,14},{3,15},{4,0},{5,1},{6,2},{7,3},{8,4},{9,5},{1... | collective-permute-start | bytes 786440 | tf_op jit(solution)/shard_map/ppermute | solution.py:19
  108.4 20.6 %collective-permute-start.13 = (bf16[512,256]{1,0:T(8,128)(2,1)S(1)}, bf16[512,256]{1,0:T(8,128)(2,1)S(1)}, u32[]{:S(2)}, u32[]{:S(2)}) collective-permute-start(bf16[512,256]{1,0:T(8,128)(2,1)S(1)} %get-tuple-element.173), channel_id=1, source_target_pairs={{0,4},{1,5},{2,6},{3,7},{4,8},{5,9},{6,10},{7,11},{8,12},{9,13},{1... | collective-permute-start | bytes 786440 | tf_op jit(solution)/shard_map/ppermute | solution.py:19
  108.5 20.6 %collective-permute-start.14 = (bf16[512,256]{1,0:T(8,128)(2,1)S(1)}, bf16[512,256]{1,0:T(8,128)(2,1)S(1)}, u32[]{:S(2)}, u32[]{:S(2)}) collective-permute-start(bf16[512,256]{1,0:T(8,128)(2,1)S(1)} %get-tuple-element.174), channel_id=1, source_target_pairs={{0,12},{1,13},{2,14},{3,15},{4,0},{5,1},{6,2},{7,3},{8,4},{9,5},{1... | collective-permute-start | bytes 786440 | tf_op jit(solution)/shard_map/ppermute | solution.py:19
  112.3 20.2 %collective-permute-start.15 = (bf16[512,256]{1,0:T(8,128)(2,1)S(1)}, bf16[512,256]{1,0:T(8,128)(2,1)S(1)}, u32[]{:S(2)}, u32[]{:S(2)}) collective-permute-start(bf16[512,256]{1,0:T(8,128)(2,1)S(1)} %get-tuple-element.172), channel_id=1, source_target_pairs={{0,4},{1,5},{2,6},{3,7},{4,8},{5,9},{6,10},{7,11},{8,12},{9,13},{1... | collective-permute-start | bytes 786440 | tf_op jit(solution)/shard_map/ppermute | solution.py:19
  116.9 12.1 %collective-permute-start.11 = (f32[114688]{0:T(1024)S(1)}, f32[114688]{0:T(1024)S(1)}, u32[]{:S(2)}, u32[]{:S(2)}) collective-permute-start(f32[114688]{0:T(1024)S(1)} %dynamic_slice.27), channel_id=1, source_target_pairs={{0,2},{1,3},{2,0},{3,1},{4,6},{5,7},{6,4},{7,5},{8,10},{9,11},{10,... | collective-permute-start | bytes 1376264 | tf_op jit(solution)/shard_map/ppermute | solution.py:25
  134.2 11.5 %collective-permute-start.17 = (bf16[256,256]{1,0:T(8,128)(2,1)S(1)}, bf16[256,256]{1,0:T(8,128)(2,1)S(1)}, u32[]{:S(2)}, u32[]{:S(2)}) collective-permute-start(bf16[256,256]{1,0:T(8,128)(2,1)S(1)} %get-tuple-element.158), channel_id=1, source_target_pairs={{0,12},{1,13},{2,14},{3,15},{4,0},{5,1},{6,2},{7,3},{8,4},{9,5},{1... | collective-permute-start | bytes 393224 | tf_op jit(solution)/shard_map/ppermute | solution.py:19
  135.7 12.1 %collective-permute-start.18 = (bf16[256,256]{1,0:T(8,128)(2,1)S(1)}, bf16[256,256]{1,0:T(8,128)(2,1)S(1)}, u32[]{:S(2)}, u32[]{:S(2)}) collective-permute-start(bf16[256,256]{1,0:T(8,128)(2,1)S(1)} %get-tuple-element.156), channel_id=1, source_target_pairs={{0,4},{1,5},{2,6},{3,7},{4,8},{5,9},{6,10},{7,11},{8,12},{9,13},{1... | collective-permute-start | bytes 393224 | tf_op jit(solution)/shard_map/ppermute | solution.py:19
  136.3 12.9 %collective-permute-start.19 = (bf16[256,256]{1,0:T(8,128)(2,1)S(1)}, bf16[256,256]{1,0:T(8,128)(2,1)S(1)}, u32[]{:S(2)}, u32[]{:S(2)}) collective-permute-start(bf16[256,256]{1,0:T(8,128)(2,1)S(1)} %get-tuple-element.157), channel_id=1, source_target_pairs={{0,12},{1,13},{2,14},{3,15},{4,0},{5,1},{6,2},{7,3},{8,4},{9,5},{1... | collective-permute-start | bytes 393224 | tf_op jit(solution)/shard_map/ppermute | solution.py:19
  139.6 12.1 %collective-permute-start.20 = (bf16[256,256]{1,0:T(8,128)(2,1)S(1)}, bf16[256,256]{1,0:T(8,128)(2,1)S(1)}, u32[]{:S(2)}, u32[]{:S(2)}) collective-permute-start(bf16[256,256]{1,0:T(8,128)(2,1)S(1)} %get-tuple-element.155), channel_id=1, source_target_pairs={{0,4},{1,5},{2,6},{3,7},{4,8},{5,9},{6,10},{7,11},{8,12},{9,13},{1... | collective-permute-start | bytes 393224 | tf_op jit(solution)/shard_map/ppermute | solution.py:19
  151.7 9.7 %collective-permute-start.21 = (f32[28672]{0:T(1024)S(1)}, f32[28672]{0:T(1024)S(1)}, u32[]{:S(2)}, u32[]{:S(2)}) collective-permute-start(f32[28672]{0:T(1024)S(1)} %dynamic_slice.31), channel_id=1, source_target_pairs={{0,8},{1,9},{2,10},{3,11},{4,12},{5,13},{6,14},{7,15},{8,0},{9,1},... | collective-permute-start | bytes 344072 | tf_op jit(solution)/shard_map/ppermute | solution.py:25
  151.8 9.6 %collective-permute-start.22 = (bf16[256,256]{1,0:T(8,128)(2,1)S(1)}, bf16[256,256]{1,0:T(8,128)(2,1)S(1)}, u32[]{:S(2)}, u32[]{:S(2)}) collective-permute-start(bf16[256,256]{1,0:T(8,128)(2,1)S(1)} %get-tuple-element.154), channel_id=1, source_target_pairs={{0,12},{1,13},{2,14},{3,15},{4,0},{5,1},{6,2},{7,3},{8,4},{9,5},{1... | collective-permute-start | bytes 393224 | tf_op jit(solution)/shard_map/ppermute | solution.py:19
  168.3 9.6 %collective-permute-start.26 = (f32[28672]{0:T(1024)S(1)}, f32[28672]{0:T(1024)S(1)}, u32[]{:S(2)}, u32[]{:S(2)}) collective-permute-start(f32[28672]{0:T(1024)S(1)} %add_multiply_fusion), channel_id=1, source_target_pairs={{0,8},{1,9},{2,10},{3,11},{4,12},{5,13},{6,14},{7,15},{8,0},{9,1},... | collective-permute-start | bytes 344072 | tf_op jit(solution)/shard_map/ppermute | solution.py:25
  172.7 9.9 %collective-permute-start.29 = (bf16[256,256]{1,0:T(8,128)(2,1)S(1)}, bf16[256,256]{1,0:T(8,128)(2,1)S(1)}, u32[]{:S(2)}, u32[]{:S(2)}) collective-permute-start(bf16[256,256]{1,0:T(8,128)(2,1)S(1)} %get-tuple-element.149), channel_id=1, source_target_pairs={{0,12},{1,13},{2,14},{3,15},{4,0},{5,1},{6,2},{7,3},{8,4},{9,5},{1... | collective-permute-start | bytes 393224 | tf_op jit(solution)/shard_map/ppermute | solution.py:19
  188.5 12.0 %collective-permute-start.33 = (bf16[256,256]{1,0:T(8,128)(2,1)S(1)}, bf16[256,256]{1,0:T(8,128)(2,1)S(1)}, u32[]{:S(2)}, u32[]{:S(2)}) collective-permute-start(bf16[256,256]{1,0:T(8,128)(2,1)S(1)} %get-tuple-element.144), channel_id=1, source_target_pairs={{0,4},{1,5},{2,6},{3,7},{4,8},{5,9},{6,10},{7,11},{8,12},{9,13},{1... | collective-permute-start | bytes 393224 | tf_op jit(solution)/shard_map/ppermute | solution.py:19
  188.6 12.0 %collective-permute-start.34 = (bf16[256,256]{1,0:T(8,128)(2,1)S(1)}, bf16[256,256]{1,0:T(8,128)(2,1)S(1)}, u32[]{:S(2)}, u32[]{:S(2)}) collective-permute-start(bf16[256,256]{1,0:T(8,128)(2,1)S(1)} %get-tuple-element.145), channel_id=1, source_target_pairs={{0,12},{1,13},{2,14},{3,15},{4,0},{5,1},{6,2},{7,3},{8,4},{9,5},{1... | collective-permute-start | bytes 393224 | tf_op jit(solution)/shard_map/ppermute | solution.py:19
  192.4 11.9 %collective-permute-start.35 = (bf16[256,256]{1,0:T(8,128)(2,1)S(1)}, bf16[256,256]{1,0:T(8,128)(2,1)S(1)}, u32[]{:S(2)}, u32[]{:S(2)}) collective-permute-start(bf16[256,256]{1,0:T(8,128)(2,1)S(1)} %get-tuple-element.143), channel_id=1, source_target_pairs={{0,4},{1,5},{2,6},{3,7},{4,8},{5,9},{6,10},{7,11},{8,12},{9,13},{1... | collective-permute-start | bytes 393224 | tf_op jit(solution)/shard_map/ppermute | solution.py:19
  204.3 9.7 %collective-permute-start.36 = (f32[114688]{0:T(1024)S(1)}, f32[114688]{0:T(1024)S(1)}, u32[]{:S(2)}, u32[]{:S(2)}) collective-permute-start(f32[114688]{0:T(1024)S(1)} %pad_maximum_fusion.8), channel_id=1, source_target_pairs={{0,2},{1,3},{2,0},{3,1},{4,6},{5,7},{6,4},{7,5},{8,10},{9,11},{10,... | collective-permute-start | bytes 1376264 | tf_op jit(solution)/shard_map/ppermute | solution.py:25
  206.8 14.1 %collective-permute-start.37 = (bf16[512,256]{1,0:T(8,128)(2,1)S(1)}, bf16[512,256]{1,0:T(8,128)(2,1)S(1)}, u32[]{:S(2)}, u32[]{:S(2)}) collective-permute-start(bf16[512,256]{1,0:T(8,128)(2,1)S(1)} %get-tuple-element.142), channel_id=1, source_target_pairs={{0,12},{1,13},{2,14},{3,15},{4,0},{5,1},{6,2},{7,3},{8,4},{9,5},{1... | collective-permute-start | bytes 786440 | tf_op jit(solution)/shard_map/ppermute | solution.py:19
  206.9 14.0 %collective-permute-start.38 = (bf16[512,256]{1,0:T(8,128)(2,1)S(1)}, bf16[512,256]{1,0:T(8,128)(2,1)S(1)}, u32[]{:S(2)}, u32[]{:S(2)}) collective-permute-start(bf16[512,256]{1,0:T(8,128)(2,1)S(1)} %get-tuple-element.140), channel_id=1, source_target_pairs={{0,4},{1,5},{2,6},{3,7},{4,8},{5,9},{6,10},{7,11},{8,12},{9,13},{1... | collective-permute-start | bytes 786440 | tf_op jit(solution)/shard_map/ppermute | solution.py:19
  209.0 19.0 %collective-permute-start.39 = (bf16[512,256]{1,0:T(8,128)(2,1)S(1)}, bf16[512,256]{1,0:T(8,128)(2,1)S(1)}, u32[]{:S(2)}, u32[]{:S(2)}) collective-permute-start(bf16[512,256]{1,0:T(8,128)(2,1)S(1)} %get-tuple-element.141), channel_id=1, source_target_pairs={{0,12},{1,13},{2,14},{3,15},{4,0},{5,1},{6,2},{7,3},{8,4},{9,5},{1... | collective-permute-start | bytes 786440 | tf_op jit(solution)/shard_map/ppermute | solution.py:19
  210.8 17.2 %collective-permute-start.40 = (bf16[512,256]{1,0:T(8,128)(2,1)S(1)}, bf16[512,256]{1,0:T(8,128)(2,1)S(1)}, u32[]{:S(2)}, u32[]{:S(2)}) collective-permute-start(bf16[512,256]{1,0:T(8,128)(2,1)S(1)} %get-tuple-element.139), channel_id=1, source_target_pairs={{0,4},{1,5},{2,6},{3,7},{4,8},{5,9},{6,10},{7,11},{8,12},{9,13},{1... | collective-permute-start | bytes 786440 | tf_op jit(solution)/shard_map/ppermute | solution.py:19
  (19 other events, 234.3 us)

commit v9 on v7

--- a/solution.py
+++ b/solution.py
@@ -117,7 +117,8 @@
         mids.append(term_mid)
         highs.append(upper_term)
     norm_factor = 1.0 / math.sqrt(positions * seq_size)
-    buf = jnp.concatenate([wconv_total.reshape(-1), wout_total.reshape(-1)])
+    wout_rows = wout_total.reshape(-1, wconv_total.shape[1])
+    buf = jnp.concatenate([wconv_total, wout_rows], axis=0)
     lower_all = jnp.concatenate(lows, axis=0)
     upper_all = jnp.concatenate(highs, axis=0)
 
@@ -166,8 +167,8 @@
     total_sum = cotangent.astype(jnp.float32) + jnp.concatenate(mids, axis=0)
     total_sum = total_sum + received_ahead.astype(jnp.float32) + received_behind.astype(jnp.float32)
     grad_input = total_sum.astype(jnp.bfloat16)
-    split = wconv_total.size
-    grad_conv = buf[:split].reshape(wconv_total.shape)
+    split = wconv_total.shape[0]
+    grad_conv = buf[:split]
     grad_out = buf[split:].reshape(wout_total.shape)
     return grad_input, grad_conv, grad_out
 

time: 226 us -> 229 us (1.013)
  waiting for transfers between devices: 82 us -> 60.9 us
  starting transfers between devices: 92.7 us -> 107 us
  matrix products: 33.6 us -> 41 us
    ppermute x8, waiting for transfers between devices: 43.7 us -> 28.6 us  [exchange(): return lax.ppermute(value, axis, pairs)]
    ppermute x8, starting transfers between devices: 12.6 us -> 25.1 us  [exchange(): return lax.ppermute(value, axis, pairs)]
    ppermute x26, waiting for transfers between devices: 38.3 us -> 32.3 us  [from_behind(): return lax.ppermute(value, axis, pairs)]
    unnamed x34 -> x75, local copies, waits for them, and re-layouts: 1.02 us -> 4.11 us
  transfers between devices with their start and end apart: 34 -> 34, of which waited for: 15 -> 15; matrix products, arithmetic and copies ran while one was open for 16% -> 18% of each run, Pallas kernels for 0% -> 0%
where the time goes in v9:
time: 229 us
  starting transfers between devices  107 us (47%)
  waiting for transfers between devices  60.9 us (27%)
  matrix products  41 us (18%)
  local copies, waits for them, and re-layouts  10.8 us (5%)
  other arithmetic  7.41 us (3%)
    ppermute x26, starting transfers between devices, from_behind(): return lax.ppermute(value, axis, pairs)  81.6 us
    ppermute x26, waiting for transfers between devices, from_behind(): return lax.ppermute(value, axis, pairs)  32.3 us
    ppermute x8, waiting for transfers between devices, exchange(): return lax.ppermute(value, axis, pairs)  28.6 us
    ppermute x8, starting transfers between devices, exchange(): return lax.ppermute(value, axis, pairs)  25.1 us
    dot_general x5, matrix products, chunk_layer(): preact = preact + jnp.dot(middle, w_mid, preferred_element_type=jnp.float32)  6.74 us
    dot_general x5, matrix products, chunk_layer(): lax.dot_general(left_tap_input, grad_pre, first_dims, preferred_element_t...  5.03 us
  transfers between devices with their start and end apart: 34, of which 15 were waited for; matrix products, arithmetic and copies ran while one was open for 18% of the time, Pallas kernels for 0%

profile of v9, /device:TPU:0, one launch (start us, length us, event | category | flops | bytes accessed | tf_op | source)
XLA Modules:
  0.0 228.6 jit_solution(13084077974387385065)
XLA Ops:
  0.7 1.9 fusion.120
  2.6 3.0 %collective-permute-start.8 = (bf16[512,256]{1,0:T(8,128)(2,1)}, bf16[512,256]{1,0:T(8,128)(2,1)S(1)}, u32[]{:S(2)}, u32[]{:S(2)}) collective-permute-start(bf16[512,256]{1,0:T(8,128)(2,1)} %get-tuple-element.131), channel_id=1, source_target_pairs={{0,4},{1,5},{2,6},{3,7},{4,8},{5,9},{6,10},{7,11},{8,12},{9,13},{1... | collective-permute-start | bytes 786440 | tf_op jit(solution)/shard_map/ppermute | solution.py:18
  5.6 2.0 collective-permute-start.9
  7.6 2.5 %fusion.119 = (bf16[1024,256]{1,0:T(8,128)(2,1)}, bf16[1024,256]{1,0:T(8,128)(2,1)}, bf16[1024,256]{1,0:T(8,128)(2,1)}) fusion(bf16[4096,256]{1,0:T(8,128)(2,1)} %param.4), kind=kLoop, calls=%fused_computation.213 | loop fusion | bytes 3145728 | tf_op jit(solution)/shard_map/slice | solution.py:95
  10.2 3.8 %collective-permute-start.1 = (bf16[1024,256]{1,0:T(8,128)(2,1)}, bf16[1024,256]{1,0:T(8,128)(2,1)}, u32[]{:S(2)}, u32[]{:S(2)}) collective-permute-start(bf16[1024,256]{1,0:T(8,128)(2,1)} %get-tuple-element.129), channel_id=1, source_target_pairs={{0,12},{1,13},{2,14},{3,15},{4,0},{5,1},{6,2},{7,3},{8,4},{9,5},{1... | collective-permute-start | bytes 1572872 | tf_op jit(solution)/shard_map/ppermute | solution.py:18
  14.0 2.8 %fusion.78 = f32[1024,512]{0,1:T(8,128)} fusion(bf16[768,512]{1,0:T(8,128)(2,1)S(1)} %copy-done.1, bf16[4096,256]{1,0:T(8,128)(2,1)} %param.4), kind=kOutput, calls=%fused_computation.177 | convolution fusion | flops 268435456 | bytes 2883584 | tf_op jit(solution)/shard_map/dot_general | solution.py:56
  20.6 11.4 %collective-permute-done = bf16[1024,256]{1,0:T(8,128)(2,1)} collective-permute-done((bf16[1024,256]{1,0:T(8,128)(2,1)}, bf16[1024,256]{1,0:T(8,128)(2,1)}, u32[]{:S(2)}, u32[]{:S(2)}) %collective-permute-start) | collective-permute-done | bytes 524320 | tf_op jit(solution)/shard_map/ppermute | solution.py:18
  32.0 13.2 %collective-permute-start.3 = (bf16[1024,256]{1,0:T(8,128)(2,1)}, bf16[1024,256]{1,0:T(8,128)(2,1)S(1)}, u32[]{:S(2)}, u32[]{:S(2)}) collective-permute-start(bf16[1024,256]{1,0:T(8,128)(2,1)} %get-tuple-element.127), channel_id=1, source_target_pairs={{0,12},{1,13},{2,14},{3,15},{4,0},{5,1},{6,2},{7,3},{8,4},{9,5},{1... | collective-permute-start | bytes 1572872 | tf_op jit(solution)/shard_map/ppermute | solution.py:18
  54.5 13.2 %collective-permute-start.5 = (bf16[1024,256]{1,0:T(8,128)(2,1)S(1)}, bf16[1024,256]{1,0:T(8,128)(2,1)S(1)}, u32[]{:S(2)}, u32[]{:S(2)}) collective-permute-start(bf16[1024,256]{1,0:T(8,128)(2,1)S(1)} %copy-done.21), channel_id=1, source_target_pairs={{0,12},{1,13},{2,14},{3,15},{4,0},{5,1},{6,2},{7,3},{8,4},{9,5},{1... | collective-permute-start | bytes 1572872 | tf_op jit(solution)/shard_map/ppermute | solution.py:18
  67.7 8.3 %collective-permute-start.6 = (bf16[512,256]{1,0:T(8,128)(2,1)S(1)}, bf16[512,256]{1,0:T(8,128)(2,1)S(1)}, u32[]{:S(2)}, u32[]{:S(2)}) collective-permute-start(bf16[512,256]{1,0:T(8,128)(2,1)S(1)} %copy-done.22), channel_id=1, source_target_pairs={{0,4},{1,5},{2,6},{3,7},{4,8},{5,9},{6,10},{7,11},{8,12},{9,13},{1... | collective-permute-start | bytes 786440 | tf_op jit(solution)/shard_map/ppermute | solution.py:18
  82.3 7.8 %collective-permute-start.7 = (bf16[512,256]{1,0:T(8,128)(2,1)S(1)}, bf16[512,256]{1,0:T(8,128)(2,1)S(1)}, u32[]{:S(2)}, u32[]{:S(2)}) collective-permute-start(bf16[512,256]{1,0:T(8,128)(2,1)S(1)} %copy-done.22), channel_id=1, source_target_pairs={{0,12},{1,13},{2,14},{3,15},{4,0},{5,1},{6,2},{7,3},{8,4},{9,5},{1... | collective-permute-start | bytes 786440 | tf_op jit(solution)/shard_map/ppermute | solution.py:18
  95.7 2.1 collective-permute-done.7
  113.1 2.4 %collective-permute-start.12 = (bf16[512,256]{1,0:T(8,128)(2,1)S(1)}, bf16[512,256]{1,0:T(8,128)(2,1)S(1)}, u32[]{:S(2)}, u32[]{:S(2)}) collective-permute-start(bf16[512,256]{1,0:T(8,128)(2,1)S(1)} %get-tuple-element.143), channel_id=1, source_target_pairs={{0,12},{1,13},{2,14},{3,15},{4,0},{5,1},{6,2},{7,3},{8,4},{9,5},{1... | collective-permute-start | bytes 786440 | tf_op jit(solution)/shard_map/ppermute | solution.py:18
  115.5 3.8 %collective-permute-start.14 = (bf16[512,256]{1,0:T(8,128)(2,1)S(1)}, bf16[512,256]{1,0:T(8,128)(2,1)S(1)}, u32[]{:S(2)}, u32[]{:S(2)}) collective-permute-start(bf16[512,256]{1,0:T(8,128)(2,1)S(1)} %get-tuple-element.142), channel_id=1, source_target_pairs={{0,12},{1,13},{2,14},{3,15},{4,0},{5,1},{6,2},{7,3},{8,4},{9,5},{1... | collective-permute-start | bytes 786440 | tf_op jit(solution)/shard_map/ppermute | solution.py:18
  129.1 9.2 %collective-permute-done.11 = f32[224,512]{1,0:T(8,128)S(1)} collective-permute-done((f32[224,512]{1,0:T(8,128)S(1)}, f32[224,512]{1,0:T(8,128)S(1)}, u32[]{:S(2)}, u32[]{:S(2)}) %collective-permute-start.11) | collective-permute-done | bytes 458784 | tf_op jit(solution)/shard_map/ppermute | solution.py:24
  142.7 6.0 %collective-permute-done.16 = f32[112,512]{1,0:T(8,128)S(1)} collective-permute-done((f32[112,512]{1,0:T(8,128)S(1)}, f32[112,512]{1,0:T(8,128)S(1)}, u32[]{:S(2)}, u32[]{:S(2)}) %collective-permute-start.16) | collective-permute-done | bytes 229408 | tf_op jit(solution)/shard_map/ppermute | solution.py:24
  148.7 6.9 %collective-permute-start.17 = (f32[56,512]{1,0:T(8,128)S(1)}, f32[56,512]{1,0:T(8,128)S(1)}, u32[]{:S(2)}, u32[]{:S(2)}) collective-permute-start(f32[56,512]{1,0:T(8,128)S(1)} %constant_dynamic-slice_fusion), channel_id=1, source_target_pairs={{0,8},{1,9},{2,10},{3,11},{4,12},{5,13},{6,14},{7,15},{8,0},{9,1},... | collective-permute-start | bytes 344072 | tf_op jit(solution)/shard_map/ppermute | solution.py:24
  155.7 2.0 collective-permute-start.21
  158.3 2.8 %collective-permute-done.17 = f32[56,512]{1,0:T(8,128)S(1)} collective-permute-done((f32[56,512]{1,0:T(8,128)S(1)}, f32[56,512]{1,0:T(8,128)S(1)}, u32[]{:S(2)}, u32[]{:S(2)}) %collective-permute-start.17) | collective-permute-done | bytes 114720 | tf_op jit(solution)/shard_map/ppermute | solution.py:24
  161.4 7.6 %collective-permute-start.20 = (f32[56,512]{1,0:T(8,128)S(1)}, f32[56,512]{1,0:T(8,128)S(1)}, u32[]{:S(2)}, u32[]{:S(2)}) collective-permute-start(f32[56,512]{1,0:T(8,128)S(1)} %add_multiply_fusion), channel_id=1, source_target_pairs={{0,8},{1,9},{2,10},{3,11},{4,12},{5,13},{6,14},{7,15},{8,0},{9,1},... | collective-permute-start | bytes 344072 | tf_op jit(solution)/shard_map/ppermute | solution.py:24
  169.1 2.1 collective-permute-start.24
  171.9 6.2 %collective-permute-done.20 = f32[56,512]{1,0:T(8,128)S(1)} collective-permute-done((f32[56,512]{1,0:T(8,128)S(1)}, f32[56,512]{1,0:T(8,128)S(1)}, u32[]{:S(2)}, u32[]{:S(2)}) %collective-permute-start.20) | collective-permute-done | bytes 114720 | tf_op jit(solution)/shard_map/ppermute | solution.py:24
  178.2 5.8 %collective-permute-start.23 = (f32[112,512]{1,0:T(8,128)S(1)}, f32[112,512]{1,0:T(8,128)S(1)}, u32[]{:S(2)}, u32[]{:S(2)}) collective-permute-start(f32[112,512]{1,0:T(8,128)S(1)} %pad_maximum_fusion.9), channel_id=1, source_target_pairs={{0,4},{1,5},{2,6},{3,7},{4,0},{5,1},{6,2},{7,3},{8,12},{9,13},{10,... | collective-permute-start | bytes 688136 | tf_op jit(solution)/shard_map/ppermute | solution.py:24
  184.0 2.9 %collective-permute-start.27 = (bf16[512,256]{1,0:T(8,128)(2,1)S(1)}, bf16[512,256]{1,0:T(8,128)(2,1)S(1)}, u32[]{:S(2)}, u32[]{:S(2)}) collective-permute-start(bf16[512,256]{1,0:T(8,128)(2,1)S(1)} %slice.168), channel_id=1, source_target_pairs={{0,12},{1,13},{2,14},{3,15},{4,0},{5,1},{6,2},{7,3},{8,4},{9,5},{1... | collective-permute-start | bytes 786440 | tf_op jit(solution)/shard_map/ppermute | solution.py:18
  187.0 4.4 %collective-permute-done.23 = f32[112,512]{1,0:T(8,128)S(1)} collective-permute-done((f32[112,512]{1,0:T(8,128)S(1)}, f32[112,512]{1,0:T(8,128)S(1)}, u32[]{:S(2)}, u32[]{:S(2)}) %collective-permute-start.23) | collective-permute-done | bytes 229408 | tf_op jit(solution)/shard_map/ppermute | solution.py:24
  193.0 9.6 %collective-permute-start.29 = (bf16[512,256]{1,0:T(8,128)(2,1)S(1)}, bf16[512,256]{1,0:T(8,128)(2,1)S(1)}, u32[]{:S(2)}, u32[]{:S(2)}) collective-permute-start(bf16[512,256]{1,0:T(8,128)(2,1)S(1)} %get-tuple-element.126), channel_id=1, source_target_pairs={{0,12},{1,13},{2,14},{3,15},{4,0},{5,1},{6,2},{7,3},{8,4},{9,5},{1... | collective-permute-start | bytes 786440 | tf_op jit(solution)/shard_map/ppermute | solution.py:18
  202.8 3.9 %collective-permute-start.31 = (bf16[512,256]{1,0:T(8,128)(2,1)S(1)}, bf16[512,256]{1,0:T(8,128)(2,1)S(1)}, u32[]{:S(2)}, u32[]{:S(2)}) collective-permute-start(bf16[512,256]{1,0:T(8,128)(2,1)S(1)} %get-tuple-element.125), channel_id=1, source_target_pairs={{0,12},{1,13},{2,14},{3,15},{4,0},{5,1},{6,2},{7,3},{8,4},{9,5},{1... | collective-permute-start | bytes 786440 | tf_op jit(solution)/shard_map/ppermute | solution.py:18
  206.9 5.0 %collective-permute-done.29 = bf16[512,256]{1,0:T(8,128)(2,1)S(1)} collective-permute-done((bf16[512,256]{1,0:T(8,128)(2,1)S(1)}, bf16[512,256]{1,0:T(8,128)(2,1)S(1)}, u32[]{:S(2)}, u32[]{:S(2)}) %collective-permute-start.29) | collective-permute-done | bytes 262176 | tf_op jit(solution)/shard_map/ppermute | solution.py:18
  211.9 3.9 %collective-permute-done.30 = bf16[512,256]{1,0:T(8,128)(2,1)S(1)} collective-permute-done((bf16[512,256]{1,0:T(8,128)(2,1)S(1)}, bf16[512,256]{1,0:T(8,128)(2,1)S(1)}, u32[]{:S(2)}, u32[]{:S(2)}) %collective-permute-start.30) | collective-permute-done | bytes 262176 | tf_op jit(solution)/shard_map/ppermute | solution.py:18
  215.8 3.4 %collective-permute-done.31 = bf16[512,256]{1,0:T(8,128)(2,1)S(1)} collective-permute-done((bf16[512,256]{1,0:T(8,128)(2,1)S(1)}, bf16[512,256]{1,0:T(8,128)(2,1)S(1)}, u32[]{:S(2)}, u32[]{:S(2)}) %collective-permute-start.31) | collective-permute-done | bytes 262176 | tf_op jit(solution)/shard_map/ppermute | solution.py:18
  219.1 4.8 %collective-permute-done.32 = bf16[512,256]{1,0:T(8,128)(2,1)S(1)} collective-permute-done((bf16[512,256]{1,0:T(8,128)(2,1)S(1)}, bf16[512,256]{1,0:T(8,128)(2,1)S(1)}, u32[]{:S(2)}, u32[]{:S(2)}) %collective-permute-start.32) | collective-permute-done | bytes 262176 | tf_op jit(solution)/shard_map/ppermute | solution.py:18
  224.1 2.2 add_convert_fusion
  (210 shorter events, 59.9 us)
Async XLA Ops:
  2.6 99.4 %collective-permute-start.8 = (bf16[512,256]{1,0:T(8,128)(2,1)}, bf16[512,256]{1,0:T(8,128)(2,1)S(1)}, u32[]{:S(2)}, u32[]{:S(2)}) collective-permute-start(bf16[512,256]{1,0:T(8,128)(2,1)} %get-tuple-element.131), channel_id=1, source_target_pairs={{0,4},{1,5},{2,6},{3,7},{4,8},{5,9},{6,10},{7,11},{8,12},{9,13},{1... | collective-permute-start | bytes 786440 | tf_op jit(solution)/shard_map/ppermute | solution.py:18
  5.6 96.4 %collective-permute-start.9 = (bf16[512,256]{1,0:T(8,128)(2,1)}, bf16[512,256]{1,0:T(8,128)(2,1)S(1)}, u32[]{:S(2)}, u32[]{:S(2)}) collective-permute-start(bf16[512,256]{1,0:T(8,128)(2,1)} %get-tuple-element.131), channel_id=1, source_target_pairs={{0,12},{1,13},{2,14},{3,15},{4,0},{5,1},{6,2},{7,3},{8,4},{9,5},{1... | collective-permute-start | bytes 786440 | tf_op jit(solution)/shard_map/ppermute | solution.py:18
  10.2 21.9 %collective-permute-start = (bf16[1024,256]{1,0:T(8,128)(2,1)}, bf16[1024,256]{1,0:T(8,128)(2,1)}, u32[]{:S(2)}, u32[]{:S(2)}) collective-permute-start(bf16[1024,256]{1,0:T(8,128)(2,1)} %get-tuple-element.129), channel_id=1, source_target_pairs={{0,4},{1,5},{2,6},{3,7},{4,8},{5,9},{6,10},{7,11},{8,12},{9,13},{1... | collective-permute-start | bytes 1572872 | tf_op jit(solution)/shard_map/ppermute | solution.py:18
  10.2 36.6 %collective-permute-start.1 = (bf16[1024,256]{1,0:T(8,128)(2,1)}, bf16[1024,256]{1,0:T(8,128)(2,1)}, u32[]{:S(2)}, u32[]{:S(2)}) collective-permute-start(bf16[1024,256]{1,0:T(8,128)(2,1)} %get-tuple-element.129), channel_id=1, source_target_pairs={{0,12},{1,13},{2,14},{3,15},{4,0},{5,1},{6,2},{7,3},{8,4},{9,5},{1... | collective-permute-start | bytes 1572872 | tf_op jit(solution)/shard_map/ppermute | solution.py:18
  14.0 40.5 %collective-permute-start.2 = (bf16[1024,256]{1,0:T(8,128)(2,1)}, bf16[1024,256]{1,0:T(8,128)(2,1)}, u32[]{:S(2)}, u32[]{:S(2)}) collective-permute-start(bf16[1024,256]{1,0:T(8,128)(2,1)} %get-tuple-element.127), channel_id=1, source_target_pairs={{0,4},{1,5},{2,6},{3,7},{4,8},{5,9},{6,10},{7,11},{8,12},{9,13},{1... | collective-permute-start | bytes 1572872 | tf_op jit(solution)/shard_map/ppermute | solution.py:18
  32.0 35.7 %collective-permute-start.3 = (bf16[1024,256]{1,0:T(8,128)(2,1)}, bf16[1024,256]{1,0:T(8,128)(2,1)S(1)}, u32[]{:S(2)}, u32[]{:S(2)}) collective-permute-start(bf16[1024,256]{1,0:T(8,128)(2,1)} %get-tuple-element.127), channel_id=1, source_target_pairs={{0,12},{1,13},{2,14},{3,15},{4,0},{5,1},{6,2},{7,3},{8,4},{9,5},{1... | collective-permute-start | bytes 1572872 | tf_op jit(solution)/shard_map/ppermute | solution.py:18
  46.8 35.5 %collective-permute-start.4 = (bf16[1024,256]{1,0:T(8,128)(2,1)S(1)}, bf16[1024,256]{1,0:T(8,128)(2,1)S(1)}, u32[]{:S(2)}, u32[]{:S(2)}) collective-permute-start(bf16[1024,256]{1,0:T(8,128)(2,1)S(1)} %copy-done.21), channel_id=1, source_target_pairs={{0,4},{1,5},{2,6},{3,7},{4,8},{5,9},{6,10},{7,11},{8,12},{9,13},{1... | collective-permute-start | bytes 1572872 | tf_op jit(solution)/shard_map/ppermute | solution.py:18
  54.5 35.5 %collective-permute-start.5 = (bf16[1024,256]{1,0:T(8,128)(2,1)S(1)}, bf16[1024,256]{1,0:T(8,128)(2,1)S(1)}, u32[]{:S(2)}, u32[]{:S(2)}) collective-permute-start(bf16[1024,256]{1,0:T(8,128)(2,1)S(1)} %copy-done.21), channel_id=1, source_target_pairs={{0,12},{1,13},{2,14},{3,15},{4,0},{5,1},{6,2},{7,3},{8,4},{9,5},{1... | collective-permute-start | bytes 1572872 | tf_op jit(solution)/shard_map/ppermute | solution.py:18
  67.7 28.0 %collective-permute-start.6 = (bf16[512,256]{1,0:T(8,128)(2,1)S(1)}, bf16[512,256]{1,0:T(8,128)(2,1)S(1)}, u32[]{:S(2)}, u32[]{:S(2)}) collective-permute-start(bf16[512,256]{1,0:T(8,128)(2,1)S(1)} %copy-done.22), channel_id=1, source_target_pairs={{0,4},{1,5},{2,6},{3,7},{4,8},{5,9},{6,10},{7,11},{8,12},{9,13},{1... | collective-permute-start | bytes 786440 | tf_op jit(solution)/shard_map/ppermute | solution.py:18
  82.3 15.6 %collective-permute-start.7 = (bf16[512,256]{1,0:T(8,128)(2,1)S(1)}, bf16[512,256]{1,0:T(8,128)(2,1)S(1)}, u32[]{:S(2)}, u32[]{:S(2)}) collective-permute-start(bf16[512,256]{1,0:T(8,128)(2,1)S(1)} %copy-done.22), channel_id=1, source_target_pairs={{0,12},{1,13},{2,14},{3,15},{4,0},{5,1},{6,2},{7,3},{8,4},{9,5},{1... | collective-permute-start | bytes 786440 | tf_op jit(solution)/shard_map/ppermute | solution.py:18
  112.3 14.2 %collective-permute-start.10 = (f32[448,512]{1,0:T(8,128)S(1)}, f32[448,512]{1,0:T(8,128)S(1)}, u32[]{:S(2)}, u32[]{:S(2)}) collective-permute-start(f32[448,512]{1,0:T(8,128)S(1)} %fusion.18), channel_id=1, source_target_pairs={{0,1},{1,0},{2,3},{3,2},{4,5},{5,4},{6,7},{7,6},{8,9},{9,8},{10,11... | collective-permute-start | bytes 2752520 | tf_op jit(solution)/shard_map/ppermute | solution.py:24
  113.1 25.3 %collective-permute-start.12 = (bf16[512,256]{1,0:T(8,128)(2,1)S(1)}, bf16[512,256]{1,0:T(8,128)(2,1)S(1)}, u32[]{:S(2)}, u32[]{:S(2)}) collective-permute-start(bf16[512,256]{1,0:T(8,128)(2,1)S(1)} %get-tuple-element.143), channel_id=1, source_target_pairs={{0,12},{1,13},{2,14},{3,15},{4,0},{5,1},{6,2},{7,3},{8,4},{9,5},{1... | collective-permute-start | bytes 786440 | tf_op jit(solution)/shard_map/ppermute | solution.py:18
  115.5 22.9 %collective-permute-start.13 = (bf16[512,256]{1,0:T(8,128)(2,1)S(1)}, bf16[512,256]{1,0:T(8,128)(2,1)S(1)}, u32[]{:S(2)}, u32[]{:S(2)}) collective-permute-start(bf16[512,256]{1,0:T(8,128)(2,1)S(1)} %get-tuple-element.141), channel_id=1, source_target_pairs={{0,4},{1,5},{2,6},{3,7},{4,8},{5,9},{6,10},{7,11},{8,12},{9,13},{1... | collective-permute-start | bytes 786440 | tf_op jit(solution)/shard_map/ppermute | solution.py:18
  115.5 22.9 %collective-permute-start.14 = (bf16[512,256]{1,0:T(8,128)(2,1)S(1)}, bf16[512,256]{1,0:T(8,128)(2,1)S(1)}, u32[]{:S(2)}, u32[]{:S(2)}) collective-permute-start(bf16[512,256]{1,0:T(8,128)(2,1)S(1)} %get-tuple-element.142), channel_id=1, source_target_pairs={{0,12},{1,13},{2,14},{3,15},{4,0},{5,1},{6,2},{7,3},{8,4},{9,5},{1... | collective-permute-start | bytes 786440 | tf_op jit(solution)/shard_map/ppermute | solution.py:18
  119.4 19.5 %collective-permute-start.15 = (bf16[512,256]{1,0:T(8,128)(2,1)S(1)}, bf16[512,256]{1,0:T(8,128)(2,1)S(1)}, u32[]{:S(2)}, u32[]{:S(2)}) collective-permute-start(bf16[512,256]{1,0:T(8,128)(2,1)S(1)} %get-tuple-element.140), channel_id=1, source_target_pairs={{0,4},{1,5},{2,6},{3,7},{4,8},{5,9},{6,10},{7,11},{8,12},{9,13},{1... | collective-permute-start | bytes 786440 | tf_op jit(solution)/shard_map/ppermute | solution.py:18
  126.8 11.5 %collective-permute-start.11 = (f32[224,512]{1,0:T(8,128)S(1)}, f32[224,512]{1,0:T(8,128)S(1)}, u32[]{:S(2)}, u32[]{:S(2)}) collective-permute-start(f32[224,512]{1,0:T(8,128)S(1)} %constant_dynamic-slice_fusion.2), channel_id=1, source_target_pairs={{0,2},{1,3},{2,0},{3,1},{4,6},{5,7},{6,4},{7,5},{8,10},{9,11},{10,... | collective-permute-start | bytes 1376264 | tf_op jit(solution)/shard_map/ppermute | solution.py:24
  140.5 20.9 %collective-permute-start.18 = (bf16[512,256]{1,0:T(8,128)(2,1)S(1)}, bf16[512,256]{1,0:T(8,128)(2,1)S(1)}, u32[]{:S(2)}, u32[]{:S(2)}) collective-permute-start(bf16[512,256]{1,0:T(8,128)(2,1)S(1)} %slice.162), channel_id=1, source_target_pairs={{0,12},{1,13},{2,14},{3,15},{4,0},{5,1},{6,2},{7,3},{8,4},{9,5},{1... | collective-permute-start | bytes 786440 | tf_op jit(solution)/shard_map/ppermute | solution.py:18
  142.1 19.3 %collective-permute-start.19 = (bf16[512,256]{1,0:T(8,128)(2,1)S(1)}, bf16[512,256]{1,0:T(8,128)(2,1)S(1)}, u32[]{:S(2)}, u32[]{:S(2)}) collective-permute-start(bf16[512,256]{1,0:T(8,128)(2,1)S(1)} %slice.163), channel_id=1, source_target_pairs={{0,4},{1,5},{2,6},{3,7},{4,8},{5,9},{6,10},{7,11},{8,12},{9,13},{1... | collective-permute-start | bytes 786440 | tf_op jit(solution)/shard_map/ppermute | solution.py:18
  148.7 12.4 %collective-permute-start.17 = (f32[56,512]{1,0:T(8,128)S(1)}, f32[56,512]{1,0:T(8,128)S(1)}, u32[]{:S(2)}, u32[]{:S(2)}) collective-permute-start(f32[56,512]{1,0:T(8,128)S(1)} %constant_dynamic-slice_fusion), channel_id=1, source_target_pairs={{0,8},{1,9},{2,10},{3,11},{4,12},{5,13},{6,14},{7,15},{8,0},{9,1},... | collective-permute-start | bytes 344072 | tf_op jit(solution)/shard_map/ppermute | solution.py:24
  155.7 22.5 %collective-permute-start.21 = (bf16[512,256]{1,0:T(8,128)(2,1)S(1)}, bf16[512,256]{1,0:T(8,128)(2,1)S(1)}, u32[]{:S(2)}, u32[]{:S(2)}) collective-permute-start(bf16[512,256]{1,0:T(8,128)(2,1)S(1)} %slice.164), channel_id=1, source_target_pairs={{0,12},{1,13},{2,14},{3,15},{4,0},{5,1},{6,2},{7,3},{8,4},{9,5},{1... | collective-permute-start | bytes 786440 | tf_op jit(solution)/shard_map/ppermute | solution.py:18
  157.7 20.5 %collective-permute-start.22 = (bf16[512,256]{1,0:T(8,128)(2,1)S(1)}, bf16[512,256]{1,0:T(8,128)(2,1)S(1)}, u32[]{:S(2)}, u32[]{:S(2)}) collective-permute-start(bf16[512,256]{1,0:T(8,128)(2,1)S(1)} %slice.165), channel_id=1, source_target_pairs={{0,4},{1,5},{2,6},{3,7},{4,8},{5,9},{6,10},{7,11},{8,12},{9,13},{1... | collective-permute-start | bytes 786440 | tf_op jit(solution)/shard_map/ppermute | solution.py:18
  161.4 16.7 %collective-permute-start.20 = (f32[56,512]{1,0:T(8,128)S(1)}, f32[56,512]{1,0:T(8,128)S(1)}, u32[]{:S(2)}, u32[]{:S(2)}) collective-permute-start(f32[56,512]{1,0:T(8,128)S(1)} %add_multiply_fusion), channel_id=1, source_target_pairs={{0,8},{1,9},{2,10},{3,11},{4,12},{5,13},{6,14},{7,15},{8,0},{9,1},... | collective-permute-start | bytes 344072 | tf_op jit(solution)/shard_map/ppermute | solution.py:24
  169.1 22.4 %collective-permute-start.24 = (bf16[512,256]{1,0:T(8,128)(2,1)S(1)}, bf16[512,256]{1,0:T(8,128)(2,1)S(1)}, u32[]{:S(2)}, u32[]{:S(2)}) collective-permute-start(bf16[512,256]{1,0:T(8,128)(2,1)S(1)} %slice.166), channel_id=1, source_target_pairs={{0,12},{1,13},{2,14},{3,15},{4,0},{5,1},{6,2},{7,3},{8,4},{9,5},{1... | collective-permute-start | bytes 786440 | tf_op jit(solution)/shard_map/ppermute | solution.py:18
  171.2 20.2 %collective-permute-start.25 = (bf16[512,256]{1,0:T(8,128)(2,1)S(1)}, bf16[512,256]{1,0:T(8,128)(2,1)S(1)}, u32[]{:S(2)}, u32[]{:S(2)}) collective-permute-start(bf16[512,256]{1,0:T(8,128)(2,1)S(1)} %slice.167), channel_id=1, source_target_pairs={{0,4},{1,5},{2,6},{3,7},{4,8},{5,9},{6,10},{7,11},{8,12},{9,13},{1... | collective-permute-start | bytes 786440 | tf_op jit(solution)/shard_map/ppermute | solution.py:18
  178.2 13.2 %collective-permute-start.23 = (f32[112,512]{1,0:T(8,128)S(1)}, f32[112,512]{1,0:T(8,128)S(1)}, u32[]{:S(2)}, u32[]{:S(2)}) collective-permute-start(f32[112,512]{1,0:T(8,128)S(1)} %pad_maximum_fusion.9), channel_id=1, source_target_pairs={{0,4},{1,5},{2,6},{3,7},{4,0},{5,1},{6,2},{7,3},{8,12},{9,13},{10,... | collective-permute-start | bytes 688136 | tf_op jit(solution)/shard_map/ppermute | solution.py:24
  184.0 18.9 %collective-permute-start.27 = (bf16[512,256]{1,0:T(8,128)(2,1)S(1)}, bf16[512,256]{1,0:T(8,128)(2,1)S(1)}, u32[]{:S(2)}, u32[]{:S(2)}) collective-permute-start(bf16[512,256]{1,0:T(8,128)(2,1)S(1)} %slice.168), channel_id=1, source_target_pairs={{0,12},{1,13},{2,14},{3,15},{4,0},{5,1},{6,2},{7,3},{8,4},{9,5},{1... | collective-permute-start | bytes 786440 | tf_op jit(solution)/shard_map/ppermute | solution.py:18
  186.9 20.0 %collective-permute-start.28 = (bf16[512,256]{1,0:T(8,128)(2,1)S(1)}, bf16[512,256]{1,0:T(8,128)(2,1)S(1)}, u32[]{:S(2)}, u32[]{:S(2)}) collective-permute-start(bf16[512,256]{1,0:T(8,128)(2,1)S(1)} %slice.169), channel_id=1, source_target_pairs={{0,4},{1,5},{2,6},{3,7},{4,8},{5,9},{6,10},{7,11},{8,12},{9,13},{1... | collective-permute-start | bytes 786440 | tf_op jit(solution)/shard_map/ppermute | solution.py:18
  191.4 15.2 %collective-permute-start.26 = (f32[224,512]{1,0:T(8,128)S(1)}, f32[224,512]{1,0:T(8,128)S(1)}, u32[]{:S(2)}, u32[]{:S(2)}) collective-permute-start(f32[224,512]{1,0:T(8,128)S(1)} %pad_maximum_fusion.8), channel_id=1, source_target_pairs={{0,2},{1,3},{2,0},{3,1},{4,6},{5,7},{6,4},{7,5},{8,10},{9,11},{10,... | collective-permute-start | bytes 1376264 | tf_op jit(solution)/shard_map/ppermute | solution.py:24
  193.0 18.8 %collective-permute-start.29 = (bf16[512,256]{1,0:T(8,128)(2,1)S(1)}, bf16[512,256]{1,0:T(8,128)(2,1)S(1)}, u32[]{:S(2)}, u32[]{:S(2)}) collective-permute-start(bf16[512,256]{1,0:T(8,128)(2,1)S(1)} %get-tuple-element.126), channel_id=1, source_target_pairs={{0,12},{1,13},{2,14},{3,15},{4,0},{5,1},{6,2},{7,3},{8,4},{9,5},{1... | collective-permute-start | bytes 786440 | tf_op jit(solution)/shard_map/ppermute | solution.py:18
  202.7 13.1 %collective-permute-start.30 = (bf16[512,256]{1,0:T(8,128)(2,1)S(1)}, bf16[512,256]{1,0:T(8,128)(2,1)S(1)}, u32[]{:S(2)}, u32[]{:S(2)}) collective-permute-start(bf16[512,256]{1,0:T(8,128)(2,1)S(1)} %get-tuple-element.124), channel_id=1, source_target_pairs={{0,4},{1,5},{2,6},{3,7},{4,8},{5,9},{6,10},{7,11},{8,12},{9,13},{1... | collective-permute-start | bytes 786440 | tf_op jit(solution)/shard_map/ppermute | solution.py:18
  202.8 16.3 %collective-permute-start.31 = (bf16[512,256]{1,0:T(8,128)(2,1)S(1)}, bf16[512,256]{1,0:T(8,128)(2,1)S(1)}, u32[]{:S(2)}, u32[]{:S(2)}) collective-permute-start(bf16[512,256]{1,0:T(8,128)(2,1)S(1)} %get-tuple-element.125), channel_id=1, source_target_pairs={{0,12},{1,13},{2,14},{3,15},{4,0},{5,1},{6,2},{7,3},{8,4},{9,5},{1... | collective-permute-start | bytes 786440 | tf_op jit(solution)/shard_map/ppermute | solution.py:18
  206.7 17.2 %collective-permute-start.32 = (bf16[512,256]{1,0:T(8,128)(2,1)S(1)}, bf16[512,256]{1,0:T(8,128)(2,1)S(1)}, u32[]{:S(2)}, u32[]{:S(2)}) collective-permute-start(bf16[512,256]{1,0:T(8,128)(2,1)S(1)} %get-tuple-element.123), channel_id=1, source_target_pairs={{0,4},{1,5},{2,6},{3,7},{4,8},{5,9},{6,10},{7,11},{8,12},{9,13},{1... | collective-permute-start | bytes 786440 | tf_op jit(solution)/shard_map/ppermute | solution.py:18
  (33 other events, 228.3 us)

commit v10 on v9

--- a/solution.py
+++ b/solution.py
@@ -10,6 +10,7 @@
 EARLY = 1
 RIDER_ROWS = 512
 RIDER_SPAN = 2
+LATE_BIT = 4
 
 
 def from_behind(value, axis, steps):
@@ -145,7 +146,7 @@
             buf, pieces = lax.optimization_barrier((buf, (lower_all, upper_all)))
             pending.append((send_rows(pieces, sent_rows, sent_rows + RIDER_ROWS), number + RIDER_SPAN))
             sent_rows += RIDER_ROWS
-        if not down and bit == 2 and not late:
+        if not down and bit == LATE_BIT and not late:
             buf, pieces = lax.optimization_barrier((buf, (lower_all, upper_all)))
             middle_row = sent_rows + (positions - sent_rows) // 2
             late.append(send_rows(pieces, sent_rows, middle_row))

time: 229 us -> 229 us (level)
    ppermute x8, waiting for transfers between devices: 28.6 us -> 31.7 us  [exchange(): return lax.ppermute(value, axis, pairs)]
    ppermute x26, waiting for transfers between devices: 32.3 us -> 29.4 us  [from_behind(): return lax.ppermute(value, axis, pairs)]
  transfers between devices with their start and end apart: 34 -> 34, of which waited for: 15 -> 16; matrix products, arithmetic and copies ran while one was open for 18% -> 18% of each run, Pallas kernels for 0% -> 0%
where the time goes in v10:
time: 229 us
  starting transfers between devices  107 us (47%)
  waiting for transfers between devices  61.1 us (27%)
  matrix products  41 us (18%)
  local copies, waits for them, and re-layouts  10.8 us (5%)
  other arithmetic  7.4 us (3%)
    ppermute x26, starting transfers between devices, from_behind(): return lax.ppermute(value, axis, pairs)  81.5 us
    ppermute x8, waiting for transfers between devices, exchange(): return lax.ppermute(value, axis, pairs)  31.7 us
    ppermute x26, waiting for transfers between devices, from_behind(): return lax.ppermute(value, axis, pairs)  29.4 us
    ppermute x8, starting transfers between devices, exchange(): return lax.ppermute(value, axis, pairs)  25.1 us
    dot_general x5, matrix products, chunk_layer(): preact = preact + jnp.dot(middle, w_mid, preferred_element_type=jnp.float32)  6.74 us
    dot_general x5, matrix products, chunk_layer(): lax.dot_general(left_tap_input, grad_pre, first_dims, preferred_element_t...  5.03 us
  transfers between devices with their start and end apart: 34, of which 16 were waited for; matrix products, arithmetic and copies ran while one was open for 18% of the time, Pallas kernels for 0%

profile of v10, /device:TPU:0, one launch (start us, length us, event | category | flops | bytes accessed | tf_op | source)
XLA Modules:
  0.0 228.6 jit_solution(9269911779501121154)
XLA Ops:
  2.6 3.0 %collective-permute-start.8 = (bf16[512,256]{1,0:T(8,128)(2,1)}, bf16[512,256]{1,0:T(8,128)(2,1)S(1)}, u32[]{:S(2)}, u32[]{:S(2)}) collective-permute-start(bf16[512,256]{1,0:T(8,128)(2,1)} %get-tuple-element.131), channel_id=1, source_target_pairs={{0,4},{1,5},{2,6},{3,7},{4,8},{5,9},{6,10},{7,11},{8,12},{9,13},{1... | collective-permute-start | bytes 786440 | tf_op jit(solution)/shard_map/ppermute | solution.py:19
  5.6 2.0 collective-permute-start.9
  7.6 2.5 %fusion.119 = (bf16[1024,256]{1,0:T(8,128)(2,1)}, bf16[1024,256]{1,0:T(8,128)(2,1)}, bf16[1024,256]{1,0:T(8,128)(2,1)}) fusion(bf16[4096,256]{1,0:T(8,128)(2,1)} %param.4), kind=kLoop, calls=%fused_computation.213 | loop fusion | bytes 3145728 | tf_op jit(solution)/shard_map/slice | solution.py:96
  10.2 3.8 %collective-permute-start.1 = (bf16[1024,256]{1,0:T(8,128)(2,1)}, bf16[1024,256]{1,0:T(8,128)(2,1)}, u32[]{:S(2)}, u32[]{:S(2)}) collective-permute-start(bf16[1024,256]{1,0:T(8,128)(2,1)} %get-tuple-element.129), channel_id=1, source_target_pairs={{0,12},{1,13},{2,14},{3,15},{4,0},{5,1},{6,2},{7,3},{8,4},{9,5},{1... | collective-permute-start | bytes 1572872 | tf_op jit(solution)/shard_map/ppermute | solution.py:19
  14.0 2.8 %fusion.78 = f32[1024,512]{0,1:T(8,128)} fusion(bf16[768,512]{1,0:T(8,128)(2,1)S(1)} %copy-done.1, bf16[4096,256]{1,0:T(8,128)(2,1)} %param.4), kind=kOutput, calls=%fused_computation.177 | convolution fusion | flops 268435456 | bytes 2883584 | tf_op jit(solution)/shard_map/dot_general | solution.py:57
  20.6 11.4 %collective-permute-done = bf16[1024,256]{1,0:T(8,128)(2,1)} collective-permute-done((bf16[1024,256]{1,0:T(8,128)(2,1)}, bf16[1024,256]{1,0:T(8,128)(2,1)}, u32[]{:S(2)}, u32[]{:S(2)}) %collective-permute-start) | collective-permute-done | bytes 524320 | tf_op jit(solution)/shard_map/ppermute | solution.py:19
  32.0 13.2 %collective-permute-start.3 = (bf16[1024,256]{1,0:T(8,128)(2,1)}, bf16[1024,256]{1,0:T(8,128)(2,1)S(1)}, u32[]{:S(2)}, u32[]{:S(2)}) collective-permute-start(bf16[1024,256]{1,0:T(8,128)(2,1)} %get-tuple-element.127), channel_id=1, source_target_pairs={{0,12},{1,13},{2,14},{3,15},{4,0},{5,1},{6,2},{7,3},{8,4},{9,5},{1... | collective-permute-start | bytes 1572872 | tf_op jit(solution)/shard_map/ppermute | solution.py:19
  54.5 13.2 %collective-permute-start.5 = (bf16[1024,256]{1,0:T(8,128)(2,1)S(1)}, bf16[1024,256]{1,0:T(8,128)(2,1)S(1)}, u32[]{:S(2)}, u32[]{:S(2)}) collective-permute-start(bf16[1024,256]{1,0:T(8,128)(2,1)S(1)} %copy-done.21), channel_id=1, source_target_pairs={{0,12},{1,13},{2,14},{3,15},{4,0},{5,1},{6,2},{7,3},{8,4},{9,5},{1... | collective-permute-start | bytes 1572872 | tf_op jit(solution)/shard_map/ppermute | solution.py:19
  67.7 8.3 %collective-permute-start.6 = (bf16[512,256]{1,0:T(8,128)(2,1)S(1)}, bf16[512,256]{1,0:T(8,128)(2,1)S(1)}, u32[]{:S(2)}, u32[]{:S(2)}) collective-permute-start(bf16[512,256]{1,0:T(8,128)(2,1)S(1)} %copy-done.22), channel_id=1, source_target_pairs={{0,4},{1,5},{2,6},{3,7},{4,8},{5,9},{6,10},{7,11},{8,12},{9,13},{1... | collective-permute-start | bytes 786440 | tf_op jit(solution)/shard_map/ppermute | solution.py:19
  82.3 7.8 %collective-permute-start.7 = (bf16[512,256]{1,0:T(8,128)(2,1)S(1)}, bf16[512,256]{1,0:T(8,128)(2,1)S(1)}, u32[]{:S(2)}, u32[]{:S(2)}) collective-permute-start(bf16[512,256]{1,0:T(8,128)(2,1)S(1)} %copy-done.22), channel_id=1, source_target_pairs={{0,12},{1,13},{2,14},{3,15},{4,0},{5,1},{6,2},{7,3},{8,4},{9,5},{1... | collective-permute-start | bytes 786440 | tf_op jit(solution)/shard_map/ppermute | solution.py:19
  95.7 2.1 collective-permute-done.7
  113.1 2.4 %collective-permute-start.12 = (bf16[512,256]{1,0:T(8,128)(2,1)S(1)}, bf16[512,256]{1,0:T(8,128)(2,1)S(1)}, u32[]{:S(2)}, u32[]{:S(2)}) collective-permute-start(bf16[512,256]{1,0:T(8,128)(2,1)S(1)} %get-tuple-element.143), channel_id=1, source_target_pairs={{0,12},{1,13},{2,14},{3,15},{4,0},{5,1},{6,2},{7,3},{8,4},{9,5},{1... | collective-permute-start | bytes 786440 | tf_op jit(solution)/shard_map/ppermute | solution.py:19
  115.5 3.8 %collective-permute-start.14 = (bf16[512,256]{1,0:T(8,128)(2,1)S(1)}, bf16[512,256]{1,0:T(8,128)(2,1)S(1)}, u32[]{:S(2)}, u32[]{:S(2)}) collective-permute-start(bf16[512,256]{1,0:T(8,128)(2,1)S(1)} %get-tuple-element.142), channel_id=1, source_target_pairs={{0,12},{1,13},{2,14},{3,15},{4,0},{5,1},{6,2},{7,3},{8,4},{9,5},{1... | collective-permute-start | bytes 786440 | tf_op jit(solution)/shard_map/ppermute | solution.py:19
  129.1 9.2 %collective-permute-done.11 = f32[224,512]{1,0:T(8,128)S(1)} collective-permute-done((f32[224,512]{1,0:T(8,128)S(1)}, f32[224,512]{1,0:T(8,128)S(1)}, u32[]{:S(2)}, u32[]{:S(2)}) %collective-permute-start.11) | collective-permute-done | bytes 458784 | tf_op jit(solution)/shard_map/ppermute | solution.py:25
  142.7 6.0 %collective-permute-done.16 = f32[112,512]{1,0:T(8,128)S(1)} collective-permute-done((f32[112,512]{1,0:T(8,128)S(1)}, f32[112,512]{1,0:T(8,128)S(1)}, u32[]{:S(2)}, u32[]{:S(2)}) %collective-permute-start.16) | collective-permute-done | bytes 229408 | tf_op jit(solution)/shard_map/ppermute | solution.py:25
  148.7 6.9 %collective-permute-start.17 = (f32[56,512]{1,0:T(8,128)S(1)}, f32[56,512]{1,0:T(8,128)S(1)}, u32[]{:S(2)}, u32[]{:S(2)}) collective-permute-start(f32[56,512]{1,0:T(8,128)S(1)} %constant_dynamic-slice_fusion), channel_id=1, source_target_pairs={{0,8},{1,9},{2,10},{3,11},{4,12},{5,13},{6,14},{7,15},{8,0},{9,1},... | collective-permute-start | bytes 344072 | tf_op jit(solution)/shard_map/ppermute | solution.py:25
  155.7 2.0 collective-permute-start.21
  158.3 2.8 %collective-permute-done.17 = f32[56,512]{1,0:T(8,128)S(1)} collective-permute-done((f32[56,512]{1,0:T(8,128)S(1)}, f32[56,512]{1,0:T(8,128)S(1)}, u32[]{:S(2)}, u32[]{:S(2)}) %collective-permute-start.17) | collective-permute-done | bytes 114720 | tf_op jit(solution)/shard_map/ppermute | solution.py:25
  161.4 7.6 %collective-permute-start.20 = (f32[56,512]{1,0:T(8,128)S(1)}, f32[56,512]{1,0:T(8,128)S(1)}, u32[]{:S(2)}, u32[]{:S(2)}) collective-permute-start(f32[56,512]{1,0:T(8,128)S(1)} %add_multiply_fusion), channel_id=1, source_target_pairs={{0,8},{1,9},{2,10},{3,11},{4,12},{5,13},{6,14},{7,15},{8,0},{9,1},... | collective-permute-start | bytes 344072 | tf_op jit(solution)/shard_map/ppermute | solution.py:25
  169.1 2.1 collective-permute-start.24
  171.9 6.2 %collective-permute-done.20 = f32[56,512]{1,0:T(8,128)S(1)} collective-permute-done((f32[56,512]{1,0:T(8,128)S(1)}, f32[56,512]{1,0:T(8,128)S(1)}, u32[]{:S(2)}, u32[]{:S(2)}) %collective-permute-start.20) | collective-permute-done | bytes 114720 | tf_op jit(solution)/shard_map/ppermute | solution.py:25
  178.2 5.8 %collective-permute-start.23 = (f32[112,512]{1,0:T(8,128)S(1)}, f32[112,512]{1,0:T(8,128)S(1)}, u32[]{:S(2)}, u32[]{:S(2)}) collective-permute-start(f32[112,512]{1,0:T(8,128)S(1)} %pad_maximum_fusion.9), channel_id=1, source_target_pairs={{0,4},{1,5},{2,6},{3,7},{4,0},{5,1},{6,2},{7,3},{8,12},{9,13},{10,... | collective-permute-start | bytes 688136 | tf_op jit(solution)/shard_map/ppermute | solution.py:25
  184.0 2.9 %collective-permute-start.27 = (bf16[512,256]{1,0:T(8,128)(2,1)S(1)}, bf16[512,256]{1,0:T(8,128)(2,1)S(1)}, u32[]{:S(2)}, u32[]{:S(2)}) collective-permute-start(bf16[512,256]{1,0:T(8,128)(2,1)S(1)} %slice.168), channel_id=1, source_target_pairs={{0,12},{1,13},{2,14},{3,15},{4,0},{5,1},{6,2},{7,3},{8,4},{9,5},{1... | collective-permute-start | bytes 786440 | tf_op jit(solution)/shard_map/ppermute | solution.py:19
  187.0 4.3 %collective-permute-done.23 = f32[112,512]{1,0:T(8,128)S(1)} collective-permute-done((f32[112,512]{1,0:T(8,128)S(1)}, f32[112,512]{1,0:T(8,128)S(1)}, u32[]{:S(2)}, u32[]{:S(2)}) %collective-permute-start.23) | collective-permute-done | bytes 229408 | tf_op jit(solution)/shard_map/ppermute | solution.py:25
  191.3 9.6 %collective-permute-start.29 = (bf16[512,256]{1,0:T(8,128)(2,1)S(1)}, bf16[512,256]{1,0:T(8,128)(2,1)S(1)}, u32[]{:S(2)}, u32[]{:S(2)}) collective-permute-start(bf16[512,256]{1,0:T(8,128)(2,1)S(1)} %get-tuple-element.126), channel_id=1, source_target_pairs={{0,12},{1,13},{2,14},{3,15},{4,0},{5,1},{6,2},{7,3},{8,4},{9,5},{1... | collective-permute-start | bytes 786440 | tf_op jit(solution)/shard_map/ppermute | solution.py:19
  202.7 3.8 %collective-permute-start.31 = (bf16[512,256]{1,0:T(8,128)(2,1)S(1)}, bf16[512,256]{1,0:T(8,128)(2,1)S(1)}, u32[]{:S(2)}, u32[]{:S(2)}) collective-permute-start(bf16[512,256]{1,0:T(8,128)(2,1)S(1)} %get-tuple-element.125), channel_id=1, source_target_pairs={{0,12},{1,13},{2,14},{3,15},{4,0},{5,1},{6,2},{7,3},{8,4},{9,5},{1... | collective-permute-start | bytes 786440 | tf_op jit(solution)/shard_map/ppermute | solution.py:19
  206.5 3.1 %collective-permute-done.26 = f32[224,512]{1,0:T(8,128)S(1)} collective-permute-done((f32[224,512]{1,0:T(8,128)S(1)}, f32[224,512]{1,0:T(8,128)S(1)}, u32[]{:S(2)}, u32[]{:S(2)}) %collective-permute-start.26) | collective-permute-done | bytes 458784 | tf_op jit(solution)/shard_map/ppermute | solution.py:25
  209.8 2.1 collective-permute-done.29
  211.9 4.0 %collective-permute-done.30 = bf16[512,256]{1,0:T(8,128)(2,1)S(1)} collective-permute-done((bf16[512,256]{1,0:T(8,128)(2,1)S(1)}, bf16[512,256]{1,0:T(8,128)(2,1)S(1)}, u32[]{:S(2)}, u32[]{:S(2)}) %collective-permute-start.30) | collective-permute-done | bytes 262176 | tf_op jit(solution)/shard_map/ppermute | solution.py:19
  215.8 3.1 %collective-permute-done.31 = bf16[512,256]{1,0:T(8,128)(2,1)S(1)} collective-permute-done((bf16[512,256]{1,0:T(8,128)(2,1)S(1)}, bf16[512,256]{1,0:T(8,128)(2,1)S(1)}, u32[]{:S(2)}, u32[]{:S(2)}) %collective-permute-start.31) | collective-permute-done | bytes 262176 | tf_op jit(solution)/shard_map/ppermute | solution.py:19
  218.9 5.0 %collective-permute-done.32 = bf16[512,256]{1,0:T(8,128)(2,1)S(1)} collective-permute-done((bf16[512,256]{1,0:T(8,128)(2,1)S(1)}, bf16[512,256]{1,0:T(8,128)(2,1)S(1)}, u32[]{:S(2)}, u32[]{:S(2)}) %collective-permute-start.32) | collective-permute-done | bytes 262176 | tf_op jit(solution)/shard_map/ppermute | solution.py:19
  224.1 2.2 add_convert_fusion
  (210 shorter events, 61.8 us)
Async XLA Ops:
  2.6 99.4 %collective-permute-start.8 = (bf16[512,256]{1,0:T(8,128)(2,1)}, bf16[512,256]{1,0:T(8,128)(2,1)S(1)}, u32[]{:S(2)}, u32[]{:S(2)}) collective-permute-start(bf16[512,256]{1,0:T(8,128)(2,1)} %get-tuple-element.131), channel_id=1, source_target_pairs={{0,4},{1,5},{2,6},{3,7},{4,8},{5,9},{6,10},{7,11},{8,12},{9,13},{1... | collective-permute-start | bytes 786440 | tf_op jit(solution)/shard_map/ppermute | solution.py:19
  5.6 96.4 %collective-permute-start.9 = (bf16[512,256]{1,0:T(8,128)(2,1)}, bf16[512,256]{1,0:T(8,128)(2,1)S(1)}, u32[]{:S(2)}, u32[]{:S(2)}) collective-permute-start(bf16[512,256]{1,0:T(8,128)(2,1)} %get-tuple-element.131), channel_id=1, source_target_pairs={{0,12},{1,13},{2,14},{3,15},{4,0},{5,1},{6,2},{7,3},{8,4},{9,5},{1... | collective-permute-start | bytes 786440 | tf_op jit(solution)/shard_map/ppermute | solution.py:19
  10.2 21.9 %collective-permute-start = (bf16[1024,256]{1,0:T(8,128)(2,1)}, bf16[1024,256]{1,0:T(8,128)(2,1)}, u32[]{:S(2)}, u32[]{:S(2)}) collective-permute-start(bf16[1024,256]{1,0:T(8,128)(2,1)} %get-tuple-element.129), channel_id=1, source_target_pairs={{0,4},{1,5},{2,6},{3,7},{4,8},{5,9},{6,10},{7,11},{8,12},{9,13},{1... | collective-permute-start | bytes 1572872 | tf_op jit(solution)/shard_map/ppermute | solution.py:19
  10.2 36.6 %collective-permute-start.1 = (bf16[1024,256]{1,0:T(8,128)(2,1)}, bf16[1024,256]{1,0:T(8,128)(2,1)}, u32[]{:S(2)}, u32[]{:S(2)}) collective-permute-start(bf16[1024,256]{1,0:T(8,128)(2,1)} %get-tuple-element.129), channel_id=1, source_target_pairs={{0,12},{1,13},{2,14},{3,15},{4,0},{5,1},{6,2},{7,3},{8,4},{9,5},{1... | collective-permute-start | bytes 1572872 | tf_op jit(solution)/shard_map/ppermute | solution.py:19
  14.0 40.5 %collective-permute-start.2 = (bf16[1024,256]{1,0:T(8,128)(2,1)}, bf16[1024,256]{1,0:T(8,128)(2,1)}, u32[]{:S(2)}, u32[]{:S(2)}) collective-permute-start(bf16[1024,256]{1,0:T(8,128)(2,1)} %get-tuple-element.127), channel_id=1, source_target_pairs={{0,4},{1,5},{2,6},{3,7},{4,8},{5,9},{6,10},{7,11},{8,12},{9,13},{1... | collective-permute-start | bytes 1572872 | tf_op jit(solution)/shard_map/ppermute | solution.py:19
  32.0 35.7 %collective-permute-start.3 = (bf16[1024,256]{1,0:T(8,128)(2,1)}, bf16[1024,256]{1,0:T(8,128)(2,1)S(1)}, u32[]{:S(2)}, u32[]{:S(2)}) collective-permute-start(bf16[1024,256]{1,0:T(8,128)(2,1)} %get-tuple-element.127), channel_id=1, source_target_pairs={{0,12},{1,13},{2,14},{3,15},{4,0},{5,1},{6,2},{7,3},{8,4},{9,5},{1... | collective-permute-start | bytes 1572872 | tf_op jit(solution)/shard_map/ppermute | solution.py:19
  46.8 35.5 %collective-permute-start.4 = (bf16[1024,256]{1,0:T(8,128)(2,1)S(1)}, bf16[1024,256]{1,0:T(8,128)(2,1)S(1)}, u32[]{:S(2)}, u32[]{:S(2)}) collective-permute-start(bf16[1024,256]{1,0:T(8,128)(2,1)S(1)} %copy-done.21), channel_id=1, source_target_pairs={{0,4},{1,5},{2,6},{3,7},{4,8},{5,9},{6,10},{7,11},{8,12},{9,13},{1... | collective-permute-start | bytes 1572872 | tf_op jit(solution)/shard_map/ppermute | solution.py:19
  54.5 35.5 %collective-permute-start.5 = (bf16[1024,256]{1,0:T(8,128)(2,1)S(1)}, bf16[1024,256]{1,0:T(8,128)(2,1)S(1)}, u32[]{:S(2)}, u32[]{:S(2)}) collective-permute-start(bf16[1024,256]{1,0:T(8,128)(2,1)S(1)} %copy-done.21), channel_id=1, source_target_pairs={{0,12},{1,13},{2,14},{3,15},{4,0},{5,1},{6,2},{7,3},{8,4},{9,5},{1... | collective-permute-start | bytes 1572872 | tf_op jit(solution)/shard_map/ppermute | solution.py:19
  67.7 28.0 %collective-permute-start.6 = (bf16[512,256]{1,0:T(8,128)(2,1)S(1)}, bf16[512,256]{1,0:T(8,128)(2,1)S(1)}, u32[]{:S(2)}, u32[]{:S(2)}) collective-permute-start(bf16[512,256]{1,0:T(8,128)(2,1)S(1)} %copy-done.22), channel_id=1, source_target_pairs={{0,4},{1,5},{2,6},{3,7},{4,8},{5,9},{6,10},{7,11},{8,12},{9,13},{1... | collective-permute-start | bytes 786440 | tf_op jit(solution)/shard_map/ppermute | solution.py:19
  82.3 15.6 %collective-permute-start.7 = (bf16[512,256]{1,0:T(8,128)(2,1)S(1)}, bf16[512,256]{1,0:T(8,128)(2,1)S(1)}, u32[]{:S(2)}, u32[]{:S(2)}) collective-permute-start(bf16[512,256]{1,0:T(8,128)(2,1)S(1)} %copy-done.22), channel_id=1, source_target_pairs={{0,12},{1,13},{2,14},{3,15},{4,0},{5,1},{6,2},{7,3},{8,4},{9,5},{1... | collective-permute-start | bytes 786440 | tf_op jit(solution)/shard_map/ppermute | solution.py:19
  112.3 14.2 %collective-permute-start.10 = (f32[448,512]{1,0:T(8,128)S(1)}, f32[448,512]{1,0:T(8,128)S(1)}, u32[]{:S(2)}, u32[]{:S(2)}) collective-permute-start(f32[448,512]{1,0:T(8,128)S(1)} %fusion.18), channel_id=1, source_target_pairs={{0,1},{1,0},{2,3},{3,2},{4,5},{5,4},{6,7},{7,6},{8,9},{9,8},{10,11... | collective-permute-start | bytes 2752520 | tf_op jit(solution)/shard_map/ppermute | solution.py:25
  113.1 25.3 %collective-permute-start.12 = (bf16[512,256]{1,0:T(8,128)(2,1)S(1)}, bf16[512,256]{1,0:T(8,128)(2,1)S(1)}, u32[]{:S(2)}, u32[]{:S(2)}) collective-permute-start(bf16[512,256]{1,0:T(8,128)(2,1)S(1)} %get-tuple-element.143), channel_id=1, source_target_pairs={{0,12},{1,13},{2,14},{3,15},{4,0},{5,1},{6,2},{7,3},{8,4},{9,5},{1... | collective-permute-start | bytes 786440 | tf_op jit(solution)/shard_map/ppermute | solution.py:19
  115.5 22.9 %collective-permute-start.13 = (bf16[512,256]{1,0:T(8,128)(2,1)S(1)}, bf16[512,256]{1,0:T(8,128)(2,1)S(1)}, u32[]{:S(2)}, u32[]{:S(2)}) collective-permute-start(bf16[512,256]{1,0:T(8,128)(2,1)S(1)} %get-tuple-element.141), channel_id=1, source_target_pairs={{0,4},{1,5},{2,6},{3,7},{4,8},{5,9},{6,10},{7,11},{8,12},{9,13},{1... | collective-permute-start | bytes 786440 | tf_op jit(solution)/shard_map/ppermute | solution.py:19
  115.5 22.9 %collective-permute-start.14 = (bf16[512,256]{1,0:T(8,128)(2,1)S(1)}, bf16[512,256]{1,0:T(8,128)(2,1)S(1)}, u32[]{:S(2)}, u32[]{:S(2)}) collective-permute-start(bf16[512,256]{1,0:T(8,128)(2,1)S(1)} %get-tuple-element.142), channel_id=1, source_target_pairs={{0,12},{1,13},{2,14},{3,15},{4,0},{5,1},{6,2},{7,3},{8,4},{9,5},{1... | collective-permute-start | bytes 786440 | tf_op jit(solution)/shard_map/ppermute | solution.py:19
  119.4 19.5 %collective-permute-start.15 = (bf16[512,256]{1,0:T(8,128)(2,1)S(1)}, bf16[512,256]{1,0:T(8,128)(2,1)S(1)}, u32[]{:S(2)}, u32[]{:S(2)}) collective-permute-start(bf16[512,256]{1,0:T(8,128)(2,1)S(1)} %get-tuple-element.140), channel_id=1, source_target_pairs={{0,4},{1,5},{2,6},{3,7},{4,8},{5,9},{6,10},{7,11},{8,12},{9,13},{1... | collective-permute-start | bytes 786440 | tf_op jit(solution)/shard_map/ppermute | solution.py:19
  126.8 11.5 %collective-permute-start.11 = (f32[224,512]{1,0:T(8,128)S(1)}, f32[224,512]{1,0:T(8,128)S(1)}, u32[]{:S(2)}, u32[]{:S(2)}) collective-permute-start(f32[224,512]{1,0:T(8,128)S(1)} %constant_dynamic-slice_fusion.2), channel_id=1, source_target_pairs={{0,2},{1,3},{2,0},{3,1},{4,6},{5,7},{6,4},{7,5},{8,10},{9,11},{10,... | collective-permute-start | bytes 1376264 | tf_op jit(solution)/shard_map/ppermute | solution.py:25
  138.8 9.8 %collective-permute-start.16 = (f32[112,512]{1,0:T(8,128)S(1)}, f32[112,512]{1,0:T(8,128)S(1)}, u32[]{:S(2)}, u32[]{:S(2)}) collective-permute-start(f32[112,512]{1,0:T(8,128)S(1)} %constant_dynamic-slice_fusion.1), channel_id=1, source_target_pairs={{0,4},{1,5},{2,6},{3,7},{4,0},{5,1},{6,2},{7,3},{8,12},{9,13},{10,... | collective-permute-start | bytes 688136 | tf_op jit(solution)/shard_map/ppermute | solution.py:25
  140.5 20.9 %collective-permute-start.18 = (bf16[512,256]{1,0:T(8,128)(2,1)S(1)}, bf16[512,256]{1,0:T(8,128)(2,1)S(1)}, u32[]{:S(2)}, u32[]{:S(2)}) collective-permute-start(bf16[512,256]{1,0:T(8,128)(2,1)S(1)} %slice.162), channel_id=1, source_target_pairs={{0,12},{1,13},{2,14},{3,15},{4,0},{5,1},{6,2},{7,3},{8,4},{9,5},{1... | collective-permute-start | bytes 786440 | tf_op jit(solution)/shard_map/ppermute | solution.py:19
  142.1 19.3 %collective-permute-start.19 = (bf16[512,256]{1,0:T(8,128)(2,1)S(1)}, bf16[512,256]{1,0:T(8,128)(2,1)S(1)}, u32[]{:S(2)}, u32[]{:S(2)}) collective-permute-start(bf16[512,256]{1,0:T(8,128)(2,1)S(1)} %slice.163), channel_id=1, source_target_pairs={{0,4},{1,5},{2,6},{3,7},{4,8},{5,9},{6,10},{7,11},{8,12},{9,13},{1... | collective-permute-start | bytes 786440 | tf_op jit(solution)/shard_map/ppermute | solution.py:19
  148.7 12.4 %collective-permute-start.17 = (f32[56,512]{1,0:T(8,128)S(1)}, f32[56,512]{1,0:T(8,128)S(1)}, u32[]{:S(2)}, u32[]{:S(2)}) collective-permute-start(f32[56,512]{1,0:T(8,128)S(1)} %constant_dynamic-slice_fusion), channel_id=1, source_target_pairs={{0,8},{1,9},{2,10},{3,11},{4,12},{5,13},{6,14},{7,15},{8,0},{9,1},... | collective-permute-start | bytes 344072 | tf_op jit(solution)/shard_map/ppermute | solution.py:25
  155.7 22.5 %collective-permute-start.21 = (bf16[512,256]{1,0:T(8,128)(2,1)S(1)}, bf16[512,256]{1,0:T(8,128)(2,1)S(1)}, u32[]{:S(2)}, u32[]{:S(2)}) collective-permute-start(bf16[512,256]{1,0:T(8,128)(2,1)S(1)} %slice.164), channel_id=1, source_target_pairs={{0,12},{1,13},{2,14},{3,15},{4,0},{5,1},{6,2},{7,3},{8,4},{9,5},{1... | collective-permute-start | bytes 786440 | tf_op jit(solution)/shard_map/ppermute | solution.py:19
  157.7 20.5 %collective-permute-start.22 = (bf16[512,256]{1,0:T(8,128)(2,1)S(1)}, bf16[512,256]{1,0:T(8,128)(2,1)S(1)}, u32[]{:S(2)}, u32[]{:S(2)}) collective-permute-start(bf16[512,256]{1,0:T(8,128)(2,1)S(1)} %slice.165), channel_id=1, source_target_pairs={{0,4},{1,5},{2,6},{3,7},{4,8},{5,9},{6,10},{7,11},{8,12},{9,13},{1... | collective-permute-start | bytes 786440 | tf_op jit(solution)/shard_map/ppermute | solution.py:19
  161.4 16.7 %collective-permute-start.20 = (f32[56,512]{1,0:T(8,128)S(1)}, f32[56,512]{1,0:T(8,128)S(1)}, u32[]{:S(2)}, u32[]{:S(2)}) collective-permute-start(f32[56,512]{1,0:T(8,128)S(1)} %add_multiply_fusion), channel_id=1, source_target_pairs={{0,8},{1,9},{2,10},{3,11},{4,12},{5,13},{6,14},{7,15},{8,0},{9,1},... | collective-permute-start | bytes 344072 | tf_op jit(solution)/shard_map/ppermute | solution.py:25
  169.1 31.9 %collective-permute-start.24 = (bf16[512,256]{1,0:T(8,128)(2,1)S(1)}, bf16[512,256]{1,0:T(8,128)(2,1)S(1)}, u32[]{:S(2)}, u32[]{:S(2)}) collective-permute-start(bf16[512,256]{1,0:T(8,128)(2,1)S(1)} %slice.166), channel_id=1, source_target_pairs={{0,12},{1,13},{2,14},{3,15},{4,0},{5,1},{6,2},{7,3},{8,4},{9,5},{1... | collective-permute-start | bytes 786440 | tf_op jit(solution)/shard_map/ppermute | solution.py:19
  171.2 29.9 %collective-permute-start.25 = (bf16[512,256]{1,0:T(8,128)(2,1)S(1)}, bf16[512,256]{1,0:T(8,128)(2,1)S(1)}, u32[]{:S(2)}, u32[]{:S(2)}) collective-permute-start(bf16[512,256]{1,0:T(8,128)(2,1)S(1)} %slice.167), channel_id=1, source_target_pairs={{0,4},{1,5},{2,6},{3,7},{4,8},{5,9},{6,10},{7,11},{8,12},{9,13},{1... | collective-permute-start | bytes 786440 | tf_op jit(solution)/shard_map/ppermute | solution.py:19
  178.2 13.2 %collective-permute-start.23 = (f32[112,512]{1,0:T(8,128)S(1)}, f32[112,512]{1,0:T(8,128)S(1)}, u32[]{:S(2)}, u32[]{:S(2)}) collective-permute-start(f32[112,512]{1,0:T(8,128)S(1)} %pad_maximum_fusion.9), channel_id=1, source_target_pairs={{0,4},{1,5},{2,6},{3,7},{4,0},{5,1},{6,2},{7,3},{8,12},{9,13},{10,... | collective-permute-start | bytes 688136 | tf_op jit(solution)/shard_map/ppermute | solution.py:25
  184.0 18.8 %collective-permute-start.27 = (bf16[512,256]{1,0:T(8,128)(2,1)S(1)}, bf16[512,256]{1,0:T(8,128)(2,1)S(1)}, u32[]{:S(2)}, u32[]{:S(2)}) collective-permute-start(bf16[512,256]{1,0:T(8,128)(2,1)S(1)} %slice.168), channel_id=1, source_target_pairs={{0,12},{1,13},{2,14},{3,15},{4,0},{5,1},{6,2},{7,3},{8,4},{9,5},{1... | collective-permute-start | bytes 786440 | tf_op jit(solution)/shard_map/ppermute | solution.py:19
  186.9 22.9 %collective-permute-start.28 = (bf16[512,256]{1,0:T(8,128)(2,1)S(1)}, bf16[512,256]{1,0:T(8,128)(2,1)S(1)}, u32[]{:S(2)}, u32[]{:S(2)}) collective-permute-start(bf16[512,256]{1,0:T(8,128)(2,1)S(1)} %slice.169), channel_id=1, source_target_pairs={{0,4},{1,5},{2,6},{3,7},{4,8},{5,9},{6,10},{7,11},{8,12},{9,13},{1... | collective-permute-start | bytes 786440 | tf_op jit(solution)/shard_map/ppermute | solution.py:19
  191.3 20.5 %collective-permute-start.29 = (bf16[512,256]{1,0:T(8,128)(2,1)S(1)}, bf16[512,256]{1,0:T(8,128)(2,1)S(1)}, u32[]{:S(2)}, u32[]{:S(2)}) collective-permute-start(bf16[512,256]{1,0:T(8,128)(2,1)S(1)} %get-tuple-element.126), channel_id=1, source_target_pairs={{0,12},{1,13},{2,14},{3,15},{4,0},{5,1},{6,2},{7,3},{8,4},{9,5},{1... | collective-permute-start | bytes 786440 | tf_op jit(solution)/shard_map/ppermute | solution.py:19
  201.0 14.8 %collective-permute-start.30 = (bf16[512,256]{1,0:T(8,128)(2,1)S(1)}, bf16[512,256]{1,0:T(8,128)(2,1)S(1)}, u32[]{:S(2)}, u32[]{:S(2)}) collective-permute-start(bf16[512,256]{1,0:T(8,128)(2,1)S(1)} %get-tuple-element.124), channel_id=1, source_target_pairs={{0,4},{1,5},{2,6},{3,7},{4,8},{5,9},{6,10},{7,11},{8,12},{9,13},{1... | collective-permute-start | bytes 786440 | tf_op jit(solution)/shard_map/ppermute | solution.py:19
  202.7 16.2 %collective-permute-start.31 = (bf16[512,256]{1,0:T(8,128)(2,1)S(1)}, bf16[512,256]{1,0:T(8,128)(2,1)S(1)}, u32[]{:S(2)}, u32[]{:S(2)}) collective-permute-start(bf16[512,256]{1,0:T(8,128)(2,1)S(1)} %get-tuple-element.125), channel_id=1, source_target_pairs={{0,12},{1,13},{2,14},{3,15},{4,0},{5,1},{6,2},{7,3},{8,4},{9,5},{1... | collective-permute-start | bytes 786440 | tf_op jit(solution)/shard_map/ppermute | solution.py:19
  209.6 14.3 %collective-permute-start.32 = (bf16[512,256]{1,0:T(8,128)(2,1)S(1)}, bf16[512,256]{1,0:T(8,128)(2,1)S(1)}, u32[]{:S(2)}, u32[]{:S(2)}) collective-permute-start(bf16[512,256]{1,0:T(8,128)(2,1)S(1)} %get-tuple-element.123), channel_id=1, source_target_pairs={{0,4},{1,5},{2,6},{3,7},{4,8},{5,9},{6,10},{7,11},{8,12},{9,13},{1... | collective-permute-start | bytes 786440 | tf_op jit(solution)/shard_map/ppermute | solution.py:19
  (33 other events, 224.0 us)

commit v11 on v9

--- a/solution.py
+++ b/solution.py
@@ -117,8 +117,7 @@
         mids.append(term_mid)
         highs.append(upper_term)
     norm_factor = 1.0 / math.sqrt(positions * seq_size)
-    wout_rows = wout_total.reshape(-1, wconv_total.shape[1])
-    buf = jnp.concatenate([wconv_total, wout_rows], axis=0)
+    buf = jnp.concatenate([wconv_total.reshape(-1), wout_total.reshape(-1)])
     lower_all = jnp.concatenate(lows, axis=0)
     upper_all = jnp.concatenate(highs, axis=0)
 
@@ -155,9 +154,9 @@
             buf, late = lax.optimization_barrier((buf, late))
         buf = chain_step(buf, "seq", bit, down)
         if down and number == len(steps) // 2 - 1:
-            buf = buf * jnp.float32(norm_factor)
+            buf = (buf * jnp.float32(norm_factor)).reshape(-1, wconv_total.shape[1])
     if not steps:
-        buf = buf * jnp.float32(norm_factor)
+        buf = (buf * jnp.float32(norm_factor)).reshape(-1, wconv_total.shape[1])
     early.extend(item[0] for item in pending)
     if sent_rows < positions:
         late.append(send_rows((lower_all, upper_all), sent_rows, positions))

time: 229 us -> 223 us (0.974)
  local copies, waits for them, and re-layouts: 10.8 us -> 19.5 us
  starting transfers between devices: 107 us -> 99.4 us
  matrix products: 41 us -> 33.5 us
    ppermute x8, starting transfers between devices: 25.1 us -> 14 us  [exchange(): return lax.ppermute(value, axis, pairs)]
    ppermute x26, waiting for transfers between devices: 32.3 us -> 36.8 us  [from_behind(): return lax.ppermute(value, axis, pairs)]
    slice x5, local copies, waits for them, and re-layouts: 0.11 us -> 4.46 us  [send_rows(): low_high[0][start:stop]]
    slice x5, local copies, waits for them, and re-layouts: 0.11 us -> 4.44 us  [send_rows(): low_high[1][start:stop]]
    ppermute x26, starting transfers between devices: 81.6 us -> 85.3 us  [from_behind(): return lax.ppermute(value, axis, pairs)]
    ppermute x8, waiting for transfers between devices: 28.6 us -> 25.8 us  [exchange(): return lax.ppermute(value, axis, pairs)]
    unnamed x75 -> x44, local copies, waits for them, and re-layouts: 4.11 us -> 5.04 us
  transfers between devices with their start and end apart: 34 -> 34, of which waited for: 15 -> 14; matrix products, arithmetic and copies ran while one was open for 18% -> 22% of each run, Pallas kernels for 0% -> 0%
where the time goes in v11:
time: 223 us
  starting transfers between devices  99.4 us (45%)
  waiting for transfers between devices  62.6 us (28%)
  matrix products  33.5 us (15%)
  local copies, waits for them, and re-layouts  19.5 us (9%)
  other arithmetic  5.76 us (3%)
    ppermute x26, starting transfers between devices, from_behind(): return lax.ppermute(value, axis, pairs)  85.3 us
    ppermute x26, waiting for transfers between devices, from_behind(): return lax.ppermute(value, axis, pairs)  36.8 us
    ppermute x8, waiting for transfers between devices, exchange(): return lax.ppermute(value, axis, pairs)  25.8 us
    ppermute x8, starting transfers between devices, exchange(): return lax.ppermute(value, axis, pairs)  14 us
    unnamed x44, local copies, waits for them, and re-layouts  5.04 us
    dot_general x5, matrix products, chunk_layer(): preact = preact + jnp.dot(middle, w_mid, preferred_element_type=jnp.float32)  4.65 us
    slice x2, local copies, waits for them, and re-layouts, body(): middle = activations[bounds[k]:bounds[k + 1]]  4.52 us
  transfers between devices with their start and end apart: 34, of which 14 were waited for; matrix products, arithmetic and copies ran while one was open for 22% of the time, Pallas kernels for 0%

profile of v11, /device:TPU:0, one launch (start us, length us, event | category | flops | bytes accessed | tf_op | source)
XLA Modules:
  0.0 222.5 jit_solution(13037291077703846166)
XLA Ops:
  0.7 2.0 fusion.119
  2.7 3.0 %collective-permute-start.8 = (bf16[512,256]{1,0:T(8,128)(2,1)}, bf16[512,256]{1,0:T(8,128)(2,1)S(1)}, u32[]{:S(2)}, u32[]{:S(2)}) collective-permute-start(bf16[512,256]{1,0:T(8,128)(2,1)} %get-tuple-element.131), channel_id=1, source_target_pairs={{0,4},{1,5},{2,6},{3,7},{4,8},{5,9},{6,10},{7,11},{8,12},{9,13},{1... | collective-permute-start | bytes 786440 | tf_op jit(solution)/shard_map/ppermute | solution.py:18
  5.7 2.0 collective-permute-start.9
  7.7 2.5 %fusion.118 = (bf16[1024,256]{1,0:T(8,128)(2,1)}, bf16[1024,256]{1,0:T(8,128)(2,1)}, bf16[1024,256]{1,0:T(8,128)(2,1)}) fusion(bf16[4096,256]{1,0:T(8,128)(2,1)} %param.4), kind=kLoop, calls=%fused_computation.208 | loop fusion | bytes 3145728 | tf_op jit(solution)/shard_map/slice | solution.py:95
  10.2 3.8 %collective-permute-start.1 = (bf16[1024,256]{1,0:T(8,128)(2,1)}, bf16[1024,256]{1,0:T(8,128)(2,1)}, u32[]{:S(2)}, u32[]{:S(2)}) collective-permute-start(bf16[1024,256]{1,0:T(8,128)(2,1)} %get-tuple-element.129), channel_id=1, source_target_pairs={{0,12},{1,13},{2,14},{3,15},{4,0},{5,1},{6,2},{7,3},{8,4},{9,5},{1... | collective-permute-start | bytes 1572872 | tf_op jit(solution)/shard_map/ppermute | solution.py:18
  14.1 1.8 fusion.77
  18.6 13.5 %collective-permute-done = bf16[1024,256]{1,0:T(8,128)(2,1)} collective-permute-done((bf16[1024,256]{1,0:T(8,128)(2,1)}, bf16[1024,256]{1,0:T(8,128)(2,1)}, u32[]{:S(2)}, u32[]{:S(2)}) %collective-permute-start) | collective-permute-done | bytes 524320 | tf_op jit(solution)/shard_map/ppermute | solution.py:18
  32.1 13.2 %collective-permute-start.3 = (bf16[1024,256]{1,0:T(8,128)(2,1)}, bf16[1024,256]{1,0:T(8,128)(2,1)S(1)}, u32[]{:S(2)}, u32[]{:S(2)}) collective-permute-start(bf16[1024,256]{1,0:T(8,128)(2,1)} %get-tuple-element.127), channel_id=1, source_target_pairs={{0,12},{1,13},{2,14},{3,15},{4,0},{5,1},{6,2},{7,3},{8,4},{9,5},{1... | collective-permute-start | bytes 1572872 | tf_op jit(solution)/shard_map/ppermute | solution.py:18
  54.6 13.2 %collective-permute-start.5 = (bf16[1024,256]{1,0:T(8,128)(2,1)S(1)}, bf16[1024,256]{1,0:T(8,128)(2,1)S(1)}, u32[]{:S(2)}, u32[]{:S(2)}) collective-permute-start(bf16[1024,256]{1,0:T(8,128)(2,1)S(1)} %copy-done.12), channel_id=1, source_target_pairs={{0,12},{1,13},{2,14},{3,15},{4,0},{5,1},{6,2},{7,3},{8,4},{9,5},{1... | collective-permute-start | bytes 1572872 | tf_op jit(solution)/shard_map/ppermute | solution.py:18
  67.8 8.3 %collective-permute-start.6 = (bf16[512,256]{1,0:T(8,128)(2,1)S(1)}, bf16[512,256]{1,0:T(8,128)(2,1)S(1)}, u32[]{:S(2)}, u32[]{:S(2)}) collective-permute-start(bf16[512,256]{1,0:T(8,128)(2,1)S(1)} %copy-done.13), channel_id=1, source_target_pairs={{0,4},{1,5},{2,6},{3,7},{4,8},{5,9},{6,10},{7,11},{8,12},{9,13},{1... | collective-permute-start | bytes 786440 | tf_op jit(solution)/shard_map/ppermute | solution.py:18
  82.3 7.8 %collective-permute-start.7 = (bf16[512,256]{1,0:T(8,128)(2,1)S(1)}, bf16[512,256]{1,0:T(8,128)(2,1)S(1)}, u32[]{:S(2)}, u32[]{:S(2)}) collective-permute-start(bf16[512,256]{1,0:T(8,128)(2,1)S(1)} %copy-done.13), channel_id=1, source_target_pairs={{0,12},{1,13},{2,14},{3,15},{4,0},{5,1},{6,2},{7,3},{8,4},{9,5},{1... | collective-permute-start | bytes 786440 | tf_op jit(solution)/shard_map/ppermute | solution.py:18
  94.8 3.1 %collective-permute-done.7 = bf16[512,256]{1,0:T(8,128)(2,1)S(1)} collective-permute-done((bf16[512,256]{1,0:T(8,128)(2,1)S(1)}, bf16[512,256]{1,0:T(8,128)(2,1)S(1)}, u32[]{:S(2)}, u32[]{:S(2)}) %collective-permute-start.7) | collective-permute-done | bytes 262176 | tf_op jit(solution)/shard_map/ppermute | solution.py:18
  106.0 2.4 %collective-permute-start.12 = (bf16[512,256]{1,0:T(8,128)(2,1)S(1)}, bf16[512,256]{1,0:T(8,128)(2,1)S(1)}, u32[]{:S(2)}, u32[]{:S(2)}) collective-permute-start(bf16[512,256]{1,0:T(8,128)(2,1)S(1)} %get-tuple-element.143), channel_id=1, source_target_pairs={{0,12},{1,13},{2,14},{3,15},{4,0},{5,1},{6,2},{7,3},{8,4},{9,5},{1... | collective-permute-start | bytes 786440 | tf_op jit(solution)/shard_map/ppermute | solution.py:18
  108.5 3.8 %collective-permute-start.14 = (bf16[512,256]{1,0:T(8,128)(2,1)S(1)}, bf16[512,256]{1,0:T(8,128)(2,1)S(1)}, u32[]{:S(2)}, u32[]{:S(2)}) collective-permute-start(bf16[512,256]{1,0:T(8,128)(2,1)S(1)} %get-tuple-element.142), channel_id=1, source_target_pairs={{0,12},{1,13},{2,14},{3,15},{4,0},{5,1},{6,2},{7,3},{8,4},{9,5},{1... | collective-permute-start | bytes 786440 | tf_op jit(solution)/shard_map/ppermute | solution.py:18
  119.1 9.9 %collective-permute-done.11 = f32[114688]{0:T(1024)S(1)} collective-permute-done((f32[114688]{0:T(1024)S(1)}, f32[114688]{0:T(1024)S(1)}, u32[]{:S(2)}, u32[]{:S(2)}) %collective-permute-start.11) | collective-permute-done | bytes 458784 | tf_op jit(solution)/shard_map/ppermute | solution.py:24
  129.0 3.4 %collective-permute-done.15 = bf16[512,256]{1,0:T(8,128)(2,1)S(1)} collective-permute-done((bf16[512,256]{1,0:T(8,128)(2,1)S(1)}, bf16[512,256]{1,0:T(8,128)(2,1)S(1)}, u32[]{:S(2)}, u32[]{:S(2)}) %collective-permute-start.15) | collective-permute-done | bytes 262176 | tf_op jit(solution)/shard_map/ppermute | solution.py:18
  138.3 2.7 %collective-permute-done.16 = f32[57344]{0:T(1024)S(1)} collective-permute-done((f32[57344]{0:T(1024)S(1)}, f32[57344]{0:T(1024)S(1)}, u32[]{:S(2)}, u32[]{:S(2)}) %collective-permute-start.16) | collective-permute-done | bytes 229408 | tf_op jit(solution)/shard_map/ppermute | solution.py:24
  141.1 1.7 collective-permute-start.17
  144.2 2.3 %collective-permute-start.21 = (bf16[512,256]{1,0:T(8,128)(2,1)}, bf16[512,256]{1,0:T(8,128)(2,1)S(1)}, u32[]{:S(2)}, u32[]{:S(2)}) collective-permute-start(bf16[512,256]{1,0:T(8,128)(2,1)} %slice.164), channel_id=1, source_target_pairs={{0,12},{1,13},{2,14},{3,15},{4,0},{5,1},{6,2},{7,3},{8,4},{9,5},{1... | collective-permute-start | bytes 786440 | tf_op jit(solution)/shard_map/ppermute | solution.py:18
  147.3 8.1 %collective-permute-done.17 = f32[28672]{0:T(1024)S(1)} collective-permute-done((f32[28672]{0:T(1024)S(1)}, f32[28672]{0:T(1024)S(1)}, u32[]{:S(2)}, u32[]{:S(2)}) %collective-permute-start.17) | collective-permute-done | bytes 114720 | tf_op jit(solution)/shard_map/ppermute | solution.py:24
  155.4 2.0 collective-permute-start.20
  158.4 6.5 %collective-permute-start.24 = (bf16[512,256]{1,0:T(8,128)(2,1)S(1)}, bf16[512,256]{1,0:T(8,128)(2,1)S(1)}, u32[]{:S(2)}, u32[]{:S(2)}) collective-permute-start(bf16[512,256]{1,0:T(8,128)(2,1)S(1)} %slice.166), channel_id=1, source_target_pairs={{0,12},{1,13},{2,14},{3,15},{4,0},{5,1},{6,2},{7,3},{8,4},{9,5},{1... | collective-permute-start | bytes 786440 | tf_op jit(solution)/shard_map/ppermute | solution.py:18
  168.3 3.5 %collective-permute-done.20 = f32[56,512]{1,0:T(8,128)S(1)} collective-permute-done((f32[56,512]{1,0:T(8,128)S(1)}, f32[56,512]{1,0:T(8,128)S(1)}, u32[]{:S(2)}, u32[]{:S(2)}) %collective-permute-start.20) | collective-permute-done | bytes 114720 | tf_op jit(solution)/shard_map/ppermute | solution.py:24
  171.8 5.5 %collective-permute-start.23 = (f32[112,512]{1,0:T(8,128)S(1)}, f32[112,512]{1,0:T(8,128)S(1)}, u32[]{:S(2)}, u32[]{:S(2)}) collective-permute-start(f32[112,512]{1,0:T(8,128)S(1)} %pad_maximum_fusion.9), channel_id=1, source_target_pairs={{0,4},{1,5},{2,6},{3,7},{4,0},{5,1},{6,2},{7,3},{8,12},{9,13},{10,... | collective-permute-start | bytes 688136 | tf_op jit(solution)/shard_map/ppermute | solution.py:24
  178.2 2.9 %collective-permute-start.27 = (bf16[512,256]{1,0:T(8,128)(2,1)S(1)}, bf16[512,256]{1,0:T(8,128)(2,1)S(1)}, u32[]{:S(2)}, u32[]{:S(2)}) collective-permute-start(bf16[512,256]{1,0:T(8,128)(2,1)S(1)} %slice.168), channel_id=1, source_target_pairs={{0,12},{1,13},{2,14},{3,15},{4,0},{5,1},{6,2},{7,3},{8,4},{9,5},{1... | collective-permute-start | bytes 786440 | tf_op jit(solution)/shard_map/ppermute | solution.py:18
  187.5 9.3 %collective-permute-start.29 = (bf16[512,256]{1,0:T(8,128)(2,1)S(1)}, bf16[512,256]{1,0:T(8,128)(2,1)S(1)}, u32[]{:S(2)}, u32[]{:S(2)}) collective-permute-start(bf16[512,256]{1,0:T(8,128)(2,1)S(1)} %get-tuple-element.126), channel_id=1, source_target_pairs={{0,12},{1,13},{2,14},{3,15},{4,0},{5,1},{6,2},{7,3},{8,4},{9,5},{1... | collective-permute-start | bytes 786440 | tf_op jit(solution)/shard_map/ppermute | solution.py:18
  198.0 3.9 %collective-permute-start.31 = (bf16[512,256]{1,0:T(8,128)(2,1)S(1)}, bf16[512,256]{1,0:T(8,128)(2,1)S(1)}, u32[]{:S(2)}, u32[]{:S(2)}) collective-permute-start(bf16[512,256]{1,0:T(8,128)(2,1)S(1)} %get-tuple-element.125), channel_id=1, source_target_pairs={{0,12},{1,13},{2,14},{3,15},{4,0},{5,1},{6,2},{7,3},{8,4},{9,5},{1... | collective-permute-start | bytes 786440 | tf_op jit(solution)/shard_map/ppermute | solution.py:18
  202.1 2.8 %collective-permute-done.29 = bf16[512,256]{1,0:T(8,128)(2,1)S(1)} collective-permute-done((bf16[512,256]{1,0:T(8,128)(2,1)S(1)}, bf16[512,256]{1,0:T(8,128)(2,1)S(1)}, u32[]{:S(2)}, u32[]{:S(2)}) %collective-permute-start.29) | collective-permute-done | bytes 262176 | tf_op jit(solution)/shard_map/ppermute | solution.py:18
  204.9 5.0 %collective-permute-done.30 = bf16[512,256]{1,0:T(8,128)(2,1)S(1)} collective-permute-done((bf16[512,256]{1,0:T(8,128)(2,1)S(1)}, bf16[512,256]{1,0:T(8,128)(2,1)S(1)}, u32[]{:S(2)}, u32[]{:S(2)}) %collective-permute-start.30) | collective-permute-done | bytes 262176 | tf_op jit(solution)/shard_map/ppermute | solution.py:18
  209.8 3.8 %collective-permute-done.31 = bf16[512,256]{1,0:T(8,128)(2,1)S(1)} collective-permute-done((bf16[512,256]{1,0:T(8,128)(2,1)S(1)}, bf16[512,256]{1,0:T(8,128)(2,1)S(1)}, u32[]{:S(2)}, u32[]{:S(2)}) %collective-permute-start.31) | collective-permute-done | bytes 262176 | tf_op jit(solution)/shard_map/ppermute | solution.py:18
  213.6 4.2 %collective-permute-done.32 = bf16[512,256]{1,0:T(8,128)(2,1)S(1)} collective-permute-done((bf16[512,256]{1,0:T(8,128)(2,1)S(1)}, bf16[512,256]{1,0:T(8,128)(2,1)S(1)}, u32[]{:S(2)}, u32[]{:S(2)}) %collective-permute-start.32) | collective-permute-done | bytes 262176 | tf_op jit(solution)/shard_map/ppermute | solution.py:18
  218.0 2.2 add_convert_fusion
  (180 shorter events, 60.7 us)
Async XLA Ops:
  2.7 98.3 %collective-permute-start.8 = (bf16[512,256]{1,0:T(8,128)(2,1)}, bf16[512,256]{1,0:T(8,128)(2,1)S(1)}, u32[]{:S(2)}, u32[]{:S(2)}) collective-permute-start(bf16[512,256]{1,0:T(8,128)(2,1)} %get-tuple-element.131), channel_id=1, source_target_pairs={{0,4},{1,5},{2,6},{3,7},{4,8},{5,9},{6,10},{7,11},{8,12},{9,13},{1... | collective-permute-start | bytes 786440 | tf_op jit(solution)/shard_map/ppermute | solution.py:18
  5.7 95.3 %collective-permute-start.9 = (bf16[512,256]{1,0:T(8,128)(2,1)}, bf16[512,256]{1,0:T(8,128)(2,1)S(1)}, u32[]{:S(2)}, u32[]{:S(2)}) collective-permute-start(bf16[512,256]{1,0:T(8,128)(2,1)} %get-tuple-element.131), channel_id=1, source_target_pairs={{0,12},{1,13},{2,14},{3,15},{4,0},{5,1},{6,2},{7,3},{8,4},{9,5},{1... | collective-permute-start | bytes 786440 | tf_op jit(solution)/shard_map/ppermute | solution.py:18
  10.2 21.9 %collective-permute-start = (bf16[1024,256]{1,0:T(8,128)(2,1)}, bf16[1024,256]{1,0:T(8,128)(2,1)}, u32[]{:S(2)}, u32[]{:S(2)}) collective-permute-start(bf16[1024,256]{1,0:T(8,128)(2,1)} %get-tuple-element.129), channel_id=1, source_target_pairs={{0,4},{1,5},{2,6},{3,7},{4,8},{5,9},{6,10},{7,11},{8,12},{9,13},{1... | collective-permute-start | bytes 1572872 | tf_op jit(solution)/shard_map/ppermute | solution.py:18
  10.2 36.6 %collective-permute-start.1 = (bf16[1024,256]{1,0:T(8,128)(2,1)}, bf16[1024,256]{1,0:T(8,128)(2,1)}, u32[]{:S(2)}, u32[]{:S(2)}) collective-permute-start(bf16[1024,256]{1,0:T(8,128)(2,1)} %get-tuple-element.129), channel_id=1, source_target_pairs={{0,12},{1,13},{2,14},{3,15},{4,0},{5,1},{6,2},{7,3},{8,4},{9,5},{1... | collective-permute-start | bytes 1572872 | tf_op jit(solution)/shard_map/ppermute | solution.py:18
  14.1 40.6 %collective-permute-start.2 = (bf16[1024,256]{1,0:T(8,128)(2,1)}, bf16[1024,256]{1,0:T(8,128)(2,1)}, u32[]{:S(2)}, u32[]{:S(2)}) collective-permute-start(bf16[1024,256]{1,0:T(8,128)(2,1)} %get-tuple-element.127), channel_id=1, source_target_pairs={{0,4},{1,5},{2,6},{3,7},{4,8},{5,9},{6,10},{7,11},{8,12},{9,13},{1... | collective-permute-start | bytes 1572872 | tf_op jit(solution)/shard_map/ppermute | solution.py:18
  32.1 35.7 %collective-permute-start.3 = (bf16[1024,256]{1,0:T(8,128)(2,1)}, bf16[1024,256]{1,0:T(8,128)(2,1)S(1)}, u32[]{:S(2)}, u32[]{:S(2)}) collective-permute-start(bf16[1024,256]{1,0:T(8,128)(2,1)} %get-tuple-element.127), channel_id=1, source_target_pairs={{0,12},{1,13},{2,14},{3,15},{4,0},{5,1},{6,2},{7,3},{8,4},{9,5},{1... | collective-permute-start | bytes 1572872 | tf_op jit(solution)/shard_map/ppermute | solution.py:18
  46.9 35.4 %collective-permute-start.4 = (bf16[1024,256]{1,0:T(8,128)(2,1)S(1)}, bf16[1024,256]{1,0:T(8,128)(2,1)S(1)}, u32[]{:S(2)}, u32[]{:S(2)}) collective-permute-start(bf16[1024,256]{1,0:T(8,128)(2,1)S(1)} %copy-done.12), channel_id=1, source_target_pairs={{0,4},{1,5},{2,6},{3,7},{4,8},{5,9},{6,10},{7,11},{8,12},{9,13},{1... | collective-permute-start | bytes 1572872 | tf_op jit(solution)/shard_map/ppermute | solution.py:18
  54.6 35.5 %collective-permute-start.5 = (bf16[1024,256]{1,0:T(8,128)(2,1)S(1)}, bf16[1024,256]{1,0:T(8,128)(2,1)S(1)}, u32[]{:S(2)}, u32[]{:S(2)}) collective-permute-start(bf16[1024,256]{1,0:T(8,128)(2,1)S(1)} %copy-done.12), channel_id=1, source_target_pairs={{0,12},{1,13},{2,14},{3,15},{4,0},{5,1},{6,2},{7,3},{8,4},{9,5},{1... | collective-permute-start | bytes 1572872 | tf_op jit(solution)/shard_map/ppermute | solution.py:18
  67.8 27.0 %collective-permute-start.6 = (bf16[512,256]{1,0:T(8,128)(2,1)S(1)}, bf16[512,256]{1,0:T(8,128)(2,1)S(1)}, u32[]{:S(2)}, u32[]{:S(2)}) collective-permute-start(bf16[512,256]{1,0:T(8,128)(2,1)S(1)} %copy-done.13), channel_id=1, source_target_pairs={{0,4},{1,5},{2,6},{3,7},{4,8},{5,9},{6,10},{7,11},{8,12},{9,13},{1... | collective-permute-start | bytes 786440 | tf_op jit(solution)/shard_map/ppermute | solution.py:18
  82.3 15.6 %collective-permute-start.7 = (bf16[512,256]{1,0:T(8,128)(2,1)S(1)}, bf16[512,256]{1,0:T(8,128)(2,1)S(1)}, u32[]{:S(2)}, u32[]{:S(2)}) collective-permute-start(bf16[512,256]{1,0:T(8,128)(2,1)S(1)} %copy-done.13), channel_id=1, source_target_pairs={{0,12},{1,13},{2,14},{3,15},{4,0},{5,1},{6,2},{7,3},{8,4},{9,5},{1... | collective-permute-start | bytes 786440 | tf_op jit(solution)/shard_map/ppermute | solution.py:18
  105.9 10.8 %collective-permute-start.10 = (f32[229376]{0:T(1024)S(1)}, f32[229376]{0:T(1024)S(1)}, u32[]{:S(2)}, u32[]{:S(2)}) collective-permute-start(f32[229376]{0:T(1024)S(1)} %dynamic_slice.25), channel_id=1, source_target_pairs={{0,1},{1,0},{2,3},{3,2},{4,5},{5,4},{6,7},{7,6},{8,9},{9,8},{10,11... | collective-permute-start | bytes 2752520 | tf_op jit(solution)/shard_map/ppermute | solution.py:24
  106.0 23.0 %collective-permute-start.12 = (bf16[512,256]{1,0:T(8,128)(2,1)S(1)}, bf16[512,256]{1,0:T(8,128)(2,1)S(1)}, u32[]{:S(2)}, u32[]{:S(2)}) collective-permute-start(bf16[512,256]{1,0:T(8,128)(2,1)S(1)} %get-tuple-element.143), channel_id=1, source_target_pairs={{0,12},{1,13},{2,14},{3,15},{4,0},{5,1},{6,2},{7,3},{8,4},{9,5},{1... | collective-permute-start | bytes 786440 | tf_op jit(solution)/shard_map/ppermute | solution.py:18
  108.4 20.6 %collective-permute-start.13 = (bf16[512,256]{1,0:T(8,128)(2,1)S(1)}, bf16[512,256]{1,0:T(8,128)(2,1)S(1)}, u32[]{:S(2)}, u32[]{:S(2)}) collective-permute-start(bf16[512,256]{1,0:T(8,128)(2,1)S(1)} %get-tuple-element.141), channel_id=1, source_target_pairs={{0,4},{1,5},{2,6},{3,7},{4,8},{5,9},{6,10},{7,11},{8,12},{9,13},{1... | collective-permute-start | bytes 786440 | tf_op jit(solution)/shard_map/ppermute | solution.py:18
  108.5 20.6 %collective-permute-start.14 = (bf16[512,256]{1,0:T(8,128)(2,1)S(1)}, bf16[512,256]{1,0:T(8,128)(2,1)S(1)}, u32[]{:S(2)}, u32[]{:S(2)}) collective-permute-start(bf16[512,256]{1,0:T(8,128)(2,1)S(1)} %get-tuple-element.142), channel_id=1, source_target_pairs={{0,12},{1,13},{2,14},{3,15},{4,0},{5,1},{6,2},{7,3},{8,4},{9,5},{1... | collective-permute-start | bytes 786440 | tf_op jit(solution)/shard_map/ppermute | solution.py:18
  112.3 20.1 %collective-permute-start.15 = (bf16[512,256]{1,0:T(8,128)(2,1)S(1)}, bf16[512,256]{1,0:T(8,128)(2,1)S(1)}, u32[]{:S(2)}, u32[]{:S(2)}) collective-permute-start(bf16[512,256]{1,0:T(8,128)(2,1)S(1)} %get-tuple-element.140), channel_id=1, source_target_pairs={{0,4},{1,5},{2,6},{3,7},{4,8},{5,9},{6,10},{7,11},{8,12},{9,13},{1... | collective-permute-start | bytes 786440 | tf_op jit(solution)/shard_map/ppermute | solution.py:18
  116.8 12.1 %collective-permute-start.11 = (f32[114688]{0:T(1024)S(1)}, f32[114688]{0:T(1024)S(1)}, u32[]{:S(2)}, u32[]{:S(2)}) collective-permute-start(f32[114688]{0:T(1024)S(1)} %dynamic_slice.27), channel_id=1, source_target_pairs={{0,2},{1,3},{2,0},{3,1},{4,6},{5,7},{6,4},{7,5},{8,10},{9,11},{10,... | collective-permute-start | bytes 1376264 | tf_op jit(solution)/shard_map/ppermute | solution.py:24
  134.8 20.6 %collective-permute-start.18 = (bf16[512,256]{1,0:T(8,128)(2,1)}, bf16[512,256]{1,0:T(8,128)(2,1)S(1)}, u32[]{:S(2)}, u32[]{:S(2)}) collective-permute-start(bf16[512,256]{1,0:T(8,128)(2,1)} %slice.162), channel_id=1, source_target_pairs={{0,12},{1,13},{2,14},{3,15},{4,0},{5,1},{6,2},{7,3},{8,4},{9,5},{1... | collective-permute-start | bytes 786440 | tf_op jit(solution)/shard_map/ppermute | solution.py:18
  137.0 18.4 %collective-permute-start.19 = (bf16[512,256]{1,0:T(8,128)(2,1)}, bf16[512,256]{1,0:T(8,128)(2,1)}, u32[]{:S(2)}, u32[]{:S(2)}) collective-permute-start(bf16[512,256]{1,0:T(8,128)(2,1)} %slice.163), channel_id=1, source_target_pairs={{0,4},{1,5},{2,6},{3,7},{4,8},{5,9},{6,10},{7,11},{8,12},{9,13},{1... | collective-permute-start | bytes 786440 | tf_op jit(solution)/shard_map/ppermute | solution.py:18
  141.1 14.3 %collective-permute-start.17 = (f32[28672]{0:T(1024)S(1)}, f32[28672]{0:T(1024)S(1)}, u32[]{:S(2)}, u32[]{:S(2)}) collective-permute-start(f32[28672]{0:T(1024)S(1)} %dynamic_slice.31), channel_id=1, source_target_pairs={{0,8},{1,9},{2,10},{3,11},{4,12},{5,13},{6,14},{7,15},{8,0},{9,1},... | collective-permute-start | bytes 344072 | tf_op jit(solution)/shard_map/ppermute | solution.py:24
  144.2 27.6 %collective-permute-start.21 = (bf16[512,256]{1,0:T(8,128)(2,1)}, bf16[512,256]{1,0:T(8,128)(2,1)S(1)}, u32[]{:S(2)}, u32[]{:S(2)}) collective-permute-start(bf16[512,256]{1,0:T(8,128)(2,1)} %slice.164), channel_id=1, source_target_pairs={{0,12},{1,13},{2,14},{3,15},{4,0},{5,1},{6,2},{7,3},{8,4},{9,5},{1... | collective-permute-start | bytes 786440 | tf_op jit(solution)/shard_map/ppermute | solution.py:18
  147.3 24.5 %collective-permute-start.22 = (bf16[512,256]{1,0:T(8,128)(2,1)}, bf16[512,256]{1,0:T(8,128)(2,1)}, u32[]{:S(2)}, u32[]{:S(2)}) collective-permute-start(bf16[512,256]{1,0:T(8,128)(2,1)} %slice.165), channel_id=1, source_target_pairs={{0,4},{1,5},{2,6},{3,7},{4,8},{5,9},{6,10},{7,11},{8,12},{9,13},{1... | collective-permute-start | bytes 786440 | tf_op jit(solution)/shard_map/ppermute | solution.py:18
  155.4 16.3 %collective-permute-start.20 = (f32[56,512]{1,0:T(8,128)S(1)}, f32[56,512]{1,0:T(8,128)S(1)}, u32[]{:S(2)}, u32[]{:S(2)}) collective-permute-start(f32[56,512]{1,0:T(8,128)S(1)} %reshape.20), channel_id=1, source_target_pairs={{0,8},{1,9},{2,10},{3,11},{4,12},{5,13},{6,14},{7,15},{8,0},{9,1},... | collective-permute-start | bytes 344072 | tf_op jit(solution)/shard_map/ppermute | solution.py:24
  158.4 26.4 %collective-permute-start.24 = (bf16[512,256]{1,0:T(8,128)(2,1)S(1)}, bf16[512,256]{1,0:T(8,128)(2,1)S(1)}, u32[]{:S(2)}, u32[]{:S(2)}) collective-permute-start(bf16[512,256]{1,0:T(8,128)(2,1)S(1)} %slice.166), channel_id=1, source_target_pairs={{0,12},{1,13},{2,14},{3,15},{4,0},{5,1},{6,2},{7,3},{8,4},{9,5},{1... | collective-permute-start | bytes 786440 | tf_op jit(solution)/shard_map/ppermute | solution.py:18
  166.0 18.9 %collective-permute-start.25 = (bf16[512,256]{1,0:T(8,128)(2,1)S(1)}, bf16[512,256]{1,0:T(8,128)(2,1)S(1)}, u32[]{:S(2)}, u32[]{:S(2)}) collective-permute-start(bf16[512,256]{1,0:T(8,128)(2,1)S(1)} %slice.167), channel_id=1, source_target_pairs={{0,4},{1,5},{2,6},{3,7},{4,8},{5,9},{6,10},{7,11},{8,12},{9,13},{1... | collective-permute-start | bytes 786440 | tf_op jit(solution)/shard_map/ppermute | solution.py:18
  171.8 13.0 %collective-permute-start.23 = (f32[112,512]{1,0:T(8,128)S(1)}, f32[112,512]{1,0:T(8,128)S(1)}, u32[]{:S(2)}, u32[]{:S(2)}) collective-permute-start(f32[112,512]{1,0:T(8,128)S(1)} %pad_maximum_fusion.9), channel_id=1, source_target_pairs={{0,4},{1,5},{2,6},{3,7},{4,0},{5,1},{6,2},{7,3},{8,12},{9,13},{10,... | collective-permute-start | bytes 688136 | tf_op jit(solution)/shard_map/ppermute | solution.py:24
  178.2 19.8 %collective-permute-start.27 = (bf16[512,256]{1,0:T(8,128)(2,1)S(1)}, bf16[512,256]{1,0:T(8,128)(2,1)S(1)}, u32[]{:S(2)}, u32[]{:S(2)}) collective-permute-start(bf16[512,256]{1,0:T(8,128)(2,1)S(1)} %slice.168), channel_id=1, source_target_pairs={{0,12},{1,13},{2,14},{3,15},{4,0},{5,1},{6,2},{7,3},{8,4},{9,5},{1... | collective-permute-start | bytes 786440 | tf_op jit(solution)/shard_map/ppermute | solution.py:18
  182.1 20.0 %collective-permute-start.28 = (bf16[512,256]{1,0:T(8,128)(2,1)S(1)}, bf16[512,256]{1,0:T(8,128)(2,1)S(1)}, u32[]{:S(2)}, u32[]{:S(2)}) collective-permute-start(bf16[512,256]{1,0:T(8,128)(2,1)S(1)} %slice.169), channel_id=1, source_target_pairs={{0,4},{1,5},{2,6},{3,7},{4,8},{5,9},{6,10},{7,11},{8,12},{9,13},{1... | collective-permute-start | bytes 786440 | tf_op jit(solution)/shard_map/ppermute | solution.py:18
  184.9 17.0 %collective-permute-start.26 = (f32[224,512]{1,0:T(8,128)S(1)}, f32[224,512]{1,0:T(8,128)S(1)}, u32[]{:S(2)}, u32[]{:S(2)}) collective-permute-start(f32[224,512]{1,0:T(8,128)S(1)} %pad_maximum_fusion.8), channel_id=1, source_target_pairs={{0,2},{1,3},{2,0},{3,1},{4,6},{5,7},{6,4},{7,5},{8,10},{9,11},{10,... | collective-permute-start | bytes 1376264 | tf_op jit(solution)/shard_map/ppermute | solution.py:24
  187.5 17.3 %collective-permute-start.29 = (bf16[512,256]{1,0:T(8,128)(2,1)S(1)}, bf16[512,256]{1,0:T(8,128)(2,1)S(1)}, u32[]{:S(2)}, u32[]{:S(2)}) collective-permute-start(bf16[512,256]{1,0:T(8,128)(2,1)S(1)} %get-tuple-element.126), channel_id=1, source_target_pairs={{0,12},{1,13},{2,14},{3,15},{4,0},{5,1},{6,2},{7,3},{8,4},{9,5},{1... | collective-permute-start | bytes 786440 | tf_op jit(solution)/shard_map/ppermute | solution.py:18
  197.9 11.9 %collective-permute-start.30 = (bf16[512,256]{1,0:T(8,128)(2,1)S(1)}, bf16[512,256]{1,0:T(8,128)(2,1)S(1)}, u32[]{:S(2)}, u32[]{:S(2)}) collective-permute-start(bf16[512,256]{1,0:T(8,128)(2,1)S(1)} %get-tuple-element.124), channel_id=1, source_target_pairs={{0,4},{1,5},{2,6},{3,7},{4,8},{5,9},{6,10},{7,11},{8,12},{9,13},{1... | collective-permute-start | bytes 786440 | tf_op jit(solution)/shard_map/ppermute | solution.py:18
  198.0 15.6 %collective-permute-start.31 = (bf16[512,256]{1,0:T(8,128)(2,1)S(1)}, bf16[512,256]{1,0:T(8,128)(2,1)S(1)}, u32[]{:S(2)}, u32[]{:S(2)}) collective-permute-start(bf16[512,256]{1,0:T(8,128)(2,1)S(1)} %get-tuple-element.125), channel_id=1, source_target_pairs={{0,12},{1,13},{2,14},{3,15},{4,0},{5,1},{6,2},{7,3},{8,4},{9,5},{1... | collective-permute-start | bytes 786440 | tf_op jit(solution)/shard_map/ppermute | solution.py:18
  201.9 15.9 %collective-permute-start.32 = (bf16[512,256]{1,0:T(8,128)(2,1)S(1)}, bf16[512,256]{1,0:T(8,128)(2,1)S(1)}, u32[]{:S(2)}, u32[]{:S(2)}) collective-permute-start(bf16[512,256]{1,0:T(8,128)(2,1)S(1)} %get-tuple-element.123), channel_id=1, source_target_pairs={{0,4},{1,5},{2,6},{3,7},{4,8},{5,9},{6,10},{7,11},{8,12},{9,13},{1... | collective-permute-start | bytes 786440 | tf_op jit(solution)/shard_map/ppermute | solution.py:18
  (16 other events, 286.7 us)

commit v12 on v11

--- a/solution.py
+++ b/solution.py
@@ -160,12 +160,18 @@
     early.extend(item[0] for item in pending)
     if sent_rows < positions:
         late.append(send_rows((lower_all, upper_all), sent_rows, positions))
-    received = early + late
-    received_ahead = jnp.concatenate([pair[0] for pair in received], axis=0)
-    received_behind = jnp.concatenate([pair[1] for pair in received], axis=0)
-    total_sum = cotangent.astype(jnp.float32) + jnp.concatenate(mids, axis=0)
-    total_sum = total_sum + received_ahead.astype(jnp.float32) + received_behind.astype(jnp.float32)
-    grad_input = total_sum.astype(jnp.bfloat16)
+    mids_all = jnp.concatenate(mids, axis=0)
+
+    def finish(pieces, start):
+        ahead = jnp.concatenate([pair[0] for pair in pieces], axis=0)
+        behind = jnp.concatenate([pair[1] for pair in pieces], axis=0)
+        stop = start + ahead.shape[0]
+        total_sum = cotangent[start:stop].astype(jnp.float32) + mids_all[start:stop]
+        total_sum = total_sum + ahead.astype(jnp.float32) + behind.astype(jnp.float32)
+        return total_sum.astype(jnp.bfloat16)
+
+    head = finish(early, 0)
+    grad_input = jnp.concatenate([head, finish(late, head.shape[0])], axis=0) if late else head
     split = wconv_total.shape[0]
     grad_conv = buf[:split]
     grad_out = buf[split:].reshape(wout_total.shape)

time: 223 us -> 225 us (level)
  matrix products: 33.5 us -> 40.5 us
  waiting for transfers between devices: 62.6 us -> 57.4 us
  starting transfers between devices: 99.4 us -> 96.6 us
    dot_general x5, matrix products: 2.16 us -> 5.93 us  [chunk_layer(): lax.dot_general(grad_pre, w_mid, last_dims, preferred_element_type=jnp.fl...]
    ppermute x8, waiting for transfers between devices: 25.8 us -> 22.6 us  [exchange(): return lax.ppermute(value, axis, pairs)]
    ppermute x26, starting transfers between devices: 85.3 us -> 82.5 us  [from_behind(): return lax.ppermute(value, axis, pairs)]
    unnamed x44, local copies, waits for them, and re-layouts: 5.04 us -> 7.88 us
  transfers between devices with their start and end apart: 34 -> 34, of which waited for: 14 -> 15; matrix products, arithmetic and copies ran while one was open for 22% -> 24% of each run, Pallas kernels for 0% -> 0%
where the time goes in v12:
time: 225 us; the launch traced here: 224 us
  starting transfers between devices  96.6 us (43%)
  waiting for transfers between devices  57.4 us (26%)
  matrix products  40.5 us (18%)
  local copies, waits for them, and re-layouts  21.7 us (10%)
  other arithmetic  6.31 us (3%)
    ppermute x26, starting transfers between devices, from_behind(): return lax.ppermute(value, axis, pairs)  82.5 us
    ppermute x26, waiting for transfers between devices, from_behind(): return lax.ppermute(value, axis, pairs)  34.8 us
    ppermute x8, waiting for transfers between devices, exchange(): return lax.ppermute(value, axis, pairs)  22.6 us
    ppermute x8, starting transfers between devices, exchange(): return lax.ppermute(value, axis, pairs)  14.1 us
    unnamed x44, local copies, waits for them, and re-layouts  7.88 us
    dot_general x5, matrix products, chunk_layer(): lax.dot_general(grad_pre, w_mid, last_dims, preferred_element_type=jnp.fl...  5.93 us
    dot_general x5, matrix products, chunk_layer(): preact = preact + jnp.dot(middle, w_mid, preferred_element_type=jnp.float32)  5.75 us
    dot_general x5, matrix products, chunk_layer(): lax.dot_general(left_tap_input, grad_pre, first_dims, preferred_element_t...  5.3 us
  transfers between devices with their start and end apart: 34, of which 15 were waited for; matrix products, arithmetic and copies ran while one was open for 24% of the time, Pallas kernels for 0%

profile of v12, /device:TPU:0, one launch (start us, length us, event | category | flops | bytes accessed | tf_op | source)
XLA Modules:
  0.0 224.3 jit_solution(3216735910111436231)
XLA Ops:
  0.7 2.7 %fusion.129 = (bf16[1024,256]{1,0:T(8,128)(2,1)}, bf16[1024,256]{1,0:T(8,128)(2,1)}, bf16[1024,256]{1,0:T(8,128)(2,1)}) fusion(bf16[4096,256]{1,0:T(8,128)(2,1)} %param.4), kind=kLoop, calls=%fused_computation.212 | loop fusion | bytes 3145728 | tf_op jit(solution)/shard_map/slice | solution.py:95
  3.4 3.0 %collective-permute-start = (bf16[1024,256]{1,0:T(8,128)(2,1)}, bf16[1024,256]{1,0:T(8,128)(2,1)}, u32[]{:S(2)}, u32[]{:S(2)}) collective-permute-start(bf16[1024,256]{1,0:T(8,128)(2,1)} %get-tuple-element.129), channel_id=1, source_target_pairs={{0,4},{1,5},{2,6},{3,7},{4,8},{5,9},{6,10},{7,11},{8,12},{9,13},{1... | collective-permute-start | bytes 1572872 | tf_op jit(solution)/shard_map/ppermute | solution.py:18
  6.4 2.0 collective-permute-start.1
  8.4 3.8 %collective-permute-start.3 = (bf16[1024,256]{1,0:T(8,128)(2,1)}, bf16[1024,256]{1,0:T(8,128)(2,1)S(1)}, u32[]{:S(2)}, u32[]{:S(2)}) collective-permute-start(bf16[1024,256]{1,0:T(8,128)(2,1)} %get-tuple-element.127), channel_id=1, source_target_pairs={{0,12},{1,13},{2,14},{3,15},{4,0},{5,1},{6,2},{7,3},{8,4},{9,5},{1... | collective-permute-start | bytes 1572872 | tf_op jit(solution)/shard_map/ppermute | solution.py:18
  12.2 1.8 fusion.88
  14.1 1.8 fusion.84
  19.0 2.5 %collective-permute-done = bf16[1024,256]{1,0:T(8,128)(2,1)} collective-permute-done((bf16[1024,256]{1,0:T(8,128)(2,1)}, bf16[1024,256]{1,0:T(8,128)(2,1)}, u32[]{:S(2)}, u32[]{:S(2)}) %collective-permute-start) | collective-permute-done | bytes 524320 | tf_op jit(solution)/shard_map/ppermute | solution.py:18
  21.5 13.2 %collective-permute-start.5 = (bf16[1024,256]{1,0:T(8,128)(2,1)}, bf16[1024,256]{1,0:T(8,128)(2,1)S(1)}, u32[]{:S(2)}, u32[]{:S(2)}) collective-permute-start(bf16[1024,256]{1,0:T(8,128)(2,1)} %get-tuple-element.128), channel_id=1, source_target_pairs={{0,12},{1,13},{2,14},{3,15},{4,0},{5,1},{6,2},{7,3},{8,4},{9,5},{1... | collective-permute-start | bytes 1572872 | tf_op jit(solution)/shard_map/ppermute | solution.py:18
  44.0 13.2 %collective-permute-start.9 = (bf16[512,256]{1,0:T(8,128)(2,1)S(1)}, bf16[512,256]{1,0:T(8,128)(2,1)S(1)}, u32[]{:S(2)}, u32[]{:S(2)}) collective-permute-start(bf16[512,256]{1,0:T(8,128)(2,1)S(1)} %get-tuple-element.130), channel_id=1, source_target_pairs={{0,12},{1,13},{2,14},{3,15},{4,0},{5,1},{6,2},{7,3},{8,4},{9,5},{1... | collective-permute-start | bytes 786440 | tf_op jit(solution)/shard_map/ppermute | solution.py:18
  63.5 3.0 %collective-permute-done.4 = bf16[1024,256]{1,0:T(8,128)(2,1)} collective-permute-done((bf16[1024,256]{1,0:T(8,128)(2,1)}, bf16[1024,256]{1,0:T(8,128)(2,1)}, u32[]{:S(2)}, u32[]{:S(2)}) %collective-permute-start.4) | collective-permute-done | bytes 524320 | tf_op jit(solution)/shard_map/ppermute | solution.py:18
  66.5 13.2 %collective-permute-start.7 = (bf16[512,256]{1,0:T(8,128)(2,1)S(1)}, bf16[512,256]{1,0:T(8,128)(2,1)S(1)}, u32[]{:S(2)}, u32[]{:S(2)}) collective-permute-start(bf16[512,256]{1,0:T(8,128)(2,1)S(1)} %get-tuple-element.131), channel_id=1, source_target_pairs={{0,12},{1,13},{2,14},{3,15},{4,0},{5,1},{6,2},{7,3},{8,4},{9,5},{1... | collective-permute-start | bytes 786440 | tf_op jit(solution)/shard_map/ppermute | solution.py:18
  86.4 2.5 %collective-permute-done.9 = bf16[512,256]{1,0:T(8,128)(2,1)S(1)} collective-permute-done((bf16[512,256]{1,0:T(8,128)(2,1)S(1)}, bf16[512,256]{1,0:T(8,128)(2,1)S(1)}, u32[]{:S(2)}, u32[]{:S(2)}) %collective-permute-start.9) | collective-permute-done | bytes 262176 | tf_op jit(solution)/shard_map/ppermute | solution.py:18
  91.9 2.7 %collective-permute-done.6 = bf16[512,256]{1,0:T(8,128)(2,1)S(1)} collective-permute-done((bf16[512,256]{1,0:T(8,128)(2,1)S(1)}, bf16[512,256]{1,0:T(8,128)(2,1)S(1)}, u32[]{:S(2)}, u32[]{:S(2)}) %collective-permute-start.6) | collective-permute-done | bytes 262176 | tf_op jit(solution)/shard_map/ppermute | solution.py:18
  94.6 4.0 %collective-permute-done.7 = bf16[512,256]{1,0:T(8,128)(2,1)S(1)} collective-permute-done((bf16[512,256]{1,0:T(8,128)(2,1)S(1)}, bf16[512,256]{1,0:T(8,128)(2,1)S(1)}, u32[]{:S(2)}, u32[]{:S(2)}) %collective-permute-start.7) | collective-permute-done | bytes 262176 | tf_op jit(solution)/shard_map/ppermute | solution.py:18
  107.2 2.4 %collective-permute-start.12 = (bf16[512,256]{1,0:T(8,128)(2,1)S(1)}, bf16[512,256]{1,0:T(8,128)(2,1)S(1)}, u32[]{:S(2)}, u32[]{:S(2)}) collective-permute-start(bf16[512,256]{1,0:T(8,128)(2,1)S(1)} %get-tuple-element.143), channel_id=1, source_target_pairs={{0,12},{1,13},{2,14},{3,15},{4,0},{5,1},{6,2},{7,3},{8,4},{9,5},{1... | collective-permute-start | bytes 786440 | tf_op jit(solution)/shard_map/ppermute | solution.py:18
  109.7 3.8 %collective-permute-start.14 = (bf16[512,256]{1,0:T(8,128)(2,1)S(1)}, bf16[512,256]{1,0:T(8,128)(2,1)S(1)}, u32[]{:S(2)}, u32[]{:S(2)}) collective-permute-start(bf16[512,256]{1,0:T(8,128)(2,1)S(1)} %get-tuple-element.142), channel_id=1, source_target_pairs={{0,12},{1,13},{2,14},{3,15},{4,0},{5,1},{6,2},{7,3},{8,4},{9,5},{1... | collective-permute-start | bytes 786440 | tf_op jit(solution)/shard_map/ppermute | solution.py:18
  120.7 8.6 %collective-permute-done.11 = f32[114688]{0:T(1024)S(1)} collective-permute-done((f32[114688]{0:T(1024)S(1)}, f32[114688]{0:T(1024)S(1)}, u32[]{:S(2)}, u32[]{:S(2)}) %collective-permute-start.11) | collective-permute-done | bytes 458784 | tf_op jit(solution)/shard_map/ppermute | solution.py:24
  129.4 4.3 %collective-permute-done.15 = bf16[512,256]{1,0:T(8,128)(2,1)S(1)} collective-permute-done((bf16[512,256]{1,0:T(8,128)(2,1)S(1)}, bf16[512,256]{1,0:T(8,128)(2,1)S(1)}, u32[]{:S(2)}, u32[]{:S(2)}) %collective-permute-start.15) | collective-permute-done | bytes 262176 | tf_op jit(solution)/shard_map/ppermute | solution.py:18
  138.9 3.4 %collective-permute-done.16 = f32[57344]{0:T(1024)S(1)} collective-permute-done((f32[57344]{0:T(1024)S(1)}, f32[57344]{0:T(1024)S(1)}, u32[]{:S(2)}, u32[]{:S(2)}) %collective-permute-start.16) | collective-permute-done | bytes 229408 | tf_op jit(solution)/shard_map/ppermute | solution.py:24
  145.9 2.3 %collective-permute-start.21 = (bf16[512,256]{1,0:T(8,128)(2,1)}, bf16[512,256]{1,0:T(8,128)(2,1)}, u32[]{:S(2)}, u32[]{:S(2)}) collective-permute-start(bf16[512,256]{1,0:T(8,128)(2,1)} %slice.175), channel_id=1, source_target_pairs={{0,12},{1,13},{2,14},{3,15},{4,0},{5,1},{6,2},{7,3},{8,4},{9,5},{1... | collective-permute-start | bytes 786440 | tf_op jit(solution)/shard_map/ppermute | solution.py:18
  149.0 7.6 %collective-permute-done.17 = f32[28672]{0:T(1024)S(1)} collective-permute-done((f32[28672]{0:T(1024)S(1)}, f32[28672]{0:T(1024)S(1)}, u32[]{:S(2)}, u32[]{:S(2)}) %collective-permute-start.17) | collective-permute-done | bytes 114720 | tf_op jit(solution)/shard_map/ppermute | solution.py:24
  156.6 2.1 collective-permute-start.20
  159.7 6.6 %collective-permute-start.24 = (bf16[512,256]{1,0:T(8,128)(2,1)S(1)}, bf16[512,256]{1,0:T(8,128)(2,1)S(1)}, u32[]{:S(2)}, u32[]{:S(2)}) collective-permute-start(bf16[512,256]{1,0:T(8,128)(2,1)S(1)} %slice.177), channel_id=1, source_target_pairs={{0,12},{1,13},{2,14},{3,15},{4,0},{5,1},{6,2},{7,3},{8,4},{9,5},{1... | collective-permute-start | bytes 786440 | tf_op jit(solution)/shard_map/ppermute | solution.py:18
  170.6 2.4 %collective-permute-done.20 = f32[56,512]{1,0:T(8,128)S(1)} collective-permute-done((f32[56,512]{1,0:T(8,128)S(1)}, f32[56,512]{1,0:T(8,128)S(1)}, u32[]{:S(2)}, u32[]{:S(2)}) %collective-permute-start.20) | collective-permute-done | bytes 114720 | tf_op jit(solution)/shard_map/ppermute | solution.py:24
  173.0 5.5 %collective-permute-start.23 = (f32[112,512]{1,0:T(8,128)S(1)}, f32[112,512]{1,0:T(8,128)S(1)}, u32[]{:S(2)}, u32[]{:S(2)}) collective-permute-start(f32[112,512]{1,0:T(8,128)S(1)} %pad_maximum_fusion.10), channel_id=1, source_target_pairs={{0,4},{1,5},{2,6},{3,7},{4,0},{5,1},{6,2},{7,3},{8,12},{9,13},{10,... | collective-permute-start | bytes 688136 | tf_op jit(solution)/shard_map/ppermute | solution.py:24
  179.5 2.9 %collective-permute-start.27 = (bf16[512,256]{1,0:T(8,128)(2,1)S(1)}, bf16[512,256]{1,0:T(8,128)(2,1)S(1)}, u32[]{:S(2)}, u32[]{:S(2)}) collective-permute-start(bf16[512,256]{1,0:T(8,128)(2,1)S(1)} %slice.179), channel_id=1, source_target_pairs={{0,12},{1,13},{2,14},{3,15},{4,0},{5,1},{6,2},{7,3},{8,4},{9,5},{1... | collective-permute-start | bytes 786440 | tf_op jit(solution)/shard_map/ppermute | solution.py:18
  188.7 9.3 %collective-permute-start.29 = (bf16[512,256]{1,0:T(8,128)(2,1)S(1)}, bf16[512,256]{1,0:T(8,128)(2,1)S(1)}, u32[]{:S(2)}, u32[]{:S(2)}) collective-permute-start(bf16[512,256]{1,0:T(8,128)(2,1)S(1)} %get-tuple-element.126), channel_id=1, source_target_pairs={{0,12},{1,13},{2,14},{3,15},{4,0},{5,1},{6,2},{7,3},{8,4},{9,5},{1... | collective-permute-start | bytes 786440 | tf_op jit(solution)/shard_map/ppermute | solution.py:18
  199.2 3.9 %collective-permute-start.31 = (bf16[512,256]{1,0:T(8,128)(2,1)S(1)}, bf16[512,256]{1,0:T(8,128)(2,1)S(1)}, u32[]{:S(2)}, u32[]{:S(2)}) collective-permute-start(bf16[512,256]{1,0:T(8,128)(2,1)S(1)} %get-tuple-element.125), channel_id=1, source_target_pairs={{0,12},{1,13},{2,14},{3,15},{4,0},{5,1},{6,2},{7,3},{8,4},{9,5},{1... | collective-permute-start | bytes 786440 | tf_op jit(solution)/shard_map/ppermute | solution.py:18
  203.3 2.8 %collective-permute-done.29 = bf16[512,256]{1,0:T(8,128)(2,1)S(1)} collective-permute-done((bf16[512,256]{1,0:T(8,128)(2,1)S(1)}, bf16[512,256]{1,0:T(8,128)(2,1)S(1)}, u32[]{:S(2)}, u32[]{:S(2)}) %collective-permute-start.29) | collective-permute-done | bytes 262176 | tf_op jit(solution)/shard_map/ppermute | solution.py:18
  206.1 4.9 %collective-permute-done.30 = bf16[512,256]{1,0:T(8,128)(2,1)S(1)} collective-permute-done((bf16[512,256]{1,0:T(8,128)(2,1)S(1)}, bf16[512,256]{1,0:T(8,128)(2,1)S(1)}, u32[]{:S(2)}, u32[]{:S(2)}) %collective-permute-start.30) | collective-permute-done | bytes 262176 | tf_op jit(solution)/shard_map/ppermute | solution.py:18
  211.0 3.8 %collective-permute-done.31 = bf16[512,256]{1,0:T(8,128)(2,1)S(1)} collective-permute-done((bf16[512,256]{1,0:T(8,128)(2,1)S(1)}, bf16[512,256]{1,0:T(8,128)(2,1)S(1)}, u32[]{:S(2)}, u32[]{:S(2)}) %collective-permute-start.31) | collective-permute-done | bytes 262176 | tf_op jit(solution)/shard_map/ppermute | solution.py:18
  214.8 4.2 %collective-permute-done.32 = bf16[512,256]{1,0:T(8,128)(2,1)S(1)} collective-permute-done((bf16[512,256]{1,0:T(8,128)(2,1)S(1)}, bf16[512,256]{1,0:T(8,128)(2,1)S(1)}, u32[]{:S(2)}, u32[]{:S(2)}) %collective-permute-start.32) | collective-permute-done | bytes 262176 | tf_op jit(solution)/shard_map/ppermute | solution.py:18
  (182 shorter events, 72.4 us)
Async XLA Ops:
  3.4 18.2 %collective-permute-start = (bf16[1024,256]{1,0:T(8,128)(2,1)}, bf16[1024,256]{1,0:T(8,128)(2,1)}, u32[]{:S(2)}, u32[]{:S(2)}) collective-permute-start(bf16[1024,256]{1,0:T(8,128)(2,1)} %get-tuple-element.129), channel_id=1, source_target_pairs={{0,4},{1,5},{2,6},{3,7},{4,8},{5,9},{6,10},{7,11},{8,12},{9,13},{1... | collective-permute-start | bytes 1572872 | tf_op jit(solution)/shard_map/ppermute | solution.py:18
  6.4 29.9 %collective-permute-start.1 = (bf16[1024,256]{1,0:T(8,128)(2,1)}, bf16[1024,256]{1,0:T(8,128)(2,1)}, u32[]{:S(2)}, u32[]{:S(2)}) collective-permute-start(bf16[1024,256]{1,0:T(8,128)(2,1)} %get-tuple-element.129), channel_id=1, source_target_pairs={{0,12},{1,13},{2,14},{3,15},{4,0},{5,1},{6,2},{7,3},{8,4},{9,5},{1... | collective-permute-start | bytes 1572872 | tf_op jit(solution)/shard_map/ppermute | solution.py:18
  8.4 35.6 %collective-permute-start.2 = (bf16[1024,256]{1,0:T(8,128)(2,1)}, bf16[1024,256]{1,0:T(8,128)(2,1)}, u32[]{:S(2)}, u32[]{:S(2)}) collective-permute-start(bf16[1024,256]{1,0:T(8,128)(2,1)} %get-tuple-element.127), channel_id=1, source_target_pairs={{0,4},{1,5},{2,6},{3,7},{4,8},{5,9},{6,10},{7,11},{8,12},{9,13},{1... | collective-permute-start | bytes 1572872 | tf_op jit(solution)/shard_map/ppermute | solution.py:18
  8.4 48.8 %collective-permute-start.3 = (bf16[1024,256]{1,0:T(8,128)(2,1)}, bf16[1024,256]{1,0:T(8,128)(2,1)S(1)}, u32[]{:S(2)}, u32[]{:S(2)}) collective-permute-start(bf16[1024,256]{1,0:T(8,128)(2,1)} %get-tuple-element.127), channel_id=1, source_target_pairs={{0,12},{1,13},{2,14},{3,15},{4,0},{5,1},{6,2},{7,3},{8,4},{9,5},{1... | collective-permute-start | bytes 1572872 | tf_op jit(solution)/shard_map/ppermute | solution.py:18
  12.2 54.3 %collective-permute-start.4 = (bf16[1024,256]{1,0:T(8,128)(2,1)}, bf16[1024,256]{1,0:T(8,128)(2,1)}, u32[]{:S(2)}, u32[]{:S(2)}) collective-permute-start(bf16[1024,256]{1,0:T(8,128)(2,1)} %get-tuple-element.128), channel_id=1, source_target_pairs={{0,4},{1,5},{2,6},{3,7},{4,8},{5,9},{6,10},{7,11},{8,12},{9,13},{1... | collective-permute-start | bytes 1572872 | tf_op jit(solution)/shard_map/ppermute | solution.py:18
  21.5 58.2 %collective-permute-start.5 = (bf16[1024,256]{1,0:T(8,128)(2,1)}, bf16[1024,256]{1,0:T(8,128)(2,1)S(1)}, u32[]{:S(2)}, u32[]{:S(2)}) collective-permute-start(bf16[1024,256]{1,0:T(8,128)(2,1)} %get-tuple-element.128), channel_id=1, source_target_pairs={{0,12},{1,13},{2,14},{3,15},{4,0},{5,1},{6,2},{7,3},{8,4},{9,5},{1... | collective-permute-start | bytes 1572872 | tf_op jit(solution)/shard_map/ppermute | solution.py:18
  36.3 50.1 %collective-permute-start.8 = (bf16[512,256]{1,0:T(8,128)(2,1)S(1)}, bf16[512,256]{1,0:T(8,128)(2,1)S(1)}, u32[]{:S(2)}, u32[]{:S(2)}) collective-permute-start(bf16[512,256]{1,0:T(8,128)(2,1)S(1)} %get-tuple-element.130), channel_id=1, source_target_pairs={{0,4},{1,5},{2,6},{3,7},{4,8},{5,9},{6,10},{7,11},{8,12},{9,13},{1... | collective-permute-start | bytes 786440 | tf_op jit(solution)/shard_map/ppermute | solution.py:18
  44.0 44.9 %collective-permute-start.9 = (bf16[512,256]{1,0:T(8,128)(2,1)S(1)}, bf16[512,256]{1,0:T(8,128)(2,1)S(1)}, u32[]{:S(2)}, u32[]{:S(2)}) collective-permute-start(bf16[512,256]{1,0:T(8,128)(2,1)S(1)} %get-tuple-element.130), channel_id=1, source_target_pairs={{0,12},{1,13},{2,14},{3,15},{4,0},{5,1},{6,2},{7,3},{8,4},{9,5},{1... | collective-permute-start | bytes 786440 | tf_op jit(solution)/shard_map/ppermute | solution.py:18
  57.2 37.4 %collective-permute-start.6 = (bf16[512,256]{1,0:T(8,128)(2,1)S(1)}, bf16[512,256]{1,0:T(8,128)(2,1)S(1)}, u32[]{:S(2)}, u32[]{:S(2)}) collective-permute-start(bf16[512,256]{1,0:T(8,128)(2,1)S(1)} %get-tuple-element.131), channel_id=1, source_target_pairs={{0,4},{1,5},{2,6},{3,7},{4,8},{5,9},{6,10},{7,11},{8,12},{9,13},{1... | collective-permute-start | bytes 786440 | tf_op jit(solution)/shard_map/ppermute | solution.py:18
  66.5 32.1 %collective-permute-start.7 = (bf16[512,256]{1,0:T(8,128)(2,1)S(1)}, bf16[512,256]{1,0:T(8,128)(2,1)S(1)}, u32[]{:S(2)}, u32[]{:S(2)}) collective-permute-start(bf16[512,256]{1,0:T(8,128)(2,1)S(1)} %get-tuple-element.131), channel_id=1, source_target_pairs={{0,12},{1,13},{2,14},{3,15},{4,0},{5,1},{6,2},{7,3},{8,4},{9,5},{1... | collective-permute-start | bytes 786440 | tf_op jit(solution)/shard_map/ppermute | solution.py:18
  107.1 9.9 %collective-permute-start.10 = (f32[229376]{0:T(1024)S(1)}, f32[229376]{0:T(1024)S(1)}, u32[]{:S(2)}, u32[]{:S(2)}) collective-permute-start(f32[229376]{0:T(1024)S(1)} %dynamic_slice.25), channel_id=1, source_target_pairs={{0,1},{1,0},{2,3},{3,2},{4,5},{5,4},{6,7},{7,6},{8,9},{9,8},{10,11... | collective-permute-start | bytes 2752520 | tf_op jit(solution)/shard_map/ppermute | solution.py:24
  107.2 22.1 %collective-permute-start.12 = (bf16[512,256]{1,0:T(8,128)(2,1)S(1)}, bf16[512,256]{1,0:T(8,128)(2,1)S(1)}, u32[]{:S(2)}, u32[]{:S(2)}) collective-permute-start(bf16[512,256]{1,0:T(8,128)(2,1)S(1)} %get-tuple-element.143), channel_id=1, source_target_pairs={{0,12},{1,13},{2,14},{3,15},{4,0},{5,1},{6,2},{7,3},{8,4},{9,5},{1... | collective-permute-start | bytes 786440 | tf_op jit(solution)/shard_map/ppermute | solution.py:18
  109.6 19.7 %collective-permute-start.13 = (bf16[512,256]{1,0:T(8,128)(2,1)S(1)}, bf16[512,256]{1,0:T(8,128)(2,1)S(1)}, u32[]{:S(2)}, u32[]{:S(2)}) collective-permute-start(bf16[512,256]{1,0:T(8,128)(2,1)S(1)} %get-tuple-element.141), channel_id=1, source_target_pairs={{0,4},{1,5},{2,6},{3,7},{4,8},{5,9},{6,10},{7,11},{8,12},{9,13},{1... | collective-permute-start | bytes 786440 | tf_op jit(solution)/shard_map/ppermute | solution.py:18
  109.7 19.7 %collective-permute-start.14 = (bf16[512,256]{1,0:T(8,128)(2,1)S(1)}, bf16[512,256]{1,0:T(8,128)(2,1)S(1)}, u32[]{:S(2)}, u32[]{:S(2)}) collective-permute-start(bf16[512,256]{1,0:T(8,128)(2,1)S(1)} %get-tuple-element.142), channel_id=1, source_target_pairs={{0,12},{1,13},{2,14},{3,15},{4,0},{5,1},{6,2},{7,3},{8,4},{9,5},{1... | collective-permute-start | bytes 786440 | tf_op jit(solution)/shard_map/ppermute | solution.py:18
  113.5 20.2 %collective-permute-start.15 = (bf16[512,256]{1,0:T(8,128)(2,1)S(1)}, bf16[512,256]{1,0:T(8,128)(2,1)S(1)}, u32[]{:S(2)}, u32[]{:S(2)}) collective-permute-start(bf16[512,256]{1,0:T(8,128)(2,1)S(1)} %get-tuple-element.140), channel_id=1, source_target_pairs={{0,4},{1,5},{2,6},{3,7},{4,8},{5,9},{6,10},{7,11},{8,12},{9,13},{1... | collective-permute-start | bytes 786440 | tf_op jit(solution)/shard_map/ppermute | solution.py:18
  117.1 12.1 %collective-permute-start.11 = (f32[114688]{0:T(1024)S(1)}, f32[114688]{0:T(1024)S(1)}, u32[]{:S(2)}, u32[]{:S(2)}) collective-permute-start(f32[114688]{0:T(1024)S(1)} %dynamic_slice.27), channel_id=1, source_target_pairs={{0,2},{1,3},{2,0},{3,1},{4,6},{5,7},{6,4},{7,5},{8,10},{9,11},{10,... | collective-permute-start | bytes 1376264 | tf_op jit(solution)/shard_map/ppermute | solution.py:24
  136.1 20.5 %collective-permute-start.18 = (bf16[512,256]{1,0:T(8,128)(2,1)}, bf16[512,256]{1,0:T(8,128)(2,1)}, u32[]{:S(2)}, u32[]{:S(2)}) collective-permute-start(bf16[512,256]{1,0:T(8,128)(2,1)} %slice.173), channel_id=1, source_target_pairs={{0,12},{1,13},{2,14},{3,15},{4,0},{5,1},{6,2},{7,3},{8,4},{9,5},{1... | collective-permute-start | bytes 786440 | tf_op jit(solution)/shard_map/ppermute | solution.py:18
  138.2 18.3 %collective-permute-start.19 = (bf16[512,256]{1,0:T(8,128)(2,1)}, bf16[512,256]{1,0:T(8,128)(2,1)}, u32[]{:S(2)}, u32[]{:S(2)}) collective-permute-start(bf16[512,256]{1,0:T(8,128)(2,1)} %slice.174), channel_id=1, source_target_pairs={{0,4},{1,5},{2,6},{3,7},{4,8},{5,9},{6,10},{7,11},{8,12},{9,13},{1... | collective-permute-start | bytes 786440 | tf_op jit(solution)/shard_map/ppermute | solution.py:18
  142.3 14.2 %collective-permute-start.17 = (f32[28672]{0:T(1024)S(1)}, f32[28672]{0:T(1024)S(1)}, u32[]{:S(2)}, u32[]{:S(2)}) collective-permute-start(f32[28672]{0:T(1024)S(1)} %dynamic_slice.31), channel_id=1, source_target_pairs={{0,8},{1,9},{2,10},{3,11},{4,12},{5,13},{6,14},{7,15},{8,0},{9,1},... | collective-permute-start | bytes 344072 | tf_op jit(solution)/shard_map/ppermute | solution.py:24
  145.9 27.1 %collective-permute-start.21 = (bf16[512,256]{1,0:T(8,128)(2,1)}, bf16[512,256]{1,0:T(8,128)(2,1)}, u32[]{:S(2)}, u32[]{:S(2)}) collective-permute-start(bf16[512,256]{1,0:T(8,128)(2,1)} %slice.175), channel_id=1, source_target_pairs={{0,12},{1,13},{2,14},{3,15},{4,0},{5,1},{6,2},{7,3},{8,4},{9,5},{1... | collective-permute-start | bytes 786440 | tf_op jit(solution)/shard_map/ppermute | solution.py:18
  148.9 24.0 %collective-permute-start.22 = (bf16[512,256]{1,0:T(8,128)(2,1)}, bf16[512,256]{1,0:T(8,128)(2,1)}, u32[]{:S(2)}, u32[]{:S(2)}) collective-permute-start(bf16[512,256]{1,0:T(8,128)(2,1)} %slice.176), channel_id=1, source_target_pairs={{0,4},{1,5},{2,6},{3,7},{4,8},{5,9},{6,10},{7,11},{8,12},{9,13},{1... | collective-permute-start | bytes 786440 | tf_op jit(solution)/shard_map/ppermute | solution.py:18
  156.6 16.3 %collective-permute-start.20 = (f32[56,512]{1,0:T(8,128)S(1)}, f32[56,512]{1,0:T(8,128)S(1)}, u32[]{:S(2)}, u32[]{:S(2)}) collective-permute-start(f32[56,512]{1,0:T(8,128)S(1)} %reshape.20), channel_id=1, source_target_pairs={{0,8},{1,9},{2,10},{3,11},{4,12},{5,13},{6,14},{7,15},{8,0},{9,1},... | collective-permute-start | bytes 344072 | tf_op jit(solution)/shard_map/ppermute | solution.py:24
  159.7 26.5 %collective-permute-start.24 = (bf16[512,256]{1,0:T(8,128)(2,1)S(1)}, bf16[512,256]{1,0:T(8,128)(2,1)S(1)}, u32[]{:S(2)}, u32[]{:S(2)}) collective-permute-start(bf16[512,256]{1,0:T(8,128)(2,1)S(1)} %slice.177), channel_id=1, source_target_pairs={{0,12},{1,13},{2,14},{3,15},{4,0},{5,1},{6,2},{7,3},{8,4},{9,5},{1... | collective-permute-start | bytes 786440 | tf_op jit(solution)/shard_map/ppermute | solution.py:18
  167.2 18.9 %collective-permute-start.25 = (bf16[512,256]{1,0:T(8,128)(2,1)S(1)}, bf16[512,256]{1,0:T(8,128)(2,1)S(1)}, u32[]{:S(2)}, u32[]{:S(2)}) collective-permute-start(bf16[512,256]{1,0:T(8,128)(2,1)S(1)} %slice.178), channel_id=1, source_target_pairs={{0,4},{1,5},{2,6},{3,7},{4,8},{5,9},{6,10},{7,11},{8,12},{9,13},{1... | collective-permute-start | bytes 786440 | tf_op jit(solution)/shard_map/ppermute | solution.py:18
  173.0 13.0 %collective-permute-start.23 = (f32[112,512]{1,0:T(8,128)S(1)}, f32[112,512]{1,0:T(8,128)S(1)}, u32[]{:S(2)}, u32[]{:S(2)}) collective-permute-start(f32[112,512]{1,0:T(8,128)S(1)} %pad_maximum_fusion.10), channel_id=1, source_target_pairs={{0,4},{1,5},{2,6},{3,7},{4,0},{5,1},{6,2},{7,3},{8,12},{9,13},{10,... | collective-permute-start | bytes 688136 | tf_op jit(solution)/shard_map/ppermute | solution.py:24
  179.5 19.7 %collective-permute-start.27 = (bf16[512,256]{1,0:T(8,128)(2,1)S(1)}, bf16[512,256]{1,0:T(8,128)(2,1)S(1)}, u32[]{:S(2)}, u32[]{:S(2)}) collective-permute-start(bf16[512,256]{1,0:T(8,128)(2,1)S(1)} %slice.179), channel_id=1, source_target_pairs={{0,12},{1,13},{2,14},{3,15},{4,0},{5,1},{6,2},{7,3},{8,4},{9,5},{1... | collective-permute-start | bytes 786440 | tf_op jit(solution)/shard_map/ppermute | solution.py:18
  183.3 20.0 %collective-permute-start.28 = (bf16[512,256]{1,0:T(8,128)(2,1)S(1)}, bf16[512,256]{1,0:T(8,128)(2,1)S(1)}, u32[]{:S(2)}, u32[]{:S(2)}) collective-permute-start(bf16[512,256]{1,0:T(8,128)(2,1)S(1)} %slice.180), channel_id=1, source_target_pairs={{0,4},{1,5},{2,6},{3,7},{4,8},{5,9},{6,10},{7,11},{8,12},{9,13},{1... | collective-permute-start | bytes 786440 | tf_op jit(solution)/shard_map/ppermute | solution.py:18
  186.1 17.0 %collective-permute-start.26 = (f32[224,512]{1,0:T(8,128)S(1)}, f32[224,512]{1,0:T(8,128)S(1)}, u32[]{:S(2)}, u32[]{:S(2)}) collective-permute-start(f32[224,512]{1,0:T(8,128)S(1)} %pad_maximum_fusion.9), channel_id=1, source_target_pairs={{0,2},{1,3},{2,0},{3,1},{4,6},{5,7},{6,4},{7,5},{8,10},{9,11},{10,... | collective-permute-start | bytes 1376264 | tf_op jit(solution)/shard_map/ppermute | solution.py:24
  188.7 17.4 %collective-permute-start.29 = (bf16[512,256]{1,0:T(8,128)(2,1)S(1)}, bf16[512,256]{1,0:T(8,128)(2,1)S(1)}, u32[]{:S(2)}, u32[]{:S(2)}) collective-permute-start(bf16[512,256]{1,0:T(8,128)(2,1)S(1)} %get-tuple-element.126), channel_id=1, source_target_pairs={{0,12},{1,13},{2,14},{3,15},{4,0},{5,1},{6,2},{7,3},{8,4},{9,5},{1... | collective-permute-start | bytes 786440 | tf_op jit(solution)/shard_map/ppermute | solution.py:18
  199.1 11.9 %collective-permute-start.30 = (bf16[512,256]{1,0:T(8,128)(2,1)S(1)}, bf16[512,256]{1,0:T(8,128)(2,1)S(1)}, u32[]{:S(2)}, u32[]{:S(2)}) collective-permute-start(bf16[512,256]{1,0:T(8,128)(2,1)S(1)} %get-tuple-element.124), channel_id=1, source_target_pairs={{0,4},{1,5},{2,6},{3,7},{4,8},{5,9},{6,10},{7,11},{8,12},{9,13},{1... | collective-permute-start | bytes 786440 | tf_op jit(solution)/shard_map/ppermute | solution.py:18
  199.2 15.6 %collective-permute-start.31 = (bf16[512,256]{1,0:T(8,128)(2,1)S(1)}, bf16[512,256]{1,0:T(8,128)(2,1)S(1)}, u32[]{:S(2)}, u32[]{:S(2)}) collective-permute-start(bf16[512,256]{1,0:T(8,128)(2,1)S(1)} %get-tuple-element.125), channel_id=1, source_target_pairs={{0,12},{1,13},{2,14},{3,15},{4,0},{5,1},{6,2},{7,3},{8,4},{9,5},{1... | collective-permute-start | bytes 786440 | tf_op jit(solution)/shard_map/ppermute | solution.py:18
  203.1 15.9 %collective-permute-start.32 = (bf16[512,256]{1,0:T(8,128)(2,1)S(1)}, bf16[512,256]{1,0:T(8,128)(2,1)S(1)}, u32[]{:S(2)}, u32[]{:S(2)}) collective-permute-start(bf16[512,256]{1,0:T(8,128)(2,1)S(1)} %get-tuple-element.123), channel_id=1, source_target_pairs={{0,4},{1,5},{2,6},{3,7},{4,8},{5,9},{6,10},{7,11},{8,12},{9,13},{1... | collective-permute-start | bytes 786440 | tf_op jit(solution)/shard_map/ppermute | solution.py:18
  (18 other events, 243.2 us)

commit v13 on v11

--- a/solution.py
+++ b/solution.py
@@ -8,7 +8,7 @@
 TAP_SPACING = 16384
 CHUNK_EIGHTHS = (2, 2, 2, 1, 1)
 EARLY = 1
-RIDER_ROWS = 512
+RIDER_ROWS = 640
 RIDER_SPAN = 2
 
 

time: 223 us -> 223 us (level)
  waiting for transfers between devices: 62.6 us -> 56.4 us
  starting transfers between devices: 99.4 us -> 104 us
    ppermute x26, waiting for transfers between devices: 36.8 us -> 29 us  [from_behind(): return lax.ppermute(value, axis, pairs)]
    ppermute x8, starting transfers between devices: 14 us -> 16.9 us  [exchange(): return lax.ppermute(value, axis, pairs)]
  transfers between devices with their start and end apart: 34 -> 34, of which waited for: 14 -> 15; matrix products, arithmetic and copies ran while one was open for 22% -> 23% of each run, Pallas kernels for 0% -> 0%
where the time goes in v13:
time: 223 us
  starting transfers between devices  104 us (47%)
  waiting for transfers between devices  56.4 us (25%)
  matrix products  33.5 us (15%)
  local copies, waits for them, and re-layouts  20.8 us (9%)
  other arithmetic  5.76 us (3%)
    ppermute x26, starting transfers between devices, from_behind(): return lax.ppermute(value, axis, pairs)  87.4 us
    ppermute x26, waiting for transfers between devices, from_behind(): return lax.ppermute(value, axis, pairs)  29 us
    ppermute x8, waiting for transfers between devices, exchange(): return lax.ppermute(value, axis, pairs)  27.4 us
    ppermute x8, starting transfers between devices, exchange(): return lax.ppermute(value, axis, pairs)  16.9 us
    unnamed x44, local copies, waits for them, and re-layouts  6.25 us
    dot_general x5, matrix products, chunk_layer(): preact = preact + jnp.dot(middle, w_mid, preferred_element_type=jnp.float32)  4.65 us
    slice x2, local copies, waits for them, and re-layouts, body(): middle = activations[bounds[k]:bounds[k + 1]]  4.52 us
    slice x5, local copies, waits for them, and re-layouts, send_rows(): low_high[0][start:stop]  4.5 us
  transfers between devices with their start and end apart: 34, of which 15 were waited for; matrix products, arithmetic and copies ran while one was open for 23% of the time, Pallas kernels for 0%

profile of v13, /device:TPU:0, one launch (start us, length us, event | category | flops | bytes accessed | tf_op | source)
XLA Modules:
  0.0 222.6 jit_solution(2416214854836335675)
XLA Ops:
  0.7 2.0 fusion.119
  2.7 3.0 %collective-permute-start.8 = (bf16[512,256]{1,0:T(8,128)(2,1)}, bf16[512,256]{1,0:T(8,128)(2,1)S(1)}, u32[]{:S(2)}, u32[]{:S(2)}) collective-permute-start(bf16[512,256]{1,0:T(8,128)(2,1)} %get-tuple-element.131), channel_id=1, source_target_pairs={{0,4},{1,5},{2,6},{3,7},{4,8},{5,9},{6,10},{7,11},{8,12},{9,13},{1... | collective-permute-start | bytes 786440 | tf_op jit(solution)/shard_map/ppermute | solution.py:18
  5.7 2.0 collective-permute-start.9
  7.7 2.5 %fusion.118 = (bf16[1024,256]{1,0:T(8,128)(2,1)}, bf16[1024,256]{1,0:T(8,128)(2,1)}, bf16[1024,256]{1,0:T(8,128)(2,1)}) fusion(bf16[4096,256]{1,0:T(8,128)(2,1)} %param.4), kind=kLoop, calls=%fused_computation.208 | loop fusion | bytes 3145728 | tf_op jit(solution)/shard_map/slice | solution.py:95
  10.2 3.8 %collective-permute-start.1 = (bf16[1024,256]{1,0:T(8,128)(2,1)}, bf16[1024,256]{1,0:T(8,128)(2,1)}, u32[]{:S(2)}, u32[]{:S(2)}) collective-permute-start(bf16[1024,256]{1,0:T(8,128)(2,1)} %get-tuple-element.129), channel_id=1, source_target_pairs={{0,12},{1,13},{2,14},{3,15},{4,0},{5,1},{6,2},{7,3},{8,4},{9,5},{1... | collective-permute-start | bytes 1572872 | tf_op jit(solution)/shard_map/ppermute | solution.py:18
  14.1 1.8 fusion.77
  18.6 13.5 %collective-permute-done = bf16[1024,256]{1,0:T(8,128)(2,1)} collective-permute-done((bf16[1024,256]{1,0:T(8,128)(2,1)}, bf16[1024,256]{1,0:T(8,128)(2,1)}, u32[]{:S(2)}, u32[]{:S(2)}) %collective-permute-start) | collective-permute-done | bytes 524320 | tf_op jit(solution)/shard_map/ppermute | solution.py:18
  32.1 13.2 %collective-permute-start.3 = (bf16[1024,256]{1,0:T(8,128)(2,1)}, bf16[1024,256]{1,0:T(8,128)(2,1)S(1)}, u32[]{:S(2)}, u32[]{:S(2)}) collective-permute-start(bf16[1024,256]{1,0:T(8,128)(2,1)} %get-tuple-element.127), channel_id=1, source_target_pairs={{0,12},{1,13},{2,14},{3,15},{4,0},{5,1},{6,2},{7,3},{8,4},{9,5},{1... | collective-permute-start | bytes 1572872 | tf_op jit(solution)/shard_map/ppermute | solution.py:18
  54.6 13.2 %collective-permute-start.5 = (bf16[1024,256]{1,0:T(8,128)(2,1)S(1)}, bf16[1024,256]{1,0:T(8,128)(2,1)S(1)}, u32[]{:S(2)}, u32[]{:S(2)}) collective-permute-start(bf16[1024,256]{1,0:T(8,128)(2,1)S(1)} %copy-done.12), channel_id=1, source_target_pairs={{0,12},{1,13},{2,14},{3,15},{4,0},{5,1},{6,2},{7,3},{8,4},{9,5},{1... | collective-permute-start | bytes 1572872 | tf_op jit(solution)/shard_map/ppermute | solution.py:18
  67.8 8.3 %collective-permute-start.6 = (bf16[512,256]{1,0:T(8,128)(2,1)S(1)}, bf16[512,256]{1,0:T(8,128)(2,1)S(1)}, u32[]{:S(2)}, u32[]{:S(2)}) collective-permute-start(bf16[512,256]{1,0:T(8,128)(2,1)S(1)} %copy-done.13), channel_id=1, source_target_pairs={{0,4},{1,5},{2,6},{3,7},{4,8},{5,9},{6,10},{7,11},{8,12},{9,13},{1... | collective-permute-start | bytes 786440 | tf_op jit(solution)/shard_map/ppermute | solution.py:18
  82.3 7.8 %collective-permute-start.7 = (bf16[512,256]{1,0:T(8,128)(2,1)S(1)}, bf16[512,256]{1,0:T(8,128)(2,1)S(1)}, u32[]{:S(2)}, u32[]{:S(2)}) collective-permute-start(bf16[512,256]{1,0:T(8,128)(2,1)S(1)} %copy-done.13), channel_id=1, source_target_pairs={{0,12},{1,13},{2,14},{3,15},{4,0},{5,1},{6,2},{7,3},{8,4},{9,5},{1... | collective-permute-start | bytes 786440 | tf_op jit(solution)/shard_map/ppermute | solution.py:18
  94.8 3.1 %collective-permute-done.7 = bf16[512,256]{1,0:T(8,128)(2,1)S(1)} collective-permute-done((bf16[512,256]{1,0:T(8,128)(2,1)S(1)}, bf16[512,256]{1,0:T(8,128)(2,1)S(1)}, u32[]{:S(2)}, u32[]{:S(2)}) %collective-permute-start.7) | collective-permute-done | bytes 262176 | tf_op jit(solution)/shard_map/ppermute | solution.py:18
  106.0 2.4 %collective-permute-start.12 = (bf16[512,256]{1,0:T(8,128)(2,1)S(1)}, bf16[512,256]{1,0:T(8,128)(2,1)S(1)}, u32[]{:S(2)}, u32[]{:S(2)}) collective-permute-start(bf16[512,256]{1,0:T(8,128)(2,1)S(1)} %get-tuple-element.143), channel_id=1, source_target_pairs={{0,12},{1,13},{2,14},{3,15},{4,0},{5,1},{6,2},{7,3},{8,4},{9,5},{1... | collective-permute-start | bytes 786440 | tf_op jit(solution)/shard_map/ppermute | solution.py:18
  108.5 3.8 %collective-permute-start.14 = (bf16[512,256]{1,0:T(8,128)(2,1)S(1)}, bf16[512,256]{1,0:T(8,128)(2,1)S(1)}, u32[]{:S(2)}, u32[]{:S(2)}) collective-permute-start(bf16[512,256]{1,0:T(8,128)(2,1)S(1)} %get-tuple-element.142), channel_id=1, source_target_pairs={{0,12},{1,13},{2,14},{3,15},{4,0},{5,1},{6,2},{7,3},{8,4},{9,5},{1... | collective-permute-start | bytes 786440 | tf_op jit(solution)/shard_map/ppermute | solution.py:18
  119.1 9.9 %collective-permute-done.11 = f32[114688]{0:T(1024)S(1)} collective-permute-done((f32[114688]{0:T(1024)S(1)}, f32[114688]{0:T(1024)S(1)}, u32[]{:S(2)}, u32[]{:S(2)}) %collective-permute-start.11) | collective-permute-done | bytes 458784 | tf_op jit(solution)/shard_map/ppermute | solution.py:24
  129.0 3.4 %collective-permute-done.15 = bf16[512,256]{1,0:T(8,128)(2,1)S(1)} collective-permute-done((bf16[512,256]{1,0:T(8,128)(2,1)S(1)}, bf16[512,256]{1,0:T(8,128)(2,1)S(1)}, u32[]{:S(2)}, u32[]{:S(2)}) %collective-permute-start.15) | collective-permute-done | bytes 262176 | tf_op jit(solution)/shard_map/ppermute | solution.py:18
  138.4 2.6 %collective-permute-done.16 = f32[57344]{0:T(1024)S(1)} collective-permute-done((f32[57344]{0:T(1024)S(1)}, f32[57344]{0:T(1024)S(1)}, u32[]{:S(2)}, u32[]{:S(2)}) %collective-permute-start.16) | collective-permute-done | bytes 229408 | tf_op jit(solution)/shard_map/ppermute | solution.py:24
  141.1 1.7 collective-permute-start.17
  144.3 2.3 %collective-permute-start.21 = (bf16[640,256]{1,0:T(8,128)(2,1)}, bf16[640,256]{1,0:T(8,128)(2,1)S(1)}, u32[]{:S(2)}, u32[]{:S(2)}) collective-permute-start(bf16[640,256]{1,0:T(8,128)(2,1)} %slice.164), channel_id=1, source_target_pairs={{0,12},{1,13},{2,14},{3,15},{4,0},{5,1},{6,2},{7,3},{8,4},{9,5},{1... | collective-permute-start | bytes 983048 | tf_op jit(solution)/shard_map/ppermute | solution.py:18
  147.3 9.4 %collective-permute-done.17 = f32[28672]{0:T(1024)S(1)} collective-permute-done((f32[28672]{0:T(1024)S(1)}, f32[28672]{0:T(1024)S(1)}, u32[]{:S(2)}, u32[]{:S(2)}) %collective-permute-start.17) | collective-permute-done | bytes 114720 | tf_op jit(solution)/shard_map/ppermute | solution.py:24
  157.6 2.6 %collective-permute-start.20 = (f32[56,512]{1,0:T(8,128)S(1)}, f32[56,512]{1,0:T(8,128)S(1)}, u32[]{:S(2)}, u32[]{:S(2)}) collective-permute-start(f32[56,512]{1,0:T(8,128)S(1)} %reshape.20), channel_id=1, source_target_pairs={{0,8},{1,9},{2,10},{3,11},{4,12},{5,13},{6,14},{7,15},{8,0},{9,1},... | collective-permute-start | bytes 344072 | tf_op jit(solution)/shard_map/ppermute | solution.py:24
  161.3 8.0 %collective-permute-start.24 = (bf16[640,256]{1,0:T(8,128)(2,1)S(1)}, bf16[640,256]{1,0:T(8,128)(2,1)S(1)}, u32[]{:S(2)}, u32[]{:S(2)}) collective-permute-start(bf16[640,256]{1,0:T(8,128)(2,1)S(1)} %slice.166), channel_id=1, source_target_pairs={{0,12},{1,13},{2,14},{3,15},{4,0},{5,1},{6,2},{7,3},{8,4},{9,5},{1... | collective-permute-start | bytes 983048 | tf_op jit(solution)/shard_map/ppermute | solution.py:18
  170.9 1.7 constant_dynamic-update-slice_fusion.16
  173.7 2.8 %collective-permute-done.20 = f32[56,512]{1,0:T(8,128)S(1)} collective-permute-done((f32[56,512]{1,0:T(8,128)S(1)}, f32[56,512]{1,0:T(8,128)S(1)}, u32[]{:S(2)}, u32[]{:S(2)}) %collective-permute-start.20) | collective-permute-done | bytes 114720 | tf_op jit(solution)/shard_map/ppermute | solution.py:24
  176.6 7.7 %collective-permute-start.23 = (f32[112,512]{1,0:T(8,128)S(1)}, f32[112,512]{1,0:T(8,128)S(1)}, u32[]{:S(2)}, u32[]{:S(2)}) collective-permute-start(f32[112,512]{1,0:T(8,128)S(1)} %pad_maximum_fusion.9), channel_id=1, source_target_pairs={{0,4},{1,5},{2,6},{3,7},{4,0},{5,1},{6,2},{7,3},{8,12},{9,13},{10,... | collective-permute-start | bytes 688136 | tf_op jit(solution)/shard_map/ppermute | solution.py:24
  185.3 2.9 %collective-permute-start.27 = (bf16[640,256]{1,0:T(8,128)(2,1)S(1)}, bf16[640,256]{1,0:T(8,128)(2,1)S(1)}, u32[]{:S(2)}, u32[]{:S(2)}) collective-permute-start(bf16[640,256]{1,0:T(8,128)(2,1)S(1)} %slice.168), channel_id=1, source_target_pairs={{0,12},{1,13},{2,14},{3,15},{4,0},{5,1},{6,2},{7,3},{8,4},{9,5},{1... | collective-permute-start | bytes 983048 | tf_op jit(solution)/shard_map/ppermute | solution.py:18
  190.3 2.7 %collective-permute-done.23 = f32[112,512]{1,0:T(8,128)S(1)} collective-permute-done((f32[112,512]{1,0:T(8,128)S(1)}, f32[112,512]{1,0:T(8,128)S(1)}, u32[]{:S(2)}, u32[]{:S(2)}) %collective-permute-start.23) | collective-permute-done | bytes 229408 | tf_op jit(solution)/shard_map/ppermute | solution.py:24
  195.7 8.9 %collective-permute-start.29 = (bf16[256,256]{1,0:T(8,128)(2,1)S(1)}, bf16[256,256]{1,0:T(8,128)(2,1)S(1)}, u32[]{:S(2)}, u32[]{:S(2)}) collective-permute-start(bf16[256,256]{1,0:T(8,128)(2,1)S(1)} %get-tuple-element.126), channel_id=1, source_target_pairs={{0,12},{1,13},{2,14},{3,15},{4,0},{5,1},{6,2},{7,3},{8,4},{9,5},{1... | collective-permute-start | bytes 393224 | tf_op jit(solution)/shard_map/ppermute | solution.py:18
  205.7 4.8 %collective-permute-start.31 = (bf16[256,256]{1,0:T(8,128)(2,1)S(1)}, bf16[256,256]{1,0:T(8,128)(2,1)S(1)}, u32[]{:S(2)}, u32[]{:S(2)}) collective-permute-start(bf16[256,256]{1,0:T(8,128)(2,1)S(1)} %get-tuple-element.125), channel_id=1, source_target_pairs={{0,12},{1,13},{2,14},{3,15},{4,0},{5,1},{6,2},{7,3},{8,4},{9,5},{1... | collective-permute-start | bytes 393224 | tf_op jit(solution)/shard_map/ppermute | solution.py:18
  211.4 2.6 %collective-permute-done.30 = bf16[256,256]{1,0:T(8,128)(2,1)S(1)} collective-permute-done((bf16[256,256]{1,0:T(8,128)(2,1)S(1)}, bf16[256,256]{1,0:T(8,128)(2,1)S(1)}, u32[]{:S(2)}, u32[]{:S(2)}) %collective-permute-start.30) | collective-permute-done | bytes 131104 | tf_op jit(solution)/shard_map/ppermute | solution.py:18
  214.9 2.9 %collective-permute-done.32 = bf16[256,256]{1,0:T(8,128)(2,1)S(1)} collective-permute-done((bf16[256,256]{1,0:T(8,128)(2,1)S(1)}, bf16[256,256]{1,0:T(8,128)(2,1)S(1)}, u32[]{:S(2)}, u32[]{:S(2)}) %collective-permute-start.32) | collective-permute-done | bytes 131104 | tf_op jit(solution)/shard_map/ppermute | solution.py:18
  218.0 2.2 add_convert_fusion
  (180 shorter events, 61.2 us)
Async XLA Ops:
  2.7 98.3 %collective-permute-start.8 = (bf16[512,256]{1,0:T(8,128)(2,1)}, bf16[512,256]{1,0:T(8,128)(2,1)S(1)}, u32[]{:S(2)}, u32[]{:S(2)}) collective-permute-start(bf16[512,256]{1,0:T(8,128)(2,1)} %get-tuple-element.131), channel_id=1, source_target_pairs={{0,4},{1,5},{2,6},{3,7},{4,8},{5,9},{6,10},{7,11},{8,12},{9,13},{1... | collective-permute-start | bytes 786440 | tf_op jit(solution)/shard_map/ppermute | solution.py:18
  5.7 95.3 %collective-permute-start.9 = (bf16[512,256]{1,0:T(8,128)(2,1)}, bf16[512,256]{1,0:T(8,128)(2,1)S(1)}, u32[]{:S(2)}, u32[]{:S(2)}) collective-permute-start(bf16[512,256]{1,0:T(8,128)(2,1)} %get-tuple-element.131), channel_id=1, source_target_pairs={{0,12},{1,13},{2,14},{3,15},{4,0},{5,1},{6,2},{7,3},{8,4},{9,5},{1... | collective-permute-start | bytes 786440 | tf_op jit(solution)/shard_map/ppermute | solution.py:18
  10.2 21.9 %collective-permute-start = (bf16[1024,256]{1,0:T(8,128)(2,1)}, bf16[1024,256]{1,0:T(8,128)(2,1)}, u32[]{:S(2)}, u32[]{:S(2)}) collective-permute-start(bf16[1024,256]{1,0:T(8,128)(2,1)} %get-tuple-element.129), channel_id=1, source_target_pairs={{0,4},{1,5},{2,6},{3,7},{4,8},{5,9},{6,10},{7,11},{8,12},{9,13},{1... | collective-permute-start | bytes 1572872 | tf_op jit(solution)/shard_map/ppermute | solution.py:18
  10.2 36.6 %collective-permute-start.1 = (bf16[1024,256]{1,0:T(8,128)(2,1)}, bf16[1024,256]{1,0:T(8,128)(2,1)}, u32[]{:S(2)}, u32[]{:S(2)}) collective-permute-start(bf16[1024,256]{1,0:T(8,128)(2,1)} %get-tuple-element.129), channel_id=1, source_target_pairs={{0,12},{1,13},{2,14},{3,15},{4,0},{5,1},{6,2},{7,3},{8,4},{9,5},{1... | collective-permute-start | bytes 1572872 | tf_op jit(solution)/shard_map/ppermute | solution.py:18
  14.1 40.6 %collective-permute-start.2 = (bf16[1024,256]{1,0:T(8,128)(2,1)}, bf16[1024,256]{1,0:T(8,128)(2,1)}, u32[]{:S(2)}, u32[]{:S(2)}) collective-permute-start(bf16[1024,256]{1,0:T(8,128)(2,1)} %get-tuple-element.127), channel_id=1, source_target_pairs={{0,4},{1,5},{2,6},{3,7},{4,8},{5,9},{6,10},{7,11},{8,12},{9,13},{1... | collective-permute-start | bytes 1572872 | tf_op jit(solution)/shard_map/ppermute | solution.py:18
  32.1 35.7 %collective-permute-start.3 = (bf16[1024,256]{1,0:T(8,128)(2,1)}, bf16[1024,256]{1,0:T(8,128)(2,1)S(1)}, u32[]{:S(2)}, u32[]{:S(2)}) collective-permute-start(bf16[1024,256]{1,0:T(8,128)(2,1)} %get-tuple-element.127), channel_id=1, source_target_pairs={{0,12},{1,13},{2,14},{3,15},{4,0},{5,1},{6,2},{7,3},{8,4},{9,5},{1... | collective-permute-start | bytes 1572872 | tf_op jit(solution)/shard_map/ppermute | solution.py:18
  46.9 35.4 %collective-permute-start.4 = (bf16[1024,256]{1,0:T(8,128)(2,1)S(1)}, bf16[1024,256]{1,0:T(8,128)(2,1)S(1)}, u32[]{:S(2)}, u32[]{:S(2)}) collective-permute-start(bf16[1024,256]{1,0:T(8,128)(2,1)S(1)} %copy-done.12), channel_id=1, source_target_pairs={{0,4},{1,5},{2,6},{3,7},{4,8},{5,9},{6,10},{7,11},{8,12},{9,13},{1... | collective-permute-start | bytes 1572872 | tf_op jit(solution)/shard_map/ppermute | solution.py:18
  54.6 35.5 %collective-permute-start.5 = (bf16[1024,256]{1,0:T(8,128)(2,1)S(1)}, bf16[1024,256]{1,0:T(8,128)(2,1)S(1)}, u32[]{:S(2)}, u32[]{:S(2)}) collective-permute-start(bf16[1024,256]{1,0:T(8,128)(2,1)S(1)} %copy-done.12), channel_id=1, source_target_pairs={{0,12},{1,13},{2,14},{3,15},{4,0},{5,1},{6,2},{7,3},{8,4},{9,5},{1... | collective-permute-start | bytes 1572872 | tf_op jit(solution)/shard_map/ppermute | solution.py:18
  67.8 27.0 %collective-permute-start.6 = (bf16[512,256]{1,0:T(8,128)(2,1)S(1)}, bf16[512,256]{1,0:T(8,128)(2,1)S(1)}, u32[]{:S(2)}, u32[]{:S(2)}) collective-permute-start(bf16[512,256]{1,0:T(8,128)(2,1)S(1)} %copy-done.13), channel_id=1, source_target_pairs={{0,4},{1,5},{2,6},{3,7},{4,8},{5,9},{6,10},{7,11},{8,12},{9,13},{1... | collective-permute-start | bytes 786440 | tf_op jit(solution)/shard_map/ppermute | solution.py:18
  82.3 15.6 %collective-permute-start.7 = (bf16[512,256]{1,0:T(8,128)(2,1)S(1)}, bf16[512,256]{1,0:T(8,128)(2,1)S(1)}, u32[]{:S(2)}, u32[]{:S(2)}) collective-permute-start(bf16[512,256]{1,0:T(8,128)(2,1)S(1)} %copy-done.13), channel_id=1, source_target_pairs={{0,12},{1,13},{2,14},{3,15},{4,0},{5,1},{6,2},{7,3},{8,4},{9,5},{1... | collective-permute-start | bytes 786440 | tf_op jit(solution)/shard_map/ppermute | solution.py:18
  105.9 10.8 %collective-permute-start.10 = (f32[229376]{0:T(1024)S(1)}, f32[229376]{0:T(1024)S(1)}, u32[]{:S(2)}, u32[]{:S(2)}) collective-permute-start(f32[229376]{0:T(1024)S(1)} %dynamic_slice.25), channel_id=1, source_target_pairs={{0,1},{1,0},{2,3},{3,2},{4,5},{5,4},{6,7},{7,6},{8,9},{9,8},{10,11... | collective-permute-start | bytes 2752520 | tf_op jit(solution)/shard_map/ppermute | solution.py:24
  106.0 23.0 %collective-permute-start.12 = (bf16[512,256]{1,0:T(8,128)(2,1)S(1)}, bf16[512,256]{1,0:T(8,128)(2,1)S(1)}, u32[]{:S(2)}, u32[]{:S(2)}) collective-permute-start(bf16[512,256]{1,0:T(8,128)(2,1)S(1)} %get-tuple-element.143), channel_id=1, source_target_pairs={{0,12},{1,13},{2,14},{3,15},{4,0},{5,1},{6,2},{7,3},{8,4},{9,5},{1... | collective-permute-start | bytes 786440 | tf_op jit(solution)/shard_map/ppermute | solution.py:18
  108.4 20.6 %collective-permute-start.13 = (bf16[512,256]{1,0:T(8,128)(2,1)S(1)}, bf16[512,256]{1,0:T(8,128)(2,1)S(1)}, u32[]{:S(2)}, u32[]{:S(2)}) collective-permute-start(bf16[512,256]{1,0:T(8,128)(2,1)S(1)} %get-tuple-element.141), channel_id=1, source_target_pairs={{0,4},{1,5},{2,6},{3,7},{4,8},{5,9},{6,10},{7,11},{8,12},{9,13},{1... | collective-permute-start | bytes 786440 | tf_op jit(solution)/shard_map/ppermute | solution.py:18
  108.5 20.6 %collective-permute-start.14 = (bf16[512,256]{1,0:T(8,128)(2,1)S(1)}, bf16[512,256]{1,0:T(8,128)(2,1)S(1)}, u32[]{:S(2)}, u32[]{:S(2)}) collective-permute-start(bf16[512,256]{1,0:T(8,128)(2,1)S(1)} %get-tuple-element.142), channel_id=1, source_target_pairs={{0,12},{1,13},{2,14},{3,15},{4,0},{5,1},{6,2},{7,3},{8,4},{9,5},{1... | collective-permute-start | bytes 786440 | tf_op jit(solution)/shard_map/ppermute | solution.py:18
  112.3 20.1 %collective-permute-start.15 = (bf16[512,256]{1,0:T(8,128)(2,1)S(1)}, bf16[512,256]{1,0:T(8,128)(2,1)S(1)}, u32[]{:S(2)}, u32[]{:S(2)}) collective-permute-start(bf16[512,256]{1,0:T(8,128)(2,1)S(1)} %get-tuple-element.140), channel_id=1, source_target_pairs={{0,4},{1,5},{2,6},{3,7},{4,8},{5,9},{6,10},{7,11},{8,12},{9,13},{1... | collective-permute-start | bytes 786440 | tf_op jit(solution)/shard_map/ppermute | solution.py:18
  116.8 12.1 %collective-permute-start.11 = (f32[114688]{0:T(1024)S(1)}, f32[114688]{0:T(1024)S(1)}, u32[]{:S(2)}, u32[]{:S(2)}) collective-permute-start(f32[114688]{0:T(1024)S(1)} %dynamic_slice.27), channel_id=1, source_target_pairs={{0,2},{1,3},{2,0},{3,1},{4,6},{5,7},{6,4},{7,5},{8,10},{9,11},{10,... | collective-permute-start | bytes 1376264 | tf_op jit(solution)/shard_map/ppermute | solution.py:24
  132.5 8.6 %collective-permute-start.16 = (f32[57344]{0:T(1024)S(1)}, f32[57344]{0:T(1024)S(1)}, u32[]{:S(2)}, u32[]{:S(2)}) collective-permute-start(f32[57344]{0:T(1024)S(1)} %dynamic_slice.29), channel_id=1, source_target_pairs={{0,4},{1,5},{2,6},{3,7},{4,0},{5,1},{6,2},{7,3},{8,12},{9,13},{10,... | collective-permute-start | bytes 688136 | tf_op jit(solution)/shard_map/ppermute | solution.py:24
  134.9 22.8 %collective-permute-start.18 = (bf16[640,256]{1,0:T(8,128)(2,1)}, bf16[640,256]{1,0:T(8,128)(2,1)}, u32[]{:S(2)}, u32[]{:S(2)}) collective-permute-start(bf16[640,256]{1,0:T(8,128)(2,1)} %slice.162), channel_id=1, source_target_pairs={{0,12},{1,13},{2,14},{3,15},{4,0},{5,1},{6,2},{7,3},{8,4},{9,5},{1... | collective-permute-start | bytes 983048 | tf_op jit(solution)/shard_map/ppermute | solution.py:18
  137.1 20.6 %collective-permute-start.19 = (bf16[640,256]{1,0:T(8,128)(2,1)}, bf16[640,256]{1,0:T(8,128)(2,1)}, u32[]{:S(2)}, u32[]{:S(2)}) collective-permute-start(bf16[640,256]{1,0:T(8,128)(2,1)} %slice.163), channel_id=1, source_target_pairs={{0,4},{1,5},{2,6},{3,7},{4,8},{5,9},{6,10},{7,11},{8,12},{9,13},{1... | collective-permute-start | bytes 983048 | tf_op jit(solution)/shard_map/ppermute | solution.py:18
  141.1 15.6 %collective-permute-start.17 = (f32[28672]{0:T(1024)S(1)}, f32[28672]{0:T(1024)S(1)}, u32[]{:S(2)}, u32[]{:S(2)}) collective-permute-start(f32[28672]{0:T(1024)S(1)} %dynamic_slice.31), channel_id=1, source_target_pairs={{0,8},{1,9},{2,10},{3,11},{4,12},{5,13},{6,14},{7,15},{8,0},{9,1},... | collective-permute-start | bytes 344072 | tf_op jit(solution)/shard_map/ppermute | solution.py:24
  144.3 32.3 %collective-permute-start.21 = (bf16[640,256]{1,0:T(8,128)(2,1)}, bf16[640,256]{1,0:T(8,128)(2,1)S(1)}, u32[]{:S(2)}, u32[]{:S(2)}) collective-permute-start(bf16[640,256]{1,0:T(8,128)(2,1)} %slice.164), channel_id=1, source_target_pairs={{0,12},{1,13},{2,14},{3,15},{4,0},{5,1},{6,2},{7,3},{8,4},{9,5},{1... | collective-permute-start | bytes 983048 | tf_op jit(solution)/shard_map/ppermute | solution.py:18
  147.3 29.2 %collective-permute-start.22 = (bf16[640,256]{1,0:T(8,128)(2,1)}, bf16[640,256]{1,0:T(8,128)(2,1)}, u32[]{:S(2)}, u32[]{:S(2)}) collective-permute-start(bf16[640,256]{1,0:T(8,128)(2,1)} %slice.165), channel_id=1, source_target_pairs={{0,4},{1,5},{2,6},{3,7},{4,8},{5,9},{6,10},{7,11},{8,12},{9,13},{1... | collective-permute-start | bytes 983048 | tf_op jit(solution)/shard_map/ppermute | solution.py:18
  157.6 18.9 %collective-permute-start.20 = (f32[56,512]{1,0:T(8,128)S(1)}, f32[56,512]{1,0:T(8,128)S(1)}, u32[]{:S(2)}, u32[]{:S(2)}) collective-permute-start(f32[56,512]{1,0:T(8,128)S(1)} %reshape.20), channel_id=1, source_target_pairs={{0,8},{1,9},{2,10},{3,11},{4,12},{5,13},{6,14},{7,15},{8,0},{9,1},... | collective-permute-start | bytes 344072 | tf_op jit(solution)/shard_map/ppermute | solution.py:24
  161.3 31.8 %collective-permute-start.24 = (bf16[640,256]{1,0:T(8,128)(2,1)S(1)}, bf16[640,256]{1,0:T(8,128)(2,1)S(1)}, u32[]{:S(2)}, u32[]{:S(2)}) collective-permute-start(bf16[640,256]{1,0:T(8,128)(2,1)S(1)} %slice.166), channel_id=1, source_target_pairs={{0,12},{1,13},{2,14},{3,15},{4,0},{5,1},{6,2},{7,3},{8,4},{9,5},{1... | collective-permute-start | bytes 983048 | tf_op jit(solution)/shard_map/ppermute | solution.py:18
  170.3 22.8 %collective-permute-start.25 = (bf16[640,256]{1,0:T(8,128)(2,1)S(1)}, bf16[640,256]{1,0:T(8,128)(2,1)S(1)}, u32[]{:S(2)}, u32[]{:S(2)}) collective-permute-start(bf16[640,256]{1,0:T(8,128)(2,1)S(1)} %slice.167), channel_id=1, source_target_pairs={{0,4},{1,5},{2,6},{3,7},{4,8},{5,9},{6,10},{7,11},{8,12},{9,13},{1... | collective-permute-start | bytes 983048 | tf_op jit(solution)/shard_map/ppermute | solution.py:18
  176.6 16.4 %collective-permute-start.23 = (f32[112,512]{1,0:T(8,128)S(1)}, f32[112,512]{1,0:T(8,128)S(1)}, u32[]{:S(2)}, u32[]{:S(2)}) collective-permute-start(f32[112,512]{1,0:T(8,128)S(1)} %pad_maximum_fusion.9), channel_id=1, source_target_pairs={{0,4},{1,5},{2,6},{3,7},{4,0},{5,1},{6,2},{7,3},{8,12},{9,13},{10,... | collective-permute-start | bytes 688136 | tf_op jit(solution)/shard_map/ppermute | solution.py:24
  185.3 25.3 %collective-permute-start.27 = (bf16[640,256]{1,0:T(8,128)(2,1)S(1)}, bf16[640,256]{1,0:T(8,128)(2,1)S(1)}, u32[]{:S(2)}, u32[]{:S(2)}) collective-permute-start(bf16[640,256]{1,0:T(8,128)(2,1)S(1)} %slice.168), channel_id=1, source_target_pairs={{0,12},{1,13},{2,14},{3,15},{4,0},{5,1},{6,2},{7,3},{8,4},{9,5},{1... | collective-permute-start | bytes 983048 | tf_op jit(solution)/shard_map/ppermute | solution.py:18
  189.2 21.5 %collective-permute-start.28 = (bf16[640,256]{1,0:T(8,128)(2,1)S(1)}, bf16[640,256]{1,0:T(8,128)(2,1)S(1)}, u32[]{:S(2)}, u32[]{:S(2)}) collective-permute-start(bf16[640,256]{1,0:T(8,128)(2,1)S(1)} %slice.169), channel_id=1, source_target_pairs={{0,4},{1,5},{2,6},{3,7},{4,8},{5,9},{6,10},{7,11},{8,12},{9,13},{1... | collective-permute-start | bytes 983048 | tf_op jit(solution)/shard_map/ppermute | solution.py:18
  193.1 12.6 %collective-permute-start.26 = (f32[224,512]{1,0:T(8,128)S(1)}, f32[224,512]{1,0:T(8,128)S(1)}, u32[]{:S(2)}, u32[]{:S(2)}) collective-permute-start(f32[224,512]{1,0:T(8,128)S(1)} %pad_maximum_fusion.8), channel_id=1, source_target_pairs={{0,2},{1,3},{2,0},{3,1},{4,6},{5,7},{6,4},{7,5},{8,10},{9,11},{10,... | collective-permute-start | bytes 1376264 | tf_op jit(solution)/shard_map/ppermute | solution.py:24
  195.7 15.8 %collective-permute-start.29 = (bf16[256,256]{1,0:T(8,128)(2,1)S(1)}, bf16[256,256]{1,0:T(8,128)(2,1)S(1)}, u32[]{:S(2)}, u32[]{:S(2)}) collective-permute-start(bf16[256,256]{1,0:T(8,128)(2,1)S(1)} %get-tuple-element.126), channel_id=1, source_target_pairs={{0,12},{1,13},{2,14},{3,15},{4,0},{5,1},{6,2},{7,3},{8,4},{9,5},{1... | collective-permute-start | bytes 393224 | tf_op jit(solution)/shard_map/ppermute | solution.py:18
  205.6 8.4 %collective-permute-start.30 = (bf16[256,256]{1,0:T(8,128)(2,1)S(1)}, bf16[256,256]{1,0:T(8,128)(2,1)S(1)}, u32[]{:S(2)}, u32[]{:S(2)}) collective-permute-start(bf16[256,256]{1,0:T(8,128)(2,1)S(1)} %get-tuple-element.124), channel_id=1, source_target_pairs={{0,4},{1,5},{2,6},{3,7},{4,8},{5,9},{6,10},{7,11},{8,12},{9,13},{1... | collective-permute-start | bytes 393224 | tf_op jit(solution)/shard_map/ppermute | solution.py:18
  205.7 9.2 %collective-permute-start.31 = (bf16[256,256]{1,0:T(8,128)(2,1)S(1)}, bf16[256,256]{1,0:T(8,128)(2,1)S(1)}, u32[]{:S(2)}, u32[]{:S(2)}) collective-permute-start(bf16[256,256]{1,0:T(8,128)(2,1)S(1)} %get-tuple-element.125), channel_id=1, source_target_pairs={{0,12},{1,13},{2,14},{3,15},{4,0},{5,1},{6,2},{7,3},{8,4},{9,5},{1... | collective-permute-start | bytes 393224 | tf_op jit(solution)/shard_map/ppermute | solution.py:18
  (16 other events, 273.1 us)

commit v14 on v11

--- a/solution.py
+++ b/solution.py
@@ -6,7 +6,7 @@
 from jax.sharding import PartitionSpec as P
 
 TAP_SPACING = 16384
-CHUNK_EIGHTHS = (2, 2, 2, 1, 1)
+CHUNK_EIGHTHS = (2, 2, 2, 2)
 EARLY = 1
 RIDER_ROWS = 512
 RIDER_SPAN = 2

time: 223 us -> 232 us (1.040)
  waiting for transfers between devices: 62.6 us -> 83.8 us
  starting transfers between devices: 99.4 us -> 83 us
  matrix products: 33.5 us -> 36.8 us
    ppermute x26 -> x24, waiting for transfers between devices: 36.8 us -> 60.2 us  [from_behind(): return lax.ppermute(value, axis, pairs)]
    ppermute x26 -> x24, starting transfers between devices: 85.3 us -> 68.7 us  [from_behind(): return lax.ppermute(value, axis, pairs)]
    unnamed x44 -> x50, local copies, waits for them, and re-layouts: 5.04 us -> 9.71 us
    slice x5, local copies, waits for them, and re-layouts: 4.44 us -> 1.53 us  [send_rows(): low_high[1][start:stop]]
    dot_general x5 -> x4, matrix products: 2.16 us -> 4.96 us  [chunk_layer(): lax.dot_general(grad_pre, w_mid, last_dims, preferred_element_type=jnp.fl...]
    dot_general x5 -> x4, matrix products: 4.24 us -> 5.08 us  [chunk_layer(): lax.dot_general(left_tap_input, grad_pre, first_dims, preferred_element_t...]
    dot_general x5 -> x4, matrix products: 4.21 us -> 5.05 us  [chunk_layer(): preact = jnp.dot(left_tap_input, w_low, preferred_element_type=jnp.float32)]
    dot_general x5 -> x4, matrix products: 4.65 us -> 4.44 us  [chunk_layer(): preact = preact + jnp.dot(middle, w_mid, preferred_element_type=jnp.float32)]
  transfers between devices with their start and end apart: 34 -> 32, of which waited for: 14 -> 15; matrix products, arithmetic and copies ran while one was open for 22% -> 20% of each run, Pallas kernels for 0% -> 0%
where the time goes in v14:
time: 232 us; the launch traced here: 231 us
  waiting for transfers between devices  83.8 us (36%)
  starting transfers between devices  83 us (36%)
  matrix products  36.8 us (16%)
  local copies, waits for them, and re-layouts  19.8 us (9%)
  other arithmetic  5.93 us (3%)
    ppermute x24, starting transfers between devices, from_behind(): return lax.ppermute(value, axis, pairs)  68.7 us
    ppermute x24, waiting for transfers between devices, from_behind(): return lax.ppermute(value, axis, pairs)  60.2 us
    ppermute x8, waiting for transfers between devices, exchange(): return lax.ppermute(value, axis, pairs)  23.6 us
    ppermute x8, starting transfers between devices, exchange(): return lax.ppermute(value, axis, pairs)  14.3 us
    unnamed x50, local copies, waits for them, and re-layouts  9.71 us
    dot_general x4, matrix products, chunk_layer(): lax.dot_general(left_tap_input, grad_pre, first_dims, preferred_element_t...  5.08 us
    dot_general x4, matrix products, chunk_layer(): preact = jnp.dot(left_tap_input, w_low, preferred_element_type=jnp.float32)  5.05 us
    dot_general x4, matrix products, chunk_layer(): lax.dot_general(grad_pre, w_mid, last_dims, preferred_element_type=jnp.fl...  4.96 us
  transfers between devices with their start and end apart: 32, of which 15 were waited for; matrix products, arithmetic and copies ran while one was open for 20% of the time, Pallas kernels for 0%

profile of v14, /device:TPU:0, one launch (start us, length us, event | category | flops | bytes accessed | tf_op | source)
XLA Modules:
  0.0 231.1 jit_solution(12678111535257462306)
XLA Ops:
  0.7 3.0 %fusion.97 = (bf16[1024,256]{1,0:T(8,128)(2,1)}, bf16[1024,256]{1,0:T(8,128)(2,1)}, bf16[1024,256]{1,0:T(8,128)(2,1)}, bf16[1024,256]{1,0:T(8,128)(2,1)}) fusion(bf16[4096,256]{1,0:T(8,128)(2,1)} %param.4), kind=kLoop, calls=%fused_computation.171 | loop fusion | bytes 4194304 | tf_op jit(solution)/shard_map/slice | solution.py:95
  3.7 3.0 %collective-permute-start.6 = (bf16[1024,256]{1,0:T(8,128)(2,1)}, bf16[1024,256]{1,0:T(8,128)(2,1)}, u32[]{:S(2)}, u32[]{:S(2)}) collective-permute-start(bf16[1024,256]{1,0:T(8,128)(2,1)} %get-tuple-element.123), channel_id=1, source_target_pairs={{0,4},{1,5},{2,6},{3,7},{4,8},{5,9},{6,10},{7,11},{8,12},{9,13},{1... | collective-permute-start | bytes 1572872 | tf_op jit(solution)/shard_map/ppermute | solution.py:18
  6.7 2.0 collective-permute-start.7
  8.8 3.8 %collective-permute-start.1 = (bf16[1024,256]{1,0:T(8,128)(2,1)}, bf16[1024,256]{1,0:T(8,128)(2,1)}, u32[]{:S(2)}, u32[]{:S(2)}) collective-permute-start(bf16[1024,256]{1,0:T(8,128)(2,1)} %get-tuple-element.122), channel_id=1, source_target_pairs={{0,12},{1,13},{2,14},{3,15},{4,0},{5,1},{6,2},{7,3},{8,4},{9,5},{1... | collective-permute-start | bytes 1572872 | tf_op jit(solution)/shard_map/ppermute | solution.py:18
  12.6 1.8 fusion.63
  17.3 27.1 %collective-permute-done = bf16[1024,256]{1,0:T(8,128)(2,1)} collective-permute-done((bf16[1024,256]{1,0:T(8,128)(2,1)}, bf16[1024,256]{1,0:T(8,128)(2,1)}, u32[]{:S(2)}, u32[]{:S(2)}) %collective-permute-start) | collective-permute-done | bytes 524320 | tf_op jit(solution)/shard_map/ppermute | solution.py:18
  44.4 13.2 %collective-permute-start.3 = (bf16[1024,256]{1,0:T(8,128)(2,1)}, bf16[1024,256]{1,0:T(8,128)(2,1)S(1)}, u32[]{:S(2)}, u32[]{:S(2)}) collective-permute-start(bf16[1024,256]{1,0:T(8,128)(2,1)} %get-tuple-element.121), channel_id=1, source_target_pairs={{0,12},{1,13},{2,14},{3,15},{4,0},{5,1},{6,2},{7,3},{8,4},{9,5},{1... | collective-permute-start | bytes 1572872 | tf_op jit(solution)/shard_map/ppermute | solution.py:18
  59.2 1.7 add_add_fusion.3
  66.9 13.2 %collective-permute-start.5 = (bf16[1024,256]{1,0:T(8,128)(2,1)S(1)}, bf16[1024,256]{1,0:T(8,128)(2,1)S(1)}, u32[]{:S(2)}, u32[]{:S(2)}) collective-permute-start(bf16[1024,256]{1,0:T(8,128)(2,1)S(1)} %copy-done.16), channel_id=1, source_target_pairs={{0,12},{1,13},{2,14},{3,15},{4,0},{5,1},{6,2},{7,3},{8,4},{9,5},{1... | collective-permute-start | bytes 1572872 | tf_op jit(solution)/shard_map/ppermute | solution.py:18
  86.8 2.5 %collective-permute-done.4 = bf16[1024,256]{1,0:T(8,128)(2,1)S(1)} collective-permute-done((bf16[1024,256]{1,0:T(8,128)(2,1)S(1)}, bf16[1024,256]{1,0:T(8,128)(2,1)S(1)}, u32[]{:S(2)}, u32[]{:S(2)}) %collective-permute-start.4) | collective-permute-done | bytes 524320 | tf_op jit(solution)/shard_map/ppermute | solution.py:18
  89.3 9.7 %collective-permute-done.5 = bf16[1024,256]{1,0:T(8,128)(2,1)S(1)} collective-permute-done((bf16[1024,256]{1,0:T(8,128)(2,1)S(1)}, bf16[1024,256]{1,0:T(8,128)(2,1)S(1)}, u32[]{:S(2)}, u32[]{:S(2)}) %collective-permute-start.5) | collective-permute-done | bytes 524320 | tf_op jit(solution)/shard_map/ppermute | solution.py:18
  114.5 2.4 %collective-permute-start.10 = (bf16[512,256]{1,0:T(8,128)(2,1)S(1)}, bf16[512,256]{1,0:T(8,128)(2,1)S(1)}, u32[]{:S(2)}, u32[]{:S(2)}) collective-permute-start(bf16[512,256]{1,0:T(8,128)(2,1)S(1)} %get-tuple-element.132), channel_id=1, source_target_pairs={{0,12},{1,13},{2,14},{3,15},{4,0},{5,1},{6,2},{7,3},{8,4},{9,5},{1... | collective-permute-start | bytes 786440 | tf_op jit(solution)/shard_map/ppermute | solution.py:18
  117.0 3.8 %collective-permute-start.12 = (bf16[512,256]{1,0:T(8,128)(2,1)S(1)}, bf16[512,256]{1,0:T(8,128)(2,1)S(1)}, u32[]{:S(2)}, u32[]{:S(2)}) collective-permute-start(bf16[512,256]{1,0:T(8,128)(2,1)S(1)} %get-tuple-element.131), channel_id=1, source_target_pairs={{0,12},{1,13},{2,14},{3,15},{4,0},{5,1},{6,2},{7,3},{8,4},{9,5},{1... | collective-permute-start | bytes 786440 | tf_op jit(solution)/shard_map/ppermute | solution.py:18
  128.2 9.8 %collective-permute-done.9 = f32[114688]{0:T(1024)S(1)} collective-permute-done((f32[114688]{0:T(1024)S(1)}, f32[114688]{0:T(1024)S(1)}, u32[]{:S(2)}, u32[]{:S(2)}) %collective-permute-start.9) | collective-permute-done | bytes 458784 | tf_op jit(solution)/shard_map/ppermute | solution.py:24
  138.2 2.8 %collective-permute-done.13 = bf16[512,256]{1,0:T(8,128)(2,1)S(1)} collective-permute-done((bf16[512,256]{1,0:T(8,128)(2,1)S(1)}, bf16[512,256]{1,0:T(8,128)(2,1)S(1)}, u32[]{:S(2)}, u32[]{:S(2)}) %collective-permute-start.13) | collective-permute-done | bytes 262176 | tf_op jit(solution)/shard_map/ppermute | solution.py:18
  140.9 1.7 collective-permute-start.14
  147.6 2.0 collective-permute-done.14
  149.6 1.7 collective-permute-start.15
  152.8 2.3 %collective-permute-start.19 = (bf16[512,256]{1,0:T(8,128)(2,1)}, bf16[512,256]{1,0:T(8,128)(2,1)}, u32[]{:S(2)}, u32[]{:S(2)}) collective-permute-start(bf16[512,256]{1,0:T(8,128)(2,1)} %slice.145), channel_id=1, source_target_pairs={{0,12},{1,13},{2,14},{3,15},{4,0},{5,1},{6,2},{7,3},{8,4},{9,5},{1... | collective-permute-start | bytes 786440 | tf_op jit(solution)/shard_map/ppermute | solution.py:18
  155.9 7.8 %collective-permute-done.15 = f32[28672]{0:T(1024)S(1)} collective-permute-done((f32[28672]{0:T(1024)S(1)}, f32[28672]{0:T(1024)S(1)}, u32[]{:S(2)}, u32[]{:S(2)}) %collective-permute-start.15) | collective-permute-done | bytes 114720 | tf_op jit(solution)/shard_map/ppermute | solution.py:24
  163.8 2.2 collective-permute-start.18
  167.0 6.5 %collective-permute-start.22 = (bf16[512,256]{1,0:T(8,128)(2,1)S(1)}, bf16[512,256]{1,0:T(8,128)(2,1)S(1)}, u32[]{:S(2)}, u32[]{:S(2)}) collective-permute-start(bf16[512,256]{1,0:T(8,128)(2,1)S(1)} %slice.147), channel_id=1, source_target_pairs={{0,12},{1,13},{2,14},{3,15},{4,0},{5,1},{6,2},{7,3},{8,4},{9,5},{1... | collective-permute-start | bytes 786440 | tf_op jit(solution)/shard_map/ppermute | solution.py:18
  177.5 2.7 %collective-permute-done.18 = f32[56,512]{1,0:T(8,128)S(1)} collective-permute-done((f32[56,512]{1,0:T(8,128)S(1)}, f32[56,512]{1,0:T(8,128)S(1)}, u32[]{:S(2)}, u32[]{:S(2)}) %collective-permute-start.18) | collective-permute-done | bytes 114720 | tf_op jit(solution)/shard_map/ppermute | solution.py:24
  180.3 5.5 %collective-permute-start.21 = (f32[112,512]{1,0:T(8,128)S(1)}, f32[112,512]{1,0:T(8,128)S(1)}, u32[]{:S(2)}, u32[]{:S(2)}) collective-permute-start(f32[112,512]{1,0:T(8,128)S(1)} %pad_maximum_fusion.10), channel_id=1, source_target_pairs={{0,4},{1,5},{2,6},{3,7},{4,0},{5,1},{6,2},{7,3},{8,12},{9,13},{10,... | collective-permute-start | bytes 688136 | tf_op jit(solution)/shard_map/ppermute | solution.py:24
  186.8 2.9 %collective-permute-start.25 = (bf16[512,256]{1,0:T(8,128)(2,1)S(1)}, bf16[512,256]{1,0:T(8,128)(2,1)S(1)}, u32[]{:S(2)}, u32[]{:S(2)}) collective-permute-start(bf16[512,256]{1,0:T(8,128)(2,1)S(1)} %slice.149), channel_id=1, source_target_pairs={{0,12},{1,13},{2,14},{3,15},{4,0},{5,1},{6,2},{7,3},{8,4},{9,5},{1... | collective-permute-start | bytes 786440 | tf_op jit(solution)/shard_map/ppermute | solution.py:18
  196.1 8.8 %collective-permute-start.27 = (bf16[512,256]{1,0:T(8,128)(2,1)S(1)}, bf16[512,256]{1,0:T(8,128)(2,1)S(1)}, u32[]{:S(2)}, u32[]{:S(2)}) collective-permute-start(bf16[512,256]{1,0:T(8,128)(2,1)S(1)} %get-tuple-element.120), channel_id=1, source_target_pairs={{0,12},{1,13},{2,14},{3,15},{4,0},{5,1},{6,2},{7,3},{8,4},{9,5},{1... | collective-permute-start | bytes 786440 | tf_op jit(solution)/shard_map/ppermute | solution.py:18
  205.1 3.9 %collective-permute-start.29 = (bf16[512,256]{1,0:T(8,128)(2,1)S(1)}, bf16[512,256]{1,0:T(8,128)(2,1)S(1)}, u32[]{:S(2)}, u32[]{:S(2)}) collective-permute-start(bf16[512,256]{1,0:T(8,128)(2,1)S(1)} %get-tuple-element.119), channel_id=1, source_target_pairs={{0,12},{1,13},{2,14},{3,15},{4,0},{5,1},{6,2},{7,3},{8,4},{9,5},{1... | collective-permute-start | bytes 786440 | tf_op jit(solution)/shard_map/ppermute | solution.py:18
  209.1 4.7 %collective-permute-done.27 = bf16[512,256]{1,0:T(8,128)(2,1)S(1)} collective-permute-done((bf16[512,256]{1,0:T(8,128)(2,1)S(1)}, bf16[512,256]{1,0:T(8,128)(2,1)S(1)}, u32[]{:S(2)}, u32[]{:S(2)}) %collective-permute-start.27) | collective-permute-done | bytes 262176 | tf_op jit(solution)/shard_map/ppermute | solution.py:18
  213.8 3.9 %collective-permute-done.28 = bf16[512,256]{1,0:T(8,128)(2,1)S(1)} collective-permute-done((bf16[512,256]{1,0:T(8,128)(2,1)S(1)}, bf16[512,256]{1,0:T(8,128)(2,1)S(1)}, u32[]{:S(2)}, u32[]{:S(2)}) %collective-permute-start.28) | collective-permute-done | bytes 262176 | tf_op jit(solution)/shard_map/ppermute | solution.py:18
  217.7 4.3 %collective-permute-done.29 = bf16[512,256]{1,0:T(8,128)(2,1)S(1)} collective-permute-done((bf16[512,256]{1,0:T(8,128)(2,1)S(1)}, bf16[512,256]{1,0:T(8,128)(2,1)S(1)}, u32[]{:S(2)}, u32[]{:S(2)}) %collective-permute-start.29) | collective-permute-done | bytes 262176 | tf_op jit(solution)/shard_map/ppermute | solution.py:18
  222.1 4.3 %collective-permute-done.30 = bf16[512,256]{1,0:T(8,128)(2,1)S(1)} collective-permute-done((bf16[512,256]{1,0:T(8,128)(2,1)S(1)}, bf16[512,256]{1,0:T(8,128)(2,1)S(1)}, u32[]{:S(2)}, u32[]{:S(2)}) %collective-permute-start.30) | collective-permute-done | bytes 262176 | tf_op jit(solution)/shard_map/ppermute | solution.py:18
  226.5 2.0 fusion.2
  (169 shorter events, 62.3 us)
Async XLA Ops:
  3.7 99.5 %collective-permute-start.6 = (bf16[1024,256]{1,0:T(8,128)(2,1)}, bf16[1024,256]{1,0:T(8,128)(2,1)}, u32[]{:S(2)}, u32[]{:S(2)}) collective-permute-start(bf16[1024,256]{1,0:T(8,128)(2,1)} %get-tuple-element.123), channel_id=1, source_target_pairs={{0,4},{1,5},{2,6},{3,7},{4,8},{5,9},{6,10},{7,11},{8,12},{9,13},{1... | collective-permute-start | bytes 1572872 | tf_op jit(solution)/shard_map/ppermute | solution.py:18
  6.7 96.5 %collective-permute-start.7 = (bf16[1024,256]{1,0:T(8,128)(2,1)}, bf16[1024,256]{1,0:T(8,128)(2,1)S(1)}, u32[]{:S(2)}, u32[]{:S(2)}) collective-permute-start(bf16[1024,256]{1,0:T(8,128)(2,1)} %get-tuple-element.123), channel_id=1, source_target_pairs={{0,12},{1,13},{2,14},{3,15},{4,0},{5,1},{6,2},{7,3},{8,4},{9,5},{1... | collective-permute-start | bytes 1572872 | tf_op jit(solution)/shard_map/ppermute | solution.py:18
  8.8 35.6 %collective-permute-start = (bf16[1024,256]{1,0:T(8,128)(2,1)}, bf16[1024,256]{1,0:T(8,128)(2,1)}, u32[]{:S(2)}, u32[]{:S(2)}) collective-permute-start(bf16[1024,256]{1,0:T(8,128)(2,1)} %get-tuple-element.122), channel_id=1, source_target_pairs={{0,4},{1,5},{2,6},{3,7},{4,8},{5,9},{6,10},{7,11},{8,12},{9,13},{1... | collective-permute-start | bytes 1572872 | tf_op jit(solution)/shard_map/ppermute | solution.py:18
  8.8 50.4 %collective-permute-start.1 = (bf16[1024,256]{1,0:T(8,128)(2,1)}, bf16[1024,256]{1,0:T(8,128)(2,1)}, u32[]{:S(2)}, u32[]{:S(2)}) collective-permute-start(bf16[1024,256]{1,0:T(8,128)(2,1)} %get-tuple-element.122), channel_id=1, source_target_pairs={{0,12},{1,13},{2,14},{3,15},{4,0},{5,1},{6,2},{7,3},{8,4},{9,5},{1... | collective-permute-start | bytes 1572872 | tf_op jit(solution)/shard_map/ppermute | solution.py:18
  12.6 54.3 %collective-permute-start.2 = (bf16[1024,256]{1,0:T(8,128)(2,1)}, bf16[1024,256]{1,0:T(8,128)(2,1)}, u32[]{:S(2)}, u32[]{:S(2)}) collective-permute-start(bf16[1024,256]{1,0:T(8,128)(2,1)} %get-tuple-element.121), channel_id=1, source_target_pairs={{0,4},{1,5},{2,6},{3,7},{4,8},{5,9},{6,10},{7,11},{8,12},{9,13},{1... | collective-permute-start | bytes 1572872 | tf_op jit(solution)/shard_map/ppermute | solution.py:18
  44.4 35.7 %collective-permute-start.3 = (bf16[1024,256]{1,0:T(8,128)(2,1)}, bf16[1024,256]{1,0:T(8,128)(2,1)S(1)}, u32[]{:S(2)}, u32[]{:S(2)}) collective-permute-start(bf16[1024,256]{1,0:T(8,128)(2,1)} %get-tuple-element.121), channel_id=1, source_target_pairs={{0,12},{1,13},{2,14},{3,15},{4,0},{5,1},{6,2},{7,3},{8,4},{9,5},{1... | collective-permute-start | bytes 1572872 | tf_op jit(solution)/shard_map/ppermute | solution.py:18
  59.1 30.2 %collective-permute-start.4 = (bf16[1024,256]{1,0:T(8,128)(2,1)S(1)}, bf16[1024,256]{1,0:T(8,128)(2,1)S(1)}, u32[]{:S(2)}, u32[]{:S(2)}) collective-permute-start(bf16[1024,256]{1,0:T(8,128)(2,1)S(1)} %copy-done.16), channel_id=1, source_target_pairs={{0,4},{1,5},{2,6},{3,7},{4,8},{5,9},{6,10},{7,11},{8,12},{9,13},{1... | collective-permute-start | bytes 1572872 | tf_op jit(solution)/shard_map/ppermute | solution.py:18
  66.9 32.1 %collective-permute-start.5 = (bf16[1024,256]{1,0:T(8,128)(2,1)S(1)}, bf16[1024,256]{1,0:T(8,128)(2,1)S(1)}, u32[]{:S(2)}, u32[]{:S(2)}) collective-permute-start(bf16[1024,256]{1,0:T(8,128)(2,1)S(1)} %copy-done.16), channel_id=1, source_target_pairs={{0,12},{1,13},{2,14},{3,15},{4,0},{5,1},{6,2},{7,3},{8,4},{9,5},{1... | collective-permute-start | bytes 1572872 | tf_op jit(solution)/shard_map/ppermute | solution.py:18
  114.4 11.4 %collective-permute-start.8 = (f32[229376]{0:T(1024)S(1)}, f32[229376]{0:T(1024)S(1)}, u32[]{:S(2)}, u32[]{:S(2)}) collective-permute-start(f32[229376]{0:T(1024)S(1)} %dynamic_slice.25), channel_id=1, source_target_pairs={{0,1},{1,0},{2,3},{3,2},{4,5},{5,4},{6,7},{7,6},{8,9},{9,8},{10,11... | collective-permute-start | bytes 2752520 | tf_op jit(solution)/shard_map/ppermute | solution.py:24
  114.5 23.6 %collective-permute-start.10 = (bf16[512,256]{1,0:T(8,128)(2,1)S(1)}, bf16[512,256]{1,0:T(8,128)(2,1)S(1)}, u32[]{:S(2)}, u32[]{:S(2)}) collective-permute-start(bf16[512,256]{1,0:T(8,128)(2,1)S(1)} %get-tuple-element.132), channel_id=1, source_target_pairs={{0,12},{1,13},{2,14},{3,15},{4,0},{5,1},{6,2},{7,3},{8,4},{9,5},{1... | collective-permute-start | bytes 786440 | tf_op jit(solution)/shard_map/ppermute | solution.py:18
  116.9 21.2 %collective-permute-start.11 = (bf16[512,256]{1,0:T(8,128)(2,1)S(1)}, bf16[512,256]{1,0:T(8,128)(2,1)S(1)}, u32[]{:S(2)}, u32[]{:S(2)}) collective-permute-start(bf16[512,256]{1,0:T(8,128)(2,1)S(1)} %get-tuple-element.130), channel_id=1, source_target_pairs={{0,4},{1,5},{2,6},{3,7},{4,8},{5,9},{6,10},{7,11},{8,12},{9,13},{1... | collective-permute-start | bytes 786440 | tf_op jit(solution)/shard_map/ppermute | solution.py:18
  117.0 21.1 %collective-permute-start.12 = (bf16[512,256]{1,0:T(8,128)(2,1)S(1)}, bf16[512,256]{1,0:T(8,128)(2,1)S(1)}, u32[]{:S(2)}, u32[]{:S(2)}) collective-permute-start(bf16[512,256]{1,0:T(8,128)(2,1)S(1)} %get-tuple-element.131), channel_id=1, source_target_pairs={{0,12},{1,13},{2,14},{3,15},{4,0},{5,1},{6,2},{7,3},{8,4},{9,5},{1... | collective-permute-start | bytes 786440 | tf_op jit(solution)/shard_map/ppermute | solution.py:18
  120.8 20.1 %collective-permute-start.13 = (bf16[512,256]{1,0:T(8,128)(2,1)S(1)}, bf16[512,256]{1,0:T(8,128)(2,1)S(1)}, u32[]{:S(2)}, u32[]{:S(2)}) collective-permute-start(bf16[512,256]{1,0:T(8,128)(2,1)S(1)} %get-tuple-element.129), channel_id=1, source_target_pairs={{0,4},{1,5},{2,6},{3,7},{4,8},{5,9},{6,10},{7,11},{8,12},{9,13},{1... | collective-permute-start | bytes 786440 | tf_op jit(solution)/shard_map/ppermute | solution.py:18
  125.9 12.1 %collective-permute-start.9 = (f32[114688]{0:T(1024)S(1)}, f32[114688]{0:T(1024)S(1)}, u32[]{:S(2)}, u32[]{:S(2)}) collective-permute-start(f32[114688]{0:T(1024)S(1)} %dynamic_slice.27), channel_id=1, source_target_pairs={{0,2},{1,3},{2,0},{3,1},{4,6},{5,7},{6,4},{7,5},{8,10},{9,11},{10,... | collective-permute-start | bytes 1376264 | tf_op jit(solution)/shard_map/ppermute | solution.py:24
  140.9 8.6 %collective-permute-start.14 = (f32[57344]{0:T(1024)S(1)}, f32[57344]{0:T(1024)S(1)}, u32[]{:S(2)}, u32[]{:S(2)}) collective-permute-start(f32[57344]{0:T(1024)S(1)} %dynamic_slice.29), channel_id=1, source_target_pairs={{0,4},{1,5},{2,6},{3,7},{4,0},{5,1},{6,2},{7,3},{8,12},{9,13},{10,... | collective-permute-start | bytes 688136 | tf_op jit(solution)/shard_map/ppermute | solution.py:24
  143.4 20.4 %collective-permute-start.16 = (bf16[512,256]{1,0:T(8,128)(2,1)}, bf16[512,256]{1,0:T(8,128)(2,1)}, u32[]{:S(2)}, u32[]{:S(2)}) collective-permute-start(bf16[512,256]{1,0:T(8,128)(2,1)} %slice.143), channel_id=1, source_target_pairs={{0,12},{1,13},{2,14},{3,15},{4,0},{5,1},{6,2},{7,3},{8,4},{9,5},{1... | collective-permute-start | bytes 786440 | tf_op jit(solution)/shard_map/ppermute | solution.py:18
  145.5 18.3 %collective-permute-start.17 = (bf16[512,256]{1,0:T(8,128)(2,1)}, bf16[512,256]{1,0:T(8,128)(2,1)}, u32[]{:S(2)}, u32[]{:S(2)}) collective-permute-start(bf16[512,256]{1,0:T(8,128)(2,1)} %slice.144), channel_id=1, source_target_pairs={{0,4},{1,5},{2,6},{3,7},{4,8},{5,9},{6,10},{7,11},{8,12},{9,13},{1... | collective-permute-start | bytes 786440 | tf_op jit(solution)/shard_map/ppermute | solution.py:18
  149.6 14.2 %collective-permute-start.15 = (f32[28672]{0:T(1024)S(1)}, f32[28672]{0:T(1024)S(1)}, u32[]{:S(2)}, u32[]{:S(2)}) collective-permute-start(f32[28672]{0:T(1024)S(1)} %dynamic_slice.31), channel_id=1, source_target_pairs={{0,8},{1,9},{2,10},{3,11},{4,12},{5,13},{6,14},{7,15},{8,0},{9,1},... | collective-permute-start | bytes 344072 | tf_op jit(solution)/shard_map/ppermute | solution.py:24
  152.8 27.4 %collective-permute-start.19 = (bf16[512,256]{1,0:T(8,128)(2,1)}, bf16[512,256]{1,0:T(8,128)(2,1)}, u32[]{:S(2)}, u32[]{:S(2)}) collective-permute-start(bf16[512,256]{1,0:T(8,128)(2,1)} %slice.145), channel_id=1, source_target_pairs={{0,12},{1,13},{2,14},{3,15},{4,0},{5,1},{6,2},{7,3},{8,4},{9,5},{1... | collective-permute-start | bytes 786440 | tf_op jit(solution)/shard_map/ppermute | solution.py:18
  155.9 24.4 %collective-permute-start.20 = (bf16[512,256]{1,0:T(8,128)(2,1)}, bf16[512,256]{1,0:T(8,128)(2,1)}, u32[]{:S(2)}, u32[]{:S(2)}) collective-permute-start(bf16[512,256]{1,0:T(8,128)(2,1)} %slice.146), channel_id=1, source_target_pairs={{0,4},{1,5},{2,6},{3,7},{4,8},{5,9},{6,10},{7,11},{8,12},{9,13},{1... | collective-permute-start | bytes 786440 | tf_op jit(solution)/shard_map/ppermute | solution.py:18
  163.8 16.4 %collective-permute-start.18 = (f32[56,512]{1,0:T(8,128)S(1)}, f32[56,512]{1,0:T(8,128)S(1)}, u32[]{:S(2)}, u32[]{:S(2)}) collective-permute-start(f32[56,512]{1,0:T(8,128)S(1)} %reshape.20), channel_id=1, source_target_pairs={{0,8},{1,9},{2,10},{3,11},{4,12},{5,13},{6,14},{7,15},{8,0},{9,1},... | collective-permute-start | bytes 344072 | tf_op jit(solution)/shard_map/ppermute | solution.py:24
  167.0 26.4 %collective-permute-start.22 = (bf16[512,256]{1,0:T(8,128)(2,1)S(1)}, bf16[512,256]{1,0:T(8,128)(2,1)S(1)}, u32[]{:S(2)}, u32[]{:S(2)}) collective-permute-start(bf16[512,256]{1,0:T(8,128)(2,1)S(1)} %slice.147), channel_id=1, source_target_pairs={{0,12},{1,13},{2,14},{3,15},{4,0},{5,1},{6,2},{7,3},{8,4},{9,5},{1... | collective-permute-start | bytes 786440 | tf_op jit(solution)/shard_map/ppermute | solution.py:18
  173.5 19.9 %collective-permute-start.23 = (bf16[512,256]{1,0:T(8,128)(2,1)S(1)}, bf16[512,256]{1,0:T(8,128)(2,1)S(1)}, u32[]{:S(2)}, u32[]{:S(2)}) collective-permute-start(bf16[512,256]{1,0:T(8,128)(2,1)S(1)} %slice.148), channel_id=1, source_target_pairs={{0,4},{1,5},{2,6},{3,7},{4,8},{5,9},{6,10},{7,11},{8,12},{9,13},{1... | collective-permute-start | bytes 786440 | tf_op jit(solution)/shard_map/ppermute | solution.py:18
  180.3 13.1 %collective-permute-start.21 = (f32[112,512]{1,0:T(8,128)S(1)}, f32[112,512]{1,0:T(8,128)S(1)}, u32[]{:S(2)}, u32[]{:S(2)}) collective-permute-start(f32[112,512]{1,0:T(8,128)S(1)} %pad_maximum_fusion.10), channel_id=1, source_target_pairs={{0,4},{1,5},{2,6},{3,7},{4,0},{5,1},{6,2},{7,3},{8,12},{9,13},{10,... | collective-permute-start | bytes 688136 | tf_op jit(solution)/shard_map/ppermute | solution.py:24
  186.8 18.3 %collective-permute-start.25 = (bf16[512,256]{1,0:T(8,128)(2,1)S(1)}, bf16[512,256]{1,0:T(8,128)(2,1)S(1)}, u32[]{:S(2)}, u32[]{:S(2)}) collective-permute-start(bf16[512,256]{1,0:T(8,128)(2,1)S(1)} %slice.149), channel_id=1, source_target_pairs={{0,12},{1,13},{2,14},{3,15},{4,0},{5,1},{6,2},{7,3},{8,4},{9,5},{1... | collective-permute-start | bytes 786440 | tf_op jit(solution)/shard_map/ppermute | solution.py:18
  189.7 19.5 %collective-permute-start.26 = (bf16[512,256]{1,0:T(8,128)(2,1)S(1)}, bf16[512,256]{1,0:T(8,128)(2,1)S(1)}, u32[]{:S(2)}, u32[]{:S(2)}) collective-permute-start(bf16[512,256]{1,0:T(8,128)(2,1)S(1)} %slice.150), channel_id=1, source_target_pairs={{0,4},{1,5},{2,6},{3,7},{4,8},{5,9},{6,10},{7,11},{8,12},{9,13},{1... | collective-permute-start | bytes 786440 | tf_op jit(solution)/shard_map/ppermute | solution.py:18
  193.4 15.5 %collective-permute-start.24 = (f32[224,512]{1,0:T(8,128)S(1)}, f32[224,512]{1,0:T(8,128)S(1)}, u32[]{:S(2)}, u32[]{:S(2)}) collective-permute-start(f32[224,512]{1,0:T(8,128)S(1)} %pad_maximum_fusion.9), channel_id=1, source_target_pairs={{0,2},{1,3},{2,0},{3,1},{4,6},{5,7},{6,4},{7,5},{8,10},{9,11},{10,... | collective-permute-start | bytes 1376264 | tf_op jit(solution)/shard_map/ppermute | solution.py:24
  196.1 17.8 %collective-permute-start.27 = (bf16[512,256]{1,0:T(8,128)(2,1)S(1)}, bf16[512,256]{1,0:T(8,128)(2,1)S(1)}, u32[]{:S(2)}, u32[]{:S(2)}) collective-permute-start(bf16[512,256]{1,0:T(8,128)(2,1)S(1)} %get-tuple-element.120), channel_id=1, source_target_pairs={{0,12},{1,13},{2,14},{3,15},{4,0},{5,1},{6,2},{7,3},{8,4},{9,5},{1... | collective-permute-start | bytes 786440 | tf_op jit(solution)/shard_map/ppermute | solution.py:18
  204.9 12.8 %collective-permute-start.28 = (bf16[512,256]{1,0:T(8,128)(2,1)S(1)}, bf16[512,256]{1,0:T(8,128)(2,1)S(1)}, u32[]{:S(2)}, u32[]{:S(2)}) collective-permute-start(bf16[512,256]{1,0:T(8,128)(2,1)S(1)} %get-tuple-element.118), channel_id=1, source_target_pairs={{0,4},{1,5},{2,6},{3,7},{4,8},{5,9},{6,10},{7,11},{8,12},{9,13},{1... | collective-permute-start | bytes 786440 | tf_op jit(solution)/shard_map/ppermute | solution.py:18
  205.1 17.0 %collective-permute-start.29 = (bf16[512,256]{1,0:T(8,128)(2,1)S(1)}, bf16[512,256]{1,0:T(8,128)(2,1)S(1)}, u32[]{:S(2)}, u32[]{:S(2)}) collective-permute-start(bf16[512,256]{1,0:T(8,128)(2,1)S(1)} %get-tuple-element.119), channel_id=1, source_target_pairs={{0,12},{1,13},{2,14},{3,15},{4,0},{5,1},{6,2},{7,3},{8,4},{9,5},{1... | collective-permute-start | bytes 786440 | tf_op jit(solution)/shard_map/ppermute | solution.py:18
  208.9 17.4 %collective-permute-start.30 = (bf16[512,256]{1,0:T(8,128)(2,1)S(1)}, bf16[512,256]{1,0:T(8,128)(2,1)S(1)}, u32[]{:S(2)}, u32[]{:S(2)}) collective-permute-start(bf16[512,256]{1,0:T(8,128)(2,1)S(1)} %get-tuple-element.117), channel_id=1, source_target_pairs={{0,4},{1,5},{2,6},{3,7},{4,8},{5,9},{6,10},{7,11},{8,12},{9,13},{1... | collective-permute-start | bytes 786440 | tf_op jit(solution)/shard_map/ppermute | solution.py:18
  226.3 2.5 %collective-permute-start.31 = (f32[448,512]{1,0:T(8,128)S(1)}, f32[448,512]{1,0:T(8,128)S(1)}, u32[]{:S(2)}, u32[]{:S(2)}) collective-permute-start(f32[448,512]{1,0:T(8,128)S(1)} %pad_maximum_fusion.8), channel_id=1, source_target_pairs={{0,1},{1,0},{2,3},{3,2},{4,5},{5,4},{6,7},{7,6},{8,9},{9,8},{10,11... | collective-permute-start | bytes 2752520 | tf_op jit(solution)/shard_map/ppermute | solution.py:24
  (17 other events, 297.0 us)

commit v15 on v14

--- a/solution.py
+++ b/solution.py
@@ -6,7 +6,7 @@
 from jax.sharding import PartitionSpec as P
 
 TAP_SPACING = 16384
-CHUNK_EIGHTHS = (2, 2, 2, 2)
+CHUNK_SIXTEENTHS = (4, 4, 4, 2, 1, 1)
 EARLY = 1
 RIDER_ROWS = 512
 RIDER_SPAN = 2
@@ -84,9 +84,9 @@
     seq_size = lax.axis_size("seq")
     spacing = TAP_SPACING // positions
     bounds = [0]
-    for eighths in CHUNK_EIGHTHS:
-        bounds.append(bounds[-1] + positions * eighths // 8)
-    chunks = len(CHUNK_EIGHTHS)
+    for sixteenths in CHUNK_SIXTEENTHS:
+        bounds.append(bounds[-1] + positions * sixteenths // 16)
+    chunks = len(CHUNK_SIXTEENTHS)
     wconv_total = None
     wout_total = None
     lows, mids, highs = [], [], []

time: 232 us -> 225 us (0.970)
  waiting for transfers between devices: 83.8 us -> 53.2 us
  starting transfers between devices: 83 us -> 105 us
    ppermute x24 -> x28, waiting for transfers between devices: 60.2 us -> 28.2 us  [from_behind(): return lax.ppermute(value, axis, pairs)]
    ppermute x24 -> x28, starting transfers between devices: 68.7 us -> 90.9 us  [from_behind(): return lax.ppermute(value, axis, pairs)]
    unnamed x50 -> x48, local copies, waits for them, and re-layouts: 9.71 us -> 4.99 us
    slice x5, local copies, waits for them, and re-layouts: 1.53 us -> 4.44 us  [send_rows(): low_high[1][start:stop]]
    dot_general x4 -> x6, matrix products: 4.96 us -> 2.36 us  [chunk_layer(): lax.dot_general(grad_pre, w_mid, last_dims, preferred_element_type=jnp.fl...]
    slice x1 -> x3, local copies, waits for them, and re-layouts: 3.03 us -> 5.12 us  [body(): middle = activations[bounds[k]:bounds[k + 1]]]
    dot_general x4 -> x6, matrix products: 4.44 us -> 6.34 us  [chunk_layer(): preact = preact + jnp.dot(middle, w_mid, preferred_element_type=jnp.float32)]
    dot_general x4 -> x6, matrix products: 5.05 us -> 5.34 us  [chunk_layer(): preact = jnp.dot(left_tap_input, w_low, preferred_element_type=jnp.float32)]
  transfers between devices with their start and end apart: 32 -> 36, of which waited for: 15 -> 13; matrix products, arithmetic and copies ran while one was open for 20% -> 24% of each run, Pallas kernels for 0% -> 0%
where the time goes in v15:
time: 225 us
  starting transfers between devices  105 us (47%)
  waiting for transfers between devices  53.2 us (24%)
  matrix products  38.6 us (17%)
  local copies, waits for them, and re-layouts  20 us (9%)
  other arithmetic  6.23 us (3%)
    ppermute x28, starting transfers between devices, from_behind(): return lax.ppermute(value, axis, pairs)  90.9 us
    ppermute x28, waiting for transfers between devices, from_behind(): return lax.ppermute(value, axis, pairs)  28.2 us
    ppermute x8, waiting for transfers between devices, exchange(): return lax.ppermute(value, axis, pairs)  25 us
    ppermute x8, starting transfers between devices, exchange(): return lax.ppermute(value, axis, pairs)  13.9 us
    dot_general x6, matrix products, chunk_layer(): preact = preact + jnp.dot(middle, w_mid, preferred_element_type=jnp.float32)  6.34 us
    dot_general x6, matrix products, chunk_layer(): preact = jnp.dot(left_tap_input, w_low, preferred_element_type=jnp.float32)  5.34 us
    dot_general x6, matrix products, chunk_layer(): lax.dot_general(left_tap_input, grad_pre, first_dims, preferred_element_t...  5.34 us
    slice x3, local copies, waits for them, and re-layouts, body(): middle = activations[bounds[k]:bounds[k + 1]]  5.12 us
  transfers between devices with their start and end apart: 36, of which 13 were waited for; matrix products, arithmetic and copies ran while one was open for 24% of the time, Pallas kernels for 0%

profile of v15, /device:TPU:0, one launch (start us, length us, event | category | flops | bytes accessed | tf_op | source)
XLA Modules:
  0.0 224.6 jit_solution(12422786812741520008)
XLA Ops:
  0.7 1.9 fusion.142
  2.5 3.0 %collective-permute-start.10 = (bf16[256,256]{1,0:T(8,128)(2,1)}, bf16[256,256]{1,0:T(8,128)(2,1)}, u32[]{:S(2)}, u32[]{:S(2)}) collective-permute-start(bf16[256,256]{1,0:T(8,128)(2,1)} %get-tuple-element.139), channel_id=1, source_target_pairs={{0,4},{1,5},{2,6},{3,7},{4,8},{5,9},{6,10},{7,11},{8,12},{9,13},{1... | collective-permute-start | bytes 393224 | tf_op jit(solution)/shard_map/ppermute | solution.py:18
  5.5 2.0 collective-permute-start.11
  7.6 2.6 %fusion.141 = (bf16[1024,256]{1,0:T(8,128)(2,1)}, bf16[1024,256]{1,0:T(8,128)(2,1)}, bf16[1024,256]{1,0:T(8,128)(2,1)}) fusion(bf16[4096,256]{1,0:T(8,128)(2,1)} %param.4), kind=kLoop, calls=%fused_computation.242 | loop fusion | bytes 3145728 | tf_op jit(solution)/shard_map/slice | solution.py:95
  10.1 3.8 %collective-permute-start.1 = (bf16[1024,256]{1,0:T(8,128)(2,1)}, bf16[1024,256]{1,0:T(8,128)(2,1)S(1)}, u32[]{:S(2)}, u32[]{:S(2)}) collective-permute-start(bf16[1024,256]{1,0:T(8,128)(2,1)} %get-tuple-element.137), channel_id=1, source_target_pairs={{0,12},{1,13},{2,14},{3,15},{4,0},{5,1},{6,2},{7,3},{8,4},{9,5},{1... | collective-permute-start | bytes 1572872 | tf_op jit(solution)/shard_map/ppermute | solution.py:18
  20.8 6.3 %collective-permute-done = bf16[1024,256]{1,0:T(8,128)(2,1)} collective-permute-done((bf16[1024,256]{1,0:T(8,128)(2,1)}, bf16[1024,256]{1,0:T(8,128)(2,1)}, u32[]{:S(2)}, u32[]{:S(2)}) %collective-permute-start) | collective-permute-done | bytes 524320 | tf_op jit(solution)/shard_map/ppermute | solution.py:18
  27.1 11.4 %collective-permute-start.3 = (bf16[1024,256]{1,0:T(8,128)(2,1)}, bf16[1024,256]{1,0:T(8,128)(2,1)S(1)}, u32[]{:S(2)}, u32[]{:S(2)}) collective-permute-start(bf16[1024,256]{1,0:T(8,128)(2,1)} %get-tuple-element.135), channel_id=1, source_target_pairs={{0,12},{1,13},{2,14},{3,15},{4,0},{5,1},{6,2},{7,3},{8,4},{9,5},{1... | collective-permute-start | bytes 1572872 | tf_op jit(solution)/shard_map/ppermute | solution.py:18
  40.0 7.4 %collective-permute-start.4 = (bf16[1024,256]{1,0:T(8,128)(2,1)S(1)}, bf16[1024,256]{1,0:T(8,128)(2,1)S(1)}, u32[]{:S(2)}, u32[]{:S(2)}) collective-permute-start(bf16[1024,256]{1,0:T(8,128)(2,1)S(1)} %copy-done.13), channel_id=1, source_target_pairs={{0,4},{1,5},{2,6},{3,7},{4,8},{5,9},{6,10},{7,11},{8,12},{9,13},{1... | collective-permute-start | bytes 1572872 | tf_op jit(solution)/shard_map/ppermute | solution.py:18
  51.9 9.0 %collective-permute-start.5 = (bf16[1024,256]{1,0:T(8,128)(2,1)S(1)}, bf16[1024,256]{1,0:T(8,128)(2,1)S(1)}, u32[]{:S(2)}, u32[]{:S(2)}) collective-permute-start(bf16[1024,256]{1,0:T(8,128)(2,1)S(1)} %copy-done.13), channel_id=1, source_target_pairs={{0,12},{1,13},{2,14},{3,15},{4,0},{5,1},{6,2},{7,3},{8,4},{9,5},{1... | collective-permute-start | bytes 1572872 | tf_op jit(solution)/shard_map/ppermute | solution.py:18
  67.6 4.4 %collective-permute-done.4 = bf16[1024,256]{1,0:T(8,128)(2,1)S(1)} collective-permute-done((bf16[1024,256]{1,0:T(8,128)(2,1)S(1)}, bf16[1024,256]{1,0:T(8,128)(2,1)S(1)}, u32[]{:S(2)}, u32[]{:S(2)}) %collective-permute-start.4) | collective-permute-done | bytes 524320 | tf_op jit(solution)/shard_map/ppermute | solution.py:18
  72.0 11.2 %collective-permute-start.7 = (bf16[512,256]{1,0:T(8,128)(2,1)S(1)}, bf16[512,256]{1,0:T(8,128)(2,1)S(1)}, u32[]{:S(2)}, u32[]{:S(2)}) collective-permute-start(bf16[512,256]{1,0:T(8,128)(2,1)S(1)} %copy-done.14), channel_id=1, source_target_pairs={{0,12},{1,13},{2,14},{3,15},{4,0},{5,1},{6,2},{7,3},{8,4},{9,5},{1... | collective-permute-start | bytes 786440 | tf_op jit(solution)/shard_map/ppermute | solution.py:18
  83.2 3.6 %collective-permute-start.8 = (bf16[256,256]{1,0:T(8,128)(2,1)S(1)}, bf16[256,256]{1,0:T(8,128)(2,1)S(1)}, u32[]{:S(2)}, u32[]{:S(2)}) collective-permute-start(bf16[256,256]{1,0:T(8,128)(2,1)S(1)} %copy-done.15), channel_id=1, source_target_pairs={{0,4},{1,5},{2,6},{3,7},{4,8},{5,9},{6,10},{7,11},{8,12},{9,13},{1... | collective-permute-start | bytes 393224 | tf_op jit(solution)/shard_map/ppermute | solution.py:18
  91.4 3.0 %collective-permute-start.9 = (bf16[256,256]{1,0:T(8,128)(2,1)S(1)}, bf16[256,256]{1,0:T(8,128)(2,1)S(1)}, u32[]{:S(2)}, u32[]{:S(2)}) collective-permute-start(bf16[256,256]{1,0:T(8,128)(2,1)S(1)} %copy-done.15), channel_id=1, source_target_pairs={{0,12},{1,13},{2,14},{3,15},{4,0},{5,1},{6,2},{7,3},{8,4},{9,5},{1... | collective-permute-start | bytes 393224 | tf_op jit(solution)/shard_map/ppermute | solution.py:18
  107.8 3.4 %collective-permute-start.14 = (bf16[512,256]{1,0:T(8,128)(2,1)S(1)}, bf16[512,256]{1,0:T(8,128)(2,1)S(1)}, u32[]{:S(2)}, u32[]{:S(2)}) collective-permute-start(bf16[512,256]{1,0:T(8,128)(2,1)S(1)} %get-tuple-element.153), channel_id=1, source_target_pairs={{0,12},{1,13},{2,14},{3,15},{4,0},{5,1},{6,2},{7,3},{8,4},{9,5},{1... | collective-permute-start | bytes 786440 | tf_op jit(solution)/shard_map/ppermute | solution.py:18
  111.2 3.8 %collective-permute-start.16 = (bf16[512,256]{1,0:T(8,128)(2,1)S(1)}, bf16[512,256]{1,0:T(8,128)(2,1)S(1)}, u32[]{:S(2)}, u32[]{:S(2)}) collective-permute-start(bf16[512,256]{1,0:T(8,128)(2,1)S(1)} %get-tuple-element.152), channel_id=1, source_target_pairs={{0,12},{1,13},{2,14},{3,15},{4,0},{5,1},{6,2},{7,3},{8,4},{9,5},{1... | collective-permute-start | bytes 786440 | tf_op jit(solution)/shard_map/ppermute | solution.py:18
  122.5 10.0 %collective-permute-done.13 = f32[114688]{0:T(1024)S(1)} collective-permute-done((f32[114688]{0:T(1024)S(1)}, f32[114688]{0:T(1024)S(1)}, u32[]{:S(2)}, u32[]{:S(2)}) %collective-permute-start.13) | collective-permute-done | bytes 458784 | tf_op jit(solution)/shard_map/ppermute | solution.py:24
  132.6 2.4 %collective-permute-done.17 = bf16[512,256]{1,0:T(8,128)(2,1)S(1)} collective-permute-done((bf16[512,256]{1,0:T(8,128)(2,1)S(1)}, bf16[512,256]{1,0:T(8,128)(2,1)S(1)}, u32[]{:S(2)}, u32[]{:S(2)}) %collective-permute-start.17) | collective-permute-done | bytes 262176 | tf_op jit(solution)/shard_map/ppermute | solution.py:18
  141.1 2.5 %collective-permute-done.18 = f32[57344]{0:T(1024)S(1)} collective-permute-done((f32[57344]{0:T(1024)S(1)}, f32[57344]{0:T(1024)S(1)}, u32[]{:S(2)}, u32[]{:S(2)}) %collective-permute-start.18) | collective-permute-done | bytes 229408 | tf_op jit(solution)/shard_map/ppermute | solution.py:24
  145.9 3.4 %collective-permute-start.23 = (bf16[512,256]{1,0:T(8,128)(2,1)}, bf16[512,256]{1,0:T(8,128)(2,1)S(1)}, u32[]{:S(2)}, u32[]{:S(2)}) collective-permute-start(bf16[512,256]{1,0:T(8,128)(2,1)} %slice.183), channel_id=1, source_target_pairs={{0,12},{1,13},{2,14},{3,15},{4,0},{5,1},{6,2},{7,3},{8,4},{9,5},{1... | collective-permute-start | bytes 786440 | tf_op jit(solution)/shard_map/ppermute | solution.py:18
  150.0 7.9 %collective-permute-done.19 = f32[28672]{0:T(1024)S(1)} collective-permute-done((f32[28672]{0:T(1024)S(1)}, f32[28672]{0:T(1024)S(1)}, u32[]{:S(2)}, u32[]{:S(2)}) %collective-permute-start.19) | collective-permute-done | bytes 114720 | tf_op jit(solution)/shard_map/ppermute | solution.py:24
  158.0 2.3 %collective-permute-start.22 = (f32[56,512]{1,0:T(8,128)S(1)}, f32[56,512]{1,0:T(8,128)S(1)}, u32[]{:S(2)}, u32[]{:S(2)}) collective-permute-start(f32[56,512]{1,0:T(8,128)S(1)} %reshape.20), channel_id=1, source_target_pairs={{0,8},{1,9},{2,10},{3,11},{4,12},{5,13},{6,14},{7,15},{8,0},{9,1},... | collective-permute-start | bytes 344072 | tf_op jit(solution)/shard_map/ppermute | solution.py:24
  161.2 6.3 %collective-permute-start.26 = (bf16[512,256]{1,0:T(8,128)(2,1)S(1)}, bf16[512,256]{1,0:T(8,128)(2,1)S(1)}, u32[]{:S(2)}, u32[]{:S(2)}) collective-permute-start(bf16[512,256]{1,0:T(8,128)(2,1)S(1)} %slice.185), channel_id=1, source_target_pairs={{0,12},{1,13},{2,14},{3,15},{4,0},{5,1},{6,2},{7,3},{8,4},{9,5},{1... | collective-permute-start | bytes 786440 | tf_op jit(solution)/shard_map/ppermute | solution.py:18
  170.8 3.3 %collective-permute-done.22 = f32[56,512]{1,0:T(8,128)S(1)} collective-permute-done((f32[56,512]{1,0:T(8,128)S(1)}, f32[56,512]{1,0:T(8,128)S(1)}, u32[]{:S(2)}, u32[]{:S(2)}) %collective-permute-start.22) | collective-permute-done | bytes 114720 | tf_op jit(solution)/shard_map/ppermute | solution.py:24
  174.1 5.8 %collective-permute-start.25 = (f32[112,512]{1,0:T(8,128)S(1)}, f32[112,512]{1,0:T(8,128)S(1)}, u32[]{:S(2)}, u32[]{:S(2)}) collective-permute-start(f32[112,512]{1,0:T(8,128)S(1)} %pad_maximum_fusion.10), channel_id=1, source_target_pairs={{0,4},{1,5},{2,6},{3,7},{4,0},{5,1},{6,2},{7,3},{8,12},{9,13},{10,... | collective-permute-start | bytes 688136 | tf_op jit(solution)/shard_map/ppermute | solution.py:24
  180.9 2.9 %collective-permute-start.29 = (bf16[512,256]{1,0:T(8,128)(2,1)S(1)}, bf16[512,256]{1,0:T(8,128)(2,1)S(1)}, u32[]{:S(2)}, u32[]{:S(2)}) collective-permute-start(bf16[512,256]{1,0:T(8,128)(2,1)S(1)} %slice.187), channel_id=1, source_target_pairs={{0,12},{1,13},{2,14},{3,15},{4,0},{5,1},{6,2},{7,3},{8,4},{9,5},{1... | collective-permute-start | bytes 786440 | tf_op jit(solution)/shard_map/ppermute | solution.py:18
  189.8 9.7 %collective-permute-start.31 = (bf16[512,256]{1,0:T(8,128)(2,1)S(1)}, bf16[512,256]{1,0:T(8,128)(2,1)S(1)}, u32[]{:S(2)}, u32[]{:S(2)}) collective-permute-start(bf16[512,256]{1,0:T(8,128)(2,1)S(1)} %get-tuple-element.134), channel_id=1, source_target_pairs={{0,12},{1,13},{2,14},{3,15},{4,0},{5,1},{6,2},{7,3},{8,4},{9,5},{1... | collective-permute-start | bytes 786440 | tf_op jit(solution)/shard_map/ppermute | solution.py:18
  200.7 3.9 %collective-permute-start.33 = (bf16[512,256]{1,0:T(8,128)(2,1)S(1)}, bf16[512,256]{1,0:T(8,128)(2,1)S(1)}, u32[]{:S(2)}, u32[]{:S(2)}) collective-permute-start(bf16[512,256]{1,0:T(8,128)(2,1)S(1)} %get-tuple-element.133), channel_id=1, source_target_pairs={{0,12},{1,13},{2,14},{3,15},{4,0},{5,1},{6,2},{7,3},{8,4},{9,5},{1... | collective-permute-start | bytes 786440 | tf_op jit(solution)/shard_map/ppermute | solution.py:18
  204.8 2.0 collective-permute-done.31
  206.8 5.8 %collective-permute-done.32 = bf16[512,256]{1,0:T(8,128)(2,1)S(1)} collective-permute-done((bf16[512,256]{1,0:T(8,128)(2,1)S(1)}, bf16[512,256]{1,0:T(8,128)(2,1)S(1)}, u32[]{:S(2)}, u32[]{:S(2)}) %collective-permute-start.32) | collective-permute-done | bytes 262176 | tf_op jit(solution)/shard_map/ppermute | solution.py:18
  212.5 4.4 %collective-permute-done.33 = bf16[512,256]{1,0:T(8,128)(2,1)S(1)} collective-permute-done((bf16[512,256]{1,0:T(8,128)(2,1)S(1)}, bf16[512,256]{1,0:T(8,128)(2,1)S(1)}, u32[]{:S(2)}, u32[]{:S(2)}) %collective-permute-start.33) | collective-permute-done | bytes 262176 | tf_op jit(solution)/shard_map/ppermute | solution.py:18
  216.9 2.9 %collective-permute-done.34 = bf16[512,256]{1,0:T(8,128)(2,1)S(1)} collective-permute-done((bf16[512,256]{1,0:T(8,128)(2,1)S(1)}, bf16[512,256]{1,0:T(8,128)(2,1)S(1)}, u32[]{:S(2)}, u32[]{:S(2)}) %collective-permute-start.34) | collective-permute-done | bytes 262176 | tf_op jit(solution)/shard_map/ppermute | solution.py:18
  220.0 2.2 add_convert_fusion
  (202 shorter events, 68.8 us)
Async XLA Ops:
  2.5 97.2 %collective-permute-start.10 = (bf16[256,256]{1,0:T(8,128)(2,1)}, bf16[256,256]{1,0:T(8,128)(2,1)}, u32[]{:S(2)}, u32[]{:S(2)}) collective-permute-start(bf16[256,256]{1,0:T(8,128)(2,1)} %get-tuple-element.139), channel_id=1, source_target_pairs={{0,4},{1,5},{2,6},{3,7},{4,8},{5,9},{6,10},{7,11},{8,12},{9,13},{1... | collective-permute-start | bytes 393224 | tf_op jit(solution)/shard_map/ppermute | solution.py:18
  5.5 94.2 %collective-permute-start.11 = (bf16[256,256]{1,0:T(8,128)(2,1)}, bf16[256,256]{1,0:T(8,128)(2,1)}, u32[]{:S(2)}, u32[]{:S(2)}) collective-permute-start(bf16[256,256]{1,0:T(8,128)(2,1)} %get-tuple-element.139), channel_id=1, source_target_pairs={{0,12},{1,13},{2,14},{3,15},{4,0},{5,1},{6,2},{7,3},{8,4},{9,5},{1... | collective-permute-start | bytes 393224 | tf_op jit(solution)/shard_map/ppermute | solution.py:18
  10.1 17.0 %collective-permute-start = (bf16[1024,256]{1,0:T(8,128)(2,1)}, bf16[1024,256]{1,0:T(8,128)(2,1)}, u32[]{:S(2)}, u32[]{:S(2)}) collective-permute-start(bf16[1024,256]{1,0:T(8,128)(2,1)} %get-tuple-element.137), channel_id=1, source_target_pairs={{0,4},{1,5},{2,6},{3,7},{4,8},{5,9},{6,10},{7,11},{8,12},{9,13},{1... | collective-permute-start | bytes 1572872 | tf_op jit(solution)/shard_map/ppermute | solution.py:18
  10.1 29.8 %collective-permute-start.1 = (bf16[1024,256]{1,0:T(8,128)(2,1)}, bf16[1024,256]{1,0:T(8,128)(2,1)S(1)}, u32[]{:S(2)}, u32[]{:S(2)}) collective-permute-start(bf16[1024,256]{1,0:T(8,128)(2,1)} %get-tuple-element.137), channel_id=1, source_target_pairs={{0,12},{1,13},{2,14},{3,15},{4,0},{5,1},{6,2},{7,3},{8,4},{9,5},{1... | collective-permute-start | bytes 1572872 | tf_op jit(solution)/shard_map/ppermute | solution.py:18
  14.0 37.9 %collective-permute-start.2 = (bf16[1024,256]{1,0:T(8,128)(2,1)}, bf16[1024,256]{1,0:T(8,128)(2,1)}, u32[]{:S(2)}, u32[]{:S(2)}) collective-permute-start(bf16[1024,256]{1,0:T(8,128)(2,1)} %get-tuple-element.135), channel_id=1, source_target_pairs={{0,4},{1,5},{2,6},{3,7},{4,8},{5,9},{6,10},{7,11},{8,12},{9,13},{1... | collective-permute-start | bytes 1572872 | tf_op jit(solution)/shard_map/ppermute | solution.py:18
  27.1 33.8 %collective-permute-start.3 = (bf16[1024,256]{1,0:T(8,128)(2,1)}, bf16[1024,256]{1,0:T(8,128)(2,1)S(1)}, u32[]{:S(2)}, u32[]{:S(2)}) collective-permute-start(bf16[1024,256]{1,0:T(8,128)(2,1)} %get-tuple-element.135), channel_id=1, source_target_pairs={{0,12},{1,13},{2,14},{3,15},{4,0},{5,1},{6,2},{7,3},{8,4},{9,5},{1... | collective-permute-start | bytes 1572872 | tf_op jit(solution)/shard_map/ppermute | solution.py:18
  40.0 32.0 %collective-permute-start.4 = (bf16[1024,256]{1,0:T(8,128)(2,1)S(1)}, bf16[1024,256]{1,0:T(8,128)(2,1)S(1)}, u32[]{:S(2)}, u32[]{:S(2)}) collective-permute-start(bf16[1024,256]{1,0:T(8,128)(2,1)S(1)} %copy-done.13), channel_id=1, source_target_pairs={{0,4},{1,5},{2,6},{3,7},{4,8},{5,9},{6,10},{7,11},{8,12},{9,13},{1... | collective-permute-start | bytes 1572872 | tf_op jit(solution)/shard_map/ppermute | solution.py:18
  51.9 31.3 %collective-permute-start.5 = (bf16[1024,256]{1,0:T(8,128)(2,1)S(1)}, bf16[1024,256]{1,0:T(8,128)(2,1)S(1)}, u32[]{:S(2)}, u32[]{:S(2)}) collective-permute-start(bf16[1024,256]{1,0:T(8,128)(2,1)S(1)} %copy-done.13), channel_id=1, source_target_pairs={{0,12},{1,13},{2,14},{3,15},{4,0},{5,1},{6,2},{7,3},{8,4},{9,5},{1... | collective-permute-start | bytes 1572872 | tf_op jit(solution)/shard_map/ppermute | solution.py:18
  60.9 30.5 %collective-permute-start.6 = (bf16[512,256]{1,0:T(8,128)(2,1)S(1)}, bf16[512,256]{1,0:T(8,128)(2,1)S(1)}, u32[]{:S(2)}, u32[]{:S(2)}) collective-permute-start(bf16[512,256]{1,0:T(8,128)(2,1)S(1)} %copy-done.14), channel_id=1, source_target_pairs={{0,4},{1,5},{2,6},{3,7},{4,8},{5,9},{6,10},{7,11},{8,12},{9,13},{1... | collective-permute-start | bytes 786440 | tf_op jit(solution)/shard_map/ppermute | solution.py:18
  72.0 22.4 %collective-permute-start.7 = (bf16[512,256]{1,0:T(8,128)(2,1)S(1)}, bf16[512,256]{1,0:T(8,128)(2,1)S(1)}, u32[]{:S(2)}, u32[]{:S(2)}) collective-permute-start(bf16[512,256]{1,0:T(8,128)(2,1)S(1)} %copy-done.14), channel_id=1, source_target_pairs={{0,12},{1,13},{2,14},{3,15},{4,0},{5,1},{6,2},{7,3},{8,4},{9,5},{1... | collective-permute-start | bytes 786440 | tf_op jit(solution)/shard_map/ppermute | solution.py:18
  83.2 14.6 %collective-permute-start.8 = (bf16[256,256]{1,0:T(8,128)(2,1)S(1)}, bf16[256,256]{1,0:T(8,128)(2,1)S(1)}, u32[]{:S(2)}, u32[]{:S(2)}) collective-permute-start(bf16[256,256]{1,0:T(8,128)(2,1)S(1)} %copy-done.15), channel_id=1, source_target_pairs={{0,4},{1,5},{2,6},{3,7},{4,8},{5,9},{6,10},{7,11},{8,12},{9,13},{1... | collective-permute-start | bytes 393224 | tf_op jit(solution)/shard_map/ppermute | solution.py:18
  107.6 12.6 %collective-permute-start.12 = (f32[229376]{0:T(1024)S(1)}, f32[229376]{0:T(1024)S(1)}, u32[]{:S(2)}, u32[]{:S(2)}) collective-permute-start(f32[229376]{0:T(1024)S(1)} %dynamic_slice.25), channel_id=1, source_target_pairs={{0,1},{1,0},{2,3},{3,2},{4,5},{5,4},{6,7},{7,6},{8,9},{9,8},{10,11... | collective-permute-start | bytes 2752520 | tf_op jit(solution)/shard_map/ppermute | solution.py:24
  107.8 24.8 %collective-permute-start.14 = (bf16[512,256]{1,0:T(8,128)(2,1)S(1)}, bf16[512,256]{1,0:T(8,128)(2,1)S(1)}, u32[]{:S(2)}, u32[]{:S(2)}) collective-permute-start(bf16[512,256]{1,0:T(8,128)(2,1)S(1)} %get-tuple-element.153), channel_id=1, source_target_pairs={{0,12},{1,13},{2,14},{3,15},{4,0},{5,1},{6,2},{7,3},{8,4},{9,5},{1... | collective-permute-start | bytes 786440 | tf_op jit(solution)/shard_map/ppermute | solution.py:18
  111.2 21.4 %collective-permute-start.15 = (bf16[512,256]{1,0:T(8,128)(2,1)S(1)}, bf16[512,256]{1,0:T(8,128)(2,1)S(1)}, u32[]{:S(2)}, u32[]{:S(2)}) collective-permute-start(bf16[512,256]{1,0:T(8,128)(2,1)S(1)} %get-tuple-element.151), channel_id=1, source_target_pairs={{0,4},{1,5},{2,6},{3,7},{4,8},{5,9},{6,10},{7,11},{8,12},{9,13},{1... | collective-permute-start | bytes 786440 | tf_op jit(solution)/shard_map/ppermute | solution.py:18
  111.2 21.3 %collective-permute-start.16 = (bf16[512,256]{1,0:T(8,128)(2,1)S(1)}, bf16[512,256]{1,0:T(8,128)(2,1)S(1)}, u32[]{:S(2)}, u32[]{:S(2)}) collective-permute-start(bf16[512,256]{1,0:T(8,128)(2,1)S(1)} %get-tuple-element.152), channel_id=1, source_target_pairs={{0,12},{1,13},{2,14},{3,15},{4,0},{5,1},{6,2},{7,3},{8,4},{9,5},{1... | collective-permute-start | bytes 786440 | tf_op jit(solution)/shard_map/ppermute | solution.py:18
  115.0 19.9 %collective-permute-start.17 = (bf16[512,256]{1,0:T(8,128)(2,1)S(1)}, bf16[512,256]{1,0:T(8,128)(2,1)S(1)}, u32[]{:S(2)}, u32[]{:S(2)}) collective-permute-start(bf16[512,256]{1,0:T(8,128)(2,1)S(1)} %get-tuple-element.150), channel_id=1, source_target_pairs={{0,4},{1,5},{2,6},{3,7},{4,8},{5,9},{6,10},{7,11},{8,12},{9,13},{1... | collective-permute-start | bytes 786440 | tf_op jit(solution)/shard_map/ppermute | solution.py:18
  120.4 12.1 %collective-permute-start.13 = (f32[114688]{0:T(1024)S(1)}, f32[114688]{0:T(1024)S(1)}, u32[]{:S(2)}, u32[]{:S(2)}) collective-permute-start(f32[114688]{0:T(1024)S(1)} %dynamic_slice.27), channel_id=1, source_target_pairs={{0,2},{1,3},{2,0},{3,1},{4,6},{5,7},{6,4},{7,5},{8,10},{9,11},{10,... | collective-permute-start | bytes 1376264 | tf_op jit(solution)/shard_map/ppermute | solution.py:24
  137.6 20.4 %collective-permute-start.20 = (bf16[512,256]{1,0:T(8,128)(2,1)}, bf16[512,256]{1,0:T(8,128)(2,1)S(1)}, u32[]{:S(2)}, u32[]{:S(2)}) collective-permute-start(bf16[512,256]{1,0:T(8,128)(2,1)} %slice.181), channel_id=1, source_target_pairs={{0,12},{1,13},{2,14},{3,15},{4,0},{5,1},{6,2},{7,3},{8,4},{9,5},{1... | collective-permute-start | bytes 786440 | tf_op jit(solution)/shard_map/ppermute | solution.py:18
  138.7 19.3 %collective-permute-start.21 = (bf16[512,256]{1,0:T(8,128)(2,1)}, bf16[512,256]{1,0:T(8,128)(2,1)}, u32[]{:S(2)}, u32[]{:S(2)}) collective-permute-start(bf16[512,256]{1,0:T(8,128)(2,1)} %slice.182), channel_id=1, source_target_pairs={{0,4},{1,5},{2,6},{3,7},{4,8},{5,9},{6,10},{7,11},{8,12},{9,13},{1... | collective-permute-start | bytes 786440 | tf_op jit(solution)/shard_map/ppermute | solution.py:18
  143.6 14.3 %collective-permute-start.19 = (f32[28672]{0:T(1024)S(1)}, f32[28672]{0:T(1024)S(1)}, u32[]{:S(2)}, u32[]{:S(2)}) collective-permute-start(f32[28672]{0:T(1024)S(1)} %dynamic_slice.31), channel_id=1, source_target_pairs={{0,8},{1,9},{2,10},{3,11},{4,12},{5,13},{6,14},{7,15},{8,0},{9,1},... | collective-permute-start | bytes 344072 | tf_op jit(solution)/shard_map/ppermute | solution.py:24
  145.9 28.2 %collective-permute-start.23 = (bf16[512,256]{1,0:T(8,128)(2,1)}, bf16[512,256]{1,0:T(8,128)(2,1)S(1)}, u32[]{:S(2)}, u32[]{:S(2)}) collective-permute-start(bf16[512,256]{1,0:T(8,128)(2,1)} %slice.183), channel_id=1, source_target_pairs={{0,12},{1,13},{2,14},{3,15},{4,0},{5,1},{6,2},{7,3},{8,4},{9,5},{1... | collective-permute-start | bytes 786440 | tf_op jit(solution)/shard_map/ppermute | solution.py:18
  150.0 24.1 %collective-permute-start.24 = (bf16[512,256]{1,0:T(8,128)(2,1)}, bf16[512,256]{1,0:T(8,128)(2,1)}, u32[]{:S(2)}, u32[]{:S(2)}) collective-permute-start(bf16[512,256]{1,0:T(8,128)(2,1)} %slice.184), channel_id=1, source_target_pairs={{0,4},{1,5},{2,6},{3,7},{4,8},{5,9},{6,10},{7,11},{8,12},{9,13},{1... | collective-permute-start | bytes 786440 | tf_op jit(solution)/shard_map/ppermute | solution.py:18
  158.0 16.1 %collective-permute-start.22 = (f32[56,512]{1,0:T(8,128)S(1)}, f32[56,512]{1,0:T(8,128)S(1)}, u32[]{:S(2)}, u32[]{:S(2)}) collective-permute-start(f32[56,512]{1,0:T(8,128)S(1)} %reshape.20), channel_id=1, source_target_pairs={{0,8},{1,9},{2,10},{3,11},{4,12},{5,13},{6,14},{7,15},{8,0},{9,1},... | collective-permute-start | bytes 344072 | tf_op jit(solution)/shard_map/ppermute | solution.py:24
  161.2 26.0 %collective-permute-start.26 = (bf16[512,256]{1,0:T(8,128)(2,1)S(1)}, bf16[512,256]{1,0:T(8,128)(2,1)S(1)}, u32[]{:S(2)}, u32[]{:S(2)}) collective-permute-start(bf16[512,256]{1,0:T(8,128)(2,1)S(1)} %slice.185), channel_id=1, source_target_pairs={{0,12},{1,13},{2,14},{3,15},{4,0},{5,1},{6,2},{7,3},{8,4},{9,5},{1... | collective-permute-start | bytes 786440 | tf_op jit(solution)/shard_map/ppermute | solution.py:18
  168.5 18.7 %collective-permute-start.27 = (bf16[512,256]{1,0:T(8,128)(2,1)S(1)}, bf16[512,256]{1,0:T(8,128)(2,1)S(1)}, u32[]{:S(2)}, u32[]{:S(2)}) collective-permute-start(bf16[512,256]{1,0:T(8,128)(2,1)S(1)} %slice.186), channel_id=1, source_target_pairs={{0,4},{1,5},{2,6},{3,7},{4,8},{5,9},{6,10},{7,11},{8,12},{9,13},{1... | collective-permute-start | bytes 786440 | tf_op jit(solution)/shard_map/ppermute | solution.py:18
  174.1 13.0 %collective-permute-start.25 = (f32[112,512]{1,0:T(8,128)S(1)}, f32[112,512]{1,0:T(8,128)S(1)}, u32[]{:S(2)}, u32[]{:S(2)}) collective-permute-start(f32[112,512]{1,0:T(8,128)S(1)} %pad_maximum_fusion.10), channel_id=1, source_target_pairs={{0,4},{1,5},{2,6},{3,7},{4,0},{5,1},{6,2},{7,3},{8,12},{9,13},{10,... | collective-permute-start | bytes 688136 | tf_op jit(solution)/shard_map/ppermute | solution.py:24
  180.9 19.8 %collective-permute-start.29 = (bf16[512,256]{1,0:T(8,128)(2,1)S(1)}, bf16[512,256]{1,0:T(8,128)(2,1)S(1)}, u32[]{:S(2)}, u32[]{:S(2)}) collective-permute-start(bf16[512,256]{1,0:T(8,128)(2,1)S(1)} %slice.187), channel_id=1, source_target_pairs={{0,12},{1,13},{2,14},{3,15},{4,0},{5,1},{6,2},{7,3},{8,4},{9,5},{1... | collective-permute-start | bytes 786440 | tf_op jit(solution)/shard_map/ppermute | solution.py:18
  184.7 20.0 %collective-permute-start.30 = (bf16[512,256]{1,0:T(8,128)(2,1)S(1)}, bf16[512,256]{1,0:T(8,128)(2,1)S(1)}, u32[]{:S(2)}, u32[]{:S(2)}) collective-permute-start(bf16[512,256]{1,0:T(8,128)(2,1)S(1)} %slice.188), channel_id=1, source_target_pairs={{0,4},{1,5},{2,6},{3,7},{4,8},{5,9},{6,10},{7,11},{8,12},{9,13},{1... | collective-permute-start | bytes 786440 | tf_op jit(solution)/shard_map/ppermute | solution.py:18
  187.2 17.4 %collective-permute-start.28 = (f32[224,512]{1,0:T(8,128)S(1)}, f32[224,512]{1,0:T(8,128)S(1)}, u32[]{:S(2)}, u32[]{:S(2)}) collective-permute-start(f32[224,512]{1,0:T(8,128)S(1)} %pad_maximum_fusion.7), channel_id=1, source_target_pairs={{0,2},{1,3},{2,0},{3,1},{4,6},{5,7},{6,4},{7,5},{8,10},{9,11},{10,... | collective-permute-start | bytes 1376264 | tf_op jit(solution)/shard_map/ppermute | solution.py:24
  189.8 16.9 %collective-permute-start.31 = (bf16[512,256]{1,0:T(8,128)(2,1)S(1)}, bf16[512,256]{1,0:T(8,128)(2,1)S(1)}, u32[]{:S(2)}, u32[]{:S(2)}) collective-permute-start(bf16[512,256]{1,0:T(8,128)(2,1)S(1)} %get-tuple-element.134), channel_id=1, source_target_pairs={{0,12},{1,13},{2,14},{3,15},{4,0},{5,1},{6,2},{7,3},{8,4},{9,5},{1... | collective-permute-start | bytes 786440 | tf_op jit(solution)/shard_map/ppermute | solution.py:18
  200.7 16.2 %collective-permute-start.33 = (bf16[512,256]{1,0:T(8,128)(2,1)S(1)}, bf16[512,256]{1,0:T(8,128)(2,1)S(1)}, u32[]{:S(2)}, u32[]{:S(2)}) collective-permute-start(bf16[512,256]{1,0:T(8,128)(2,1)S(1)} %get-tuple-element.133), channel_id=1, source_target_pairs={{0,12},{1,13},{2,14},{3,15},{4,0},{5,1},{6,2},{7,3},{8,4},{9,5},{1... | collective-permute-start | bytes 786440 | tf_op jit(solution)/shard_map/ppermute | solution.py:18
  204.6 15.2 %collective-permute-start.34 = (bf16[512,256]{1,0:T(8,128)(2,1)S(1)}, bf16[512,256]{1,0:T(8,128)(2,1)S(1)}, u32[]{:S(2)}, u32[]{:S(2)}) collective-permute-start(bf16[512,256]{1,0:T(8,128)(2,1)S(1)} %get-tuple-element.131), channel_id=1, source_target_pairs={{0,4},{1,5},{2,6},{3,7},{4,8},{5,9},{6,10},{7,11},{8,12},{9,13},{1... | collective-permute-start | bytes 786440 | tf_op jit(solution)/shard_map/ppermute | solution.py:18
  (20 other events, 334.9 us)

commit v16 on v11

--- a/solution.py
+++ b/solution.py
@@ -10,6 +10,7 @@
 EARLY = 1
 RIDER_ROWS = 512
 RIDER_SPAN = 2
+LATE_PARTS = 1
 
 
 def from_behind(value, axis, steps):
@@ -146,9 +147,10 @@
             sent_rows += RIDER_ROWS
         if not down and bit == 2 and not late:
             buf, pieces = lax.optimization_barrier((buf, (lower_all, upper_all)))
-            middle_row = sent_rows + (positions - sent_rows) // 2
-            late.append(send_rows(pieces, sent_rows, middle_row))
-            late.append(send_rows(pieces, middle_row, positions))
+            for part in range(LATE_PARTS):
+                start = sent_rows + part * (positions - sent_rows) // LATE_PARTS
+                stop = sent_rows + (part + 1) * (positions - sent_rows) // LATE_PARTS
+                late.append(send_rows(pieces, start, stop))
             sent_rows = positions
         if not down and bit == 1 and late:
             buf, late = lax.optimization_barrier((buf, late))

time: 223 us -> 228 us (1.022)
  waiting for transfers between devices: 62.6 us -> 84.6 us
  starting transfers between devices: 99.4 us -> 81.7 us
    ppermute x26 -> x24, starting transfers between devices: 85.3 us -> 71.5 us  [from_behind(): return lax.ppermute(value, axis, pairs)]
    ppermute x26 -> x24, waiting for transfers between devices: 36.8 us -> 49.5 us  [from_behind(): return lax.ppermute(value, axis, pairs)]
    ppermute x8, waiting for transfers between devices: 25.8 us -> 35.1 us  [exchange(): return lax.ppermute(value, axis, pairs)]
    ppermute x8, starting transfers between devices: 14 us -> 10.2 us  [exchange(): return lax.ppermute(value, axis, pairs)]
    unnamed x44 -> x46, local copies, waits for them, and re-layouts: 5.04 us -> 5.44 us
  transfers between devices with their start and end apart: 34 -> 32, of which waited for: 14 -> 13; matrix products, arithmetic and copies ran while one was open for 22% -> 21% of each run, Pallas kernels for 0% -> 0%
where the time goes in v16:
time: 228 us; the launch traced here: 227 us
  waiting for transfers between devices  84.6 us (37%)
  starting transfers between devices  81.7 us (36%)
  matrix products  33.5 us (15%)
  local copies, waits for them, and re-layouts  19.9 us (9%)
  other arithmetic  5.76 us (3%)
    ppermute x24, starting transfers between devices, from_behind(): return lax.ppermute(value, axis, pairs)  71.5 us
    ppermute x24, waiting for transfers between devices, from_behind(): return lax.ppermute(value, axis, pairs)  49.5 us
    ppermute x8, waiting for transfers between devices, exchange(): return lax.ppermute(value, axis, pairs)  35.1 us
    ppermute x8, starting transfers between devices, exchange(): return lax.ppermute(value, axis, pairs)  10.2 us
    unnamed x46, local copies, waits for them, and re-layouts  5.44 us
    slice x5, local copies, waits for them, and re-layouts, send_rows(): low_high[1][start:stop]  4.7 us
    dot_general x5, matrix products, chunk_layer(): preact = preact + jnp.dot(middle, w_mid, preferred_element_type=jnp.float32)  4.65 us
  transfers between devices with their start and end apart: 32, of which 13 were waited for; matrix products, arithmetic and copies ran while one was open for 21% of the time, Pallas kernels for 0%

profile of v16, /device:TPU:0, one launch (start us, length us, event | category | flops | bytes accessed | tf_op | source)
XLA Modules:
  0.0 227.2 jit_solution(4830372715686147162)
XLA Ops:
  0.7 2.0 fusion.117
  2.7 3.0 %collective-permute-start.8 = (bf16[512,256]{1,0:T(8,128)(2,1)}, bf16[512,256]{1,0:T(8,128)(2,1)S(1)}, u32[]{:S(2)}, u32[]{:S(2)}) collective-permute-start(bf16[512,256]{1,0:T(8,128)(2,1)} %get-tuple-element.123), channel_id=1, source_target_pairs={{0,4},{1,5},{2,6},{3,7},{4,8},{5,9},{6,10},{7,11},{8,12},{9,13},{1... | collective-permute-start | bytes 786440 | tf_op jit(solution)/shard_map/ppermute | solution.py:19
  5.7 2.0 collective-permute-start.9
  7.7 2.5 %fusion.116 = (bf16[1024,256]{1,0:T(8,128)(2,1)}, bf16[1024,256]{1,0:T(8,128)(2,1)}, bf16[1024,256]{1,0:T(8,128)(2,1)}) fusion(bf16[4096,256]{1,0:T(8,128)(2,1)} %param.4), kind=kLoop, calls=%fused_computation.204 | loop fusion | bytes 3145728 | tf_op jit(solution)/shard_map/slice | solution.py:96
  10.3 3.8 %collective-permute-start.1 = (bf16[1024,256]{1,0:T(8,128)(2,1)}, bf16[1024,256]{1,0:T(8,128)(2,1)}, u32[]{:S(2)}, u32[]{:S(2)}) collective-permute-start(bf16[1024,256]{1,0:T(8,128)(2,1)} %get-tuple-element.121), channel_id=1, source_target_pairs={{0,12},{1,13},{2,14},{3,15},{4,0},{5,1},{6,2},{7,3},{8,4},{9,5},{1... | collective-permute-start | bytes 1572872 | tf_op jit(solution)/shard_map/ppermute | solution.py:19
  14.1 1.8 fusion.77
  16.5 1.7 fusion.71
  18.6 13.5 %collective-permute-done = bf16[1024,256]{1,0:T(8,128)(2,1)} collective-permute-done((bf16[1024,256]{1,0:T(8,128)(2,1)}, bf16[1024,256]{1,0:T(8,128)(2,1)}, u32[]{:S(2)}, u32[]{:S(2)}) %collective-permute-start) | collective-permute-done | bytes 524320 | tf_op jit(solution)/shard_map/ppermute | solution.py:19
  32.1 13.2 %collective-permute-start.3 = (bf16[1024,256]{1,0:T(8,128)(2,1)}, bf16[1024,256]{1,0:T(8,128)(2,1)S(1)}, u32[]{:S(2)}, u32[]{:S(2)}) collective-permute-start(bf16[1024,256]{1,0:T(8,128)(2,1)} %get-tuple-element.119), channel_id=1, source_target_pairs={{0,12},{1,13},{2,14},{3,15},{4,0},{5,1},{6,2},{7,3},{8,4},{9,5},{1... | collective-permute-start | bytes 1572872 | tf_op jit(solution)/shard_map/ppermute | solution.py:19
  46.9 1.7 add_add_fusion.2
  54.6 13.2 %collective-permute-start.5 = (bf16[1024,256]{1,0:T(8,128)(2,1)S(1)}, bf16[1024,256]{1,0:T(8,128)(2,1)S(1)}, u32[]{:S(2)}, u32[]{:S(2)}) collective-permute-start(bf16[1024,256]{1,0:T(8,128)(2,1)S(1)} %copy-done.12), channel_id=1, source_target_pairs={{0,12},{1,13},{2,14},{3,15},{4,0},{5,1},{6,2},{7,3},{8,4},{9,5},{1... | collective-permute-start | bytes 1572872 | tf_op jit(solution)/shard_map/ppermute | solution.py:19
  67.8 8.3 %collective-permute-start.6 = (bf16[512,256]{1,0:T(8,128)(2,1)S(1)}, bf16[512,256]{1,0:T(8,128)(2,1)S(1)}, u32[]{:S(2)}, u32[]{:S(2)}) collective-permute-start(bf16[512,256]{1,0:T(8,128)(2,1)S(1)} %copy-done.13), channel_id=1, source_target_pairs={{0,4},{1,5},{2,6},{3,7},{4,8},{5,9},{6,10},{7,11},{8,12},{9,13},{1... | collective-permute-start | bytes 786440 | tf_op jit(solution)/shard_map/ppermute | solution.py:19
  82.3 7.8 %collective-permute-start.7 = (bf16[512,256]{1,0:T(8,128)(2,1)S(1)}, bf16[512,256]{1,0:T(8,128)(2,1)S(1)}, u32[]{:S(2)}, u32[]{:S(2)}) collective-permute-start(bf16[512,256]{1,0:T(8,128)(2,1)S(1)} %copy-done.13), channel_id=1, source_target_pairs={{0,12},{1,13},{2,14},{3,15},{4,0},{5,1},{6,2},{7,3},{8,4},{9,5},{1... | collective-permute-start | bytes 786440 | tf_op jit(solution)/shard_map/ppermute | solution.py:19
  94.8 3.1 %collective-permute-done.7 = bf16[512,256]{1,0:T(8,128)(2,1)S(1)} collective-permute-done((bf16[512,256]{1,0:T(8,128)(2,1)S(1)}, bf16[512,256]{1,0:T(8,128)(2,1)S(1)}, u32[]{:S(2)}, u32[]{:S(2)}) %collective-permute-start.7) | collective-permute-done | bytes 262176 | tf_op jit(solution)/shard_map/ppermute | solution.py:19
  105.5 2.4 %collective-permute-start.12 = (bf16[512,256]{1,0:T(8,128)(2,1)S(1)}, bf16[512,256]{1,0:T(8,128)(2,1)S(1)}, u32[]{:S(2)}, u32[]{:S(2)}) collective-permute-start(bf16[512,256]{1,0:T(8,128)(2,1)S(1)} %get-tuple-element.135), channel_id=1, source_target_pairs={{0,12},{1,13},{2,14},{3,15},{4,0},{5,1},{6,2},{7,3},{8,4},{9,5},{1... | collective-permute-start | bytes 786440 | tf_op jit(solution)/shard_map/ppermute | solution.py:19
  108.0 3.8 %collective-permute-start.14 = (bf16[512,256]{1,0:T(8,128)(2,1)S(1)}, bf16[512,256]{1,0:T(8,128)(2,1)S(1)}, u32[]{:S(2)}, u32[]{:S(2)}) collective-permute-start(bf16[512,256]{1,0:T(8,128)(2,1)S(1)} %get-tuple-element.134), channel_id=1, source_target_pairs={{0,12},{1,13},{2,14},{3,15},{4,0},{5,1},{6,2},{7,3},{8,4},{9,5},{1... | collective-permute-start | bytes 786440 | tf_op jit(solution)/shard_map/ppermute | solution.py:19
  118.8 9.9 %collective-permute-done.11 = f32[114688]{0:T(1024)S(1)} collective-permute-done((f32[114688]{0:T(1024)S(1)}, f32[114688]{0:T(1024)S(1)}, u32[]{:S(2)}, u32[]{:S(2)}) %collective-permute-start.11) | collective-permute-done | bytes 458784 | tf_op jit(solution)/shard_map/ppermute | solution.py:25
  128.7 3.2 %collective-permute-done.15 = bf16[512,256]{1,0:T(8,128)(2,1)S(1)} collective-permute-done((bf16[512,256]{1,0:T(8,128)(2,1)S(1)}, bf16[512,256]{1,0:T(8,128)(2,1)S(1)}, u32[]{:S(2)}, u32[]{:S(2)}) %collective-permute-start.15) | collective-permute-done | bytes 262176 | tf_op jit(solution)/shard_map/ppermute | solution.py:19
  134.0 2.0 copy-done.5
  140.5 1.8 collective-permute-start.17
  143.0 11.1 %collective-permute-done.17 = f32[28672]{0:T(1024)S(1)} collective-permute-done((f32[28672]{0:T(1024)S(1)}, f32[28672]{0:T(1024)S(1)}, u32[]{:S(2)}, u32[]{:S(2)}) %collective-permute-start.17) | collective-permute-done | bytes 114720 | tf_op jit(solution)/shard_map/ppermute | solution.py:25
  155.7 1.8 constant_dynamic-update-slice_fusion.8
  158.6 2.1 collective-permute-start.21
  163.2 3.3 %collective-permute-start.24 = (bf16[512,256]{1,0:T(8,128)(2,1)S(1)}, bf16[512,256]{1,0:T(8,128)(2,1)S(1)}, u32[]{:S(2)}, u32[]{:S(2)}) collective-permute-start(bf16[512,256]{1,0:T(8,128)(2,1)S(1)} %slice.160), channel_id=1, source_target_pairs={{0,12},{1,13},{2,14},{3,15},{4,0},{5,1},{6,2},{7,3},{8,4},{9,5},{1... | collective-permute-start | bytes 786440 | tf_op jit(solution)/shard_map/ppermute | solution.py:19
  167.6 6.4 %collective-permute-done.21 = bf16[512,256]{1,0:T(8,128)(2,1)S(1)} collective-permute-done((bf16[512,256]{1,0:T(8,128)(2,1)S(1)}, bf16[512,256]{1,0:T(8,128)(2,1)S(1)}, u32[]{:S(2)}, u32[]{:S(2)}) %collective-permute-start.21) | collective-permute-done | bytes 262176 | tf_op jit(solution)/shard_map/ppermute | solution.py:19
  174.1 2.0 collective-permute-start.23
  177.1 2.0 collective-permute-start.27
  180.2 10.0 %collective-permute-done.23 = f32[112,512]{1,0:T(8,128)S(1)} collective-permute-done((f32[112,512]{1,0:T(8,128)S(1)}, f32[112,512]{1,0:T(8,128)S(1)}, u32[]{:S(2)}, u32[]{:S(2)}) %collective-permute-start.23) | collective-permute-done | bytes 229408 | tf_op jit(solution)/shard_map/ppermute | solution.py:25
  193.0 3.5 %collective-permute-start.29 = (bf16[1024,256]{1,0:T(8,128)(2,1)S(1)}, bf16[1024,256]{1,0:T(8,128)(2,1)S(1)}, u32[]{:S(2)}, u32[]{:S(2)}) collective-permute-start(bf16[1024,256]{1,0:T(8,128)(2,1)S(1)} %slice.164), channel_id=1, source_target_pairs={{0,12},{1,13},{2,14},{3,15},{4,0},{5,1},{6,2},{7,3},{8,4},{9,5},{1... | collective-permute-start | bytes 1572872 | tf_op jit(solution)/shard_map/ppermute | solution.py:19
  197.7 2.4 %collective-permute-done.26 = f32[224,512]{1,0:T(8,128)S(1)} collective-permute-done((f32[224,512]{1,0:T(8,128)S(1)}, f32[224,512]{1,0:T(8,128)S(1)}, u32[]{:S(2)}, u32[]{:S(2)}) %collective-permute-start.26) | collective-permute-done | bytes 458784 | tf_op jit(solution)/shard_map/ppermute | solution.py:25
  201.5 21.0 %collective-permute-done.29 = bf16[1024,256]{1,0:T(8,128)(2,1)S(1)} collective-permute-done((bf16[1024,256]{1,0:T(8,128)(2,1)S(1)}, bf16[1024,256]{1,0:T(8,128)(2,1)S(1)}, u32[]{:S(2)}, u32[]{:S(2)}) %collective-permute-start.29) | collective-permute-done | bytes 524320 | tf_op jit(solution)/shard_map/ppermute | solution.py:19
  222.6 2.2 add_convert_fusion
  (178 shorter events, 56.9 us)
Async XLA Ops:
  2.7 98.3 %collective-permute-start.8 = (bf16[512,256]{1,0:T(8,128)(2,1)}, bf16[512,256]{1,0:T(8,128)(2,1)S(1)}, u32[]{:S(2)}, u32[]{:S(2)}) collective-permute-start(bf16[512,256]{1,0:T(8,128)(2,1)} %get-tuple-element.123), channel_id=1, source_target_pairs={{0,4},{1,5},{2,6},{3,7},{4,8},{5,9},{6,10},{7,11},{8,12},{9,13},{1... | collective-permute-start | bytes 786440 | tf_op jit(solution)/shard_map/ppermute | solution.py:19
  5.7 95.3 %collective-permute-start.9 = (bf16[512,256]{1,0:T(8,128)(2,1)}, bf16[512,256]{1,0:T(8,128)(2,1)S(1)}, u32[]{:S(2)}, u32[]{:S(2)}) collective-permute-start(bf16[512,256]{1,0:T(8,128)(2,1)} %get-tuple-element.123), channel_id=1, source_target_pairs={{0,12},{1,13},{2,14},{3,15},{4,0},{5,1},{6,2},{7,3},{8,4},{9,5},{1... | collective-permute-start | bytes 786440 | tf_op jit(solution)/shard_map/ppermute | solution.py:19
  10.3 21.9 %collective-permute-start = (bf16[1024,256]{1,0:T(8,128)(2,1)}, bf16[1024,256]{1,0:T(8,128)(2,1)}, u32[]{:S(2)}, u32[]{:S(2)}) collective-permute-start(bf16[1024,256]{1,0:T(8,128)(2,1)} %get-tuple-element.121), channel_id=1, source_target_pairs={{0,4},{1,5},{2,6},{3,7},{4,8},{5,9},{6,10},{7,11},{8,12},{9,13},{1... | collective-permute-start | bytes 1572872 | tf_op jit(solution)/shard_map/ppermute | solution.py:19
  10.3 36.6 %collective-permute-start.1 = (bf16[1024,256]{1,0:T(8,128)(2,1)}, bf16[1024,256]{1,0:T(8,128)(2,1)}, u32[]{:S(2)}, u32[]{:S(2)}) collective-permute-start(bf16[1024,256]{1,0:T(8,128)(2,1)} %get-tuple-element.121), channel_id=1, source_target_pairs={{0,12},{1,13},{2,14},{3,15},{4,0},{5,1},{6,2},{7,3},{8,4},{9,5},{1... | collective-permute-start | bytes 1572872 | tf_op jit(solution)/shard_map/ppermute | solution.py:19
  14.1 40.5 %collective-permute-start.2 = (bf16[1024,256]{1,0:T(8,128)(2,1)}, bf16[1024,256]{1,0:T(8,128)(2,1)}, u32[]{:S(2)}, u32[]{:S(2)}) collective-permute-start(bf16[1024,256]{1,0:T(8,128)(2,1)} %get-tuple-element.119), channel_id=1, source_target_pairs={{0,4},{1,5},{2,6},{3,7},{4,8},{5,9},{6,10},{7,11},{8,12},{9,13},{1... | collective-permute-start | bytes 1572872 | tf_op jit(solution)/shard_map/ppermute | solution.py:19
  32.1 35.7 %collective-permute-start.3 = (bf16[1024,256]{1,0:T(8,128)(2,1)}, bf16[1024,256]{1,0:T(8,128)(2,1)S(1)}, u32[]{:S(2)}, u32[]{:S(2)}) collective-permute-start(bf16[1024,256]{1,0:T(8,128)(2,1)} %get-tuple-element.119), channel_id=1, source_target_pairs={{0,12},{1,13},{2,14},{3,15},{4,0},{5,1},{6,2},{7,3},{8,4},{9,5},{1... | collective-permute-start | bytes 1572872 | tf_op jit(solution)/shard_map/ppermute | solution.py:19
  46.9 35.4 %collective-permute-start.4 = (bf16[1024,256]{1,0:T(8,128)(2,1)S(1)}, bf16[1024,256]{1,0:T(8,128)(2,1)S(1)}, u32[]{:S(2)}, u32[]{:S(2)}) collective-permute-start(bf16[1024,256]{1,0:T(8,128)(2,1)S(1)} %copy-done.12), channel_id=1, source_target_pairs={{0,4},{1,5},{2,6},{3,7},{4,8},{5,9},{6,10},{7,11},{8,12},{9,13},{1... | collective-permute-start | bytes 1572872 | tf_op jit(solution)/shard_map/ppermute | solution.py:19
  54.6 35.5 %collective-permute-start.5 = (bf16[1024,256]{1,0:T(8,128)(2,1)S(1)}, bf16[1024,256]{1,0:T(8,128)(2,1)S(1)}, u32[]{:S(2)}, u32[]{:S(2)}) collective-permute-start(bf16[1024,256]{1,0:T(8,128)(2,1)S(1)} %copy-done.12), channel_id=1, source_target_pairs={{0,12},{1,13},{2,14},{3,15},{4,0},{5,1},{6,2},{7,3},{8,4},{9,5},{1... | collective-permute-start | bytes 1572872 | tf_op jit(solution)/shard_map/ppermute | solution.py:19
  67.8 27.0 %collective-permute-start.6 = (bf16[512,256]{1,0:T(8,128)(2,1)S(1)}, bf16[512,256]{1,0:T(8,128)(2,1)S(1)}, u32[]{:S(2)}, u32[]{:S(2)}) collective-permute-start(bf16[512,256]{1,0:T(8,128)(2,1)S(1)} %copy-done.13), channel_id=1, source_target_pairs={{0,4},{1,5},{2,6},{3,7},{4,8},{5,9},{6,10},{7,11},{8,12},{9,13},{1... | collective-permute-start | bytes 786440 | tf_op jit(solution)/shard_map/ppermute | solution.py:19
  82.3 15.6 %collective-permute-start.7 = (bf16[512,256]{1,0:T(8,128)(2,1)S(1)}, bf16[512,256]{1,0:T(8,128)(2,1)S(1)}, u32[]{:S(2)}, u32[]{:S(2)}) collective-permute-start(bf16[512,256]{1,0:T(8,128)(2,1)S(1)} %copy-done.13), channel_id=1, source_target_pairs={{0,12},{1,13},{2,14},{3,15},{4,0},{5,1},{6,2},{7,3},{8,4},{9,5},{1... | collective-permute-start | bytes 786440 | tf_op jit(solution)/shard_map/ppermute | solution.py:19
  105.4 10.9 %collective-permute-start.10 = (f32[229376]{0:T(1024)S(1)}, f32[229376]{0:T(1024)S(1)}, u32[]{:S(2)}, u32[]{:S(2)}) collective-permute-start(f32[229376]{0:T(1024)S(1)} %dynamic_slice.25), channel_id=1, source_target_pairs={{0,1},{1,0},{2,3},{3,2},{4,5},{5,4},{6,7},{7,6},{8,9},{9,8},{10,11... | collective-permute-start | bytes 2752520 | tf_op jit(solution)/shard_map/ppermute | solution.py:25
  105.5 23.2 %collective-permute-start.12 = (bf16[512,256]{1,0:T(8,128)(2,1)S(1)}, bf16[512,256]{1,0:T(8,128)(2,1)S(1)}, u32[]{:S(2)}, u32[]{:S(2)}) collective-permute-start(bf16[512,256]{1,0:T(8,128)(2,1)S(1)} %get-tuple-element.135), channel_id=1, source_target_pairs={{0,12},{1,13},{2,14},{3,15},{4,0},{5,1},{6,2},{7,3},{8,4},{9,5},{1... | collective-permute-start | bytes 786440 | tf_op jit(solution)/shard_map/ppermute | solution.py:19
  107.9 20.8 %collective-permute-start.13 = (bf16[512,256]{1,0:T(8,128)(2,1)S(1)}, bf16[512,256]{1,0:T(8,128)(2,1)S(1)}, u32[]{:S(2)}, u32[]{:S(2)}) collective-permute-start(bf16[512,256]{1,0:T(8,128)(2,1)S(1)} %get-tuple-element.133), channel_id=1, source_target_pairs={{0,4},{1,5},{2,6},{3,7},{4,8},{5,9},{6,10},{7,11},{8,12},{9,13},{1... | collective-permute-start | bytes 786440 | tf_op jit(solution)/shard_map/ppermute | solution.py:19
  108.0 20.7 %collective-permute-start.14 = (bf16[512,256]{1,0:T(8,128)(2,1)S(1)}, bf16[512,256]{1,0:T(8,128)(2,1)S(1)}, u32[]{:S(2)}, u32[]{:S(2)}) collective-permute-start(bf16[512,256]{1,0:T(8,128)(2,1)S(1)} %get-tuple-element.134), channel_id=1, source_target_pairs={{0,12},{1,13},{2,14},{3,15},{4,0},{5,1},{6,2},{7,3},{8,4},{9,5},{1... | collective-permute-start | bytes 786440 | tf_op jit(solution)/shard_map/ppermute | solution.py:19
  111.8 20.2 %collective-permute-start.15 = (bf16[512,256]{1,0:T(8,128)(2,1)S(1)}, bf16[512,256]{1,0:T(8,128)(2,1)S(1)}, u32[]{:S(2)}, u32[]{:S(2)}) collective-permute-start(bf16[512,256]{1,0:T(8,128)(2,1)S(1)} %get-tuple-element.132), channel_id=1, source_target_pairs={{0,4},{1,5},{2,6},{3,7},{4,8},{5,9},{6,10},{7,11},{8,12},{9,13},{1... | collective-permute-start | bytes 786440 | tf_op jit(solution)/shard_map/ppermute | solution.py:19
  116.5 12.1 %collective-permute-start.11 = (f32[114688]{0:T(1024)S(1)}, f32[114688]{0:T(1024)S(1)}, u32[]{:S(2)}, u32[]{:S(2)}) collective-permute-start(f32[114688]{0:T(1024)S(1)} %dynamic_slice.27), channel_id=1, source_target_pairs={{0,2},{1,3},{2,0},{3,1},{4,6},{5,7},{6,4},{7,5},{8,10},{9,11},{10,... | collective-permute-start | bytes 1376264 | tf_op jit(solution)/shard_map/ppermute | solution.py:25
  132.0 8.4 %collective-permute-start.16 = (f32[57344]{0:T(1024)S(1)}, f32[57344]{0:T(1024)S(1)}, u32[]{:S(2)}, u32[]{:S(2)}) collective-permute-start(f32[57344]{0:T(1024)S(1)} %dynamic_slice.29), channel_id=1, source_target_pairs={{0,4},{1,5},{2,6},{3,7},{4,0},{5,1},{6,2},{7,3},{8,12},{9,13},{10,... | collective-permute-start | bytes 688136 | tf_op jit(solution)/shard_map/ppermute | solution.py:25
  136.0 18.2 %collective-permute-start.18 = (bf16[512,256]{1,0:T(8,128)(2,1)S(1)}, bf16[512,256]{1,0:T(8,128)(2,1)S(1)}, u32[]{:S(2)}, u32[]{:S(2)}) collective-permute-start(bf16[512,256]{1,0:T(8,128)(2,1)S(1)} %slice.156), channel_id=1, source_target_pairs={{0,12},{1,13},{2,14},{3,15},{4,0},{5,1},{6,2},{7,3},{8,4},{9,5},{1... | collective-permute-start | bytes 786440 | tf_op jit(solution)/shard_map/ppermute | solution.py:19
  138.2 15.9 %collective-permute-start.19 = (bf16[512,256]{1,0:T(8,128)(2,1)}, bf16[512,256]{1,0:T(8,128)(2,1)S(1)}, u32[]{:S(2)}, u32[]{:S(2)}) collective-permute-start(bf16[512,256]{1,0:T(8,128)(2,1)} %slice.157), channel_id=1, source_target_pairs={{0,4},{1,5},{2,6},{3,7},{4,8},{5,9},{6,10},{7,11},{8,12},{9,13},{1... | collective-permute-start | bytes 786440 | tf_op jit(solution)/shard_map/ppermute | solution.py:19
  140.5 13.7 %collective-permute-start.17 = (f32[28672]{0:T(1024)S(1)}, f32[28672]{0:T(1024)S(1)}, u32[]{:S(2)}, u32[]{:S(2)}) collective-permute-start(f32[28672]{0:T(1024)S(1)} %dynamic_slice.31), channel_id=1, source_target_pairs={{0,8},{1,9},{2,10},{3,11},{4,12},{5,13},{6,14},{7,15},{8,0},{9,1},... | collective-permute-start | bytes 344072 | tf_op jit(solution)/shard_map/ppermute | solution.py:25
  154.2 13.4 %collective-permute-start.20 = (f32[56,512]{1,0:T(8,128)S(1)}, f32[56,512]{1,0:T(8,128)S(1)}, u32[]{:S(2)}, u32[]{:S(2)}) collective-permute-start(f32[56,512]{1,0:T(8,128)S(1)} %reshape.20), channel_id=1, source_target_pairs={{0,8},{1,9},{2,10},{3,11},{4,12},{5,13},{6,14},{7,15},{8,0},{9,1},... | collective-permute-start | bytes 344072 | tf_op jit(solution)/shard_map/ppermute | solution.py:25
  158.6 15.5 %collective-permute-start.21 = (bf16[512,256]{1,0:T(8,128)(2,1)S(1)}, bf16[512,256]{1,0:T(8,128)(2,1)S(1)}, u32[]{:S(2)}, u32[]{:S(2)}) collective-permute-start(bf16[512,256]{1,0:T(8,128)(2,1)S(1)} %slice.158), channel_id=1, source_target_pairs={{0,12},{1,13},{2,14},{3,15},{4,0},{5,1},{6,2},{7,3},{8,4},{9,5},{1... | collective-permute-start | bytes 786440 | tf_op jit(solution)/shard_map/ppermute | solution.py:19
  161.6 12.4 %collective-permute-start.22 = (bf16[512,256]{1,0:T(8,128)(2,1)S(1)}, bf16[512,256]{1,0:T(8,128)(2,1)S(1)}, u32[]{:S(2)}, u32[]{:S(2)}) collective-permute-start(bf16[512,256]{1,0:T(8,128)(2,1)S(1)} %slice.159), channel_id=1, source_target_pairs={{0,4},{1,5},{2,6},{3,7},{4,8},{5,9},{6,10},{7,11},{8,12},{9,13},{1... | collective-permute-start | bytes 786440 | tf_op jit(solution)/shard_map/ppermute | solution.py:19
  163.2 27.1 %collective-permute-start.24 = (bf16[512,256]{1,0:T(8,128)(2,1)S(1)}, bf16[512,256]{1,0:T(8,128)(2,1)S(1)}, u32[]{:S(2)}, u32[]{:S(2)}) collective-permute-start(bf16[512,256]{1,0:T(8,128)(2,1)S(1)} %slice.160), channel_id=1, source_target_pairs={{0,12},{1,13},{2,14},{3,15},{4,0},{5,1},{6,2},{7,3},{8,4},{9,5},{1... | collective-permute-start | bytes 786440 | tf_op jit(solution)/shard_map/ppermute | solution.py:19
  167.5 22.8 %collective-permute-start.25 = (bf16[512,256]{1,0:T(8,128)(2,1)S(1)}, bf16[512,256]{1,0:T(8,128)(2,1)S(1)}, u32[]{:S(2)}, u32[]{:S(2)}) collective-permute-start(bf16[512,256]{1,0:T(8,128)(2,1)S(1)} %slice.161), channel_id=1, source_target_pairs={{0,4},{1,5},{2,6},{3,7},{4,8},{5,9},{6,10},{7,11},{8,12},{9,13},{1... | collective-permute-start | bytes 786440 | tf_op jit(solution)/shard_map/ppermute | solution.py:19
  174.1 16.1 %collective-permute-start.23 = (f32[112,512]{1,0:T(8,128)S(1)}, f32[112,512]{1,0:T(8,128)S(1)}, u32[]{:S(2)}, u32[]{:S(2)}) collective-permute-start(f32[112,512]{1,0:T(8,128)S(1)} %pad_maximum_fusion.9), channel_id=1, source_target_pairs={{0,4},{1,5},{2,6},{3,7},{4,0},{5,1},{6,2},{7,3},{8,12},{9,13},{10,... | collective-permute-start | bytes 688136 | tf_op jit(solution)/shard_map/ppermute | solution.py:25
  177.1 24.3 %collective-permute-start.27 = (bf16[512,256]{1,0:T(8,128)(2,1)S(1)}, bf16[512,256]{1,0:T(8,128)(2,1)S(1)}, u32[]{:S(2)}, u32[]{:S(2)}) collective-permute-start(bf16[512,256]{1,0:T(8,128)(2,1)S(1)} %slice.162), channel_id=1, source_target_pairs={{0,12},{1,13},{2,14},{3,15},{4,0},{5,1},{6,2},{7,3},{8,4},{9,5},{1... | collective-permute-start | bytes 786440 | tf_op jit(solution)/shard_map/ppermute | solution.py:19
  180.1 21.4 %collective-permute-start.28 = (bf16[512,256]{1,0:T(8,128)(2,1)S(1)}, bf16[512,256]{1,0:T(8,128)(2,1)S(1)}, u32[]{:S(2)}, u32[]{:S(2)}) collective-permute-start(bf16[512,256]{1,0:T(8,128)(2,1)S(1)} %slice.163), channel_id=1, source_target_pairs={{0,4},{1,5},{2,6},{3,7},{4,8},{5,9},{6,10},{7,11},{8,12},{9,13},{1... | collective-permute-start | bytes 786440 | tf_op jit(solution)/shard_map/ppermute | solution.py:19
  190.3 9.7 %collective-permute-start.26 = (f32[224,512]{1,0:T(8,128)S(1)}, f32[224,512]{1,0:T(8,128)S(1)}, u32[]{:S(2)}, u32[]{:S(2)}) collective-permute-start(f32[224,512]{1,0:T(8,128)S(1)} %pad_maximum_fusion.8), channel_id=1, source_target_pairs={{0,2},{1,3},{2,0},{3,1},{4,6},{5,7},{6,4},{7,5},{8,10},{9,11},{10,... | collective-permute-start | bytes 1376264 | tf_op jit(solution)/shard_map/ppermute | solution.py:25
  193.0 29.5 %collective-permute-start.29 = (bf16[1024,256]{1,0:T(8,128)(2,1)S(1)}, bf16[1024,256]{1,0:T(8,128)(2,1)S(1)}, u32[]{:S(2)}, u32[]{:S(2)}) collective-permute-start(bf16[1024,256]{1,0:T(8,128)(2,1)S(1)} %slice.164), channel_id=1, source_target_pairs={{0,12},{1,13},{2,14},{3,15},{4,0},{5,1},{6,2},{7,3},{8,4},{9,5},{1... | collective-permute-start | bytes 1572872 | tf_op jit(solution)/shard_map/ppermute | solution.py:19
  197.5 24.9 %collective-permute-start.30 = (bf16[1024,256]{1,0:T(8,128)(2,1)S(1)}, bf16[1024,256]{1,0:T(8,128)(2,1)S(1)}, u32[]{:S(2)}, u32[]{:S(2)}) collective-permute-start(bf16[1024,256]{1,0:T(8,128)(2,1)S(1)} %slice.165), channel_id=1, source_target_pairs={{0,4},{1,5},{2,6},{3,7},{4,8},{5,9},{6,10},{7,11},{8,12},{9,13},{1... | collective-permute-start | bytes 1572872 | tf_op jit(solution)/shard_map/ppermute | solution.py:19
  222.5 2.5 %collective-permute-start.31 = (f32[448,512]{1,0:T(8,128)S(1)}, f32[448,512]{1,0:T(8,128)S(1)}, u32[]{:S(2)}, u32[]{:S(2)}) collective-permute-start(f32[448,512]{1,0:T(8,128)S(1)} %pad_maximum_fusion.5), channel_id=1, source_target_pairs={{0,1},{1,0},{2,3},{3,2},{4,5},{5,4},{6,7},{7,6},{8,9},{9,8},{10,11... | collective-permute-start | bytes 2752520 | tf_op jit(solution)/shard_map/ppermute | solution.py:25
  (16 other events, 275.7 us)

commit v17 on v16

--- a/solution.py
+++ b/solution.py
@@ -10,7 +10,7 @@
 EARLY = 1
 RIDER_ROWS = 512
 RIDER_SPAN = 2
-LATE_PARTS = 1
+LATE_PARTS = 4
 
 
 def from_behind(value, axis, steps):

time: 228 us -> 223 us (0.978)
  waiting for transfers between devices: 84.6 us -> 54.5 us
  starting transfers between devices: 81.7 us -> 108 us
    ppermute x24 -> x30, starting transfers between devices: 71.5 us -> 93.6 us  [from_behind(): return lax.ppermute(value, axis, pairs)]
    ppermute x24 -> x30, waiting for transfers between devices: 49.5 us -> 28.6 us  [from_behind(): return lax.ppermute(value, axis, pairs)]
    ppermute x8, waiting for transfers between devices: 35.1 us -> 25.9 us  [exchange(): return lax.ppermute(value, axis, pairs)]
    ppermute x8, starting transfers between devices: 10.2 us -> 13.9 us  [exchange(): return lax.ppermute(value, axis, pairs)]
    unnamed x46 -> x48, local copies, waits for them, and re-layouts: 5.44 us -> 5.07 us
  transfers between devices with their start and end apart: 32 -> 38, of which waited for: 13 -> 14; matrix products, arithmetic and copies ran while one was open for 21% -> 22% of each run, Pallas kernels for 0% -> 0%
where the time goes in v17:
time: 223 us
  starting transfers between devices  108 us (48%)
  waiting for transfers between devices  54.5 us (24%)
  matrix products  33.5 us (15%)
  local copies, waits for them, and re-layouts  19.6 us (9%)
  other arithmetic  5.77 us (3%)
    ppermute x30, starting transfers between devices, from_behind(): return lax.ppermute(value, axis, pairs)  93.6 us
    ppermute x30, waiting for transfers between devices, from_behind(): return lax.ppermute(value, axis, pairs)  28.6 us
    ppermute x8, waiting for transfers between devices, exchange(): return lax.ppermute(value, axis, pairs)  25.9 us
    ppermute x8, starting transfers between devices, exchange(): return lax.ppermute(value, axis, pairs)  13.9 us
    unnamed x48, local copies, waits for them, and re-layouts  5.07 us
    dot_general x5, matrix products, chunk_layer(): preact = preact + jnp.dot(middle, w_mid, preferred_element_type=jnp.float32)  4.65 us
    slice x2, local copies, waits for them, and re-layouts, body(): middle = activations[bounds[k]:bounds[k + 1]]  4.52 us
    slice x5, local copies, waits for them, and re-layouts, send_rows(): low_high[1][start:stop]  4.5 us
  transfers between devices with their start and end apart: 38, of which 14 were waited for; matrix products, arithmetic and copies ran while one was open for 22% of the time, Pallas kernels for 0%

profile of v17, /device:TPU:0, one launch (start us, length us, event | category | flops | bytes accessed | tf_op | source)
XLA Modules:
  0.0 222.7 jit_solution(7918732216044964946)
XLA Ops:
  0.7 2.0 fusion.119
  2.7 3.0 %collective-permute-start.8 = (bf16[512,256]{1,0:T(8,128)(2,1)}, bf16[512,256]{1,0:T(8,128)(2,1)S(1)}, u32[]{:S(2)}, u32[]{:S(2)}) collective-permute-start(bf16[512,256]{1,0:T(8,128)(2,1)} %get-tuple-element.143), channel_id=1, source_target_pairs={{0,4},{1,5},{2,6},{3,7},{4,8},{5,9},{6,10},{7,11},{8,12},{9,13},{1... | collective-permute-start | bytes 786440 | tf_op jit(solution)/shard_map/ppermute | solution.py:19
  5.7 2.0 collective-permute-start.9
  7.7 2.5 %fusion.118 = (bf16[1024,256]{1,0:T(8,128)(2,1)}, bf16[1024,256]{1,0:T(8,128)(2,1)}, bf16[1024,256]{1,0:T(8,128)(2,1)}) fusion(bf16[4096,256]{1,0:T(8,128)(2,1)} %param.4), kind=kLoop, calls=%fused_computation.212 | loop fusion | bytes 3145728 | tf_op jit(solution)/shard_map/slice | solution.py:96
  10.2 3.8 %collective-permute-start.1 = (bf16[1024,256]{1,0:T(8,128)(2,1)}, bf16[1024,256]{1,0:T(8,128)(2,1)}, u32[]{:S(2)}, u32[]{:S(2)}) collective-permute-start(bf16[1024,256]{1,0:T(8,128)(2,1)} %get-tuple-element.141), channel_id=1, source_target_pairs={{0,12},{1,13},{2,14},{3,15},{4,0},{5,1},{6,2},{7,3},{8,4},{9,5},{1... | collective-permute-start | bytes 1572872 | tf_op jit(solution)/shard_map/ppermute | solution.py:19
  14.1 1.8 fusion.77
  18.6 13.5 %collective-permute-done = bf16[1024,256]{1,0:T(8,128)(2,1)} collective-permute-done((bf16[1024,256]{1,0:T(8,128)(2,1)}, bf16[1024,256]{1,0:T(8,128)(2,1)}, u32[]{:S(2)}, u32[]{:S(2)}) %collective-permute-start) | collective-permute-done | bytes 524320 | tf_op jit(solution)/shard_map/ppermute | solution.py:19
  32.1 13.2 %collective-permute-start.3 = (bf16[1024,256]{1,0:T(8,128)(2,1)}, bf16[1024,256]{1,0:T(8,128)(2,1)S(1)}, u32[]{:S(2)}, u32[]{:S(2)}) collective-permute-start(bf16[1024,256]{1,0:T(8,128)(2,1)} %get-tuple-element.139), channel_id=1, source_target_pairs={{0,12},{1,13},{2,14},{3,15},{4,0},{5,1},{6,2},{7,3},{8,4},{9,5},{1... | collective-permute-start | bytes 1572872 | tf_op jit(solution)/shard_map/ppermute | solution.py:19
  54.6 13.2 %collective-permute-start.5 = (bf16[1024,256]{1,0:T(8,128)(2,1)S(1)}, bf16[1024,256]{1,0:T(8,128)(2,1)S(1)}, u32[]{:S(2)}, u32[]{:S(2)}) collective-permute-start(bf16[1024,256]{1,0:T(8,128)(2,1)S(1)} %copy-done.12), channel_id=1, source_target_pairs={{0,12},{1,13},{2,14},{3,15},{4,0},{5,1},{6,2},{7,3},{8,4},{9,5},{1... | collective-permute-start | bytes 1572872 | tf_op jit(solution)/shard_map/ppermute | solution.py:19
  67.8 8.3 %collective-permute-start.6 = (bf16[512,256]{1,0:T(8,128)(2,1)S(1)}, bf16[512,256]{1,0:T(8,128)(2,1)S(1)}, u32[]{:S(2)}, u32[]{:S(2)}) collective-permute-start(bf16[512,256]{1,0:T(8,128)(2,1)S(1)} %copy-done.13), channel_id=1, source_target_pairs={{0,4},{1,5},{2,6},{3,7},{4,8},{5,9},{6,10},{7,11},{8,12},{9,13},{1... | collective-permute-start | bytes 786440 | tf_op jit(solution)/shard_map/ppermute | solution.py:19
  82.3 7.8 %collective-permute-start.7 = (bf16[512,256]{1,0:T(8,128)(2,1)S(1)}, bf16[512,256]{1,0:T(8,128)(2,1)S(1)}, u32[]{:S(2)}, u32[]{:S(2)}) collective-permute-start(bf16[512,256]{1,0:T(8,128)(2,1)S(1)} %copy-done.13), channel_id=1, source_target_pairs={{0,12},{1,13},{2,14},{3,15},{4,0},{5,1},{6,2},{7,3},{8,4},{9,5},{1... | collective-permute-start | bytes 786440 | tf_op jit(solution)/shard_map/ppermute | solution.py:19
  94.8 3.1 %collective-permute-done.7 = bf16[512,256]{1,0:T(8,128)(2,1)S(1)} collective-permute-done((bf16[512,256]{1,0:T(8,128)(2,1)S(1)}, bf16[512,256]{1,0:T(8,128)(2,1)S(1)}, u32[]{:S(2)}, u32[]{:S(2)}) %collective-permute-start.7) | collective-permute-done | bytes 262176 | tf_op jit(solution)/shard_map/ppermute | solution.py:19
  106.0 2.4 %collective-permute-start.12 = (bf16[512,256]{1,0:T(8,128)(2,1)S(1)}, bf16[512,256]{1,0:T(8,128)(2,1)S(1)}, u32[]{:S(2)}, u32[]{:S(2)}) collective-permute-start(bf16[512,256]{1,0:T(8,128)(2,1)S(1)} %get-tuple-element.155), channel_id=1, source_target_pairs={{0,12},{1,13},{2,14},{3,15},{4,0},{5,1},{6,2},{7,3},{8,4},{9,5},{1... | collective-permute-start | bytes 786440 | tf_op jit(solution)/shard_map/ppermute | solution.py:19
  108.5 3.8 %collective-permute-start.14 = (bf16[512,256]{1,0:T(8,128)(2,1)S(1)}, bf16[512,256]{1,0:T(8,128)(2,1)S(1)}, u32[]{:S(2)}, u32[]{:S(2)}) collective-permute-start(bf16[512,256]{1,0:T(8,128)(2,1)S(1)} %get-tuple-element.154), channel_id=1, source_target_pairs={{0,12},{1,13},{2,14},{3,15},{4,0},{5,1},{6,2},{7,3},{8,4},{9,5},{1... | collective-permute-start | bytes 786440 | tf_op jit(solution)/shard_map/ppermute | solution.py:19
  119.1 9.8 %collective-permute-done.11 = f32[114688]{0:T(1024)S(1)} collective-permute-done((f32[114688]{0:T(1024)S(1)}, f32[114688]{0:T(1024)S(1)}, u32[]{:S(2)}, u32[]{:S(2)}) %collective-permute-start.11) | collective-permute-done | bytes 458784 | tf_op jit(solution)/shard_map/ppermute | solution.py:25
  129.0 3.4 %collective-permute-done.15 = bf16[512,256]{1,0:T(8,128)(2,1)S(1)} collective-permute-done((bf16[512,256]{1,0:T(8,128)(2,1)S(1)}, bf16[512,256]{1,0:T(8,128)(2,1)S(1)}, u32[]{:S(2)}, u32[]{:S(2)}) %collective-permute-start.15) | collective-permute-done | bytes 262176 | tf_op jit(solution)/shard_map/ppermute | solution.py:19
  138.3 2.7 %collective-permute-done.16 = f32[57344]{0:T(1024)S(1)} collective-permute-done((f32[57344]{0:T(1024)S(1)}, f32[57344]{0:T(1024)S(1)}, u32[]{:S(2)}, u32[]{:S(2)}) %collective-permute-start.16) | collective-permute-done | bytes 229408 | tf_op jit(solution)/shard_map/ppermute | solution.py:25
  141.1 1.7 collective-permute-start.17
  144.2 2.3 %collective-permute-start.21 = (bf16[512,256]{1,0:T(8,128)(2,1)}, bf16[512,256]{1,0:T(8,128)(2,1)S(1)}, u32[]{:S(2)}, u32[]{:S(2)}) collective-permute-start(bf16[512,256]{1,0:T(8,128)(2,1)} %slice.176), channel_id=1, source_target_pairs={{0,12},{1,13},{2,14},{3,15},{4,0},{5,1},{6,2},{7,3},{8,4},{9,5},{1... | collective-permute-start | bytes 786440 | tf_op jit(solution)/shard_map/ppermute | solution.py:19
  147.3 8.1 %collective-permute-done.17 = f32[28672]{0:T(1024)S(1)} collective-permute-done((f32[28672]{0:T(1024)S(1)}, f32[28672]{0:T(1024)S(1)}, u32[]{:S(2)}, u32[]{:S(2)}) %collective-permute-start.17) | collective-permute-done | bytes 114720 | tf_op jit(solution)/shard_map/ppermute | solution.py:25
  155.5 2.0 collective-permute-start.20
  158.4 6.5 %collective-permute-start.24 = (bf16[512,256]{1,0:T(8,128)(2,1)S(1)}, bf16[512,256]{1,0:T(8,128)(2,1)S(1)}, u32[]{:S(2)}, u32[]{:S(2)}) collective-permute-start(bf16[512,256]{1,0:T(8,128)(2,1)S(1)} %slice.178), channel_id=1, source_target_pairs={{0,12},{1,13},{2,14},{3,15},{4,0},{5,1},{6,2},{7,3},{8,4},{9,5},{1... | collective-permute-start | bytes 786440 | tf_op jit(solution)/shard_map/ppermute | solution.py:19
  168.2 3.5 %collective-permute-done.20 = f32[56,512]{1,0:T(8,128)S(1)} collective-permute-done((f32[56,512]{1,0:T(8,128)S(1)}, f32[56,512]{1,0:T(8,128)S(1)}, u32[]{:S(2)}, u32[]{:S(2)}) %collective-permute-start.20) | collective-permute-done | bytes 114720 | tf_op jit(solution)/shard_map/ppermute | solution.py:25
  171.8 5.4 %collective-permute-start.23 = (f32[112,512]{1,0:T(8,128)S(1)}, f32[112,512]{1,0:T(8,128)S(1)}, u32[]{:S(2)}, u32[]{:S(2)}) collective-permute-start(f32[112,512]{1,0:T(8,128)S(1)} %pad_maximum_fusion.9), channel_id=1, source_target_pairs={{0,4},{1,5},{2,6},{3,7},{4,0},{5,1},{6,2},{7,3},{8,12},{9,13},{10,... | collective-permute-start | bytes 688136 | tf_op jit(solution)/shard_map/ppermute | solution.py:25
  178.2 2.9 %collective-permute-start.27 = (bf16[512,256]{1,0:T(8,128)(2,1)S(1)}, bf16[512,256]{1,0:T(8,128)(2,1)S(1)}, u32[]{:S(2)}, u32[]{:S(2)}) collective-permute-start(bf16[512,256]{1,0:T(8,128)(2,1)S(1)} %slice.180), channel_id=1, source_target_pairs={{0,12},{1,13},{2,14},{3,15},{4,0},{5,1},{6,2},{7,3},{8,4},{9,5},{1... | collective-permute-start | bytes 786440 | tf_op jit(solution)/shard_map/ppermute | solution.py:19
  187.6 9.2 %collective-permute-start.29 = (bf16[256,256]{1,0:T(8,128)(2,1)S(1)}, bf16[256,256]{1,0:T(8,128)(2,1)S(1)}, u32[]{:S(2)}, u32[]{:S(2)}) collective-permute-start(bf16[256,256]{1,0:T(8,128)(2,1)S(1)} %get-tuple-element.138), channel_id=1, source_target_pairs={{0,12},{1,13},{2,14},{3,15},{4,0},{5,1},{6,2},{7,3},{8,4},{9,5},{1... | collective-permute-start | bytes 393224 | tf_op jit(solution)/shard_map/ppermute | solution.py:19
  198.0 4.6 %collective-permute-start.31 = (bf16[256,256]{1,0:T(8,128)(2,1)S(1)}, bf16[256,256]{1,0:T(8,128)(2,1)S(1)}, u32[]{:S(2)}, u32[]{:S(2)}) collective-permute-start(bf16[256,256]{1,0:T(8,128)(2,1)S(1)} %get-tuple-element.137), channel_id=1, source_target_pairs={{0,12},{1,13},{2,14},{3,15},{4,0},{5,1},{6,2},{7,3},{8,4},{9,5},{1... | collective-permute-start | bytes 393224 | tf_op jit(solution)/shard_map/ppermute | solution.py:19
  202.8 3.8 %collective-permute-start.33 = (bf16[256,256]{1,0:T(8,128)(2,1)S(1)}, bf16[256,256]{1,0:T(8,128)(2,1)S(1)}, u32[]{:S(2)}, u32[]{:S(2)}) collective-permute-start(bf16[256,256]{1,0:T(8,128)(2,1)S(1)} %get-tuple-element.136), channel_id=1, source_target_pairs={{0,12},{1,13},{2,14},{3,15},{4,0},{5,1},{6,2},{7,3},{8,4},{9,5},{1... | collective-permute-start | bytes 393224 | tf_op jit(solution)/shard_map/ppermute | solution.py:19
  206.6 3.8 %collective-permute-start.35 = (bf16[256,256]{1,0:T(8,128)(2,1)S(1)}, bf16[256,256]{1,0:T(8,128)(2,1)S(1)}, u32[]{:S(2)}, u32[]{:S(2)}) collective-permute-start(bf16[256,256]{1,0:T(8,128)(2,1)S(1)} %get-tuple-element.135), channel_id=1, source_target_pairs={{0,12},{1,13},{2,14},{3,15},{4,0},{5,1},{6,2},{7,3},{8,4},{9,5},{1... | collective-permute-start | bytes 393224 | tf_op jit(solution)/shard_map/ppermute | solution.py:19
  212.7 2.7 %collective-permute-done.34 = bf16[256,256]{1,0:T(8,128)(2,1)S(1)} collective-permute-done((bf16[256,256]{1,0:T(8,128)(2,1)S(1)}, bf16[256,256]{1,0:T(8,128)(2,1)S(1)}, u32[]{:S(2)}, u32[]{:S(2)}) %collective-permute-start.34) | collective-permute-done | bytes 131104 | tf_op jit(solution)/shard_map/ppermute | solution.py:19
  215.6 2.5 %collective-permute-done.36 = bf16[256,256]{1,0:T(8,128)(2,1)S(1)} collective-permute-done((bf16[256,256]{1,0:T(8,128)(2,1)S(1)}, bf16[256,256]{1,0:T(8,128)(2,1)S(1)}, u32[]{:S(2)}, u32[]{:S(2)}) %collective-permute-start.36) | collective-permute-done | bytes 131104 | tf_op jit(solution)/shard_map/ppermute | solution.py:19
  218.3 2.2 add_convert_fusion
  (192 shorter events, 63.2 us)
Async XLA Ops:
  2.7 98.3 %collective-permute-start.8 = (bf16[512,256]{1,0:T(8,128)(2,1)}, bf16[512,256]{1,0:T(8,128)(2,1)S(1)}, u32[]{:S(2)}, u32[]{:S(2)}) collective-permute-start(bf16[512,256]{1,0:T(8,128)(2,1)} %get-tuple-element.143), channel_id=1, source_target_pairs={{0,4},{1,5},{2,6},{3,7},{4,8},{5,9},{6,10},{7,11},{8,12},{9,13},{1... | collective-permute-start | bytes 786440 | tf_op jit(solution)/shard_map/ppermute | solution.py:19
  5.7 95.3 %collective-permute-start.9 = (bf16[512,256]{1,0:T(8,128)(2,1)}, bf16[512,256]{1,0:T(8,128)(2,1)S(1)}, u32[]{:S(2)}, u32[]{:S(2)}) collective-permute-start(bf16[512,256]{1,0:T(8,128)(2,1)} %get-tuple-element.143), channel_id=1, source_target_pairs={{0,12},{1,13},{2,14},{3,15},{4,0},{5,1},{6,2},{7,3},{8,4},{9,5},{1... | collective-permute-start | bytes 786440 | tf_op jit(solution)/shard_map/ppermute | solution.py:19
  10.2 21.9 %collective-permute-start = (bf16[1024,256]{1,0:T(8,128)(2,1)}, bf16[1024,256]{1,0:T(8,128)(2,1)}, u32[]{:S(2)}, u32[]{:S(2)}) collective-permute-start(bf16[1024,256]{1,0:T(8,128)(2,1)} %get-tuple-element.141), channel_id=1, source_target_pairs={{0,4},{1,5},{2,6},{3,7},{4,8},{5,9},{6,10},{7,11},{8,12},{9,13},{1... | collective-permute-start | bytes 1572872 | tf_op jit(solution)/shard_map/ppermute | solution.py:19
  10.2 36.6 %collective-permute-start.1 = (bf16[1024,256]{1,0:T(8,128)(2,1)}, bf16[1024,256]{1,0:T(8,128)(2,1)}, u32[]{:S(2)}, u32[]{:S(2)}) collective-permute-start(bf16[1024,256]{1,0:T(8,128)(2,1)} %get-tuple-element.141), channel_id=1, source_target_pairs={{0,12},{1,13},{2,14},{3,15},{4,0},{5,1},{6,2},{7,3},{8,4},{9,5},{1... | collective-permute-start | bytes 1572872 | tf_op jit(solution)/shard_map/ppermute | solution.py:19
  14.1 40.6 %collective-permute-start.2 = (bf16[1024,256]{1,0:T(8,128)(2,1)}, bf16[1024,256]{1,0:T(8,128)(2,1)}, u32[]{:S(2)}, u32[]{:S(2)}) collective-permute-start(bf16[1024,256]{1,0:T(8,128)(2,1)} %get-tuple-element.139), channel_id=1, source_target_pairs={{0,4},{1,5},{2,6},{3,7},{4,8},{5,9},{6,10},{7,11},{8,12},{9,13},{1... | collective-permute-start | bytes 1572872 | tf_op jit(solution)/shard_map/ppermute | solution.py:19
  32.1 35.7 %collective-permute-start.3 = (bf16[1024,256]{1,0:T(8,128)(2,1)}, bf16[1024,256]{1,0:T(8,128)(2,1)S(1)}, u32[]{:S(2)}, u32[]{:S(2)}) collective-permute-start(bf16[1024,256]{1,0:T(8,128)(2,1)} %get-tuple-element.139), channel_id=1, source_target_pairs={{0,12},{1,13},{2,14},{3,15},{4,0},{5,1},{6,2},{7,3},{8,4},{9,5},{1... | collective-permute-start | bytes 1572872 | tf_op jit(solution)/shard_map/ppermute | solution.py:19
  46.9 35.4 %collective-permute-start.4 = (bf16[1024,256]{1,0:T(8,128)(2,1)S(1)}, bf16[1024,256]{1,0:T(8,128)(2,1)S(1)}, u32[]{:S(2)}, u32[]{:S(2)}) collective-permute-start(bf16[1024,256]{1,0:T(8,128)(2,1)S(1)} %copy-done.12), channel_id=1, source_target_pairs={{0,4},{1,5},{2,6},{3,7},{4,8},{5,9},{6,10},{7,11},{8,12},{9,13},{1... | collective-permute-start | bytes 1572872 | tf_op jit(solution)/shard_map/ppermute | solution.py:19
  54.6 35.5 %collective-permute-start.5 = (bf16[1024,256]{1,0:T(8,128)(2,1)S(1)}, bf16[1024,256]{1,0:T(8,128)(2,1)S(1)}, u32[]{:S(2)}, u32[]{:S(2)}) collective-permute-start(bf16[1024,256]{1,0:T(8,128)(2,1)S(1)} %copy-done.12), channel_id=1, source_target_pairs={{0,12},{1,13},{2,14},{3,15},{4,0},{5,1},{6,2},{7,3},{8,4},{9,5},{1... | collective-permute-start | bytes 1572872 | tf_op jit(solution)/shard_map/ppermute | solution.py:19
  67.8 27.0 %collective-permute-start.6 = (bf16[512,256]{1,0:T(8,128)(2,1)S(1)}, bf16[512,256]{1,0:T(8,128)(2,1)S(1)}, u32[]{:S(2)}, u32[]{:S(2)}) collective-permute-start(bf16[512,256]{1,0:T(8,128)(2,1)S(1)} %copy-done.13), channel_id=1, source_target_pairs={{0,4},{1,5},{2,6},{3,7},{4,8},{5,9},{6,10},{7,11},{8,12},{9,13},{1... | collective-permute-start | bytes 786440 | tf_op jit(solution)/shard_map/ppermute | solution.py:19
  82.3 15.6 %collective-permute-start.7 = (bf16[512,256]{1,0:T(8,128)(2,1)S(1)}, bf16[512,256]{1,0:T(8,128)(2,1)S(1)}, u32[]{:S(2)}, u32[]{:S(2)}) collective-permute-start(bf16[512,256]{1,0:T(8,128)(2,1)S(1)} %copy-done.13), channel_id=1, source_target_pairs={{0,12},{1,13},{2,14},{3,15},{4,0},{5,1},{6,2},{7,3},{8,4},{9,5},{1... | collective-permute-start | bytes 786440 | tf_op jit(solution)/shard_map/ppermute | solution.py:19
  105.9 10.8 %collective-permute-start.10 = (f32[229376]{0:T(1024)S(1)}, f32[229376]{0:T(1024)S(1)}, u32[]{:S(2)}, u32[]{:S(2)}) collective-permute-start(f32[229376]{0:T(1024)S(1)} %dynamic_slice.25), channel_id=1, source_target_pairs={{0,1},{1,0},{2,3},{3,2},{4,5},{5,4},{6,7},{7,6},{8,9},{9,8},{10,11... | collective-permute-start | bytes 2752520 | tf_op jit(solution)/shard_map/ppermute | solution.py:25
  106.0 23.0 %collective-permute-start.12 = (bf16[512,256]{1,0:T(8,128)(2,1)S(1)}, bf16[512,256]{1,0:T(8,128)(2,1)S(1)}, u32[]{:S(2)}, u32[]{:S(2)}) collective-permute-start(bf16[512,256]{1,0:T(8,128)(2,1)S(1)} %get-tuple-element.155), channel_id=1, source_target_pairs={{0,12},{1,13},{2,14},{3,15},{4,0},{5,1},{6,2},{7,3},{8,4},{9,5},{1... | collective-permute-start | bytes 786440 | tf_op jit(solution)/shard_map/ppermute | solution.py:19
  108.4 20.6 %collective-permute-start.13 = (bf16[512,256]{1,0:T(8,128)(2,1)S(1)}, bf16[512,256]{1,0:T(8,128)(2,1)S(1)}, u32[]{:S(2)}, u32[]{:S(2)}) collective-permute-start(bf16[512,256]{1,0:T(8,128)(2,1)S(1)} %get-tuple-element.153), channel_id=1, source_target_pairs={{0,4},{1,5},{2,6},{3,7},{4,8},{5,9},{6,10},{7,11},{8,12},{9,13},{1... | collective-permute-start | bytes 786440 | tf_op jit(solution)/shard_map/ppermute | solution.py:19
  108.5 20.6 %collective-permute-start.14 = (bf16[512,256]{1,0:T(8,128)(2,1)S(1)}, bf16[512,256]{1,0:T(8,128)(2,1)S(1)}, u32[]{:S(2)}, u32[]{:S(2)}) collective-permute-start(bf16[512,256]{1,0:T(8,128)(2,1)S(1)} %get-tuple-element.154), channel_id=1, source_target_pairs={{0,12},{1,13},{2,14},{3,15},{4,0},{5,1},{6,2},{7,3},{8,4},{9,5},{1... | collective-permute-start | bytes 786440 | tf_op jit(solution)/shard_map/ppermute | solution.py:19
  112.3 20.2 %collective-permute-start.15 = (bf16[512,256]{1,0:T(8,128)(2,1)S(1)}, bf16[512,256]{1,0:T(8,128)(2,1)S(1)}, u32[]{:S(2)}, u32[]{:S(2)}) collective-permute-start(bf16[512,256]{1,0:T(8,128)(2,1)S(1)} %get-tuple-element.152), channel_id=1, source_target_pairs={{0,4},{1,5},{2,6},{3,7},{4,8},{5,9},{6,10},{7,11},{8,12},{9,13},{1... | collective-permute-start | bytes 786440 | tf_op jit(solution)/shard_map/ppermute | solution.py:19
  116.8 12.1 %collective-permute-start.11 = (f32[114688]{0:T(1024)S(1)}, f32[114688]{0:T(1024)S(1)}, u32[]{:S(2)}, u32[]{:S(2)}) collective-permute-start(f32[114688]{0:T(1024)S(1)} %dynamic_slice.27), channel_id=1, source_target_pairs={{0,2},{1,3},{2,0},{3,1},{4,6},{5,7},{6,4},{7,5},{8,10},{9,11},{10,... | collective-permute-start | bytes 1376264 | tf_op jit(solution)/shard_map/ppermute | solution.py:25
  134.8 20.6 %collective-permute-start.18 = (bf16[512,256]{1,0:T(8,128)(2,1)}, bf16[512,256]{1,0:T(8,128)(2,1)S(1)}, u32[]{:S(2)}, u32[]{:S(2)}) collective-permute-start(bf16[512,256]{1,0:T(8,128)(2,1)} %slice.174), channel_id=1, source_target_pairs={{0,12},{1,13},{2,14},{3,15},{4,0},{5,1},{6,2},{7,3},{8,4},{9,5},{1... | collective-permute-start | bytes 786440 | tf_op jit(solution)/shard_map/ppermute | solution.py:19
  137.0 18.5 %collective-permute-start.19 = (bf16[512,256]{1,0:T(8,128)(2,1)}, bf16[512,256]{1,0:T(8,128)(2,1)}, u32[]{:S(2)}, u32[]{:S(2)}) collective-permute-start(bf16[512,256]{1,0:T(8,128)(2,1)} %slice.175), channel_id=1, source_target_pairs={{0,4},{1,5},{2,6},{3,7},{4,8},{5,9},{6,10},{7,11},{8,12},{9,13},{1... | collective-permute-start | bytes 786440 | tf_op jit(solution)/shard_map/ppermute | solution.py:19
  141.1 14.3 %collective-permute-start.17 = (f32[28672]{0:T(1024)S(1)}, f32[28672]{0:T(1024)S(1)}, u32[]{:S(2)}, u32[]{:S(2)}) collective-permute-start(f32[28672]{0:T(1024)S(1)} %dynamic_slice.31), channel_id=1, source_target_pairs={{0,8},{1,9},{2,10},{3,11},{4,12},{5,13},{6,14},{7,15},{8,0},{9,1},... | collective-permute-start | bytes 344072 | tf_op jit(solution)/shard_map/ppermute | solution.py:25
  144.2 27.6 %collective-permute-start.21 = (bf16[512,256]{1,0:T(8,128)(2,1)}, bf16[512,256]{1,0:T(8,128)(2,1)S(1)}, u32[]{:S(2)}, u32[]{:S(2)}) collective-permute-start(bf16[512,256]{1,0:T(8,128)(2,1)} %slice.176), channel_id=1, source_target_pairs={{0,12},{1,13},{2,14},{3,15},{4,0},{5,1},{6,2},{7,3},{8,4},{9,5},{1... | collective-permute-start | bytes 786440 | tf_op jit(solution)/shard_map/ppermute | solution.py:19
  147.3 24.6 %collective-permute-start.22 = (bf16[512,256]{1,0:T(8,128)(2,1)}, bf16[512,256]{1,0:T(8,128)(2,1)}, u32[]{:S(2)}, u32[]{:S(2)}) collective-permute-start(bf16[512,256]{1,0:T(8,128)(2,1)} %slice.177), channel_id=1, source_target_pairs={{0,4},{1,5},{2,6},{3,7},{4,8},{5,9},{6,10},{7,11},{8,12},{9,13},{1... | collective-permute-start | bytes 786440 | tf_op jit(solution)/shard_map/ppermute | solution.py:19
  155.5 16.3 %collective-permute-start.20 = (f32[56,512]{1,0:T(8,128)S(1)}, f32[56,512]{1,0:T(8,128)S(1)}, u32[]{:S(2)}, u32[]{:S(2)}) collective-permute-start(f32[56,512]{1,0:T(8,128)S(1)} %reshape.20), channel_id=1, source_target_pairs={{0,8},{1,9},{2,10},{3,11},{4,12},{5,13},{6,14},{7,15},{8,0},{9,1},... | collective-permute-start | bytes 344072 | tf_op jit(solution)/shard_map/ppermute | solution.py:25
  158.4 26.5 %collective-permute-start.24 = (bf16[512,256]{1,0:T(8,128)(2,1)S(1)}, bf16[512,256]{1,0:T(8,128)(2,1)S(1)}, u32[]{:S(2)}, u32[]{:S(2)}) collective-permute-start(bf16[512,256]{1,0:T(8,128)(2,1)S(1)} %slice.178), channel_id=1, source_target_pairs={{0,12},{1,13},{2,14},{3,15},{4,0},{5,1},{6,2},{7,3},{8,4},{9,5},{1... | collective-permute-start | bytes 786440 | tf_op jit(solution)/shard_map/ppermute | solution.py:19
  165.9 19.0 %collective-permute-start.25 = (bf16[512,256]{1,0:T(8,128)(2,1)S(1)}, bf16[512,256]{1,0:T(8,128)(2,1)S(1)}, u32[]{:S(2)}, u32[]{:S(2)}) collective-permute-start(bf16[512,256]{1,0:T(8,128)(2,1)S(1)} %slice.179), channel_id=1, source_target_pairs={{0,4},{1,5},{2,6},{3,7},{4,8},{5,9},{6,10},{7,11},{8,12},{9,13},{1... | collective-permute-start | bytes 786440 | tf_op jit(solution)/shard_map/ppermute | solution.py:19
  171.8 13.0 %collective-permute-start.23 = (f32[112,512]{1,0:T(8,128)S(1)}, f32[112,512]{1,0:T(8,128)S(1)}, u32[]{:S(2)}, u32[]{:S(2)}) collective-permute-start(f32[112,512]{1,0:T(8,128)S(1)} %pad_maximum_fusion.9), channel_id=1, source_target_pairs={{0,4},{1,5},{2,6},{3,7},{4,0},{5,1},{6,2},{7,3},{8,12},{9,13},{10,... | collective-permute-start | bytes 688136 | tf_op jit(solution)/shard_map/ppermute | solution.py:25
  178.2 24.5 %collective-permute-start.27 = (bf16[512,256]{1,0:T(8,128)(2,1)S(1)}, bf16[512,256]{1,0:T(8,128)(2,1)S(1)}, u32[]{:S(2)}, u32[]{:S(2)}) collective-permute-start(bf16[512,256]{1,0:T(8,128)(2,1)S(1)} %slice.180), channel_id=1, source_target_pairs={{0,12},{1,13},{2,14},{3,15},{4,0},{5,1},{6,2},{7,3},{8,4},{9,5},{1... | collective-permute-start | bytes 786440 | tf_op jit(solution)/shard_map/ppermute | solution.py:19
  182.1 20.7 %collective-permute-start.28 = (bf16[512,256]{1,0:T(8,128)(2,1)S(1)}, bf16[512,256]{1,0:T(8,128)(2,1)S(1)}, u32[]{:S(2)}, u32[]{:S(2)}) collective-permute-start(bf16[512,256]{1,0:T(8,128)(2,1)S(1)} %slice.181), channel_id=1, source_target_pairs={{0,4},{1,5},{2,6},{3,7},{4,8},{5,9},{6,10},{7,11},{8,12},{9,13},{1... | collective-permute-start | bytes 786440 | tf_op jit(solution)/shard_map/ppermute | solution.py:19
  184.9 13.1 %collective-permute-start.26 = (f32[224,512]{1,0:T(8,128)S(1)}, f32[224,512]{1,0:T(8,128)S(1)}, u32[]{:S(2)}, u32[]{:S(2)}) collective-permute-start(f32[224,512]{1,0:T(8,128)S(1)} %pad_maximum_fusion.8), channel_id=1, source_target_pairs={{0,2},{1,3},{2,0},{3,1},{4,6},{5,7},{6,4},{7,5},{8,10},{9,11},{10,... | collective-permute-start | bytes 1376264 | tf_op jit(solution)/shard_map/ppermute | solution.py:25
  187.6 19.0 %collective-permute-start.29 = (bf16[256,256]{1,0:T(8,128)(2,1)S(1)}, bf16[256,256]{1,0:T(8,128)(2,1)S(1)}, u32[]{:S(2)}, u32[]{:S(2)}) collective-permute-start(bf16[256,256]{1,0:T(8,128)(2,1)S(1)} %get-tuple-element.138), channel_id=1, source_target_pairs={{0,12},{1,13},{2,14},{3,15},{4,0},{5,1},{6,2},{7,3},{8,4},{9,5},{1... | collective-permute-start | bytes 393224 | tf_op jit(solution)/shard_map/ppermute | solution.py:19
  198.0 12.4 %collective-permute-start.31 = (bf16[256,256]{1,0:T(8,128)(2,1)S(1)}, bf16[256,256]{1,0:T(8,128)(2,1)S(1)}, u32[]{:S(2)}, u32[]{:S(2)}) collective-permute-start(bf16[256,256]{1,0:T(8,128)(2,1)S(1)} %get-tuple-element.137), channel_id=1, source_target_pairs={{0,12},{1,13},{2,14},{3,15},{4,0},{5,1},{6,2},{7,3},{8,4},{9,5},{1... | collective-permute-start | bytes 393224 | tf_op jit(solution)/shard_map/ppermute | solution.py:19
  202.7 9.3 %collective-permute-start.32 = (bf16[256,256]{1,0:T(8,128)(2,1)S(1)}, bf16[256,256]{1,0:T(8,128)(2,1)S(1)}, u32[]{:S(2)}, u32[]{:S(2)}) collective-permute-start(bf16[256,256]{1,0:T(8,128)(2,1)S(1)} %get-tuple-element.133), channel_id=1, source_target_pairs={{0,4},{1,5},{2,6},{3,7},{4,8},{5,9},{6,10},{7,11},{8,12},{9,13},{1... | collective-permute-start | bytes 393224 | tf_op jit(solution)/shard_map/ppermute | solution.py:19
  202.8 9.9 %collective-permute-start.33 = (bf16[256,256]{1,0:T(8,128)(2,1)S(1)}, bf16[256,256]{1,0:T(8,128)(2,1)S(1)}, u32[]{:S(2)}, u32[]{:S(2)}) collective-permute-start(bf16[256,256]{1,0:T(8,128)(2,1)S(1)} %get-tuple-element.136), channel_id=1, source_target_pairs={{0,12},{1,13},{2,14},{3,15},{4,0},{5,1},{6,2},{7,3},{8,4},{9,5},{1... | collective-permute-start | bytes 393224 | tf_op jit(solution)/shard_map/ppermute | solution.py:19
  (20 other events, 312.1 us)

commit v18 on v11

--- a/solution.py
+++ b/solution.py
@@ -9,7 +9,7 @@
 CHUNK_EIGHTHS = (2, 2, 2, 1, 1)
 EARLY = 1
 RIDER_ROWS = 512
-RIDER_SPAN = 2
+RIDER_SPANS = (1, 2, 2, 2)
 
 
 def from_behind(value, axis, steps):
@@ -132,6 +132,7 @@
     sent_rows = bounds[EARLY]
     pending = []
     late = []
+    riders_sent = 0
     for number, (bit, down) in enumerate(steps):
         if down and bit == 4:
             buf, early = lax.optimization_barrier((buf, early))
@@ -142,7 +143,9 @@
             pending = [item for item in pending if item[1] > number]
         if (bit, down) in rider_steps and sent_rows + RIDER_ROWS <= positions:
             buf, pieces = lax.optimization_barrier((buf, (lower_all, upper_all)))
-            pending.append((send_rows(pieces, sent_rows, sent_rows + RIDER_ROWS), number + RIDER_SPAN))
+            span = RIDER_SPANS[min(riders_sent, len(RIDER_SPANS) - 1)]
+            riders_sent += 1
+            pending.append((send_rows(pieces, sent_rows, sent_rows + RIDER_ROWS), number + span))
             sent_rows += RIDER_ROWS
         if not down and bit == 2 and not late:
             buf, pieces = lax.optimization_barrier((buf, (lower_all, upper_all)))

time: 223 us -> 230 us (1.031)
  waiting for transfers between devices: 62.6 us -> 73 us
  starting transfers between devices: 99.4 us -> 92.8 us
    ppermute x26, waiting for transfers between devices: 36.8 us -> 46.9 us  [from_behind(): return lax.ppermute(value, axis, pairs)]
    ppermute x8, starting transfers between devices: 14 us -> 7.02 us  [exchange(): return lax.ppermute(value, axis, pairs)]
  transfers between devices with their start and end apart: 34 -> 34, of which waited for: 14 -> 15; matrix products, arithmetic and copies ran while one was open for 22% -> 23% of each run, Pallas kernels for 0% -> 0%
where the time goes in v18:
time: 230 us; the launch traced here: 229 us
  starting transfers between devices  92.8 us (40%)
  waiting for transfers between devices  73 us (32%)
  matrix products  33.5 us (15%)
  local copies, waits for them, and re-layouts  20.6 us (9%)
  other arithmetic  7.35 us (3%)
    ppermute x26, starting transfers between devices, from_behind(): return lax.ppermute(value, axis, pairs)  85.8 us
    ppermute x26, waiting for transfers between devices, from_behind(): return lax.ppermute(value, axis, pairs)  46.9 us
    ppermute x8, waiting for transfers between devices, exchange(): return lax.ppermute(value, axis, pairs)  26.1 us
    ppermute x8, starting transfers between devices, exchange(): return lax.ppermute(value, axis, pairs)  7.02 us
    unnamed x44, local copies, waits for them, and re-layouts  6.9 us
    dot_general x5, matrix products, chunk_layer(): preact = preact + jnp.dot(middle, w_mid, preferred_element_type=jnp.float32)  4.65 us
  transfers between devices with their start and end apart: 34, of which 15 were waited for; matrix products, arithmetic and copies ran while one was open for 23% of the time, Pallas kernels for 0%

profile of v18, /device:TPU:0, one launch (start us, length us, event | category | flops | bytes accessed | tf_op | source)
XLA Modules:
  0.0 229.1 jit_solution(15427260948715682783)
XLA Ops:
  0.7 2.0 fusion.119
  2.7 3.0 %collective-permute-start.8 = (bf16[512,256]{1,0:T(8,128)(2,1)}, bf16[512,256]{1,0:T(8,128)(2,1)S(1)}, u32[]{:S(2)}, u32[]{:S(2)}) collective-permute-start(bf16[512,256]{1,0:T(8,128)(2,1)} %get-tuple-element.131), channel_id=1, source_target_pairs={{0,4},{1,5},{2,6},{3,7},{4,8},{5,9},{6,10},{7,11},{8,12},{9,13},{1... | collective-permute-start | bytes 786440 | tf_op jit(solution)/shard_map/ppermute | solution.py:18
  5.7 2.0 collective-permute-start.9
  7.7 2.5 %fusion.118 = (bf16[1024,256]{1,0:T(8,128)(2,1)}, bf16[1024,256]{1,0:T(8,128)(2,1)}, bf16[1024,256]{1,0:T(8,128)(2,1)}) fusion(bf16[4096,256]{1,0:T(8,128)(2,1)} %param.4), kind=kLoop, calls=%fused_computation.208 | loop fusion | bytes 3145728 | tf_op jit(solution)/shard_map/slice | solution.py:95
  10.2 3.8 %collective-permute-start.1 = (bf16[1024,256]{1,0:T(8,128)(2,1)}, bf16[1024,256]{1,0:T(8,128)(2,1)}, u32[]{:S(2)}, u32[]{:S(2)}) collective-permute-start(bf16[1024,256]{1,0:T(8,128)(2,1)} %get-tuple-element.129), channel_id=1, source_target_pairs={{0,12},{1,13},{2,14},{3,15},{4,0},{5,1},{6,2},{7,3},{8,4},{9,5},{1... | collective-permute-start | bytes 1572872 | tf_op jit(solution)/shard_map/ppermute | solution.py:18
  14.1 1.8 fusion.77
  18.6 13.5 %collective-permute-done = bf16[1024,256]{1,0:T(8,128)(2,1)} collective-permute-done((bf16[1024,256]{1,0:T(8,128)(2,1)}, bf16[1024,256]{1,0:T(8,128)(2,1)}, u32[]{:S(2)}, u32[]{:S(2)}) %collective-permute-start) | collective-permute-done | bytes 524320 | tf_op jit(solution)/shard_map/ppermute | solution.py:18
  32.1 13.2 %collective-permute-start.3 = (bf16[1024,256]{1,0:T(8,128)(2,1)}, bf16[1024,256]{1,0:T(8,128)(2,1)S(1)}, u32[]{:S(2)}, u32[]{:S(2)}) collective-permute-start(bf16[1024,256]{1,0:T(8,128)(2,1)} %get-tuple-element.127), channel_id=1, source_target_pairs={{0,12},{1,13},{2,14},{3,15},{4,0},{5,1},{6,2},{7,3},{8,4},{9,5},{1... | collective-permute-start | bytes 1572872 | tf_op jit(solution)/shard_map/ppermute | solution.py:18
  54.6 13.2 %collective-permute-start.5 = (bf16[1024,256]{1,0:T(8,128)(2,1)S(1)}, bf16[1024,256]{1,0:T(8,128)(2,1)S(1)}, u32[]{:S(2)}, u32[]{:S(2)}) collective-permute-start(bf16[1024,256]{1,0:T(8,128)(2,1)S(1)} %copy-done.11), channel_id=1, source_target_pairs={{0,12},{1,13},{2,14},{3,15},{4,0},{5,1},{6,2},{7,3},{8,4},{9,5},{1... | collective-permute-start | bytes 1572872 | tf_op jit(solution)/shard_map/ppermute | solution.py:18
  67.8 8.3 %collective-permute-start.6 = (bf16[512,256]{1,0:T(8,128)(2,1)S(1)}, bf16[512,256]{1,0:T(8,128)(2,1)S(1)}, u32[]{:S(2)}, u32[]{:S(2)}) collective-permute-start(bf16[512,256]{1,0:T(8,128)(2,1)S(1)} %copy-done.13), channel_id=1, source_target_pairs={{0,4},{1,5},{2,6},{3,7},{4,8},{5,9},{6,10},{7,11},{8,12},{9,13},{1... | collective-permute-start | bytes 786440 | tf_op jit(solution)/shard_map/ppermute | solution.py:18
  82.3 7.8 %collective-permute-start.7 = (bf16[512,256]{1,0:T(8,128)(2,1)S(1)}, bf16[512,256]{1,0:T(8,128)(2,1)S(1)}, u32[]{:S(2)}, u32[]{:S(2)}) collective-permute-start(bf16[512,256]{1,0:T(8,128)(2,1)S(1)} %copy-done.13), channel_id=1, source_target_pairs={{0,12},{1,13},{2,14},{3,15},{4,0},{5,1},{6,2},{7,3},{8,4},{9,5},{1... | collective-permute-start | bytes 786440 | tf_op jit(solution)/shard_map/ppermute | solution.py:18
  94.8 3.1 %collective-permute-done.7 = bf16[512,256]{1,0:T(8,128)(2,1)S(1)} collective-permute-done((bf16[512,256]{1,0:T(8,128)(2,1)S(1)}, bf16[512,256]{1,0:T(8,128)(2,1)S(1)}, u32[]{:S(2)}, u32[]{:S(2)}) %collective-permute-start.7) | collective-permute-done | bytes 262176 | tf_op jit(solution)/shard_map/ppermute | solution.py:18
  106.0 2.4 %collective-permute-start.12 = (bf16[512,256]{1,0:T(8,128)(2,1)S(1)}, bf16[512,256]{1,0:T(8,128)(2,1)S(1)}, u32[]{:S(2)}, u32[]{:S(2)}) collective-permute-start(bf16[512,256]{1,0:T(8,128)(2,1)S(1)} %get-tuple-element.143), channel_id=1, source_target_pairs={{0,12},{1,13},{2,14},{3,15},{4,0},{5,1},{6,2},{7,3},{8,4},{9,5},{1... | collective-permute-start | bytes 786440 | tf_op jit(solution)/shard_map/ppermute | solution.py:18
  108.5 3.8 %collective-permute-start.14 = (bf16[512,256]{1,0:T(8,128)(2,1)S(1)}, bf16[512,256]{1,0:T(8,128)(2,1)S(1)}, u32[]{:S(2)}, u32[]{:S(2)}) collective-permute-start(bf16[512,256]{1,0:T(8,128)(2,1)S(1)} %get-tuple-element.142), channel_id=1, source_target_pairs={{0,12},{1,13},{2,14},{3,15},{4,0},{5,1},{6,2},{7,3},{8,4},{9,5},{1... | collective-permute-start | bytes 786440 | tf_op jit(solution)/shard_map/ppermute | solution.py:18
  119.1 9.9 %collective-permute-done.11 = f32[114688]{0:T(1024)S(1)} collective-permute-done((f32[114688]{0:T(1024)S(1)}, f32[114688]{0:T(1024)S(1)}, u32[]{:S(2)}, u32[]{:S(2)}) %collective-permute-start.11) | collective-permute-done | bytes 458784 | tf_op jit(solution)/shard_map/ppermute | solution.py:24
  129.0 3.4 %collective-permute-done.15 = bf16[512,256]{1,0:T(8,128)(2,1)S(1)} collective-permute-done((bf16[512,256]{1,0:T(8,128)(2,1)S(1)}, bf16[512,256]{1,0:T(8,128)(2,1)S(1)}, u32[]{:S(2)}, u32[]{:S(2)}) %collective-permute-start.15) | collective-permute-done | bytes 262176 | tf_op jit(solution)/shard_map/ppermute | solution.py:18
  137.8 3.3 %collective-permute-done.16 = f32[57344]{0:T(1024)S(1)} collective-permute-done((f32[57344]{0:T(1024)S(1)}, f32[57344]{0:T(1024)S(1)}, u32[]{:S(2)}, u32[]{:S(2)}) %collective-permute-start.16) | collective-permute-done | bytes 229408 | tf_op jit(solution)/shard_map/ppermute | solution.py:24
  141.1 5.2 %collective-permute-done.17 = bf16[512,256]{1,0:T(8,128)(2,1)S(1)} collective-permute-done((bf16[512,256]{1,0:T(8,128)(2,1)S(1)}, bf16[512,256]{1,0:T(8,128)(2,1)S(1)}, u32[]{:S(2)}, u32[]{:S(2)}) %collective-permute-start.17) | collective-permute-done | bytes 262176 | tf_op jit(solution)/shard_map/ppermute | solution.py:18
  146.3 5.4 %collective-permute-done.18 = bf16[512,256]{1,0:T(8,128)(2,1)S(1)} collective-permute-done((bf16[512,256]{1,0:T(8,128)(2,1)S(1)}, bf16[512,256]{1,0:T(8,128)(2,1)S(1)}, u32[]{:S(2)}, u32[]{:S(2)}) %collective-permute-start.18) | collective-permute-done | bytes 262176 | tf_op jit(solution)/shard_map/ppermute | solution.py:18
  152.5 3.3 %collective-permute-start.21 = (bf16[512,256]{1,0:T(8,128)(2,1)}, bf16[512,256]{1,0:T(8,128)(2,1)S(1)}, u32[]{:S(2)}, u32[]{:S(2)}) collective-permute-start(bf16[512,256]{1,0:T(8,128)(2,1)} %slice.164), channel_id=1, source_target_pairs={{0,12},{1,13},{2,14},{3,15},{4,0},{5,1},{6,2},{7,3},{8,4},{9,5},{1... | collective-permute-start | bytes 786440 | tf_op jit(solution)/shard_map/ppermute | solution.py:18
  157.2 2.7 %collective-permute-done.19 = f32[28672]{0:T(1024)S(1)} collective-permute-done((f32[28672]{0:T(1024)S(1)}, f32[28672]{0:T(1024)S(1)}, u32[]{:S(2)}, u32[]{:S(2)}) %collective-permute-start.19) | collective-permute-done | bytes 114720 | tf_op jit(solution)/shard_map/ppermute | solution.py:24
  162.1 5.8 %collective-permute-start.24 = (bf16[512,256]{1,0:T(8,128)(2,1)S(1)}, bf16[512,256]{1,0:T(8,128)(2,1)S(1)}, u32[]{:S(2)}, u32[]{:S(2)}) collective-permute-start(bf16[512,256]{1,0:T(8,128)(2,1)S(1)} %slice.166), channel_id=1, source_target_pairs={{0,12},{1,13},{2,14},{3,15},{4,0},{5,1},{6,2},{7,3},{8,4},{9,5},{1... | collective-permute-start | bytes 786440 | tf_op jit(solution)/shard_map/ppermute | solution.py:18
  169.4 8.3 %collective-permute-done.20 = f32[56,512]{1,0:T(8,128)S(1)} collective-permute-done((f32[56,512]{1,0:T(8,128)S(1)}, f32[56,512]{1,0:T(8,128)S(1)}, u32[]{:S(2)}, u32[]{:S(2)}) %collective-permute-start.20) | collective-permute-done | bytes 114720 | tf_op jit(solution)/shard_map/ppermute | solution.py:24
  177.8 2.0 collective-permute-start.23
  180.8 2.9 %collective-permute-start.27 = (bf16[512,256]{1,0:T(8,128)(2,1)S(1)}, bf16[512,256]{1,0:T(8,128)(2,1)S(1)}, u32[]{:S(2)}, u32[]{:S(2)}) collective-permute-start(bf16[512,256]{1,0:T(8,128)(2,1)S(1)} %slice.168), channel_id=1, source_target_pairs={{0,12},{1,13},{2,14},{3,15},{4,0},{5,1},{6,2},{7,3},{8,4},{9,5},{1... | collective-permute-start | bytes 786440 | tf_op jit(solution)/shard_map/ppermute | solution.py:18
  185.5 1.8 collective-permute-done.23
  190.1 9.5 %collective-permute-start.29 = (bf16[512,256]{1,0:T(8,128)(2,1)S(1)}, bf16[512,256]{1,0:T(8,128)(2,1)S(1)}, u32[]{:S(2)}, u32[]{:S(2)}) collective-permute-start(bf16[512,256]{1,0:T(8,128)(2,1)S(1)} %get-tuple-element.126), channel_id=1, source_target_pairs={{0,12},{1,13},{2,14},{3,15},{4,0},{5,1},{6,2},{7,3},{8,4},{9,5},{1... | collective-permute-start | bytes 786440 | tf_op jit(solution)/shard_map/ppermute | solution.py:18
  201.4 3.9 %collective-permute-start.31 = (bf16[512,256]{1,0:T(8,128)(2,1)S(1)}, bf16[512,256]{1,0:T(8,128)(2,1)S(1)}, u32[]{:S(2)}, u32[]{:S(2)}) collective-permute-start(bf16[512,256]{1,0:T(8,128)(2,1)S(1)} %get-tuple-element.125), channel_id=1, source_target_pairs={{0,12},{1,13},{2,14},{3,15},{4,0},{5,1},{6,2},{7,3},{8,4},{9,5},{1... | collective-permute-start | bytes 786440 | tf_op jit(solution)/shard_map/ppermute | solution.py:18
  207.2 5.2 %collective-permute-done.30 = bf16[512,256]{1,0:T(8,128)(2,1)S(1)} collective-permute-done((bf16[512,256]{1,0:T(8,128)(2,1)S(1)}, bf16[512,256]{1,0:T(8,128)(2,1)S(1)}, u32[]{:S(2)}, u32[]{:S(2)}) %collective-permute-start.30) | collective-permute-done | bytes 262176 | tf_op jit(solution)/shard_map/ppermute | solution.py:18
  212.4 4.8 %collective-permute-done.31 = bf16[512,256]{1,0:T(8,128)(2,1)S(1)} collective-permute-done((bf16[512,256]{1,0:T(8,128)(2,1)S(1)}, bf16[512,256]{1,0:T(8,128)(2,1)S(1)}, u32[]{:S(2)}, u32[]{:S(2)}) %collective-permute-start.31) | collective-permute-done | bytes 262176 | tf_op jit(solution)/shard_map/ppermute | solution.py:18
  217.2 3.6 %collective-permute-done.32 = bf16[512,256]{1,0:T(8,128)(2,1)S(1)} collective-permute-done((bf16[512,256]{1,0:T(8,128)(2,1)S(1)}, bf16[512,256]{1,0:T(8,128)(2,1)S(1)}, u32[]{:S(2)}, u32[]{:S(2)}) %collective-permute-start.32) | collective-permute-done | bytes 262176 | tf_op jit(solution)/shard_map/ppermute | solution.py:18
  223.0 3.8 %add_convert_fusion = bf16[4096,256]{1,0:T(8,128)(2,1)} fusion(bf16[4096,256]{1,0:T(8,128)(2,1)} %constant_dynamic-update-slice_fusion.11, bf16[4096,256]{1,0:T(8,128)(2,1)S(1)} %constant_dynamic-update-slice_fusion.3, f32[4096,256]{1,0:T(8,128)S(1)} %copy-done.6, bf16[4096,256]{1,0:T(8,128)(2,1)S(1)} %copy-done.8), kind=kLoop, calls=%fused_computation | loop fusion | flops 7340032 | bytes 12582912 | tf_op jit(solution)/shard_map/convert_element_type | solution.py:171
  (180 shorter events, 62.1 us)
Async XLA Ops:
  2.7 98.3 %collective-permute-start.8 = (bf16[512,256]{1,0:T(8,128)(2,1)}, bf16[512,256]{1,0:T(8,128)(2,1)S(1)}, u32[]{:S(2)}, u32[]{:S(2)}) collective-permute-start(bf16[512,256]{1,0:T(8,128)(2,1)} %get-tuple-element.131), channel_id=1, source_target_pairs={{0,4},{1,5},{2,6},{3,7},{4,8},{5,9},{6,10},{7,11},{8,12},{9,13},{1... | collective-permute-start | bytes 786440 | tf_op jit(solution)/shard_map/ppermute | solution.py:18
  5.7 95.3 %collective-permute-start.9 = (bf16[512,256]{1,0:T(8,128)(2,1)}, bf16[512,256]{1,0:T(8,128)(2,1)S(1)}, u32[]{:S(2)}, u32[]{:S(2)}) collective-permute-start(bf16[512,256]{1,0:T(8,128)(2,1)} %get-tuple-element.131), channel_id=1, source_target_pairs={{0,12},{1,13},{2,14},{3,15},{4,0},{5,1},{6,2},{7,3},{8,4},{9,5},{1... | collective-permute-start | bytes 786440 | tf_op jit(solution)/shard_map/ppermute | solution.py:18
  10.2 21.9 %collective-permute-start = (bf16[1024,256]{1,0:T(8,128)(2,1)}, bf16[1024,256]{1,0:T(8,128)(2,1)}, u32[]{:S(2)}, u32[]{:S(2)}) collective-permute-start(bf16[1024,256]{1,0:T(8,128)(2,1)} %get-tuple-element.129), channel_id=1, source_target_pairs={{0,4},{1,5},{2,6},{3,7},{4,8},{5,9},{6,10},{7,11},{8,12},{9,13},{1... | collective-permute-start | bytes 1572872 | tf_op jit(solution)/shard_map/ppermute | solution.py:18
  10.2 36.6 %collective-permute-start.1 = (bf16[1024,256]{1,0:T(8,128)(2,1)}, bf16[1024,256]{1,0:T(8,128)(2,1)}, u32[]{:S(2)}, u32[]{:S(2)}) collective-permute-start(bf16[1024,256]{1,0:T(8,128)(2,1)} %get-tuple-element.129), channel_id=1, source_target_pairs={{0,12},{1,13},{2,14},{3,15},{4,0},{5,1},{6,2},{7,3},{8,4},{9,5},{1... | collective-permute-start | bytes 1572872 | tf_op jit(solution)/shard_map/ppermute | solution.py:18
  14.1 40.6 %collective-permute-start.2 = (bf16[1024,256]{1,0:T(8,128)(2,1)}, bf16[1024,256]{1,0:T(8,128)(2,1)}, u32[]{:S(2)}, u32[]{:S(2)}) collective-permute-start(bf16[1024,256]{1,0:T(8,128)(2,1)} %get-tuple-element.127), channel_id=1, source_target_pairs={{0,4},{1,5},{2,6},{3,7},{4,8},{5,9},{6,10},{7,11},{8,12},{9,13},{1... | collective-permute-start | bytes 1572872 | tf_op jit(solution)/shard_map/ppermute | solution.py:18
  32.1 35.7 %collective-permute-start.3 = (bf16[1024,256]{1,0:T(8,128)(2,1)}, bf16[1024,256]{1,0:T(8,128)(2,1)S(1)}, u32[]{:S(2)}, u32[]{:S(2)}) collective-permute-start(bf16[1024,256]{1,0:T(8,128)(2,1)} %get-tuple-element.127), channel_id=1, source_target_pairs={{0,12},{1,13},{2,14},{3,15},{4,0},{5,1},{6,2},{7,3},{8,4},{9,5},{1... | collective-permute-start | bytes 1572872 | tf_op jit(solution)/shard_map/ppermute | solution.py:18
  46.9 35.4 %collective-permute-start.4 = (bf16[1024,256]{1,0:T(8,128)(2,1)S(1)}, bf16[1024,256]{1,0:T(8,128)(2,1)S(1)}, u32[]{:S(2)}, u32[]{:S(2)}) collective-permute-start(bf16[1024,256]{1,0:T(8,128)(2,1)S(1)} %copy-done.11), channel_id=1, source_target_pairs={{0,4},{1,5},{2,6},{3,7},{4,8},{5,9},{6,10},{7,11},{8,12},{9,13},{1... | collective-permute-start | bytes 1572872 | tf_op jit(solution)/shard_map/ppermute | solution.py:18
  54.6 35.5 %collective-permute-start.5 = (bf16[1024,256]{1,0:T(8,128)(2,1)S(1)}, bf16[1024,256]{1,0:T(8,128)(2,1)S(1)}, u32[]{:S(2)}, u32[]{:S(2)}) collective-permute-start(bf16[1024,256]{1,0:T(8,128)(2,1)S(1)} %copy-done.11), channel_id=1, source_target_pairs={{0,12},{1,13},{2,14},{3,15},{4,0},{5,1},{6,2},{7,3},{8,4},{9,5},{1... | collective-permute-start | bytes 1572872 | tf_op jit(solution)/shard_map/ppermute | solution.py:18
  67.8 27.0 %collective-permute-start.6 = (bf16[512,256]{1,0:T(8,128)(2,1)S(1)}, bf16[512,256]{1,0:T(8,128)(2,1)S(1)}, u32[]{:S(2)}, u32[]{:S(2)}) collective-permute-start(bf16[512,256]{1,0:T(8,128)(2,1)S(1)} %copy-done.13), channel_id=1, source_target_pairs={{0,4},{1,5},{2,6},{3,7},{4,8},{5,9},{6,10},{7,11},{8,12},{9,13},{1... | collective-permute-start | bytes 786440 | tf_op jit(solution)/shard_map/ppermute | solution.py:18
  82.3 15.6 %collective-permute-start.7 = (bf16[512,256]{1,0:T(8,128)(2,1)S(1)}, bf16[512,256]{1,0:T(8,128)(2,1)S(1)}, u32[]{:S(2)}, u32[]{:S(2)}) collective-permute-start(bf16[512,256]{1,0:T(8,128)(2,1)S(1)} %copy-done.13), channel_id=1, source_target_pairs={{0,12},{1,13},{2,14},{3,15},{4,0},{5,1},{6,2},{7,3},{8,4},{9,5},{1... | collective-permute-start | bytes 786440 | tf_op jit(solution)/shard_map/ppermute | solution.py:18
  105.9 10.8 %collective-permute-start.10 = (f32[229376]{0:T(1024)S(1)}, f32[229376]{0:T(1024)S(1)}, u32[]{:S(2)}, u32[]{:S(2)}) collective-permute-start(f32[229376]{0:T(1024)S(1)} %dynamic_slice.25), channel_id=1, source_target_pairs={{0,1},{1,0},{2,3},{3,2},{4,5},{5,4},{6,7},{7,6},{8,9},{9,8},{10,11... | collective-permute-start | bytes 2752520 | tf_op jit(solution)/shard_map/ppermute | solution.py:24
  106.0 23.0 %collective-permute-start.12 = (bf16[512,256]{1,0:T(8,128)(2,1)S(1)}, bf16[512,256]{1,0:T(8,128)(2,1)S(1)}, u32[]{:S(2)}, u32[]{:S(2)}) collective-permute-start(bf16[512,256]{1,0:T(8,128)(2,1)S(1)} %get-tuple-element.143), channel_id=1, source_target_pairs={{0,12},{1,13},{2,14},{3,15},{4,0},{5,1},{6,2},{7,3},{8,4},{9,5},{1... | collective-permute-start | bytes 786440 | tf_op jit(solution)/shard_map/ppermute | solution.py:18
  108.4 20.6 %collective-permute-start.13 = (bf16[512,256]{1,0:T(8,128)(2,1)S(1)}, bf16[512,256]{1,0:T(8,128)(2,1)S(1)}, u32[]{:S(2)}, u32[]{:S(2)}) collective-permute-start(bf16[512,256]{1,0:T(8,128)(2,1)S(1)} %get-tuple-element.141), channel_id=1, source_target_pairs={{0,4},{1,5},{2,6},{3,7},{4,8},{5,9},{6,10},{7,11},{8,12},{9,13},{1... | collective-permute-start | bytes 786440 | tf_op jit(solution)/shard_map/ppermute | solution.py:18
  108.5 20.6 %collective-permute-start.14 = (bf16[512,256]{1,0:T(8,128)(2,1)S(1)}, bf16[512,256]{1,0:T(8,128)(2,1)S(1)}, u32[]{:S(2)}, u32[]{:S(2)}) collective-permute-start(bf16[512,256]{1,0:T(8,128)(2,1)S(1)} %get-tuple-element.142), channel_id=1, source_target_pairs={{0,12},{1,13},{2,14},{3,15},{4,0},{5,1},{6,2},{7,3},{8,4},{9,5},{1... | collective-permute-start | bytes 786440 | tf_op jit(solution)/shard_map/ppermute | solution.py:18
  112.3 20.1 %collective-permute-start.15 = (bf16[512,256]{1,0:T(8,128)(2,1)S(1)}, bf16[512,256]{1,0:T(8,128)(2,1)S(1)}, u32[]{:S(2)}, u32[]{:S(2)}) collective-permute-start(bf16[512,256]{1,0:T(8,128)(2,1)S(1)} %get-tuple-element.140), channel_id=1, source_target_pairs={{0,4},{1,5},{2,6},{3,7},{4,8},{5,9},{6,10},{7,11},{8,12},{9,13},{1... | collective-permute-start | bytes 786440 | tf_op jit(solution)/shard_map/ppermute | solution.py:18
  116.8 12.1 %collective-permute-start.11 = (f32[114688]{0:T(1024)S(1)}, f32[114688]{0:T(1024)S(1)}, u32[]{:S(2)}, u32[]{:S(2)}) collective-permute-start(f32[114688]{0:T(1024)S(1)} %dynamic_slice.27), channel_id=1, source_target_pairs={{0,2},{1,3},{2,0},{3,1},{4,6},{5,7},{6,4},{7,5},{8,10},{9,11},{10,... | collective-permute-start | bytes 1376264 | tf_op jit(solution)/shard_map/ppermute | solution.py:24
  132.5 8.6 %collective-permute-start.16 = (f32[57344]{0:T(1024)S(1)}, f32[57344]{0:T(1024)S(1)}, u32[]{:S(2)}, u32[]{:S(2)}) collective-permute-start(f32[57344]{0:T(1024)S(1)} %dynamic_slice.29), channel_id=1, source_target_pairs={{0,4},{1,5},{2,6},{3,7},{4,0},{5,1},{6,2},{7,3},{8,12},{9,13},{10,... | collective-permute-start | bytes 688136 | tf_op jit(solution)/shard_map/ppermute | solution.py:24
  134.2 12.2 %collective-permute-start.17 = (bf16[512,256]{1,0:T(8,128)(2,1)S(1)}, bf16[512,256]{1,0:T(8,128)(2,1)S(1)}, u32[]{:S(2)}, u32[]{:S(2)}) collective-permute-start(bf16[512,256]{1,0:T(8,128)(2,1)S(1)} %slice.162), channel_id=1, source_target_pairs={{0,12},{1,13},{2,14},{3,15},{4,0},{5,1},{6,2},{7,3},{8,4},{9,5},{1... | collective-permute-start | bytes 786440 | tf_op jit(solution)/shard_map/ppermute | solution.py:18
  135.7 16.0 %collective-permute-start.18 = (bf16[512,256]{1,0:T(8,128)(2,1)S(1)}, bf16[512,256]{1,0:T(8,128)(2,1)S(1)}, u32[]{:S(2)}, u32[]{:S(2)}) collective-permute-start(bf16[512,256]{1,0:T(8,128)(2,1)S(1)} %slice.163), channel_id=1, source_target_pairs={{0,4},{1,5},{2,6},{3,7},{4,8},{5,9},{6,10},{7,11},{8,12},{9,13},{1... | collective-permute-start | bytes 786440 | tf_op jit(solution)/shard_map/ppermute | solution.py:18
  152.5 25.3 %collective-permute-start.21 = (bf16[512,256]{1,0:T(8,128)(2,1)}, bf16[512,256]{1,0:T(8,128)(2,1)S(1)}, u32[]{:S(2)}, u32[]{:S(2)}) collective-permute-start(bf16[512,256]{1,0:T(8,128)(2,1)} %slice.164), channel_id=1, source_target_pairs={{0,12},{1,13},{2,14},{3,15},{4,0},{5,1},{6,2},{7,3},{8,4},{9,5},{1... | collective-permute-start | bytes 786440 | tf_op jit(solution)/shard_map/ppermute | solution.py:18
  156.5 21.3 %collective-permute-start.22 = (bf16[512,256]{1,0:T(8,128)(2,1)}, bf16[512,256]{1,0:T(8,128)(2,1)S(1)}, u32[]{:S(2)}, u32[]{:S(2)}) collective-permute-start(bf16[512,256]{1,0:T(8,128)(2,1)} %slice.165), channel_id=1, source_target_pairs={{0,4},{1,5},{2,6},{3,7},{4,8},{5,9},{6,10},{7,11},{8,12},{9,13},{1... | collective-permute-start | bytes 786440 | tf_op jit(solution)/shard_map/ppermute | solution.py:18
  160.0 17.7 %collective-permute-start.20 = (f32[56,512]{1,0:T(8,128)S(1)}, f32[56,512]{1,0:T(8,128)S(1)}, u32[]{:S(2)}, u32[]{:S(2)}) collective-permute-start(f32[56,512]{1,0:T(8,128)S(1)} %reshape.20), channel_id=1, source_target_pairs={{0,8},{1,9},{2,10},{3,11},{4,12},{5,13},{6,14},{7,15},{8,0},{9,1},... | collective-permute-start | bytes 344072 | tf_op jit(solution)/shard_map/ppermute | solution.py:24
  162.1 25.3 %collective-permute-start.24 = (bf16[512,256]{1,0:T(8,128)(2,1)S(1)}, bf16[512,256]{1,0:T(8,128)(2,1)S(1)}, u32[]{:S(2)}, u32[]{:S(2)}) collective-permute-start(bf16[512,256]{1,0:T(8,128)(2,1)S(1)} %slice.166), channel_id=1, source_target_pairs={{0,12},{1,13},{2,14},{3,15},{4,0},{5,1},{6,2},{7,3},{8,4},{9,5},{1... | collective-permute-start | bytes 786440 | tf_op jit(solution)/shard_map/ppermute | solution.py:18
  168.8 18.6 %collective-permute-start.25 = (bf16[512,256]{1,0:T(8,128)(2,1)S(1)}, bf16[512,256]{1,0:T(8,128)(2,1)S(1)}, u32[]{:S(2)}, u32[]{:S(2)}) collective-permute-start(bf16[512,256]{1,0:T(8,128)(2,1)S(1)} %slice.167), channel_id=1, source_target_pairs={{0,4},{1,5},{2,6},{3,7},{4,8},{5,9},{6,10},{7,11},{8,12},{9,13},{1... | collective-permute-start | bytes 786440 | tf_op jit(solution)/shard_map/ppermute | solution.py:18
  177.8 9.5 %collective-permute-start.23 = (f32[112,512]{1,0:T(8,128)S(1)}, f32[112,512]{1,0:T(8,128)S(1)}, u32[]{:S(2)}, u32[]{:S(2)}) collective-permute-start(f32[112,512]{1,0:T(8,128)S(1)} %pad_maximum_fusion.9), channel_id=1, source_target_pairs={{0,4},{1,5},{2,6},{3,7},{4,0},{5,1},{6,2},{7,3},{8,12},{9,13},{10,... | collective-permute-start | bytes 688136 | tf_op jit(solution)/shard_map/ppermute | solution.py:24
  180.8 20.6 %collective-permute-start.27 = (bf16[512,256]{1,0:T(8,128)(2,1)S(1)}, bf16[512,256]{1,0:T(8,128)(2,1)S(1)}, u32[]{:S(2)}, u32[]{:S(2)}) collective-permute-start(bf16[512,256]{1,0:T(8,128)(2,1)S(1)} %slice.168), channel_id=1, source_target_pairs={{0,12},{1,13},{2,14},{3,15},{4,0},{5,1},{6,2},{7,3},{8,4},{9,5},{1... | collective-permute-start | bytes 786440 | tf_op jit(solution)/shard_map/ppermute | solution.py:18
  184.7 20.8 %collective-permute-start.28 = (bf16[512,256]{1,0:T(8,128)(2,1)S(1)}, bf16[512,256]{1,0:T(8,128)(2,1)S(1)}, u32[]{:S(2)}, u32[]{:S(2)}) collective-permute-start(bf16[512,256]{1,0:T(8,128)(2,1)S(1)} %slice.169), channel_id=1, source_target_pairs={{0,4},{1,5},{2,6},{3,7},{4,8},{5,9},{6,10},{7,11},{8,12},{9,13},{1... | collective-permute-start | bytes 786440 | tf_op jit(solution)/shard_map/ppermute | solution.py:18
  187.4 17.9 %collective-permute-start.26 = (f32[224,512]{1,0:T(8,128)S(1)}, f32[224,512]{1,0:T(8,128)S(1)}, u32[]{:S(2)}, u32[]{:S(2)}) collective-permute-start(f32[224,512]{1,0:T(8,128)S(1)} %pad_maximum_fusion.8), channel_id=1, source_target_pairs={{0,2},{1,3},{2,0},{3,1},{4,6},{5,7},{6,4},{7,5},{8,10},{9,11},{10,... | collective-permute-start | bytes 1376264 | tf_op jit(solution)/shard_map/ppermute | solution.py:24
  190.1 17.1 %collective-permute-start.29 = (bf16[512,256]{1,0:T(8,128)(2,1)S(1)}, bf16[512,256]{1,0:T(8,128)(2,1)S(1)}, u32[]{:S(2)}, u32[]{:S(2)}) collective-permute-start(bf16[512,256]{1,0:T(8,128)(2,1)S(1)} %get-tuple-element.126), channel_id=1, source_target_pairs={{0,12},{1,13},{2,14},{3,15},{4,0},{5,1},{6,2},{7,3},{8,4},{9,5},{1... | collective-permute-start | bytes 786440 | tf_op jit(solution)/shard_map/ppermute | solution.py:18
  200.6 11.8 %collective-permute-start.30 = (bf16[512,256]{1,0:T(8,128)(2,1)S(1)}, bf16[512,256]{1,0:T(8,128)(2,1)S(1)}, u32[]{:S(2)}, u32[]{:S(2)}) collective-permute-start(bf16[512,256]{1,0:T(8,128)(2,1)S(1)} %get-tuple-element.124), channel_id=1, source_target_pairs={{0,4},{1,5},{2,6},{3,7},{4,8},{5,9},{6,10},{7,11},{8,12},{9,13},{1... | collective-permute-start | bytes 786440 | tf_op jit(solution)/shard_map/ppermute | solution.py:18
  201.4 15.8 %collective-permute-start.31 = (bf16[512,256]{1,0:T(8,128)(2,1)S(1)}, bf16[512,256]{1,0:T(8,128)(2,1)S(1)}, u32[]{:S(2)}, u32[]{:S(2)}) collective-permute-start(bf16[512,256]{1,0:T(8,128)(2,1)S(1)} %get-tuple-element.125), channel_id=1, source_target_pairs={{0,12},{1,13},{2,14},{3,15},{4,0},{5,1},{6,2},{7,3},{8,4},{9,5},{1... | collective-permute-start | bytes 786440 | tf_op jit(solution)/shard_map/ppermute | solution.py:18
  205.3 15.5 %collective-permute-start.32 = (bf16[512,256]{1,0:T(8,128)(2,1)S(1)}, bf16[512,256]{1,0:T(8,128)(2,1)S(1)}, u32[]{:S(2)}, u32[]{:S(2)}) collective-permute-start(bf16[512,256]{1,0:T(8,128)(2,1)S(1)} %get-tuple-element.123), channel_id=1, source_target_pairs={{0,4},{1,5},{2,6},{3,7},{4,8},{5,9},{6,10},{7,11},{8,12},{9,13},{1... | collective-permute-start | bytes 786440 | tf_op jit(solution)/shard_map/ppermute | solution.py:18
  (16 other events, 307.2 us)

commit v19 on v11

--- a/solution.py
+++ b/solution.py
@@ -132,6 +132,9 @@
     sent_rows = bounds[EARLY]
     pending = []
     late = []
+    finished = None
+    head_rows = 0
+    head_count = 0
     for number, (bit, down) in enumerate(steps):
         if down and bit == 4:
             buf, early = lax.optimization_barrier((buf, early))
@@ -145,6 +148,13 @@
             pending.append((send_rows(pieces, sent_rows, sent_rows + RIDER_ROWS), number + RIDER_SPAN))
             sent_rows += RIDER_ROWS
         if not down and bit == 2 and not late:
+            landed = jnp.concatenate([pair[0] for pair in early], axis=0).astype(jnp.float32)
+            landed = landed + jnp.concatenate([pair[1] for pair in early], axis=0).astype(jnp.float32)
+            head_rows = landed.shape[0]
+            head_count = len(early)
+            landed = jnp.pad(landed, ((0, positions - head_rows), (0, 0)))
+            finished = (cotangent.astype(jnp.float32) + jnp.concatenate(mids, axis=0) + landed).astype(jnp.bfloat16)
+            buf, finished = lax.optimization_barrier((buf, finished))
             buf, pieces = lax.optimization_barrier((buf, (lower_all, upper_all)))
             middle_row = sent_rows + (positions - sent_rows) // 2
             late.append(send_rows(pieces, sent_rows, middle_row))
@@ -160,12 +170,21 @@
     early.extend(item[0] for item in pending)
     if sent_rows < positions:
         late.append(send_rows((lower_all, upper_all), sent_rows, positions))
-    received = early + late
-    received_ahead = jnp.concatenate([pair[0] for pair in received], axis=0)
-    received_behind = jnp.concatenate([pair[1] for pair in received], axis=0)
-    total_sum = cotangent.astype(jnp.float32) + jnp.concatenate(mids, axis=0)
-    total_sum = total_sum + received_ahead.astype(jnp.float32) + received_behind.astype(jnp.float32)
-    grad_input = total_sum.astype(jnp.bfloat16)
+    mids_all = jnp.concatenate(mids, axis=0)
+    if finished is not None:
+        tail = early[head_count:] + late
+        ahead = jnp.concatenate([pair[0] for pair in tail], axis=0)
+        behind = jnp.concatenate([pair[1] for pair in tail], axis=0)
+        late_sum = cotangent[head_rows:].astype(jnp.float32) + mids_all[head_rows:]
+        late_sum = late_sum + ahead.astype(jnp.float32) + behind.astype(jnp.float32)
+        grad_input = lax.dynamic_update_slice(finished, late_sum.astype(jnp.bfloat16), (head_rows, 0))
+    else:
+        received = early + late
+        received_ahead = jnp.concatenate([pair[0] for pair in received], axis=0)
+        received_behind = jnp.concatenate([pair[1] for pair in received], axis=0)
+        total_sum = cotangent.astype(jnp.float32) + mids_all
+        total_sum = total_sum + received_ahead.astype(jnp.float32) + received_behind.astype(jnp.float32)
+        grad_input = total_sum.astype(jnp.bfloat16)
     split = wconv_total.shape[0]
     grad_conv = buf[:split]
     grad_out = buf[split:].reshape(wout_total.shape)

time: 223 us -> 226 us (1.013)
  waiting for transfers between devices: 62.6 us -> 55.2 us
  other arithmetic: 5.76 us -> 11.7 us
  local copies, waits for them, and re-layouts: 19.5 us -> 23.4 us
    ppermute x26, waiting for transfers between devices: 36.8 us -> 31.7 us  [from_behind(): return lax.ppermute(value, axis, pairs)]
    dynamic_update_slice x0 -> x1, other arithmetic: none -> 2.75 us  [body(): lax.dynamic_update_slice(finished, late_sum.astype(jnp.bfloat16), (head_r...]
    unnamed x44 -> x48, local copies, waits for them, and re-layouts: 5.04 us -> 7.51 us
    ppermute x8, waiting for transfers between devices: 25.8 us -> 23.5 us  [exchange(): return lax.ppermute(value, axis, pairs)]
  transfers between devices with their start and end apart: 34 -> 34, of which waited for: 14 -> 13; matrix products, arithmetic and copies ran while one was open for 22% -> 26% of each run, Pallas kernels for 0% -> 0%
where the time goes in v19:
time: 226 us; the launch traced here: 225 us
  starting transfers between devices  98.1 us (43%)
  waiting for transfers between devices  55.2 us (24%)
  matrix products  34.7 us (15%)
  local copies, waits for them, and re-layouts  23.4 us (10%)
  other arithmetic  11.7 us (5%)
    ppermute x26, starting transfers between devices, from_behind(): return lax.ppermute(value, axis, pairs)  84.1 us
    ppermute x26, waiting for transfers between devices, from_behind(): return lax.ppermute(value, axis, pairs)  31.7 us
    ppermute x8, waiting for transfers between devices, exchange(): return lax.ppermute(value, axis, pairs)  23.5 us
    ppermute x8, starting transfers between devices, exchange(): return lax.ppermute(value, axis, pairs)  14 us
    unnamed x48, local copies, waits for them, and re-layouts  7.51 us
    dot_general x5, matrix products, chunk_layer(): preact = preact + jnp.dot(middle, w_mid, preferred_element_type=jnp.float32)  4.65 us
    slice x2, local copies, waits for them, and re-layouts, body(): middle = activations[bounds[k]:bounds[k + 1]]  4.54 us
  transfers between devices with their start and end apart: 34, of which 13 were waited for; matrix products, arithmetic and copies ran while one was open for 26% of the time, Pallas kernels for 0%

profile of v19, /device:TPU:0, one launch (start us, length us, event | category | flops | bytes accessed | tf_op | source)
XLA Modules:
  0.0 224.9 jit_solution(9487904186415976683)
XLA Ops:
  0.7 2.0 fusion.127
  2.7 3.0 %collective-permute-start = (bf16[512,256]{1,0:T(8,128)(2,1)}, bf16[512,256]{1,0:T(8,128)(2,1)S(1)}, u32[]{:S(2)}, u32[]{:S(2)}) collective-permute-start(bf16[512,256]{1,0:T(8,128)(2,1)} %get-tuple-element.135), channel_id=1, source_target_pairs={{0,4},{1,5},{2,6},{3,7},{4,8},{5,9},{6,10},{7,11},{8,12},{9,13},{1... | collective-permute-start | bytes 786440 | tf_op jit(solution)/shard_map/ppermute | solution.py:18
  5.7 2.0 collective-permute-start.1
  7.7 2.5 %fusion.126 = (bf16[1024,256]{1,0:T(8,128)(2,1)}, bf16[1024,256]{1,0:T(8,128)(2,1)}, bf16[1024,256]{1,0:T(8,128)(2,1)}) fusion(bf16[4096,256]{1,0:T(8,128)(2,1)} %param.4), kind=kLoop, calls=%fused_computation.213 | loop fusion | bytes 3145728 | tf_op jit(solution)/shard_map/slice | solution.py:95
  10.3 3.8 %collective-permute-start.3 = (bf16[1024,256]{1,0:T(8,128)(2,1)}, bf16[1024,256]{1,0:T(8,128)(2,1)}, u32[]{:S(2)}, u32[]{:S(2)}) collective-permute-start(bf16[1024,256]{1,0:T(8,128)(2,1)} %get-tuple-element.132), channel_id=1, source_target_pairs={{0,12},{1,13},{2,14},{3,15},{4,0},{5,1},{6,2},{7,3},{8,4},{9,5},{1... | collective-permute-start | bytes 1572872 | tf_op jit(solution)/shard_map/ppermute | solution.py:18
  14.1 1.8 fusion.85
  18.6 13.5 %collective-permute-done.2 = bf16[1024,256]{1,0:T(8,128)(2,1)} collective-permute-done((bf16[1024,256]{1,0:T(8,128)(2,1)}, bf16[1024,256]{1,0:T(8,128)(2,1)}, u32[]{:S(2)}, u32[]{:S(2)}) %collective-permute-start.2) | collective-permute-done | bytes 524320 | tf_op jit(solution)/shard_map/ppermute | solution.py:18
  32.1 13.2 %collective-permute-start.9 = (bf16[1024,256]{1,0:T(8,128)(2,1)}, bf16[1024,256]{1,0:T(8,128)(2,1)S(1)}, u32[]{:S(2)}, u32[]{:S(2)}) collective-permute-start(bf16[1024,256]{1,0:T(8,128)(2,1)} %get-tuple-element.131), channel_id=1, source_target_pairs={{0,12},{1,13},{2,14},{3,15},{4,0},{5,1},{6,2},{7,3},{8,4},{9,5},{1... | collective-permute-start | bytes 1572872 | tf_op jit(solution)/shard_map/ppermute | solution.py:18
  54.6 13.2 %collective-permute-start.7 = (bf16[1024,256]{1,0:T(8,128)(2,1)S(1)}, bf16[1024,256]{1,0:T(8,128)(2,1)S(1)}, u32[]{:S(2)}, u32[]{:S(2)}) collective-permute-start(bf16[1024,256]{1,0:T(8,128)(2,1)S(1)} %copy-done.12), channel_id=1, source_target_pairs={{0,12},{1,13},{2,14},{3,15},{4,0},{5,1},{6,2},{7,3},{8,4},{9,5},{1... | collective-permute-start | bytes 1572872 | tf_op jit(solution)/shard_map/ppermute | solution.py:18
  67.8 8.3 %collective-permute-start.4 = (bf16[512,256]{1,0:T(8,128)(2,1)S(1)}, bf16[512,256]{1,0:T(8,128)(2,1)S(1)}, u32[]{:S(2)}, u32[]{:S(2)}) collective-permute-start(bf16[512,256]{1,0:T(8,128)(2,1)S(1)} %copy-done.18), channel_id=1, source_target_pairs={{0,4},{1,5},{2,6},{3,7},{4,8},{5,9},{6,10},{7,11},{8,12},{9,13},{1... | collective-permute-start | bytes 786440 | tf_op jit(solution)/shard_map/ppermute | solution.py:18
  82.3 7.8 %collective-permute-start.5 = (bf16[512,256]{1,0:T(8,128)(2,1)S(1)}, bf16[512,256]{1,0:T(8,128)(2,1)S(1)}, u32[]{:S(2)}, u32[]{:S(2)}) collective-permute-start(bf16[512,256]{1,0:T(8,128)(2,1)S(1)} %copy-done.18), channel_id=1, source_target_pairs={{0,12},{1,13},{2,14},{3,15},{4,0},{5,1},{6,2},{7,3},{8,4},{9,5},{1... | collective-permute-start | bytes 786440 | tf_op jit(solution)/shard_map/ppermute | solution.py:18
  94.8 3.1 %collective-permute-done.5 = bf16[512,256]{1,0:T(8,128)(2,1)S(1)} collective-permute-done((bf16[512,256]{1,0:T(8,128)(2,1)S(1)}, bf16[512,256]{1,0:T(8,128)(2,1)S(1)}, u32[]{:S(2)}, u32[]{:S(2)}) %collective-permute-start.5) | collective-permute-done | bytes 262176 | tf_op jit(solution)/shard_map/ppermute | solution.py:18
  106.0 2.4 %collective-permute-start.12 = (bf16[512,256]{1,0:T(8,128)(2,1)S(1)}, bf16[512,256]{1,0:T(8,128)(2,1)S(1)}, u32[]{:S(2)}, u32[]{:S(2)}) collective-permute-start(bf16[512,256]{1,0:T(8,128)(2,1)S(1)} %get-tuple-element.147), channel_id=1, source_target_pairs={{0,12},{1,13},{2,14},{3,15},{4,0},{5,1},{6,2},{7,3},{8,4},{9,5},{1... | collective-permute-start | bytes 786440 | tf_op jit(solution)/shard_map/ppermute | solution.py:18
  108.5 3.8 %collective-permute-start.14 = (bf16[512,256]{1,0:T(8,128)(2,1)S(1)}, bf16[512,256]{1,0:T(8,128)(2,1)S(1)}, u32[]{:S(2)}, u32[]{:S(2)}) collective-permute-start(bf16[512,256]{1,0:T(8,128)(2,1)S(1)} %get-tuple-element.146), channel_id=1, source_target_pairs={{0,12},{1,13},{2,14},{3,15},{4,0},{5,1},{6,2},{7,3},{8,4},{9,5},{1... | collective-permute-start | bytes 786440 | tf_op jit(solution)/shard_map/ppermute | solution.py:18
  120.3 8.7 %collective-permute-done.11 = f32[114688]{0:T(1024)S(1)} collective-permute-done((f32[114688]{0:T(1024)S(1)}, f32[114688]{0:T(1024)S(1)}, u32[]{:S(2)}, u32[]{:S(2)}) %collective-permute-start.11) | collective-permute-done | bytes 458784 | tf_op jit(solution)/shard_map/ppermute | solution.py:24
  129.1 3.4 %collective-permute-done.15 = bf16[512,256]{1,0:T(8,128)(2,1)S(1)} collective-permute-done((bf16[512,256]{1,0:T(8,128)(2,1)S(1)}, bf16[512,256]{1,0:T(8,128)(2,1)S(1)}, u32[]{:S(2)}, u32[]{:S(2)}) %collective-permute-start.15) | collective-permute-done | bytes 262176 | tf_op jit(solution)/shard_map/ppermute | solution.py:18
  139.0 2.0 collective-permute-done.16
  144.3 2.3 %collective-permute-start.21 = (bf16[512,256]{1,0:T(8,128)(2,1)}, bf16[512,256]{1,0:T(8,128)(2,1)S(1)}, u32[]{:S(2)}, u32[]{:S(2)}) collective-permute-start(bf16[512,256]{1,0:T(8,128)(2,1)} %slice.170), channel_id=1, source_target_pairs={{0,12},{1,13},{2,14},{3,15},{4,0},{5,1},{6,2},{7,3},{8,4},{9,5},{1... | collective-permute-start | bytes 786440 | tf_op jit(solution)/shard_map/ppermute | solution.py:18
  147.4 7.9 %collective-permute-done.17 = f32[28672]{0:T(1024)S(1)} collective-permute-done((f32[28672]{0:T(1024)S(1)}, f32[28672]{0:T(1024)S(1)}, u32[]{:S(2)}, u32[]{:S(2)}) %collective-permute-start.17) | collective-permute-done | bytes 114720 | tf_op jit(solution)/shard_map/ppermute | solution.py:24
  155.4 2.1 collective-permute-start.20
  158.5 6.5 %collective-permute-start.24 = (bf16[512,256]{1,0:T(8,128)(2,1)S(1)}, bf16[512,256]{1,0:T(8,128)(2,1)S(1)}, u32[]{:S(2)}, u32[]{:S(2)}) collective-permute-start(bf16[512,256]{1,0:T(8,128)(2,1)S(1)} %slice.172), channel_id=1, source_target_pairs={{0,12},{1,13},{2,14},{3,15},{4,0},{5,1},{6,2},{7,3},{8,4},{9,5},{1... | collective-permute-start | bytes 786440 | tf_op jit(solution)/shard_map/ppermute | solution.py:18
  168.1 3.7 %collective-permute-done.20 = f32[56,512]{1,0:T(8,128)S(1)} collective-permute-done((f32[56,512]{1,0:T(8,128)S(1)}, f32[56,512]{1,0:T(8,128)S(1)}, u32[]{:S(2)}, u32[]{:S(2)}) %collective-permute-start.20) | collective-permute-done | bytes 114720 | tf_op jit(solution)/shard_map/ppermute | solution.py:24
  171.8 5.5 %collective-permute-start.23 = (f32[112,512]{1,0:T(8,128)S(1)}, f32[112,512]{1,0:T(8,128)S(1)}, u32[]{:S(2)}, u32[]{:S(2)}) collective-permute-start(f32[112,512]{1,0:T(8,128)S(1)} %pad_maximum_fusion.11), channel_id=1, source_target_pairs={{0,4},{1,5},{2,6},{3,7},{4,0},{5,1},{6,2},{7,3},{8,12},{9,13},{10,... | collective-permute-start | bytes 688136 | tf_op jit(solution)/shard_map/ppermute | solution.py:24
  178.3 2.9 %collective-permute-start.27 = (bf16[512,256]{1,0:T(8,128)(2,1)S(1)}, bf16[512,256]{1,0:T(8,128)(2,1)S(1)}, u32[]{:S(2)}, u32[]{:S(2)}) collective-permute-start(bf16[512,256]{1,0:T(8,128)(2,1)S(1)} %slice.176), channel_id=1, source_target_pairs={{0,12},{1,13},{2,14},{3,15},{4,0},{5,1},{6,2},{7,3},{8,4},{9,5},{1... | collective-permute-start | bytes 786440 | tf_op jit(solution)/shard_map/ppermute | solution.py:18
  186.4 2.1 convert_add_fusion
  189.4 2.1 add_convert_fusion
  194.0 8.1 %collective-permute-start.29 = (bf16[512,256]{1,0:T(8,128)(2,1)S(1)}, bf16[512,256]{1,0:T(8,128)(2,1)S(1)}, u32[]{:S(2)}, u32[]{:S(2)}) collective-permute-start(bf16[512,256]{1,0:T(8,128)(2,1)S(1)} %get-tuple-element.130), channel_id=1, source_target_pairs={{0,12},{1,13},{2,14},{3,15},{4,0},{5,1},{6,2},{7,3},{8,4},{9,5},{1... | collective-permute-start | bytes 786440 | tf_op jit(solution)/shard_map/ppermute | solution.py:18
  203.3 3.8 %collective-permute-start.31 = (bf16[512,256]{1,0:T(8,128)(2,1)S(1)}, bf16[512,256]{1,0:T(8,128)(2,1)S(1)}, u32[]{:S(2)}, u32[]{:S(2)}) collective-permute-start(bf16[512,256]{1,0:T(8,128)(2,1)S(1)} %get-tuple-element.129), channel_id=1, source_target_pairs={{0,12},{1,13},{2,14},{3,15},{4,0},{5,1},{6,2},{7,3},{8,4},{9,5},{1... | collective-permute-start | bytes 786440 | tf_op jit(solution)/shard_map/ppermute | solution.py:18
  208.3 4.1 %collective-permute-done.30 = bf16[512,256]{1,0:T(8,128)(2,1)S(1)} collective-permute-done((bf16[512,256]{1,0:T(8,128)(2,1)S(1)}, bf16[512,256]{1,0:T(8,128)(2,1)S(1)}, u32[]{:S(2)}, u32[]{:S(2)}) %collective-permute-start.30) | collective-permute-done | bytes 262176 | tf_op jit(solution)/shard_map/ppermute | solution.py:18
  212.4 2.7 %collective-permute-done.31 = bf16[512,256]{1,0:T(8,128)(2,1)S(1)} collective-permute-done((bf16[512,256]{1,0:T(8,128)(2,1)S(1)}, bf16[512,256]{1,0:T(8,128)(2,1)S(1)}, u32[]{:S(2)}, u32[]{:S(2)}) %collective-permute-start.31) | collective-permute-done | bytes 262176 | tf_op jit(solution)/shard_map/ppermute | solution.py:18
  215.1 2.9 %collective-permute-done.32 = bf16[512,256]{1,0:T(8,128)(2,1)S(1)} collective-permute-done((bf16[512,256]{1,0:T(8,128)(2,1)S(1)}, bf16[512,256]{1,0:T(8,128)(2,1)S(1)}, u32[]{:S(2)}, u32[]{:S(2)}) %collective-permute-start.32) | collective-permute-done | bytes 262176 | tf_op jit(solution)/shard_map/ppermute | solution.py:18
  218.8 2.7 %fusion.24 = bf16[4096,256]{1,0:T(8,128)(2,1)} fusion(bf16[4096,256]{1,0:T(8,128)(2,1)} %add_convert_fusion, f32[512,256]{1,0:T(8,128)S(1)} %copy-done.9, f32[512,256]{1,0:T(8,128)S(1)} %get-tuple-element.159, f32[1024,256]{1,0:T(8,128)S(1)} %get-tuple-element.157, bf16[512,256]{1,0:T(8,128)(2,1)} %copy-done.16, ...), kind=kLoop, calls=%fused_computation.80 | loop fusion | flops 7471104 | bytes 5242880 | tf_op jit(solution)/shard_map/dynamic_update_slice | solution.py:180
  (186 shorter events, 69.1 us)
Async XLA Ops:
  2.7 98.3 %collective-permute-start = (bf16[512,256]{1,0:T(8,128)(2,1)}, bf16[512,256]{1,0:T(8,128)(2,1)S(1)}, u32[]{:S(2)}, u32[]{:S(2)}) collective-permute-start(bf16[512,256]{1,0:T(8,128)(2,1)} %get-tuple-element.135), channel_id=1, source_target_pairs={{0,4},{1,5},{2,6},{3,7},{4,8},{5,9},{6,10},{7,11},{8,12},{9,13},{1... | collective-permute-start | bytes 786440 | tf_op jit(solution)/shard_map/ppermute | solution.py:18
  5.7 95.3 %collective-permute-start.1 = (bf16[512,256]{1,0:T(8,128)(2,1)}, bf16[512,256]{1,0:T(8,128)(2,1)S(1)}, u32[]{:S(2)}, u32[]{:S(2)}) collective-permute-start(bf16[512,256]{1,0:T(8,128)(2,1)} %get-tuple-element.135), channel_id=1, source_target_pairs={{0,12},{1,13},{2,14},{3,15},{4,0},{5,1},{6,2},{7,3},{8,4},{9,5},{1... | collective-permute-start | bytes 786440 | tf_op jit(solution)/shard_map/ppermute | solution.py:18
  10.3 21.8 %collective-permute-start.2 = (bf16[1024,256]{1,0:T(8,128)(2,1)}, bf16[1024,256]{1,0:T(8,128)(2,1)}, u32[]{:S(2)}, u32[]{:S(2)}) collective-permute-start(bf16[1024,256]{1,0:T(8,128)(2,1)} %get-tuple-element.132), channel_id=1, source_target_pairs={{0,4},{1,5},{2,6},{3,7},{4,8},{5,9},{6,10},{7,11},{8,12},{9,13},{1... | collective-permute-start | bytes 1572872 | tf_op jit(solution)/shard_map/ppermute | solution.py:18
  10.3 36.6 %collective-permute-start.3 = (bf16[1024,256]{1,0:T(8,128)(2,1)}, bf16[1024,256]{1,0:T(8,128)(2,1)}, u32[]{:S(2)}, u32[]{:S(2)}) collective-permute-start(bf16[1024,256]{1,0:T(8,128)(2,1)} %get-tuple-element.132), channel_id=1, source_target_pairs={{0,12},{1,13},{2,14},{3,15},{4,0},{5,1},{6,2},{7,3},{8,4},{9,5},{1... | collective-permute-start | bytes 1572872 | tf_op jit(solution)/shard_map/ppermute | solution.py:18
  14.1 40.5 %collective-permute-start.8 = (bf16[1024,256]{1,0:T(8,128)(2,1)}, bf16[1024,256]{1,0:T(8,128)(2,1)}, u32[]{:S(2)}, u32[]{:S(2)}) collective-permute-start(bf16[1024,256]{1,0:T(8,128)(2,1)} %get-tuple-element.131), channel_id=1, source_target_pairs={{0,4},{1,5},{2,6},{3,7},{4,8},{5,9},{6,10},{7,11},{8,12},{9,13},{1... | collective-permute-start | bytes 1572872 | tf_op jit(solution)/shard_map/ppermute | solution.py:18
  32.1 35.7 %collective-permute-start.9 = (bf16[1024,256]{1,0:T(8,128)(2,1)}, bf16[1024,256]{1,0:T(8,128)(2,1)S(1)}, u32[]{:S(2)}, u32[]{:S(2)}) collective-permute-start(bf16[1024,256]{1,0:T(8,128)(2,1)} %get-tuple-element.131), channel_id=1, source_target_pairs={{0,12},{1,13},{2,14},{3,15},{4,0},{5,1},{6,2},{7,3},{8,4},{9,5},{1... | collective-permute-start | bytes 1572872 | tf_op jit(solution)/shard_map/ppermute | solution.py:18
  46.9 35.4 %collective-permute-start.6 = (bf16[1024,256]{1,0:T(8,128)(2,1)S(1)}, bf16[1024,256]{1,0:T(8,128)(2,1)S(1)}, u32[]{:S(2)}, u32[]{:S(2)}) collective-permute-start(bf16[1024,256]{1,0:T(8,128)(2,1)S(1)} %copy-done.12), channel_id=1, source_target_pairs={{0,4},{1,5},{2,6},{3,7},{4,8},{5,9},{6,10},{7,11},{8,12},{9,13},{1... | collective-permute-start | bytes 1572872 | tf_op jit(solution)/shard_map/ppermute | solution.py:18
  54.6 35.5 %collective-permute-start.7 = (bf16[1024,256]{1,0:T(8,128)(2,1)S(1)}, bf16[1024,256]{1,0:T(8,128)(2,1)S(1)}, u32[]{:S(2)}, u32[]{:S(2)}) collective-permute-start(bf16[1024,256]{1,0:T(8,128)(2,1)S(1)} %copy-done.12), channel_id=1, source_target_pairs={{0,12},{1,13},{2,14},{3,15},{4,0},{5,1},{6,2},{7,3},{8,4},{9,5},{1... | collective-permute-start | bytes 1572872 | tf_op jit(solution)/shard_map/ppermute | solution.py:18
  67.8 27.0 %collective-permute-start.4 = (bf16[512,256]{1,0:T(8,128)(2,1)S(1)}, bf16[512,256]{1,0:T(8,128)(2,1)S(1)}, u32[]{:S(2)}, u32[]{:S(2)}) collective-permute-start(bf16[512,256]{1,0:T(8,128)(2,1)S(1)} %copy-done.18), channel_id=1, source_target_pairs={{0,4},{1,5},{2,6},{3,7},{4,8},{5,9},{6,10},{7,11},{8,12},{9,13},{1... | collective-permute-start | bytes 786440 | tf_op jit(solution)/shard_map/ppermute | solution.py:18
  82.3 15.6 %collective-permute-start.5 = (bf16[512,256]{1,0:T(8,128)(2,1)S(1)}, bf16[512,256]{1,0:T(8,128)(2,1)S(1)}, u32[]{:S(2)}, u32[]{:S(2)}) collective-permute-start(bf16[512,256]{1,0:T(8,128)(2,1)S(1)} %copy-done.18), channel_id=1, source_target_pairs={{0,12},{1,13},{2,14},{3,15},{4,0},{5,1},{6,2},{7,3},{8,4},{9,5},{1... | collective-permute-start | bytes 786440 | tf_op jit(solution)/shard_map/ppermute | solution.py:18
  105.9 10.8 %collective-permute-start.10 = (f32[229376]{0:T(1024)S(1)}, f32[229376]{0:T(1024)S(1)}, u32[]{:S(2)}, u32[]{:S(2)}) collective-permute-start(f32[229376]{0:T(1024)S(1)} %dynamic_slice.25), channel_id=1, source_target_pairs={{0,1},{1,0},{2,3},{3,2},{4,5},{5,4},{6,7},{7,6},{8,9},{9,8},{10,11... | collective-permute-start | bytes 2752520 | tf_op jit(solution)/shard_map/ppermute | solution.py:24
  106.0 23.0 %collective-permute-start.12 = (bf16[512,256]{1,0:T(8,128)(2,1)S(1)}, bf16[512,256]{1,0:T(8,128)(2,1)S(1)}, u32[]{:S(2)}, u32[]{:S(2)}) collective-permute-start(bf16[512,256]{1,0:T(8,128)(2,1)S(1)} %get-tuple-element.147), channel_id=1, source_target_pairs={{0,12},{1,13},{2,14},{3,15},{4,0},{5,1},{6,2},{7,3},{8,4},{9,5},{1... | collective-permute-start | bytes 786440 | tf_op jit(solution)/shard_map/ppermute | solution.py:18
  108.4 20.6 %collective-permute-start.13 = (bf16[512,256]{1,0:T(8,128)(2,1)S(1)}, bf16[512,256]{1,0:T(8,128)(2,1)S(1)}, u32[]{:S(2)}, u32[]{:S(2)}) collective-permute-start(bf16[512,256]{1,0:T(8,128)(2,1)S(1)} %get-tuple-element.145), channel_id=1, source_target_pairs={{0,4},{1,5},{2,6},{3,7},{4,8},{5,9},{6,10},{7,11},{8,12},{9,13},{1... | collective-permute-start | bytes 786440 | tf_op jit(solution)/shard_map/ppermute | solution.py:18
  108.5 20.6 %collective-permute-start.14 = (bf16[512,256]{1,0:T(8,128)(2,1)S(1)}, bf16[512,256]{1,0:T(8,128)(2,1)S(1)}, u32[]{:S(2)}, u32[]{:S(2)}) collective-permute-start(bf16[512,256]{1,0:T(8,128)(2,1)S(1)} %get-tuple-element.146), channel_id=1, source_target_pairs={{0,12},{1,13},{2,14},{3,15},{4,0},{5,1},{6,2},{7,3},{8,4},{9,5},{1... | collective-permute-start | bytes 786440 | tf_op jit(solution)/shard_map/ppermute | solution.py:18
  112.3 20.2 %collective-permute-start.15 = (bf16[512,256]{1,0:T(8,128)(2,1)S(1)}, bf16[512,256]{1,0:T(8,128)(2,1)S(1)}, u32[]{:S(2)}, u32[]{:S(2)}) collective-permute-start(bf16[512,256]{1,0:T(8,128)(2,1)S(1)} %get-tuple-element.144), channel_id=1, source_target_pairs={{0,4},{1,5},{2,6},{3,7},{4,8},{5,9},{6,10},{7,11},{8,12},{9,13},{1... | collective-permute-start | bytes 786440 | tf_op jit(solution)/shard_map/ppermute | solution.py:18
  116.8 12.1 %collective-permute-start.11 = (f32[114688]{0:T(1024)S(1)}, f32[114688]{0:T(1024)S(1)}, u32[]{:S(2)}, u32[]{:S(2)}) collective-permute-start(f32[114688]{0:T(1024)S(1)} %dynamic_slice.27), channel_id=1, source_target_pairs={{0,2},{1,3},{2,0},{3,1},{4,6},{5,7},{6,4},{7,5},{8,10},{9,11},{10,... | collective-permute-start | bytes 1376264 | tf_op jit(solution)/shard_map/ppermute | solution.py:24
  134.8 20.5 %collective-permute-start.18 = (bf16[512,256]{1,0:T(8,128)(2,1)}, bf16[512,256]{1,0:T(8,128)(2,1)S(1)}, u32[]{:S(2)}, u32[]{:S(2)}) collective-permute-start(bf16[512,256]{1,0:T(8,128)(2,1)} %slice.168), channel_id=1, source_target_pairs={{0,12},{1,13},{2,14},{3,15},{4,0},{5,1},{6,2},{7,3},{8,4},{9,5},{1... | collective-permute-start | bytes 786440 | tf_op jit(solution)/shard_map/ppermute | solution.py:18
  137.0 18.3 %collective-permute-start.19 = (bf16[512,256]{1,0:T(8,128)(2,1)}, bf16[512,256]{1,0:T(8,128)(2,1)S(1)}, u32[]{:S(2)}, u32[]{:S(2)}) collective-permute-start(bf16[512,256]{1,0:T(8,128)(2,1)} %slice.169), channel_id=1, source_target_pairs={{0,4},{1,5},{2,6},{3,7},{4,8},{5,9},{6,10},{7,11},{8,12},{9,13},{1... | collective-permute-start | bytes 786440 | tf_op jit(solution)/shard_map/ppermute | solution.py:18
  141.1 14.2 %collective-permute-start.17 = (f32[28672]{0:T(1024)S(1)}, f32[28672]{0:T(1024)S(1)}, u32[]{:S(2)}, u32[]{:S(2)}) collective-permute-start(f32[28672]{0:T(1024)S(1)} %dynamic_slice.31), channel_id=1, source_target_pairs={{0,8},{1,9},{2,10},{3,11},{4,12},{5,13},{6,14},{7,15},{8,0},{9,1},... | collective-permute-start | bytes 344072 | tf_op jit(solution)/shard_map/ppermute | solution.py:24
  144.3 27.4 %collective-permute-start.21 = (bf16[512,256]{1,0:T(8,128)(2,1)}, bf16[512,256]{1,0:T(8,128)(2,1)S(1)}, u32[]{:S(2)}, u32[]{:S(2)}) collective-permute-start(bf16[512,256]{1,0:T(8,128)(2,1)} %slice.170), channel_id=1, source_target_pairs={{0,12},{1,13},{2,14},{3,15},{4,0},{5,1},{6,2},{7,3},{8,4},{9,5},{1... | collective-permute-start | bytes 786440 | tf_op jit(solution)/shard_map/ppermute | solution.py:18
  147.4 24.4 %collective-permute-start.22 = (bf16[512,256]{1,0:T(8,128)(2,1)}, bf16[512,256]{1,0:T(8,128)(2,1)S(1)}, u32[]{:S(2)}, u32[]{:S(2)}) collective-permute-start(bf16[512,256]{1,0:T(8,128)(2,1)} %slice.171), channel_id=1, source_target_pairs={{0,4},{1,5},{2,6},{3,7},{4,8},{5,9},{6,10},{7,11},{8,12},{9,13},{1... | collective-permute-start | bytes 786440 | tf_op jit(solution)/shard_map/ppermute | solution.py:18
  155.4 16.3 %collective-permute-start.20 = (f32[56,512]{1,0:T(8,128)S(1)}, f32[56,512]{1,0:T(8,128)S(1)}, u32[]{:S(2)}, u32[]{:S(2)}) collective-permute-start(f32[56,512]{1,0:T(8,128)S(1)} %reshape.20), channel_id=1, source_target_pairs={{0,8},{1,9},{2,10},{3,11},{4,12},{5,13},{6,14},{7,15},{8,0},{9,1},... | collective-permute-start | bytes 344072 | tf_op jit(solution)/shard_map/ppermute | solution.py:24
  158.5 26.4 %collective-permute-start.24 = (bf16[512,256]{1,0:T(8,128)(2,1)S(1)}, bf16[512,256]{1,0:T(8,128)(2,1)S(1)}, u32[]{:S(2)}, u32[]{:S(2)}) collective-permute-start(bf16[512,256]{1,0:T(8,128)(2,1)S(1)} %slice.172), channel_id=1, source_target_pairs={{0,12},{1,13},{2,14},{3,15},{4,0},{5,1},{6,2},{7,3},{8,4},{9,5},{1... | collective-permute-start | bytes 786440 | tf_op jit(solution)/shard_map/ppermute | solution.py:18
  166.0 18.9 %collective-permute-start.25 = (bf16[512,256]{1,0:T(8,128)(2,1)S(1)}, bf16[512,256]{1,0:T(8,128)(2,1)S(1)}, u32[]{:S(2)}, u32[]{:S(2)}) collective-permute-start(bf16[512,256]{1,0:T(8,128)(2,1)S(1)} %slice.173), channel_id=1, source_target_pairs={{0,4},{1,5},{2,6},{3,7},{4,8},{5,9},{6,10},{7,11},{8,12},{9,13},{1... | collective-permute-start | bytes 786440 | tf_op jit(solution)/shard_map/ppermute | solution.py:18
  171.8 13.0 %collective-permute-start.23 = (f32[112,512]{1,0:T(8,128)S(1)}, f32[112,512]{1,0:T(8,128)S(1)}, u32[]{:S(2)}, u32[]{:S(2)}) collective-permute-start(f32[112,512]{1,0:T(8,128)S(1)} %pad_maximum_fusion.11), channel_id=1, source_target_pairs={{0,4},{1,5},{2,6},{3,7},{4,0},{5,1},{6,2},{7,3},{8,12},{9,13},{10,... | collective-permute-start | bytes 688136 | tf_op jit(solution)/shard_map/ppermute | solution.py:24
  178.3 25.0 %collective-permute-start.27 = (bf16[512,256]{1,0:T(8,128)(2,1)S(1)}, bf16[512,256]{1,0:T(8,128)(2,1)S(1)}, u32[]{:S(2)}, u32[]{:S(2)}) collective-permute-start(bf16[512,256]{1,0:T(8,128)(2,1)S(1)} %slice.176), channel_id=1, source_target_pairs={{0,12},{1,13},{2,14},{3,15},{4,0},{5,1},{6,2},{7,3},{8,4},{9,5},{1... | collective-permute-start | bytes 786440 | tf_op jit(solution)/shard_map/ppermute | solution.py:18
  182.1 25.1 %collective-permute-start.28 = (bf16[512,256]{1,0:T(8,128)(2,1)S(1)}, bf16[512,256]{1,0:T(8,128)(2,1)S(1)}, u32[]{:S(2)}, u32[]{:S(2)}) collective-permute-start(bf16[512,256]{1,0:T(8,128)(2,1)S(1)} %slice.177), channel_id=1, source_target_pairs={{0,4},{1,5},{2,6},{3,7},{4,8},{5,9},{6,10},{7,11},{8,12},{9,13},{1... | collective-permute-start | bytes 786440 | tf_op jit(solution)/shard_map/ppermute | solution.py:18
  191.4 15.6 %collective-permute-start.26 = (f32[224,512]{1,0:T(8,128)S(1)}, f32[224,512]{1,0:T(8,128)S(1)}, u32[]{:S(2)}, u32[]{:S(2)}) collective-permute-start(f32[224,512]{1,0:T(8,128)S(1)} %pad_maximum_fusion.10), channel_id=1, source_target_pairs={{0,2},{1,3},{2,0},{3,1},{4,6},{5,7},{6,4},{7,5},{8,10},{9,11},{10,... | collective-permute-start | bytes 1376264 | tf_op jit(solution)/shard_map/ppermute | solution.py:24
  194.0 14.3 %collective-permute-start.29 = (bf16[512,256]{1,0:T(8,128)(2,1)S(1)}, bf16[512,256]{1,0:T(8,128)(2,1)S(1)}, u32[]{:S(2)}, u32[]{:S(2)}) collective-permute-start(bf16[512,256]{1,0:T(8,128)(2,1)S(1)} %get-tuple-element.130), channel_id=1, source_target_pairs={{0,12},{1,13},{2,14},{3,15},{4,0},{5,1},{6,2},{7,3},{8,4},{9,5},{1... | collective-permute-start | bytes 786440 | tf_op jit(solution)/shard_map/ppermute | solution.py:18
  203.2 9.2 %collective-permute-start.30 = (bf16[512,256]{1,0:T(8,128)(2,1)S(1)}, bf16[512,256]{1,0:T(8,128)(2,1)S(1)}, u32[]{:S(2)}, u32[]{:S(2)}) collective-permute-start(bf16[512,256]{1,0:T(8,128)(2,1)S(1)} %get-tuple-element.128), channel_id=1, source_target_pairs={{0,4},{1,5},{2,6},{3,7},{4,8},{5,9},{6,10},{7,11},{8,12},{9,13},{1... | collective-permute-start | bytes 786440 | tf_op jit(solution)/shard_map/ppermute | solution.py:18
  203.3 11.8 %collective-permute-start.31 = (bf16[512,256]{1,0:T(8,128)(2,1)S(1)}, bf16[512,256]{1,0:T(8,128)(2,1)S(1)}, u32[]{:S(2)}, u32[]{:S(2)}) collective-permute-start(bf16[512,256]{1,0:T(8,128)(2,1)S(1)} %get-tuple-element.129), channel_id=1, source_target_pairs={{0,12},{1,13},{2,14},{3,15},{4,0},{5,1},{6,2},{7,3},{8,4},{9,5},{1... | collective-permute-start | bytes 786440 | tf_op jit(solution)/shard_map/ppermute | solution.py:18
  207.1 10.9 %collective-permute-start.32 = (bf16[512,256]{1,0:T(8,128)(2,1)S(1)}, bf16[512,256]{1,0:T(8,128)(2,1)S(1)}, u32[]{:S(2)}, u32[]{:S(2)}) collective-permute-start(bf16[512,256]{1,0:T(8,128)(2,1)S(1)} %get-tuple-element.127), channel_id=1, source_target_pairs={{0,4},{1,5},{2,6},{3,7},{4,8},{5,9},{6,10},{7,11},{8,12},{9,13},{1... | collective-permute-start | bytes 786440 | tf_op jit(solution)/shard_map/ppermute | solution.py:18
  (21 other events, 294.2 us)

commit v20 on v11

--- a/solution.py
+++ b/solution.py
@@ -101,9 +101,7 @@
                 (left_tap_input, right_tap_input, lows[:EARLY], highs[:EARLY])
             )
             for low, high in zip(lows_early, highs_early):
-                half = low.shape[0] // 2
-                for part in (slice(0, half), slice(half, low.shape[0])):
-                    early.append((from_behind(low[part], "seq", -spacing), from_behind(high[part], "seq", spacing)))
+                early.append((from_behind(low, "seq", -spacing), from_behind(high, "seq", spacing)))
         if wconv_total is not None:
             left_tap_input, right_tap_input, wconv_total, wout_total = lax.optimization_barrier(
                 (left_tap_input, right_tap_input, wconv_total, wout_total)

time: 223 us -> 222 us (level)
  waiting for transfers between devices: 62.6 us -> 66.7 us
  starting transfers between devices: 99.4 us -> 96.2 us
    ppermute x26 -> x24, starting transfers between devices: 85.3 us -> 82 us  [from_behind(): return lax.ppermute(value, axis, pairs)]
    ppermute x26 -> x24, waiting for transfers between devices: 36.8 us -> 39.6 us  [from_behind(): return lax.ppermute(value, axis, pairs)]
    unnamed x44 -> x42, local copies, waits for them, and re-layouts: 5.04 us -> 3.48 us
  transfers between devices with their start and end apart: 34 -> 32, of which waited for: 14 -> 14; matrix products, arithmetic and copies ran while one was open for 22% -> 22% of each run, Pallas kernels for 0% -> 0%
where the time goes in v20:
time: 222 us
  starting transfers between devices  96.2 us (43%)
  waiting for transfers between devices  66.7 us (30%)
  matrix products  33.5 us (15%)
  local copies, waits for them, and re-layouts  17.9 us (8%)
  other arithmetic  5.77 us (3%)
    ppermute x24, starting transfers between devices, from_behind(): return lax.ppermute(value, axis, pairs)  82 us
    ppermute x24, waiting for transfers between devices, from_behind(): return lax.ppermute(value, axis, pairs)  39.6 us
    ppermute x8, waiting for transfers between devices, exchange(): return lax.ppermute(value, axis, pairs)  27 us
    ppermute x8, starting transfers between devices, exchange(): return lax.ppermute(value, axis, pairs)  14.2 us
    dot_general x5, matrix products, chunk_layer(): preact = preact + jnp.dot(middle, w_mid, preferred_element_type=jnp.float32)  4.64 us
    slice x2, local copies, waits for them, and re-layouts, body(): middle = activations[bounds[k]:bounds[k + 1]]  4.54 us
    slice x5, local copies, waits for them, and re-layouts, send_rows(): low_high[0][start:stop]  4.47 us
  transfers between devices with their start and end apart: 32, of which 14 were waited for; matrix products, arithmetic and copies ran while one was open for 22% of the time, Pallas kernels for 0%

profile of v20, /device:TPU:0, one launch (start us, length us, event | category | flops | bytes accessed | tf_op | source)
XLA Modules:
  0.0 221.8 jit_solution(15517058344009474636)
XLA Ops:
  0.7 2.0 fusion.119
  2.7 3.0 %collective-permute-start.8 = (bf16[512,256]{1,0:T(8,128)(2,1)}, bf16[512,256]{1,0:T(8,128)(2,1)S(1)}, u32[]{:S(2)}, u32[]{:S(2)}) collective-permute-start(bf16[512,256]{1,0:T(8,128)(2,1)} %get-tuple-element.127), channel_id=1, source_target_pairs={{0,4},{1,5},{2,6},{3,7},{4,8},{5,9},{6,10},{7,11},{8,12},{9,13},{1... | collective-permute-start | bytes 786440 | tf_op jit(solution)/shard_map/ppermute | solution.py:18
  5.7 2.0 collective-permute-start.9
  7.7 2.5 %fusion.118 = (bf16[1024,256]{1,0:T(8,128)(2,1)}, bf16[1024,256]{1,0:T(8,128)(2,1)}, bf16[1024,256]{1,0:T(8,128)(2,1)}) fusion(bf16[4096,256]{1,0:T(8,128)(2,1)} %param.4), kind=kLoop, calls=%fused_computation.206 | loop fusion | bytes 3145728 | tf_op jit(solution)/shard_map/slice | solution.py:95
  10.3 3.8 %collective-permute-start.1 = (bf16[1024,256]{1,0:T(8,128)(2,1)}, bf16[1024,256]{1,0:T(8,128)(2,1)}, u32[]{:S(2)}, u32[]{:S(2)}) collective-permute-start(bf16[1024,256]{1,0:T(8,128)(2,1)} %get-tuple-element.125), channel_id=1, source_target_pairs={{0,12},{1,13},{2,14},{3,15},{4,0},{5,1},{6,2},{7,3},{8,4},{9,5},{1... | collective-permute-start | bytes 1572872 | tf_op jit(solution)/shard_map/ppermute | solution.py:18
  14.1 1.8 fusion.77
  18.6 13.5 %collective-permute-done = bf16[1024,256]{1,0:T(8,128)(2,1)} collective-permute-done((bf16[1024,256]{1,0:T(8,128)(2,1)}, bf16[1024,256]{1,0:T(8,128)(2,1)}, u32[]{:S(2)}, u32[]{:S(2)}) %collective-permute-start) | collective-permute-done | bytes 524320 | tf_op jit(solution)/shard_map/ppermute | solution.py:18
  32.1 13.2 %collective-permute-start.3 = (bf16[1024,256]{1,0:T(8,128)(2,1)}, bf16[1024,256]{1,0:T(8,128)(2,1)S(1)}, u32[]{:S(2)}, u32[]{:S(2)}) collective-permute-start(bf16[1024,256]{1,0:T(8,128)(2,1)} %get-tuple-element.123), channel_id=1, source_target_pairs={{0,12},{1,13},{2,14},{3,15},{4,0},{5,1},{6,2},{7,3},{8,4},{9,5},{1... | collective-permute-start | bytes 1572872 | tf_op jit(solution)/shard_map/ppermute | solution.py:18
  47.0 1.7 add_add_fusion.2
  54.6 13.2 %collective-permute-start.5 = (bf16[1024,256]{1,0:T(8,128)(2,1)S(1)}, bf16[1024,256]{1,0:T(8,128)(2,1)S(1)}, u32[]{:S(2)}, u32[]{:S(2)}) collective-permute-start(bf16[1024,256]{1,0:T(8,128)(2,1)S(1)} %copy-done.12), channel_id=1, source_target_pairs={{0,12},{1,13},{2,14},{3,15},{4,0},{5,1},{6,2},{7,3},{8,4},{9,5},{1... | collective-permute-start | bytes 1572872 | tf_op jit(solution)/shard_map/ppermute | solution.py:18
  67.8 8.3 %collective-permute-start.6 = (bf16[512,256]{1,0:T(8,128)(2,1)S(1)}, bf16[512,256]{1,0:T(8,128)(2,1)S(1)}, u32[]{:S(2)}, u32[]{:S(2)}) collective-permute-start(bf16[512,256]{1,0:T(8,128)(2,1)S(1)} %copy-done.13), channel_id=1, source_target_pairs={{0,4},{1,5},{2,6},{3,7},{4,8},{5,9},{6,10},{7,11},{8,12},{9,13},{1... | collective-permute-start | bytes 786440 | tf_op jit(solution)/shard_map/ppermute | solution.py:18
  82.3 7.8 %collective-permute-start.7 = (bf16[512,256]{1,0:T(8,128)(2,1)S(1)}, bf16[512,256]{1,0:T(8,128)(2,1)S(1)}, u32[]{:S(2)}, u32[]{:S(2)}) collective-permute-start(bf16[512,256]{1,0:T(8,128)(2,1)S(1)} %copy-done.13), channel_id=1, source_target_pairs={{0,12},{1,13},{2,14},{3,15},{4,0},{5,1},{6,2},{7,3},{8,4},{9,5},{1... | collective-permute-start | bytes 786440 | tf_op jit(solution)/shard_map/ppermute | solution.py:18
  94.8 3.1 %collective-permute-done.7 = bf16[512,256]{1,0:T(8,128)(2,1)S(1)} collective-permute-done((bf16[512,256]{1,0:T(8,128)(2,1)S(1)}, bf16[512,256]{1,0:T(8,128)(2,1)S(1)}, u32[]{:S(2)}, u32[]{:S(2)}) %collective-permute-start.7) | collective-permute-done | bytes 262176 | tf_op jit(solution)/shard_map/ppermute | solution.py:18
  105.5 2.4 %collective-permute-start.12 = (bf16[1024,256]{1,0:T(8,128)(2,1)S(1)}, bf16[1024,256]{1,0:T(8,128)(2,1)S(1)}, u32[]{:S(2)}, u32[]{:S(2)}) collective-permute-start(bf16[1024,256]{1,0:T(8,128)(2,1)S(1)} %get-tuple-element.76), channel_id=1, source_target_pairs={{0,12},{1,13},{2,14},{3,15},{4,0},{5,1},{6,2},{7,3},{8,4},{9,5},{1... | collective-permute-start | bytes 1572872 | tf_op jit(solution)/shard_map/ppermute | solution.py:18
  114.8 10.4 %collective-permute-done.11 = f32[114688]{0:T(1024)S(1)} collective-permute-done((f32[114688]{0:T(1024)S(1)}, f32[114688]{0:T(1024)S(1)}, u32[]{:S(2)}, u32[]{:S(2)}) %collective-permute-start.11) | collective-permute-done | bytes 458784 | tf_op jit(solution)/shard_map/ppermute | solution.py:24
  125.2 6.6 %collective-permute-done.13 = bf16[1024,256]{1,0:T(8,128)(2,1)S(1)} collective-permute-done((bf16[1024,256]{1,0:T(8,128)(2,1)S(1)}, bf16[1024,256]{1,0:T(8,128)(2,1)S(1)}, u32[]{:S(2)}, u32[]{:S(2)}) %collective-permute-start.13) | collective-permute-done | bytes 524320 | tf_op jit(solution)/shard_map/ppermute | solution.py:18
  137.3 3.1 %collective-permute-done.14 = f32[57344]{0:T(1024)S(1)} collective-permute-done((f32[57344]{0:T(1024)S(1)}, f32[57344]{0:T(1024)S(1)}, u32[]{:S(2)}, u32[]{:S(2)}) %collective-permute-start.14) | collective-permute-done | bytes 229408 | tf_op jit(solution)/shard_map/ppermute | solution.py:24
  143.7 2.4 %collective-permute-start.19 = (bf16[512,256]{1,0:T(8,128)(2,1)}, bf16[512,256]{1,0:T(8,128)(2,1)S(1)}, u32[]{:S(2)}, u32[]{:S(2)}) collective-permute-start(bf16[512,256]{1,0:T(8,128)(2,1)} %slice.148), channel_id=1, source_target_pairs={{0,12},{1,13},{2,14},{3,15},{4,0},{5,1},{6,2},{7,3},{8,4},{9,5},{1... | collective-permute-start | bytes 786440 | tf_op jit(solution)/shard_map/ppermute | solution.py:18
  146.8 7.9 %collective-permute-done.15 = f32[28672]{0:T(1024)S(1)} collective-permute-done((f32[28672]{0:T(1024)S(1)}, f32[28672]{0:T(1024)S(1)}, u32[]{:S(2)}, u32[]{:S(2)}) %collective-permute-start.15) | collective-permute-done | bytes 114720 | tf_op jit(solution)/shard_map/ppermute | solution.py:24
  154.7 2.1 collective-permute-start.18
  157.8 6.7 %collective-permute-start.22 = (bf16[512,256]{1,0:T(8,128)(2,1)S(1)}, bf16[512,256]{1,0:T(8,128)(2,1)S(1)}, u32[]{:S(2)}, u32[]{:S(2)}) collective-permute-start(bf16[512,256]{1,0:T(8,128)(2,1)S(1)} %slice.150), channel_id=1, source_target_pairs={{0,12},{1,13},{2,14},{3,15},{4,0},{5,1},{6,2},{7,3},{8,4},{9,5},{1... | collective-permute-start | bytes 786440 | tf_op jit(solution)/shard_map/ppermute | solution.py:18
  167.8 3.3 %collective-permute-done.18 = f32[56,512]{1,0:T(8,128)S(1)} collective-permute-done((f32[56,512]{1,0:T(8,128)S(1)}, f32[56,512]{1,0:T(8,128)S(1)}, u32[]{:S(2)}, u32[]{:S(2)}) %collective-permute-start.18) | collective-permute-done | bytes 114720 | tf_op jit(solution)/shard_map/ppermute | solution.py:24
  171.1 5.7 %collective-permute-start.21 = (f32[112,512]{1,0:T(8,128)S(1)}, f32[112,512]{1,0:T(8,128)S(1)}, u32[]{:S(2)}, u32[]{:S(2)}) collective-permute-start(f32[112,512]{1,0:T(8,128)S(1)} %pad_maximum_fusion.9), channel_id=1, source_target_pairs={{0,4},{1,5},{2,6},{3,7},{4,0},{5,1},{6,2},{7,3},{8,12},{9,13},{10,... | collective-permute-start | bytes 688136 | tf_op jit(solution)/shard_map/ppermute | solution.py:24
  177.8 2.9 %collective-permute-start.25 = (bf16[512,256]{1,0:T(8,128)(2,1)S(1)}, bf16[512,256]{1,0:T(8,128)(2,1)S(1)}, u32[]{:S(2)}, u32[]{:S(2)}) collective-permute-start(bf16[512,256]{1,0:T(8,128)(2,1)S(1)} %slice.152), channel_id=1, source_target_pairs={{0,12},{1,13},{2,14},{3,15},{4,0},{5,1},{6,2},{7,3},{8,4},{9,5},{1... | collective-permute-start | bytes 786440 | tf_op jit(solution)/shard_map/ppermute | solution.py:18
  181.8 2.3 %collective-permute-done.21 = f32[112,512]{1,0:T(8,128)S(1)} collective-permute-done((f32[112,512]{1,0:T(8,128)S(1)}, f32[112,512]{1,0:T(8,128)S(1)}, u32[]{:S(2)}, u32[]{:S(2)}) %collective-permute-start.21) | collective-permute-done | bytes 229408 | tf_op jit(solution)/shard_map/ppermute | solution.py:24
  186.8 9.7 %collective-permute-start.27 = (bf16[512,256]{1,0:T(8,128)(2,1)S(1)}, bf16[512,256]{1,0:T(8,128)(2,1)S(1)}, u32[]{:S(2)}, u32[]{:S(2)}) collective-permute-start(bf16[512,256]{1,0:T(8,128)(2,1)S(1)} %get-tuple-element.122), channel_id=1, source_target_pairs={{0,12},{1,13},{2,14},{3,15},{4,0},{5,1},{6,2},{7,3},{8,4},{9,5},{1... | collective-permute-start | bytes 786440 | tf_op jit(solution)/shard_map/ppermute | solution.py:18
  197.7 3.9 %collective-permute-start.29 = (bf16[512,256]{1,0:T(8,128)(2,1)S(1)}, bf16[512,256]{1,0:T(8,128)(2,1)S(1)}, u32[]{:S(2)}, u32[]{:S(2)}) collective-permute-start(bf16[512,256]{1,0:T(8,128)(2,1)S(1)} %get-tuple-element.121), channel_id=1, source_target_pairs={{0,12},{1,13},{2,14},{3,15},{4,0},{5,1},{6,2},{7,3},{8,4},{9,5},{1... | collective-permute-start | bytes 786440 | tf_op jit(solution)/shard_map/ppermute | solution.py:18
  201.7 2.0 collective-permute-done.27
  203.7 5.7 %collective-permute-done.28 = bf16[512,256]{1,0:T(8,128)(2,1)S(1)} collective-permute-done((bf16[512,256]{1,0:T(8,128)(2,1)S(1)}, bf16[512,256]{1,0:T(8,128)(2,1)S(1)}, u32[]{:S(2)}, u32[]{:S(2)}) %collective-permute-start.28) | collective-permute-done | bytes 262176 | tf_op jit(solution)/shard_map/ppermute | solution.py:18
  209.5 4.4 %collective-permute-done.29 = bf16[512,256]{1,0:T(8,128)(2,1)S(1)} collective-permute-done((bf16[512,256]{1,0:T(8,128)(2,1)S(1)}, bf16[512,256]{1,0:T(8,128)(2,1)S(1)}, u32[]{:S(2)}, u32[]{:S(2)}) %collective-permute-start.29) | collective-permute-done | bytes 262176 | tf_op jit(solution)/shard_map/ppermute | solution.py:18
  213.8 3.3 %collective-permute-done.30 = bf16[512,256]{1,0:T(8,128)(2,1)S(1)} collective-permute-done((bf16[512,256]{1,0:T(8,128)(2,1)S(1)}, bf16[512,256]{1,0:T(8,128)(2,1)S(1)}, u32[]{:S(2)}, u32[]{:S(2)}) %collective-permute-start.30) | collective-permute-done | bytes 262176 | tf_op jit(solution)/shard_map/ppermute | solution.py:18
  217.3 2.2 add_convert_fusion
  (172 shorter events, 57.3 us)
Async XLA Ops:
  2.7 98.3 %collective-permute-start.8 = (bf16[512,256]{1,0:T(8,128)(2,1)}, bf16[512,256]{1,0:T(8,128)(2,1)S(1)}, u32[]{:S(2)}, u32[]{:S(2)}) collective-permute-start(bf16[512,256]{1,0:T(8,128)(2,1)} %get-tuple-element.127), channel_id=1, source_target_pairs={{0,4},{1,5},{2,6},{3,7},{4,8},{5,9},{6,10},{7,11},{8,12},{9,13},{1... | collective-permute-start | bytes 786440 | tf_op jit(solution)/shard_map/ppermute | solution.py:18
  5.7 95.3 %collective-permute-start.9 = (bf16[512,256]{1,0:T(8,128)(2,1)}, bf16[512,256]{1,0:T(8,128)(2,1)S(1)}, u32[]{:S(2)}, u32[]{:S(2)}) collective-permute-start(bf16[512,256]{1,0:T(8,128)(2,1)} %get-tuple-element.127), channel_id=1, source_target_pairs={{0,12},{1,13},{2,14},{3,15},{4,0},{5,1},{6,2},{7,3},{8,4},{9,5},{1... | collective-permute-start | bytes 786440 | tf_op jit(solution)/shard_map/ppermute | solution.py:18
  10.3 21.9 %collective-permute-start = (bf16[1024,256]{1,0:T(8,128)(2,1)}, bf16[1024,256]{1,0:T(8,128)(2,1)}, u32[]{:S(2)}, u32[]{:S(2)}) collective-permute-start(bf16[1024,256]{1,0:T(8,128)(2,1)} %get-tuple-element.125), channel_id=1, source_target_pairs={{0,4},{1,5},{2,6},{3,7},{4,8},{5,9},{6,10},{7,11},{8,12},{9,13},{1... | collective-permute-start | bytes 1572872 | tf_op jit(solution)/shard_map/ppermute | solution.py:18
  10.3 36.6 %collective-permute-start.1 = (bf16[1024,256]{1,0:T(8,128)(2,1)}, bf16[1024,256]{1,0:T(8,128)(2,1)}, u32[]{:S(2)}, u32[]{:S(2)}) collective-permute-start(bf16[1024,256]{1,0:T(8,128)(2,1)} %get-tuple-element.125), channel_id=1, source_target_pairs={{0,12},{1,13},{2,14},{3,15},{4,0},{5,1},{6,2},{7,3},{8,4},{9,5},{1... | collective-permute-start | bytes 1572872 | tf_op jit(solution)/shard_map/ppermute | solution.py:18
  14.1 40.5 %collective-permute-start.2 = (bf16[1024,256]{1,0:T(8,128)(2,1)}, bf16[1024,256]{1,0:T(8,128)(2,1)}, u32[]{:S(2)}, u32[]{:S(2)}) collective-permute-start(bf16[1024,256]{1,0:T(8,128)(2,1)} %get-tuple-element.123), channel_id=1, source_target_pairs={{0,4},{1,5},{2,6},{3,7},{4,8},{5,9},{6,10},{7,11},{8,12},{9,13},{1... | collective-permute-start | bytes 1572872 | tf_op jit(solution)/shard_map/ppermute | solution.py:18
  32.1 35.7 %collective-permute-start.3 = (bf16[1024,256]{1,0:T(8,128)(2,1)}, bf16[1024,256]{1,0:T(8,128)(2,1)S(1)}, u32[]{:S(2)}, u32[]{:S(2)}) collective-permute-start(bf16[1024,256]{1,0:T(8,128)(2,1)} %get-tuple-element.123), channel_id=1, source_target_pairs={{0,12},{1,13},{2,14},{3,15},{4,0},{5,1},{6,2},{7,3},{8,4},{9,5},{1... | collective-permute-start | bytes 1572872 | tf_op jit(solution)/shard_map/ppermute | solution.py:18
  46.9 35.4 %collective-permute-start.4 = (bf16[1024,256]{1,0:T(8,128)(2,1)S(1)}, bf16[1024,256]{1,0:T(8,128)(2,1)S(1)}, u32[]{:S(2)}, u32[]{:S(2)}) collective-permute-start(bf16[1024,256]{1,0:T(8,128)(2,1)S(1)} %copy-done.12), channel_id=1, source_target_pairs={{0,4},{1,5},{2,6},{3,7},{4,8},{5,9},{6,10},{7,11},{8,12},{9,13},{1... | collective-permute-start | bytes 1572872 | tf_op jit(solution)/shard_map/ppermute | solution.py:18
  54.6 35.5 %collective-permute-start.5 = (bf16[1024,256]{1,0:T(8,128)(2,1)S(1)}, bf16[1024,256]{1,0:T(8,128)(2,1)S(1)}, u32[]{:S(2)}, u32[]{:S(2)}) collective-permute-start(bf16[1024,256]{1,0:T(8,128)(2,1)S(1)} %copy-done.12), channel_id=1, source_target_pairs={{0,12},{1,13},{2,14},{3,15},{4,0},{5,1},{6,2},{7,3},{8,4},{9,5},{1... | collective-permute-start | bytes 1572872 | tf_op jit(solution)/shard_map/ppermute | solution.py:18
  67.8 27.0 %collective-permute-start.6 = (bf16[512,256]{1,0:T(8,128)(2,1)S(1)}, bf16[512,256]{1,0:T(8,128)(2,1)S(1)}, u32[]{:S(2)}, u32[]{:S(2)}) collective-permute-start(bf16[512,256]{1,0:T(8,128)(2,1)S(1)} %copy-done.13), channel_id=1, source_target_pairs={{0,4},{1,5},{2,6},{3,7},{4,8},{5,9},{6,10},{7,11},{8,12},{9,13},{1... | collective-permute-start | bytes 786440 | tf_op jit(solution)/shard_map/ppermute | solution.py:18
  82.3 15.6 %collective-permute-start.7 = (bf16[512,256]{1,0:T(8,128)(2,1)S(1)}, bf16[512,256]{1,0:T(8,128)(2,1)S(1)}, u32[]{:S(2)}, u32[]{:S(2)}) collective-permute-start(bf16[512,256]{1,0:T(8,128)(2,1)S(1)} %copy-done.13), channel_id=1, source_target_pairs={{0,12},{1,13},{2,14},{3,15},{4,0},{5,1},{6,2},{7,3},{8,4},{9,5},{1... | collective-permute-start | bytes 786440 | tf_op jit(solution)/shard_map/ppermute | solution.py:18
  105.4 7.0 %collective-permute-start.10 = (f32[229376]{0:T(1024)S(1)}, f32[229376]{0:T(1024)S(1)}, u32[]{:S(2)}, u32[]{:S(2)}) collective-permute-start(f32[229376]{0:T(1024)S(1)} %dynamic_slice.25), channel_id=1, source_target_pairs={{0,1},{1,0},{2,3},{3,2},{4,5},{5,4},{6,7},{7,6},{8,9},{9,8},{10,11... | collective-permute-start | bytes 2752520 | tf_op jit(solution)/shard_map/ppermute | solution.py:24
  105.5 19.8 %collective-permute-start.12 = (bf16[1024,256]{1,0:T(8,128)(2,1)S(1)}, bf16[1024,256]{1,0:T(8,128)(2,1)S(1)}, u32[]{:S(2)}, u32[]{:S(2)}) collective-permute-start(bf16[1024,256]{1,0:T(8,128)(2,1)S(1)} %get-tuple-element.76), channel_id=1, source_target_pairs={{0,12},{1,13},{2,14},{3,15},{4,0},{5,1},{6,2},{7,3},{8,4},{9,5},{1... | collective-permute-start | bytes 1572872 | tf_op jit(solution)/shard_map/ppermute | solution.py:18
  107.8 24.0 %collective-permute-start.13 = (bf16[1024,256]{1,0:T(8,128)(2,1)S(1)}, bf16[1024,256]{1,0:T(8,128)(2,1)S(1)}, u32[]{:S(2)}, u32[]{:S(2)}) collective-permute-start(bf16[1024,256]{1,0:T(8,128)(2,1)S(1)} %get-tuple-element.77), channel_id=1, source_target_pairs={{0,4},{1,5},{2,6},{3,7},{4,8},{5,9},{6,10},{7,11},{8,12},{9,13},{1... | collective-permute-start | bytes 1572872 | tf_op jit(solution)/shard_map/ppermute | solution.py:18
  112.5 12.7 %collective-permute-start.11 = (f32[114688]{0:T(1024)S(1)}, f32[114688]{0:T(1024)S(1)}, u32[]{:S(2)}, u32[]{:S(2)}) collective-permute-start(f32[114688]{0:T(1024)S(1)} %dynamic_slice.27), channel_id=1, source_target_pairs={{0,2},{1,3},{2,0},{3,1},{4,6},{5,7},{6,4},{7,5},{8,10},{9,11},{10,... | collective-permute-start | bytes 1376264 | tf_op jit(solution)/shard_map/ppermute | solution.py:24
  131.8 8.6 %collective-permute-start.14 = (f32[57344]{0:T(1024)S(1)}, f32[57344]{0:T(1024)S(1)}, u32[]{:S(2)}, u32[]{:S(2)}) collective-permute-start(f32[57344]{0:T(1024)S(1)} %dynamic_slice.29), channel_id=1, source_target_pairs={{0,4},{1,5},{2,6},{3,7},{4,0},{5,1},{6,2},{7,3},{8,12},{9,13},{10,... | collective-permute-start | bytes 688136 | tf_op jit(solution)/shard_map/ppermute | solution.py:24
  134.6 20.1 %collective-permute-start.16 = (bf16[512,256]{1,0:T(8,128)(2,1)}, bf16[512,256]{1,0:T(8,128)(2,1)S(1)}, u32[]{:S(2)}, u32[]{:S(2)}) collective-permute-start(bf16[512,256]{1,0:T(8,128)(2,1)} %slice.146), channel_id=1, source_target_pairs={{0,12},{1,13},{2,14},{3,15},{4,0},{5,1},{6,2},{7,3},{8,4},{9,5},{1... | collective-permute-start | bytes 786440 | tf_op jit(solution)/shard_map/ppermute | solution.py:18
  136.7 18.0 %collective-permute-start.17 = (bf16[512,256]{1,0:T(8,128)(2,1)}, bf16[512,256]{1,0:T(8,128)(2,1)}, u32[]{:S(2)}, u32[]{:S(2)}) collective-permute-start(bf16[512,256]{1,0:T(8,128)(2,1)} %slice.147), channel_id=1, source_target_pairs={{0,4},{1,5},{2,6},{3,7},{4,8},{5,9},{6,10},{7,11},{8,12},{9,13},{1... | collective-permute-start | bytes 786440 | tf_op jit(solution)/shard_map/ppermute | solution.py:18
  140.5 14.2 %collective-permute-start.15 = (f32[28672]{0:T(1024)S(1)}, f32[28672]{0:T(1024)S(1)}, u32[]{:S(2)}, u32[]{:S(2)}) collective-permute-start(f32[28672]{0:T(1024)S(1)} %dynamic_slice.31), channel_id=1, source_target_pairs={{0,8},{1,9},{2,10},{3,11},{4,12},{5,13},{6,14},{7,15},{8,0},{9,1},... | collective-permute-start | bytes 344072 | tf_op jit(solution)/shard_map/ppermute | solution.py:24
  143.7 27.4 %collective-permute-start.19 = (bf16[512,256]{1,0:T(8,128)(2,1)}, bf16[512,256]{1,0:T(8,128)(2,1)S(1)}, u32[]{:S(2)}, u32[]{:S(2)}) collective-permute-start(bf16[512,256]{1,0:T(8,128)(2,1)} %slice.148), channel_id=1, source_target_pairs={{0,12},{1,13},{2,14},{3,15},{4,0},{5,1},{6,2},{7,3},{8,4},{9,5},{1... | collective-permute-start | bytes 786440 | tf_op jit(solution)/shard_map/ppermute | solution.py:18
  146.8 24.4 %collective-permute-start.20 = (bf16[512,256]{1,0:T(8,128)(2,1)}, bf16[512,256]{1,0:T(8,128)(2,1)S(1)}, u32[]{:S(2)}, u32[]{:S(2)}) collective-permute-start(bf16[512,256]{1,0:T(8,128)(2,1)} %slice.149), channel_id=1, source_target_pairs={{0,4},{1,5},{2,6},{3,7},{4,8},{5,9},{6,10},{7,11},{8,12},{9,13},{1... | collective-permute-start | bytes 786440 | tf_op jit(solution)/shard_map/ppermute | solution.py:18
  154.7 16.3 %collective-permute-start.18 = (f32[56,512]{1,0:T(8,128)S(1)}, f32[56,512]{1,0:T(8,128)S(1)}, u32[]{:S(2)}, u32[]{:S(2)}) collective-permute-start(f32[56,512]{1,0:T(8,128)S(1)} %reshape.20), channel_id=1, source_target_pairs={{0,8},{1,9},{2,10},{3,11},{4,12},{5,13},{6,14},{7,15},{8,0},{9,1},... | collective-permute-start | bytes 344072 | tf_op jit(solution)/shard_map/ppermute | solution.py:24
  157.8 26.3 %collective-permute-start.22 = (bf16[512,256]{1,0:T(8,128)(2,1)S(1)}, bf16[512,256]{1,0:T(8,128)(2,1)S(1)}, u32[]{:S(2)}, u32[]{:S(2)}) collective-permute-start(bf16[512,256]{1,0:T(8,128)(2,1)S(1)} %slice.150), channel_id=1, source_target_pairs={{0,12},{1,13},{2,14},{3,15},{4,0},{5,1},{6,2},{7,3},{8,4},{9,5},{1... | collective-permute-start | bytes 786440 | tf_op jit(solution)/shard_map/ppermute | solution.py:18
  165.5 18.7 %collective-permute-start.23 = (bf16[512,256]{1,0:T(8,128)(2,1)S(1)}, bf16[512,256]{1,0:T(8,128)(2,1)S(1)}, u32[]{:S(2)}, u32[]{:S(2)}) collective-permute-start(bf16[512,256]{1,0:T(8,128)(2,1)S(1)} %slice.151), channel_id=1, source_target_pairs={{0,4},{1,5},{2,6},{3,7},{4,8},{5,9},{6,10},{7,11},{8,12},{9,13},{1... | collective-permute-start | bytes 786440 | tf_op jit(solution)/shard_map/ppermute | solution.py:18
  171.1 12.9 %collective-permute-start.21 = (f32[112,512]{1,0:T(8,128)S(1)}, f32[112,512]{1,0:T(8,128)S(1)}, u32[]{:S(2)}, u32[]{:S(2)}) collective-permute-start(f32[112,512]{1,0:T(8,128)S(1)} %pad_maximum_fusion.9), channel_id=1, source_target_pairs={{0,4},{1,5},{2,6},{3,7},{4,0},{5,1},{6,2},{7,3},{8,12},{9,13},{10,... | collective-permute-start | bytes 688136 | tf_op jit(solution)/shard_map/ppermute | solution.py:24
  177.8 19.9 %collective-permute-start.25 = (bf16[512,256]{1,0:T(8,128)(2,1)S(1)}, bf16[512,256]{1,0:T(8,128)(2,1)S(1)}, u32[]{:S(2)}, u32[]{:S(2)}) collective-permute-start(bf16[512,256]{1,0:T(8,128)(2,1)S(1)} %slice.152), channel_id=1, source_target_pairs={{0,12},{1,13},{2,14},{3,15},{4,0},{5,1},{6,2},{7,3},{8,4},{9,5},{1... | collective-permute-start | bytes 786440 | tf_op jit(solution)/shard_map/ppermute | solution.py:18
  181.6 20.1 %collective-permute-start.26 = (bf16[512,256]{1,0:T(8,128)(2,1)S(1)}, bf16[512,256]{1,0:T(8,128)(2,1)S(1)}, u32[]{:S(2)}, u32[]{:S(2)}) collective-permute-start(bf16[512,256]{1,0:T(8,128)(2,1)S(1)} %slice.153), channel_id=1, source_target_pairs={{0,4},{1,5},{2,6},{3,7},{4,8},{5,9},{6,10},{7,11},{8,12},{9,13},{1... | collective-permute-start | bytes 786440 | tf_op jit(solution)/shard_map/ppermute | solution.py:18
  184.2 17.4 %collective-permute-start.24 = (f32[224,512]{1,0:T(8,128)S(1)}, f32[224,512]{1,0:T(8,128)S(1)}, u32[]{:S(2)}, u32[]{:S(2)}) collective-permute-start(f32[224,512]{1,0:T(8,128)S(1)} %pad_maximum_fusion.8), channel_id=1, source_target_pairs={{0,2},{1,3},{2,0},{3,1},{4,6},{5,7},{6,4},{7,5},{8,10},{9,11},{10,... | collective-permute-start | bytes 1376264 | tf_op jit(solution)/shard_map/ppermute | solution.py:24
  186.8 17.0 %collective-permute-start.27 = (bf16[512,256]{1,0:T(8,128)(2,1)S(1)}, bf16[512,256]{1,0:T(8,128)(2,1)S(1)}, u32[]{:S(2)}, u32[]{:S(2)}) collective-permute-start(bf16[512,256]{1,0:T(8,128)(2,1)S(1)} %get-tuple-element.122), channel_id=1, source_target_pairs={{0,12},{1,13},{2,14},{3,15},{4,0},{5,1},{6,2},{7,3},{8,4},{9,5},{1... | collective-permute-start | bytes 786440 | tf_op jit(solution)/shard_map/ppermute | solution.py:18
  197.5 11.9 %collective-permute-start.28 = (bf16[512,256]{1,0:T(8,128)(2,1)S(1)}, bf16[512,256]{1,0:T(8,128)(2,1)S(1)}, u32[]{:S(2)}, u32[]{:S(2)}) collective-permute-start(bf16[512,256]{1,0:T(8,128)(2,1)S(1)} %get-tuple-element.120), channel_id=1, source_target_pairs={{0,4},{1,5},{2,6},{3,7},{4,8},{5,9},{6,10},{7,11},{8,12},{9,13},{1... | collective-permute-start | bytes 786440 | tf_op jit(solution)/shard_map/ppermute | solution.py:18
  197.7 16.2 %collective-permute-start.29 = (bf16[512,256]{1,0:T(8,128)(2,1)S(1)}, bf16[512,256]{1,0:T(8,128)(2,1)S(1)}, u32[]{:S(2)}, u32[]{:S(2)}) collective-permute-start(bf16[512,256]{1,0:T(8,128)(2,1)S(1)} %get-tuple-element.121), channel_id=1, source_target_pairs={{0,12},{1,13},{2,14},{3,15},{4,0},{5,1},{6,2},{7,3},{8,4},{9,5},{1... | collective-permute-start | bytes 786440 | tf_op jit(solution)/shard_map/ppermute | solution.py:18
  201.5 15.6 %collective-permute-start.30 = (bf16[512,256]{1,0:T(8,128)(2,1)S(1)}, bf16[512,256]{1,0:T(8,128)(2,1)S(1)}, u32[]{:S(2)}, u32[]{:S(2)}) collective-permute-start(bf16[512,256]{1,0:T(8,128)(2,1)S(1)} %get-tuple-element.119), channel_id=1, source_target_pairs={{0,4},{1,5},{2,6},{3,7},{4,8},{5,9},{6,10},{7,11},{8,12},{9,13},{1... | collective-permute-start | bytes 786440 | tf_op jit(solution)/shard_map/ppermute | solution.py:18
  217.1 2.5 %collective-permute-start.31 = (f32[448,512]{1,0:T(8,128)S(1)}, f32[448,512]{1,0:T(8,128)S(1)}, u32[]{:S(2)}, u32[]{:S(2)}) collective-permute-start(f32[448,512]{1,0:T(8,128)S(1)} %pad_maximum_fusion.5), channel_id=1, source_target_pairs={{0,1},{1,0},{2,3},{3,2},{4,5},{5,4},{6,7},{7,6},{8,9},{9,8},{10,11... | collective-permute-start | bytes 2752520 | tf_op jit(solution)/shard_map/ppermute | solution.py:24
  (14 other events, 270.7 us)

commit v21 on v20

--- a/solution.py
+++ b/solution.py
@@ -140,7 +140,8 @@
             pending = [item for item in pending if item[1] > number]
         if (bit, down) in rider_steps and sent_rows + RIDER_ROWS <= positions:
             buf, pieces = lax.optimization_barrier((buf, (lower_all, upper_all)))
-            pending.append((send_rows(pieces, sent_rows, sent_rows + RIDER_ROWS), number + RIDER_SPAN))
+            span = RIDER_SPAN if sent_rows + 2 * RIDER_ROWS <= positions and (bit, down) != rider_steps[-1] else 1
+            pending.append((send_rows(pieces, sent_rows, sent_rows + RIDER_ROWS), number + span))
             sent_rows += RIDER_ROWS
         if not down and bit == 2 and not late:
             buf, pieces = lax.optimization_barrier((buf, (lower_all, upper_all)))

time: 222 us -> 225 us (1.014)
  waiting for transfers between devices: 66.7 us -> 77.9 us
  starting transfers between devices: 96.2 us -> 87.9 us
    ppermute x24, waiting for transfers between devices: 39.6 us -> 50.1 us  [from_behind(): return lax.ppermute(value, axis, pairs)]
    ppermute x24, starting transfers between devices: 82 us -> 73.7 us  [from_behind(): return lax.ppermute(value, axis, pairs)]
  transfers between devices with their start and end apart: 32 -> 32, of which waited for: 14 -> 15; matrix products, arithmetic and copies ran while one was open for 22% -> 22% of each run, Pallas kernels for 0% -> 0%
where the time goes in v21:
time: 225 us
  starting transfers between devices  87.9 us (39%)
  waiting for transfers between devices  77.9 us (35%)
  matrix products  33.5 us (15%)
  local copies, waits for them, and re-layouts  17.9 us (8%)
  other arithmetic  5.77 us (3%)
    ppermute x24, starting transfers between devices, from_behind(): return lax.ppermute(value, axis, pairs)  73.7 us
    ppermute x24, waiting for transfers between devices, from_behind(): return lax.ppermute(value, axis, pairs)  50.1 us
    ppermute x8, waiting for transfers between devices, exchange(): return lax.ppermute(value, axis, pairs)  27.8 us
    ppermute x8, starting transfers between devices, exchange(): return lax.ppermute(value, axis, pairs)  14.1 us
    dot_general x5, matrix products, chunk_layer(): preact = preact + jnp.dot(middle, w_mid, preferred_element_type=jnp.float32)  4.64 us
    slice x2, local copies, waits for them, and re-layouts, body(): middle = activations[bounds[k]:bounds[k + 1]]  4.54 us
  transfers between devices with their start and end apart: 32, of which 15 were waited for; matrix products, arithmetic and copies ran while one was open for 22% of the time, Pallas kernels for 0%

profile of v21, /device:TPU:0, one launch (start us, length us, event | category | flops | bytes accessed | tf_op | source)
XLA Modules:
  0.0 224.7 jit_solution(375475675149946758)
XLA Ops:
  0.7 2.0 fusion.119
  2.7 3.0 %collective-permute-start.8 = (bf16[512,256]{1,0:T(8,128)(2,1)}, bf16[512,256]{1,0:T(8,128)(2,1)S(1)}, u32[]{:S(2)}, u32[]{:S(2)}) collective-permute-start(bf16[512,256]{1,0:T(8,128)(2,1)} %get-tuple-element.125), channel_id=1, source_target_pairs={{0,4},{1,5},{2,6},{3,7},{4,8},{5,9},{6,10},{7,11},{8,12},{9,13},{1... | collective-permute-start | bytes 786440 | tf_op jit(solution)/shard_map/ppermute | solution.py:18
  5.7 2.0 collective-permute-start.9
  7.7 2.5 %fusion.118 = (bf16[1024,256]{1,0:T(8,128)(2,1)}, bf16[1024,256]{1,0:T(8,128)(2,1)}, bf16[1024,256]{1,0:T(8,128)(2,1)}) fusion(bf16[4096,256]{1,0:T(8,128)(2,1)} %param.4), kind=kLoop, calls=%fused_computation.206 | loop fusion | bytes 3145728 | tf_op jit(solution)/shard_map/slice | solution.py:95
  10.3 3.8 %collective-permute-start.1 = (bf16[1024,256]{1,0:T(8,128)(2,1)}, bf16[1024,256]{1,0:T(8,128)(2,1)}, u32[]{:S(2)}, u32[]{:S(2)}) collective-permute-start(bf16[1024,256]{1,0:T(8,128)(2,1)} %get-tuple-element.123), channel_id=1, source_target_pairs={{0,12},{1,13},{2,14},{3,15},{4,0},{5,1},{6,2},{7,3},{8,4},{9,5},{1... | collective-permute-start | bytes 1572872 | tf_op jit(solution)/shard_map/ppermute | solution.py:18
  14.1 1.8 fusion.77
  16.5 1.7 fusion.71
  18.6 13.5 %collective-permute-done = bf16[1024,256]{1,0:T(8,128)(2,1)} collective-permute-done((bf16[1024,256]{1,0:T(8,128)(2,1)}, bf16[1024,256]{1,0:T(8,128)(2,1)}, u32[]{:S(2)}, u32[]{:S(2)}) %collective-permute-start) | collective-permute-done | bytes 524320 | tf_op jit(solution)/shard_map/ppermute | solution.py:18
  32.1 13.2 %collective-permute-start.3 = (bf16[1024,256]{1,0:T(8,128)(2,1)}, bf16[1024,256]{1,0:T(8,128)(2,1)S(1)}, u32[]{:S(2)}, u32[]{:S(2)}) collective-permute-start(bf16[1024,256]{1,0:T(8,128)(2,1)} %get-tuple-element.121), channel_id=1, source_target_pairs={{0,12},{1,13},{2,14},{3,15},{4,0},{5,1},{6,2},{7,3},{8,4},{9,5},{1... | collective-permute-start | bytes 1572872 | tf_op jit(solution)/shard_map/ppermute | solution.py:18
  47.0 1.7 add_add_fusion.2
  54.6 13.2 %collective-permute-start.5 = (bf16[1024,256]{1,0:T(8,128)(2,1)S(1)}, bf16[1024,256]{1,0:T(8,128)(2,1)S(1)}, u32[]{:S(2)}, u32[]{:S(2)}) collective-permute-start(bf16[1024,256]{1,0:T(8,128)(2,1)S(1)} %copy-done.12), channel_id=1, source_target_pairs={{0,12},{1,13},{2,14},{3,15},{4,0},{5,1},{6,2},{7,3},{8,4},{9,5},{1... | collective-permute-start | bytes 1572872 | tf_op jit(solution)/shard_map/ppermute | solution.py:18
  67.8 8.3 %collective-permute-start.6 = (bf16[512,256]{1,0:T(8,128)(2,1)S(1)}, bf16[512,256]{1,0:T(8,128)(2,1)S(1)}, u32[]{:S(2)}, u32[]{:S(2)}) collective-permute-start(bf16[512,256]{1,0:T(8,128)(2,1)S(1)} %copy-done.13), channel_id=1, source_target_pairs={{0,4},{1,5},{2,6},{3,7},{4,8},{5,9},{6,10},{7,11},{8,12},{9,13},{1... | collective-permute-start | bytes 786440 | tf_op jit(solution)/shard_map/ppermute | solution.py:18
  82.3 7.8 %collective-permute-start.7 = (bf16[512,256]{1,0:T(8,128)(2,1)S(1)}, bf16[512,256]{1,0:T(8,128)(2,1)S(1)}, u32[]{:S(2)}, u32[]{:S(2)}) collective-permute-start(bf16[512,256]{1,0:T(8,128)(2,1)S(1)} %copy-done.13), channel_id=1, source_target_pairs={{0,12},{1,13},{2,14},{3,15},{4,0},{5,1},{6,2},{7,3},{8,4},{9,5},{1... | collective-permute-start | bytes 786440 | tf_op jit(solution)/shard_map/ppermute | solution.py:18
  94.8 3.1 %collective-permute-done.7 = bf16[512,256]{1,0:T(8,128)(2,1)S(1)} collective-permute-done((bf16[512,256]{1,0:T(8,128)(2,1)S(1)}, bf16[512,256]{1,0:T(8,128)(2,1)S(1)}, u32[]{:S(2)}, u32[]{:S(2)}) %collective-permute-start.7) | collective-permute-done | bytes 262176 | tf_op jit(solution)/shard_map/ppermute | solution.py:18
  105.5 2.4 %collective-permute-start.12 = (bf16[1024,256]{1,0:T(8,128)(2,1)S(1)}, bf16[1024,256]{1,0:T(8,128)(2,1)S(1)}, u32[]{:S(2)}, u32[]{:S(2)}) collective-permute-start(bf16[1024,256]{1,0:T(8,128)(2,1)S(1)} %get-tuple-element.75), channel_id=1, source_target_pairs={{0,12},{1,13},{2,14},{3,15},{4,0},{5,1},{6,2},{7,3},{8,4},{9,5},{1... | collective-permute-start | bytes 1572872 | tf_op jit(solution)/shard_map/ppermute | solution.py:18
  114.8 10.4 %collective-permute-done.11 = f32[114688]{0:T(1024)S(1)} collective-permute-done((f32[114688]{0:T(1024)S(1)}, f32[114688]{0:T(1024)S(1)}, u32[]{:S(2)}, u32[]{:S(2)}) %collective-permute-start.11) | collective-permute-done | bytes 458784 | tf_op jit(solution)/shard_map/ppermute | solution.py:24
  125.2 6.6 %collective-permute-done.13 = bf16[1024,256]{1,0:T(8,128)(2,1)S(1)} collective-permute-done((bf16[1024,256]{1,0:T(8,128)(2,1)S(1)}, bf16[1024,256]{1,0:T(8,128)(2,1)S(1)}, u32[]{:S(2)}, u32[]{:S(2)}) %collective-permute-start.13) | collective-permute-done | bytes 524320 | tf_op jit(solution)/shard_map/ppermute | solution.py:18
  137.3 3.1 %collective-permute-done.14 = f32[57344]{0:T(1024)S(1)} collective-permute-done((f32[57344]{0:T(1024)S(1)}, f32[57344]{0:T(1024)S(1)}, u32[]{:S(2)}, u32[]{:S(2)}) %collective-permute-start.14) | collective-permute-done | bytes 229408 | tf_op jit(solution)/shard_map/ppermute | solution.py:24
  143.7 2.4 %collective-permute-start.19 = (bf16[512,256]{1,0:T(8,128)(2,1)}, bf16[512,256]{1,0:T(8,128)(2,1)S(1)}, u32[]{:S(2)}, u32[]{:S(2)}) collective-permute-start(bf16[512,256]{1,0:T(8,128)(2,1)} %slice.148), channel_id=1, source_target_pairs={{0,12},{1,13},{2,14},{3,15},{4,0},{5,1},{6,2},{7,3},{8,4},{9,5},{1... | collective-permute-start | bytes 786440 | tf_op jit(solution)/shard_map/ppermute | solution.py:18
  146.8 7.9 %collective-permute-done.15 = f32[28672]{0:T(1024)S(1)} collective-permute-done((f32[28672]{0:T(1024)S(1)}, f32[28672]{0:T(1024)S(1)}, u32[]{:S(2)}, u32[]{:S(2)}) %collective-permute-start.15) | collective-permute-done | bytes 114720 | tf_op jit(solution)/shard_map/ppermute | solution.py:24
  154.7 2.1 collective-permute-start.18
  157.8 6.7 %collective-permute-start.22 = (bf16[512,256]{1,0:T(8,128)(2,1)S(1)}, bf16[512,256]{1,0:T(8,128)(2,1)S(1)}, u32[]{:S(2)}, u32[]{:S(2)}) collective-permute-start(bf16[512,256]{1,0:T(8,128)(2,1)S(1)} %slice.150), channel_id=1, source_target_pairs={{0,12},{1,13},{2,14},{3,15},{4,0},{5,1},{6,2},{7,3},{8,4},{9,5},{1... | collective-permute-start | bytes 786440 | tf_op jit(solution)/shard_map/ppermute | solution.py:18
  167.8 3.3 %collective-permute-done.18 = f32[56,512]{1,0:T(8,128)S(1)} collective-permute-done((f32[56,512]{1,0:T(8,128)S(1)}, f32[56,512]{1,0:T(8,128)S(1)}, u32[]{:S(2)}, u32[]{:S(2)}) %collective-permute-start.18) | collective-permute-done | bytes 114720 | tf_op jit(solution)/shard_map/ppermute | solution.py:24
  171.1 5.7 %collective-permute-start.21 = (f32[112,512]{1,0:T(8,128)S(1)}, f32[112,512]{1,0:T(8,128)S(1)}, u32[]{:S(2)}, u32[]{:S(2)}) collective-permute-start(f32[112,512]{1,0:T(8,128)S(1)} %pad_maximum_fusion.9), channel_id=1, source_target_pairs={{0,4},{1,5},{2,6},{3,7},{4,0},{5,1},{6,2},{7,3},{8,12},{9,13},{10,... | collective-permute-start | bytes 688136 | tf_op jit(solution)/shard_map/ppermute | solution.py:24
  177.8 2.9 %collective-permute-start.24 = (bf16[512,256]{1,0:T(8,128)(2,1)S(1)}, bf16[512,256]{1,0:T(8,128)(2,1)S(1)}, u32[]{:S(2)}, u32[]{:S(2)}) collective-permute-start(bf16[512,256]{1,0:T(8,128)(2,1)S(1)} %slice.152), channel_id=1, source_target_pairs={{0,12},{1,13},{2,14},{3,15},{4,0},{5,1},{6,2},{7,3},{8,4},{9,5},{1... | collective-permute-start | bytes 786440 | tf_op jit(solution)/shard_map/ppermute | solution.py:18
  181.8 2.3 %collective-permute-done.21 = f32[112,512]{1,0:T(8,128)S(1)} collective-permute-done((f32[112,512]{1,0:T(8,128)S(1)}, f32[112,512]{1,0:T(8,128)S(1)}, u32[]{:S(2)}, u32[]{:S(2)}) %collective-permute-start.21) | collective-permute-done | bytes 229408 | tf_op jit(solution)/shard_map/ppermute | solution.py:24
  184.2 6.7 %collective-permute-done.24 = bf16[512,256]{1,0:T(8,128)(2,1)S(1)} collective-permute-done((bf16[512,256]{1,0:T(8,128)(2,1)S(1)}, bf16[512,256]{1,0:T(8,128)(2,1)S(1)}, u32[]{:S(2)}, u32[]{:S(2)}) %collective-permute-start.24) | collective-permute-done | bytes 262176 | tf_op jit(solution)/shard_map/ppermute | solution.py:18
  190.9 3.7 %collective-permute-done.25 = bf16[512,256]{1,0:T(8,128)(2,1)S(1)} collective-permute-done((bf16[512,256]{1,0:T(8,128)(2,1)S(1)}, bf16[512,256]{1,0:T(8,128)(2,1)S(1)}, u32[]{:S(2)}, u32[]{:S(2)}) %collective-permute-start.25) | collective-permute-done | bytes 262176 | tf_op jit(solution)/shard_map/ppermute | solution.py:18
  200.4 3.2 %collective-permute-start.29 = (bf16[512,256]{1,0:T(8,128)(2,1)S(1)}, bf16[512,256]{1,0:T(8,128)(2,1)S(1)}, u32[]{:S(2)}, u32[]{:S(2)}) collective-permute-start(bf16[512,256]{1,0:T(8,128)(2,1)S(1)} %get-tuple-element.119), channel_id=1, source_target_pairs={{0,12},{1,13},{2,14},{3,15},{4,0},{5,1},{6,2},{7,3},{8,4},{9,5},{1... | collective-permute-start | bytes 786440 | tf_op jit(solution)/shard_map/ppermute | solution.py:18
  204.6 7.6 %collective-permute-done.27 = bf16[512,256]{1,0:T(8,128)(2,1)S(1)} collective-permute-done((bf16[512,256]{1,0:T(8,128)(2,1)S(1)}, bf16[512,256]{1,0:T(8,128)(2,1)S(1)}, u32[]{:S(2)}, u32[]{:S(2)}) %collective-permute-start.27) | collective-permute-done | bytes 262176 | tf_op jit(solution)/shard_map/ppermute | solution.py:18
  212.1 7.9 %collective-permute-done.29 = bf16[512,256]{1,0:T(8,128)(2,1)S(1)} collective-permute-done((bf16[512,256]{1,0:T(8,128)(2,1)S(1)}, bf16[512,256]{1,0:T(8,128)(2,1)S(1)}, u32[]{:S(2)}, u32[]{:S(2)}) %collective-permute-start.29) | collective-permute-done | bytes 262176 | tf_op jit(solution)/shard_map/ppermute | solution.py:18
  220.1 2.2 add_convert_fusion
  (172 shorter events, 58.4 us)
Async XLA Ops:
  2.7 98.3 %collective-permute-start.8 = (bf16[512,256]{1,0:T(8,128)(2,1)}, bf16[512,256]{1,0:T(8,128)(2,1)S(1)}, u32[]{:S(2)}, u32[]{:S(2)}) collective-permute-start(bf16[512,256]{1,0:T(8,128)(2,1)} %get-tuple-element.125), channel_id=1, source_target_pairs={{0,4},{1,5},{2,6},{3,7},{4,8},{5,9},{6,10},{7,11},{8,12},{9,13},{1... | collective-permute-start | bytes 786440 | tf_op jit(solution)/shard_map/ppermute | solution.py:18
  5.7 95.3 %collective-permute-start.9 = (bf16[512,256]{1,0:T(8,128)(2,1)}, bf16[512,256]{1,0:T(8,128)(2,1)S(1)}, u32[]{:S(2)}, u32[]{:S(2)}) collective-permute-start(bf16[512,256]{1,0:T(8,128)(2,1)} %get-tuple-element.125), channel_id=1, source_target_pairs={{0,12},{1,13},{2,14},{3,15},{4,0},{5,1},{6,2},{7,3},{8,4},{9,5},{1... | collective-permute-start | bytes 786440 | tf_op jit(solution)/shard_map/ppermute | solution.py:18
  10.3 21.9 %collective-permute-start = (bf16[1024,256]{1,0:T(8,128)(2,1)}, bf16[1024,256]{1,0:T(8,128)(2,1)}, u32[]{:S(2)}, u32[]{:S(2)}) collective-permute-start(bf16[1024,256]{1,0:T(8,128)(2,1)} %get-tuple-element.123), channel_id=1, source_target_pairs={{0,4},{1,5},{2,6},{3,7},{4,8},{5,9},{6,10},{7,11},{8,12},{9,13},{1... | collective-permute-start | bytes 1572872 | tf_op jit(solution)/shard_map/ppermute | solution.py:18
  10.3 36.6 %collective-permute-start.1 = (bf16[1024,256]{1,0:T(8,128)(2,1)}, bf16[1024,256]{1,0:T(8,128)(2,1)}, u32[]{:S(2)}, u32[]{:S(2)}) collective-permute-start(bf16[1024,256]{1,0:T(8,128)(2,1)} %get-tuple-element.123), channel_id=1, source_target_pairs={{0,12},{1,13},{2,14},{3,15},{4,0},{5,1},{6,2},{7,3},{8,4},{9,5},{1... | collective-permute-start | bytes 1572872 | tf_op jit(solution)/shard_map/ppermute | solution.py:18
  14.1 40.5 %collective-permute-start.2 = (bf16[1024,256]{1,0:T(8,128)(2,1)}, bf16[1024,256]{1,0:T(8,128)(2,1)}, u32[]{:S(2)}, u32[]{:S(2)}) collective-permute-start(bf16[1024,256]{1,0:T(8,128)(2,1)} %get-tuple-element.121), channel_id=1, source_target_pairs={{0,4},{1,5},{2,6},{3,7},{4,8},{5,9},{6,10},{7,11},{8,12},{9,13},{1... | collective-permute-start | bytes 1572872 | tf_op jit(solution)/shard_map/ppermute | solution.py:18
  32.1 35.7 %collective-permute-start.3 = (bf16[1024,256]{1,0:T(8,128)(2,1)}, bf16[1024,256]{1,0:T(8,128)(2,1)S(1)}, u32[]{:S(2)}, u32[]{:S(2)}) collective-permute-start(bf16[1024,256]{1,0:T(8,128)(2,1)} %get-tuple-element.121), channel_id=1, source_target_pairs={{0,12},{1,13},{2,14},{3,15},{4,0},{5,1},{6,2},{7,3},{8,4},{9,5},{1... | collective-permute-start | bytes 1572872 | tf_op jit(solution)/shard_map/ppermute | solution.py:18
  46.9 35.4 %collective-permute-start.4 = (bf16[1024,256]{1,0:T(8,128)(2,1)S(1)}, bf16[1024,256]{1,0:T(8,128)(2,1)S(1)}, u32[]{:S(2)}, u32[]{:S(2)}) collective-permute-start(bf16[1024,256]{1,0:T(8,128)(2,1)S(1)} %copy-done.12), channel_id=1, source_target_pairs={{0,4},{1,5},{2,6},{3,7},{4,8},{5,9},{6,10},{7,11},{8,12},{9,13},{1... | collective-permute-start | bytes 1572872 | tf_op jit(solution)/shard_map/ppermute | solution.py:18
  54.6 35.5 %collective-permute-start.5 = (bf16[1024,256]{1,0:T(8,128)(2,1)S(1)}, bf16[1024,256]{1,0:T(8,128)(2,1)S(1)}, u32[]{:S(2)}, u32[]{:S(2)}) collective-permute-start(bf16[1024,256]{1,0:T(8,128)(2,1)S(1)} %copy-done.12), channel_id=1, source_target_pairs={{0,12},{1,13},{2,14},{3,15},{4,0},{5,1},{6,2},{7,3},{8,4},{9,5},{1... | collective-permute-start | bytes 1572872 | tf_op jit(solution)/shard_map/ppermute | solution.py:18
  67.8 27.0 %collective-permute-start.6 = (bf16[512,256]{1,0:T(8,128)(2,1)S(1)}, bf16[512,256]{1,0:T(8,128)(2,1)S(1)}, u32[]{:S(2)}, u32[]{:S(2)}) collective-permute-start(bf16[512,256]{1,0:T(8,128)(2,1)S(1)} %copy-done.13), channel_id=1, source_target_pairs={{0,4},{1,5},{2,6},{3,7},{4,8},{5,9},{6,10},{7,11},{8,12},{9,13},{1... | collective-permute-start | bytes 786440 | tf_op jit(solution)/shard_map/ppermute | solution.py:18
  82.3 15.6 %collective-permute-start.7 = (bf16[512,256]{1,0:T(8,128)(2,1)S(1)}, bf16[512,256]{1,0:T(8,128)(2,1)S(1)}, u32[]{:S(2)}, u32[]{:S(2)}) collective-permute-start(bf16[512,256]{1,0:T(8,128)(2,1)S(1)} %copy-done.13), channel_id=1, source_target_pairs={{0,12},{1,13},{2,14},{3,15},{4,0},{5,1},{6,2},{7,3},{8,4},{9,5},{1... | collective-permute-start | bytes 786440 | tf_op jit(solution)/shard_map/ppermute | solution.py:18
  105.4 7.0 %collective-permute-start.10 = (f32[229376]{0:T(1024)S(1)}, f32[229376]{0:T(1024)S(1)}, u32[]{:S(2)}, u32[]{:S(2)}) collective-permute-start(f32[229376]{0:T(1024)S(1)} %dynamic_slice.25), channel_id=1, source_target_pairs={{0,1},{1,0},{2,3},{3,2},{4,5},{5,4},{6,7},{7,6},{8,9},{9,8},{10,11... | collective-permute-start | bytes 2752520 | tf_op jit(solution)/shard_map/ppermute | solution.py:24
  105.5 19.8 %collective-permute-start.12 = (bf16[1024,256]{1,0:T(8,128)(2,1)S(1)}, bf16[1024,256]{1,0:T(8,128)(2,1)S(1)}, u32[]{:S(2)}, u32[]{:S(2)}) collective-permute-start(bf16[1024,256]{1,0:T(8,128)(2,1)S(1)} %get-tuple-element.75), channel_id=1, source_target_pairs={{0,12},{1,13},{2,14},{3,15},{4,0},{5,1},{6,2},{7,3},{8,4},{9,5},{1... | collective-permute-start | bytes 1572872 | tf_op jit(solution)/shard_map/ppermute | solution.py:18
  107.8 24.0 %collective-permute-start.13 = (bf16[1024,256]{1,0:T(8,128)(2,1)S(1)}, bf16[1024,256]{1,0:T(8,128)(2,1)S(1)}, u32[]{:S(2)}, u32[]{:S(2)}) collective-permute-start(bf16[1024,256]{1,0:T(8,128)(2,1)S(1)} %get-tuple-element.76), channel_id=1, source_target_pairs={{0,4},{1,5},{2,6},{3,7},{4,8},{5,9},{6,10},{7,11},{8,12},{9,13},{1... | collective-permute-start | bytes 1572872 | tf_op jit(solution)/shard_map/ppermute | solution.py:18
  112.5 12.7 %collective-permute-start.11 = (f32[114688]{0:T(1024)S(1)}, f32[114688]{0:T(1024)S(1)}, u32[]{:S(2)}, u32[]{:S(2)}) collective-permute-start(f32[114688]{0:T(1024)S(1)} %dynamic_slice.27), channel_id=1, source_target_pairs={{0,2},{1,3},{2,0},{3,1},{4,6},{5,7},{6,4},{7,5},{8,10},{9,11},{10,... | collective-permute-start | bytes 1376264 | tf_op jit(solution)/shard_map/ppermute | solution.py:24
  131.8 8.6 %collective-permute-start.14 = (f32[57344]{0:T(1024)S(1)}, f32[57344]{0:T(1024)S(1)}, u32[]{:S(2)}, u32[]{:S(2)}) collective-permute-start(f32[57344]{0:T(1024)S(1)} %dynamic_slice.29), channel_id=1, source_target_pairs={{0,4},{1,5},{2,6},{3,7},{4,0},{5,1},{6,2},{7,3},{8,12},{9,13},{10,... | collective-permute-start | bytes 688136 | tf_op jit(solution)/shard_map/ppermute | solution.py:24
  134.6 20.1 %collective-permute-start.16 = (bf16[512,256]{1,0:T(8,128)(2,1)}, bf16[512,256]{1,0:T(8,128)(2,1)S(1)}, u32[]{:S(2)}, u32[]{:S(2)}) collective-permute-start(bf16[512,256]{1,0:T(8,128)(2,1)} %slice.146), channel_id=1, source_target_pairs={{0,12},{1,13},{2,14},{3,15},{4,0},{5,1},{6,2},{7,3},{8,4},{9,5},{1... | collective-permute-start | bytes 786440 | tf_op jit(solution)/shard_map/ppermute | solution.py:18
  136.7 18.0 %collective-permute-start.17 = (bf16[512,256]{1,0:T(8,128)(2,1)}, bf16[512,256]{1,0:T(8,128)(2,1)}, u32[]{:S(2)}, u32[]{:S(2)}) collective-permute-start(bf16[512,256]{1,0:T(8,128)(2,1)} %slice.147), channel_id=1, source_target_pairs={{0,4},{1,5},{2,6},{3,7},{4,8},{5,9},{6,10},{7,11},{8,12},{9,13},{1... | collective-permute-start | bytes 786440 | tf_op jit(solution)/shard_map/ppermute | solution.py:18
  140.5 14.2 %collective-permute-start.15 = (f32[28672]{0:T(1024)S(1)}, f32[28672]{0:T(1024)S(1)}, u32[]{:S(2)}, u32[]{:S(2)}) collective-permute-start(f32[28672]{0:T(1024)S(1)} %dynamic_slice.31), channel_id=1, source_target_pairs={{0,8},{1,9},{2,10},{3,11},{4,12},{5,13},{6,14},{7,15},{8,0},{9,1},... | collective-permute-start | bytes 344072 | tf_op jit(solution)/shard_map/ppermute | solution.py:24
  143.7 27.4 %collective-permute-start.19 = (bf16[512,256]{1,0:T(8,128)(2,1)}, bf16[512,256]{1,0:T(8,128)(2,1)S(1)}, u32[]{:S(2)}, u32[]{:S(2)}) collective-permute-start(bf16[512,256]{1,0:T(8,128)(2,1)} %slice.148), channel_id=1, source_target_pairs={{0,12},{1,13},{2,14},{3,15},{4,0},{5,1},{6,2},{7,3},{8,4},{9,5},{1... | collective-permute-start | bytes 786440 | tf_op jit(solution)/shard_map/ppermute | solution.py:18
  146.8 24.4 %collective-permute-start.20 = (bf16[512,256]{1,0:T(8,128)(2,1)}, bf16[512,256]{1,0:T(8,128)(2,1)S(1)}, u32[]{:S(2)}, u32[]{:S(2)}) collective-permute-start(bf16[512,256]{1,0:T(8,128)(2,1)} %slice.149), channel_id=1, source_target_pairs={{0,4},{1,5},{2,6},{3,7},{4,8},{5,9},{6,10},{7,11},{8,12},{9,13},{1... | collective-permute-start | bytes 786440 | tf_op jit(solution)/shard_map/ppermute | solution.py:18
  154.7 16.3 %collective-permute-start.18 = (f32[56,512]{1,0:T(8,128)S(1)}, f32[56,512]{1,0:T(8,128)S(1)}, u32[]{:S(2)}, u32[]{:S(2)}) collective-permute-start(f32[56,512]{1,0:T(8,128)S(1)} %reshape.20), channel_id=1, source_target_pairs={{0,8},{1,9},{2,10},{3,11},{4,12},{5,13},{6,14},{7,15},{8,0},{9,1},... | collective-permute-start | bytes 344072 | tf_op jit(solution)/shard_map/ppermute | solution.py:24
  157.8 26.3 %collective-permute-start.22 = (bf16[512,256]{1,0:T(8,128)(2,1)S(1)}, bf16[512,256]{1,0:T(8,128)(2,1)S(1)}, u32[]{:S(2)}, u32[]{:S(2)}) collective-permute-start(bf16[512,256]{1,0:T(8,128)(2,1)S(1)} %slice.150), channel_id=1, source_target_pairs={{0,12},{1,13},{2,14},{3,15},{4,0},{5,1},{6,2},{7,3},{8,4},{9,5},{1... | collective-permute-start | bytes 786440 | tf_op jit(solution)/shard_map/ppermute | solution.py:18
  165.5 18.7 %collective-permute-start.23 = (bf16[512,256]{1,0:T(8,128)(2,1)S(1)}, bf16[512,256]{1,0:T(8,128)(2,1)S(1)}, u32[]{:S(2)}, u32[]{:S(2)}) collective-permute-start(bf16[512,256]{1,0:T(8,128)(2,1)S(1)} %slice.151), channel_id=1, source_target_pairs={{0,4},{1,5},{2,6},{3,7},{4,8},{5,9},{6,10},{7,11},{8,12},{9,13},{1... | collective-permute-start | bytes 786440 | tf_op jit(solution)/shard_map/ppermute | solution.py:18
  171.1 12.9 %collective-permute-start.21 = (f32[112,512]{1,0:T(8,128)S(1)}, f32[112,512]{1,0:T(8,128)S(1)}, u32[]{:S(2)}, u32[]{:S(2)}) collective-permute-start(f32[112,512]{1,0:T(8,128)S(1)} %pad_maximum_fusion.9), channel_id=1, source_target_pairs={{0,4},{1,5},{2,6},{3,7},{4,0},{5,1},{6,2},{7,3},{8,12},{9,13},{10,... | collective-permute-start | bytes 688136 | tf_op jit(solution)/shard_map/ppermute | solution.py:24
  177.8 13.1 %collective-permute-start.24 = (bf16[512,256]{1,0:T(8,128)(2,1)S(1)}, bf16[512,256]{1,0:T(8,128)(2,1)S(1)}, u32[]{:S(2)}, u32[]{:S(2)}) collective-permute-start(bf16[512,256]{1,0:T(8,128)(2,1)S(1)} %slice.152), channel_id=1, source_target_pairs={{0,12},{1,13},{2,14},{3,15},{4,0},{5,1},{6,2},{7,3},{8,4},{9,5},{1... | collective-permute-start | bytes 786440 | tf_op jit(solution)/shard_map/ppermute | solution.py:18
  181.6 13.0 %collective-permute-start.25 = (bf16[512,256]{1,0:T(8,128)(2,1)S(1)}, bf16[512,256]{1,0:T(8,128)(2,1)S(1)}, u32[]{:S(2)}, u32[]{:S(2)}) collective-permute-start(bf16[512,256]{1,0:T(8,128)(2,1)S(1)} %slice.153), channel_id=1, source_target_pairs={{0,4},{1,5},{2,6},{3,7},{4,8},{5,9},{6,10},{7,11},{8,12},{9,13},{1... | collective-permute-start | bytes 786440 | tf_op jit(solution)/shard_map/ppermute | solution.py:18
  194.6 9.8 %collective-permute-start.26 = (f32[224,512]{1,0:T(8,128)S(1)}, f32[224,512]{1,0:T(8,128)S(1)}, u32[]{:S(2)}, u32[]{:S(2)}) collective-permute-start(f32[224,512]{1,0:T(8,128)S(1)} %pad_maximum_fusion.8), channel_id=1, source_target_pairs={{0,2},{1,3},{2,0},{3,1},{4,6},{5,7},{6,4},{7,5},{8,10},{9,11},{10,... | collective-permute-start | bytes 1376264 | tf_op jit(solution)/shard_map/ppermute | solution.py:24
  197.2 15.0 %collective-permute-start.27 = (bf16[512,256]{1,0:T(8,128)(2,1)S(1)}, bf16[512,256]{1,0:T(8,128)(2,1)S(1)}, u32[]{:S(2)}, u32[]{:S(2)}) collective-permute-start(bf16[512,256]{1,0:T(8,128)(2,1)S(1)} %get-tuple-element.120), channel_id=1, source_target_pairs={{0,12},{1,13},{2,14},{3,15},{4,0},{5,1},{6,2},{7,3},{8,4},{9,5},{1... | collective-permute-start | bytes 786440 | tf_op jit(solution)/shard_map/ppermute | solution.py:18
  199.7 12.5 %collective-permute-start.28 = (bf16[512,256]{1,0:T(8,128)(2,1)S(1)}, bf16[512,256]{1,0:T(8,128)(2,1)S(1)}, u32[]{:S(2)}, u32[]{:S(2)}) collective-permute-start(bf16[512,256]{1,0:T(8,128)(2,1)S(1)} %get-tuple-element.118), channel_id=1, source_target_pairs={{0,4},{1,5},{2,6},{3,7},{4,8},{5,9},{6,10},{7,11},{8,12},{9,13},{1... | collective-permute-start | bytes 786440 | tf_op jit(solution)/shard_map/ppermute | solution.py:18
  200.4 19.6 %collective-permute-start.29 = (bf16[512,256]{1,0:T(8,128)(2,1)S(1)}, bf16[512,256]{1,0:T(8,128)(2,1)S(1)}, u32[]{:S(2)}, u32[]{:S(2)}) collective-permute-start(bf16[512,256]{1,0:T(8,128)(2,1)S(1)} %get-tuple-element.119), channel_id=1, source_target_pairs={{0,12},{1,13},{2,14},{3,15},{4,0},{5,1},{6,2},{7,3},{8,4},{9,5},{1... | collective-permute-start | bytes 786440 | tf_op jit(solution)/shard_map/ppermute | solution.py:18
  203.5 16.5 %collective-permute-start.30 = (bf16[512,256]{1,0:T(8,128)(2,1)S(1)}, bf16[512,256]{1,0:T(8,128)(2,1)S(1)}, u32[]{:S(2)}, u32[]{:S(2)}) collective-permute-start(bf16[512,256]{1,0:T(8,128)(2,1)S(1)} %get-tuple-element.117), channel_id=1, source_target_pairs={{0,4},{1,5},{2,6},{3,7},{4,8},{5,9},{6,10},{7,11},{8,12},{9,13},{1... | collective-permute-start | bytes 786440 | tf_op jit(solution)/shard_map/ppermute | solution.py:18
  220.0 2.5 %collective-permute-start.31 = (f32[448,512]{1,0:T(8,128)S(1)}, f32[448,512]{1,0:T(8,128)S(1)}, u32[]{:S(2)}, u32[]{:S(2)}) collective-permute-start(f32[448,512]{1,0:T(8,128)S(1)} %pad_maximum_fusion.5), channel_id=1, source_target_pairs={{0,1},{1,0},{2,3},{3,2},{4,5},{5,4},{6,7},{7,6},{8,9},{9,8},{10,11... | collective-permute-start | bytes 2752520 | tf_op jit(solution)/shard_map/ppermute | solution.py:24
  (14 other events, 271.5 us)
